TPU v7x, 32 devices: a whole 2x2x4 slice. The times are simulated.
32 devices in a mesh: wide: 4 (over y, core), narrow: 8 (over z, x).
Axes of the slice: x: 2, y: 2, z: 4, core: 2. Of those that a mesh axis runs over, the one named last changes fastest.
Arguments:
- tokens: bfloat16 [16384, 1024], P(('wide', 'narrow')), may hold values from -6 to 6
- cotangent: bfloat16 [16384, 1024], P(('wide', 'narrow')), may hold values from -6 to 6
- corpus_ids: int32 [8], P('wide'), may hold values from 0 to 7
- corpus_weights: float32 [8], replicated, may hold values from 0.3 to 3
- qkv_weight: bfloat16 [3, 1024, 1024], P(None, None, 'narrow'), may hold values from -0.1875 to 0.1875
- qkv_bias: float32 [3, 1024], P(None, 'narrow'), may hold values from -2 to 2
- out_weight: bfloat16 [1024, 1024], P('narrow'), may hold values from -0.75 to 0.75
- out_bias: float32 [1024], replicated, may hold values from -2 to 2
- up_weight: bfloat16 [1024, 4096], P(None, 'narrow'), may hold values from -0.1875 to 0.1875
- up_bias: float32 [4096], P('narrow'), may hold values from -3 to 3
- down_weight: bfloat16 [4096, 1024], P('narrow'), may hold values from -0.09375 to 0.09375
- down_bias: float32 [1024], replicated, may hold values from -2 to 2
- norm_gains: float32 [4, 1024], replicated, may hold values from 0.5 to 1.5
- norm_biases: float32 [4, 1024], replicated, may hold values from -2 to 2
Outputs:
- layer_out: bfloat16 [16384, 1024], P(('wide', 'narrow'))
- input_grad: bfloat16 [16384, 1024], P(('wide', 'narrow'))
- qkv_wgrad: float32 [3, 1024, 1024], P(None, None, 'narrow')
- qkv_bgrad: float32 [3, 1024], P(None, 'narrow')
- out_wgrad: float32 [1024, 1024], P('narrow')
- out_bgrad: float32 [1024], replicated
- up_wgrad: float32 [1024, 4096], P(None, 'narrow')
- up_bgrad: float32 [4096], P('narrow')
- down_wgrad: float32 [4096, 1024], P('narrow')
- down_bgrad: float32 [1024], replicated
- gain_grads: float32 [4, 1024], replicated
- bias_grads: float32 [4, 1024], replicated
All inputs are finite; a program needn't handle non-finite values.
Results may differ from a plain program's by a relative error of at most 0.023.
Values may be sent and summed in bfloat16 or wider, within the bound.
No kernel may reach another device: no remote copies, remote signals or barrier semaphores. Data moves between devices by JAX's collectives and lax.ppermute only.
A program may use at most 256 MiB of HBM per device.

v0:
```python
import math

import jax
import jax.numpy as jnp
from jax import lax
from jax.sharding import PartitionSpec as P

HEAD = 64


epsilon = 1e-05
root_half = 0.7071067811865476
gauss_norm = 0.3989422804014327
masked_score = -1e30


def norm_stats(vec_in):
    center = vec_in - jnp.mean(vec_in, axis=-1, keepdims=True)
    inverse = lax.rsqrt(jnp.mean(center * center, axis=-1, keepdims=True) + epsilon)
    return (center * inverse, inverse)


def norm_back(normed, inverse, gain_row, upstream):
    scaled = upstream * gain_row
    return inverse * (
        scaled
        - jnp.mean(scaled, axis=-1, keepdims=True)
        - normed * jnp.mean(scaled * normed, axis=-1, keepdims=True)
    )


def rotary_tables(length, head_size):
    half_size = head_size // 2
    inv_freq = jnp.exp(jnp.arange(half_size, dtype=jnp.float32) * (-math.log(10000.0) / half_size))
    angles = jnp.arange(length, dtype=jnp.float32)[:, None] * inv_freq[None, :]
    return (jnp.cos(angles), jnp.sin(angles))


def rotate(vectors, cos_table, sine_table):
    half_size = vectors.shape[-1] // 2
    front_half = vectors[..., :half_size]
    back_half = vectors[..., half_size:]
    cos_grid = cos_table[:, None, :]
    sin_grid = sine_table[:, None, :]
    return jnp.concatenate(
        [
            front_half * cos_grid - back_half * sin_grid,
            front_half * sin_grid + back_half * cos_grid,
        ],
        axis=-1,
    )


def rotate_back(vectors, cos_table, sine_table):
    half_size = vectors.shape[-1] // 2
    front_half = vectors[..., :half_size]
    back_half = vectors[..., half_size:]
    cos_grid = cos_table[:, None, :]
    sin_grid = sine_table[:, None, :]
    return jnp.concatenate(
        [
            front_half * cos_grid + back_half * sin_grid,
            back_half * cos_grid - front_half * sin_grid,
        ],
        axis=-1,
    )


def gelu_value(hidden):
    return 0.5 * hidden * (1.0 + lax.erf(hidden * root_half))


def gelu_slope(hidden):
    return (
        0.5 * (1.0 + lax.erf(hidden * root_half))
        + hidden * jnp.exp(-0.5 * hidden * hidden) * gauss_norm
    )


def project_qkv(gathered, qkv_weight, qkv_bias, cos_table, sine_table, seq_count, length):
    heads_here = qkv_weight.shape[2] // HEAD
    qkv_pre = (
        jnp.einsum("sd,tde->tse", gathered, qkv_weight, preferred_element_type=jnp.float32)
        + qkv_bias[:, None, :]
    )
    shaped = qkv_pre.reshape(3, seq_count, length, heads_here, HEAD)
    query = rotate(shaped[0], cos_table, sine_table).astype(jnp.bfloat16)
    key_rows = rotate(shaped[1], cos_table, sine_table).astype(jnp.bfloat16)
    values = shaped[2].astype(jnp.bfloat16)
    return (query, key_rows, values)


def block_scores(query, key_rows, block_start, block_rows):
    key_stop = block_start + block_rows
    query_block = query[:, block_start:key_stop]
    key_block = key_rows[:, :key_stop]
    scores = jnp.einsum(
        "bqhd,bkhd->bhqk", query_block, key_block, preferred_element_type=jnp.float32
    ) * (1.0 / math.sqrt(HEAD))
    query_pos = block_start + jnp.arange(block_rows)
    key_pos = jnp.arange(key_stop)
    allowed = key_pos[None, :] <= query_pos[:, None]
    return (jnp.where(allowed[None, None], scores, masked_score), query_block, key_block)


def attend_forward(query, key_rows, values, block_rows):
    length = query.shape[1]
    outputs = []
    totals = []
    for block_start in range(0, length, block_rows):
        key_stop = block_start + block_rows
        scores, query_block, key_block = block_scores(query, key_rows, block_start, block_rows)
        row_max = jnp.max(scores, axis=-1, keepdims=True)
        log_total = row_max + jnp.log(jnp.sum(jnp.exp(scores - row_max), axis=-1, keepdims=True))
        probs_low = jnp.exp(scores - log_total).astype(jnp.bfloat16)
        outputs.append(
            jnp.einsum(
                "bhqk,bkhd->bqhd",
                probs_low,
                values[:, :key_stop],
                preferred_element_type=jnp.float32,
            )
        )
        totals.append(log_total)
    return (jnp.concatenate(outputs, axis=1), totals)


def attend_backward(query, key_rows, values, attn_grad, totals, block_rows):
    length = query.shape[1]
    score_scale = 1.0 / math.sqrt(HEAD)
    keys_grad = jnp.zeros(key_rows.shape, jnp.float32)
    values_grad = jnp.zeros(values.shape, jnp.float32)
    query_grads = []
    outputs = []
    for block_number, block_start in enumerate(range(0, length, block_rows)):
        key_stop = block_start + block_rows
        scores, query_block, key_block = block_scores(query, key_rows, block_start, block_rows)
        value_block = values[:, :key_stop]
        grad_block = attn_grad[:, block_start:key_stop]
        probs_full = jnp.exp(scores - totals[block_number])
        probs_low = probs_full.astype(jnp.bfloat16)
        outputs.append(
            jnp.einsum(
                "bhqk,bkhd->bqhd", probs_low, value_block, preferred_element_type=jnp.float32
            )
        )
        probs_grad = jnp.einsum(
            "bqhd,bkhd->bhqk", grad_block, value_block, preferred_element_type=jnp.float32
        )
        row_dot = jnp.sum(probs_full * probs_grad, axis=-1, keepdims=True)
        scores_grad = (probs_full * (probs_grad - row_dot)).astype(jnp.bfloat16)
        query_grads.append(
            jnp.einsum(
                "bhqk,bkhd->bqhd", scores_grad, key_block, preferred_element_type=jnp.float32
            )
            * score_scale
        )
        pad_rows = ((0, 0), (0, length - key_stop), (0, 0), (0, 0))
        keys_grad = keys_grad + jnp.pad(
            jnp.einsum(
                "bhqk,bqhd->bkhd", scores_grad, query_block, preferred_element_type=jnp.float32
            )
            * score_scale,
            pad_rows,
        )
        values_grad = values_grad + jnp.pad(
            jnp.einsum(
                "bhqk,bqhd->bkhd", probs_low, grad_block, preferred_element_type=jnp.float32
            ),
            pad_rows,
        )
    return (
        jnp.concatenate(query_grads, axis=1),
        keys_grad,
        values_grad,
        jnp.concatenate(outputs, axis=1),
    )


def shards(
    tokens,
    cotangent,
    corpus_ids,
    corpus_weights,
    qkv_weight,
    qkv_bias,
    out_weight,
    out_bias,
    up_weight,
    up_bias,
    down_weight,
    down_bias,
    norm_gains,
    norm_biases,
):
    shard_rows = tokens.shape[0]
    group_rows = shard_rows * lax.axis_size("narrow")
    seq_count = corpus_ids.shape[0]
    length = group_rows // seq_count
    block_rows = min(512, length)
    inner = qkv_weight.shape[2]
    first_row = lax.axis_index("narrow") * shard_rows
    cos_table, sine_table = rotary_tables(length, HEAD)
    layer_in = tokens.astype(jnp.float32)
    normed_first, inverse_first = norm_stats(layer_in)
    low_first = (normed_first * norm_gains[0] + norm_biases[0]).astype(jnp.bfloat16)
    gathered_first = lax.all_gather(low_first, "narrow", axis=0, tiled=True)
    query, key_rows, values = project_qkv(
        gathered_first, qkv_weight, qkv_bias, cos_table, sine_table, seq_count, length
    )
    attn_heads, totals = attend_forward(query, key_rows, values, block_rows)
    attn_low = attn_heads.reshape(group_rows, inner).astype(jnp.bfloat16)
    pre_attn = (
        lax.psum_scatter(
            jnp.dot(attn_low, out_weight, preferred_element_type=jnp.float32).astype(jnp.bfloat16),
            "narrow",
            scatter_dimension=0,
            tiled=True,
        ).astype(jnp.float32)
        + out_bias
    )
    normed_second, inverse_second = norm_stats(pre_attn)
    residual = layer_in + normed_second * norm_gains[1] + norm_biases[1]
    normed_third, inverse_third = norm_stats(residual)
    low_third = (normed_third * norm_gains[2] + norm_biases[2]).astype(jnp.bfloat16)
    gathered_third = lax.all_gather(low_third, "narrow", axis=0, tiled=True)
    hidden = jnp.dot(gathered_third, up_weight, preferred_element_type=jnp.float32) + up_bias
    act_low = gelu_value(hidden).astype(jnp.bfloat16)
    pre_mlp = (
        lax.psum_scatter(
            jnp.dot(act_low, down_weight, preferred_element_type=jnp.float32).astype(jnp.bfloat16),
            "narrow",
            scatter_dimension=0,
            tiled=True,
        ).astype(jnp.float32)
        + down_bias
    )
    normed_fourth, inverse_fourth = norm_stats(pre_mlp)
    final_sum = residual + normed_fourth * norm_gains[3] + norm_biases[3]
    layer_out = final_sum.astype(jnp.bfloat16)
    row_sequence = (first_row + jnp.arange(shard_rows, dtype=jnp.int32)) // length
    row_corpus = jnp.sum(
        jnp.where(
            row_sequence[:, None] == jnp.arange(seq_count, dtype=jnp.int32)[None, :],
            corpus_ids[None, :],
            0,
        ),
        axis=1,
    )
    row_weight = jnp.sum(
        jnp.where(
            row_corpus[:, None] == jnp.arange(corpus_weights.shape[0], dtype=jnp.int32)[None, :],
            corpus_weights[None, :],
            0.0,
        ),
        axis=1,
    )
    upstream = cotangent.astype(jnp.float32) * row_weight[:, None]
    mlp_grad = norm_back(normed_fourth, inverse_fourth, norm_gains[3], upstream).astype(
        jnp.bfloat16
    )
    mlp_full = lax.all_gather(mlp_grad, "narrow", axis=0, tiled=True)
    gathered_third = lax.all_gather(low_third, "narrow", axis=0, tiled=True)
    hidden = jnp.dot(gathered_third, up_weight, preferred_element_type=jnp.float32) + up_bias
    act_low = gelu_value(hidden).astype(jnp.bfloat16)
    down_wgrad = lax.dot_general(
        act_low, mlp_full, (((0,), (0,)), ((), ())), preferred_element_type=jnp.float32
    )
    act_grad = lax.dot_general(
        mlp_full, down_weight, (((1,), (1,)), ((), ())), preferred_element_type=jnp.float32
    )
    hidden_grad = (act_grad * gelu_slope(hidden)).astype(jnp.bfloat16)
    up_bgrad = jnp.sum(hidden_grad.astype(jnp.float32), axis=0)
    up_wgrad = lax.dot_general(
        gathered_third, hidden_grad, (((0,), (0,)), ((), ())), preferred_element_type=jnp.float32
    )
    rows_here = hidden_grad
    third_grad = lax.psum_scatter(
        lax.dot_general(
            rows_here, up_weight, (((1,), (1,)), ((), ())), preferred_element_type=jnp.float32
        ).astype(jnp.bfloat16),
        "narrow",
        scatter_dimension=0,
        tiled=True,
    ).astype(jnp.float32)
    residual_grad = upstream + norm_back(normed_third, inverse_third, norm_gains[2], third_grad)
    branch_grad = norm_back(normed_second, inverse_second, norm_gains[1], residual_grad).astype(
        jnp.bfloat16
    )
    branch_full = lax.all_gather(branch_grad, "narrow", axis=0, tiled=True)
    gathered_first = lax.all_gather(low_first, "narrow", axis=0, tiled=True)
    query, key_rows, values = project_qkv(
        gathered_first, qkv_weight, qkv_bias, cos_table, sine_table, seq_count, length
    )
    attn_grad = lax.dot_general(
        branch_full, out_weight, (((1,), (1,)), ((), ())), preferred_element_type=jnp.float32
    ).astype(jnp.bfloat16)
    attn_grad = attn_grad.reshape(query.shape)
    query_grad, keys_grad, values_grad, attn_again = attend_backward(
        query, key_rows, values, attn_grad, totals, block_rows
    )
    attn_again_low = attn_again.reshape(group_rows, inner).astype(jnp.bfloat16)
    out_wgrad = lax.dot_general(
        attn_again_low, branch_full, (((0,), (0,)), ((), ())), preferred_element_type=jnp.float32
    )
    qkv_grad = jnp.stack(
        [
            rotate_back(query_grad, cos_table, sine_table),
            rotate_back(keys_grad, cos_table, sine_table),
            values_grad,
        ]
    )
    qkv_grad = qkv_grad.reshape(3, group_rows, inner).astype(jnp.bfloat16)
    qkv_bgrad = jnp.sum(qkv_grad.astype(jnp.float32), axis=1)
    qkv_wgrad = jnp.einsum(
        "sd,tse->tde", gathered_first, qkv_grad, preferred_element_type=jnp.float32
    )
    rows_here = qkv_grad
    first_grad = lax.psum_scatter(
        jnp.einsum("tse,tde->sd", rows_here, qkv_weight, preferred_element_type=jnp.float32).astype(
            jnp.bfloat16
        ),
        "narrow",
        scatter_dimension=0,
        tiled=True,
    ).astype(jnp.float32)
    input_grad = (
        residual_grad + norm_back(normed_first, inverse_first, norm_gains[0], first_grad)
    ).astype(jnp.bfloat16)
    gain_local = jnp.stack(
        [
            jnp.sum(first_grad * normed_first, axis=0),
            jnp.sum(residual_grad * normed_second, axis=0),
            jnp.sum(third_grad * normed_third, axis=0),
            jnp.sum(upstream * normed_fourth, axis=0),
        ]
    )
    bias_local = jnp.stack(
        [
            jnp.sum(first_grad, axis=0),
            jnp.sum(residual_grad, axis=0),
            jnp.sum(third_grad, axis=0),
            jnp.sum(upstream, axis=0),
        ]
    )
    out_blocal = jnp.sum(branch_grad.astype(jnp.float32), axis=0)
    down_blocal = jnp.sum(mlp_grad.astype(jnp.float32), axis=0)
    weight_sums = (
        lax.psum(qkv_wgrad.astype(jnp.bfloat16), "wide").astype(jnp.float32),
        lax.psum(qkv_bgrad.astype(jnp.bfloat16), "wide").astype(jnp.float32),
        lax.psum(out_wgrad.astype(jnp.bfloat16), "wide").astype(jnp.float32),
        lax.psum(up_wgrad.astype(jnp.bfloat16), "wide").astype(jnp.float32),
        lax.psum(up_bgrad.astype(jnp.bfloat16), "wide").astype(jnp.float32),
        lax.psum(down_wgrad.astype(jnp.bfloat16), "wide").astype(jnp.float32),
    )
    small_sums = lax.psum((gain_local, bias_local, out_blocal, down_blocal), ("wide", "narrow"))
    return (
        layer_out,
        input_grad,
        weight_sums[0],
        weight_sums[1],
        weight_sums[2],
        small_sums[2],
        weight_sums[3],
        weight_sums[4],
        weight_sums[5],
        small_sums[3],
        small_sums[0],
        small_sums[1],
    )


def solution(mesh):
    return jax.shard_map(
        shards,
        mesh=mesh,
        in_specs=(
            P(("wide", "narrow"), None),
            P(("wide", "narrow"), None),
            P("wide"),
            P(),
            P(None, None, "narrow"),
            P(None, "narrow"),
            P("narrow", None),
            P(),
            P(None, "narrow"),
            P("narrow"),
            P("narrow", None),
            P(),
            P(),
            P(),
        ),
        out_specs=(
            P(("wide", "narrow"), None),
            P(("wide", "narrow"), None),
            P(None, None, "narrow"),
            P(None, "narrow"),
            P("narrow", None),
            P(),
            P(None, "narrow"),
            P("narrow"),
            P("narrow", None),
            P(),
            P(),
            P(),
        ),
        check_vma=False,
    )
```

profile of v0, /device:TPU:0, one launch (start us, length us, event | category | flops | bytes accessed | tf_op | source)
XLA Modules:
  0.0 1568.4 jit_solution(3756451614995006625)
XLA Ops:
  12.2 2.6 fusion.36
  19.2 123.0 %all-gather.5.cloned.1.call-done = bf16[4096,1024]{1,0:T(8,128)(2,1)} async-done(((bf16[512,1024]{1,0:T(8,128)(2,1)}), bf16[4096,1024]{1,0:T(8,128)(2,1)}) %all-gather.5.cloned.1.call-update) | async-done | bytes 8388624 | tf_op jit(solution)/shard_map/all_gather | solution.py:207
  142.2 7.1 add_bitcast_fusion
  152.8 5.0 reshape.328
  157.7 5.9 copy.76
  163.6 5.6 reshape.330
  169.2 5.6 reshape.329
  174.8 9.8 fusion.123
  184.6 6.4 copy.124
  191.0 6.4 copy.125
  197.4 10.1 fusion.122
  207.6 6.4 copy.126
  214.0 6.4 copy.127
  220.4 3.0 subtract_convert_fusion.2
  235.9 3.7 exponential_reduce_fusion.1
  240.4 3.6 fusion.73
  244.0 3.2 fusion
  247.2 4.3 exponential_reduce_fusion
  253.0 4.4 fusion.74
  259.0 5.6 convolution_convert_fusion.2
  264.7 145.7 %reduce-scatter.5.cloned.1.call-done = bf16[512,1024]{1,0:T(8,128)(2,1)} async-done(((bf16[4096,1024]{1,0:T(8,128)(2,1)}), bf16[512,1024]{1,0:T(8,128)(2,1)}) %reduce-scatter.5.cloned.1.call-update) | async-done | bytes 1048592 | tf_op jit(solution)/shard_map/reduce_scatter | solution.py:214
  416.7 3.1 add_convert_fusion.1
  419.9 123.7 %all-gather.7.cloned.1.call-done = bf16[4096,1024]{1,0:T(8,128)(2,1)} async-done(((bf16[512,1024]{1,0:T(8,128)(2,1)}), bf16[4096,1024]{1,0:T(8,128)(2,1)}) %all-gather.7.cloned.1.call-update) | async-done | bytes 8388624 | tf_op jit(solution)/shard_map/all_gather | solution.py:226
  543.6 10.3 multiply_convert_fusion.3
  555.9 6.6 convolution_convert_fusion.1
  563.3 145.0 %reduce-scatter.7.cloned.1.call-done = bf16[512,1024]{1,0:T(8,128)(2,1)} async-done(((bf16[4096,1024]{1,0:T(8,128)(2,1)}), bf16[512,1024]{1,0:T(8,128)(2,1)}) %reduce-scatter.7.cloned.1.call-update) | async-done | bytes 1048592 | tf_op jit(solution)/shard_map/reduce_scatter | solution.py:230
  711.7 3.3 multiply_reduce_fusion.4
  717.6 123.7 %all-gather.9.cloned.1.call-done = bf16[4096,1024]{1,0:T(8,128)(2,1)} async-done(((bf16[512,1024]{1,0:T(8,128)(2,1)}), bf16[4096,1024]{1,0:T(8,128)(2,1)}) %all-gather.9.cloned.1.call-update) | async-done | bytes 8388624 | tf_op jit(solution)/shard_map/all_gather | solution.py:262
  841.3 12.4 fusion.127
  855.6 7.2 convolution_convert_fusion
  862.9 145.7 %reduce-scatter.9.cloned.1.call-done = bf16[512,1024]{1,0:T(8,128)(2,1)} async-done(((bf16[4096,1024]{1,0:T(8,128)(2,1)}), bf16[512,1024]{1,0:T(8,128)(2,1)}) %reduce-scatter.9.cloned.1.call-update) | async-done | bytes 1048592 | tf_op jit(solution)/shard_map/reduce_scatter | solution.py:278
  1008.7 4.4 fusion.48
  1013.0 2.6 multiply_reduce_fusion.5
  1017.6 10.3 convolution_convert_fusion.4
  1027.8 8.3 convolution_convert_fusion.5
  1036.1 105.1 %all-gather.11.cloned.1.call-done = bf16[4096,1024]{1,0:T(8,128)(2,1)} async-done(((bf16[512,1024]{1,0:T(8,128)(2,1)}), bf16[4096,1024]{1,0:T(8,128)(2,1)}) %all-gather.11.cloned.1.call-update) | async-done | bytes 8388624 | tf_op jit(solution)/shard_map/all_gather | solution.py:290
  1141.2 5.7 convolution_convert_fusion.3
  1148.8 3.5 fusion.124
  1152.6 4.3 convolution_bitcast_fusion.3
  1164.9 5.8 convolution_bitcast_fusion.2
  1170.7 6.3 multiply_reduce_fusion.2
  1184.9 7.7 convolution_bitcast_fusion.1
  1192.6 10.0 multiply_reduce_fusion.1
  1202.6 6.8 multiply_convert_fusion.1
  1211.8 2.8 fusion.66
  1215.9 12.8 multiply_reduce_fusion
  1228.7 8.5 fusion.29
  1237.2 3.7 copy.112
  1240.9 3.9 reshape.327
  1244.8 12.6 multiply_convert_fusion
  1257.5 2.7 fusion.67
  1264.6 3.7 copy.111
  1268.3 4.7 reshape.326
  1274.4 3.7 copy.110
  1278.1 4.8 reshape.325
  1286.0 6.5 convolution_convert_fusion.6
  1292.6 4.3 fusion.63
  1297.0 9.0 bitcast_convert_fusion
  1308.5 6.6 all-reduce.7
  1316.3 47.6 %all-reduce.11.cloned.1.call-done = (bf16[3,1024,128]{1,2,0:T(8,128)(2,1)}, bf16[128,1024]{1,0:T(8,128)(2,1)}, bf16[1024,512]{1,0:T(8,128)(2,1)}, bf16[512,1024]{1,0:T(8,128)(2,1)}) async-done(((bf16[3,1024,128]{1,2,0:T(8,128)(2,1)}, bf16[128,1024]{1,0:T(8,128)(2,1)}, bf16[1024,512]{1,0:T(8,128)(2,1)}, bf16[512,1024]{1,0:T(8,128)(2,1)}), (bf16[3,1024,128]{1,2,0:T(8,128)(2,1)}, bf16[128,1024]{1,0:T(8,128)(2,1)}, ...) | async-done | bytes 3145744 | tf_op jit(solution)/shard_map/psum | solution.py:349
  1368.3 2.9 convert_element_type.190
  1372.8 142.3 %reduce-scatter.11.cloned.1.call-done = bf16[512,1024]{1,0:T(8,128)(2,1)} async-done(((bf16[4096,1024]{1,0:T(8,128)(2,1)}), bf16[512,1024]{1,0:T(8,128)(2,1)}) %reduce-scatter.11.cloned.1.call-update) | async-done | bytes 1048592 | tf_op jit(solution)/shard_map/reduce_scatter | solution.py:319
  1517.4 40.4 %all-reduce.6 = (f32[1024]{0:T(1024)}, f32[1024]{0:T(1024)}, f32[4,1024]{1,0:T(4,128)}, f32[4,1024]{1,0:T(4,128)}) all-reduce(f32[1024]{0:T(1024)S(1)} %get-tuple-element.76, f32[1024]{0:T(1024)S(1)} %copy-done.64, f32[4,1024]{1,0:T(4,128)S(1)} %pad_maximum_fusion.9, ...), channel_id=1, replica_groups=mesh['wide'=4,'narrow'=8] {'wide','narrow'}, use_global_device_ids=true, to_apply=%region_39.40 | all-reduce | flops 10240 | bytes 81920 | tf_op jit(solution)/shard_map/psum | solution.py:356
  1557.8 3.6 fusion.40
  (282 shorter events, 90.0 us)
Async XLA Ops:
  7.2 536.4 %copy-start = (bf16[1024,512]{1,0:T(8,128)(2,1)S(1)}, bf16[1024,512]{1,0:T(8,128)(2,1)}, u32[]{:S(2)}) copy-start(bf16[1024,512]{1,0:T(8,128)(2,1)} %param.22) | copy-start | bytes 3145732
  7.2 135.0 %copy-start.72 = (f32[3,128]{1,0:T(4,128)S(1)}, f32[3,128]{1,0:T(4,128)}, u32[]{:S(2)}) copy-start(f32[3,128]{1,0:T(4,128)} %param.19) | copy-start | bytes 4612
  7.2 135.0 %all-gather.5.cloned.1.call-start = ((), (), s32[]{:S(2)}) async-start(), calls=%async_computation.4 | async-start | bytes 9437184 | tf_op jit(solution)/shard_map/all_gather | solution.py:207
  8.8 140.6 %copy-start.60 = (f32[512]{0:T(512)}, f32[512]{0:T(512)S(1)}, u32[]{:S(2)}) copy-start(f32[512]{0:T(512)S(1)} %broadcast_multiply_fusion.11) | copy-start | bytes 6148
  10.4 139.0 %copy-start.62 = (f32[512]{0:T(512)}, f32[512]{0:T(512)S(1)}, u32[]{:S(2)}) copy-start(f32[512]{0:T(512)S(1)} %add_rsqrt_fusion.3) | copy-start | bytes 6148
  11.3 6.7 copy-start.58
  14.9 395.5 %reduce-scatter.5.cloned.1.call-start = ((), (), s32[]{:S(2)}) async-start(), calls=%async_computation.5 | async-start | bytes 9437184 | tf_op jit(solution)/shard_map/reduce_scatter | solution.py:214
  16.2 214.7 %copy-start.22 = (pred[512,1024]{1,0:T(8,128)(4,1)}, pred[512,1024]{1,0:T(8,128)(4,1)S(1)}, u32[]{:S(2)}) copy-start(pred[512,1024]{1,0:T(8,128)(4,1)S(1)} %iota_compare_fusion.2) | copy-start | bytes 1572868
  18.5 221.1 %copy-start.13 = (pred[512,1536]{1,0:T(8,128)(4,1)}, pred[512,1536]{1,0:T(8,128)(4,1)S(1)}, u32[]{:S(2)}) copy-start(pred[512,1536]{1,0:T(8,128)(4,1)S(1)} %iota_compare_fusion.1) | copy-start | bytes 2359300
  19.2 232.4 %copy-start.9 = (pred[512,2048]{1,0:T(8,128)(4,1)}, pred[512,2048]{1,0:T(8,128)(4,1)S(1)}, u32[]{:S(2)}) copy-start(pred[512,2048]{1,0:T(8,128)(4,1)S(1)} %iota_compare_fusion) | copy-start | bytes 3145732
  223.4 9.9 copy-start.16
  223.4 9.9 copy-start.18
  223.4 20.6 %copy-start.24 = (bf16[2,2048,2,32]{1,3,2,0:T(8,128)(2,1)}, bf16[2,2048,2,32]{1,3,2,0:T(8,128)(2,1)S(1)}, u32[]{:S(2)}) copy-start(bf16[2,2048,2,32]{1,3,2,0:T(8,128)(2,1)S(1)} %get-tuple-element.89) | copy-start | bytes 1572868
  223.4 20.6 %copy-start.28 = (bf16[2,2048,2,32]{1,3,2,0:T(8,128)(2,1)}, bf16[2,2048,2,32]{1,3,2,0:T(8,128)(2,1)S(1)}, u32[]{:S(2)}) copy-start(bf16[2,2048,2,32]{1,3,2,0:T(8,128)(2,1)S(1)} %get-tuple-element.90) | copy-start | bytes 1572868
  223.5 20.5 %copy-start.53 = (bf16[2,512,2,64]{1,3,2,0:T(8,128)(2,1)}, bf16[2,512,2,64]{1,3,2,0:T(8,128)(2,1)S(1)}, u32[]{:S(2)}) copy-start(bf16[2,512,2,64]{1,3,2,0:T(8,128)(2,1)S(1)} %get-tuple-element.132) | copy-start | bytes 786436
  224.5 5.2 copy-start.6
  235.9 4.5 copy-start.3
  247.2 5.7 copy-start.2
  259.0 5.6 copy-start.20
  264.6 145.8 %copy-start.56 = (f32[1024]{0:T(1024)S(1)}, f32[1024]{0:T(1024)}, u32[]{:S(2)}) copy-start(f32[1024]{0:T(1024)} %param.21) | copy-start | bytes 12292
  264.6 149.1 %copy-start.4 = (bf16[512,1024]{1,0:T(8,128)(2,1)S(1)}, bf16[512,1024]{1,0:T(8,128)(2,1)}, u32[]{:S(2)}) copy-start(bf16[512,1024]{1,0:T(8,128)(2,1)} %param.14) | copy-start | bytes 3145732
  264.6 278.9 %all-gather.7.cloned.1.call-start = ((), (), s32[]{:S(2)}) async-start(), calls=%async_computation.6 | async-start | bytes 9437184 | tf_op jit(solution)/shard_map/all_gather | solution.py:226
  410.4 5.3 copy-start.8
  413.7 129.9 %copy-start.73 = (f32[512]{0:T(512)S(1)}, f32[512]{0:T(512)}, u32[]{:S(2)}) copy-start(f32[512]{0:T(512)} %param.23) | copy-start | bytes 6148
  419.8 288.5 %reduce-scatter.7.cloned.1.call-start = ((), (), s32[]{:S(2)}) async-start(), calls=%async_computation.7 | async-start | bytes 9437184 | tf_op jit(solution)/shard_map/reduce_scatter | solution.py:230
  543.6 12.3 copy-start.70
  562.5 145.8 %copy-start.57 = (f32[1024]{0:T(1024)S(1)}, f32[1024]{0:T(1024)}, u32[]{:S(2)}) copy-start(f32[1024]{0:T(1024)} %param.25) | copy-start | bytes 12292
  562.5 278.7 %all-gather.9.cloned.1.call-start = ((), (), s32[]{:S(2)}) async-start(), calls=%async_computation.8 | async-start | bytes 9437184 | tf_op jit(solution)/shard_map/all_gather | solution.py:262
  708.4 6.7 copy-start.11
  708.4 6.7 copy-start.38
  717.5 291.1 %reduce-scatter.9.cloned.1.call-start = ((), (), s32[]{:S(2)}) async-start(), calls=%async_computation.9 | async-start | bytes 9437184 | tf_op jit(solution)/shard_map/reduce_scatter | solution.py:278
  862.8 145.8 %copy-start.12 = (bf16[512,1024]{1,0:T(8,128)(2,1)S(1)}, bf16[512,1024]{1,0:T(8,128)(2,1)}, u32[]{:S(2)}) copy-start(bf16[512,1024]{1,0:T(8,128)(2,1)} %reduce-scatter.7.cloned.1.call-done) | copy-start | bytes 3145732
  862.9 278.3 %all-gather.11.cloned.1.call-start = ((), (), s32[]{:S(2)}) async-start(), calls=%async_computation.10 | async-start | bytes 9437184 | tf_op jit(solution)/shard_map/all_gather | solution.py:290
  1008.6 4.4 copy-start.39
  1008.6 4.4 copy-start.42
  1017.5 346.4 %all-reduce.11.cloned.1.call-start = ((), (), s32[]{:S(2)}) async-start(), calls=%async_computation.12 | async-start | bytes 6291456 | tf_op jit(solution)/shard_map/psum | solution.py:349
  1017.5 10.3 copy-start.77
  1146.9 5.7 copy-start.37
  1164.9 5.8 copy-start.33
  1164.9 12.1 slice-start.3
  1170.7 6.3 slice-start.4
  1184.8 7.7 copy-start.34
  1184.8 17.7 %slice-start = ((s8[12582912]{0:T(1024)(128)(4,1)}), s8[4194304]{0:T(1024)(128)(4,1)S(1)}, s32[]{:S(2)}) async-start(s8[12582912]{0:T(1024)(128)(4,1)} %bitcast.120), calls=%async_computation.13 | async-start | bytes 8388608
  1184.8 17.7 %slice-start.1 = ((s8[12582912]{0:T(1024)(128)(4,1)}), s8[4194304]{0:T(1024)(128)(4,1)S(1)}, s32[]{:S(2)}) async-start(s8[12582912]{0:T(1024)(128)(4,1)} %bitcast.120), calls=%async_computation.14 | async-start | bytes 8388608
  1192.6 10.0 slice-start.2
  1215.9 12.8 copy-start.74
  1215.9 12.8 copy-start.78
  1215.9 12.8 copy-start.79
  1244.8 12.6 copy-start.27
  1244.8 12.6 copy-start.31
  1278.1 7.9 copy-start.21
  1282.9 9.6 slice-start.5
  1286.0 6.5 copy-start.41
  1286.0 6.5 slice-start.6
  1292.6 4.4 copy-start.71
  1296.9 218.2 %reduce-scatter.11.cloned.1.call-start = ((), (), s32[]{:S(2)}) async-start(), calls=%async_computation.11 | async-start | bytes 9437184 | tf_op jit(solution)/shard_map/reduce_scatter | solution.py:319
  1363.9 7.3 copy-start.52
  1365.8 149.3 %copy-start.59 = (f32[1,1024]{1,0:T(1,128)S(1)}, f32[1,1024]{1,0:T(1,128)}, u32[]{:S(2)}) copy-start(f32[1,1024]{1,0:T(1,128)} %copy-done.58) | copy-start | bytes 12292
  1365.8 149.3 %copy-start.61 = (f32[512]{0:T(512)S(1)}, f32[512]{0:T(512)}, u32[]{:S(2)}) copy-start(f32[512]{0:T(512)} %copy-done.60) | copy-start | bytes 6148
  1365.8 149.3 %copy-start.63 = (f32[512]{0:T(512)S(1)}, f32[512]{0:T(512)}, u32[]{:S(2)}) copy-start(f32[512]{0:T(512)} %copy-done.62) | copy-start | bytes 6148
  1368.3 149.0 %copy-start.66 = (f32[1024]{0:T(1024)S(1)}, f32[1024]{0:T(1024)}, u32[]{:S(2)}) copy-start(f32[1024]{0:T(1024)} %get-tuple-element.52) | copy-start | bytes 12292
  1368.3 149.1 %copy-start.65 = (f32[1024]{0:T(1024)S(1)}, f32[1024]{0:T(1024)}, u32[]{:S(2)}) copy-start(f32[1024]{0:T(1024)} %get-tuple-element.61) | copy-start | bytes 12292
  1368.3 149.1 %copy-start.64 = (f32[1024]{0:T(1024)S(1)}, f32[1024]{0:T(1024)}, u32[]{:S(2)}) copy-start(f32[1024]{0:T(1024)} %get-tuple-element.74) | copy-start | bytes 12292
  1371.2 190.2 %copy-start.1 = (bf16[1024,512]{1,0:T(8,128)(2,1)S(1)}, bf16[1024,512]{1,0:T(8,128)(2,1)}, u32[]{:S(2)}) copy-start(bf16[1024,512]{1,0:T(8,128)(2,1)} %param.22) | copy-start | bytes 3145732
  (32 other events, 76.1 us)
Sparse Core Ops, SparseCore 0:
  15.0 127.1 all-gather.4
  264.7 145.6 reduce-scatter.4
  419.9 123.5 all-gather.6
  562.7 145.6 reduce-scatter.6
  717.7 123.5 all-gather.8
  863.0 145.6 reduce-scatter.8
  1017.6 123.5 all-gather.10
  1297.0 66.8 all-reduce.10
  1367.5 147.5 reduce-scatter.10
where the time goes:
time: 1580 us; the launch traced here: 1570 us
  waiting for transfers between devices  1100 us (70%)
  matrix products  187 us (12%)
  local copies, waits for them, and re-layouts  122 us (8%)
  other arithmetic  94.2 us (6%)
  blocking collectives  47 us (3%)
    reduce_scatter x1, waiting for transfers between devices, shards(): lax.psum_scatter(jnp.dot(attn_low, out_weight, preferred_element_type=jnp...  146 us
    reduce_scatter x1, waiting for transfers between devices, shards(): lax.psum_scatter(lax.dot_general(rows_here, up_weight, (((1,), (1,)), (()...  146 us
    reduce_scatter x1, waiting for transfers between devices, shards(): lax.psum_scatter(jnp.dot(act_low, down_weight, preferred_element_type=jnp...  145 us
    reduce_scatter x1, waiting for transfers between devices, shards(): lax.psum_scatter(jnp.einsum('tse,tde->sd', rows_here, qkv_weight, preferr...  142 us
    all_gather x1, waiting for transfers between devices, shards(): mlp_full = lax.all_gather(mlp_grad, 'narrow', axis=0, tiled=True)  124 us
    all_gather x1, waiting for transfers between devices, shards(): gathered_third = lax.all_gather(low_third, 'narrow', axis=0, tiled=True)  124 us
    all_gather x1, waiting for transfers between devices, shards(): gathered_first = lax.all_gather(low_first, 'narrow', axis=0, tiled=True)  123 us
    all_gather x1, waiting for transfers between devices, shards(): branch_full = lax.all_gather(branch_grad, 'narrow', axis=0, tiled=True)  105 us
  transfers between devices with their start and end apart: 9, of which 9 were waited for; matrix products, arithmetic and copies ran while one was open for 3% of the time, Pallas kernels for 0%

commit v1 on v0

--- a/solution.py
+++ b/solution.py
@@ -131,7 +131,6 @@
     keys_grad = jnp.zeros(key_rows.shape, jnp.float32)
     values_grad = jnp.zeros(values.shape, jnp.float32)
     query_grads = []
-    outputs = []
     for block_number, block_start in enumerate(range(0, length, block_rows)):
         key_stop = block_start + block_rows
         scores, query_block, key_block = block_scores(query, key_rows, block_start, block_rows)
@@ -139,11 +138,6 @@
         grad_block = attn_grad[:, block_start:key_stop]
         probs_full = jnp.exp(scores - totals[block_number])
         probs_low = probs_full.astype(jnp.bfloat16)
-        outputs.append(
-            jnp.einsum(
-                "bhqk,bkhd->bqhd", probs_low, value_block, preferred_element_type=jnp.float32
-            )
-        )
         probs_grad = jnp.einsum(
             "bqhd,bkhd->bhqk", grad_block, value_block, preferred_element_type=jnp.float32
         )
@@ -173,7 +167,6 @@
         jnp.concatenate(query_grads, axis=1),
         keys_grad,
         values_grad,
-        jnp.concatenate(outputs, axis=1),
     )
 
 
@@ -210,15 +203,9 @@
     )
     attn_heads, totals = attend_forward(query, key_rows, values, block_rows)
     attn_low = attn_heads.reshape(group_rows, inner).astype(jnp.bfloat16)
-    pre_attn = (
-        lax.psum_scatter(
-            jnp.dot(attn_low, out_weight, preferred_element_type=jnp.float32).astype(jnp.bfloat16),
-            "narrow",
-            scatter_dimension=0,
-            tiled=True,
-        ).astype(jnp.float32)
-        + out_bias
-    )
+    attn_rows = lax.all_to_all(attn_low, "narrow", 0, 1, tiled=True)
+    out_full = lax.all_gather(out_weight, "narrow", axis=0, tiled=True)
+    pre_attn = jnp.dot(attn_rows, out_full, preferred_element_type=jnp.float32) + out_bias
     normed_second, inverse_second = norm_stats(pre_attn)
     residual = layer_in + normed_second * norm_gains[1] + norm_biases[1]
     normed_third, inverse_third = norm_stats(residual)
@@ -287,21 +274,23 @@
     branch_grad = norm_back(normed_second, inverse_second, norm_gains[1], residual_grad).astype(
         jnp.bfloat16
     )
-    branch_full = lax.all_gather(branch_grad, "narrow", axis=0, tiled=True)
     gathered_first = lax.all_gather(low_first, "narrow", axis=0, tiled=True)
     query, key_rows, values = project_qkv(
         gathered_first, qkv_weight, qkv_bias, cos_table, sine_table, seq_count, length
     )
-    attn_grad = lax.dot_general(
-        branch_full, out_weight, (((1,), (1,)), ((), ())), preferred_element_type=jnp.float32
+    attn_grad_rows = lax.dot_general(
+        branch_grad, out_full, (((1,), (1,)), ((), ())), preferred_element_type=jnp.float32
     ).astype(jnp.bfloat16)
+    attn_grad = lax.all_to_all(attn_grad_rows, "narrow", 1, 0, tiled=True)
     attn_grad = attn_grad.reshape(query.shape)
-    query_grad, keys_grad, values_grad, attn_again = attend_backward(
+    query_grad, keys_grad, values_grad = attend_backward(
         query, key_rows, values, attn_grad, totals, block_rows
     )
-    attn_again_low = attn_again.reshape(group_rows, inner).astype(jnp.bfloat16)
-    out_wgrad = lax.dot_general(
-        attn_again_low, branch_full, (((0,), (0,)), ((), ())), preferred_element_type=jnp.float32
+    out_wgrad_rows = lax.dot_general(
+        attn_rows, branch_grad, (((0,), (0,)), ((), ())), preferred_element_type=jnp.float32
+    )
+    out_wgrad = lax.psum_scatter(
+        out_wgrad_rows.astype(jnp.bfloat16), "narrow", scatter_dimension=0, tiled=True
     )
     qkv_grad = jnp.stack(
         [
@@ -348,7 +337,7 @@
     weight_sums = (
         lax.psum(qkv_wgrad.astype(jnp.bfloat16), "wide").astype(jnp.float32),
         lax.psum(qkv_bgrad.astype(jnp.bfloat16), "wide").astype(jnp.float32),
-        lax.psum(out_wgrad.astype(jnp.bfloat16), "wide").astype(jnp.float32),
+        lax.psum(out_wgrad, "wide").astype(jnp.float32),
         lax.psum(up_wgrad.astype(jnp.bfloat16), "wide").astype(jnp.float32),
         lax.psum(up_bgrad.astype(jnp.bfloat16), "wide").astype(jnp.float32),
         lax.psum(down_wgrad.astype(jnp.bfloat16), "wide").astype(jnp.float32),

time: 1580 us -> 1340 us (0.85)
  waiting for transfers between devices: 1100 us -> 881 us
  matrix products: 187 us -> 168 us
    reduce_scatter x1, waiting for transfers between devices: 146 us -> 0.01 us  [shards(): lax.psum_scatter(out_wgrad_rows.astype(jnp.bfloat16), 'narrow', scatter_d...]
    all_gather x1, waiting for transfers between devices: 105 us -> 0.02 us  [shards(): out_full = lax.all_gather(out_weight, 'narrow', axis=0, tiled=True)]
    all_to_all x0 -> x2, waiting for transfers between devices: none -> 29.6 us  [the longest x1 25.4 us: shards(): attn_rows = lax.all_to_all(attn_low, 'narrow', 0, 1, tiled=True)]
    unnamed x186 -> x199, local copies, waits for them, and re-layouts: 43.6 us -> 42.6 us
  transfers between devices with their start and end apart: 9 -> 11, of which waited for: 9 -> 9; matrix products, arithmetic and copies ran while one was open for 3% -> 21% of each run, Pallas kernels for 0% -> 0%
where the time goes in v1:
time: 1340 us; the launch traced here: 1330 us
  waiting for transfers between devices  881 us (66%)
  matrix products  168 us (13%)
  local copies, waits for them, and re-layouts  110 us (8%)
  other arithmetic  96.1 us (7%)
  blocking collectives  46.8 us (3%)
  between operations  15.4 us (1%)
    reduce_scatter x1, waiting for transfers between devices, shards(): lax.psum_scatter(lax.dot_general(rows_here, up_weight, (((1,), (1,)), (()...  146 us
    reduce_scatter x1, waiting for transfers between devices, shards(): lax.psum_scatter(jnp.dot(act_low, down_weight, preferred_element_type=jnp...  145 us
    reduce_scatter x1, waiting for transfers between devices, shards(): lax.psum_scatter(jnp.einsum('tse,tde->sd', rows_here, qkv_weight, preferr...  142 us
    all_gather x1, waiting for transfers between devices, shards(): mlp_full = lax.all_gather(mlp_grad, 'narrow', axis=0, tiled=True)  124 us
    all_gather x1, waiting for transfers between devices, shards(): gathered_third = lax.all_gather(low_third, 'narrow', axis=0, tiled=True)  123 us
    all_gather x1, waiting for transfers between devices, shards(): gathered_first = lax.all_gather(low_first, 'narrow', axis=0, tiled=True)  122 us
    psum x1, waiting for transfers between devices, shards(): lax.psum(qkv_wgrad.astype(jnp.bfloat16), 'wide').astype(jnp.float32)  48.5 us
    unnamed x199, local copies, waits for them, and re-layouts  42.6 us
  transfers between devices with their start and end apart: 11, of which 9 were waited for; matrix products, arithmetic and copies ran while one was open for 21% of the time, Pallas kernels for 0%

profile of v1, /device:TPU:0, one launch (start us, length us, event | category | flops | bytes accessed | tf_op | source)
XLA Modules:
  0.0 1326.1 jit_solution(15998260063616890509)
XLA Ops:
  12.3 2.6 fusion.36
  19.9 122.4 %all-gather.5.cloned.1.call-done = bf16[4096,1024]{1,0:T(8,128)(2,1)} async-done(((bf16[512,1024]{1,0:T(8,128)(2,1)}), bf16[4096,1024]{1,0:T(8,128)(2,1)}) %all-gather.5.cloned.1.call-update) | async-done | bytes 8388624 | tf_op jit(solution)/shard_map/all_gather | solution.py:200
  142.3 7.1 add_bitcast_fusion
  152.9 5.0 reshape.335
  157.9 5.9 copy.105
  163.7 5.6 reshape.337
  169.3 5.7 reshape.336
  175.0 9.7 fusion.130
  184.7 6.4 copy.154
  191.2 6.4 copy.155
  197.6 10.1 fusion.129
  207.7 6.4 copy.156
  214.1 6.4 copy.157
  220.5 3.0 subtract_convert_fusion.2
  230.6 2.5 fusion.1
  233.1 3.5 exponential_reduce_fusion.1
  236.7 3.2 fusion.68
  239.9 4.3 fusion.70
  244.2 3.2 fusion
  247.5 4.3 exponential_reduce_fusion
  253.4 4.2 fusion.71
  260.9 3.6 all-to-all-start
  264.5 25.4 %all-to-all-done = bf16[8,512,128]{1,2,0:T(8,128)(2,1)S(1)} async-done(((bf16[8,512,128]{1,2,0:T(8,128)(2,1)}), bf16[8,512,128]{1,2,0:T(8,128)(2,1)S(1)}, u32[]{:S(2)}, u32[]{:S(2)}) %all-to-all-start) | async-done | bytes 1048608 | tf_op jit(solution)/shard_map/all_to_all | solution.py:206
  290.9 3.3 add_reduce_fusion
  299.3 123.4 %all-gather.9.cloned.1.call-done = bf16[4096,1024]{1,0:T(8,128)(2,1)} async-done(((bf16[512,1024]{1,0:T(8,128)(2,1)}), bf16[4096,1024]{1,0:T(8,128)(2,1)}) %all-gather.9.cloned.1.call-update) | async-done | bytes 8388624 | tf_op jit(solution)/shard_map/all_gather | solution.py:213
  422.7 10.0 multiply_convert_fusion.3
  434.7 6.7 convolution_convert_fusion.1
  442.1 145.0 %reduce-scatter.5.cloned.1.call-done = bf16[512,1024]{1,0:T(8,128)(2,1)} async-done(((bf16[4096,1024]{1,0:T(8,128)(2,1)}), bf16[512,1024]{1,0:T(8,128)(2,1)}) %reduce-scatter.5.cloned.1.call-update) | async-done | bytes 1048592 | tf_op jit(solution)/shard_map/reduce_scatter | solution.py:217
  590.5 3.3 multiply_reduce_fusion.4
  593.9 2.5 convert_reduce_fusion.3
  596.4 123.7 %all-gather.11.cloned.1.call-done = bf16[4096,1024]{1,0:T(8,128)(2,1)} async-done(((bf16[512,1024]{1,0:T(8,128)(2,1)}), bf16[4096,1024]{1,0:T(8,128)(2,1)}) %all-gather.11.cloned.1.call-update) | async-done | bytes 8388624 | tf_op jit(solution)/shard_map/all_gather | solution.py:249
  720.1 12.4 fusion.134
  734.5 7.3 convolution_convert_fusion
  741.8 145.8 %reduce-scatter.7.cloned.1.call-done = bf16[512,1024]{1,0:T(8,128)(2,1)} async-done(((bf16[4096,1024]{1,0:T(8,128)(2,1)}), bf16[512,1024]{1,0:T(8,128)(2,1)}) %reduce-scatter.7.cloned.1.call-update) | async-done | bytes 1048592 | tf_op jit(solution)/shard_map/reduce_scatter | solution.py:265
  887.6 4.7 fusion.48
  892.4 3.0 multiply_reduce_fusion.5
  900.4 3.7 all-to-all-start.1
  904.2 10.3 convolution_convert_fusion.3
  914.4 8.2 convolution_convert_fusion.4
  922.7 2.6 convolution_convert_fusion.2
  925.7 4.3 all-to-all-done.1
  932.5 4.6 convolution_bitcast_fusion.3
  942.8 3.4 convolution_bitcast_fusion.2
  946.2 5.5 multiply_reduce_fusion.2
  951.6 5.0 multiply_convert_fusion.2
  960.8 4.7 convolution_bitcast_fusion.1
  965.5 7.4 multiply_reduce_fusion.1
  972.9 10.6 multiply_convert_fusion.1
  985.9 2.8 fusion.63
  988.7 11.6 multiply_reduce_fusion
  1000.4 7.5 fusion.29
  1007.8 4.5 copy.144
  1014.2 12.4 multiply_convert_fusion
  1026.6 2.7 fusion.64
  1047.2 6.9 fusion.60
  1054.1 8.8 bitcast_convert_fusion
  1062.9 2.5 reduce_sum.374
  1065.4 6.5 all-reduce.7
  1073.1 48.5 %all-reduce.11.cloned.1.call-done = (bf16[3,1024,128]{1,2,0:T(8,128)(2,1)}, bf16[128,1024]{1,0:T(8,128)(2,1)}, bf16[1024,512]{1,0:T(8,128)(2,1)}, bf16[512,1024]{1,0:T(8,128)(2,1)}) async-done(((bf16[3,1024,128]{1,2,0:T(8,128)(2,1)}, bf16[128,1024]{1,0:T(8,128)(2,1)}, bf16[1024,512]{1,0:T(8,128)(2,1)}, bf16[512,1024]{1,0:T(8,128)(2,1)}), (bf16[3,1024,128]{1,2,0:T(8,128)(2,1)}, bf16[128,1024]{1,0:T(8,128)(2,1)}, ...) | async-done | bytes 3145744 | tf_op jit(solution)/shard_map/psum | solution.py:338
  1123.4 2.6 copy.135
  1126.1 2.9 convert_element_type.182
  1130.6 142.2 %reduce-scatter.9.cloned.1.call-done = bf16[512,1024]{1,0:T(8,128)(2,1)} async-done(((bf16[4096,1024]{1,0:T(8,128)(2,1)}), bf16[512,1024]{1,0:T(8,128)(2,1)}) %reduce-scatter.9.cloned.1.call-update) | async-done | bytes 1048592 | tf_op jit(solution)/shard_map/reduce_scatter | solution.py:308
  1275.2 40.3 %all-reduce.6 = (f32[1024]{0:T(1024)}, f32[1024]{0:T(1024)}, f32[4,1024]{1,0:T(4,128)}, f32[4,1024]{1,0:T(4,128)}) all-reduce(f32[1024]{0:T(1024)S(1)} %copy-done.74, f32[1024]{0:T(1024)S(1)} %copy-done.70, f32[4,1024]{1,0:T(4,128)S(1)} %pad_maximum_fusion.9, ...), channel_id=1, replica_groups=mesh['wide'=4,'narrow'=8] {'wide','narrow'}, use_global_device_ids=true, to_apply=%region_39.40 | all-reduce | flops 10240 | bytes 81920 | tf_op jit(solution)/shard_map/psum | solution.py:345
  1315.5 3.6 fusion.40
  (302 shorter events, 86.1 us)
Async XLA Ops:
  7.2 415.5 %copy-start = (bf16[1024,512]{1,0:T(8,128)(2,1)S(1)}, bf16[1024,512]{1,0:T(8,128)(2,1)}, u32[]{:S(2)}) copy-start(bf16[1024,512]{1,0:T(8,128)(2,1)} %param.22) | copy-start | bytes 3145732
  7.2 135.1 %copy-start.82 = (f32[3,128]{1,0:T(4,128)S(1)}, f32[3,128]{1,0:T(4,128)}, u32[]{:S(2)}) copy-start(f32[3,128]{1,0:T(4,128)} %param.19) | copy-start | bytes 4612
  7.2 135.1 %all-gather.5.cloned.1.call-start = ((), (), s32[]{:S(2)}) async-start(), calls=%async_computation.6 | async-start | bytes 9437184 | tf_op jit(solution)/shard_map/all_gather | solution.py:200
  14.9 249.6 %all-gather.7.cloned.1.call-start = ((), (), s32[]{:S(2)}) async-start(), calls=%async_computation.7 | async-start | bytes 2359296 | tf_op jit(solution)/shard_map/all_gather | solution.py:207
  16.9 219.8 %copy-start.21 = (pred[512,1024]{1,0:T(8,128)(4,1)}, pred[512,1024]{1,0:T(8,128)(4,1)S(1)}, u32[]{:S(2)}) copy-start(pred[512,1024]{1,0:T(8,128)(4,1)S(1)} %iota_compare_fusion.2) | copy-start | bytes 1572868
  19.2 220.7 %copy-start.14 = (pred[512,1536]{1,0:T(8,128)(4,1)}, pred[512,1536]{1,0:T(8,128)(4,1)S(1)}, u32[]{:S(2)}) copy-start(pred[512,1536]{1,0:T(8,128)(4,1)S(1)} %iota_compare_fusion.1) | copy-start | bytes 2359300
  19.9 233.1 %copy-start.10 = (pred[512,2048]{1,0:T(8,128)(4,1)}, pred[512,2048]{1,0:T(8,128)(4,1)S(1)}, u32[]{:S(2)}) copy-start(pred[512,2048]{1,0:T(8,128)(4,1)S(1)} %iota_compare_fusion) | copy-start | bytes 3145732
  223.5 7.0 copy-start.16
  223.5 7.0 copy-start.18
  223.5 20.7 %copy-start.23 = (bf16[2,2048,2,32]{1,3,2,0:T(8,128)(2,1)}, bf16[2,2048,2,32]{1,3,2,0:T(8,128)(2,1)S(1)}, u32[]{:S(2)}) copy-start(bf16[2,2048,2,32]{1,3,2,0:T(8,128)(2,1)S(1)} %get-tuple-element.103) | copy-start | bytes 1572868
  223.6 20.7 %copy-start.27 = (bf16[2,2048,2,32]{1,3,2,0:T(8,128)(2,1)}, bf16[2,2048,2,32]{1,3,2,0:T(8,128)(2,1)S(1)}, u32[]{:S(2)}) copy-start(bf16[2,2048,2,32]{1,3,2,0:T(8,128)(2,1)S(1)} %get-tuple-element.104) | copy-start | bytes 1572868
  225.4 26.4 %copy-start.5 = (f32[2,2,512,512]{2,3,1,0:T(8,128)}, f32[2,2,512,512]{2,3,1,0:T(8,128)S(1)}, u32[]{:S(2)}) copy-start(f32[2,2,512,512]{2,3,1,0:T(8,128)S(1)} %get-tuple-element.133) | copy-start | bytes 12582916
  228.1 8.6 copy-start.4
  233.1 6.8 copy-start.3
  247.4 6.0 copy-start.2
  257.8 33.1 %copy-start.61 = (f32[1024]{0:T(1024)S(1)}, f32[1024]{0:T(1024)}, u32[]{:S(2)}) copy-start(f32[1024]{0:T(1024)} %param.21) | copy-start | bytes 12292
  260.9 29.0 %all-to-all-start = ((bf16[8,512,128]{1,2,0:T(8,128)(2,1)}), bf16[8,512,128]{1,2,0:T(8,128)(2,1)S(1)}, u32[]{:S(2)}, u32[]{:S(2)}) async-start(bf16[8,512,128]{1,2,0:T(8,128)(2,1)} %copy.117), calls=%async_computation | async-start | bytes 2097152 | tf_op jit(solution)/shard_map/all_to_all | solution.py:206
  264.5 158.2 %all-gather.9.cloned.1.call-start = ((), (), s32[]{:S(2)}) async-start(), calls=%async_computation.8 | async-start | bytes 9437184 | tf_op jit(solution)/shard_map/all_gather | solution.py:213
  296.5 126.1 %copy-start.83 = (f32[512]{0:T(512)S(1)}, f32[512]{0:T(512)}, u32[]{:S(2)}) copy-start(f32[512]{0:T(512)} %param.23) | copy-start | bytes 6148
  299.3 287.9 %reduce-scatter.5.cloned.1.call-start = ((), (), s32[]{:S(2)}) async-start(), calls=%async_computation.9 | async-start | bytes 9437184 | tf_op jit(solution)/shard_map/reduce_scatter | solution.py:217
  422.7 12.0 copy-start.80
  441.3 145.8 %copy-start.62 = (f32[1024]{0:T(1024)S(1)}, f32[1024]{0:T(1024)}, u32[]{:S(2)}) copy-start(f32[1024]{0:T(1024)} %param.25) | copy-start | bytes 12292
  441.3 278.7 %all-gather.11.cloned.1.call-start = ((), (), s32[]{:S(2)}) async-start(), calls=%async_computation.10 | async-start | bytes 9437184 | tf_op jit(solution)/shard_map/all_gather | solution.py:249
  587.2 6.7 copy-start.12
  587.2 6.7 copy-start.36
  596.4 291.3 %reduce-scatter.7.cloned.1.call-start = ((), (), s32[]{:S(2)}) async-start(), calls=%async_computation.11 | async-start | bytes 9437184 | tf_op jit(solution)/shard_map/reduce_scatter | solution.py:265
  741.8 145.8 %copy-start.13 = (bf16[512,1024]{1,0:T(8,128)(2,1)S(1)}, bf16[512,1024]{1,0:T(8,128)(2,1)}, u32[]{:S(2)}) copy-start(bf16[512,1024]{1,0:T(8,128)(2,1)} %reduce-scatter.5.cloned.1.call-done) | copy-start | bytes 3145732
  887.6 4.7 copy-start.37
  887.6 4.7 copy-start.43
  900.4 29.6 %all-to-all-start.1 = ((bf16[512,8,128]{0,2,1:T(8,128)(2,1)}), bf16[512,8,128]{0,2,1:T(8,128)(2,1)S(1)}, u32[]{:S(2)}, u32[]{:S(2)}) async-start(bf16[512,8,128]{0,2,1:T(8,128)(2,1)} %bitcast.16), calls=%async_computation.3 | async-start | bytes 2097152 | tf_op jit(solution)/shard_map/all_to_all | solution.py:284
  904.1 150.0 %reduce-scatter.11.cloned.1.call-start = ((), (), s32[]{:S(2)}) async-start(), calls=%async_computation.13 | async-start | bytes 2359296 | tf_op jit(solution)/shard_map/reduce_scatter | solution.py:292
  904.1 10.3 copy-start.86
  914.4 8.3 copy-start.41
  914.4 8.3 copy-start.58
  925.3 196.3 %all-reduce.11.cloned.1.call-start = ((), (), s32[]{:S(2)}) async-start(), calls=%async_computation.14 | async-start | bytes 6291456 | tf_op jit(solution)/shard_map/psum | solution.py:338
  931.0 6.0 copy-start.6
  931.0 6.0 copy-start.33
  937.1 5.7 slice-start.7
  951.6 5.1 copy-start.24
  951.6 5.1 copy-start.28
  951.6 9.1 slice-start.4
  951.6 9.1 slice-start.5
  972.9 15.8 %slice-start = ((s8[16777216]{0:T(1024)(128)(4,1)}), s8[4194304]{0:T(1024)(128)(4,1)S(1)}, s32[]{:S(2)}) async-start(s8[16777216]{0:T(1024)(128)(4,1)} %bitcast.116), calls=%async_computation.15 | async-start | bytes 8388608
  972.9 15.8 %slice-start.1 = ((s8[16777216]{0:T(1024)(128)(4,1)}), s8[4194304]{0:T(1024)(128)(4,1)S(1)}, s32[]{:S(2)}) async-start(s8[16777216]{0:T(1024)(128)(4,1)} %bitcast.116), calls=%async_computation.16 | async-start | bytes 8388608
  972.9 15.8 %slice-start.2 = ((s8[16777216]{0:T(1024)(128)(4,1)}), s8[4194304]{0:T(1024)(128)(4,1)S(1)}, s32[]{:S(2)}) async-start(s8[16777216]{0:T(1024)(128)(4,1)} %bitcast.116), calls=%async_computation.17 | async-start | bytes 8388608
  983.5 5.2 slice-start.3
  1007.8 6.3 copy-start.69
  1014.2 12.4 copy-start.26
  1014.2 12.4 copy-start.30
  1047.2 7.0 copy-start.81
  1054.1 218.7 %reduce-scatter.9.cloned.1.call-start = ((), (), s32[]{:S(2)}) async-start(), calls=%async_computation.12 | async-start | bytes 9437184 | tf_op jit(solution)/shard_map/reduce_scatter | solution.py:308
  1121.6 7.4 copy-start.54
  1123.4 149.3 %copy-start.9 = (bf16[512,1024]{1,0:T(8,128)(2,1)S(1)}, bf16[512,1024]{1,0:T(8,128)(2,1)}, u32[]{:S(2)}) copy-start(bf16[512,1024]{1,0:T(8,128)(2,1)} %param.14) | copy-start | bytes 3145732
  1123.4 149.3 %copy-start.64 = (f32[1,1024]{1,0:T(1,128)S(1)}, f32[1,1024]{1,0:T(1,128)}, u32[]{:S(2)}) copy-start(f32[1,1024]{1,0:T(1,128)} %copy-done.63) | copy-start | bytes 12292
  1123.4 149.3 %copy-start.66 = (f32[512]{0:T(512)S(1)}, f32[512]{0:T(512)}, u32[]{:S(2)}) copy-start(f32[512]{0:T(512)} %copy-done.65) | copy-start | bytes 6148
  1123.4 149.3 %copy-start.68 = (f32[512]{0:T(512)S(1)}, f32[512]{0:T(512)}, u32[]{:S(2)}) copy-start(f32[512]{0:T(512)} %copy-done.67) | copy-start | bytes 6148
  1126.1 148.9 %copy-start.72 = (f32[1024]{0:T(1024)S(1)}, f32[1024]{0:T(1024)}, u32[]{:S(2)}) copy-start(f32[1024]{0:T(1024)} %get-tuple-element.64) | copy-start | bytes 12292
  1126.1 149.0 %copy-start.73 = (f32[1024]{0:T(1024)S(1)}, f32[1024]{0:T(1024)}, u32[]{:S(2)}) copy-start(f32[1024]{0:T(1024)} %get-tuple-element.60) | copy-start | bytes 12292
  1126.1 149.0 %copy-start.76 = (f32[1024]{0:T(1024)S(1)}, f32[1024]{0:T(1024)}, u32[]{:S(2)}) copy-start(f32[1024]{0:T(1024)} %get-tuple-element.62) | copy-start | bytes 12292
  1126.1 149.0 %copy-start.71 = (f32[1024]{0:T(1024)S(1)}, f32[1024]{0:T(1024)}, u32[]{:S(2)}) copy-start(f32[1024]{0:T(1024)} %get-tuple-element.73) | copy-start | bytes 12292
  1126.1 149.0 %copy-start.75 = (f32[1024]{0:T(1024)S(1)}, f32[1024]{0:T(1024)}, u32[]{:S(2)}) copy-start(f32[1024]{0:T(1024)} %get-tuple-element.75) | copy-start | bytes 12292
  1126.1 149.0 %copy-start.70 = (f32[1024]{0:T(1024)S(1)}, f32[1024]{0:T(1024)}, u32[]{:S(2)}) copy-start(f32[1024]{0:T(1024)} %get-tuple-element.86) | copy-start | bytes 12292
  1126.1 149.0 %copy-start.74 = (f32[1024]{0:T(1024)S(1)}, f32[1024]{0:T(1024)}, u32[]{:S(2)}) copy-start(f32[1024]{0:T(1024)} %get-tuple-element.88) | copy-start | bytes 12292
  1129.0 190.1 %copy-start.1 = (bf16[1024,512]{1,0:T(8,128)(2,1)S(1)}, bf16[1024,512]{1,0:T(8,128)(2,1)}, u32[]{:S(2)}) copy-start(bf16[1024,512]{1,0:T(8,128)(2,1)} %param.22) | copy-start | bytes 3145732
  (43 other events, 108.2 us)
Sparse Core Ops, SparseCore 0:
  15.0 127.2 all-gather.4
  144.4 47.2 all-gather.6
  299.4 123.2 all-gather.8
  441.5 145.6 reduce-scatter.4
  596.5 123.5 all-gather.10
  742.0 145.6 reduce-scatter.6
  925.4 69.7 reduce-scatter.10
  1054.2 67.3 all-reduce.10
  1125.2 147.5 reduce-scatter.8

commit v2 on v1

--- a/solution.py
+++ b/solution.py
@@ -170,6 +170,41 @@
     )
 
 
+def swap_cores(block):
+    count = lax.axis_size("wide")
+    return lax.ppermute(block, "wide", [(index, index ^ 1) for index in range(count)])
+
+
+def gather_halves(shard, core, split_axis, gather_axis):
+    half = shard.shape[split_axis] // 2
+    mine = lax.dynamic_slice_in_dim(shard, core * half, half, axis=split_axis)
+    gathered = lax.all_gather(mine, "narrow", axis=gather_axis, tiled=True)
+    partner = swap_cores(gathered)
+    first = jnp.where(core == 0, gathered, partner)
+    second = jnp.where(core == 0, partner, gathered)
+    return jnp.concatenate([first, second], axis=split_axis)
+
+
+def reduce_halves(rows, core, split_axis, scatter_axis):
+    half = rows.shape[split_axis] // 2
+    mine = lax.dynamic_slice_in_dim(rows, core * half, half, axis=split_axis)
+    other = lax.dynamic_slice_in_dim(rows, (1 - core) * half, half, axis=split_axis)
+    chip_sum = mine + swap_cores(other.astype(jnp.bfloat16)).astype(jnp.float32)
+    part = lax.psum_scatter(
+        chip_sum.astype(jnp.bfloat16), "narrow", scatter_dimension=scatter_axis, tiled=True
+    )
+    empty = jnp.zeros_like(part)
+    return jnp.stack(
+        [jnp.where(core == 0, part, empty), jnp.where(core == 0, empty, part)], axis=split_axis
+    )
+
+
+def merge_slots(slots, split_axis):
+    shape = list(slots.shape)
+    shape[split_axis : split_axis + 2] = [shape[split_axis] * shape[split_axis + 1]]
+    return slots.reshape(shape)
+
+
 def shards(
     tokens,
     cotangent,
@@ -210,18 +245,13 @@
     residual = layer_in + normed_second * norm_gains[1] + norm_biases[1]
     normed_third, inverse_third = norm_stats(residual)
     low_third = (normed_third * norm_gains[2] + norm_biases[2]).astype(jnp.bfloat16)
-    gathered_third = lax.all_gather(low_third, "narrow", axis=0, tiled=True)
-    hidden = jnp.dot(gathered_third, up_weight, preferred_element_type=jnp.float32) + up_bias
+    core = lax.axis_index("wide") % 2
+    up_full = gather_halves(up_weight, core, 0, 1)
+    down_full = gather_halves(down_weight, core, 1, 0)
+    up_bias_full = lax.all_gather(up_bias, "narrow", axis=0, tiled=True)
+    hidden = jnp.dot(low_third, up_full, preferred_element_type=jnp.float32) + up_bias_full
     act_low = gelu_value(hidden).astype(jnp.bfloat16)
-    pre_mlp = (
-        lax.psum_scatter(
-            jnp.dot(act_low, down_weight, preferred_element_type=jnp.float32).astype(jnp.bfloat16),
-            "narrow",
-            scatter_dimension=0,
-            tiled=True,
-        ).astype(jnp.float32)
-        + down_bias
-    )
+    pre_mlp = jnp.dot(act_low, down_full, preferred_element_type=jnp.float32) + down_bias
     normed_fourth, inverse_fourth = norm_stats(pre_mlp)
     final_sum = residual + normed_fourth * norm_gains[3] + norm_biases[3]
     layer_out = final_sum.astype(jnp.bfloat16)
@@ -246,30 +276,22 @@
     mlp_grad = norm_back(normed_fourth, inverse_fourth, norm_gains[3], upstream).astype(
         jnp.bfloat16
     )
-    mlp_full = lax.all_gather(mlp_grad, "narrow", axis=0, tiled=True)
-    gathered_third = lax.all_gather(low_third, "narrow", axis=0, tiled=True)
-    hidden = jnp.dot(gathered_third, up_weight, preferred_element_type=jnp.float32) + up_bias
-    act_low = gelu_value(hidden).astype(jnp.bfloat16)
-    down_wgrad = lax.dot_general(
-        act_low, mlp_full, (((0,), (0,)), ((), ())), preferred_element_type=jnp.float32
+    down_wgrad_rows = lax.dot_general(
+        act_low, mlp_grad, (((0,), (0,)), ((), ())), preferred_element_type=jnp.float32
     )
     act_grad = lax.dot_general(
-        mlp_full, down_weight, (((1,), (1,)), ((), ())), preferred_element_type=jnp.float32
+        mlp_grad, down_full, (((1,), (1,)), ((), ())), preferred_element_type=jnp.float32
     )
     hidden_grad = (act_grad * gelu_slope(hidden)).astype(jnp.bfloat16)
-    up_bgrad = jnp.sum(hidden_grad.astype(jnp.float32), axis=0)
-    up_wgrad = lax.dot_general(
-        gathered_third, hidden_grad, (((0,), (0,)), ((), ())), preferred_element_type=jnp.float32
-    )
-    rows_here = hidden_grad
-    third_grad = lax.psum_scatter(
-        lax.dot_general(
-            rows_here, up_weight, (((1,), (1,)), ((), ())), preferred_element_type=jnp.float32
-        ).astype(jnp.bfloat16),
-        "narrow",
-        scatter_dimension=0,
-        tiled=True,
-    ).astype(jnp.float32)
+    up_bgrad_rows = jnp.sum(hidden_grad.astype(jnp.float32), axis=0)
+    up_wgrad_rows = lax.dot_general(
+        low_third, hidden_grad, (((0,), (0,)), ((), ())), preferred_element_type=jnp.float32
+    )
+    third_grad = lax.dot_general(
+        hidden_grad, up_full, (((1,), (1,)), ((), ())), preferred_element_type=jnp.float32
+    )
+    up_slots = reduce_halves(up_wgrad_rows, core, 0, 1)
+    down_slots = reduce_halves(down_wgrad_rows, core, 1, 0)
     residual_grad = upstream + norm_back(normed_third, inverse_third, norm_gains[2], third_grad)
     branch_grad = norm_back(normed_second, inverse_second, norm_gains[1], residual_grad).astype(
         jnp.bfloat16
@@ -338,11 +360,17 @@
         lax.psum(qkv_wgrad.astype(jnp.bfloat16), "wide").astype(jnp.float32),
         lax.psum(qkv_bgrad.astype(jnp.bfloat16), "wide").astype(jnp.float32),
         lax.psum(out_wgrad, "wide").astype(jnp.float32),
-        lax.psum(up_wgrad.astype(jnp.bfloat16), "wide").astype(jnp.float32),
-        lax.psum(up_bgrad.astype(jnp.bfloat16), "wide").astype(jnp.float32),
-        lax.psum(down_wgrad.astype(jnp.bfloat16), "wide").astype(jnp.float32),
-    )
-    small_sums = lax.psum((gain_local, bias_local, out_blocal, down_blocal), ("wide", "narrow"))
+        lax.psum(up_slots, "wide").astype(jnp.float32),
+        None,
+        lax.psum(down_slots, "wide").astype(jnp.float32),
+    )
+    small_sums = lax.psum(
+        (gain_local, bias_local, out_blocal, down_blocal, up_bgrad_rows), ("wide", "narrow")
+    )
+    units = up_bias.shape[0]
+    up_bgrad = lax.dynamic_slice_in_dim(small_sums[4], lax.axis_index("narrow") * units, units)
+    up_wgrad = merge_slots(weight_sums[3], 0)
+    down_wgrad = merge_slots(weight_sums[5], 1)
     return (
         layer_out,
         input_grad,
@@ -350,9 +378,9 @@
         weight_sums[1],
         weight_sums[2],
         small_sums[2],
-        weight_sums[3],
-        weight_sums[4],
-        weight_sums[5],
+        up_wgrad,
+        up_bgrad,
+        down_wgrad,
         small_sums[3],
         small_sums[0],
         small_sums[1],

time: 1340 us -> 1050 us (0.78)
  waiting for transfers between devices: 881 us -> 538 us
  blocking collectives: 46.8 us -> 75.6 us
  other arithmetic: 96.1 us -> 110 us
    reduce_scatter x2, waiting for transfers between devices: 291 us -> 0.01 us  [reduce_halves(): lax.psum_scatter(chip_sum.astype(jnp.bfloat16), 'narrow', scatter_dimensi...]
    all_gather x2, waiting for transfers between devices: 247 us -> 114 us  [gather_halves(): gathered = lax.all_gather(mine, 'narrow', axis=gather_axis, tiled=True)]
    all_to_all x1, waiting for transfers between devices: 4.27 us -> 40.5 us  [shards(): attn_grad = lax.all_to_all(attn_grad_rows, 'narrow', 1, 0, tiled=True)]
    reduce_scatter x1, waiting for transfers between devices: 0.01 us -> 34.8 us  [shards(): lax.psum_scatter(out_wgrad_rows.astype(jnp.bfloat16), 'narrow', scatter_d...]
    all_gather x0 -> x1, blocking collectives: none -> 28.6 us  [shards(): up_bias_full = lax.all_gather(up_bias, 'narrow', axis=0, tiled=True)]
    ppermute x0 -> x4, waiting for transfers between devices: none -> 14.3 us  [swap_cores(): lax.ppermute(block, 'wide', [(index, index ^ 1) for index in range(count)])]
    unnamed x199 -> x214, local copies, waits for them, and re-layouts: 42.6 us -> 49.2 us
  transfers between devices with their start and end apart: 11 -> 15, of which waited for: 9 -> 10; matrix products, arithmetic and copies ran while one was open for 21% -> 33% of each run, Pallas kernels for 0% -> 0%
where the time goes in v2:
time: 1050 us; the launch traced here: 1040 us
  waiting for transfers between devices  538 us (51%)
  matrix products  174 us (17%)
  local copies, waits for them, and re-layouts  121 us (12%)
  other arithmetic  110 us (10%)
  blocking collectives  75.6 us (7%)
  between operations  15.8 us (2%)
    reduce_scatter x1, waiting for transfers between devices, shards(): lax.psum_scatter(jnp.einsum('tse,tde->sd', rows_here, qkv_weight, preferr...  142 us
    all_gather x1, waiting for transfers between devices, shards(): gathered_first = lax.all_gather(low_first, 'narrow', axis=0, tiled=True)  125 us
    all_gather x2, waiting for transfers between devices, gather_halves(): gathered = lax.all_gather(mine, 'narrow', axis=gather_axis, tiled=True)  114 us
    psum x1, waiting for transfers between devices, shards(): lax.psum(qkv_wgrad.astype(jnp.bfloat16), 'wide').astype(jnp.float32)  52.5 us
    unnamed x214, local copies, waits for them, and re-layouts  49.2 us
    psum x1, blocking collectives, shards(): lax.psum((gain_local, bias_local, out_blocal, down_blocal, up_bgrad_rows)...  40.5 us
    all_to_all x1, waiting for transfers between devices, shards(): attn_grad = lax.all_to_all(attn_grad_rows, 'narrow', 1, 0, tiled=True)  40.5 us
    reduce_scatter x1, waiting for transfers between devices, shards(): lax.psum_scatter(out_wgrad_rows.astype(jnp.bfloat16), 'narrow', scatter_d...  34.8 us
  transfers between devices with their start and end apart: 15, of which 10 were waited for; matrix products, arithmetic and copies ran while one was open for 33% of the time, Pallas kernels for 0%

profile of v2, /device:TPU:0, one launch (start us, length us, event | category | flops | bytes accessed | tf_op | source)
XLA Modules:
  0.0 1041.8 jit_solution(4207119873639760609)
XLA Ops:
  16.2 28.6 %all-gather = f32[8,1,512]{2,1,0:T(1,128)S(1)} all-gather(f32[1,1,512]{2,1,0:T(1,128)S(1)} %bitcast.160), channel_id=1, replica_groups=mesh['wide'=4,'narrow'=8] {'narrow'}, dimensions={0}, use_global_device_ids=true | all-gather | bytes 18432 | tf_op jit(solution)/shard_map/all_gather | solution.py:251
  48.5 38.1 %all-gather.12.cloned.1.call-done = bf16[4096,512]{1,0:T(8,128)(2,1)} async-done(((bf16[512,512]{1,0:T(8,128)(2,1)}), bf16[4096,512]{1,0:T(8,128)(2,1)}) %all-gather.12.cloned.1.call-update) | async-done | bytes 4194320 | tf_op jit(solution)/shard_map/all_gather | solution.py:181
  86.5 75.8 %all-gather.10.cloned.1.call-done = bf16[512,4096]{1,0:T(8,128)(2,1)} async-done(((bf16[512,512]{1,0:T(8,128)(2,1)}), bf16[512,4096]{1,0:T(8,128)(2,1)}) %all-gather.10.cloned.1.call-update) | async-done | bytes 4194320 | tf_op jit(solution)/shard_map/all_gather | solution.py:181
  162.3 125.4 %all-gather.6.cloned.1.call-done = bf16[4096,1024]{1,0:T(8,128)(2,1)} async-done(((bf16[512,1024]{1,0:T(8,128)(2,1)}), bf16[4096,1024]{1,0:T(8,128)(2,1)}) %all-gather.6.cloned.1.call-update) | async-done | bytes 8388624 | tf_op jit(solution)/shard_map/all_gather | solution.py:235
  287.7 6.9 add_bitcast_fusion
  298.9 4.6 copy.109
  303.5 6.1 reshape.355
  309.6 5.6 reshape.354
  315.2 9.9 fusion.126
  325.2 6.4 copy.160
  331.6 6.4 copy.161
  338.0 9.7 fusion.125
  347.7 6.4 copy.162
  354.1 6.6 copy.163
  360.7 3.0 subtract_convert_fusion.2
  365.7 4.8 fusion.14
  374.3 3.7 exponential_reduce_fusion.1
  378.1 3.3 fusion
  381.4 4.5 exponential_reduce_fusion
  386.0 7.7 fusion.62
  393.7 4.6 exponential_reduce_fusion.2
  398.3 4.4 fusion.63
  402.8 5.6 fusion.60
  411.3 3.6 all-to-all-start
  414.9 6.5 broadcast_select_fusion.1
  421.4 5.2 broadcast_select_fusion.3
  426.6 13.7 %all-to-all-done = bf16[8,512,128]{1,2,0:T(8,128)(2,1)S(1)} async-done(((bf16[8,512,128]{1,2,0:T(8,128)(2,1)}), bf16[8,512,128]{1,2,0:T(8,128)(2,1)S(1)}, u32[]{:S(2)}, u32[]{:S(2)}) %all-to-all-start) | async-done | bytes 1048608 | tf_op jit(solution)/shard_map/all_to_all | solution.py:241
  441.2 3.3 add_reduce_fusion.1
  448.8 8.5 multiply_convert_fusion.3
  457.4 6.9 add_reduce_fusion
  466.4 2.8 convert_reduce_fusion.3
  470.2 4.7 fusion.130
  474.9 5.7 copy-done.35
  483.3 7.4 collective-permute-done.3
  490.7 6.8 add_convert_fusion
  497.6 11.8 %convert_reduce_fusion = (f32[4096]{0:T(1024)}, bf16[512,4096]{1,0:T(8,128)(2,1)S(1)}) fusion(f32[512,4096]{1,0:T(8,128)} %get-tuple-element.144, f32[4096]{0:T(1024)S(1)} %bitcast.155, bf16[512,1024]{1,0:T(8,128)(2,1)} %copy-done.58, bf16[4096,512]{1,0:T(8,128)(2,1)} %get-tuple-element.93, bf16[4096,512]{1,0:T(8,128)(2,1)} %get-tuple-element.92), kind=kOutput, calls=%fused_computation.29 | convolution fusion | flops 4339003392 | bytes 22052864 | tf_op jit(solution)/shard_map/dot_general | solution.py:282
  509.4 8.6 fusion.121
  518.0 4.1 dynamic-slice_convert_fusion.1
  522.5 6.9 collective-permute-done.2
  529.4 6.7 add_convert_fusion.1
  536.2 11.3 %multiply_reduce_fusion.5 = (f32[1024]{0:T(1024)}, f32[512]{0:T(512)S(1)}, f32[512]{0:T(512)S(1)}, f32[1024]{0:T(1024)}, f32[512,1024]{1,0:T(8,128)S(1)}) fusion(f32[512,1024]{1,0:T(8,128)} %copy-done.9, f32[512]{0:T(512)S(1)} %add_rsqrt_fusion.1, f32[512]{0:T(512)S(1)} %broadcast_multiply_fusion.9, f32[1024]{0:T(1024)S(1)} %bitcast.143, ...), kind=kOutput, calls=%fused_computation.94 | convolution fusion | flops 4316460032 | bytes 16797696 | tf_op jit(solution)/shard_map/dot_general | solution.py:290
  547.5 3.3 multiply_reduce_fusion.6
  555.8 3.6 all-to-all-start.1
  562.1 40.5 %all-to-all-done.1 = bf16[512,8,128]{0,2,1:T(8,128)(2,1)S(1)} async-done(((bf16[512,8,128]{0,2,1:T(8,128)(2,1)}), bf16[512,8,128]{0,2,1:T(8,128)(2,1)S(1)}, u32[]{:S(2)}, u32[]{:S(2)}) %all-to-all-start.1) | async-done | bytes 1048608 | tf_op jit(solution)/shard_map/all_to_all | solution.py:306
  605.0 4.4 convolution_bitcast_fusion.3
  615.2 3.4 convolution_bitcast_fusion.2
  618.6 5.4 multiply_reduce_fusion.2
  624.0 5.1 multiply_convert_fusion.2
  633.2 4.7 convolution_bitcast_fusion.1
  637.9 7.4 multiply_reduce_fusion.1
  645.3 10.7 %multiply_convert_fusion.1 = bf16[2,2,512,1536]{3,2,1,0:T(8,128)(2,1)S(1)} fusion(f32[2,2,512,1536]{3,2,1,0:T(8,128)} %get-tuple-element.151, f32[2,2,512,1536]{3,2,1,0:T(8,128)} %copy-done.3, f32[2,2,512]{2,1,0:T(2,128)S(1)} %get-tuple-element.150, f32[2,2,512]{2,1,0:T(2,128)S(1)} %copy-done.65, pred[512,1536]{1,0:T(8,128)(4,1)S(1)} %copy-done.15), kind=kLoop, calls=%fused_computation.7 | loop fusion | flops 18874368 | bytes 32260096 | tf_op jit(solution)/shard_map/convert_element_type | solution.py:145
  658.4 2.8 fusion.55
  661.3 11.6 %multiply_reduce_fusion = (f32[2,2,512]{2,1,0:T(2,128)}, f32[2,2,512,2048]{3,2,1,0:T(8,128)}) fusion(f32[2,2,512,2048]{3,2,1,0:T(8,128)S(1)} %bitcast.123, f32[2,2,512]{2,1,0:T(2,128)S(1)} %copy-done.67, pred[512,2048]{1,0:T(8,128)(4,1)S(1)} %copy-done.13, bf16[2,2048,2,64]{1,3,2,0:T(8,128)(2,1)} %copy-done.31, bf16[2,512,2,64]{1,0,3,2:T(2,128)(2,1)} %get-tuple-element.114), kind=kOutput, calls=%fused_computation.2 | convolution fusion | flops 557840384 | bytes 35930112 | tf_op jit(solution)/shard_map/bqhd,bkhd->bhqk/dot_general | solution.py:141
  672.9 7.5 fusion.29
  680.4 4.5 copy.150
  686.8 12.5 %multiply_convert_fusion = bf16[2,2,512,2048]{3,2,1,0:T(8,128)(2,1)S(1)} fusion(f32[2,2,512,2048]{3,2,1,0:T(8,128)} %get-tuple-element.149, f32[2,2,512,2048]{3,2,1,0:T(8,128)} %copy-done.2, f32[2,2,512]{2,1,0:T(2,128)S(1)} %copy-done.75, f32[2,2,512]{2,1,0:T(2,128)S(1)} %copy-done.67, pred[512,2048]{1,0:T(8,128)(4,1)S(1)} %copy-done.13), kind=kLoop, calls=%fused_computation.1 | loop fusion | flops 25165824 | bytes 43008000 | tf_op jit(solution)/shard_map/convert_element_type | solution.py:145
  719.2 6.8 fusion.52
  730.8 34.8 %reduce-scatter.7.cloned.1.call-done = bf16[128,1024]{1,0:T(8,128)(2,1)} async-done(((bf16[1024,1024]{1,0:T(8,128)(2,1)}), bf16[128,1024]{1,0:T(8,128)(2,1)}) %reduce-scatter.7.cloned.1.call-update) | async-done | bytes 262160 | tf_op jit(solution)/shard_map/reduce_scatter | solution.py:314
  765.6 8.8 bitcast_convert_fusion
  776.9 6.5 psum.71
  784.0 52.5 %all-reduce.10.cloned.1.call-done = (bf16[3,1024,128]{1,2,0:T(8,128)(2,1)}, bf16[512,1024]{0,1:T(8,128)(2,1)}, bf16[128,1024]{1,0:T(8,128)(2,1)}, bf16[1024,512]{1,0:T(8,128)(2,1)}) async-done(((bf16[3,1024,128]{1,2,0:T(8,128)(2,1)}, bf16[512,1024]{0,1:T(8,128)(2,1)}, bf16[128,1024]{1,0:T(8,128)(2,1)}, bf16[1024,512]{1,0:T(8,128)(2,1)}), (bf16[3,1024,128]{1,2,0:T(8,128)(2,1)}, bf16[512,1024]{0,1:T(8,128)(2,1)}, ...) | async-done | bytes 3145744 | tf_op jit(solution)/shard_map/psum | solution.py:360
  845.2 142.4 %reduce-scatter.5.cloned.1.call-done = bf16[512,1024]{1,0:T(8,128)(2,1)} async-done(((bf16[4096,1024]{1,0:T(8,128)(2,1)}), bf16[512,1024]{1,0:T(8,128)(2,1)}) %reduce-scatter.5.cloned.1.call-update) | async-done | bytes 1048592 | tf_op jit(solution)/shard_map/reduce_scatter | solution.py:330
  990.0 40.5 %all-reduce.6 = (f32[1024]{0:T(1024)}, f32[4096]{0:T(1024)S(1)}, f32[1024]{0:T(1024)}, f32[4,1024]{1,0:T(4,128)}, f32[4,1024]{1,0:T(4,128)}) all-reduce(f32[1024]{0:T(1024)S(1)} %copy-done.83, f32[4096]{0:T(1024)S(1)} %copy-done.80, f32[1024]{0:T(1024)S(1)} %copy-done.76, ...), channel_id=1, replica_groups=mesh['wide'=4,'narrow'=8] {'wide','narrow'}, use_global_device_ids=true, to_apply=%region_37.38 | all-reduce | flops 14336 | bytes 114688 | tf_op jit(solution)/shard_map/psum | solution.py:367
  1031.2 3.6 fusion.40
  (335 shorter events, 99.7 us)
Async XLA Ops:
  7.2 79.3 %all-gather.12.cloned.1.call-start = ((), (), s32[]{:S(2)}) async-start(), calls=%async_computation.9 | async-start | bytes 4718592 | tf_op jit(solution)/shard_map/all_gather | solution.py:181
  9.3 153.1 %all-gather.10.cloned.1.call-start = ((), (), s32[]{:S(2)}) async-start(), calls=%async_computation.8 | async-start | bytes 4718592 | tf_op jit(solution)/shard_map/all_gather | solution.py:181
  11.2 37.1 %copy-start.87 = (s32[2]{0:T(128)S(1)}, s32[2]{0:T(128)}, u32[]{:S(2)}) copy-start(s32[2]{0:T(128)} %param.16) | copy-start | bytes 28
  11.2 37.1 %copy-start.88 = (f32[8]{0:T(128)S(1)}, f32[8]{0:T(128)}, u32[]{:S(2)}) copy-start(f32[8]{0:T(128)} %param.17) | copy-start | bytes 100
  11.2 276.5 %copy-start.89 = (bf16[3,1024,128]{2,1,0:T(8,128)(2,1)S(1)}, bf16[3,1024,128]{2,1,0:T(8,128)(2,1)}, u32[]{:S(2)}) copy-start(bf16[3,1024,128]{2,1,0:T(8,128)(2,1)} %param.18) | copy-start | bytes 2359300
  11.3 276.5 %copy-start.91 = (f32[3,128]{1,0:T(4,128)S(1)}, f32[3,128]{1,0:T(4,128)}, u32[]{:S(2)}) copy-start(f32[3,128]{1,0:T(4,128)} %param.19) | copy-start | bytes 4612
  11.3 276.5 %all-gather.6.cloned.1.call-start = ((), (), s32[]{:S(2)}) async-start(), calls=%async_computation.6 | async-start | bytes 9437184 | tf_op jit(solution)/shard_map/all_gather | solution.py:235
  12.8 34.2 %copy-start.70 = (f32[512]{0:T(512)}, f32[512]{0:T(512)S(1)}, u32[]{:S(2)}) copy-start(f32[512]{0:T(512)S(1)} %broadcast_multiply_fusion.11) | copy-start | bytes 6148
  13.3 33.8 %copy-start.73 = (f32[512]{0:T(512)}, f32[512]{0:T(512)S(1)}, u32[]{:S(2)}) copy-start(f32[512]{0:T(512)S(1)} %add_rsqrt_fusion.3) | copy-start | bytes 6148
  13.3 33.8 %copy-start.68 = (f32[1,1024]{1,0:T(1,128)}, f32[1,1024]{1,0:T(1,128)S(1)}, u32[]{:S(2)}) copy-start(f32[1,1024]{1,0:T(1,128)S(1)} %get-tuple-element.125) | copy-start | bytes 12292
  14.8 411.8 %all-gather.8.cloned.1.call-start = ((), (), s32[]{:S(2)}) async-start(), calls=%async_computation.7 | async-start | bytes 2359296 | tf_op jit(solution)/shard_map/all_gather | solution.py:242
  45.2 357.6 %copy-start.21 = (pred[512,1024]{1,0:T(8,128)(4,1)}, pred[512,1024]{1,0:T(8,128)(4,1)S(1)}, u32[]{:S(2)}) copy-start(pred[512,1024]{1,0:T(8,128)(4,1)S(1)} %iota_compare_fusion.2) | copy-start | bytes 1572868
  47.6 338.4 %copy-start.14 = (pred[512,1536]{1,0:T(8,128)(4,1)}, pred[512,1536]{1,0:T(8,128)(4,1)S(1)}, u32[]{:S(2)}) copy-start(pred[512,1536]{1,0:T(8,128)(4,1)S(1)} %iota_compare_fusion.1) | copy-start | bytes 2359300
  48.3 350.1 %copy-start.12 = (pred[512,2048]{1,0:T(8,128)(4,1)}, pred[512,2048]{1,0:T(8,128)(4,1)S(1)}, u32[]{:S(2)}) copy-start(pred[512,2048]{1,0:T(8,128)(4,1)S(1)} %iota_compare_fusion) | copy-start | bytes 3145732
  86.5 328.4 %collective-permute-start.1 = (bf16[4096,512]{1,0:T(8,128)(2,1)}, bf16[4096,512]{1,0:T(8,128)(2,1)}, u32[]{:S(2)}, u32[]{:S(2)}) collective-permute-start(bf16[4096,512]{1,0:T(8,128)(2,1)} %all-gather.12.cloned.1.call-done), channel_id=1, source_target_pairs={{0,8},{8,0},{16,24},{24,16},{1,9},{9,1},{17,25},{25,17},{2,10},{10... | collective-permute-start | bytes 12582920 | tf_op jit(solution)/shard_map/ppermute | solution.py:175
  162.3 259.0 %collective-permute-start = (bf16[512,4096]{1,0:T(8,128)(2,1)}, bf16[512,4096]{1,0:T(8,128)(2,1)}, u32[]{:S(2)}, u32[]{:S(2)}) collective-permute-start(bf16[512,4096]{1,0:T(8,128)(2,1)} %all-gather.10.cloned.1.call-done), channel_id=1, source_target_pairs={{0,8},{8,0},{16,24},{24,16},{1,9},{9,1},{17,25},{25,17},{2,10},{10... | collective-permute-start | bytes 12582920 | tf_op jit(solution)/shard_map/ppermute | solution.py:175
  303.5 99.3 %copy-start.31 = (bf16[2,2048,2,64]{1,3,2,0:T(8,128)(2,1)}, bf16[2,2048,2,64]{1,3,2,0:T(8,128)(2,1)S(1)}, u32[]{:S(2)}) copy-start(bf16[2,2048,2,64]{1,3,2,0:T(8,128)(2,1)S(1)} %copy.109) | copy-start | bytes 3145732
  363.7 14.3 %copy-start.23 = (bf16[2,2048,2,32]{1,3,2,0:T(8,128)(2,1)}, bf16[2,2048,2,32]{1,3,2,0:T(8,128)(2,1)S(1)}, u32[]{:S(2)}) copy-start(bf16[2,2048,2,32]{1,3,2,0:T(8,128)(2,1)S(1)} %get-tuple-element.106) | copy-start | bytes 1572868
  363.8 14.3 %copy-start.27 = (bf16[2,2048,2,32]{1,3,2,0:T(8,128)(2,1)}, bf16[2,2048,2,32]{1,3,2,0:T(8,128)(2,1)S(1)}, u32[]{:S(2)}) copy-start(bf16[2,2048,2,32]{1,3,2,0:T(8,128)(2,1)S(1)} %get-tuple-element.107) | copy-start | bytes 1572868
  363.8 14.3 %copy-start.59 = (bf16[2,512,2,64]{1,3,2,0:T(8,128)(2,1)}, bf16[2,512,2,64]{1,3,2,0:T(8,128)(2,1)S(1)}, u32[]{:S(2)}) copy-start(bf16[2,512,2,64]{1,3,2,0:T(8,128)(2,1)S(1)} %get-tuple-element.158) | copy-start | bytes 786436
  364.8 8.3 copy-start.4
  381.4 16.9 %copy-start.2 = (f32[2,2,512,2048]{3,2,1,0:T(8,128)}, f32[2,2,512,2048]{3,2,1,0:T(8,128)S(1)}, u32[]{:S(2)}) copy-start(f32[2,2,512,2048]{3,2,1,0:T(8,128)S(1)} %get-tuple-element.134) | copy-start | bytes 50331652
  385.9 7.7 copy-start.64
  386.0 12.4 %copy-start.66 = (f32[2,2,512]{2,1,0:T(2,128)}, f32[2,2,512]{2,1,0:T(2,128)S(1)}, u32[]{:S(2)}) copy-start(f32[2,2,512]{2,1,0:T(2,128)S(1)} %log_add_fusion) | copy-start | bytes 24580
  411.3 29.0 %all-to-all-start = ((bf16[8,512,128]{1,2,0:T(8,128)(2,1)}), bf16[8,512,128]{1,2,0:T(8,128)(2,1)S(1)}, u32[]{:S(2)}, u32[]{:S(2)}) async-start(bf16[8,512,128]{1,2,0:T(8,128)(2,1)} %copy.121), calls=%async_computation | async-start | bytes 2097152 | tf_op jit(solution)/shard_map/all_to_all | solution.py:241
  414.8 311.2 %reduce-scatter.11.cloned.1.call-start = ((), (), s32[]{:S(2)}) async-start(), calls=%async_computation.13 | async-start | bytes 4718592 | tf_op jit(solution)/shard_map/reduce_scatter | solution.py:193
  421.4 19.8 %copy-start.63 = (f32[1024]{0:T(1024)S(1)}, f32[1024]{0:T(1024)}, u32[]{:S(2)}) copy-start(f32[1024]{0:T(1024)} %param.21) | copy-start | bytes 12292
  426.5 18.4 %copy-start.7 = (bf16[512,1024]{1,0:T(8,128)(2,1)S(1)}, bf16[512,1024]{1,0:T(8,128)(2,1)}, u32[]{:S(2)}) copy-start(bf16[512,1024]{1,0:T(8,128)(2,1)} %param.14) | copy-start | bytes 3145732
  445.7 20.7 %copy-start.9 = (f32[512,1024]{1,0:T(8,128)}, f32[512,1024]{1,0:T(8,128)S(1)}, u32[]{:S(2)}) copy-start(f32[512,1024]{1,0:T(8,128)S(1)} %get-tuple-element.91) | copy-start | bytes 6291460
  448.8 8.5 copy-start.42
  448.8 8.5 copy-start.43
  448.8 8.5 copy-start.72
  483.3 7.4 collective-permute-start.3
  497.5 231.1 %reduce-scatter.9.cloned.1.call-start = ((), (), s32[]{:S(2)}) async-start(), calls=%async_computation.12 | async-start | bytes 4718592 | tf_op jit(solution)/shard_map/reduce_scatter | solution.py:193
  497.6 11.8 %copy-start.10 = (f32[512,1024]{1,0:T(8,128)S(1)}, f32[512,1024]{1,0:T(8,128)}, u32[]{:S(2)}) copy-start(f32[512,1024]{1,0:T(8,128)} %copy-done.9) | copy-start | bytes 6291460
  509.4 8.6 copy-start.93
  522.2 7.2 collective-permute-start.2
  536.2 11.3 %copy-start.11 = (f32[512,1024]{1,0:T(8,128)S(1)}, f32[512,1024]{1,0:T(8,128)}, u32[]{:S(2)}) copy-start(f32[512,1024]{1,0:T(8,128)} %copy-done.9) | copy-start | bytes 6291460
  555.8 46.7 %all-to-all-start.1 = ((bf16[512,8,128]{0,2,1:T(8,128)(2,1)}), bf16[512,8,128]{0,2,1:T(8,128)(2,1)S(1)}, u32[]{:S(2)}, u32[]{:S(2)}) async-start(bf16[512,8,128]{0,2,1:T(8,128)(2,1)} %bitcast.18), calls=%async_computation.1 | async-start | bytes 2097152 | tf_op jit(solution)/shard_map/all_to_all | solution.py:306
  559.4 206.1 %reduce-scatter.7.cloned.1.call-start = ((), (), s32[]{:S(2)}) async-start(), calls=%async_computation.11 | async-start | bytes 2359296 | tf_op jit(solution)/shard_map/reduce_scatter | solution.py:314
  562.0 43.0 %copy-start.34 = (pred[512,512]{0,1:T(8,128)(4,1)S(1)}, pred[512,512]{0,1:T(8,128)(4,1)}, u32[]{:S(2)}) copy-start(pred[512,512]{0,1:T(8,128)(4,1)} %iota_compare_fusion.3) | copy-start | bytes 786436
  562.1 274.4 %all-reduce.10.cloned.1.call-start = ((), (), s32[]{:S(2)}) async-start(), calls=%async_computation.14 | async-start | bytes 6291456 | tf_op jit(solution)/shard_map/psum | solution.py:360
  624.0 9.2 slice-start.4
  624.0 9.2 slice-start.5
  645.3 15.9 %slice-start = ((s8[16777216]{0:T(1024)(128)(4,1)}), s8[4194304]{0:T(1024)(128)(4,1)S(1)}, s32[]{:S(2)}) async-start(s8[16777216]{0:T(1024)(128)(4,1)} %bitcast.122), calls=%async_computation.15 | async-start | bytes 8388608
  645.3 15.9 %slice-start.1 = ((s8[16777216]{0:T(1024)(128)(4,1)}), s8[4194304]{0:T(1024)(128)(4,1)S(1)}, s32[]{:S(2)}) async-start(s8[16777216]{0:T(1024)(128)(4,1)} %bitcast.122), calls=%async_computation.16 | async-start | bytes 8388608
  645.3 15.9 %slice-start.2 = ((s8[16777216]{0:T(1024)(128)(4,1)}), s8[4194304]{0:T(1024)(128)(4,1)S(1)}, s32[]{:S(2)}) async-start(s8[16777216]{0:T(1024)(128)(4,1)} %bitcast.122), calls=%async_computation.17 | async-start | bytes 8388608
  686.8 12.6 %copy-start.26 = (bf16[2,2048,2,32]{1,3,2,0:T(8,128)(2,1)S(1)}, bf16[2,2048,2,32]{1,3,2,0:T(8,128)(2,1)}, u32[]{:S(2)}) copy-start(bf16[2,2048,2,32]{1,3,2,0:T(8,128)(2,1)} %copy-done.23) | copy-start | bytes 1572868
  686.8 12.6 %copy-start.30 = (bf16[2,2048,2,32]{1,3,2,0:T(8,128)(2,1)S(1)}, bf16[2,2048,2,32]{1,3,2,0:T(8,128)(2,1)}, u32[]{:S(2)}) copy-start(bf16[2,2048,2,32]{1,3,2,0:T(8,128)(2,1)} %copy-done.27) | copy-start | bytes 1572868
  727.2 38.4 %copy-start.90 = (bf16[3,1024,128]{2,1,0:T(8,128)(2,1)S(1)}, bf16[3,1024,128]{2,1,0:T(8,128)(2,1)}, u32[]{:S(2)}) copy-start(bf16[3,1024,128]{2,1,0:T(8,128)(2,1)} %param.18) | copy-start | bytes 2359300
  765.5 222.1 %reduce-scatter.5.cloned.1.call-start = ((), (), s32[]{:S(2)}) async-start(), calls=%async_computation.10 | async-start | bytes 9437184 | tf_op jit(solution)/shard_map/reduce_scatter | solution.py:330
  838.3 149.3 %copy-start.8 = (bf16[512,1024]{1,0:T(8,128)(2,1)S(1)}, bf16[512,1024]{1,0:T(8,128)(2,1)}, u32[]{:S(2)}) copy-start(bf16[512,1024]{1,0:T(8,128)(2,1)} %param.14) | copy-start | bytes 3145732
  838.3 149.3 %copy-start.69 = (f32[1,1024]{1,0:T(1,128)S(1)}, f32[1,1024]{1,0:T(1,128)}, u32[]{:S(2)}) copy-start(f32[1,1024]{1,0:T(1,128)} %copy-done.68) | copy-start | bytes 12292
  838.3 149.3 %copy-start.71 = (f32[512]{0:T(512)S(1)}, f32[512]{0:T(512)}, u32[]{:S(2)}) copy-start(f32[512]{0:T(512)} %copy-done.70) | copy-start | bytes 6148
  838.3 149.3 %copy-start.74 = (f32[512]{0:T(512)S(1)}, f32[512]{0:T(512)}, u32[]{:S(2)}) copy-start(f32[512]{0:T(512)} %copy-done.73) | copy-start | bytes 6148
  841.0 148.9 %copy-start.77 = (f32[1024]{0:T(1024)S(1)}, f32[1024]{0:T(1024)}, u32[]{:S(2)}) copy-start(f32[1024]{0:T(1024)} %get-tuple-element.60) | copy-start | bytes 12292
  841.0 149.0 %copy-start.79 = (f32[1024]{0:T(1024)S(1)}, f32[1024]{0:T(1024)}, u32[]{:S(2)}) copy-start(f32[1024]{0:T(1024)} %get-tuple-element.64) | copy-start | bytes 12292
  841.0 149.0 %copy-start.85 = (f32[1024]{0:T(1024)S(1)}, f32[1024]{0:T(1024)}, u32[]{:S(2)}) copy-start(f32[1024]{0:T(1024)} %get-tuple-element.62) | copy-start | bytes 12292
  841.0 149.0 %copy-start.78 = (f32[1024]{0:T(1024)S(1)}, f32[1024]{0:T(1024)}, u32[]{:S(2)}) copy-start(f32[1024]{0:T(1024)} %get-tuple-element.74) | copy-start | bytes 12292
  841.0 149.0 %copy-start.84 = (f32[1024]{0:T(1024)S(1)}, f32[1024]{0:T(1024)}, u32[]{:S(2)}) copy-start(f32[1024]{0:T(1024)} %get-tuple-element.71) | copy-start | bytes 12292
  841.0 149.0 %copy-start.76 = (f32[1024]{0:T(1024)S(1)}, f32[1024]{0:T(1024)}, u32[]{:S(2)}) copy-start(f32[1024]{0:T(1024)} %get-tuple-element.85) | copy-start | bytes 12292
  841.0 149.0 %copy-start.80 = (f32[4096]{0:T(1024)S(1)}, f32[4096]{0:T(1024)}, u32[]{:S(2)}) copy-start(f32[4096]{0:T(1024)} %get-tuple-element.156) | copy-start | bytes 49156
  841.0 149.0 %copy-start.83 = (f32[1024]{0:T(1024)S(1)}, f32[1024]{0:T(1024)}, u32[]{:S(2)}) copy-start(f32[1024]{0:T(1024)} %get-tuple-element.87) | copy-start | bytes 12292
  843.6 191.2 %copy-start.1 = (bf16[512,1024]{1,0:T(8,128)(2,1)S(1)}, bf16[512,1024]{1,0:T(8,128)(2,1)}, u32[]{:S(2)}) copy-start(bf16[512,1024]{1,0:T(8,128)(2,1)} %param.24) | copy-start | bytes 3145732
  (54 other events, 197.9 us)
Sparse Core Ops, SparseCore 0:
  10.7 75.7 all-gather.11
  89.1 73.1 all-gather.9
  165.0 122.6 all-gather.5
  289.7 47.2 all-gather.7
  497.6 105.9 reduce-scatter.10
  607.1 86.0 reduce-scatter.8
  697.3 68.1 reduce-scatter.6
  768.7 67.7 all-reduce.9
  840.1 147.5 reduce-scatter.4

commit v3 on v2

--- a/solution.py
+++ b/solution.py
@@ -233,6 +233,9 @@
     normed_first, inverse_first = norm_stats(layer_in)
     low_first = (normed_first * norm_gains[0] + norm_biases[0]).astype(jnp.bfloat16)
     gathered_first = lax.all_gather(low_first, "narrow", axis=0, tiled=True)
+    gathered_first, up_weight, down_weight = lax.optimization_barrier(
+        (gathered_first, up_weight, down_weight)
+    )
     query, key_rows, values = project_qkv(
         gathered_first, qkv_weight, qkv_bias, cos_table, sine_table, seq_count, length
     )
@@ -335,6 +338,9 @@
         scatter_dimension=0,
         tiled=True,
     ).astype(jnp.float32)
+    first_grad, qkv_wgrad, qkv_bgrad, out_wgrad, up_slots, down_slots = lax.optimization_barrier(
+        (first_grad, qkv_wgrad, qkv_bgrad, out_wgrad, up_slots, down_slots)
+    )
     input_grad = (
         residual_grad + norm_back(normed_first, inverse_first, norm_gains[0], first_grad)
     ).astype(jnp.bfloat16)

time: 1050 us -> 1060 us (level)
  waiting for transfers between devices: 538 us -> 390 us
  local copies, waits for them, and re-layouts: 121 us -> 204 us
  matrix products: 174 us -> 214 us
  blocking collectives: 75.6 us -> 92.7 us
  other arithmetic: 110 us -> 125 us
    all_gather x2, waiting for transfers between devices: 114 us -> 0.01 us  [gather_halves(): gathered = lax.all_gather(mine, 'narrow', axis=gather_axis, tiled=True)]
    psum x1, waiting for transfers between devices: 52.5 us -> 14.9 us  [shards(): lax.psum(qkv_wgrad.astype(jnp.bfloat16), 'wide').astype(jnp.float32)]
    all_to_all x1, waiting for transfers between devices: 40.5 us -> 4.67 us  [shards(): attn_grad = lax.all_to_all(attn_grad_rows, 'narrow', 1, 0, tiled=True)]
    reduce_scatter x1, waiting for transfers between devices: 34.8 us -> 68.1 us  [shards(): lax.psum_scatter(out_wgrad_rows.astype(jnp.bfloat16), 'narrow', scatter_d...]
    unnamed x214 -> x208, local copies, waits for them, and re-layouts: 49.2 us -> 75.5 us
    reduce_scatter x2, waiting for transfers between devices: 0.01 us -> 26.2 us  [reduce_halves(): lax.psum_scatter(chip_sum.astype(jnp.bfloat16), 'narrow', scatter_dimensi...]
    dot_general x4 -> x8, matrix products: 11.6 us -> 33.3 us  [block_scores(): jnp.einsum('bqhd,bkhd->bhqk', query_block, key_block, preferred_element_t...]
    slice x2 -> x4, local copies, waits for them, and re-layouts: 19.6 us -> 39.8 us  [rotate(): front_half = vectors[..., :half_size]]
  transfers between devices with their start and end apart: 15 -> 15, of which waited for: 10 -> 6; matrix products, arithmetic and copies ran while one was open for 33% -> 43% of each run, Pallas kernels for 0% -> 0%
where the time goes in v3:
time: 1060 us; the launch traced here: 1050 us
  waiting for transfers between devices  390 us (37%)
  matrix products  214 us (20%)
  local copies, waits for them, and re-layouts  204 us (19%)
  other arithmetic  125 us (12%)
  blocking collectives  92.7 us (9%)
  between operations  15.7 us (1%)
    reduce_scatter x1, waiting for transfers between devices, shards(): lax.psum_scatter(jnp.einsum('tse,tde->sd', rows_here, qkv_weight, preferr...  149 us
    all_gather x1, waiting for transfers between devices, shards(): gathered_first = lax.all_gather(low_first, 'narrow', axis=0, tiled=True)  127 us
    unnamed x208, local copies, waits for them, and re-layouts  75.5 us
    reduce_scatter x1, waiting for transfers between devices, shards(): lax.psum_scatter(out_wgrad_rows.astype(jnp.bfloat16), 'narrow', scatter_d...  68.1 us
    all_gather x1, blocking collectives, shards(): up_bias_full = lax.all_gather(up_bias, 'narrow', axis=0, tiled=True)  45.1 us
    psum x1, blocking collectives, shards(): lax.psum((gain_local, bias_local, out_blocal, down_blocal, up_bgrad_rows)...  41.9 us
    slice x4, local copies, waits for them, and re-layouts, rotate(): front_half = vectors[..., :half_size]  39.8 us
    convert_element_type x4, other arithmetic, attend_backward(): scores_grad = (probs_full * (probs_grad - row_dot)).astype(jnp.bfloat16)  36.9 us
  transfers between devices with their start and end apart: 15, of which 6 were waited for; matrix products, arithmetic and copies ran while one was open for 43% of the time, Pallas kernels for 0%

profile of v3, /device:TPU:0, one launch (start us, length us, event | category | flops | bytes accessed | tf_op | source)
XLA Modules:
  0.0 1050.8 jit_solution(9982411832661431766)
XLA Ops:
  16.2 127.3 %all-gather.6.cloned.1.call-done = bf16[4096,1024]{1,0:T(8,128)(2,1)} async-done(((bf16[512,1024]{1,0:T(8,128)(2,1)}), bf16[4096,1024]{1,0:T(8,128)(2,1)}) %all-gather.6.cloned.1.call-update) | async-done | bytes 8388624 | tf_op jit(solution)/shard_map/all_gather | solution.py:235
  151.1 7.5 add_bitcast_fusion.1
  169.4 5.9 reshape.362
  178.9 10.1 fusion.194
  189.0 6.4 copy.205
  195.5 6.4 copy.206
  201.9 10.0 fusion.193
  211.9 6.5 copy.203
  218.5 6.4 copy.204
  224.9 7.3 add_bitcast_fusion
  235.5 5.7 reshape.364
  244.8 9.8 fusion.192
  254.6 6.4 copy.209
  261.0 6.4 copy.210
  267.5 9.9 fusion.191
  277.3 6.4 copy.207
  283.8 6.8 copy.208
  290.6 4.9 subtract_convert_fusion.3
  311.0 4.3 fusion.100
  315.2 4.2 fusion
  319.4 4.3 exponential_reduce_fusion
  325.7 5.5 fusion.99
  337.2 4.2 all-to-all-start
  341.5 45.1 %all-gather = f32[8,1,512]{2,1,0:T(1,128)S(1)} all-gather(f32[1,1,512]{2,1,0:T(1,128)S(1)} %bitcast.163), channel_id=1, replica_groups=mesh['wide'=4,'narrow'=8] {'narrow'}, dimensions={0}, use_global_device_ids=true | all-gather | bytes 18432 | tf_op jit(solution)/shard_map/all_gather | solution.py:254
  390.5 5.9 copy.159
  396.5 4.5 fusion.177
  403.8 8.1 fusion.110
  417.9 3.9 broadcast_select_fusion.3
  421.8 10.2 multiply_convert_fusion.3
  432.0 5.5 broadcast_select_fusion.1
  437.6 9.3 add_reduce_fusion
  451.7 13.0 %convert_reduce_fusion = (f32[4096]{0:T(1024)}, bf16[512,4096]{1,0:T(8,128)(2,1)}) fusion(f32[512,4096]{1,0:T(8,128)} %get-tuple-element.176, f32[4096]{0:T(1024)S(1)} %bitcast.158, bf16[512,1024]{1,0:T(8,128)(2,1)S(1)} %get-tuple-element.104, bf16[4096,512]{1,0:T(8,128)(2,1)} %get-tuple-element.111, bf16[4096,512]{1,0:T(8,128)(2,1)} %get-tuple-element.110), kind=kOutput, calls=%fused_computation.31 | convolution fusion | flops 4339003392 | bytes 22052864 | tf_op jit(solution)/shard_map/dot_general | solution.py:285
  464.7 9.1 multiply_reduce_fusion.5
  473.8 10.6 %fusion.186 = f32[1024,4096]{1,0:T(8,128)} fusion(bf16[512,4096]{1,0:T(8,128)(2,1)} %get-tuple-element.189, f32[512,1024]{1,0:T(8,128)S(1)} %get-tuple-element.109, f32[1024]{0:T(1024)S(1)} %bitcast.160, f32[1024]{0:T(1024)S(1)} %bitcast.146, f32[512]{0:T(512)S(1)} %add_rsqrt_fusion.1, f32[512]{0:T(512)S(1)} %broadcast_multiply_fusion.9), kind=kOutput, calls=%fused_computation.324 | convolution fusion | flops 4297588736 | bytes 23080960 | tf_op jit(solution)/shard_map/dot_general | solution.py:290
  492.4 4.2 all-to-all-start.1
  496.7 6.1 dynamic-slice_convert_fusion.1
  503.2 6.8 fusion.198
  510.1 5.7 copy-done.27
  518.6 4.7 all-to-all-done.1
  531.0 5.6 multiply_reduce_fusion.3
  538.5 8.5 multiply_reduce_fusion.1
  547.1 6.9 fusion.40
  554.0 8.0 add_convert_fusion.1
  562.2 6.1 multiply_convert_fusion.4
  568.3 6.0 fusion.82
  574.3 5.5 multiply_reduce_fusion.2
  579.8 6.3 multiply_convert_fusion.2
  586.1 4.9 fusion.88
  591.0 7.6 fusion.51
  598.6 11.5 %multiply_reduce_fusion = (f32[2,2,512]{2,1,0:T(2,128)}, f32[2,2,512,2048]{3,2,1,0:T(8,128)}) fusion(f32[2,2,512,2048]{3,2,1,0:T(8,128)S(1)} %bitcast.129, f32[2,2,512]{2,1,0:T(2,128)S(1)} %copy-done.63, pred[512,2048]{1,0:T(8,128)(4,1)S(1)} %copy-done.15, bf16[2,2048,2,64]{1,3,2,0:T(8,128)(2,1)} %copy.159, bf16[2,512,2,64]{1,0,3,2:T(2,128)(2,1)} %get-tuple-element.142), kind=kOutput, calls=%fused_computation.2 | convolution fusion | flops 557840384 | bytes 35930112 | tf_op jit(solution)/shard_map/bqhd,bkhd->bhqk/dot_general | solution.py:141
  610.1 12.1 %multiply_convert_fusion.1 = bf16[2,2,512,1536]{3,2,1,0:T(8,128)(2,1)} fusion(f32[2,2,512,1536]{3,2,1,0:T(8,128)} %get-tuple-element.183, f32[2,2,512,1536]{3,2,1,0:T(8,128)} %copy-done.2, f32[2,2,512]{2,1,0:T(2,128)} %get-tuple-element.182), kind=kLoop, calls=%fused_computation.8 | loop fusion | flops 9437184 | bytes 31465472 | tf_op jit(solution)/shard_map/convert_element_type | solution.py:145
  622.2 8.1 add_convert_fusion
  633.4 6.2 copy.187
  639.6 4.8 reshape.360
  648.0 4.9 fusion.86
  652.8 12.4 %multiply_convert_fusion = bf16[2,2,512,2048]{3,2,1,0:T(8,128)(2,1)S(1)} fusion(f32[2,2,512,2048]{3,2,1,0:T(8,128)} %get-tuple-element.181, f32[2,2,512,2048]{3,2,1,0:T(8,128)} %fusion.110, f32[2,2,512]{2,1,0:T(2,128)S(1)} %copy-done.72, f32[2,2,512]{2,1,0:T(2,128)S(1)} %copy-done.63, pred[512,2048]{1,0:T(8,128)(4,1)S(1)} %copy-done.15), kind=kLoop, calls=%fused_computation.1 | loop fusion | flops 25165824 | bytes 43008000 | tf_op jit(solution)/shard_map/convert_element_type | solution.py:145
  689.5 6.9 bitcast_convert_fusion
  704.1 8.9 fusion.79
  715.2 26.2 %reduce-scatter.11.cloned.1.call-done = bf16[512,512]{1,0:T(8,128)(2,1)} async-done(((bf16[4096,512]{1,0:T(8,128)(2,1)}), bf16[512,512]{1,0:T(8,128)(2,1)}) %reduce-scatter.11.cloned.1.call-update) | async-done | bytes 524304 | tf_op jit(solution)/shard_map/reduce_scatter | solution.py:193
  743.5 148.6 %reduce-scatter.5.cloned.1.call-done = bf16[512,1024]{1,0:T(8,128)(2,1)} async-done(((bf16[4096,1024]{1,0:T(8,128)(2,1)}), bf16[512,1024]{1,0:T(8,128)(2,1)}) %reduce-scatter.5.cloned.1.call-update) | async-done | bytes 1048592 | tf_op jit(solution)/shard_map/reduce_scatter | solution.py:333
  895.0 68.1 %reduce-scatter.7.cloned.1.call-done = bf16[128,1024]{1,0:T(8,128)(2,1)} async-done(((bf16[1024,1024]{1,0:T(8,128)(2,1)}), bf16[128,1024]{1,0:T(8,128)(2,1)}) %reduce-scatter.7.cloned.1.call-update) | async-done | bytes 262160 | tf_op jit(solution)/shard_map/reduce_scatter | solution.py:317
  965.4 5.7 psum.71
  974.3 41.9 %all-reduce.6 = (f32[1024]{0:T(1024)}, f32[4096]{0:T(1024)S(1)}, f32[1024]{0:T(1024)}, f32[4,1024]{1,0:T(4,128)}, f32[4,1024]{1,0:T(4,128)}) all-reduce(f32[1024]{0:T(1024)S(1)} %copy-done.80, f32[4096]{0:T(1024)S(1)} %copy-done.79, f32[1024]{0:T(1024)S(1)} %copy-done.73, ...), channel_id=1, replica_groups=mesh['wide'=4,'narrow'=8] {'wide','narrow'}, use_global_device_ids=true, to_apply=%region_39.40 | all-reduce | flops 14336 | bytes 114688 | tf_op jit(solution)/shard_map/psum | solution.py:373
  1020.3 14.9 %all-reduce.10.cloned.1.call-done = (bf16[3,1024,128]{1,2,0:T(8,128)(2,1)}, bf16[512,1024]{0,1:T(8,128)(2,1)}, bf16[128,1024]{1,0:T(8,128)(2,1)}, bf16[1024,512]{1,0:T(8,128)(2,1)}) async-done(((bf16[3,1024,128]{1,2,0:T(8,128)(2,1)}, bf16[512,1024]{0,1:T(8,128)(2,1)}, bf16[128,1024]{1,0:T(8,128)(2,1)}, bf16[1024,512]{1,0:T(8,128)(2,1)}), (bf16[3,1024,128]{1,2,0:T(8,128)(2,1)}, bf16[512,1024]{0,1:T(8,128)(2,1)}, ...) | async-done | bytes 3145744 | tf_op jit(solution)/shard_map/psum | solution.py:366
  (342 shorter events, 163.1 us)
Async XLA Ops:
  7.2 136.3 %copy-start = (bf16[1024,512]{1,0:T(8,128)(2,1)S(1)}, bf16[1024,512]{1,0:T(8,128)(2,1)}, u32[]{:S(2)}) copy-start(bf16[1024,512]{1,0:T(8,128)(2,1)} %param.22) | copy-start | bytes 3145732
  7.2 137.2 %copy-start.59 = (bf16[512,1024]{1,0:T(8,128)(2,1)S(1)}, bf16[512,1024]{1,0:T(8,128)(2,1)}, u32[]{:S(2)}) copy-start(bf16[512,1024]{1,0:T(8,128)(2,1)} %param.24) | copy-start | bytes 3145732
  7.2 136.3 %all-gather.6.cloned.1.call-start = ((), (), s32[]{:S(2)}) async-start(), calls=%async_computation.6 | async-start | bytes 9437184 | tf_op jit(solution)/shard_map/all_gather | solution.py:235
  8.8 138.3 %copy-start.66 = (f32[512]{0:T(512)}, f32[512]{0:T(512)S(1)}, u32[]{:S(2)}) copy-start(f32[512]{0:T(512)S(1)} %broadcast_multiply_fusion.11) | copy-start | bytes 6148
  10.5 140.0 %copy-start.70 = (f32[512]{0:T(512)}, f32[512]{0:T(512)S(1)}, u32[]{:S(2)}) copy-start(f32[512]{0:T(512)S(1)} %add_rsqrt_fusion.3) | copy-start | bytes 6148
  12.0 138.5 %copy-start.64 = (f32[1,1024]{1,0:T(1,128)}, f32[1,1024]{1,0:T(1,128)S(1)}, u32[]{:S(2)}) copy-start(f32[1,1024]{1,0:T(1,128)S(1)} %get-tuple-element.157) | copy-start | bytes 12292
  16.1 135.0 %copy-start.86 = (bf16[3,1024,128]{2,1,0:T(8,128)(2,1)S(1)}, bf16[3,1024,128]{2,1,0:T(8,128)(2,1)}, u32[]{:S(2)}) copy-start(bf16[3,1024,128]{2,1,0:T(8,128)(2,1)} %param.18) | copy-start | bytes 2359300
  16.1 135.0 %copy-start.89 = (f32[3,128]{1,0:T(4,128)S(1)}, f32[3,128]{1,0:T(4,128)}, u32[]{:S(2)}) copy-start(f32[3,128]{1,0:T(4,128)} %param.19) | copy-start | bytes 4612
  16.1 315.0 %all-gather.10.cloned.1.call-start = ((), (), s32[]{:S(2)}) async-start(), calls=%async_computation.8 | async-start | bytes 4718592 | tf_op jit(solution)/shard_map/all_gather | solution.py:181
  144.3 267.6 %all-gather.12.cloned.1.call-start = ((), (), s32[]{:S(2)}) async-start(), calls=%async_computation.9 | async-start | bytes 4718592 | tf_op jit(solution)/shard_map/all_gather | solution.py:181
  145.3 266.7 %all-gather.8.cloned.1.call-start = ((), (), s32[]{:S(2)}) async-start(), calls=%async_computation.7 | async-start | bytes 2359296 | tf_op jit(solution)/shard_map/all_gather | solution.py:245
  146.0 416.1 %copy-start.23 = (pred[512,512]{0,1:T(8,128)(4,1)}, pred[512,512]{0,1:T(8,128)(4,1)S(1)}, u32[]{:S(2)}) copy-start(pred[512,512]{0,1:T(8,128)(4,1)S(1)} %iota_compare_fusion.3) | copy-start | bytes 786436
  151.1 174.6 %copy-start.14 = (pred[512,2048]{1,0:T(8,128)(4,1)}, pred[512,2048]{1,0:T(8,128)(4,1)S(1)}, u32[]{:S(2)}) copy-start(pred[512,2048]{1,0:T(8,128)(4,1)S(1)} %iota_compare_fusion) | copy-start | bytes 3145732
  211.9 12.9 %copy-start.87 = (bf16[3,1024,128]{2,1,0:T(8,128)(2,1)S(1)}, bf16[3,1024,128]{2,1,0:T(8,128)(2,1)}, u32[]{:S(2)}) copy-start(bf16[3,1024,128]{2,1,0:T(8,128)(2,1)} %param.18) | copy-start | bytes 2359300
  295.5 243.0 %copy-start.6 = (bf16[2,2048,2,32]{1,3,2,0:T(8,128)(2,1)}, bf16[2,2048,2,32]{1,3,2,0:T(8,128)(2,1)S(1)}, u32[]{:S(2)}) copy-start(bf16[2,2048,2,32]{1,3,2,0:T(8,128)(2,1)S(1)} %get-tuple-element.151) | copy-start | bytes 1572868
  295.5 243.0 %copy-start.8 = (bf16[2,2048,2,32]{1,3,2,0:T(8,128)(2,1)}, bf16[2,2048,2,32]{1,3,2,0:T(8,128)(2,1)S(1)}, u32[]{:S(2)}) copy-start(bf16[2,2048,2,32]{1,3,2,0:T(8,128)(2,1)S(1)} %get-tuple-element.152) | copy-start | bytes 1572868
  295.5 243.0 %copy-start.10 = (bf16[2,2048,2,32]{1,3,2,0:T(8,128)(2,1)}, bf16[2,2048,2,32]{1,3,2,0:T(8,128)(2,1)S(1)}, u32[]{:S(2)}) copy-start(bf16[2,2048,2,32]{1,3,2,0:T(8,128)(2,1)S(1)} %get-tuple-element.130) | copy-start | bytes 1572868
  295.5 243.0 %copy-start.12 = (bf16[2,2048,2,32]{1,3,2,0:T(8,128)(2,1)}, bf16[2,2048,2,32]{1,3,2,0:T(8,128)(2,1)S(1)}, u32[]{:S(2)}) copy-start(bf16[2,2048,2,32]{1,3,2,0:T(8,128)(2,1)S(1)} %get-tuple-element.131) | copy-start | bytes 1572868
  323.8 7.3 copy-start.62
  331.1 85.8 %collective-permute-start = (bf16[512,4096]{1,0:T(8,128)(2,1)}, bf16[512,4096]{1,0:T(8,128)(2,1)}, u32[]{:S(2)}, u32[]{:S(2)}) collective-permute-start(bf16[512,4096]{1,0:T(8,128)(2,1)} %all-gather.10.cloned.1.call-done), channel_id=1, source_target_pairs={{0,8},{8,0},{16,24},{24,16},{1,9},{9,1},{17,25},{25,17},{2,10},{10... | collective-permute-start | bytes 12582920 | tf_op jit(solution)/shard_map/ppermute | solution.py:175
  332.4 9.0 copy-start.84
  332.5 9.1 copy-start.83
  332.5 54.2 %copy-start.85 = (f32[8]{0:T(128)S(1)}, f32[8]{0:T(128)}, u32[]{:S(2)}) copy-start(f32[8]{0:T(128)} %param.17) | copy-start | bytes 100
  337.2 74.8 %all-to-all-start = ((bf16[8,512,128]{1,2,0:T(8,128)(2,1)}), bf16[8,512,128]{1,2,0:T(8,128)(2,1)}, u32[]{:S(2)}, u32[]{:S(2)}) async-start(bf16[8,512,128]{1,2,0:T(8,128)(2,1)} %copy.148), calls=%async_computation | async-start | bytes 2097152 | tf_op jit(solution)/shard_map/all_to_all | solution.py:244
  403.8 8.2 copy-start.58
  411.9 20.1 %collective-permute-start.1 = (bf16[4096,512]{1,0:T(8,128)(2,1)}, bf16[4096,512]{1,0:T(8,128)(2,1)}, u32[]{:S(2)}, u32[]{:S(2)}) collective-permute-start(bf16[4096,512]{1,0:T(8,128)(2,1)} %all-gather.12.cloned.1.call-done), channel_id=1, source_target_pairs={{0,8},{8,0},{16,24},{24,16},{1,9},{9,1},{17,25},{25,17},{2,10},{10... | collective-permute-start | bytes 12582920 | tf_op jit(solution)/shard_map/ppermute | solution.py:175
  421.8 10.2 copy-start.32
  437.5 9.7 copy-start.28
  437.6 9.7 copy-start.69
  451.7 13.0 %copy-start.52 = (bf16[512,1024]{1,0:T(8,128)(2,1)}, bf16[512,1024]{1,0:T(8,128)(2,1)S(1)}, u32[]{:S(2)}) copy-start(bf16[512,1024]{1,0:T(8,128)(2,1)S(1)} %get-tuple-element.104) | copy-start | bytes 3145732
  451.7 13.0 %copy-start.34 = (bf16[512,4096]{1,0:T(8,128)(2,1)S(1)}, bf16[512,4096]{1,0:T(8,128)(2,1)}, u32[]{:S(2)}) copy-start(bf16[512,4096]{1,0:T(8,128)(2,1)} %get-tuple-element.113) | copy-start | bytes 12582916
  473.8 10.6 %copy-start.43 = (f32[512,1024]{1,0:T(8,128)S(1)}, f32[512,1024]{1,0:T(8,128)}, u32[]{:S(2)}) copy-start(f32[512,1024]{1,0:T(8,128)} %get-tuple-element.179) | copy-start | bytes 6291460
  492.4 30.9 %all-to-all-start.1 = ((bf16[512,8,128]{0,2,1:T(8,128)(2,1)}), bf16[512,8,128]{0,2,1:T(8,128)(2,1)}, u32[]{:S(2)}, u32[]{:S(2)}) async-start(bf16[512,8,128]{0,2,1:T(8,128)(2,1)} %bitcast.20), calls=%async_computation.1 | async-start | bytes 2097152 | tf_op jit(solution)/shard_map/all_to_all | solution.py:309
  496.7 216.2 %reduce-scatter.9.cloned.1.call-start = ((), (), s32[]{:S(2)}) async-start(), calls=%async_computation.12 | async-start | bytes 4718592 | tf_op jit(solution)/shard_map/reduce_scatter | solution.py:193
  502.8 51.2 %collective-permute-start.2 = (bf16[512,4096]{1,0:T(8,128)(2,1)}, bf16[512,4096]{1,0:T(8,128)(2,1)}, u32[]{:S(2)}, u32[]{:S(2)}) collective-permute-start(bf16[512,4096]{1,0:T(8,128)(2,1)} %dynamic-slice_convert_fusion.1), channel_id=1, source_target_pairs={{0,8},{8,0},{16,24},{24,16},{1,9},{9,1},{17,25},{25,17},{2,10},{10... | collective-permute-start | bytes 12582920 | tf_op jit(solution)/shard_map/ppermute | solution.py:175
  518.5 12.5 %copy-start.21 = (bf16[2,2048,2,64]{1,3,2,0:T(8,128)(2,1)S(1)}, bf16[2,2048,2,64]{1,3,2,0:T(8,128)(2,1)}, u32[]{:S(2)}) copy-start(bf16[2,2048,2,64]{1,3,2,0:T(8,128)(2,1)} %copy.159) | copy-start | bytes 3145732
  518.5 103.7 %collective-permute-start.3 = (bf16[4096,512]{1,0:T(8,128)(2,1)}, bf16[4096,512]{1,0:T(8,128)(2,1)}, u32[]{:S(2)}, u32[]{:S(2)}) collective-permute-start(bf16[4096,512]{1,0:T(8,128)(2,1)} %dynamic-slice_convert_fusion), channel_id=1, source_target_pairs={{0,8},{8,0},{16,24},{24,16},{1,9},{9,1},{17,25},{25,17},{2,10},{10... | collective-permute-start | bytes 12582920 | tf_op jit(solution)/shard_map/ppermute | solution.py:175
  538.5 8.5 copy-start.2
  562.0 179.3 %reduce-scatter.11.cloned.1.call-start = ((), (), s32[]{:S(2)}) async-start(), calls=%async_computation.13 | async-start | bytes 4718592 | tf_op jit(solution)/shard_map/reduce_scatter | solution.py:193
  562.1 12.2 %slice-start.4 = ((s8[8388608]{0:T(1024)(128)(4,1)}), s8[4194304]{0:T(1024)(128)(4,1)S(1)}, s32[]{:S(2)}) async-start(s8[8388608]{0:T(1024)(128)(4,1)} %bitcast.130), calls=%async_computation.19 | async-start | bytes 8388608
  574.3 16.7 %slice-start = ((s8[16777216]{0:T(1024)(128)(4,1)}), s8[4194304]{0:T(1024)(128)(4,1)S(1)}, s32[]{:S(2)}) async-start(s8[16777216]{0:T(1024)(128)(4,1)} %bitcast.128), calls=%async_computation.15 | async-start | bytes 8388608
  574.3 16.7 %slice-start.1 = ((s8[16777216]{0:T(1024)(128)(4,1)}), s8[4194304]{0:T(1024)(128)(4,1)S(1)}, s32[]{:S(2)}) async-start(s8[16777216]{0:T(1024)(128)(4,1)} %bitcast.128), calls=%async_computation.16 | async-start | bytes 8388608
  579.8 11.2 %slice-start.2 = ((s8[16777216]{0:T(1024)(128)(4,1)}), s8[4194304]{0:T(1024)(128)(4,1)S(1)}, s32[]{:S(2)}) async-start(s8[16777216]{0:T(1024)(128)(4,1)} %bitcast.128), calls=%async_computation.17 | async-start | bytes 8388608
  579.8 11.2 %slice-start.3 = ((s8[16777216]{0:T(1024)(128)(4,1)}), s8[4194304]{0:T(1024)(128)(4,1)S(1)}, s32[]{:S(2)}) async-start(s8[16777216]{0:T(1024)(128)(4,1)} %bitcast.128), calls=%async_computation.18 | async-start | bytes 8388608
  591.0 7.6 copy-start.63
  630.4 14.0 %copy-start.11 = (bf16[2,2048,2,32]{1,3,2,0:T(8,128)(2,1)S(1)}, bf16[2,2048,2,32]{1,3,2,0:T(8,128)(2,1)}, u32[]{:S(2)}) copy-start(bf16[2,2048,2,32]{1,3,2,0:T(8,128)(2,1)} %copy-done.10) | copy-start | bytes 1572868
  630.4 14.0 %copy-start.13 = (bf16[2,2048,2,32]{1,3,2,0:T(8,128)(2,1)S(1)}, bf16[2,2048,2,32]{1,3,2,0:T(8,128)(2,1)}, u32[]{:S(2)}) copy-start(bf16[2,2048,2,32]{1,3,2,0:T(8,128)(2,1)} %copy-done.12) | copy-start | bytes 1572868
  630.4 261.7 %reduce-scatter.5.cloned.1.call-start = ((), (), s32[]{:S(2)}) async-start(), calls=%async_computation.10 | async-start | bytes 9437184 | tf_op jit(solution)/shard_map/reduce_scatter | solution.py:333
  696.4 266.7 %reduce-scatter.7.cloned.1.call-start = ((), (), s32[]{:S(2)}) async-start(), calls=%async_computation.11 | async-start | bytes 2359296 | tf_op jit(solution)/shard_map/reduce_scatter | solution.py:317
  701.5 333.6 %all-reduce.10.cloned.1.call-start = ((), (), s32[]{:S(2)}) async-start(), calls=%async_computation.14 | async-start | bytes 6291456 | tf_op jit(solution)/shard_map/psum | solution.py:366
  743.5 228.1 %copy-start.4 = (bf16[512,1024]{1,0:T(8,128)(2,1)S(1)}, bf16[512,1024]{1,0:T(8,128)(2,1)}, u32[]{:S(2)}) copy-start(bf16[512,1024]{1,0:T(8,128)(2,1)} %param.14) | copy-start | bytes 3145732
  743.5 228.1 %copy-start.65 = (f32[1,1024]{1,0:T(1,128)S(1)}, f32[1,1024]{1,0:T(1,128)}, u32[]{:S(2)}) copy-start(f32[1,1024]{1,0:T(1,128)} %copy-done.64) | copy-start | bytes 12292
  743.5 228.1 %copy-start.67 = (f32[512]{0:T(512)S(1)}, f32[512]{0:T(512)}, u32[]{:S(2)}) copy-start(f32[512]{0:T(512)} %copy-done.66) | copy-start | bytes 6148
  743.5 228.1 %copy-start.71 = (f32[512]{0:T(512)S(1)}, f32[512]{0:T(512)}, u32[]{:S(2)}) copy-start(f32[512]{0:T(512)} %copy-done.70) | copy-start | bytes 6148
  894.9 79.3 %copy-start.76 = (f32[1024]{0:T(1024)S(1)}, f32[1024]{0:T(1024)}, u32[]{:S(2)}) copy-start(f32[1024]{0:T(1024)} %get-tuple-element.78) | copy-start | bytes 12292
  894.9 79.3 %copy-start.78 = (f32[1024]{0:T(1024)S(1)}, f32[1024]{0:T(1024)}, u32[]{:S(2)}) copy-start(f32[1024]{0:T(1024)} %get-tuple-element.82) | copy-start | bytes 12292
  894.9 79.3 %copy-start.82 = (f32[1024]{0:T(1024)S(1)}, f32[1024]{0:T(1024)}, u32[]{:S(2)}) copy-start(f32[1024]{0:T(1024)} %get-tuple-element.80) | copy-start | bytes 12292
  894.9 79.4 %copy-start.75 = (f32[1024]{0:T(1024)S(1)}, f32[1024]{0:T(1024)}, u32[]{:S(2)}) copy-start(f32[1024]{0:T(1024)} %get-tuple-element.90) | copy-start | bytes 12292
  894.9 79.4 %copy-start.77 = (f32[1024]{0:T(1024)S(1)}, f32[1024]{0:T(1024)}, u32[]{:S(2)}) copy-start(f32[1024]{0:T(1024)} %get-tuple-element.93) | copy-start | bytes 12292
  894.9 79.4 %copy-start.81 = (f32[1024]{0:T(1024)S(1)}, f32[1024]{0:T(1024)}, u32[]{:S(2)}) copy-start(f32[1024]{0:T(1024)} %get-tuple-element.91) | copy-start | bytes 12292
  894.9 79.4 %copy-start.73 = (f32[1024]{0:T(1024)S(1)}, f32[1024]{0:T(1024)}, u32[]{:S(2)}) copy-start(f32[1024]{0:T(1024)} %get-tuple-element.103) | copy-start | bytes 12292
  894.9 79.4 %copy-start.79 = (f32[4096]{0:T(1024)S(1)}, f32[4096]{0:T(1024)}, u32[]{:S(2)}) copy-start(f32[4096]{0:T(1024)} %get-tuple-element.188) | copy-start | bytes 49156
  894.9 79.4 %copy-start.80 = (f32[1024]{0:T(1024)S(1)}, f32[1024]{0:T(1024)}, u32[]{:S(2)}) copy-start(f32[1024]{0:T(1024)} %get-tuple-element.105) | copy-start | bytes 12292
  895.0 122.0 %copy-start.17 = (f32[512,1024]{1,0:T(8,128)S(1)}, f32[512,1024]{1,0:T(8,128)}, u32[]{:S(2)}) copy-start(f32[512,1024]{1,0:T(8,128)} %copy-done.16) | copy-start | bytes 6291460
  (49 other events, 203.0 us)
Sparse Core Ops, SparseCore 0:
  16.2 127.1 all-gather.5
  146.1 72.8 all-gather.9
  221.1 70.9 all-gather.11
  294.1 47.7 all-gather.7
  562.2 87.6 reduce-scatter.8
  653.4 87.9 reduce-scatter.10
  745.0 147.0 reduce-scatter.4
  895.6 67.4 reduce-scatter.6
  966.3 68.8 all-reduce.9

commit v4 on v2

--- a/solution.py
+++ b/solution.py
@@ -197,6 +197,30 @@
     return jnp.stack(
         [jnp.where(core == 0, part, empty), jnp.where(core == 0, empty, part)], axis=split_axis
     )
+
+
+def reduce_column_halves(mats, core):
+    count = lax.axis_size("narrow")
+    pieces = []
+    for rows in mats:
+        half = rows.shape[1] // 2
+        mine = lax.dynamic_slice_in_dim(rows, core * half, half, axis=1)
+        other = lax.dynamic_slice_in_dim(rows, (1 - core) * half, half, axis=1)
+        chip_sum = mine + swap_cores(other.astype(jnp.bfloat16)).astype(jnp.float32)
+        pieces.append(chip_sum.astype(jnp.bfloat16).reshape(count, -1, half))
+    joined = lax.psum_scatter(
+        jnp.concatenate(pieces, axis=1), "narrow", scatter_dimension=0, tiled=True
+    )[0]
+    results = []
+    start = 0
+    for piece in pieces:
+        part = joined[start : start + piece.shape[1]]
+        start += piece.shape[1]
+        empty = jnp.zeros_like(part)
+        results.append(
+            jnp.stack([jnp.where(core == 0, part, empty), jnp.where(core == 0, empty, part)], axis=1)
+        )
+    return results
 
 
 def merge_slots(slots, split_axis):
@@ -232,7 +256,11 @@
     layer_in = tokens.astype(jnp.float32)
     normed_first, inverse_first = norm_stats(layer_in)
     low_first = (normed_first * norm_gains[0] + norm_biases[0]).astype(jnp.bfloat16)
+    up_bias_full = lax.all_gather(up_bias, "narrow", axis=0, tiled=True)
     gathered_first = lax.all_gather(low_first, "narrow", axis=0, tiled=True)
+    gathered_first, up_weight, down_weight, up_bias_full = lax.optimization_barrier(
+        (gathered_first, up_weight, down_weight, up_bias_full)
+    )
     query, key_rows, values = project_qkv(
         gathered_first, qkv_weight, qkv_bias, cos_table, sine_table, seq_count, length
     )
@@ -248,7 +276,6 @@
     core = lax.axis_index("wide") % 2
     up_full = gather_halves(up_weight, core, 0, 1)
     down_full = gather_halves(down_weight, core, 1, 0)
-    up_bias_full = lax.all_gather(up_bias, "narrow", axis=0, tiled=True)
     hidden = jnp.dot(low_third, up_full, preferred_element_type=jnp.float32) + up_bias_full
     act_low = gelu_value(hidden).astype(jnp.bfloat16)
     pre_mlp = jnp.dot(act_low, down_full, preferred_element_type=jnp.float32) + down_bias
@@ -291,7 +318,6 @@
         hidden_grad, up_full, (((1,), (1,)), ((), ())), preferred_element_type=jnp.float32
     )
     up_slots = reduce_halves(up_wgrad_rows, core, 0, 1)
-    down_slots = reduce_halves(down_wgrad_rows, core, 1, 0)
     residual_grad = upstream + norm_back(normed_third, inverse_third, norm_gains[2], third_grad)
     branch_grad = norm_back(normed_second, inverse_second, norm_gains[1], residual_grad).astype(
         jnp.bfloat16
@@ -311,9 +337,7 @@
     out_wgrad_rows = lax.dot_general(
         attn_rows, branch_grad, (((0,), (0,)), ((), ())), preferred_element_type=jnp.float32
     )
-    out_wgrad = lax.psum_scatter(
-        out_wgrad_rows.astype(jnp.bfloat16), "narrow", scatter_dimension=0, tiled=True
-    )
+    down_slots, out_slots = reduce_column_halves((down_wgrad_rows, out_wgrad_rows), core)
     qkv_grad = jnp.stack(
         [
             rotate_back(query_grad, cos_table, sine_table),
@@ -335,6 +359,7 @@
         scatter_dimension=0,
         tiled=True,
     ).astype(jnp.float32)
+    first_grad, qkv_wgrad, qkv_bgrad = lax.optimization_barrier((first_grad, qkv_wgrad, qkv_bgrad))
     input_grad = (
         residual_grad + norm_back(normed_first, inverse_first, norm_gains[0], first_grad)
     ).astype(jnp.bfloat16)
@@ -359,7 +384,7 @@
     weight_sums = (
         lax.psum(qkv_wgrad.astype(jnp.bfloat16), "wide").astype(jnp.float32),
         lax.psum(qkv_bgrad.astype(jnp.bfloat16), "wide").astype(jnp.float32),
-        lax.psum(out_wgrad, "wide").astype(jnp.float32),
+        lax.psum(out_slots, "wide").astype(jnp.float32),
         lax.psum(up_slots, "wide").astype(jnp.float32),
         None,
         lax.psum(down_slots, "wide").astype(jnp.float32),
@@ -371,12 +396,13 @@
     up_bgrad = lax.dynamic_slice_in_dim(small_sums[4], lax.axis_index("narrow") * units, units)
     up_wgrad = merge_slots(weight_sums[3], 0)
     down_wgrad = merge_slots(weight_sums[5], 1)
+    out_wgrad = merge_slots(weight_sums[2], 1)
     return (
         layer_out,
         input_grad,
         weight_sums[0],
         weight_sums[1],
-        weight_sums[2],
+        out_wgrad,
         small_sums[2],
         up_wgrad,
         up_bgrad,

time: 1050 us -> 955 us (0.910)
  waiting for transfers between devices: 538 us -> 305 us
  local copies, waits for them, and re-layouts: 121 us -> 203 us
  matrix products: 174 us -> 214 us
    all_gather x2, waiting for transfers between devices: 114 us -> 0.01 us  [gather_halves(): gathered = lax.all_gather(mine, 'narrow', axis=gather_axis, tiled=True)]
    psum x1, waiting for transfers between devices: 52.5 us -> 14.6 us  [shards(): lax.psum(qkv_wgrad.astype(jnp.bfloat16), 'wide').astype(jnp.float32)]
    all_to_all x1, waiting for transfers between devices: 40.5 us -> 6.28 us  [shards(): attn_grad = lax.all_to_all(attn_grad_rows, 'narrow', 1, 0, tiled=True)]
    unnamed x214 -> x247, local copies, waits for them, and re-layouts: 49.2 us -> 77.9 us
    all_gather x1, waiting for transfers between devices: 125 us -> 98.5 us  [shards(): gathered_first = lax.all_gather(low_first, 'narrow', axis=0, tiled=True)]
    dot_general x4 -> x8, matrix products: 11.6 us -> 37.2 us  [block_scores(): jnp.einsum('bqhd,bkhd->bhqk', query_block, key_block, preferred_element_t...]
    slice x2 -> x4, local copies, waits for them, and re-layouts: 19.6 us -> 39.3 us  [rotate(): front_half = vectors[..., :half_size]]
    ppermute x4 -> x5, waiting for transfers between devices: 14.3 us -> 0.01 us  [swap_cores(): lax.ppermute(block, 'wide', [(index, index ^ 1) for index in range(count)])]
  transfers between devices with their start and end apart: 15 -> 15, of which waited for: 10 -> 6; matrix products, arithmetic and copies ran while one was open for 33% -> 46% of each run, Pallas kernels for 0% -> 0%
where the time goes in v4:
time: 955 us; the launch traced here: 942 us
  waiting for transfers between devices  305 us (32%)
  matrix products  214 us (22%)
  local copies, waits for them, and re-layouts  203 us (21%)
  other arithmetic  116 us (12%)
  blocking collectives  76.4 us (8%)
  between operations  16.1 us (2%)
  starting transfers between devices  11.4 us (1%)
    reduce_scatter x1, waiting for transfers between devices, shards(): lax.psum_scatter(jnp.einsum('tse,tde->sd', rows_here, qkv_weight, preferr...  147 us
    all_gather x1, waiting for transfers between devices, shards(): gathered_first = lax.all_gather(low_first, 'narrow', axis=0, tiled=True)  98.5 us
    unnamed x247, local copies, waits for them, and re-layouts  77.9 us
    psum x1, blocking collectives, shards(): lax.psum((gain_local, bias_local, out_blocal, down_blocal, up_bgrad_rows)...  41.2 us
    slice x4, local copies, waits for them, and re-layouts, rotate(): front_half = vectors[..., :half_size]  39.3 us
    dot_general x8, matrix products, block_scores(): jnp.einsum('bqhd,bkhd->bhqk', query_block, key_block, preferred_element_t...  37.2 us
    reduce_scatter x1, waiting for transfers between devices, reduce_column_halves(): lax.psum_scatter(jnp.concatenate(pieces, axis=1), 'narrow', scatter_dimen...  37.1 us
    dot_general x4, matrix products, attend_backward(): jnp.einsum('bqhd,bkhd->bhqk', grad_block, value_block, preferred_element_...  29.3 us
  transfers between devices with their start and end apart: 15, of which 6 were waited for; matrix products, arithmetic and copies ran while one was open for 46% of the time, Pallas kernels for 0%

profile of v4, /device:TPU:0, one launch (start us, length us, event | category | flops | bytes accessed | tf_op | source)
XLA Modules:
  0.0 941.9 jit_solution(15028123445727380458)
XLA Ops:
  16.2 28.9 %all-gather = f32[8,1,512]{2,1,0:T(1,128)S(1)} all-gather(f32[1,1,512]{2,1,0:T(1,128)S(1)} %bitcast.179), channel_id=1, replica_groups=mesh['wide'=4,'narrow'=8] {'narrow'}, dimensions={0}, use_global_device_ids=true | all-gather | bytes 18432 | tf_op jit(solution)/shard_map/all_gather | solution.py:259
  45.1 98.5 %all-gather.6.cloned.1.call-done = bf16[4096,1024]{1,0:T(8,128)(2,1)} async-done(((bf16[512,1024]{1,0:T(8,128)(2,1)}), bf16[4096,1024]{1,0:T(8,128)(2,1)}) %all-gather.6.cloned.1.call-update) | async-done | bytes 8388624 | tf_op jit(solution)/shard_map/all_gather | solution.py:260
  151.3 7.5 add_bitcast_fusion.1
  162.2 3.9 reshape.431
  166.0 3.5 copy.138
  169.5 5.8 reshape.432
  175.4 3.8 reshape.433
  179.1 9.9 %fusion.194 = (f32[2,2048,2,32]{3,2,1,0:T(2,128)}, f32[2,2048,2,32]{3,2,1,0:T(2,128)}) fusion(f32[2,2048,2,64]{3,2,1,0:T(2,128)} %reshape.433), kind=kLoop, calls=%fused_computation.336 | loop fusion | bytes 4194304 | tf_op jit(solution)/shard_map/slice | solution.py:41
  189.0 6.4 copy.207
  195.4 6.4 copy.208
  201.8 10.0 %fusion.193 = (f32[2,2048,2,32]{3,2,1,0:T(2,128)}, f32[2,2048,2,32]{3,2,1,0:T(2,128)}) fusion(f32[2,2048,2,64]{3,2,1,0:T(2,128)} %reshape.432), kind=kLoop, calls=%fused_computation.335 | loop fusion | bytes 4194304 | tf_op jit(solution)/shard_map/slice | solution.py:41
  211.8 6.5 copy.205
  218.3 6.4 copy.206
  224.8 7.3 add_bitcast_fusion
  235.3 5.7 reshape.434
  241.0 3.6 reshape.435
  244.7 9.7 %fusion.192 = (f32[2,2048,2,32]{3,2,1,0:T(2,128)}, f32[2,2048,2,32]{3,2,1,0:T(2,128)}) fusion(f32[2,2048,2,64]{3,2,1,0:T(2,128)} %reshape.435), kind=kLoop, calls=%fused_computation.334 | loop fusion | bytes 4194304 | tf_op jit(solution)/shard_map/slice | solution.py:41
  254.4 6.4 copy.211
  260.8 6.4 copy.212
  267.2 9.8 %fusion.191 = (f32[2,2048,2,32]{3,2,1,0:T(2,128)}, f32[2,2048,2,32]{3,2,1,0:T(2,128)}) fusion(f32[2,2048,2,64]{3,2,1,0:T(2,128)} %reshape.434), kind=kLoop, calls=%fused_computation.333 | loop fusion | bytes 4194304 | tf_op jit(solution)/shard_map/slice | solution.py:41
  277.0 6.5 copy.209
  283.4 6.8 copy.210
  290.3 4.9 subtract_convert_fusion.3
  303.9 3.5 exponential_reduce_fusion.1
  310.7 4.3 fusion.100
  315.0 4.2 fusion
  319.1 4.3 exponential_reduce_fusion
  325.4 5.5 fusion.99
  336.9 4.5 all-to-all-start
  345.1 5.9 copy.161
  351.0 4.7 fusion.177
  358.4 8.2 fusion.110
  373.9 3.9 broadcast_select_fusion.3
  377.9 10.1 %multiply_convert_fusion.3 = (bf16[512,4096]{1,0:T(8,128)(2,1)}, f32[512,4096]{1,0:T(8,128)}) fusion(f32[4096]{0:T(1024)S(1)} %bitcast.173, bf16[512,4096]{1,0:T(8,128)(2,1)} %get-tuple-element.109, bf16[512,4096]{1,0:T(8,128)(2,1)S(1)} %get-tuple-element.108, f32[512,1024]{1,0:T(8,128)S(1)} %get-tuple-element.105, f32[1024]{0:T(1024)S(1)} %bitcast.175, ...), kind=kOutput, calls=%fused_computation.39 | convolution fusion | flops 4326948864 | bytes 23097344 | tf_op jit(solution)/shard_map/dot_general | solution.py:279
  388.0 5.5 broadcast_select_fusion.1
  393.6 9.3 add_reduce_fusion
  407.8 13.0 %convert_reduce_fusion = (f32[4096]{0:T(1024)}, bf16[512,4096]{1,0:T(8,128)(2,1)}) fusion(f32[512,4096]{1,0:T(8,128)} %get-tuple-element.174, f32[4096]{0:T(1024)S(1)} %bitcast.174, bf16[512,1024]{1,0:T(8,128)(2,1)S(1)} %get-tuple-element.100, bf16[4096,512]{1,0:T(8,128)(2,1)} %get-tuple-element.107, bf16[4096,512]{1,0:T(8,128)(2,1)} %get-tuple-element.106), kind=kOutput, calls=%fused_computation.31 | convolution fusion | flops 4339003392 | bytes 22052864 | tf_op jit(solution)/shard_map/dot_general | solution.py:309
  420.8 9.1 multiply_reduce_fusion.5
  429.8 10.7 %fusion.186 = f32[1024,4096]{1,0:T(8,128)} fusion(bf16[512,4096]{1,0:T(8,128)(2,1)} %get-tuple-element.187, f32[512,1024]{1,0:T(8,128)S(1)} %get-tuple-element.105, f32[1024]{0:T(1024)S(1)} %bitcast.176, f32[1024]{0:T(1024)S(1)} %bitcast.162, f32[512]{0:T(512)S(1)} %add_rsqrt_fusion.1, f32[512]{0:T(512)S(1)} %broadcast_multiply_fusion.9), kind=kOutput, calls=%fused_computation.329 | convolution fusion | flops 4297588736 | bytes 23080960 | tf_op jit(solution)/shard_map/dot_general | solution.py:314
  443.5 6.8 dynamic-slice_convert_fusion
  455.3 5.0 all-to-all-start.1
  465.6 4.7 fusion.198
  474.0 3.3 copy-done.34
  480.3 6.3 all-to-all-done.1
  494.4 6.4 fusion.107
  500.7 8.1 add_convert_fusion
  509.8 4.2 fusion.88
  514.0 12.4 %multiply_reduce_fusion.1 = (f32[2,2,512]{2,1,0:T(2,128)}, f32[2,2,512,1536]{3,2,1,0:T(8,128)}) fusion(f32[2,2,512,1536]{3,2,1,0:T(8,128)} %fusion.107, f32[2,2,512]{2,1,0:T(2,128)S(1)} %log_add_fusion.1, bf16[2,2048,2,32]{1,3,2,0:T(8,128)(2,1)S(1)} %get-tuple-element.126, bf16[2,2048,2,32]{1,3,2,0:T(8,128)(2,1)S(1)} %get-tuple-element.127, ...), kind=kOutput, calls=%fused_computation.9 | convolution fusion | flops 420476928 | bytes 28065792 | tf_op jit(solution)/shard_map/bqhd,bkhd->bhqk/dot_general | solution.py:97
  526.4 7.2 fusion.40
  533.7 6.0 fusion.82
  539.7 7.5 fusion.51
  547.2 4.7 copy.189
  553.9 3.9 multiply_reduce_fusion.3
  571.5 6.2 add_convert_fusion.1
  581.3 9.4 multiply_convert_fusion.1
  596.1 15.8 %multiply_reduce_fusion = (f32[2,2,512]{2,1,0:T(2,128)}, f32[2,2,512,2048]{3,2,1,0:T(8,128)}) fusion(f32[2,2,512,2048]{3,2,1,0:T(8,128)} %fusion.110, f32[2,2,512]{2,1,0:T(2,128)S(1)} %copy-done.78, pred[512,2048]{1,0:T(8,128)(4,1)} %copy-done.18, bf16[2,2048,2,64]{1,3,2,0:T(8,128)(2,1)} %copy.161, bf16[2,512,2,64]{1,0,3,2:T(2,128)(2,1)} %get-tuple-element.138), kind=kOutput, calls=%fused_computation.2 | convolution fusion | flops 557840384 | bytes 35930112 | tf_op jit(solution)/shard_map/bqhd,bkhd->bhqk/dot_general | solution.py:141
  612.3 8.5 multiply_convert_fusion
  645.3 6.9 bitcast_convert_fusion
  654.8 8.7 fusion.79
  665.6 37.1 %reduce-scatter.6.cloned.1.call-done = bf16[1,640,512]{2,1,0:T(8,128)(2,1)} async-done(((bf16[8,640,512]{2,1,0:T(8,128)(2,1)}), bf16[1,640,512]{2,1,0:T(8,128)(2,1)}) %reduce-scatter.6.cloned.1.call-update) | async-done | bytes 655376 | tf_op jit(solution)/shard_map/reduce_scatter | solution.py:211
  706.9 146.6 %reduce-scatter.4.cloned.1.call-done = bf16[512,1024]{1,0:T(8,128)(2,1)} async-done(((bf16[4096,1024]{1,0:T(8,128)(2,1)}), bf16[512,1024]{1,0:T(8,128)(2,1)}) %reduce-scatter.4.cloned.1.call-update) | async-done | bytes 1048592 | tf_op jit(solution)/shard_map/reduce_scatter | solution.py:354
  856.3 6.3 psum.71
  865.9 41.2 %all-reduce.6 = (f32[1024]{0:T(1024)}, f32[4096]{0:T(1024)S(1)}, f32[1024]{0:T(1024)}, f32[4,1024]{1,0:T(4,128)}, f32[4,1024]{1,0:T(4,128)}) all-reduce(f32[1024]{0:T(1024)S(1)} %copy-done.95, f32[4096]{0:T(1024)S(1)} %copy-done.94, f32[1024]{0:T(1024)S(1)} %copy-done.88, ...), channel_id=1, replica_groups=mesh['wide'=4,'narrow'=8] {'wide','narrow'}, use_global_device_ids=true, to_apply=%region_37.38 | all-reduce | flops 14336 | bytes 114688 | tf_op jit(solution)/shard_map/psum | solution.py:392
  911.1 14.6 %all-reduce.10.cloned.1.call-done = (bf16[3,1024,128]{1,2,0:T(8,128)(2,1)}, bf16[128,1024]{1,0:T(8,128)(2,1)}, bf16[1024,512]{1,0:T(8,128)(2,1)}, bf16[512,1024]{1,0:T(8,128)(2,1)}) async-done(((bf16[3,1024,128]{1,2,0:T(8,128)(2,1)}, bf16[128,1024]{1,0:T(8,128)(2,1)}, bf16[1024,512]{1,0:T(8,128)(2,1)}, bf16[512,1024]{1,0:T(8,128)(2,1)}), (bf16[3,1024,128]{1,2,0:T(8,128)(2,1)}, bf16[128,1024]{1,0:T(8,128)(2,1)}, ...) | async-done | bytes 3145744 | tf_op jit(solution)/shard_map/psum | solution.py:385
  (388 shorter events, 166.8 us)
Async XLA Ops:
  7.2 136.5 %copy-start = (bf16[1024,512]{1,0:T(8,128)(2,1)S(1)}, bf16[1024,512]{1,0:T(8,128)(2,1)}, u32[]{:S(2)}) copy-start(bf16[1024,512]{1,0:T(8,128)(2,1)} %param.22) | copy-start | bytes 3145732
  7.2 137.3 %copy-start.72 = (bf16[512,1024]{1,0:T(8,128)(2,1)S(1)}, bf16[512,1024]{1,0:T(8,128)(2,1)}, u32[]{:S(2)}) copy-start(bf16[512,1024]{1,0:T(8,128)(2,1)} %param.24) | copy-start | bytes 3145732
  7.2 136.4 %all-gather.6.cloned.1.call-start = ((), (), s32[]{:S(2)}) async-start(), calls=%async_computation.5 | async-start | bytes 9437184 | tf_op jit(solution)/shard_map/all_gather | solution.py:260
  8.8 138.5 %copy-start.81 = (f32[512]{0:T(512)}, f32[512]{0:T(512)S(1)}, u32[]{:S(2)}) copy-start(f32[512]{0:T(512)S(1)} %broadcast_multiply_fusion.11) | copy-start | bytes 6148
  10.5 140.1 %copy-start.86 = (f32[512]{0:T(512)}, f32[512]{0:T(512)S(1)}, u32[]{:S(2)}) copy-start(f32[512]{0:T(512)S(1)} %add_rsqrt_fusion.3) | copy-start | bytes 6148
  12.0 138.6 %copy-start.79 = (f32[1,1024]{1,0:T(1,128)}, f32[1,1024]{1,0:T(1,128)S(1)}, u32[]{:S(2)}) copy-start(f32[1,1024]{1,0:T(1,128)S(1)} %get-tuple-element.155) | copy-start | bytes 12292
  16.1 135.2 %copy-start.101 = (bf16[3,1024,128]{2,1,0:T(8,128)(2,1)S(1)}, bf16[3,1024,128]{2,1,0:T(8,128)(2,1)}, u32[]{:S(2)}) copy-start(bf16[3,1024,128]{2,1,0:T(8,128)(2,1)} %param.18) | copy-start | bytes 2359300
  16.1 135.2 %copy-start.104 = (f32[3,128]{1,0:T(4,128)S(1)}, f32[3,128]{1,0:T(4,128)}, u32[]{:S(2)}) copy-start(f32[3,128]{1,0:T(4,128)} %param.19) | copy-start | bytes 4612
  16.1 314.7 %all-gather.10.cloned.1.call-start = ((), (), s32[]{:S(2)}) async-start(), calls=%async_computation.7 | async-start | bytes 4718592 | tf_op jit(solution)/shard_map/all_gather | solution.py:181
  144.5 222.1 %all-gather.12.cloned.1.call-start = ((), (), s32[]{:S(2)}) async-start(), calls=%async_computation.8 | async-start | bytes 4718592 | tf_op jit(solution)/shard_map/all_gather | solution.py:181
  145.4 221.6 %all-gather.8.cloned.1.call-start = ((), (), s32[]{:S(2)}) async-start(), calls=%async_computation.6 | async-start | bytes 2359296 | tf_op jit(solution)/shard_map/all_gather | solution.py:270
  146.1 363.2 %copy-start.30 = (pred[512,512]{0,1:T(8,128)(4,1)}, pred[512,512]{0,1:T(8,128)(4,1)S(1)}, u32[]{:S(2)}) copy-start(pred[512,512]{0,1:T(8,128)(4,1)S(1)} %iota_compare_fusion.3) | copy-start | bytes 786436
  151.3 174.1 %copy-start.18 = (pred[512,2048]{1,0:T(8,128)(4,1)}, pred[512,2048]{1,0:T(8,128)(4,1)S(1)}, u32[]{:S(2)}) copy-start(pred[512,2048]{1,0:T(8,128)(4,1)S(1)} %iota_compare_fusion) | copy-start | bytes 3145732
  211.8 12.9 %copy-start.102 = (bf16[3,1024,128]{2,1,0:T(8,128)(2,1)S(1)}, bf16[3,1024,128]{2,1,0:T(8,128)(2,1)}, u32[]{:S(2)}) copy-start(bf16[3,1024,128]{2,1,0:T(8,128)(2,1)} %param.18) | copy-start | bytes 2359300
  295.2 218.7 %copy-start.8 = (bf16[2,2048,2,32]{1,3,2,0:T(8,128)(2,1)}, bf16[2,2048,2,32]{1,3,2,0:T(8,128)(2,1)S(1)}, u32[]{:S(2)}) copy-start(bf16[2,2048,2,32]{1,3,2,0:T(8,128)(2,1)S(1)} %get-tuple-element.149) | copy-start | bytes 1572868
  295.2 218.7 %copy-start.10 = (bf16[2,2048,2,32]{1,3,2,0:T(8,128)(2,1)}, bf16[2,2048,2,32]{1,3,2,0:T(8,128)(2,1)S(1)}, u32[]{:S(2)}) copy-start(bf16[2,2048,2,32]{1,3,2,0:T(8,128)(2,1)S(1)} %get-tuple-element.150) | copy-start | bytes 1572868
  295.2 218.7 %copy-start.12 = (bf16[2,2048,2,32]{1,3,2,0:T(8,128)(2,1)}, bf16[2,2048,2,32]{1,3,2,0:T(8,128)(2,1)S(1)}, u32[]{:S(2)}) copy-start(bf16[2,2048,2,32]{1,3,2,0:T(8,128)(2,1)S(1)} %get-tuple-element.126) | copy-start | bytes 1572868
  295.2 218.7 %copy-start.15 = (bf16[2,2048,2,32]{1,3,2,0:T(8,128)(2,1)}, bf16[2,2048,2,32]{1,3,2,0:T(8,128)(2,1)S(1)}, u32[]{:S(2)}) copy-start(bf16[2,2048,2,32]{1,3,2,0:T(8,128)(2,1)S(1)} %get-tuple-element.127) | copy-start | bytes 1572868
  297.1 212.2 %copy-start.75 = (f32[2,2,512]{2,1,0:T(2,128)}, f32[2,2,512]{2,1,0:T(2,128)S(1)}, u32[]{:S(2)}) copy-start(f32[2,2,512]{2,1,0:T(2,128)S(1)} %log_add_fusion.3) | copy-start | bytes 24580
  330.9 42.1 %collective-permute-start = (bf16[512,4096]{1,0:T(8,128)(2,1)}, bf16[512,4096]{1,0:T(8,128)(2,1)}, u32[]{:S(2)}, u32[]{:S(2)}) collective-permute-start(bf16[512,4096]{1,0:T(8,128)(2,1)} %all-gather.10.cloned.1.call-done), channel_id=1, source_target_pairs={{0,8},{8,0},{16,24},{24,16},{1,9},{9,1},{17,25},{25,17},{2,10},{10... | collective-permute-start | bytes 12582920 | tf_op jit(solution)/shard_map/ppermute | solution.py:175
  332.2 9.2 copy-start.99
  332.2 9.3 copy-start.100
  336.9 31.2 %all-to-all-start = ((bf16[8,512,128]{1,2,0:T(8,128)(2,1)}), bf16[8,512,128]{1,2,0:T(8,128)(2,1)}, u32[]{:S(2)}, u32[]{:S(2)}) async-start(bf16[8,512,128]{1,2,0:T(8,128)(2,1)} %copy.150), calls=%async_computation | async-start | bytes 2097152 | tf_op jit(solution)/shard_map/all_to_all | solution.py:269
  358.4 9.7 %copy-start.71 = (f32[1024]{0:T(1024)S(1)}, f32[1024]{0:T(1024)}, u32[]{:S(2)}) copy-start(f32[1024]{0:T(1024)} %param.21) | copy-start | bytes 12292
  366.6 21.5 %collective-permute-start.1 = (bf16[4096,512]{1,0:T(8,128)(2,1)}, bf16[4096,512]{1,0:T(8,128)(2,1)}, u32[]{:S(2)}, u32[]{:S(2)}) collective-permute-start(bf16[4096,512]{1,0:T(8,128)(2,1)} %all-gather.12.cloned.1.call-done), channel_id=1, source_target_pairs={{0,8},{8,0},{16,24},{24,16},{1,9},{9,1},{17,25},{25,17},{2,10},{10... | collective-permute-start | bytes 12582920 | tf_op jit(solution)/shard_map/ppermute | solution.py:175
  377.9 10.2 %copy-start.39 = (bf16[4096,512]{1,0:T(8,128)(2,1)S(1)}, bf16[4096,512]{1,0:T(8,128)(2,1)}, u32[]{:S(2)}) copy-start(bf16[4096,512]{1,0:T(8,128)(2,1)} %all-gather.12.cloned.1.call-done) | copy-start | bytes 12582916
  393.6 9.7 %copy-start.35 = (bf16[512,1024]{1,0:T(8,128)(2,1)S(1)}, bf16[512,1024]{1,0:T(8,128)(2,1)}, u32[]{:S(2)}) copy-start(bf16[512,1024]{1,0:T(8,128)(2,1)} %param.15) | copy-start | bytes 3145732
  393.6 9.7 %copy-start.84 = (f32[1,1024]{1,0:T(1,128)S(1)}, f32[1,1024]{1,0:T(1,128)}, u32[]{:S(2)}) copy-start(f32[1,1024]{1,0:T(1,128)} %get-tuple-element.156) | copy-start | bytes 12292
  407.8 13.0 %copy-start.66 = (bf16[512,1024]{1,0:T(8,128)(2,1)}, bf16[512,1024]{1,0:T(8,128)(2,1)S(1)}, u32[]{:S(2)}) copy-start(bf16[512,1024]{1,0:T(8,128)(2,1)S(1)} %get-tuple-element.100) | copy-start | bytes 3145732
  407.8 13.0 %copy-start.41 = (bf16[512,4096]{1,0:T(8,128)(2,1)S(1)}, bf16[512,4096]{1,0:T(8,128)(2,1)}, u32[]{:S(2)}) copy-start(bf16[512,4096]{1,0:T(8,128)(2,1)} %get-tuple-element.109) | copy-start | bytes 12582916
  429.8 10.7 %copy-start.54 = (f32[512,1024]{1,0:T(8,128)S(1)}, f32[512,1024]{1,0:T(8,128)}, u32[]{:S(2)}) copy-start(f32[512,1024]{1,0:T(8,128)} %get-tuple-element.177) | copy-start | bytes 6291460
  450.3 50.4 %collective-permute-start.4 = (bf16[512,4096]{1,0:T(8,128)(2,1)}, bf16[512,4096]{1,0:T(8,128)(2,1)}, u32[]{:S(2)}, u32[]{:S(2)}) collective-permute-start(bf16[512,4096]{1,0:T(8,128)(2,1)} %dynamic-slice_convert_fusion), channel_id=1, source_target_pairs={{0,8},{8,0},{16,24},{24,16},{1,9},{9,1},{17,25},{25,17},{2,10},{10... | collective-permute-start | bytes 12582920 | tf_op jit(solution)/shard_map/ppermute | solution.py:175
  455.3 31.3 %all-to-all-start.1 = ((bf16[512,8,128]{0,2,1:T(8,128)(2,1)}), bf16[512,8,128]{0,2,1:T(8,128)(2,1)}, u32[]{:S(2)}, u32[]{:S(2)}) async-start(bf16[512,8,128]{0,2,1:T(8,128)(2,1)} %bitcast.20), calls=%async_computation.1 | async-start | bytes 2097152 | tf_op jit(solution)/shard_map/all_to_all | solution.py:332
  460.3 203.2 %reduce-scatter.8.cloned.1.call-start = ((), (), s32[]{:S(2)}) async-start(), calls=%async_computation.11 | async-start | bytes 4718592 | tf_op jit(solution)/shard_map/reduce_scatter | solution.py:193
  465.6 8.4 collective-permute-start.3
  473.5 98.0 %collective-permute-start.2 = (bf16[4096,512]{1,0:T(8,128)(2,1)}, bf16[4096,512]{1,0:T(8,128)(2,1)}, u32[]{:S(2)}, u32[]{:S(2)}) collective-permute-start(bf16[4096,512]{1,0:T(8,128)(2,1)} %dynamic-slice_convert_fusion.1), channel_id=1, source_target_pairs={{0,8},{8,0},{16,24},{24,16},{1,9},{9,1},{17,25},{25,17},{2,10},{10... | collective-permute-start | bytes 12582920 | tf_op jit(solution)/shard_map/ppermute | solution.py:175
  480.3 14.0 %copy-start.28 = (bf16[2,2048,2,64]{1,3,2,0:T(8,128)(2,1)S(1)}, bf16[2,2048,2,64]{1,3,2,0:T(8,128)(2,1)}, u32[]{:S(2)}) copy-start(bf16[2,2048,2,64]{1,3,2,0:T(8,128)(2,1)} %copy.161) | copy-start | bytes 3145732
  508.8 193.9 %reduce-scatter.6.cloned.1.call-start = ((), (), s32[]{:S(2)}) async-start(), calls=%async_computation.10 | async-start | bytes 5898240 | tf_op jit(solution)/shard_map/reduce_scatter | solution.py:211
  514.0 12.4 %copy-start.48 = (bf16[2,512,2,64]{1,0,3,2:T(2,128)(2,1)S(1)}, bf16[2,512,2,64]{1,0,3,2:T(2,128)(2,1)}, u32[]{:S(2)}) copy-start(bf16[2,512,2,64]{1,0,3,2:T(2,128)(2,1)} %copy-done.47) | copy-start | bytes 786436
  514.0 25.7 %slice-start = ((s8[16777216]{0:T(1024)(128)(4,1)}), s8[4194304]{0:T(1024)(128)(4,1)S(1)}, s32[]{:S(2)}) async-start(s8[16777216]{0:T(1024)(128)(4,1)} %bitcast.139), calls=%async_computation.13 | async-start | bytes 8388608
  514.0 25.7 %slice-start.1 = ((s8[16777216]{0:T(1024)(128)(4,1)}), s8[4194304]{0:T(1024)(128)(4,1)S(1)}, s32[]{:S(2)}) async-start(s8[16777216]{0:T(1024)(128)(4,1)} %bitcast.139), calls=%async_computation.14 | async-start | bytes 8388608
  514.0 25.7 %slice-start.2 = ((s8[16777216]{0:T(1024)(128)(4,1)}), s8[4194304]{0:T(1024)(128)(4,1)S(1)}, s32[]{:S(2)}) async-start(s8[16777216]{0:T(1024)(128)(4,1)} %bitcast.139), calls=%async_computation.15 | async-start | bytes 8388608
  526.4 13.3 %slice-start.3 = ((s8[16777216]{0:T(1024)(128)(4,1)}), s8[4194304]{0:T(1024)(128)(4,1)S(1)}, s32[]{:S(2)}) async-start(s8[16777216]{0:T(1024)(128)(4,1)} %bitcast.139), calls=%async_computation.16 | async-start | bytes 8388608
  580.6 272.9 %reduce-scatter.4.cloned.1.call-start = ((), (), s32[]{:S(2)}) async-start(), calls=%async_computation.9 | async-start | bytes 9437184 | tf_op jit(solution)/shard_map/reduce_scatter | solution.py:354
  593.3 18.7 %slice-start.4 = ((s8[16777216]{0:T(1024)(128)(4,1)}), s8[4194304]{0:T(1024)(128)(4,1)S(1)}, s32[]{:S(2)}) async-start(s8[16777216]{0:T(1024)(128)(4,1)} %bitcast.141), calls=%async_computation.17 | async-start | bytes 8388608
  596.1 15.9 %slice-start.5 = ((s8[16777216]{0:T(1024)(128)(4,1)}), s8[4194304]{0:T(1024)(128)(4,1)S(1)}, s32[]{:S(2)}) async-start(s8[16777216]{0:T(1024)(128)(4,1)} %bitcast.141), calls=%async_computation.18 | async-start | bytes 8388608
  596.1 15.9 %slice-start.6 = ((s8[16777216]{0:T(1024)(128)(4,1)}), s8[4194304]{0:T(1024)(128)(4,1)S(1)}, s32[]{:S(2)}) async-start(s8[16777216]{0:T(1024)(128)(4,1)} %bitcast.141), calls=%async_computation.19 | async-start | bytes 8388608
  596.1 15.9 %slice-start.7 = ((s8[16777216]{0:T(1024)(128)(4,1)}), s8[4194304]{0:T(1024)(128)(4,1)S(1)}, s32[]{:S(2)}) async-start(s8[16777216]{0:T(1024)(128)(4,1)} %bitcast.141), calls=%async_computation.20 | async-start | bytes 8388608
  596.1 16.2 %copy-start.20 = (pred[512,2048]{1,0:T(8,128)(4,1)S(1)}, pred[512,2048]{1,0:T(8,128)(4,1)}, u32[]{:S(2)}) copy-start(pred[512,2048]{1,0:T(8,128)(4,1)} %copy-done.18) | copy-start | bytes 3145732
  652.2 273.4 %all-reduce.10.cloned.1.call-start = ((), (), s32[]{:S(2)}) async-start(), calls=%async_computation.12 | async-start | bytes 6291456 | tf_op jit(solution)/shard_map/psum | solution.py:385
  705.7 157.5 %copy-start.5 = (bf16[512,1024]{1,0:T(8,128)(2,1)S(1)}, bf16[512,1024]{1,0:T(8,128)(2,1)}, u32[]{:S(2)}) copy-start(bf16[512,1024]{1,0:T(8,128)(2,1)} %param.14) | copy-start | bytes 3145732
  705.7 157.5 %copy-start.80 = (f32[1,1024]{1,0:T(1,128)S(1)}, f32[1,1024]{1,0:T(1,128)}, u32[]{:S(2)}) copy-start(f32[1,1024]{1,0:T(1,128)} %copy-done.79) | copy-start | bytes 12292
  705.7 157.5 %copy-start.82 = (f32[512]{0:T(512)S(1)}, f32[512]{0:T(512)}, u32[]{:S(2)}) copy-start(f32[512]{0:T(512)} %copy-done.81) | copy-start | bytes 6148
  705.7 157.5 %copy-start.87 = (f32[512]{0:T(512)S(1)}, f32[512]{0:T(512)}, u32[]{:S(2)}) copy-start(f32[512]{0:T(512)} %copy-done.86) | copy-start | bytes 6148
  706.8 158.9 %copy-start.91 = (f32[1024]{0:T(1024)S(1)}, f32[1024]{0:T(1024)}, u32[]{:S(2)}) copy-start(f32[1024]{0:T(1024)} %get-tuple-element.74) | copy-start | bytes 12292
  706.8 158.9 %copy-start.93 = (f32[1024]{0:T(1024)S(1)}, f32[1024]{0:T(1024)}, u32[]{:S(2)}) copy-start(f32[1024]{0:T(1024)} %get-tuple-element.78) | copy-start | bytes 12292
  706.8 158.9 %copy-start.97 = (f32[1024]{0:T(1024)S(1)}, f32[1024]{0:T(1024)}, u32[]{:S(2)}) copy-start(f32[1024]{0:T(1024)} %get-tuple-element.76) | copy-start | bytes 12292
  706.8 158.9 %copy-start.90 = (f32[1024]{0:T(1024)S(1)}, f32[1024]{0:T(1024)}, u32[]{:S(2)}) copy-start(f32[1024]{0:T(1024)} %get-tuple-element.86) | copy-start | bytes 12292
  706.9 158.9 %copy-start.92 = (f32[1024]{0:T(1024)S(1)}, f32[1024]{0:T(1024)}, u32[]{:S(2)}) copy-start(f32[1024]{0:T(1024)} %get-tuple-element.89) | copy-start | bytes 12292
  706.9 158.9 %copy-start.96 = (f32[1024]{0:T(1024)S(1)}, f32[1024]{0:T(1024)}, u32[]{:S(2)}) copy-start(f32[1024]{0:T(1024)} %get-tuple-element.87) | copy-start | bytes 12292
  706.9 159.0 %copy-start.88 = (f32[1024]{0:T(1024)S(1)}, f32[1024]{0:T(1024)}, u32[]{:S(2)}) copy-start(f32[1024]{0:T(1024)} %get-tuple-element.99) | copy-start | bytes 12292
  706.9 159.0 %copy-start.94 = (f32[4096]{0:T(1024)S(1)}, f32[4096]{0:T(1024)}, u32[]{:S(2)}) copy-start(f32[4096]{0:T(1024)} %get-tuple-element.186) | copy-start | bytes 49156
  706.9 159.0 %copy-start.95 = (f32[1024]{0:T(1024)S(1)}, f32[1024]{0:T(1024)}, u32[]{:S(2)}) copy-start(f32[1024]{0:T(1024)} %get-tuple-element.101) | copy-start | bytes 12292
  706.9 200.9 %copy-start.22 = (f32[512,1024]{1,0:T(8,128)S(1)}, f32[512,1024]{1,0:T(8,128)}, u32[]{:S(2)}) copy-start(f32[512,1024]{1,0:T(8,128)} %copy-done.21) | copy-start | bytes 6291460
  (69 other events, 301.9 us)
Sparse Core Ops, SparseCore 0:
  16.2 127.3 all-gather.5
  146.2 72.8 all-gather.9
  221.2 70.9 all-gather.11
  294.2 47.3 all-gather.7
  509.0 87.6 reduce-scatter.7
  600.1 102.6 reduce-scatter.5
  706.4 147.0 reduce-scatter.3
  856.7 68.9 all-reduce.9

commit v5 on v4

--- a/solution.py
+++ b/solution.py
@@ -175,10 +175,17 @@
     return lax.ppermute(block, "wide", [(index, index ^ 1) for index in range(count)])
 
 
-def gather_halves(shard, core, split_axis, gather_axis):
+def gather_mine(shard, core, split_axis, gather_axis):
     half = shard.shape[split_axis] // 2
     mine = lax.dynamic_slice_in_dim(shard, core * half, half, axis=split_axis)
-    gathered = lax.all_gather(mine, "narrow", axis=gather_axis, tiled=True)
+    return lax.all_gather(mine, "narrow", axis=gather_axis, tiled=True)
+
+
+def gather_halves(shard, core, split_axis, gather_axis):
+    return join_halves(gather_mine(shard, core, split_axis, gather_axis), core, split_axis)
+
+
+def join_halves(gathered, core, split_axis):
     partner = swap_cores(gathered)
     first = jnp.where(core == 0, gathered, partner)
     second = jnp.where(core == 0, partner, gathered)
@@ -256,14 +263,38 @@
     layer_in = tokens.astype(jnp.float32)
     normed_first, inverse_first = norm_stats(layer_in)
     low_first = (normed_first * norm_gains[0] + norm_biases[0]).astype(jnp.bfloat16)
-    up_bias_full = lax.all_gather(up_bias, "narrow", axis=0, tiled=True)
-    gathered_first = lax.all_gather(low_first, "narrow", axis=0, tiled=True)
-    gathered_first, up_weight, down_weight, up_bias_full = lax.optimization_barrier(
-        (gathered_first, up_weight, down_weight, up_bias_full)
-    )
-    query, key_rows, values = project_qkv(
-        gathered_first, qkv_weight, qkv_bias, cos_table, sine_table, seq_count, length
-    )
+    core = lax.axis_index("wide") % 2
+    model = layer_in.shape[1]
+    heads_here = inner // HEAD
+    bias_flat = jnp.concatenate([qkv_bias.reshape(-1), up_bias])
+    bias_full = lax.all_gather(bias_flat, "narrow", axis=0)
+    qkv_gathered = gather_mine(qkv_weight, core, 1, 2)
+    qkv_gathered, up_weight, down_weight, bias_full = lax.optimization_barrier(
+        (qkv_gathered, up_weight, down_weight, bias_full)
+    )
+    qkv_full = join_halves(qkv_gathered, core, 1)
+    qkv_bias_full = jnp.swapaxes(bias_full[:, : 3 * inner].reshape(-1, 3, inner), 0, 1).reshape(
+        3, model
+    )
+    up_bias_full = bias_full[:, 3 * inner :].reshape(-1)
+    position_start = first_row % length
+    cos_rows = lax.dynamic_slice_in_dim(cos_table, position_start, shard_rows, 0)
+    sine_rows = lax.dynamic_slice_in_dim(sine_table, position_start, shard_rows, 0)
+    qkv_rows = (
+        jnp.einsum("sd,tde->tse", low_first, qkv_full, preferred_element_type=jnp.float32)
+        + qkv_bias_full[:, None, :]
+    )
+    shaped = qkv_rows.reshape(3, shard_rows, model // HEAD, HEAD)
+    qkv_tok = jnp.stack(
+        [
+            rotate(shaped[0], cos_rows, sine_rows),
+            rotate(shaped[1], cos_rows, sine_rows),
+            shaped[2],
+        ]
+    ).astype(jnp.bfloat16)
+    qkv_heads = lax.all_to_all(qkv_tok, "narrow", 2, 1, tiled=True)
+    qkv_heads = qkv_heads.reshape(3, seq_count, length, heads_here, HEAD)
+    query, key_rows, values = qkv_heads[0], qkv_heads[1], qkv_heads[2]
     attn_heads, totals = attend_forward(query, key_rows, values, block_rows)
     attn_low = attn_heads.reshape(group_rows, inner).astype(jnp.bfloat16)
     attn_rows = lax.all_to_all(attn_low, "narrow", 0, 1, tiled=True)
@@ -273,7 +304,6 @@
     residual = layer_in + normed_second * norm_gains[1] + norm_biases[1]
     normed_third, inverse_third = norm_stats(residual)
     low_third = (normed_third * norm_gains[2] + norm_biases[2]).astype(jnp.bfloat16)
-    core = lax.axis_index("wide") % 2
     up_full = gather_halves(up_weight, core, 0, 1)
     down_full = gather_halves(down_weight, core, 1, 0)
     hidden = jnp.dot(low_third, up_full, preferred_element_type=jnp.float32) + up_bias_full
@@ -322,10 +352,6 @@
     branch_grad = norm_back(normed_second, inverse_second, norm_gains[1], residual_grad).astype(
         jnp.bfloat16
     )
-    gathered_first = lax.all_gather(low_first, "narrow", axis=0, tiled=True)
-    query, key_rows, values = project_qkv(
-        gathered_first, qkv_weight, qkv_bias, cos_table, sine_table, seq_count, length
-    )
     attn_grad_rows = lax.dot_general(
         branch_grad, out_full, (((1,), (1,)), ((), ())), preferred_element_type=jnp.float32
     ).astype(jnp.bfloat16)
@@ -347,19 +373,16 @@
     )
     qkv_grad = qkv_grad.reshape(3, group_rows, inner).astype(jnp.bfloat16)
     qkv_bgrad = jnp.sum(qkv_grad.astype(jnp.float32), axis=1)
-    qkv_wgrad = jnp.einsum(
-        "sd,tse->tde", gathered_first, qkv_grad, preferred_element_type=jnp.float32
-    )
-    rows_here = qkv_grad
-    first_grad = lax.psum_scatter(
-        jnp.einsum("tse,tde->sd", rows_here, qkv_weight, preferred_element_type=jnp.float32).astype(
-            jnp.bfloat16
-        ),
-        "narrow",
-        scatter_dimension=0,
-        tiled=True,
-    ).astype(jnp.float32)
-    first_grad, qkv_wgrad, qkv_bgrad = lax.optimization_barrier((first_grad, qkv_wgrad, qkv_bgrad))
+    qkv_grad_rows = lax.all_to_all(
+        qkv_grad.reshape(3, group_rows, heads_here, HEAD), "narrow", 1, 2, tiled=True
+    ).reshape(3, shard_rows, model)
+    qkv_wgrad_rows = jnp.einsum(
+        "sd,tse->tde", low_first, qkv_grad_rows, preferred_element_type=jnp.float32
+    )
+    first_grad = jnp.einsum(
+        "tse,tde->sd", qkv_grad_rows, qkv_full, preferred_element_type=jnp.float32
+    )
+    qkv_slots = reduce_halves(qkv_wgrad_rows, core, 1, 2)
     input_grad = (
         residual_grad + norm_back(normed_first, inverse_first, norm_gains[0], first_grad)
     ).astype(jnp.bfloat16)
@@ -382,7 +405,7 @@
     out_blocal = jnp.sum(branch_grad.astype(jnp.float32), axis=0)
     down_blocal = jnp.sum(mlp_grad.astype(jnp.float32), axis=0)
     weight_sums = (
-        lax.psum(qkv_wgrad.astype(jnp.bfloat16), "wide").astype(jnp.float32),
+        lax.psum(qkv_slots, "wide").astype(jnp.float32),
         lax.psum(qkv_bgrad.astype(jnp.bfloat16), "wide").astype(jnp.float32),
         lax.psum(out_slots, "wide").astype(jnp.float32),
         lax.psum(up_slots, "wide").astype(jnp.float32),
@@ -397,10 +420,11 @@
     up_wgrad = merge_slots(weight_sums[3], 0)
     down_wgrad = merge_slots(weight_sums[5], 1)
     out_wgrad = merge_slots(weight_sums[2], 1)
+    qkv_wgrad = merge_slots(weight_sums[0], 1)
     return (
         layer_out,
         input_grad,
-        weight_sums[0],
+        qkv_wgrad,
         weight_sums[1],
         out_wgrad,
         small_sums[2],

time: 955 us -> 949 us (level)
  blocking collectives: 76.4 us -> 198 us
  local copies, waits for them, and re-layouts: 203 us -> 132 us
  matrix products: 214 us -> 177 us
  waiting for transfers between devices: 305 us -> 285 us
    reduce_scatter x1 -> x0, waiting for transfers between devices: 147 us -> none  [shards(): lax.psum_scatter(jnp.einsum('tse,tde->sd', rows_here, qkv_weight, preferr...]
    all_to_all x0 -> x1, blocking collectives: none -> 116 us  [shards(): lax.all_to_all(qkv_grad.reshape(3, group_rows, heads_here, HEAD), 'narrow...]
    reduce_scatter x1 -> x2, waiting for transfers between devices: 0.01 us -> 59.3 us  [reduce_halves(): lax.psum_scatter(chip_sum.astype(jnp.bfloat16), 'narrow', scatter_dimensi...]
    all_gather x1, waiting for transfers between devices: 0.01 us -> 55.1 us  [shards(): out_full = lax.all_gather(out_weight, 'narrow', axis=0, tiled=True)]
    unnamed x247 -> x223, local copies, waits for them, and re-layouts: 77.9 us -> 26.4 us
    all_gather x3, waiting for transfers between devices: 98.5 us -> 139 us  [gather_mine(): return lax.all_gather(mine, 'narrow', axis=gather_axis, tiled=True)]
    reduce_scatter x1, waiting for transfers between devices: 37.1 us -> 0.01 us  [reduce_column_halves(): lax.psum_scatter(jnp.concatenate(pieces, axis=1), 'narrow', scatter_dimen...]
    slice x8 -> x7, local copies, waits for them, and re-layouts: 46.2 us -> 12.1 us  [the longest x4 8.7 us: shards(): query, key_rows, values = (qkv_heads[0], qkv_heads[1], qkv_heads[2])]
  transfers between devices with their start and end apart: 15 -> 18, of which waited for: 6 -> 8; matrix products, arithmetic and copies ran while one was open for 46% -> 36% of each run, Pallas kernels for 0% -> 0%
where the time goes in v5:
time: 949 us; the launch traced here: 938 us
  waiting for transfers between devices  285 us (30%)
  blocking collectives  198 us (21%)
  matrix products  177 us (19%)
  local copies, waits for them, and re-layouts  132 us (14%)
  other arithmetic  116 us (12%)
  between operations  16.1 us (2%)
  starting transfers between devices  14.8 us (2%)
    all_gather x3, waiting for transfers between devices, gather_mine(): return lax.all_gather(mine, 'narrow', axis=gather_axis, tiled=True)  139 us
    all_to_all x1, blocking collectives, shards(): lax.all_to_all(qkv_grad.reshape(3, group_rows, heads_here, HEAD), 'narrow...  116 us
    reduce_scatter x2, waiting for transfers between devices, reduce_halves(): lax.psum_scatter(chip_sum.astype(jnp.bfloat16), 'narrow', scatter_dimensi...  59.3 us
    all_gather x1, waiting for transfers between devices, shards(): out_full = lax.all_gather(out_weight, 'narrow', axis=0, tiled=True)  55.1 us
    psum x1, blocking collectives, shards(): lax.psum((gain_local, bias_local, out_blocal, down_blocal, up_bgrad_rows)...  41.9 us
    all_gather x1, blocking collectives, shards(): bias_full = lax.all_gather(bias_flat, 'narrow', axis=0)  32.8 us
    dot_general x4, matrix products, attend_backward(): jnp.einsum('bqhd,bkhd->bhqk', grad_block, value_block, preferred_element_...  28.5 us
    unnamed x223, local copies, waits for them, and re-layouts  26.4 us
  transfers between devices with their start and end apart: 18, of which 8 were waited for; matrix products, arithmetic and copies ran while one was open for 36% of the time, Pallas kernels for 0%

profile of v5, /device:TPU:0, one launch (start us, length us, event | category | flops | bytes accessed | tf_op | source)
XLA Modules:
  0.0 938.5 jit_solution(6358795677307603225)
XLA Ops:
  10.2 32.8 %all-gather.1 = f32[8,1,896]{2,1,0:T(1,128)S(1)} all-gather(f32[1,1,896]{2,1,0:T(1,128)S(1)} %reshape.456), channel_id=2, replica_groups=mesh['wide'=4,'narrow'=8] {'narrow'}, dimensions={0}, use_global_device_ids=true | all-gather | bytes 32256 | tf_op jit(solution)/shard_map/all_gather | solution.py:270
  43.0 30.6 %all-gather.7.cloned.1.call-done = bf16[3,512,1024]{1,2,0:T(8,128)(2,1)} async-done(((bf16[3,512,128]{1,2,0:T(8,128)(2,1)}), bf16[3,512,1024]{1,2,0:T(8,128)(2,1)}) %all-gather.7.cloned.1.call-update) | async-done | bytes 3145744 | tf_op jit(solution)/shard_map/all_gather | solution.py:181
  80.6 3.6 broadcast_select_fusion.5
  84.3 3.7 add_bitcast_fusion
  91.4 4.5 all-to-all-start
  98.9 108.8 %all-gather.11.cloned.1.call-done = bf16[512,4096]{1,0:T(8,128)(2,1)} async-done(((bf16[512,512]{1,0:T(8,128)(2,1)}), bf16[512,4096]{1,0:T(8,128)(2,1)}) %all-gather.11.cloned.1.call-update) | async-done | bytes 4194320 | tf_op jit(solution)/shard_map/all_gather | solution.py:181
  215.6 2.7 copy.170
  218.3 2.8 copy.167
  223.3 2.8 fusion.126
  226.1 2.8 copy.165
  242.9 3.5 exponential_reduce_fusion.1
  246.4 3.4 fusion.52
  249.9 4.3 fusion.54
  254.1 4.9 fusion
  259.1 4.6 exponential_reduce_fusion
  264.8 7.1 fusion.55
  281.1 4.5 all-to-all-start.1
  286.4 55.1 %all-gather.9.cloned.1.call-done = bf16[1024,1024]{1,0:T(8,128)(2,1)} async-done(((bf16[128,1024]{1,0:T(8,128)(2,1)}), bf16[1024,1024]{1,0:T(8,128)(2,1)}) %all-gather.9.cloned.1.call-update) | async-done | bytes 2097168 | tf_op jit(solution)/shard_map/all_gather | solution.py:301
  341.5 3.3 add_reduce_fusion.1
  347.3 3.8 broadcast_select_fusion.3
  351.2 10.1 %multiply_convert_fusion.3 = (bf16[512,4096]{1,0:T(8,128)(2,1)}, f32[512,4096]{1,0:T(8,128)}) fusion(f32[4096]{0:T(1024)S(1)} %bitcast.235, bf16[512,4096]{1,0:T(8,128)(2,1)} %get-tuple-element.55, bf16[512,4096]{1,0:T(8,128)(2,1)S(1)} %get-tuple-element.54, f32[512,1024]{1,0:T(8,128)S(1)} %get-tuple-element.51, f32[1024]{0:T(1024)S(1)} %bitcast.245, ...), kind=kOutput, calls=%fused_computation.29 | convolution fusion | flops 4326948864 | bytes 23097344 | tf_op jit(solution)/shard_map/dot_general | solution.py:309
  361.3 5.2 broadcast_select_fusion.1
  366.4 9.3 add_reduce_fusion
  377.9 2.7 convert_reduce_fusion.2
  380.6 12.7 %convert_reduce_fusion = (f32[4096]{0:T(1024)}, bf16[512,4096]{1,0:T(8,128)(2,1)}) fusion(f32[512,4096]{1,0:T(8,128)} %get-tuple-element.113, f32[4096]{0:T(1024)S(1)} %bitcast.236, bf16[512,1024]{1,0:T(8,128)(2,1)S(1)} %get-tuple-element.46, bf16[4096,512]{1,0:T(8,128)(2,1)} %get-tuple-element.53, bf16[4096,512]{1,0:T(8,128)(2,1)} %get-tuple-element.52), kind=kOutput, calls=%fused_computation.22 | convolution fusion | flops 4339003392 | bytes 22052864 | tf_op jit(solution)/shard_map/dot_general | solution.py:339
  393.3 10.3 %multiply_reduce_fusion.5 = (f32[1024]{0:T(1024)}, f32[512]{0:T(512)S(1)}, f32[512]{0:T(512)S(1)}, f32[1024]{0:T(1024)}, f32[512,1024]{1,0:T(8,128)}) fusion(f32[512,1024]{1,0:T(8,128)S(1)} %get-tuple-element.51, f32[512]{0:T(512)S(1)} %add_rsqrt_fusion.1, f32[512]{0:T(512)S(1)} %broadcast_multiply_fusion.9, f32[1024]{0:T(1024)S(1)} %bitcast.227, ...), kind=kOutput, calls=%fused_computation.102 | convolution fusion | flops 4316460032 | bytes 16797696 | tf_op jit(solution)/shard_map/dot_general | solution.py:347
  403.6 10.7 %fusion.120 = f32[1024,4096]{1,0:T(8,128)} fusion(bf16[512,4096]{1,0:T(8,128)(2,1)} %get-tuple-element.127, f32[512,1024]{1,0:T(8,128)S(1)} %get-tuple-element.51, f32[1024]{0:T(1024)S(1)} %bitcast.246, f32[1024]{0:T(1024)S(1)} %bitcast.228, f32[512]{0:T(512)S(1)} %add_rsqrt_fusion.1, f32[512]{0:T(512)S(1)} %broadcast_multiply_fusion.9), kind=kOutput, calls=%fused_computation.279 | convolution fusion | flops 4297588736 | bytes 23080960 | tf_op jit(solution)/shard_map/dot_general | solution.py:344
  414.2 8.2 fusion.129
  422.4 3.1 multiply_reduce_fusion.6
  430.6 4.2 all-to-all-start.2
  434.9 2.8 fusion.130
  438.0 6.1 dynamic-slice_convert_fusion
  444.6 5.9 dynamic-slice_convert_fusion.1
  451.9 8.0 all-to-all-done.2
  459.9 2.8 copy.184
  467.0 6.2 multiply_reduce_fusion.2
  484.0 7.0 multiply_reduce_fusion.1
  492.3 7.2 multiply_convert_fusion.1
  500.8 2.8 fusion.47
  503.6 13.8 %multiply_reduce_fusion = (f32[2,2,512]{2,1,0:T(2,128)S(1)}, f32[2,2,512,2048]{3,2,1,0:T(8,128)}) fusion(f32[2,2,512,2048]{3,2,1,0:T(8,128)} %copy-done.2, f32[2,2,512]{2,1,0:T(2,128)S(1)} %log_add_fusion, pred[512,2048]{1,0:T(8,128)(4,1)S(1)} %iota_compare_fusion, bf16[2,2048,2,64]{1,0,3,2:T(2,128)(2,1)S(1)} %copy-done.18, ...), kind=kOutput, calls=%fused_computation.1 | convolution fusion | flops 557840384 | bytes 35930112 | tf_op jit(solution)/shard_map/bqhd,bkhd->bhqk/dot_general | solution.py:141
  517.3 8.1 add_convert_fusion
  525.6 12.7 %multiply_convert_fusion = bf16[2,2,512,2048]{3,2,1,0:T(8,128)(2,1)S(1)} fusion(f32[2,2,512,2048]{3,2,1,0:T(8,128)} %get-tuple-element.118, f32[2,2,512,2048]{3,2,1,0:T(8,128)} %copy-done.2, f32[2,2,512]{2,1,0:T(2,128)S(1)} %get-tuple-element.117, f32[2,2,512]{2,1,0:T(2,128)S(1)} %log_add_fusion, pred[512,2048]{1,0:T(8,128)(4,1)S(1)} %iota_compare_fusion), kind=kLoop, calls=%fused_computation | loop fusion | flops 25165824 | bytes 43008000 | tf_op jit(solution)/shard_map/convert_element_type | solution.py:145
  538.3 2.7 fusion.48
  550.2 3.3 convolution_bitcast_fusion.2
  553.6 6.1 convolution_bitcast_fusion.1
  559.7 7.7 fusion.24
  567.5 6.3 add_convert_fusion.1
  573.8 2.9 pad_maximum_fusion.7
  588.2 3.8 pad_maximum_fusion.11
  592.0 14.5 %copy.197 = bf16[3,4096,2,64]{3,2,0,1:T(2,128)(2,1)} copy(bf16[3,4096,2,64]{1,3,2,0:T(8,128)(2,1)} %pad_maximum_fusion.11) | data formatting | bytes 6291456 | tf_op jit(solution)/shard_map/stack | solution.py:367
  606.5 8.9 reshape.461
  615.5 116.3 %all_to_all.62 = bf16[8,2,98304]{2,1,0:T(2,128)(2,1)} all-to-all(bf16[8,2,98304]{2,1,0:T(2,128)(2,1)} %reshape.461), channel_id=1, replica_groups=mesh['wide'=4,'narrow'=8] {'narrow'}, dimensions={0} | all-to-all | bytes 6291456 | tf_op jit(solution)/shard_map/all_to_all | solution.py:376
  731.7 8.7 reshape.462
  740.5 15.5 %copy.216 = bf16[3,8,512,2,64]{2,4,3,1,0:T(8,128)(2,1)} copy(bf16[3,8,512,2,64]{4,3,0,2,1:T(2,128)(2,1)} %bitcast.204) | data formatting | bytes 6291456 | tf_op jit(solution)/shard_map/all_to_all | solution.py:376
  756.0 5.5 fusion.69
  762.1 5.6 collective-permute-done.3
  767.7 2.7 fusion.11
  777.3 6.9 psum.71
  791.0 59.3 %reduce-scatter.4.cloned.1.call-done = bf16[3,512,128]{1,2,0:T(8,128)(2,1)} async-done(((bf16[3,512,1024]{1,2,0:T(8,128)(2,1)}), bf16[3,512,128]{1,2,0:T(8,128)(2,1)}) %reduce-scatter.4.cloned.1.call-update) | async-done | bytes 393232 | tf_op jit(solution)/shard_map/reduce_scatter | solution.py:200
  852.8 9.0 fusion.39
  861.9 41.9 %all-reduce.6 = (f32[1024]{0:T(1024)}, f32[4096]{0:T(1024)S(1)}, f32[1024]{0:T(1024)}, f32[4,1024]{1,0:T(4,128)}, f32[4,1024]{1,0:T(4,128)}) all-reduce(f32[1024]{0:T(1024)S(1)} %copy-done.80, f32[4096]{0:T(1024)S(1)} %copy-done.77, f32[1024]{0:T(1024)S(1)} %copy-done.69, ...), channel_id=1, replica_groups=mesh['wide'=4,'narrow'=8] {'wide','narrow'}, use_global_device_ids=true, to_apply=%region_37.38 | all-reduce | flops 14336 | bytes 114688 | tf_op jit(solution)/shard_map/psum | solution.py:415
  904.5 3.3 fusion.38
  907.8 14.7 %all-reduce.10.cloned.1.call-done = (bf16[3,1024,128]{2,1,0:T(8,128)(2,1)}, bf16[128,1024]{1,0:T(8,128)(2,1)}, bf16[1024,512]{1,0:T(8,128)(2,1)}, bf16[512,1024]{1,0:T(8,128)(2,1)}) async-done(((bf16[3,1024,128]{2,1,0:T(8,128)(2,1)}, bf16[128,1024]{1,0:T(8,128)(2,1)}, bf16[1024,512]{1,0:T(8,128)(2,1)}, bf16[512,1024]{1,0:T(8,128)(2,1)}), (bf16[3,1024,128]{2,1,0:T(8,128)(2,1)}, bf16[128,1024]{1,0:T(8,128)(2,1)}, ...) | async-done | bytes 3145744 | tf_op jit(solution)/shard_map/psum | solution.py:408
  926.8 2.8 reshape.452
  (379 shorter events, 124.6 us)
Async XLA Ops:
  7.2 66.5 %copy-start = (bf16[1024,512]{1,0:T(8,128)(2,1)S(1)}, bf16[1024,512]{1,0:T(8,128)(2,1)}, u32[]{:S(2)}) copy-start(bf16[1024,512]{1,0:T(8,128)(2,1)} %param.22) | copy-start | bytes 3145732
  7.2 67.5 %copy-start.11 = (bf16[512,1024]{1,0:T(8,128)(2,1)S(1)}, bf16[512,1024]{1,0:T(8,128)(2,1)}, u32[]{:S(2)}) copy-start(bf16[512,1024]{1,0:T(8,128)(2,1)} %param.14) | copy-start | bytes 3145732
  7.2 70.1 %copy-start.78 = (f32[4,1024]{1,0:T(4,128)S(1)}, f32[4,1024]{1,0:T(4,128)}, u32[]{:S(2)}) copy-start(f32[4,1024]{1,0:T(4,128)} %param.26) | copy-start | bytes 49156
  7.2 70.7 %copy-start.79 = (f32[4,1024]{1,0:T(4,128)S(1)}, f32[4,1024]{1,0:T(4,128)}, u32[]{:S(2)}) copy-start(f32[4,1024]{1,0:T(4,128)} %param.27) | copy-start | bytes 49156
  7.2 66.4 %all-gather.7.cloned.1.call-start = ((), (), s32[]{:S(2)}) async-start(), calls=%async_computation.7 | async-start | bytes 3538944 | tf_op jit(solution)/shard_map/all_gather | solution.py:181
  9.4 66.9 %copy-start.59 = (bf16[512,1024]{1,0:T(8,128)(2,1)S(1)}, bf16[512,1024]{1,0:T(8,128)(2,1)}, u32[]{:S(2)}) copy-start(bf16[512,1024]{1,0:T(8,128)(2,1)} %param.24) | copy-start | bytes 3145732
  9.4 198.3 %all-gather.11.cloned.1.call-start = ((), (), s32[]{:S(2)}) async-start(), calls=%async_computation.9 | async-start | bytes 4718592 | tf_op jit(solution)/shard_map/all_gather | solution.py:181
  74.5 211.3 %all-gather.13.cloned.1.call-start = ((), (), s32[]{:S(2)}) async-start(), calls=%async_computation.10 | async-start | bytes 4718592 | tf_op jit(solution)/shard_map/all_gather | solution.py:181
  74.5 6.1 collective-permute-start
  74.9 9.4 copy-start.67
  76.3 7.9 copy-start.39
  76.3 7.9 copy-start.41
  91.4 116.3 %all-to-all-start = ((bf16[3,512,16,64]{1,3,0,2:T(8,128)(2,1)}), bf16[3,512,16,64]{1,3,0,2:T(8,128)(2,1)}, u32[]{:S(2)}, u32[]{:S(2)}) async-start(bf16[3,512,16,64]{1,3,0,2:T(8,128)(2,1)} %pad_maximum_fusion.10), calls=%async_computation | async-start | bytes 6291456 | tf_op jit(solution)/shard_map/all_to_all | solution.py:295
  95.9 245.6 %all-gather.9.cloned.1.call-start = ((), (), s32[]{:S(2)}) async-start(), calls=%async_computation.8 | async-start | bytes 2359296 | tf_op jit(solution)/shard_map/all_gather | solution.py:301
  98.3 394.1 %copy-start.8 = (pred[512,1536]{1,0:T(8,128)(4,1)}, pred[512,1536]{1,0:T(8,128)(4,1)S(1)}, u32[]{:S(2)}) copy-start(pred[512,1536]{1,0:T(8,128)(4,1)S(1)} %iota_compare_fusion.1) | copy-start | bytes 2359300
  207.7 138.7 %collective-permute-start.1 = (bf16[512,4096]{1,0:T(8,128)(2,1)}, bf16[512,4096]{1,0:T(8,128)(2,1)}, u32[]{:S(2)}, u32[]{:S(2)}) collective-permute-start(bf16[512,4096]{1,0:T(8,128)(2,1)} %all-gather.11.cloned.1.call-done), channel_id=1, source_target_pairs={{0,8},{8,0},{16,24},{24,16},{1,9},{9,1},{17,25},{25,17},{2,10},{10... | collective-permute-start | bytes 12582920 | tf_op jit(solution)/shard_map/ppermute | solution.py:175
  232.7 17.2 %copy-start.22 = (bf16[2,2048,2,64]{1,3,2,0:T(8,128)(2,1)}, bf16[2,2048,2,64]{1,3,2,0:T(8,128)(2,1)S(1)}, u32[]{:S(2)}) copy-start(bf16[2,2048,2,64]{1,3,2,0:T(8,128)(2,1)S(1)} %copy.166) | copy-start | bytes 3145732
  235.1 36.8 %copy-start.5 = (f32[2,2,512,512]{2,3,1,0:T(8,128)}, f32[2,2,512,512]{2,3,1,0:T(8,128)S(1)}, u32[]{:S(2)}) copy-start(f32[2,2,512,512]{2,3,1,0:T(8,128)S(1)} %get-tuple-element.109) | copy-start | bytes 12582916
  237.8 8.6 copy-start.4
  246.4 245.9 %copy-start.63 = (f32[2,2,512]{2,1,0:T(2,128)}, f32[2,2,512]{2,1,0:T(2,128)S(1)}, u32[]{:S(2)}) copy-start(f32[2,2,512]{2,1,0:T(2,128)S(1)} %log_add_fusion.1) | copy-start | bytes 24580
  264.8 260.7 %copy-start.64 = (f32[2,2,512]{2,1,0:T(2,128)}, f32[2,2,512]{2,1,0:T(2,128)S(1)}, u32[]{:S(2)}) copy-start(f32[2,2,512]{2,1,0:T(2,128)S(1)} %log_add_fusion) | copy-start | bytes 24580
  274.4 11.2 %copy-start.90 = (s32[2]{0:T(128)S(1)}, s32[2]{0:T(128)}, u32[]{:S(2)}) copy-start(s32[2]{0:T(128)} %param.16) | copy-start | bytes 28
  274.4 11.3 %copy-start.91 = (f32[8]{0:T(128)S(1)}, f32[8]{0:T(128)}, u32[]{:S(2)}) copy-start(f32[8]{0:T(128)} %param.17) | copy-start | bytes 100
  274.4 67.1 %copy-start.58 = (f32[1024]{0:T(1024)S(1)}, f32[1024]{0:T(1024)}, u32[]{:S(2)}) copy-start(f32[1024]{0:T(1024)} %param.21) | copy-start | bytes 12292
  281.1 60.4 %all-to-all-start.1 = ((bf16[8,512,128]{1,2,0:T(8,128)(2,1)}), bf16[8,512,128]{1,2,0:T(8,128)(2,1)}, u32[]{:S(2)}, u32[]{:S(2)}) async-start(bf16[8,512,128]{1,2,0:T(8,128)(2,1)} %copy.182), calls=%async_computation.1 | async-start | bytes 2097152 | tf_op jit(solution)/shard_map/all_to_all | solution.py:300
  285.5 59.6 %copy-start.76 = (f32[1,1024]{1,0:T(1,128)S(1)}, f32[1,1024]{1,0:T(1,128)}, u32[]{:S(2)}) copy-start(f32[1,1024]{1,0:T(1,128)} %get-tuple-element.97) | copy-start | bytes 12292
  285.8 75.5 %collective-permute-start.2 = (bf16[4096,512]{1,0:T(8,128)(2,1)}, bf16[4096,512]{1,0:T(8,128)(2,1)}, u32[]{:S(2)}, u32[]{:S(2)}) collective-permute-start(bf16[4096,512]{1,0:T(8,128)(2,1)} %all-gather.13.cloned.1.call-done), channel_id=1, source_target_pairs={{0,8},{8,0},{16,24},{24,16},{1,9},{9,1},{17,25},{25,17},{2,10},{10... | collective-permute-start | bytes 12582920 | tf_op jit(solution)/shard_map/ppermute | solution.py:175
  351.2 10.1 %copy-start.25 = (bf16[4096,512]{1,0:T(8,128)(2,1)S(1)}, bf16[4096,512]{1,0:T(8,128)(2,1)}, u32[]{:S(2)}) copy-start(bf16[4096,512]{1,0:T(8,128)(2,1)} %all-gather.13.cloned.1.call-done) | copy-start | bytes 12582916
  366.4 9.7 %copy-start.16 = (bf16[512,1024]{1,0:T(8,128)(2,1)S(1)}, bf16[512,1024]{1,0:T(8,128)(2,1)}, u32[]{:S(2)}) copy-start(bf16[512,1024]{1,0:T(8,128)(2,1)} %param.15) | copy-start | bytes 3145732
  403.6 10.7 %copy-start.92 = (bf16[512,4096]{1,0:T(8,128)(2,1)S(1)}, bf16[512,4096]{1,0:T(8,128)(2,1)}, u32[]{:S(2)}) copy-start(bf16[512,4096]{1,0:T(8,128)(2,1)} %get-tuple-element.112) | copy-start | bytes 12582916
  414.2 8.2 copy-start.33
  430.6 29.2 %all-to-all-start.2 = ((bf16[512,8,128]{0,2,1:T(8,128)(2,1)}), bf16[512,8,128]{0,2,1:T(8,128)(2,1)}, u32[]{:S(2)}, u32[]{:S(2)}) async-start(bf16[512,8,128]{0,2,1:T(8,128)(2,1)} %bitcast.29), calls=%async_computation.2 | async-start | bytes 2097152 | tf_op jit(solution)/shard_map/all_to_all | solution.py:358
  434.9 349.9 %reduce-scatter.8.cloned.1.call-start = ((), (), s32[]{:S(2)}) async-start(), calls=%async_computation.13 | async-start | bytes 4718592 | tf_op jit(solution)/shard_map/reduce_scatter | solution.py:200
  437.9 12.6 %collective-permute-start.5 = (bf16[1024,512]{1,0:T(8,128)(2,1)S(1)}, bf16[1024,512]{1,0:T(8,128)(2,1)S(1)}, u32[]{:S(2)}, u32[]{:S(2)}) collective-permute-start(bf16[1024,512]{1,0:T(8,128)(2,1)S(1)} %dynamic-slice_convert_fusion.3), channel_id=1, source_target_pairs={{0,8},{8,0},{16,24},{24,16},{1,9},{9,1},{17,25},{25,17},{2,10},{10... | collective-permute-start | bytes 3145736 | tf_op jit(solution)/shard_map/ppermute | solution.py:175
  444.1 73.3 %collective-permute-start.6 = (bf16[512,4096]{1,0:T(8,128)(2,1)}, bf16[512,4096]{1,0:T(8,128)(2,1)}, u32[]{:S(2)}, u32[]{:S(2)}) collective-permute-start(bf16[512,4096]{1,0:T(8,128)(2,1)} %dynamic-slice_convert_fusion), channel_id=1, source_target_pairs={{0,8},{8,0},{16,24},{24,16},{1,9},{9,1},{17,25},{25,17},{2,10},{10... | collective-permute-start | bytes 12582920 | tf_op jit(solution)/shard_map/ppermute | solution.py:175
  450.5 117.0 %collective-permute-start.4 = (bf16[4096,512]{1,0:T(8,128)(2,1)}, bf16[4096,512]{1,0:T(8,128)(2,1)}, u32[]{:S(2)}, u32[]{:S(2)}) collective-permute-start(bf16[4096,512]{1,0:T(8,128)(2,1)} %dynamic-slice_convert_fusion.1), channel_id=1, source_target_pairs={{0,8},{8,0},{16,24},{24,16},{1,9},{9,1},{17,25},{25,17},{2,10},{10... | collective-permute-start | bytes 12582920 | tf_op jit(solution)/shard_map/ppermute | solution.py:175
  451.9 15.2 %copy-start.14 = (pred[512,1024]{1,0:T(8,128)(4,1)S(1)}, pred[512,1024]{1,0:T(8,128)(4,1)}, u32[]{:S(2)}) copy-start(pred[512,1024]{1,0:T(8,128)(4,1)} %iota_compare_fusion.2) | copy-start | bytes 1572868
  467.0 12.1 %copy-start.53 = (bf16[2,512,2,64]{1,0,3,2:T(2,128)(2,1)}, bf16[2,512,2,64]{1,0,3,2:T(2,128)(2,1)S(1)}, u32[]{:S(2)}) copy-start(bf16[2,512,2,64]{1,0,3,2:T(2,128)(2,1)S(1)} %get-tuple-element.75) | copy-start | bytes 786436
  467.0 16.9 %copy-start.44 = (bf16[2,512,2,64]{1,0,3,2:T(2,128)(2,1)}, bf16[2,512,2,64]{1,0,3,2:T(2,128)(2,1)S(1)}, u32[]{:S(2)}) copy-start(bf16[2,512,2,64]{1,0,3,2:T(2,128)(2,1)S(1)} %get-tuple-element.73) | copy-start | bytes 786436
  467.0 36.6 %copy-start.43 = (bf16[2,512,2,64]{1,0,3,2:T(2,128)(2,1)}, bf16[2,512,2,64]{1,0,3,2:T(2,128)(2,1)S(1)}, u32[]{:S(2)}) copy-start(bf16[2,512,2,64]{1,0,3,2:T(2,128)(2,1)S(1)} %get-tuple-element.72) | copy-start | bytes 786436
  525.5 261.4 %reduce-scatter.6.cloned.1.call-start = ((), (), s32[]{:S(2)}) async-start(), calls=%async_computation.12 | async-start | bytes 5898240 | tf_op jit(solution)/shard_map/reduce_scatter | solution.py:218
  525.6 12.7 %copy-start.17 = (bf16[2,2048,2,64]{1,0,3,2:T(2,128)(2,1)S(1)}, bf16[2,2048,2,64]{1,0,3,2:T(2,128)(2,1)}, u32[]{:S(2)}) copy-start(bf16[2,2048,2,64]{1,0,3,2:T(2,128)(2,1)} %squeeze.20) | copy-start | bytes 3145732
  541.1 12.5 %slice-start.7 = ((s8[12582912]{0:T(1024)(128)(4,1)}), s8[4194304]{0:T(1024)(128)(4,1)S(1)}, s32[]{:S(2)}) async-start(s8[12582912]{0:T(1024)(128)(4,1)} %bitcast.197), calls=%async_computation.22 | async-start | bytes 8388608
  542.8 10.8 %slice-start.8 = ((s8[12582912]{0:T(1024)(128)(4,1)}), s8[4194304]{0:T(1024)(128)(4,1)S(1)}, s32[]{:S(2)}) async-start(s8[12582912]{0:T(1024)(128)(4,1)} %bitcast.197), calls=%async_computation.23 | async-start | bytes 8388608
  550.2 9.5 %slice-start = ((s8[16777216]{0:T(1024)(128)(4,1)}), s8[4194304]{0:T(1024)(128)(4,1)S(1)}, s32[]{:S(2)}) async-start(s8[16777216]{0:T(1024)(128)(4,1)} %bitcast.193), calls=%async_computation.15 | async-start | bytes 8388608
  550.2 9.5 %slice-start.1 = ((s8[16777216]{0:T(1024)(128)(4,1)}), s8[4194304]{0:T(1024)(128)(4,1)S(1)}, s32[]{:S(2)}) async-start(s8[16777216]{0:T(1024)(128)(4,1)} %bitcast.193), calls=%async_computation.16 | async-start | bytes 8388608
  576.7 273.7 %reduce-scatter.4.cloned.1.call-start = ((), (), s32[]{:S(2)}) async-start(), calls=%async_computation.11 | async-start | bytes 3538944 | tf_op jit(solution)/shard_map/reduce_scatter | solution.py:200
  740.5 15.5 %copy-start.12 = (bf16[512,1024]{1,0:T(8,128)(2,1)S(1)}, bf16[512,1024]{1,0:T(8,128)(2,1)}, u32[]{:S(2)}) copy-start(bf16[512,1024]{1,0:T(8,128)(2,1)} %param.14) | copy-start | bytes 3145732
  740.5 15.5 %copy-start.68 = (f32[512]{0:T(512)S(1)}, f32[512]{0:T(512)}, u32[]{:S(2)}) copy-start(f32[512]{0:T(512)} %copy-done.67) | copy-start | bytes 6148
  740.5 15.5 %copy-start.82 = (f32[1,1024]{1,0:T(1,128)S(1)}, f32[1,1024]{1,0:T(1,128)}, u32[]{:S(2)}) copy-start(f32[1,1024]{1,0:T(1,128)} %copy-done.81) | copy-start | bytes 12292
  740.5 15.5 %copy-start.84 = (f32[512]{0:T(512)S(1)}, f32[512]{0:T(512)}, u32[]{:S(2)}) copy-start(f32[512]{0:T(512)} %copy-done.83) | copy-start | bytes 6148
  740.5 15.5 %copy-start.86 = (f32[1,1024]{1,0:T(1,128)S(1)}, f32[1,1024]{1,0:T(1,128)}, u32[]{:S(2)}) copy-start(f32[1,1024]{1,0:T(1,128)} %copy-done.85) | copy-start | bytes 12292
  762.0 5.7 collective-permute-start.3
  770.5 152.0 %all-reduce.10.cloned.1.call-start = ((), (), s32[]{:S(2)}) async-start(), calls=%async_computation.14 | async-start | bytes 6291456 | tf_op jit(solution)/shard_map/psum | solution.py:408
  852.7 9.2 copy-start.71
  852.7 9.1 copy-start.75
  852.7 9.1 copy-start.88
  852.7 9.2 copy-start.70
  852.7 9.2 copy-start.74
  852.7 9.2 copy-start.87
  852.7 9.2 copy-start.69
  852.7 9.2 copy-start.77
  852.7 9.2 copy-start.80
  852.8 51.7 %copy-start.10 = (f32[512,1024]{1,0:T(8,128)S(1)}, f32[512,1024]{1,0:T(8,128)}, u32[]{:S(2)}) copy-start(f32[512,1024]{1,0:T(8,128)} %copy-done.9) | copy-start | bytes 6291460
  (61 other events, 245.3 us)
Sparse Core Ops, SparseCore 0:
  10.8 62.7 all-gather.6
  76.2 131.4 all-gather.10
  209.8 69.9 all-gather.12
  281.8 59.5 all-gather.8
  525.6 86.9 reduce-scatter.7
  616.1 156.1 reduce-scatter.5
  775.9 74.3 reduce-scatter.3
  853.5 68.8 all-reduce.9

commit v6 on v5

--- a/solution.py
+++ b/solution.py
@@ -170,70 +170,77 @@
     )
 
 
-def swap_cores(block):
+def swap(block, bit):
     count = lax.axis_size("wide")
-    return lax.ppermute(block, "wide", [(index, index ^ 1) for index in range(count)])
-
-
-def gather_mine(shard, core, split_axis, gather_axis):
-    half = shard.shape[split_axis] // 2
-    mine = lax.dynamic_slice_in_dim(shard, core * half, half, axis=split_axis)
+    return lax.ppermute(block, "wide", [(index, index ^ bit) for index in range(count)])
+
+
+def order_pair(low_bit, mine, theirs, axis):
+    first = jnp.where(low_bit == 0, mine, theirs)
+    second = jnp.where(low_bit == 0, theirs, mine)
+    return jnp.concatenate([first, second], axis=axis)
+
+
+def gather_quarter(shard, core, pair, split_axis, gather_axis):
+    quarter = shard.shape[split_axis] // 4
+    mine = lax.dynamic_slice_in_dim(shard, (2 * core + pair) * quarter, quarter, axis=split_axis)
     return lax.all_gather(mine, "narrow", axis=gather_axis, tiled=True)
 
 
-def gather_halves(shard, core, split_axis, gather_axis):
-    return join_halves(gather_mine(shard, core, split_axis, gather_axis), core, split_axis)
-
-
-def join_halves(gathered, core, split_axis):
-    partner = swap_cores(gathered)
-    first = jnp.where(core == 0, gathered, partner)
-    second = jnp.where(core == 0, partner, gathered)
-    return jnp.concatenate([first, second], axis=split_axis)
-
-
-def reduce_halves(rows, core, split_axis, scatter_axis):
+def join_quarters(gathered, core, pair, split_axis):
+    half = order_pair(pair, gathered, swap(gathered, 2), split_axis)
+    return order_pair(core, half, swap(half, 1), split_axis)
+
+
+def reduce_quarters(rows, core, pair, split_axis):
     half = rows.shape[split_axis] // 2
     mine = lax.dynamic_slice_in_dim(rows, core * half, half, axis=split_axis)
     other = lax.dynamic_slice_in_dim(rows, (1 - core) * half, half, axis=split_axis)
-    chip_sum = mine + swap_cores(other.astype(jnp.bfloat16)).astype(jnp.float32)
+    chip_sum = mine + swap(other.astype(jnp.bfloat16), 1).astype(jnp.float32)
+    quarter = half // 2
+    keep = lax.dynamic_slice_in_dim(chip_sum, pair * quarter, quarter, axis=split_axis)
+    give = lax.dynamic_slice_in_dim(chip_sum, (1 - pair) * quarter, quarter, axis=split_axis)
+    return (keep + swap(give.astype(jnp.bfloat16), 2).astype(jnp.float32)).astype(jnp.bfloat16)
+
+
+def spread_quarters(part, core, pair, split_axis):
+    if lax.axis_size("wide") == 4:
+        return join_quarters(part, core, pair, split_axis).astype(jnp.float32)
+    slot = 2 * core + pair
+    empty = jnp.zeros_like(part)
+    slots = jnp.stack([jnp.where(slot == index, part, empty) for index in range(4)], axis=split_axis)
+    total = lax.psum(slots, "wide")
+    shape = list(part.shape)
+    shape[split_axis] *= 4
+    return total.reshape(shape).astype(jnp.float32)
+
+
+def reduce_weight(rows, core, pair, split_axis, scatter_axis):
     part = lax.psum_scatter(
-        chip_sum.astype(jnp.bfloat16), "narrow", scatter_dimension=scatter_axis, tiled=True
-    )
-    empty = jnp.zeros_like(part)
-    return jnp.stack(
-        [jnp.where(core == 0, part, empty), jnp.where(core == 0, empty, part)], axis=split_axis
-    )
-
-
-def reduce_column_halves(mats, core):
+        reduce_quarters(rows, core, pair, split_axis),
+        "narrow",
+        scatter_dimension=scatter_axis,
+        tiled=True,
+    )
+    return spread_quarters(part, core, pair, split_axis)
+
+
+def reduce_column_weights(mats, core, pair):
     count = lax.axis_size("narrow")
-    pieces = []
-    for rows in mats:
-        half = rows.shape[1] // 2
-        mine = lax.dynamic_slice_in_dim(rows, core * half, half, axis=1)
-        other = lax.dynamic_slice_in_dim(rows, (1 - core) * half, half, axis=1)
-        chip_sum = mine + swap_cores(other.astype(jnp.bfloat16)).astype(jnp.float32)
-        pieces.append(chip_sum.astype(jnp.bfloat16).reshape(count, -1, half))
+    pieces = [reduce_quarters(rows, core, pair, 1) for rows in mats]
     joined = lax.psum_scatter(
-        jnp.concatenate(pieces, axis=1), "narrow", scatter_dimension=0, tiled=True
+        jnp.concatenate([piece.reshape(count, -1, piece.shape[1]) for piece in pieces], axis=1),
+        "narrow",
+        scatter_dimension=0,
+        tiled=True,
     )[0]
     results = []
     start = 0
     for piece in pieces:
-        part = joined[start : start + piece.shape[1]]
-        start += piece.shape[1]
-        empty = jnp.zeros_like(part)
-        results.append(
-            jnp.stack([jnp.where(core == 0, part, empty), jnp.where(core == 0, empty, part)], axis=1)
-        )
+        rows_here = piece.shape[0] // count
+        results.append(spread_quarters(joined[start : start + rows_here], core, pair, 1))
+        start += rows_here
     return results
-
-
-def merge_slots(slots, split_axis):
-    shape = list(slots.shape)
-    shape[split_axis : split_axis + 2] = [shape[split_axis] * shape[split_axis + 1]]
-    return slots.reshape(shape)
 
 
 def shards(
@@ -268,11 +275,12 @@
     heads_here = inner // HEAD
     bias_flat = jnp.concatenate([qkv_bias.reshape(-1), up_bias])
     bias_full = lax.all_gather(bias_flat, "narrow", axis=0)
-    qkv_gathered = gather_mine(qkv_weight, core, 1, 2)
-    qkv_gathered, up_weight, down_weight, bias_full = lax.optimization_barrier(
-        (qkv_gathered, up_weight, down_weight, bias_full)
-    )
-    qkv_full = join_halves(qkv_gathered, core, 1)
+    pair = (lax.axis_index("wide") // 2) % 2
+    qkv_gathered = gather_quarter(qkv_weight, core, pair, 1, 2)
+    qkv_gathered, up_weight, down_weight, out_weight, bias_full = lax.optimization_barrier(
+        (qkv_gathered, up_weight, down_weight, out_weight, bias_full)
+    )
+    qkv_full = join_quarters(qkv_gathered, core, pair, 1)
     qkv_bias_full = jnp.swapaxes(bias_full[:, : 3 * inner].reshape(-1, 3, inner), 0, 1).reshape(
         3, model
     )
@@ -298,14 +306,14 @@
     attn_heads, totals = attend_forward(query, key_rows, values, block_rows)
     attn_low = attn_heads.reshape(group_rows, inner).astype(jnp.bfloat16)
     attn_rows = lax.all_to_all(attn_low, "narrow", 0, 1, tiled=True)
-    out_full = lax.all_gather(out_weight, "narrow", axis=0, tiled=True)
+    out_full = join_quarters(gather_quarter(out_weight, core, pair, 1, 0), core, pair, 1)
     pre_attn = jnp.dot(attn_rows, out_full, preferred_element_type=jnp.float32) + out_bias
     normed_second, inverse_second = norm_stats(pre_attn)
     residual = layer_in + normed_second * norm_gains[1] + norm_biases[1]
     normed_third, inverse_third = norm_stats(residual)
     low_third = (normed_third * norm_gains[2] + norm_biases[2]).astype(jnp.bfloat16)
-    up_full = gather_halves(up_weight, core, 0, 1)
-    down_full = gather_halves(down_weight, core, 1, 0)
+    up_full = join_quarters(gather_quarter(up_weight, core, pair, 0, 1), core, pair, 0)
+    down_full = join_quarters(gather_quarter(down_weight, core, pair, 1, 0), core, pair, 1)
     hidden = jnp.dot(low_third, up_full, preferred_element_type=jnp.float32) + up_bias_full
     act_low = gelu_value(hidden).astype(jnp.bfloat16)
     pre_mlp = jnp.dot(act_low, down_full, preferred_element_type=jnp.float32) + down_bias
@@ -347,7 +355,7 @@
     third_grad = lax.dot_general(
         hidden_grad, up_full, (((1,), (1,)), ((), ())), preferred_element_type=jnp.float32
     )
-    up_slots = reduce_halves(up_wgrad_rows, core, 0, 1)
+    up_wgrad = reduce_weight(up_wgrad_rows, core, pair, 0, 1)
     residual_grad = upstream + norm_back(normed_third, inverse_third, norm_gains[2], third_grad)
     branch_grad = norm_back(normed_second, inverse_second, norm_gains[1], residual_grad).astype(
         jnp.bfloat16
@@ -363,7 +371,7 @@
     out_wgrad_rows = lax.dot_general(
         attn_rows, branch_grad, (((0,), (0,)), ((), ())), preferred_element_type=jnp.float32
     )
-    down_slots, out_slots = reduce_column_halves((down_wgrad_rows, out_wgrad_rows), core)
+    down_wgrad, out_wgrad = reduce_column_weights((down_wgrad_rows, out_wgrad_rows), core, pair)
     qkv_grad = jnp.stack(
         [
             rotate_back(query_grad, cos_table, sine_table),
@@ -382,7 +390,7 @@
     first_grad = jnp.einsum(
         "tse,tde->sd", qkv_grad_rows, qkv_full, preferred_element_type=jnp.float32
     )
-    qkv_slots = reduce_halves(qkv_wgrad_rows, core, 1, 2)
+    qkv_wgrad = reduce_weight(qkv_wgrad_rows, core, pair, 1, 2)
     input_grad = (
         residual_grad + norm_back(normed_first, inverse_first, norm_gains[0], first_grad)
     ).astype(jnp.bfloat16)
@@ -404,28 +412,17 @@
     )
     out_blocal = jnp.sum(branch_grad.astype(jnp.float32), axis=0)
     down_blocal = jnp.sum(mlp_grad.astype(jnp.float32), axis=0)
-    weight_sums = (
-        lax.psum(qkv_slots, "wide").astype(jnp.float32),
-        lax.psum(qkv_bgrad.astype(jnp.bfloat16), "wide").astype(jnp.float32),
-        lax.psum(out_slots, "wide").astype(jnp.float32),
-        lax.psum(up_slots, "wide").astype(jnp.float32),
-        None,
-        lax.psum(down_slots, "wide").astype(jnp.float32),
-    )
+    qkv_bgrad = lax.psum(qkv_bgrad.astype(jnp.bfloat16), "wide").astype(jnp.float32)
     small_sums = lax.psum(
         (gain_local, bias_local, out_blocal, down_blocal, up_bgrad_rows), ("wide", "narrow")
     )
     units = up_bias.shape[0]
     up_bgrad = lax.dynamic_slice_in_dim(small_sums[4], lax.axis_index("narrow") * units, units)
-    up_wgrad = merge_slots(weight_sums[3], 0)
-    down_wgrad = merge_slots(weight_sums[5], 1)
-    out_wgrad = merge_slots(weight_sums[2], 1)
-    qkv_wgrad = merge_slots(weight_sums[0], 1)
     return (
         layer_out,
         input_grad,
         qkv_wgrad,
-        weight_sums[1],
+        qkv_bgrad,
         out_wgrad,
         small_sums[2],
         up_wgrad,

time: 949 us -> 954 us (level)
  blocking collectives: 198 us -> 134 us
  other arithmetic: 116 us -> 146 us
  local copies, waits for them, and re-layouts: 132 us -> 157 us
  starting transfers between devices: 14.8 us -> 36.2 us
  waiting for transfers between devices: 285 us -> 270 us
    ppermute x7 -> x24, waiting for transfers between devices: 7.69 us -> 143 us  [swap(): lax.ppermute(block, 'wide', [(index, index ^ bit) for index in range(coun...]
    all_to_all x1 -> x0, blocking collectives: 116 us -> none  [shards(): lax.all_to_all(qkv_grad.reshape(3, group_rows, heads_here, HEAD), 'narrow...]
    all_gather x4 -> x3, waiting for transfers between devices: 194 us -> 89.5 us  [gather_quarter(): return lax.all_gather(mine, 'narrow', axis=gather_axis, tiled=True)]
    reduce_scatter x3, waiting for transfers between devices: 59.3 us -> 17.6 us  [the longest x2 17.6 us: reduce_weight(): lax.psum_scatter(reduce_quarters(rows, core, pair, split_axis), 'narrow',...]
    all_gather x0 -> x1, blocking collectives: none -> 32.2 us  [gather_quarter(): return lax.all_gather(mine, 'narrow', axis=gather_axis, tiled=True)]
    unnamed x223 -> x268, local copies, waits for them, and re-layouts: 26.4 us -> 49.4 us
    psum x1, blocking collectives: 6.89 us -> 27.8 us  [shards(): lax.psum(qkv_bgrad.astype(jnp.bfloat16), 'wide').astype(jnp.float32)]
    add x0 -> x4, other arithmetic: none -> 18.4 us  [reduce_quarters(): chip_sum = mine + swap(other.astype(jnp.bfloat16), 1).astype(jnp.float32)]
  transfers between devices with their start and end apart: 18 -> 34, of which waited for: 8 -> 14; matrix products, arithmetic and copies ran while one was open for 36% -> 41% of each run, Pallas kernels for 0% -> 0%
where the time goes in v6:
time: 954 us; the launch traced here: 944 us
  waiting for transfers between devices  270 us (28%)
  matrix products  185 us (19%)
  local copies, waits for them, and re-layouts  157 us (16%)
  other arithmetic  146 us (15%)
  blocking collectives  134 us (14%)
  starting transfers between devices  36.2 us (4%)
  between operations  16.6 us (2%)
    ppermute x24, waiting for transfers between devices, swap(): lax.ppermute(block, 'wide', [(index, index ^ bit) for index in range(coun...  143 us
    all_gather x3, waiting for transfers between devices, gather_quarter(): return lax.all_gather(mine, 'narrow', axis=gather_axis, tiled=True)  89.5 us
    unnamed x268, local copies, waits for them, and re-layouts  49.4 us
    psum x1, blocking collectives, shards(): lax.psum((gain_local, bias_local, out_blocal, down_blocal, up_bgrad_rows)...  41.3 us
    all_gather x1, blocking collectives, shards(): bias_full = lax.all_gather(bias_flat, 'narrow', axis=0)  32.5 us
    all_gather x1, blocking collectives, gather_quarter(): return lax.all_gather(mine, 'narrow', axis=gather_axis, tiled=True)  32.2 us
    dot_general x4, matrix products, attend_backward(): jnp.einsum('bqhd,bkhd->bhqk', grad_block, value_block, preferred_element_...  31.3 us
    convert_element_type x4, other arithmetic, attend_backward(): scores_grad = (probs_full * (probs_grad - row_dot)).astype(jnp.bfloat16)  30.6 us
  transfers between devices with their start and end apart: 34, of which 14 were waited for; matrix products, arithmetic and copies ran while one was open for 41% of the time, Pallas kernels for 0%

profile of v6, /device:TPU:0, one launch (start us, length us, event | category | flops | bytes accessed | tf_op | source)
XLA Modules:
  0.0 944.0 jit_solution(15856348130558831251)
XLA Ops:
  9.9 32.5 %all-gather.1 = f32[8,1,896]{2,1,0:T(1,128)S(1)} all-gather(f32[1,1,896]{2,1,0:T(1,128)S(1)} %reshape.372), channel_id=2, replica_groups=mesh['wide'=4,'narrow'=8] {'narrow'}, dimensions={0}, use_global_device_ids=true | all-gather | bytes 32256 | tf_op jit(solution)/shard_map/all_gather | solution.py:277
  42.5 15.3 %all-gather.6.cloned.1.call-done = bf16[3,256,1024]{1,2,0:T(8,128)(2,1)} async-done(((bf16[3,256,128]{1,2,0:T(8,128)(2,1)}), bf16[3,256,1024]{1,2,0:T(8,128)(2,1)}) %all-gather.6.cloned.1.call-update) | async-done | bytes 1572880 | tf_op jit(solution)/shard_map/all_gather | solution.py:187
  60.1 33.0 %collective-permute-done = bf16[3,256,1024]{1,2,0:T(8,128)(2,1)S(1)} collective-permute-done((bf16[3,256,1024]{1,2,0:T(8,128)(2,1)}, bf16[3,256,1024]{1,2,0:T(8,128)(2,1)S(1)}, u32[]{:S(2)}, u32[]{:S(2)}) %collective-permute-start) | collective-permute-done | bytes 1572896 | tf_op jit(solution)/shard_map/ppermute | solution.py:175
  100.5 32.2 %all_gather.21 = bf16[1024,256]{1,0:T(8,128)(2,1)S(1)} all-gather(bf16[128,256]{1,0:T(8,128)(2,1)S(1)} %constant_dynamic-slice_fusion.2), channel_id=1, replica_groups=mesh['wide'=4,'narrow'=8] {'narrow'}, dimensions={0}, use_global_device_ids=true | all-gather | bytes 589824 | tf_op jit(solution)/shard_map/all_gather | solution.py:187
  136.5 3.4 broadcast_select_fusion.5
  140.0 3.6 add_bitcast_fusion
  147.1 4.7 all-to-all-start
  156.1 74.2 %all-gather.8.cloned.1.call-done = bf16[256,4096]{1,0:T(8,128)(2,1)} async-done(((bf16[256,512]{1,0:T(8,128)(2,1)}), bf16[256,4096]{1,0:T(8,128)(2,1)}) %all-gather.8.cloned.1.call-update) | async-done | bytes 2097168 | tf_op jit(solution)/shard_map/all_gather | solution.py:187
  240.7 37.2 %collective-permute-done.4 = bf16[256,4096]{1,0:T(8,128)(2,1)S(1)} collective-permute-done((bf16[256,4096]{1,0:T(8,128)(2,1)}, bf16[256,4096]{1,0:T(8,128)(2,1)S(1)}, u32[]{:S(2)}, u32[]{:S(2)}) %collective-permute-start.4) | collective-permute-done | bytes 2097184 | tf_op jit(solution)/shard_map/ppermute | solution.py:175
  311.2 3.5 exponential_reduce_fusion.1
  315.9 4.0 fusion
  319.9 4.4 exponential_reduce_fusion
  331.4 3.7 fusion.53
  335.2 5.8 fusion.52
  341.0 6.8 fusion.54
  348.2 5.1 fusion.55
  360.1 4.5 all-to-all-start.1
  364.6 6.5 broadcast_select_fusion.1
  371.1 6.1 broadcast_select_fusion.3
  377.2 14.1 %all-to-all-done.1 = bf16[8,512,128]{1,2,0:T(8,128)(2,1)} async-done(((bf16[8,512,128]{1,2,0:T(8,128)(2,1)}), bf16[8,512,128]{1,2,0:T(8,128)(2,1)}, u32[]{:S(2)}, u32[]{:S(2)}) %all-to-all-start.1) | async-done | bytes 1048608 | tf_op jit(solution)/shard_map/all_to_all | solution.py:308
  396.1 11.0 %multiply_convert_fusion.3 = (bf16[512,4096]{1,0:T(8,128)(2,1)}, f32[512,4096]{1,0:T(8,128)}) fusion(f32[4096]{0:T(1024)S(1)} %bitcast.219, bf16[512,4096]{1,0:T(8,128)(2,1)} %get-tuple-element.113, bf16[512,4096]{1,0:T(8,128)(2,1)} %get-tuple-element.112, f32[512,1024]{1,0:T(8,128)S(1)} %get-tuple-element.109, f32[1024]{0:T(1024)S(1)} %bitcast.229, ...), kind=kOutput, calls=%fused_computation.29 | convolution fusion | flops 4326948864 | bytes 23097344 | tf_op jit(solution)/shard_map/dot_general | solution.py:317
  407.1 6.9 add_reduce_fusion
  418.9 12.4 %convert_reduce_fusion = (f32[4096]{0:T(1024)}, bf16[512,4096]{1,0:T(8,128)(2,1)}) fusion(f32[512,4096]{1,0:T(8,128)} %get-tuple-element.189, f32[4096]{0:T(1024)S(1)} %bitcast.220, bf16[512,1024]{1,0:T(8,128)(2,1)S(1)} %get-tuple-element.104, bf16[4096,512]{1,0:T(8,128)(2,1)} %get-tuple-element.111, bf16[4096,512]{1,0:T(8,128)(2,1)S(1)} %copy-done.47), kind=kOutput, calls=%fused_computation.22 | convolution fusion | flops 4339003392 | bytes 22052864 | tf_op jit(solution)/shard_map/dot_general | solution.py:347
  431.3 10.0 %multiply_reduce_fusion.5 = (f32[1024]{0:T(1024)}, f32[512]{0:T(512)S(1)}, f32[512]{0:T(512)S(1)}, f32[1024]{0:T(1024)}, f32[512,1024]{1,0:T(8,128)S(1)}) fusion(f32[512,1024]{1,0:T(8,128)S(1)} %get-tuple-element.109, f32[512]{0:T(512)S(1)} %add_rsqrt_fusion.1, f32[512]{0:T(512)S(1)} %broadcast_multiply_fusion.9, f32[1024]{0:T(1024)S(1)} %bitcast.211, ...), kind=kOutput, calls=%fused_computation.111 | convolution fusion | flops 4316460032 | bytes 16797696 | tf_op jit(solution)/shard_map/dot_general | solution.py:355
  441.3 8.5 fusion.122
  459.6 3.8 all-to-all-start.2
  463.5 6.0 dynamic-slice_convert_fusion
  469.5 6.5 fusion.131
  476.0 5.8 copy-done.34
  485.0 4.4 all-to-all-done.2
  496.0 4.4 convolution_bitcast_fusion.3
  500.4 3.4 multiply_reduce_fusion.3
  507.0 5.3 multiply_reduce_fusion.2
  512.4 4.5 convolution_bitcast_fusion.1
  516.8 7.7 multiply_reduce_fusion.1
  524.6 4.7 multiply_convert_fusion.2
  531.5 14.9 %multiply_reduce_fusion = (f32[2,2,512]{2,1,0:T(2,128)}, f32[2,2,512,2048]{3,2,1,0:T(8,128)}) fusion(f32[2,2,512,2048]{3,2,1,0:T(8,128)} %copy-done.2, f32[2,2,512]{2,1,0:T(2,128)S(1)} %log_add_fusion, pred[512,2048]{1,0:T(8,128)(4,1)S(1)} %iota_compare_fusion, bf16[2,2048,2,64]{1,0,3,2:T(2,128)(2,1)S(1)} %copy-done.33, ...), kind=kOutput, calls=%fused_computation.1 | convolution fusion | flops 557840384 | bytes 35930112 | tf_op jit(solution)/shard_map/bqhd,bkhd->bhqk/dot_general | solution.py:141
  549.1 12.5 %multiply_convert_fusion.1 = bf16[2,2,512,1536]{3,2,1,0:T(8,128)(2,1)} fusion(f32[2,2,512,1536]{3,2,1,0:T(8,128)} %get-tuple-element.196, f32[2,2,512,1536]{3,2,1,0:T(8,128)} %copy-done.3, f32[2,2,512]{2,1,0:T(2,128)S(1)} %copy-done.88, f32[2,2,512]{2,1,0:T(2,128)S(1)} %log_add_fusion.1, pred[512,1536]{1,0:T(8,128)(4,1)S(1)} %copy-done.13), kind=kLoop, calls=%fused_computation.6 | loop fusion | flops 18874368 | bytes 32260096 | tf_op jit(solution)/shard_map/convert_element_type | solution.py:145
  564.4 10.9 %multiply_convert_fusion = bf16[2,2,512,2048]{3,2,1,0:T(8,128)(2,1)} fusion(f32[2,2,512,2048]{3,2,1,0:T(8,128)} %get-tuple-element.194, f32[2,2,512,2048]{3,2,1,0:T(8,128)S(1)} %bitcast.180, f32[2,2,512]{2,1,0:T(2,128)S(1)} %copy-done.89, f32[2,2,512]{2,1,0:T(2,128)S(1)} %copy-done.84, pred[512,2048]{1,0:T(8,128)(4,1)S(1)} %iota_compare_fusion), kind=kLoop, calls=%fused_computation | loop fusion | flops 25165824 | bytes 43008000 | tf_op jit(solution)/shard_map/convert_element_type | solution.py:145
  575.3 7.5 fusion.23
  589.9 4.9 fusion.47
  594.9 6.2 fusion.48
  614.1 5.8 convert_add_fusion
  619.9 3.3 copy-done.11
  628.5 14.7 %copy.190 = bf16[3,4096,2,64]{3,2,0,1:T(2,128)(2,1)} copy(bf16[3,4096,2,64]{1,3,2,0:T(8,128)(2,1)} %pad_maximum_fusion.13) | data formatting | bytes 6291456 | tf_op jit(solution)/shard_map/stack | solution.py:375
  643.2 8.9 reshape.377
  652.2 4.6 all-to-all-start.3
  661.6 10.1 %collective-permute-done.19 = bf16[256,4096]{1,0:T(8,128)(2,1)} collective-permute-done((bf16[256,4096]{1,0:T(8,128)(2,1)}, bf16[256,4096]{1,0:T(8,128)(2,1)}, u32[]{:S(2)}, u32[]{:S(2)}) %collective-permute-start.19) | collective-permute-done | bytes 2097184 | tf_op jit(solution)/shard_map/ppermute | solution.py:175
  671.7 4.7 add_convert_fusion
  676.5 6.0 convert_add_fusion.1
  691.2 50.0 %collective-permute-done.15 = bf16[1024,256]{1,0:T(8,128)(2,1)S(1)} collective-permute-done((bf16[1024,256]{1,0:T(8,128)(2,1)S(1)}, bf16[1024,256]{1,0:T(8,128)(2,1)S(1)}, u32[]{:S(2)}, u32[]{:S(2)}) %collective-permute-start.15) | collective-permute-done | bytes 524320 | tf_op jit(solution)/shard_map/ppermute | solution.py:175
  743.6 8.7 reshape.378
  752.4 15.5 %copy.207 = bf16[3,8,512,2,64]{2,4,3,1,0:T(8,128)(2,1)} copy(bf16[3,8,512,2,64]{4,3,0,2,1:T(2,128)(2,1)} %bitcast.190) | data formatting | bytes 6291456 | tf_op jit(solution)/shard_map/all_to_all | solution.py:384
  767.9 5.5 fusion.69
  775.9 6.3 add_convert_fusion.1
  784.0 5.0 bitcast_add_fusion
  802.4 27.8 %psum.42 = bf16[3,128]{1,0:T(4,128)(2,1)S(1)} all-reduce(bf16[3,128]{1,0:T(4,128)(2,1)S(1)} %maximum_reduce_fusion), channel_id=1, replica_groups=mesh['wide'=4,'narrow'=8] {'wide'}, use_global_device_ids=true, to_apply=%region_32.33 | all-reduce | flops 384 | bytes 1536 | tf_op jit(solution)/shard_map/psum | solution.py:415
  830.8 3.9 add_convert_fusion.2
  834.9 9.0 fusion.38
  844.0 41.3 %all-reduce.6 = (f32[1024]{0:T(1024)}, f32[4096]{0:T(1024)S(1)}, f32[1024]{0:T(1024)}, f32[4,1024]{1,0:T(4,128)}, f32[4,1024]{1,0:T(4,128)}) all-reduce(f32[1024]{0:T(1024)S(1)} %copy-done.100, f32[4096]{0:T(1024)S(1)} %copy-done.97, f32[1024]{0:T(1024)S(1)} %copy-done.92, ...), channel_id=1, replica_groups=mesh['wide'=4,'narrow'=8] {'wide','narrow'}, use_global_device_ids=true, to_apply=%region_35.36 | all-reduce | flops 14336 | bytes 114688 | tf_op jit(solution)/shard_map/psum | solution.py:416
  888.3 3.3 fusion.37
  900.8 4.6 collective-permute-done.22
  906.5 17.6 %reduce-scatter.4.cloned.1.call-done = bf16[3,256,128]{1,2,0:T(8,128)(2,1)} async-done(((bf16[3,256,1024]{1,2,0:T(8,128)(2,1)}), bf16[3,256,128]{1,2,0:T(8,128)(2,1)}) %reduce-scatter.4.cloned.1.call-update) | async-done | bytes 196624 | tf_op jit(solution)/shard_map/reduce_scatter | solution.py:219
  926.5 3.5 collective-permute-done.10
  (475 shorter events, 204.5 us)
Async XLA Ops:
  7.2 52.1 %copy-start = (bf16[512,1024]{1,0:T(8,128)(2,1)S(1)}, bf16[512,1024]{1,0:T(8,128)(2,1)}, u32[]{:S(2)}) copy-start(bf16[512,1024]{1,0:T(8,128)(2,1)} %param.24) | copy-start | bytes 3145732
  7.2 50.6 %all-gather.6.cloned.1.call-start = ((), (), s32[]{:S(2)}) async-start(), calls=%async_computation.7 | async-start | bytes 1769472 | tf_op jit(solution)/shard_map/all_gather | solution.py:187
  9.2 126.6 %all-gather.10.cloned.1.call-start = ((), (), s32[]{:S(2)}) async-start(), calls=%async_computation.9 | async-start | bytes 2359296 | tf_op jit(solution)/shard_map/all_gather | solution.py:187
  57.7 35.3 %collective-permute-start = (bf16[3,256,1024]{1,2,0:T(8,128)(2,1)}, bf16[3,256,1024]{1,2,0:T(8,128)(2,1)S(1)}, u32[]{:S(2)}, u32[]{:S(2)}) collective-permute-start(bf16[3,256,1024]{1,2,0:T(8,128)(2,1)} %all-gather.6.cloned.1.call-done), channel_id=1, source_target_pairs={{0,16},{8,24},{16,0},{24,8},{1,17},{9,25},{17,1},{25,9},{2,18},{10... | collective-permute-start | bytes 4718600 | tf_op jit(solution)/shard_map/ppermute | solution.py:175
  60.0 170.2 %all-gather.8.cloned.1.call-start = ((), (), s32[]{:S(2)}) async-start(), calls=%async_computation.8 | async-start | bytes 2359296 | tf_op jit(solution)/shard_map/all_gather | solution.py:187
  96.7 39.8 %collective-permute-start.1 = (bf16[3,512,1024]{1,2,0:T(8,128)(2,1)}, bf16[3,512,1024]{1,2,0:T(8,128)(2,1)}, u32[]{:S(2)}, u32[]{:S(2)}) collective-permute-start(bf16[3,512,1024]{1,2,0:T(8,128)(2,1)} %pad_maximum_fusion.11), channel_id=1, source_target_pairs={{0,8},{8,0},{16,24},{24,16},{1,9},{9,1},{17,25},{25,17},{2,10},{10... | collective-permute-start | bytes 9437192 | tf_op jit(solution)/shard_map/ppermute | solution.py:175
  97.9 42.0 %copy-start.63 = (f32[2048,32]{0,1:T(8,128)}, f32[2048,32]{0,1:T(8,128)S(1)}, u32[]{:S(2)}) copy-start(f32[2048,32]{0,1:T(8,128)S(1)} %get-tuple-element.176) | copy-start | bytes 786436
  97.9 42.0 %copy-start.65 = (f32[2048,32]{0,1:T(8,128)}, f32[2048,32]{0,1:T(8,128)S(1)}, u32[]{:S(2)}) copy-start(f32[2048,32]{0,1:T(8,128)S(1)} %get-tuple-element.177) | copy-start | bytes 786436
  99.0 40.9 %copy-start.90 = (f32[512]{0:T(512)}, f32[512]{0:T(512)S(1)}, u32[]{:S(2)}) copy-start(f32[512]{0:T(512)S(1)} %broadcast_multiply_fusion.11) | copy-start | bytes 6148
  99.5 40.5 %copy-start.103 = (f32[512]{0:T(512)}, f32[512]{0:T(512)S(1)}, u32[]{:S(2)}) copy-start(f32[512]{0:T(512)S(1)} %add_rsqrt_fusion.3) | copy-start | bytes 6148
  99.5 40.5 %copy-start.101 = (f32[1,1024]{1,0:T(1,128)}, f32[1,1024]{1,0:T(1,128)S(1)}, u32[]{:S(2)}) copy-start(f32[1,1024]{1,0:T(1,128)S(1)} %get-tuple-element.170) | copy-start | bytes 12292
  99.6 40.4 %copy-start.105 = (f32[1,1024]{1,0:T(1,128)}, f32[1,1024]{1,0:T(1,128)S(1)}, u32[]{:S(2)}) copy-start(f32[1,1024]{1,0:T(1,128)S(1)} %get-tuple-element.174) | copy-start | bytes 12292
  132.7 19.6 %collective-permute-start.2 = (bf16[1024,256]{1,0:T(8,128)(2,1)S(1)}, bf16[1024,256]{1,0:T(8,128)(2,1)}, u32[]{:S(2)}, u32[]{:S(2)}) collective-permute-start(bf16[1024,256]{1,0:T(8,128)(2,1)S(1)} %all_gather.21), channel_id=1, source_target_pairs={{0,16},{8,24},{16,0},{24,8},{1,17},{9,25},{17,1},{25,9},{2,18},{10... | collective-permute-start | bytes 1572872 | tf_op jit(solution)/shard_map/ppermute | solution.py:175
  135.8 99.3 %collective-permute-start.6 = (bf16[4096,256]{1,0:T(8,128)(2,1)}, bf16[4096,256]{1,0:T(8,128)(2,1)}, u32[]{:S(2)}, u32[]{:S(2)}) collective-permute-start(bf16[4096,256]{1,0:T(8,128)(2,1)} %all-gather.10.cloned.1.call-done), channel_id=1, source_target_pairs={{0,16},{8,24},{16,0},{24,8},{1,17},{9,25},{17,1},{25,9},{2,18},{10... | collective-permute-start | bytes 6291464 | tf_op jit(solution)/shard_map/ppermute | solution.py:175
  147.1 134.4 %all-to-all-start = ((bf16[3,512,16,64]{1,3,0,2:T(8,128)(2,1)}), bf16[3,512,16,64]{1,3,0,2:T(8,128)(2,1)}, u32[]{:S(2)}, u32[]{:S(2)}) async-start(bf16[3,512,16,64]{1,3,0,2:T(8,128)(2,1)} %pad_maximum_fusion.12), calls=%async_computation | async-start | bytes 6291456 | tf_op jit(solution)/shard_map/all_to_all | solution.py:303
  152.3 364.5 %copy-start.12 = (pred[512,1536]{1,0:T(8,128)(4,1)}, pred[512,1536]{1,0:T(8,128)(4,1)S(1)}, u32[]{:S(2)}) copy-start(pred[512,1536]{1,0:T(8,128)(4,1)S(1)} %iota_compare_fusion.1) | copy-start | bytes 2359300
  154.9 77.0 %collective-permute-start.3 = (bf16[1024,512]{1,0:T(8,128)(2,1)}, bf16[1024,512]{1,0:T(8,128)(2,1)}, u32[]{:S(2)}, u32[]{:S(2)}) collective-permute-start(bf16[1024,512]{1,0:T(8,128)(2,1)} %pad_maximum_fusion.22), channel_id=1, source_target_pairs={{0,8},{8,0},{16,24},{24,16},{1,9},{9,1},{17,25},{25,17},{2,10},{10... | collective-permute-start | bytes 3145736 | tf_op jit(solution)/shard_map/ppermute | solution.py:175
  230.2 47.7 %collective-permute-start.4 = (bf16[256,4096]{1,0:T(8,128)(2,1)}, bf16[256,4096]{1,0:T(8,128)(2,1)S(1)}, u32[]{:S(2)}, u32[]{:S(2)}) collective-permute-start(bf16[256,4096]{1,0:T(8,128)(2,1)} %all-gather.8.cloned.1.call-done), channel_id=1, source_target_pairs={{0,16},{8,24},{16,0},{24,8},{1,17},{9,25},{17,1},{25,9},{2,18},{10... | collective-permute-start | bytes 6291464 | tf_op jit(solution)/shard_map/ppermute | solution.py:175
  237.3 40.7 %copy-start.60 = (bf16[256,4096]{1,0:T(8,128)(2,1)S(1)}, bf16[256,4096]{1,0:T(8,128)(2,1)}, u32[]{:S(2)}) copy-start(bf16[256,4096]{1,0:T(8,128)(2,1)} %all-gather.8.cloned.1.call-done) | copy-start | bytes 6291460
  240.7 123.9 %collective-permute-start.7 = (bf16[4096,512]{1,0:T(8,128)(2,1)}, bf16[4096,512]{1,0:T(8,128)(2,1)}, u32[]{:S(2)}, u32[]{:S(2)}) collective-permute-start(bf16[4096,512]{1,0:T(8,128)(2,1)} %pad_maximum_fusion.8), channel_id=1, source_target_pairs={{0,8},{8,0},{16,24},{24,16},{1,9},{9,1},{17,25},{25,17},{2,10},{10... | collective-permute-start | bytes 12582920 | tf_op jit(solution)/shard_map/ppermute | solution.py:175
  281.5 89.6 %collective-permute-start.5 = (bf16[512,4096]{1,0:T(8,128)(2,1)}, bf16[512,4096]{1,0:T(8,128)(2,1)}, u32[]{:S(2)}, u32[]{:S(2)}) collective-permute-start(bf16[512,4096]{1,0:T(8,128)(2,1)} %pad_maximum_fusion.7), channel_id=1, source_target_pairs={{0,8},{8,0},{16,24},{24,16},{1,9},{9,1},{17,25},{25,17},{2,10},{10... | collective-permute-start | bytes 12582920 | tf_op jit(solution)/shard_map/ppermute | solution.py:175
  298.7 17.1 %copy-start.74 = (bf16[2,512,2,64]{1,0,3,2:T(2,128)(2,1)}, bf16[2,512,2,64]{1,0,3,2:T(2,128)(2,1)S(1)}, u32[]{:S(2)}) copy-start(bf16[2,512,2,64]{1,0,3,2:T(2,128)(2,1)S(1)} %get-tuple-element.151) | copy-start | bytes 786436
  331.4 200.1 %copy-start.83 = (f32[2,2,512]{2,1,0:T(2,128)}, f32[2,2,512]{2,1,0:T(2,128)S(1)}, u32[]{:S(2)}) copy-start(f32[2,2,512]{2,1,0:T(2,128)S(1)} %log_add_fusion) | copy-start | bytes 24580
  335.1 12.6 %slice-start = ((s8[16777216]{0:T(1024)(128)(4,1)}), s8[4194304]{0:T(1024)(128)(4,1)S(1)}, s32[]{:S(2)}) async-start(s8[16777216]{0:T(1024)(128)(4,1)} %bitcast.177), calls=%async_computation.13 | async-start | bytes 8388608
  335.2 12.6 %slice-start.1 = ((s8[16777216]{0:T(1024)(128)(4,1)}), s8[4194304]{0:T(1024)(128)(4,1)S(1)}, s32[]{:S(2)}) async-start(s8[16777216]{0:T(1024)(128)(4,1)} %bitcast.177), calls=%async_computation.14 | async-start | bytes 8388608
  360.1 31.2 %all-to-all-start.1 = ((bf16[8,512,128]{1,2,0:T(8,128)(2,1)}), bf16[8,512,128]{1,2,0:T(8,128)(2,1)}, u32[]{:S(2)}, u32[]{:S(2)}) async-start(bf16[8,512,128]{1,2,0:T(8,128)(2,1)} %copy.175), calls=%async_computation.1 | async-start | bytes 2097152 | tf_op jit(solution)/shard_map/all_to_all | solution.py:308
  371.1 20.2 %copy-start.86 = (f32[1024]{0:T(1024)S(1)}, f32[1024]{0:T(1024)}, u32[]{:S(2)}) copy-start(f32[1024]{0:T(1024)} %param.21) | copy-start | bytes 12292
  418.9 12.4 %copy-start.70 = (bf16[512,1024]{1,0:T(8,128)(2,1)}, bf16[512,1024]{1,0:T(8,128)(2,1)S(1)}, u32[]{:S(2)}) copy-start(bf16[512,1024]{1,0:T(8,128)(2,1)S(1)} %get-tuple-element.104) | copy-start | bytes 3145732
  459.6 29.8 %all-to-all-start.2 = ((bf16[512,8,128]{0,2,1:T(8,128)(2,1)}), bf16[512,8,128]{0,2,1:T(8,128)(2,1)S(1)}, u32[]{:S(2)}, u32[]{:S(2)}) async-start(bf16[512,8,128]{0,2,1:T(8,128)(2,1)} %bitcast.196), calls=%async_computation.2 | async-start | bytes 2097152 | tf_op jit(solution)/shard_map/all_to_all | solution.py:366
  469.5 144.6 %collective-permute-start.18 = (bf16[512,4096]{1,0:T(8,128)(2,1)}, bf16[512,4096]{1,0:T(8,128)(2,1)}, u32[]{:S(2)}, u32[]{:S(2)}) collective-permute-start(bf16[512,4096]{1,0:T(8,128)(2,1)} %dynamic-slice_convert_fusion), channel_id=1, source_target_pairs={{0,8},{8,0},{16,24},{24,16},{1,9},{9,1},{17,25},{25,17},{2,10},{10... | collective-permute-start | bytes 12582920 | tf_op jit(solution)/shard_map/ppermute | solution.py:175
  484.5 192.0 %collective-permute-start.12 = (bf16[4096,512]{1,0:T(8,128)(2,1)}, bf16[4096,512]{1,0:T(8,128)(2,1)}, u32[]{:S(2)}, u32[]{:S(2)}) collective-permute-start(bf16[4096,512]{1,0:T(8,128)(2,1)} %dynamic-slice_convert_fusion.1), channel_id=1, source_target_pairs={{0,8},{8,0},{16,24},{24,16},{1,9},{9,1},{17,25},{25,17},{2,10},{10... | collective-permute-start | bytes 12582920 | tf_op jit(solution)/shard_map/ppermute | solution.py:175
  531.5 14.9 %copy-start.7 = (f32[2,2,512,512]{2,3,1,0:T(8,128)S(1)}, f32[2,2,512,512]{2,3,1,0:T(8,128)}, u32[]{:S(2)}) copy-start(f32[2,2,512,512]{2,3,1,0:T(8,128)} %copy-done.5) | copy-start | bytes 12582916
  531.5 14.9 %copy-start.24 = (f32[2,2,512,512]{2,3,1,0:T(8,128)S(1)}, f32[2,2,512,512]{2,3,1,0:T(8,128)}, u32[]{:S(2)}) copy-start(f32[2,2,512,512]{2,3,1,0:T(8,128)} %get-tuple-element.200) | copy-start | bytes 12582916
  531.5 14.9 %copy-start.44 = (pred[512,512]{0,1:T(8,128)(4,1)S(1)}, pred[512,512]{0,1:T(8,128)(4,1)}, u32[]{:S(2)}) copy-start(pred[512,512]{0,1:T(8,128)(4,1)} %iota_compare_fusion.3) | copy-start | bytes 786436
  549.1 12.5 %slice-start.4 = ((s8[16777216]{0:T(1024)(128)(4,1)}), s8[4194304]{0:T(1024)(128)(4,1)S(1)}, s32[]{:S(2)}) async-start(s8[16777216]{0:T(1024)(128)(4,1)} %bitcast.179), calls=%async_computation.17 | async-start | bytes 8388608
  549.1 12.5 %slice-start.5 = ((s8[16777216]{0:T(1024)(128)(4,1)}), s8[4194304]{0:T(1024)(128)(4,1)S(1)}, s32[]{:S(2)}) async-start(s8[16777216]{0:T(1024)(128)(4,1)} %bitcast.179), calls=%async_computation.18 | async-start | bytes 8388608
  549.1 14.1 %slice-start.6 = ((s8[16777216]{0:T(1024)(128)(4,1)}), s8[4194304]{0:T(1024)(128)(4,1)S(1)}, s32[]{:S(2)}) async-start(s8[16777216]{0:T(1024)(128)(4,1)} %bitcast.179), calls=%async_computation.19 | async-start | bytes 8388608
  549.1 15.3 %slice-start.7 = ((s8[16777216]{0:T(1024)(128)(4,1)}), s8[4194304]{0:T(1024)(128)(4,1)S(1)}, s32[]{:S(2)}) async-start(s8[16777216]{0:T(1024)(128)(4,1)} %bitcast.179), calls=%async_computation.20 | async-start | bytes 8388608
  549.1 15.3 %copy-start.84 = (f32[2,2,512]{2,1,0:T(2,128)S(1)}, f32[2,2,512]{2,1,0:T(2,128)}, u32[]{:S(2)}) copy-start(f32[2,2,512]{2,1,0:T(2,128)} %copy-done.83) | copy-start | bytes 24580
  549.1 15.3 %copy-start.89 = (f32[2,2,512]{2,1,0:T(2,128)S(1)}, f32[2,2,512]{2,1,0:T(2,128)}, u32[]{:S(2)}) copy-start(f32[2,2,512]{2,1,0:T(2,128)} %get-tuple-element.193) | copy-start | bytes 24580
  624.8 46.9 %collective-permute-start.19 = (bf16[256,4096]{1,0:T(8,128)(2,1)}, bf16[256,4096]{1,0:T(8,128)(2,1)}, u32[]{:S(2)}, u32[]{:S(2)}) collective-permute-start(bf16[256,4096]{1,0:T(8,128)(2,1)} %dynamic-slice_convert_fusion.3), channel_id=1, source_target_pairs={{0,16},{8,24},{16,0},{24,8},{1,17},{9,25},{17,1},{25,9},{2,18},{10... | collective-permute-start | bytes 6291464 | tf_op jit(solution)/shard_map/ppermute | solution.py:175
  652.2 91.4 %all-to-all-start.3 = ((bf16[8,2,98304]{2,1,0:T(2,128)(2,1)}), bf16[8,2,98304]{2,1,0:T(2,128)(2,1)}, u32[]{:S(2)}, u32[]{:S(2)}) async-start(bf16[8,2,98304]{2,1,0:T(2,128)(2,1)} %reshape.377), calls=%async_computation.3 | async-start | bytes 6291456 | tf_op jit(solution)/shard_map/all_to_all | solution.py:384
  656.8 229.2 %reduce-scatter.8.cloned.1.call-start = ((), (), s32[]{:S(2)}) async-start(), calls=%async_computation.12 | async-start | bytes 2359296 | tf_op jit(solution)/shard_map/reduce_scatter | solution.py:219
  661.6 24.2 %collective-permute-start.14 = (bf16[1024,512]{1,0:T(8,128)(2,1)S(1)}, bf16[1024,512]{1,0:T(8,128)(2,1)}, u32[]{:S(2)}, u32[]{:S(2)}) collective-permute-start(bf16[1024,512]{1,0:T(8,128)(2,1)S(1)} %dynamic-slice_convert_fusion.6), channel_id=1, source_target_pairs={{0,8},{8,0},{16,24},{24,16},{1,9},{9,1},{17,25},{25,17},{2,10},{10... | collective-permute-start | bytes 3145736 | tf_op jit(solution)/shard_map/ppermute | solution.py:175
  676.4 218.1 %reduce-scatter.6.cloned.1.call-start = ((), (), s32[]{:S(2)}) async-start(), calls=%async_computation.11 | async-start | bytes 2949120 | tf_op jit(solution)/shard_map/reduce_scatter | solution.py:231
  684.1 91.8 %collective-permute-start.13 = (bf16[4096,256]{1,0:T(8,128)(2,1)}, bf16[4096,256]{1,0:T(8,128)(2,1)}, u32[]{:S(2)}, u32[]{:S(2)}) collective-permute-start(bf16[4096,256]{1,0:T(8,128)(2,1)} %dynamic-slice_convert_fusion.4), channel_id=1, source_target_pairs={{0,16},{8,24},{16,0},{24,8},{1,17},{9,25},{17,1},{25,9},{2,18},{10... | collective-permute-start | bytes 6291464 | tf_op jit(solution)/shard_map/ppermute | solution.py:175
  689.5 51.7 %collective-permute-start.15 = (bf16[1024,256]{1,0:T(8,128)(2,1)S(1)}, bf16[1024,256]{1,0:T(8,128)(2,1)S(1)}, u32[]{:S(2)}, u32[]{:S(2)}) collective-permute-start(bf16[1024,256]{1,0:T(8,128)(2,1)S(1)} %dynamic-slice_convert_fusion.7), channel_id=1, source_target_pairs={{0,16},{8,24},{16,0},{24,8},{1,17},{9,25},{17,1},{25,9},{2,18},{10... | collective-permute-start | bytes 1572872 | tf_op jit(solution)/shard_map/ppermute | solution.py:175
  752.3 15.5 %copy-start.26 = (bf16[512,1024]{1,0:T(8,128)(2,1)S(1)}, bf16[512,1024]{1,0:T(8,128)(2,1)}, u32[]{:S(2)}) copy-start(bf16[512,1024]{1,0:T(8,128)(2,1)} %param.14) | copy-start | bytes 3145732
  752.3 15.5 %copy-start.91 = (f32[512]{0:T(512)S(1)}, f32[512]{0:T(512)}, u32[]{:S(2)}) copy-start(f32[512]{0:T(512)} %copy-done.90) | copy-start | bytes 6148
  752.3 15.5 %copy-start.102 = (f32[1,1024]{1,0:T(1,128)S(1)}, f32[1,1024]{1,0:T(1,128)}, u32[]{:S(2)}) copy-start(f32[1,1024]{1,0:T(1,128)} %copy-done.101) | copy-start | bytes 12292
  752.3 15.5 %copy-start.104 = (f32[512]{0:T(512)S(1)}, f32[512]{0:T(512)}, u32[]{:S(2)}) copy-start(f32[512]{0:T(512)} %copy-done.103) | copy-start | bytes 6148
  752.4 15.5 %copy-start.106 = (f32[1,1024]{1,0:T(1,128)S(1)}, f32[1,1024]{1,0:T(1,128)}, u32[]{:S(2)}) copy-start(f32[1,1024]{1,0:T(1,128)} %copy-done.105) | copy-start | bytes 12292
  775.9 8.1 collective-permute-start.8
  783.9 140.3 %reduce-scatter.4.cloned.1.call-start = ((), (), s32[]{:S(2)}) async-start(), calls=%async_computation.10 | async-start | bytes 1769472 | tf_op jit(solution)/shard_map/reduce_scatter | solution.py:219
  792.9 37.9 %collective-permute-start.9 = (bf16[3,256,1024]{1,2,0:T(8,128)(2,1)}, bf16[3,256,1024]{1,2,0:T(8,128)(2,1)}, u32[]{:S(2)}, u32[]{:S(2)}) collective-permute-start(bf16[3,256,1024]{1,2,0:T(8,128)(2,1)} %dynamic-slice_convert_fusion.5), channel_id=1, source_target_pairs={{0,16},{8,24},{16,0},{24,8},{1,17},{9,25},{17,1},{25,9},{2,18},{10... | collective-permute-start | bytes 4718600 | tf_op jit(solution)/shard_map/ppermute | solution.py:175
  834.8 53.5 %copy-start.16 = (f32[512,1024]{1,0:T(8,128)S(1)}, f32[512,1024]{1,0:T(8,128)}, u32[]{:S(2)}) copy-start(f32[512,1024]{1,0:T(8,128)} %copy-done.15) | copy-start | bytes 6291460
  886.0 8.3 collective-permute-start.20
  894.4 36.8 %collective-permute-start.21 = (bf16[512,512]{1,0:T(8,128)(2,1)S(1)}, bf16[512,512]{1,0:T(8,128)(2,1)S(1)}, u32[]{:S(2)}, u32[]{:S(2)}) collective-permute-start(bf16[512,512]{1,0:T(8,128)(2,1)S(1)} %pad_maximum_fusion.23), channel_id=1, source_target_pairs={{0,8},{8,0},{16,24},{24,16},{1,9},{9,1},{17,25},{25,17},{2,10},{10... | collective-permute-start | bytes 1572872 | tf_op jit(solution)/shard_map/ppermute | solution.py:175
  895.3 4.5 collective-permute-start.16
  896.9 8.5 collective-permute-start.22
  900.7 24.9 %collective-permute-start.17 = (bf16[128,512]{1,0:T(8,128)(2,1)S(1)}, bf16[128,512]{1,0:T(8,128)(2,1)S(1)}, u32[]{:S(2)}, u32[]{:S(2)}) collective-permute-start(bf16[128,512]{1,0:T(8,128)(2,1)S(1)} %pad_maximum_fusion.26), channel_id=1, source_target_pairs={{0,8},{8,0},{16,24},{24,16},{1,9},{9,1},{17,25},{25,17},{2,10},{10... | collective-permute-start | bytes 393224 | tf_op jit(solution)/shard_map/ppermute | solution.py:175
  906.5 24.7 %collective-permute-start.23 = (bf16[512,512]{1,0:T(8,128)(2,1)S(1)}, bf16[512,512]{1,0:T(8,128)(2,1)S(1)}, u32[]{:S(2)}, u32[]{:S(2)}) collective-permute-start(bf16[512,512]{1,0:T(8,128)(2,1)S(1)} %pad_maximum_fusion.24), channel_id=1, source_target_pairs={{0,8},{8,0},{16,24},{24,16},{1,9},{9,1},{17,25},{25,17},{2,10},{10... | collective-permute-start | bytes 1572872 | tf_op jit(solution)/shard_map/ppermute | solution.py:175
  924.2 5.9 collective-permute-start.10
  931.1 3.7 collective-permute-start.11
  (99 other events, 529.4 us)
Sparse Core Ops, SparseCore 0:
  10.8 46.9 all-gather.5
  60.4 48.1 all-gather.9
  135.9 94.2 all-gather.7
  676.5 103.0 reduce-scatter.7
  784.0 71.0 reduce-scatter.5
  859.0 65.1 reduce-scatter.3

commit v7 on v5

--- a/solution.py
+++ b/solution.py
@@ -192,14 +192,20 @@
     return jnp.concatenate([first, second], axis=split_axis)
 
 
-def reduce_halves(rows, core, split_axis, scatter_axis):
+def chip_half(rows, core, split_axis):
     half = rows.shape[split_axis] // 2
     mine = lax.dynamic_slice_in_dim(rows, core * half, half, axis=split_axis)
     other = lax.dynamic_slice_in_dim(rows, (1 - core) * half, half, axis=split_axis)
     chip_sum = mine + swap_cores(other.astype(jnp.bfloat16)).astype(jnp.float32)
-    part = lax.psum_scatter(
-        chip_sum.astype(jnp.bfloat16), "narrow", scatter_dimension=scatter_axis, tiled=True
-    )
+    return chip_sum.astype(jnp.bfloat16)
+
+
+def reduce_halves(rows, core, split_axis, scatter_axis):
+    return scatter_slots(chip_half(rows, core, split_axis), core, split_axis, scatter_axis)
+
+
+def scatter_slots(chip_sum, core, split_axis, scatter_axis):
+    part = lax.psum_scatter(chip_sum, "narrow", scatter_dimension=scatter_axis, tiled=True)
     empty = jnp.zeros_like(part)
     return jnp.stack(
         [jnp.where(core == 0, part, empty), jnp.where(core == 0, empty, part)], axis=split_axis
@@ -285,13 +291,17 @@
         + qkv_bias_full[:, None, :]
     )
     shaped = qkv_rows.reshape(3, shard_rows, model // HEAD, HEAD)
-    qkv_tok = jnp.stack(
-        [
-            rotate(shaped[0], cos_rows, sine_rows),
-            rotate(shaped[1], cos_rows, sine_rows),
-            shaped[2],
-        ]
-    ).astype(jnp.bfloat16)
+    qkv_tok = (
+        jnp.stack(
+            [
+                rotate(shaped[0], cos_rows, sine_rows),
+                rotate(shaped[1], cos_rows, sine_rows),
+                shaped[2],
+            ]
+        )
+        .astype(jnp.bfloat16)
+        .reshape(3, shard_rows, model)
+    )
     qkv_heads = lax.all_to_all(qkv_tok, "narrow", 2, 1, tiled=True)
     qkv_heads = qkv_heads.reshape(3, seq_count, length, heads_here, HEAD)
     query, key_rows, values = qkv_heads[0], qkv_heads[1], qkv_heads[2]
@@ -347,7 +357,8 @@
     third_grad = lax.dot_general(
         hidden_grad, up_full, (((1,), (1,)), ((), ())), preferred_element_type=jnp.float32
     )
-    up_slots = reduce_halves(up_wgrad_rows, core, 0, 1)
+    up_chip = chip_half(up_wgrad_rows, core, 0)
+    down_chip = chip_half(down_wgrad_rows, core, 1)
     residual_grad = upstream + norm_back(normed_third, inverse_third, norm_gains[2], third_grad)
     branch_grad = norm_back(normed_second, inverse_second, norm_gains[1], residual_grad).astype(
         jnp.bfloat16
@@ -355,6 +366,11 @@
     attn_grad_rows = lax.dot_general(
         branch_grad, out_full, (((1,), (1,)), ((), ())), preferred_element_type=jnp.float32
     ).astype(jnp.bfloat16)
+    attn_grad_rows, up_chip, down_chip = lax.optimization_barrier(
+        (attn_grad_rows, up_chip, down_chip)
+    )
+    up_slots = scatter_slots(up_chip, core, 0, 1)
+    down_slots = scatter_slots(down_chip, core, 1, 0)
     attn_grad = lax.all_to_all(attn_grad_rows, "narrow", 1, 0, tiled=True)
     attn_grad = attn_grad.reshape(query.shape)
     query_grad, keys_grad, values_grad = attend_backward(
@@ -363,7 +379,7 @@
     out_wgrad_rows = lax.dot_general(
         attn_rows, branch_grad, (((0,), (0,)), ((), ())), preferred_element_type=jnp.float32
     )
-    down_slots, out_slots = reduce_column_halves((down_wgrad_rows, out_wgrad_rows), core)
+    out_slots = reduce_halves(out_wgrad_rows, core, 1, 0)
     qkv_grad = jnp.stack(
         [
             rotate_back(query_grad, cos_table, sine_table),
@@ -373,9 +389,7 @@
     )
     qkv_grad = qkv_grad.reshape(3, group_rows, inner).astype(jnp.bfloat16)
     qkv_bgrad = jnp.sum(qkv_grad.astype(jnp.float32), axis=1)
-    qkv_grad_rows = lax.all_to_all(
-        qkv_grad.reshape(3, group_rows, heads_here, HEAD), "narrow", 1, 2, tiled=True
-    ).reshape(3, shard_rows, model)
+    qkv_grad_rows = lax.all_to_all(qkv_grad, "narrow", 1, 2, tiled=True)
     qkv_wgrad_rows = jnp.einsum(
         "sd,tse->tde", low_first, qkv_grad_rows, preferred_element_type=jnp.float32
     )
@@ -406,15 +420,21 @@
     down_blocal = jnp.sum(mlp_grad.astype(jnp.float32), axis=0)
     weight_sums = (
         lax.psum(qkv_slots, "wide").astype(jnp.float32),
-        lax.psum(qkv_bgrad.astype(jnp.bfloat16), "wide").astype(jnp.float32),
+        None,
         lax.psum(out_slots, "wide").astype(jnp.float32),
         lax.psum(up_slots, "wide").astype(jnp.float32),
         None,
         lax.psum(down_slots, "wide").astype(jnp.float32),
     )
+    narrow_index = lax.axis_index("narrow")
+    bias_slots = jnp.where(
+        jnp.arange(lax.axis_size("narrow"))[:, None, None] == narrow_index, qkv_bgrad[None], 0.0
+    )
     small_sums = lax.psum(
-        (gain_local, bias_local, out_blocal, down_blocal, up_bgrad_rows), ("wide", "narrow")
-    )
+        (gain_local, bias_local, out_blocal, down_blocal, up_bgrad_rows, bias_slots),
+        ("wide", "narrow"),
+    )
+    qkv_bgrad = small_sums[5][narrow_index]
     units = up_bias.shape[0]
     up_bgrad = lax.dynamic_slice_in_dim(small_sums[4], lax.axis_index("narrow") * units, units)
     up_wgrad = merge_slots(weight_sums[3], 0)
@@ -425,7 +445,7 @@
         layer_out,
         input_grad,
         qkv_wgrad,
-        weight_sums[1],
+        qkv_bgrad,
         out_wgrad,
         small_sums[2],
         up_wgrad,

time: 949 us -> 1110 us (1.17)
  waiting for transfers between devices: 285 us -> 633 us
  blocking collectives: 198 us -> 32.8 us
  local copies, waits for them, and re-layouts: 132 us -> 99.6 us
  matrix products: 177 us -> 190 us
    psum x1 -> x2, waiting for transfers between devices: 14.7 us -> 193 us  [the longest x1 121 us: shards(): lax.psum((gain_local, bias_local, out_blocal, down_blocal, up_bgrad_rows,...]
    all_to_all x0 -> x1, waiting for transfers between devices: none -> 125 us  [shards(): qkv_grad_rows = lax.all_to_all(qkv_grad, 'narrow', 1, 2, tiled=True)]
    all_to_all x1 -> x0, blocking collectives: 116 us -> none  [shards(): lax.all_to_all(qkv_grad.reshape(3, group_rows, heads_here, HEAD), 'narrow...]
    psum x2 -> x0, blocking collectives: 48.8 us -> none  [the longest x1 41.9 us: shards(): lax.psum((gain_local, bias_local, out_blocal, down_blocal, up_bgrad_rows)...]
    all_to_all x1, waiting for transfers between devices: 7.98 us -> 27.1 us  [shards(): attn_grad = lax.all_to_all(attn_grad_rows, 'narrow', 1, 0, tiled=True)]
    reduce_scatter x3 -> x4, waiting for transfers between devices: 59.3 us -> 74.3 us  [scatter_slots(): lax.psum_scatter(chip_sum, 'narrow', scatter_dimension=scatter_axis, tile...]
    all_to_all x1, local copies, waits for them, and re-layouts: 15.5 us -> 2.64 us  [shards(): qkv_grad_rows = lax.all_to_all(qkv_grad, 'narrow', 1, 2, tiled=True)]
    all_gather x3, waiting for transfers between devices: 139 us -> 151 us  [gather_mine(): return lax.all_gather(mine, 'narrow', axis=gather_axis, tiled=True)]
  transfers between devices with their start and end apart: 18 -> 21, of which waited for: 8 -> 12; matrix products, arithmetic and copies ran while one was open for 36% -> 28% of each run, Pallas kernels for 0% -> 0%
where the time goes in v7:
time: 1110 us; the launch traced here: 1100 us
  waiting for transfers between devices  633 us (57%)
  matrix products  190 us (17%)
  other arithmetic  107 us (10%)
  local copies, waits for them, and re-layouts  99.6 us (9%)
  blocking collectives  32.8 us (3%)
  starting transfers between devices  18 us (2%)
  between operations  15.8 us (1%)
    all_gather x3, waiting for transfers between devices, gather_mine(): return lax.all_gather(mine, 'narrow', axis=gather_axis, tiled=True)  151 us
    all_to_all x1, waiting for transfers between devices, shards(): qkv_grad_rows = lax.all_to_all(qkv_grad, 'narrow', 1, 2, tiled=True)  125 us
    psum x1, waiting for transfers between devices, shards(): lax.psum((gain_local, bias_local, out_blocal, down_blocal, up_bgrad_rows,...  121 us
    reduce_scatter x4, waiting for transfers between devices, scatter_slots(): lax.psum_scatter(chip_sum, 'narrow', scatter_dimension=scatter_axis, tile...  74.3 us
    psum x1, waiting for transfers between devices, shards(): lax.psum(out_slots, 'wide').astype(jnp.float32)  72.2 us
    all_gather x1, waiting for transfers between devices, shards(): out_full = lax.all_gather(out_weight, 'narrow', axis=0, tiled=True)  44.3 us
    all_gather x1, blocking collectives, shards(): bias_full = lax.all_gather(bias_flat, 'narrow', axis=0)  32.8 us
    dot_general x4, matrix products, attend_backward(): jnp.einsum('bqhd,bkhd->bhqk', grad_block, value_block, preferred_element_...  29.9 us
  transfers between devices with their start and end apart: 21, of which 12 were waited for; matrix products, arithmetic and copies ran while one was open for 28% of the time, Pallas kernels for 0%

profile of v7, /device:TPU:0, one launch (start us, length us, event | category | flops | bytes accessed | tf_op | source)
XLA Modules:
  0.0 1096.4 jit_solution(8690143320121579746)
XLA Ops:
  10.2 32.8 %all-gather.1 = f32[8,1,896]{2,1,0:T(1,128)S(1)} all-gather(f32[1,1,896]{2,1,0:T(1,128)S(1)} %reshape.393), channel_id=2, replica_groups=mesh['wide'=4,'narrow'=8] {'narrow'}, dimensions={0}, use_global_device_ids=true | all-gather | bytes 32256 | tf_op jit(solution)/shard_map/all_gather | solution.py:276
  43.0 30.6 %all-gather.7.cloned.1.call-done = bf16[3,512,1024]{1,2,0:T(8,128)(2,1)} async-done(((bf16[3,512,128]{1,2,0:T(8,128)(2,1)}), bf16[3,512,1024]{1,2,0:T(8,128)(2,1)}) %all-gather.7.cloned.1.call-update) | async-done | bytes 3145744 | tf_op jit(solution)/shard_map/all_gather | solution.py:181
  80.6 3.6 broadcast_select_fusion.5
  84.3 3.7 add_bitcast_fusion
  89.8 4.7 copy.115
  94.5 4.6 all-to-all-start
  102.1 120.3 %all-gather.11.cloned.1.call-done = bf16[512,4096]{1,0:T(8,128)(2,1)} async-done(((bf16[512,512]{1,0:T(8,128)(2,1)}), bf16[512,4096]{1,0:T(8,128)(2,1)}) %all-gather.11.cloned.1.call-update) | async-done | bytes 4194320 | tf_op jit(solution)/shard_map/all_gather | solution.py:181
  222.4 8.4 all-to-all-done
  230.8 4.6 copy.249
  239.4 2.6 copy.119
  249.1 2.7 fusion.131
  261.7 3.5 exponential_reduce_fusion.1
  265.2 14.4 %fusion.57 = bf16[2,512,2,64]{1,3,2,0:T(8,128)(2,1)} fusion(bf16[2,2048,2,64]{1,3,2,0:T(8,128)(2,1)S(1)} %copy-done.24, f32[2,2,512,1024]{3,2,1,0:T(8,128)S(1)} %get-tuple-element.150, f32[2,2,512]{2,1,0:T(2,128)S(1)} %log_add_fusion.2, pred[512,1024]{1,0:T(8,128)(4,1)S(1)} %copy-done.17), kind=kOutput, calls=%fused_computation.153 | convolution fusion | flops 276955136 | bytes 9707520 | tf_op jit(solution)/shard_map/bhqk,bkhd->bqhd/dot_general | solution.py:117
  279.6 4.3 fusion.59
  283.9 4.9 fusion
  288.8 4.5 exponential_reduce_fusion
  294.6 7.1 fusion.60
  308.9 3.6 all-to-all-start.1
  312.8 44.3 %all-gather.9.cloned.1.call-done = bf16[1024,1024]{1,0:T(8,128)(2,1)} async-done(((bf16[128,1024]{1,0:T(8,128)(2,1)}), bf16[1024,1024]{1,0:T(8,128)(2,1)}) %all-gather.9.cloned.1.call-update) | async-done | bytes 2097168 | tf_op jit(solution)/shard_map/all_gather | solution.py:311
  357.1 3.3 add_reduce_fusion.1
  363.1 4.2 broadcast_select_fusion.3
  367.3 10.1 multiply_convert_fusion.3
  377.5 5.1 broadcast_select_fusion.1
  382.6 9.3 add_reduce_fusion
  394.1 2.7 convert_reduce_fusion.3
  396.7 12.7 %convert_reduce_fusion = (f32[4096]{0:T(1024)}, bf16[512,4096]{1,0:T(8,128)(2,1)}) fusion(f32[512,4096]{1,0:T(8,128)} %get-tuple-element.156, f32[4096]{0:T(1024)S(1)} %bitcast.218, bf16[512,1024]{1,0:T(8,128)(2,1)S(1)} %get-tuple-element.89, bf16[4096,512]{1,0:T(8,128)(2,1)} %get-tuple-element.96, bf16[4096,512]{1,0:T(8,128)(2,1)} %get-tuple-element.95), kind=kOutput, calls=%fused_computation.22 | convolution fusion | flops 4339003392 | bytes 22052864 | tf_op jit(solution)/shard_map/dot_general | solution.py:349
  409.5 9.1 multiply_reduce_fusion.5
  418.6 10.6 fusion.125
  429.2 8.2 fusion.134
  437.4 6.0 dynamic-slice_convert_fusion.1
  443.4 6.0 dynamic-slice_convert_fusion
  449.9 3.2 multiply_reduce_fusion.6
  460.7 8.0 add_convert_fusion.1
  468.7 8.2 add_convert_fusion
  478.2 3.7 all-to-all-start.2
  482.5 27.1 %all-to-all-done.2 = bf16[512,8,128]{0,2,1:T(8,128)(2,1)S(1)} async-done(((bf16[512,8,128]{0,2,1:T(8,128)(2,1)}), bf16[512,8,128]{0,2,1:T(8,128)(2,1)S(1)}, u32[]{:S(2)}, u32[]{:S(2)}) %all-to-all-start.2) | async-done | bytes 1048608 | tf_op jit(solution)/shard_map/all_to_all | solution.py:374
  511.8 4.7 convolution_bitcast_fusion.3
  516.4 3.4 multiply_reduce_fusion.3
  519.9 3.3 convolution_bitcast_fusion.2
  523.2 5.1 multiply_reduce_fusion.2
  528.3 4.5 convolution_bitcast_fusion.1
  532.8 7.3 multiply_reduce_fusion.1
  540.1 6.3 multiply_convert_fusion.2
  546.4 4.4 fusion.54
  550.8 6.9 multiply_convert_fusion.1
  557.7 2.6 copy-done.5
  560.3 2.8 fusion.52
  563.1 14.1 %multiply_reduce_fusion = (f32[2,2,512]{2,1,0:T(2,128)S(1)}, f32[2,2,512,2048]{3,2,1,0:T(8,128)}) fusion(f32[2,2,512,2048]{3,2,1,0:T(8,128)} %copy-done.2, f32[2,2,512]{2,1,0:T(2,128)S(1)} %copy-done.61, pred[512,2048]{1,0:T(8,128)(4,1)S(1)} %copy-done.11, bf16[2,2048,2,64]{1,0,3,2:T(2,128)(2,1)S(1)} %copy-done.21, ...), kind=kOutput, calls=%fused_computation.1 | convolution fusion | flops 557840384 | bytes 35930112 | tf_op jit(solution)/shard_map/bqhd,bkhd->bhqk/dot_general | solution.py:141
  578.7 9.4 fusion.29
  591.4 2.6 stack.92
  594.0 12.6 %multiply_convert_fusion = bf16[2,2,512,2048]{3,2,1,0:T(8,128)(2,1)S(1)} fusion(f32[2,2,512,2048]{3,2,1,0:T(8,128)} %get-tuple-element.161, f32[2,2,512,2048]{3,2,1,0:T(8,128)} %copy-done.2, f32[2,2,512]{2,1,0:T(2,128)S(1)} %get-tuple-element.160, f32[2,2,512]{2,1,0:T(2,128)S(1)} %copy-done.61, pred[512,2048]{1,0:T(8,128)(4,1)S(1)} %copy-done.11), kind=kLoop, calls=%fused_computation | loop fusion | flops 25165824 | bytes 43008000 | tf_op jit(solution)/shard_map/convert_element_type | solution.py:145
  606.7 2.7 fusion.53
  626.4 7.2 copy.146
  633.6 4.5 all-to-all-start.3
  639.1 125.1 %all-to-all-done.3 = bf16[3,4096,128]{2,0,1:T(4,128)(2,1)} async-done(((bf16[3,4096,128]{2,0,1:T(4,128)(2,1)}), bf16[3,4096,128]{2,0,1:T(4,128)(2,1)}, u32[]{:S(2)}, u32[]{:S(2)}) %all-to-all-start.3) | async-done | bytes 3145760 | tf_op jit(solution)/shard_map/all_to_all | solution.py:392
  764.2 2.6 copy.147
  768.6 3.6 fusion.20
  772.8 5.6 collective-permute-done.5
  778.5 2.7 fusion.11
  786.3 9.0 fusion.44
  800.5 74.2 %reduce-scatter.5.cloned.1.call-done = bf16[3,512,128]{1,2,0:T(8,128)(2,1)} async-done(((bf16[3,512,1024]{1,2,0:T(8,128)(2,1)}), bf16[3,512,128]{1,2,0:T(8,128)(2,1)}) %reduce-scatter.5.cloned.1.call-update) | async-done | bytes 393232 | tf_op jit(solution)/shard_map/reduce_scatter | solution.py:208
  879.1 3.3 fusion.43
  882.4 121.2 %all-reduce.11.cloned.1.call-done = (f32[8,3,128]{2,1,0:T(4,128)}, f32[1024]{0:T(1024)}, f32[4096]{0:T(1024)}, f32[1024]{0:T(1024)}, f32[4,1024]{1,0:T(4,128)}, /*index=5*/f32[4,1024]{1,0:T(4,128)}) async-done(((f32[8,3,128]{2,1,0:T(4,128)}, f32[1024]{0:T(1024)}, f32[4096]{0:T(1024)}, f32[1024]{0:T(1024)}, f32[4,1024]{1,0:T(4,128)}, /*index=5*/f32[4,1024]{1,0:T(4,128)}), (f32[8,3,128]{2,1,0:T(4,128)}, ...) | async-done | bytes 69648 | tf_op jit(solution)/shard_map/psum | solution.py:433
  1006.1 72.2 %all-reduce.13.cloned.1.call-done = (bf16[128,1024]{0,1:T(8,128)(2,1)}, bf16[512,1024]{0,1:T(8,128)(2,1)}, bf16[3,1024,128]{2,1,0:T(8,128)(2,1)}, bf16[1024,512]{1,0:T(8,128)(2,1)}) async-done(((bf16[128,1024]{0,1:T(8,128)(2,1)}, bf16[512,1024]{0,1:T(8,128)(2,1)}, bf16[3,1024,128]{2,1,0:T(8,128)(2,1)}, bf16[1024,512]{1,0:T(8,128)(2,1)}), (bf16[128,1024]{0,1:T(8,128)(2,1)}, bf16[512,1024]{0,1:T(8,128)(2,1)}, ...) | async-done | bytes 3145744 | tf_op jit(solution)/shard_map/psum | solution.py:424
  (365 shorter events, 114.0 us)
Async XLA Ops:
  7.2 66.5 %copy-start = (bf16[1024,512]{1,0:T(8,128)(2,1)S(1)}, bf16[1024,512]{1,0:T(8,128)(2,1)}, u32[]{:S(2)}) copy-start(bf16[1024,512]{1,0:T(8,128)(2,1)} %param.22) | copy-start | bytes 3145732
  7.2 68.5 %copy-start.15 = (bf16[512,1024]{1,0:T(8,128)(2,1)S(1)}, bf16[512,1024]{1,0:T(8,128)(2,1)}, u32[]{:S(2)}) copy-start(bf16[512,1024]{1,0:T(8,128)(2,1)} %param.14) | copy-start | bytes 3145732
  7.2 70.0 %copy-start.72 = (f32[4,1024]{1,0:T(4,128)S(1)}, f32[4,1024]{1,0:T(4,128)}, u32[]{:S(2)}) copy-start(f32[4,1024]{1,0:T(4,128)} %param.26) | copy-start | bytes 49156
  7.2 70.6 %copy-start.73 = (f32[4,1024]{1,0:T(4,128)S(1)}, f32[4,1024]{1,0:T(4,128)}, u32[]{:S(2)}) copy-start(f32[4,1024]{1,0:T(4,128)} %param.27) | copy-start | bytes 49156
  7.2 66.4 %all-gather.7.cloned.1.call-start = ((), (), s32[]{:S(2)}) async-start(), calls=%async_computation.8 | async-start | bytes 3538944 | tf_op jit(solution)/shard_map/all_gather | solution.py:181
  9.4 67.0 %copy-start.56 = (bf16[512,1024]{1,0:T(8,128)(2,1)S(1)}, bf16[512,1024]{1,0:T(8,128)(2,1)}, u32[]{:S(2)}) copy-start(bf16[512,1024]{1,0:T(8,128)(2,1)} %param.24) | copy-start | bytes 3145732
  9.4 213.0 %all-gather.11.cloned.1.call-start = ((), (), s32[]{:S(2)}) async-start(), calls=%async_computation.10 | async-start | bytes 4718592 | tf_op jit(solution)/shard_map/all_gather | solution.py:181
  74.5 238.2 %all-gather.13.cloned.1.call-start = ((), (), s32[]{:S(2)}) async-start(), calls=%async_computation.11 | async-start | bytes 4718592 | tf_op jit(solution)/shard_map/all_gather | solution.py:181
  74.5 6.1 collective-permute-start
  75.7 8.6 copy-start.40
  75.7 8.6 copy-start.42
  75.9 8.3 copy-start.63
  94.5 136.3 %all-to-all-start = ((bf16[3,512,1024]{1,0,2:T(4,128)(2,1)}), bf16[3,512,1024]{1,0,2:T(4,128)(2,1)}, u32[]{:S(2)}, u32[]{:S(2)}) async-start(bf16[3,512,1024]{1,0,2:T(4,128)(2,1)} %copy.115), calls=%async_computation | async-start | bytes 8388608 | tf_op jit(solution)/shard_map/all_to_all | solution.py:305
  99.1 258.1 %all-gather.9.cloned.1.call-start = ((), (), s32[]{:S(2)}) async-start(), calls=%async_computation.9 | async-start | bytes 2359296 | tf_op jit(solution)/shard_map/all_gather | solution.py:311
  102.1 191.3 %copy-start.10 = (pred[512,2048]{1,0:T(8,128)(4,1)}, pred[512,2048]{1,0:T(8,128)(4,1)S(1)}, u32[]{:S(2)}) copy-start(pred[512,2048]{1,0:T(8,128)(4,1)S(1)} %iota_compare_fusion) | copy-start | bytes 3145732
  222.4 139.7 %collective-permute-start.1 = (bf16[512,4096]{1,0:T(8,128)(2,1)}, bf16[512,4096]{1,0:T(8,128)(2,1)}, u32[]{:S(2)}, u32[]{:S(2)}) collective-permute-start(bf16[512,4096]{1,0:T(8,128)(2,1)} %all-gather.11.cloned.1.call-done), channel_id=1, source_target_pairs={{0,8},{8,0},{16,24},{24,16},{1,9},{9,1},{17,25},{25,17},{2,10},{10... | collective-permute-start | bytes 12582920 | tf_op jit(solution)/shard_map/ppermute | solution.py:175
  253.9 47.7 %copy-start.6 = (f32[2,2,512,512]{2,3,1,0:T(8,128)}, f32[2,2,512,512]{2,3,1,0:T(8,128)S(1)}, u32[]{:S(2)}) copy-start(f32[2,2,512,512]{2,3,1,0:T(8,128)S(1)} %get-tuple-element.152) | copy-start | bytes 12582916
  256.6 8.6 copy-start.4
  261.7 18.0 %copy-start.3 = (f32[2,2,512,1536]{3,2,1,0:T(8,128)}, f32[2,2,512,1536]{3,2,1,0:T(8,128)S(1)}, u32[]{:S(2)}) copy-start(f32[2,2,512,1536]{3,2,1,0:T(8,128)S(1)} %get-tuple-element.148) | copy-start | bytes 37748740
  304.1 8.4 copy-start.87
  304.1 8.5 copy-start.88
  304.2 53.0 %copy-start.55 = (f32[1024]{0:T(1024)S(1)}, f32[1024]{0:T(1024)}, u32[]{:S(2)}) copy-start(f32[1024]{0:T(1024)} %param.21) | copy-start | bytes 12292
  308.9 48.3 %all-to-all-start.1 = ((bf16[8,512,128]{1,2,0:T(8,128)(2,1)}), bf16[8,512,128]{1,2,0:T(8,128)(2,1)S(1)}, u32[]{:S(2)}, u32[]{:S(2)}) async-start(bf16[8,512,128]{1,2,0:T(8,128)(2,1)} %copy.131), calls=%async_computation.1 | async-start | bytes 2097152 | tf_op jit(solution)/shard_map/all_to_all | solution.py:310
  312.4 48.5 %copy-start.71 = (f32[1,1024]{1,0:T(1,128)S(1)}, f32[1,1024]{1,0:T(1,128)}, u32[]{:S(2)}) copy-start(f32[1,1024]{1,0:T(1,128)} %get-tuple-element.140) | copy-start | bytes 12292
  312.4 468.9 %reduce-scatter.7.cloned.1.call-start = ((), (), s32[]{:S(2)}) async-start(), calls=%async_computation.13 | async-start | bytes 1179648 | tf_op jit(solution)/shard_map/reduce_scatter | solution.py:208
  312.7 64.7 %collective-permute-start.2 = (bf16[4096,512]{1,0:T(8,128)(2,1)}, bf16[4096,512]{1,0:T(8,128)(2,1)}, u32[]{:S(2)}, u32[]{:S(2)}) collective-permute-start(bf16[4096,512]{1,0:T(8,128)(2,1)} %all-gather.13.cloned.1.call-done), channel_id=1, source_target_pairs={{0,8},{8,0},{16,24},{24,16},{1,9},{9,1},{17,25},{25,17},{2,10},{10... | collective-permute-start | bytes 12582920 | tf_op jit(solution)/shard_map/ppermute | solution.py:175
  367.3 10.2 copy-start.27
  382.6 9.7 copy-start.19
  396.7 12.7 %copy-start.28 = (bf16[512,4096]{1,0:T(8,128)(2,1)S(1)}, bf16[512,4096]{1,0:T(8,128)(2,1)}, u32[]{:S(2)}) copy-start(bf16[512,4096]{1,0:T(8,128)(2,1)} %get-tuple-element.98) | copy-start | bytes 12582916
  418.6 10.6 copy-start.89
  443.3 17.3 %collective-permute-start.3 = (bf16[512,4096]{1,0:T(8,128)(2,1)}, bf16[512,4096]{1,0:T(8,128)(2,1)}, u32[]{:S(2)}, u32[]{:S(2)}) collective-permute-start(bf16[512,4096]{1,0:T(8,128)(2,1)} %dynamic-slice_convert_fusion.1), channel_id=1, source_target_pairs={{0,8},{8,0},{16,24},{24,16},{1,9},{9,1},{17,25},{25,17},{2,10},{10... | collective-permute-start | bytes 12582920 | tf_op jit(solution)/shard_map/ppermute | solution.py:175
  449.4 19.3 %collective-permute-start.4 = (bf16[4096,512]{1,0:T(8,128)(2,1)}, bf16[4096,512]{1,0:T(8,128)(2,1)}, u32[]{:S(2)}, u32[]{:S(2)}) collective-permute-start(bf16[4096,512]{1,0:T(8,128)(2,1)} %dynamic-slice_convert_fusion), channel_id=1, source_target_pairs={{0,8},{8,0},{16,24},{24,16},{1,9},{9,1},{17,25},{25,17},{2,10},{10... | collective-permute-start | bytes 12582920 | tf_op jit(solution)/shard_map/ppermute | solution.py:175
  456.5 2.7 collective-permute-start.6
  468.7 8.2 copy-start.47
  478.2 31.3 %all-to-all-start.2 = ((bf16[512,8,128]{0,2,1:T(8,128)(2,1)}), bf16[512,8,128]{0,2,1:T(8,128)(2,1)S(1)}, u32[]{:S(2)}, u32[]{:S(2)}) async-start(bf16[512,8,128]{0,2,1:T(8,128)(2,1)} %bitcast.25), calls=%async_computation.2 | async-start | bytes 2097152 | tf_op jit(solution)/shard_map/all_to_all | solution.py:374
  481.9 314.7 %reduce-scatter.9.cloned.1.call-start = ((), (), s32[]{:S(2)}) async-start(), calls=%async_computation.14 | async-start | bytes 4718592 | tf_op jit(solution)/shard_map/reduce_scatter | solution.py:208
  511.7 51.3 %copy-start.44 = (bf16[2,512,2,64]{1,0,3,2:T(2,128)(2,1)}, bf16[2,512,2,64]{1,0,3,2:T(2,128)(2,1)S(1)}, u32[]{:S(2)}) copy-start(bf16[2,512,2,64]{1,0,3,2:T(2,128)(2,1)S(1)} %get-tuple-element.118) | copy-start | bytes 786436
  511.8 8.1 slice-start.3
  519.9 8.4 slice-start
  519.9 8.4 slice-start.1
  563.1 14.1 %copy-start.8 = (f32[2,2,512,512]{2,3,1,0:T(8,128)S(1)}, f32[2,2,512,512]{2,3,1,0:T(8,128)}, u32[]{:S(2)}) copy-start(f32[2,2,512,512]{2,3,1,0:T(8,128)} %copy-done.6) | copy-start | bytes 12582916
  563.1 14.1 %copy-start.14 = (f32[2,2,512,512]{2,3,1,0:T(8,128)S(1)}, f32[2,2,512,512]{2,3,1,0:T(8,128)}, u32[]{:S(2)}) copy-start(f32[2,2,512,512]{2,3,1,0:T(8,128)} %get-tuple-element.167) | copy-start | bytes 12582916
  594.0 12.6 %copy-start.20 = (bf16[2,2048,2,64]{1,0,3,2:T(2,128)(2,1)S(1)}, bf16[2,2048,2,64]{1,0,3,2:T(2,128)(2,1)}, u32[]{:S(2)}) copy-start(bf16[2,2048,2,64]{1,0,3,2:T(2,128)(2,1)} %squeeze.22) | copy-start | bytes 3145732
  633.6 130.6 %all-to-all-start.3 = ((bf16[3,4096,128]{2,0,1:T(4,128)(2,1)}), bf16[3,4096,128]{2,0,1:T(4,128)(2,1)}, u32[]{:S(2)}, u32[]{:S(2)}) async-start(bf16[3,4096,128]{2,0,1:T(4,128)(2,1)} %copy.146), calls=%async_computation.3 | async-start | bytes 8388608 | tf_op jit(solution)/shard_map/all_to_all | solution.py:392
  638.1 158.5 %reduce-scatter.11.cloned.1.call-start = ((), (), s32[]{:S(2)}) async-start(), calls=%async_computation.15 | async-start | bytes 4718592 | tf_op jit(solution)/shard_map/reduce_scatter | solution.py:208
  638.9 129.7 %copy-start.16 = (bf16[512,1024]{1,0:T(8,128)(2,1)S(1)}, bf16[512,1024]{1,0:T(8,128)(2,1)}, u32[]{:S(2)}) copy-start(bf16[512,1024]{1,0:T(8,128)(2,1)} %param.14) | copy-start | bytes 3145732
  638.9 129.7 %copy-start.64 = (f32[512]{0:T(512)S(1)}, f32[512]{0:T(512)}, u32[]{:S(2)}) copy-start(f32[512]{0:T(512)} %copy-done.63) | copy-start | bytes 6148
  638.9 129.7 %copy-start.77 = (f32[1,1024]{1,0:T(1,128)S(1)}, f32[1,1024]{1,0:T(1,128)}, u32[]{:S(2)}) copy-start(f32[1,1024]{1,0:T(1,128)} %copy-done.76) | copy-start | bytes 12292
  638.9 129.7 %copy-start.79 = (f32[512]{0:T(512)S(1)}, f32[512]{0:T(512)}, u32[]{:S(2)}) copy-start(f32[512]{0:T(512)} %copy-done.78) | copy-start | bytes 6148
  638.9 129.7 %copy-start.83 = (f32[1,1024]{1,0:T(1,128)S(1)}, f32[1,1024]{1,0:T(1,128)}, u32[]{:S(2)}) copy-start(f32[1,1024]{1,0:T(1,128)} %copy-done.82) | copy-start | bytes 12292
  638.9 235.8 %reduce-scatter.5.cloned.1.call-start = ((), (), s32[]{:S(2)}) async-start(), calls=%async_computation.12 | async-start | bytes 3538944 | tf_op jit(solution)/shard_map/reduce_scatter | solution.py:208
  772.8 5.7 collective-permute-start.5
  781.3 222.3 %all-reduce.11.cloned.1.call-start = ((), (), s32[]{:S(2)}) async-start(), calls=%async_computation.16 | async-start | bytes 147456 | tf_op jit(solution)/shard_map/psum | solution.py:433
  786.2 9.0 copy-start.67
  786.2 9.0 copy-start.70
  786.2 9.0 copy-start.85
  786.2 9.6 copy-start.66
  786.3 9.6 copy-start.69
  786.3 9.6 copy-start.84
  796.5 281.8 %all-reduce.13.cloned.1.call-start = ((), (), s32[]{:S(2)}) async-start(), calls=%async_computation.17 | async-start | bytes 6291456 | tf_op jit(solution)/shard_map/psum | solution.py:424
  800.5 78.5 %copy-start.13 = (f32[512,1024]{1,0:T(8,128)S(1)}, f32[512,1024]{1,0:T(8,128)}, u32[]{:S(2)}) copy-start(f32[512,1024]{1,0:T(8,128)} %copy-done.12) | copy-start | bytes 6291460
  1080.3 9.1 copy-start.1
  1080.3 7.9 copy-start.75
  1080.4 8.5 copy-start.74
  (56 other events, 212.1 us)
Sparse Core Ops, SparseCore 0:
  10.8 62.7 all-gather.6
  76.2 146.1 all-gather.10
  225.1 70.0 all-gather.12
  297.2 59.9 all-gather.8
  460.8 72.5 reduce-scatter.6
  536.8 87.6 reduce-scatter.8
  642.6 154.0 reduce-scatter.10
  800.2 74.4 reduce-scatter.4
  881.7 121.8 all-reduce.10
  1006.6 71.7 all-reduce.12

commit v8 on v7

--- a/solution.py
+++ b/solution.py
@@ -420,21 +420,15 @@
     down_blocal = jnp.sum(mlp_grad.astype(jnp.float32), axis=0)
     weight_sums = (
         lax.psum(qkv_slots, "wide").astype(jnp.float32),
-        None,
+        lax.psum(qkv_bgrad.astype(jnp.bfloat16), "wide").astype(jnp.float32),
         lax.psum(out_slots, "wide").astype(jnp.float32),
         lax.psum(up_slots, "wide").astype(jnp.float32),
         None,
         lax.psum(down_slots, "wide").astype(jnp.float32),
     )
-    narrow_index = lax.axis_index("narrow")
-    bias_slots = jnp.where(
-        jnp.arange(lax.axis_size("narrow"))[:, None, None] == narrow_index, qkv_bgrad[None], 0.0
-    )
     small_sums = lax.psum(
-        (gain_local, bias_local, out_blocal, down_blocal, up_bgrad_rows, bias_slots),
-        ("wide", "narrow"),
-    )
-    qkv_bgrad = small_sums[5][narrow_index]
+        (gain_local, bias_local, out_blocal, down_blocal, up_bgrad_rows), ("wide", "narrow")
+    )
     units = up_bias.shape[0]
     up_bgrad = lax.dynamic_slice_in_dim(small_sums[4], lax.axis_index("narrow") * units, units)
     up_wgrad = merge_slots(weight_sums[3], 0)
@@ -445,7 +439,7 @@
         layer_out,
         input_grad,
         qkv_wgrad,
-        qkv_bgrad,
+        weight_sums[1],
         out_wgrad,
         small_sums[2],
         up_wgrad,

time: 1110 us -> 972 us (0.88)
  waiting for transfers between devices: 633 us -> 458 us
  blocking collectives: 32.8 us -> 81.9 us
    psum x1 -> x0, waiting for transfers between devices: 121 us -> none  [shards(): lax.psum((gain_local, bias_local, out_blocal, down_blocal, up_bgrad_rows,...]
    psum x1, waiting for transfers between devices: 72.2 us -> 14.8 us  [shards(): lax.psum(out_slots, 'wide').astype(jnp.float32)]
    psum x0 -> x2, blocking collectives: none -> 49.2 us  [the longest x1 41.9 us: shards(): lax.psum((gain_local, bias_local, out_blocal, down_blocal, up_bgrad_rows)...]
  transfers between devices with their start and end apart: 21 -> 20, of which waited for: 12 -> 12; matrix products, arithmetic and copies ran while one was open for 28% -> 31% of each run, Pallas kernels for 0% -> 0%
where the time goes in v8:
time: 972 us; the launch traced here: 962 us
  waiting for transfers between devices  458 us (47%)
  matrix products  190 us (20%)
  other arithmetic  105 us (11%)
  local copies, waits for them, and re-layouts  94.1 us (10%)
  blocking collectives  81.9 us (8%)
  starting transfers between devices  17.9 us (2%)
  between operations  15.6 us (2%)
    all_gather x3, waiting for transfers between devices, gather_mine(): return lax.all_gather(mine, 'narrow', axis=gather_axis, tiled=True)  151 us
    all_to_all x1, waiting for transfers between devices, shards(): qkv_grad_rows = lax.all_to_all(qkv_grad, 'narrow', 1, 2, tiled=True)  125 us
    reduce_scatter x4, waiting for transfers between devices, scatter_slots(): lax.psum_scatter(chip_sum, 'narrow', scatter_dimension=scatter_axis, tile...  77.6 us
    all_gather x1, waiting for transfers between devices, shards(): out_full = lax.all_gather(out_weight, 'narrow', axis=0, tiled=True)  44.5 us
    psum x1, blocking collectives, shards(): lax.psum((gain_local, bias_local, out_blocal, down_blocal, up_bgrad_rows)...  41.9 us
    all_gather x1, blocking collectives, shards(): bias_full = lax.all_gather(bias_flat, 'narrow', axis=0)  32.8 us
    dot_general x4, matrix products, attend_backward(): jnp.einsum('bqhd,bkhd->bhqk', grad_block, value_block, preferred_element_...  29.9 us
    dot_general x4, matrix products, attend_forward(): jnp.einsum('bhqk,bkhd->bqhd', probs_low, values[:, :key_stop], preferred_...  28 us
  transfers between devices with their start and end apart: 20, of which 12 were waited for; matrix products, arithmetic and copies ran while one was open for 31% of the time, Pallas kernels for 0%

profile of v8, /device:TPU:0, one launch (start us, length us, event | category | flops | bytes accessed | tf_op | source)
XLA Modules:
  0.0 962.4 jit_solution(15048010545347814604)
XLA Ops:
  10.2 32.8 %all-gather.1 = f32[8,1,896]{2,1,0:T(1,128)S(1)} all-gather(f32[1,1,896]{2,1,0:T(1,128)S(1)} %reshape.387), channel_id=2, replica_groups=mesh['wide'=4,'narrow'=8] {'narrow'}, dimensions={0}, use_global_device_ids=true | all-gather | bytes 32256 | tf_op jit(solution)/shard_map/all_gather | solution.py:276
  43.0 30.6 %all-gather.7.cloned.1.call-done = bf16[3,512,1024]{1,2,0:T(8,128)(2,1)} async-done(((bf16[3,512,128]{1,2,0:T(8,128)(2,1)}), bf16[3,512,1024]{1,2,0:T(8,128)(2,1)}) %all-gather.7.cloned.1.call-update) | async-done | bytes 3145744 | tf_op jit(solution)/shard_map/all_gather | solution.py:181
  80.6 3.6 broadcast_select_fusion.5
  84.3 3.7 add_bitcast_fusion
  89.8 4.7 copy.115
  94.5 4.6 all-to-all-start
  102.1 120.3 %all-gather.11.cloned.1.call-done = bf16[512,4096]{1,0:T(8,128)(2,1)} async-done(((bf16[512,512]{1,0:T(8,128)(2,1)}), bf16[512,4096]{1,0:T(8,128)(2,1)}) %all-gather.11.cloned.1.call-update) | async-done | bytes 4194320 | tf_op jit(solution)/shard_map/all_gather | solution.py:181
  222.4 8.4 all-to-all-done
  230.8 4.6 copy.249
  249.0 2.6 fusion.130
  261.6 3.5 exponential_reduce_fusion.1
  265.2 14.4 %fusion.57 = bf16[2,512,2,64]{1,3,2,0:T(8,128)(2,1)} fusion(bf16[2,2048,2,64]{1,3,2,0:T(8,128)(2,1)S(1)} %copy-done.24, f32[2,2,512,1024]{3,2,1,0:T(8,128)S(1)} %get-tuple-element.149, f32[2,2,512]{2,1,0:T(2,128)S(1)} %log_add_fusion.2, pred[512,1024]{1,0:T(8,128)(4,1)S(1)} %copy-done.17), kind=kOutput, calls=%fused_computation.152 | convolution fusion | flops 276955136 | bytes 9707520 | tf_op jit(solution)/shard_map/bhqk,bkhd->bqhd/dot_general | solution.py:117
  279.6 4.3 fusion.59
  283.9 4.9 fusion
  288.8 4.5 exponential_reduce_fusion
  294.6 7.1 fusion.60
  308.8 3.6 all-to-all-start.1
  312.8 44.5 %all-gather.9.cloned.1.call-done = bf16[1024,1024]{1,0:T(8,128)(2,1)} async-done(((bf16[128,1024]{1,0:T(8,128)(2,1)}), bf16[1024,1024]{1,0:T(8,128)(2,1)}) %all-gather.9.cloned.1.call-update) | async-done | bytes 2097168 | tf_op jit(solution)/shard_map/all_gather | solution.py:311
  357.2 3.3 add_reduce_fusion.1
  363.2 4.3 broadcast_select_fusion.3
  367.5 10.2 %multiply_convert_fusion.3 = (bf16[512,4096]{1,0:T(8,128)(2,1)}, f32[512,4096]{1,0:T(8,128)}) fusion(f32[4096]{0:T(1024)S(1)} %bitcast.215, bf16[512,4096]{1,0:T(8,128)(2,1)} %get-tuple-element.97, bf16[512,4096]{1,0:T(8,128)(2,1)S(1)} %get-tuple-element.96, f32[512,1024]{1,0:T(8,128)S(1)} %get-tuple-element.93, f32[1024]{0:T(1024)S(1)} %bitcast.225, ...), kind=kOutput, calls=%fused_computation.29 | convolution fusion | flops 4326948864 | bytes 23097344 | tf_op jit(solution)/shard_map/dot_general | solution.py:319
  377.6 5.1 broadcast_select_fusion.1
  382.8 9.3 add_reduce_fusion
  394.3 2.7 convert_reduce_fusion.2
  396.9 12.7 %convert_reduce_fusion = (f32[4096]{0:T(1024)}, bf16[512,4096]{1,0:T(8,128)(2,1)}) fusion(f32[512,4096]{1,0:T(8,128)} %get-tuple-element.155, f32[4096]{0:T(1024)S(1)} %bitcast.216, bf16[512,1024]{1,0:T(8,128)(2,1)S(1)} %get-tuple-element.88, bf16[4096,512]{1,0:T(8,128)(2,1)} %get-tuple-element.95, bf16[4096,512]{1,0:T(8,128)(2,1)} %get-tuple-element.94), kind=kOutput, calls=%fused_computation.22 | convolution fusion | flops 4339003392 | bytes 22052864 | tf_op jit(solution)/shard_map/dot_general | solution.py:349
  409.6 9.1 multiply_reduce_fusion.5
  418.7 10.6 %fusion.124 = f32[1024,4096]{1,0:T(8,128)} fusion(bf16[512,4096]{1,0:T(8,128)(2,1)} %get-tuple-element.169, f32[512,1024]{1,0:T(8,128)S(1)} %get-tuple-element.93, f32[1024]{0:T(1024)S(1)} %bitcast.226, f32[1024]{0:T(1024)S(1)} %bitcast.208, f32[512]{0:T(512)S(1)} %add_rsqrt_fusion.1, f32[512]{0:T(512)S(1)} %broadcast_multiply_fusion.9), kind=kOutput, calls=%fused_computation.284 | convolution fusion | flops 4297588736 | bytes 23080960 | tf_op jit(solution)/shard_map/dot_general | solution.py:354
  429.3 8.1 fusion.133
  437.4 6.0 dynamic-slice_convert_fusion.1
  443.5 6.0 dynamic-slice_convert_fusion
  450.0 3.2 multiply_reduce_fusion.6
  460.8 8.1 add_convert_fusion.1
  468.9 8.2 add_convert_fusion
  478.5 3.7 all-to-all-start.2
  482.7 27.0 %all-to-all-done.2 = bf16[512,8,128]{0,2,1:T(8,128)(2,1)S(1)} async-done(((bf16[512,8,128]{0,2,1:T(8,128)(2,1)}), bf16[512,8,128]{0,2,1:T(8,128)(2,1)S(1)}, u32[]{:S(2)}, u32[]{:S(2)}) %all-to-all-start.2) | async-done | bytes 1048608 | tf_op jit(solution)/shard_map/all_to_all | solution.py:374
  511.9 4.7 convolution_bitcast_fusion.3
  516.6 3.4 multiply_reduce_fusion.3
  520.1 3.3 convolution_bitcast_fusion.2
  523.3 5.1 multiply_reduce_fusion.2
  528.5 4.5 convolution_bitcast_fusion.1
  533.0 7.3 multiply_reduce_fusion.1
  540.2 6.4 multiply_convert_fusion.2
  546.6 4.4 fusion.54
  551.0 6.9 multiply_convert_fusion.1
  560.4 2.8 fusion.52
  563.3 14.1 %multiply_reduce_fusion = (f32[2,2,512]{2,1,0:T(2,128)S(1)}, f32[2,2,512,2048]{3,2,1,0:T(8,128)}) fusion(f32[2,2,512,2048]{3,2,1,0:T(8,128)} %copy-done.2, f32[2,2,512]{2,1,0:T(2,128)S(1)} %copy-done.61, pred[512,2048]{1,0:T(8,128)(4,1)S(1)} %copy-done.11, bf16[2,2048,2,64]{1,0,3,2:T(2,128)(2,1)S(1)} %copy-done.21, ...), kind=kOutput, calls=%fused_computation.1 | convolution fusion | flops 557840384 | bytes 35930112 | tf_op jit(solution)/shard_map/bqhd,bkhd->bhqk/dot_general | solution.py:141
  578.8 9.4 fusion.29
  591.6 2.6 stack.92
  594.2 12.6 %multiply_convert_fusion = bf16[2,2,512,2048]{3,2,1,0:T(8,128)(2,1)S(1)} fusion(f32[2,2,512,2048]{3,2,1,0:T(8,128)} %get-tuple-element.160, f32[2,2,512,2048]{3,2,1,0:T(8,128)} %copy-done.2, f32[2,2,512]{2,1,0:T(2,128)S(1)} %get-tuple-element.159, f32[2,2,512]{2,1,0:T(2,128)S(1)} %copy-done.61, pred[512,2048]{1,0:T(8,128)(4,1)S(1)} %copy-done.11), kind=kLoop, calls=%fused_computation | loop fusion | flops 25165824 | bytes 43008000 | tf_op jit(solution)/shard_map/convert_element_type | solution.py:145
  606.8 2.7 fusion.53
  626.4 7.2 copy.146
  633.6 4.5 all-to-all-start.3
  639.2 125.1 %all-to-all-done.3 = bf16[3,4096,128]{2,0,1:T(4,128)(2,1)} async-done(((bf16[3,4096,128]{2,0,1:T(4,128)(2,1)}), bf16[3,4096,128]{2,0,1:T(4,128)(2,1)}, u32[]{:S(2)}, u32[]{:S(2)}) %all-to-all-start.3) | async-done | bytes 3145760 | tf_op jit(solution)/shard_map/all_to_all | solution.py:392
  764.3 2.6 copy.147
  768.6 3.6 fusion.20
  772.8 5.6 collective-permute-done.5
  778.4 2.8 fusion.11
  785.6 7.3 psum.71
  793.4 3.6 reduce-scatter.11.cloned.1.call-done
  800.8 74.0 %reduce-scatter.5.cloned.1.call-done = bf16[3,512,128]{1,2,0:T(8,128)(2,1)} async-done(((bf16[3,512,1024]{1,2,0:T(8,128)(2,1)}), bf16[3,512,128]{1,2,0:T(8,128)(2,1)}) %reduce-scatter.5.cloned.1.call-update) | async-done | bytes 393232 | tf_op jit(solution)/shard_map/reduce_scatter | solution.py:208
  877.3 9.0 fusion.44
  886.4 41.9 %all-reduce.6 = (f32[1024]{0:T(1024)}, f32[4096]{0:T(1024)S(1)}, f32[1024]{0:T(1024)}, f32[4,1024]{1,0:T(4,128)}, f32[4,1024]{1,0:T(4,128)}) all-reduce(f32[1024]{0:T(1024)S(1)} %copy-done.76, f32[4096]{0:T(1024)S(1)} %copy-done.73, f32[1024]{0:T(1024)S(1)} %copy-done.65, ...), channel_id=1, replica_groups=mesh['wide'=4,'narrow'=8] {'wide','narrow'}, use_global_device_ids=true, to_apply=%region_37.38 | all-reduce | flops 14336 | bytes 114688 | tf_op jit(solution)/shard_map/psum | solution.py:429
  929.0 3.3 fusion.43
  932.3 14.8 %all-reduce.10.cloned.1.call-done = (bf16[128,1024]{0,1:T(8,128)(2,1)}, bf16[512,1024]{0,1:T(8,128)(2,1)}, bf16[3,1024,128]{2,1,0:T(8,128)(2,1)}, bf16[1024,512]{1,0:T(8,128)(2,1)}) async-done(((bf16[128,1024]{0,1:T(8,128)(2,1)}, bf16[512,1024]{0,1:T(8,128)(2,1)}, bf16[3,1024,128]{2,1,0:T(8,128)(2,1)}, bf16[1024,512]{1,0:T(8,128)(2,1)}), (bf16[128,1024]{0,1:T(8,128)(2,1)}, bf16[512,1024]{0,1:T(8,128)(2,1)}, ...) | async-done | bytes 3145744 | tf_op jit(solution)/shard_map/psum | solution.py:424
  (356 shorter events, 111.3 us)
Async XLA Ops:
  7.2 66.5 %copy-start = (bf16[1024,512]{1,0:T(8,128)(2,1)S(1)}, bf16[1024,512]{1,0:T(8,128)(2,1)}, u32[]{:S(2)}) copy-start(bf16[1024,512]{1,0:T(8,128)(2,1)} %param.22) | copy-start | bytes 3145732
  7.2 68.5 %copy-start.15 = (bf16[512,1024]{1,0:T(8,128)(2,1)S(1)}, bf16[512,1024]{1,0:T(8,128)(2,1)}, u32[]{:S(2)}) copy-start(bf16[512,1024]{1,0:T(8,128)(2,1)} %param.14) | copy-start | bytes 3145732
  7.2 70.0 %copy-start.74 = (f32[4,1024]{1,0:T(4,128)S(1)}, f32[4,1024]{1,0:T(4,128)}, u32[]{:S(2)}) copy-start(f32[4,1024]{1,0:T(4,128)} %param.26) | copy-start | bytes 49156
  7.2 70.7 %copy-start.75 = (f32[4,1024]{1,0:T(4,128)S(1)}, f32[4,1024]{1,0:T(4,128)}, u32[]{:S(2)}) copy-start(f32[4,1024]{1,0:T(4,128)} %param.27) | copy-start | bytes 49156
  7.2 66.4 %all-gather.7.cloned.1.call-start = ((), (), s32[]{:S(2)}) async-start(), calls=%async_computation.8 | async-start | bytes 3538944 | tf_op jit(solution)/shard_map/all_gather | solution.py:181
  9.4 67.0 %copy-start.56 = (bf16[512,1024]{1,0:T(8,128)(2,1)S(1)}, bf16[512,1024]{1,0:T(8,128)(2,1)}, u32[]{:S(2)}) copy-start(bf16[512,1024]{1,0:T(8,128)(2,1)} %param.24) | copy-start | bytes 3145732
  9.4 213.0 %all-gather.11.cloned.1.call-start = ((), (), s32[]{:S(2)}) async-start(), calls=%async_computation.10 | async-start | bytes 4718592 | tf_op jit(solution)/shard_map/all_gather | solution.py:181
  74.5 238.2 %all-gather.13.cloned.1.call-start = ((), (), s32[]{:S(2)}) async-start(), calls=%async_computation.11 | async-start | bytes 4718592 | tf_op jit(solution)/shard_map/all_gather | solution.py:181
  74.5 6.1 collective-permute-start
  75.6 8.6 copy-start.40
  75.7 8.6 copy-start.42
  75.9 8.3 copy-start.63
  94.5 136.3 %all-to-all-start = ((bf16[3,512,1024]{1,0,2:T(4,128)(2,1)}), bf16[3,512,1024]{1,0,2:T(4,128)(2,1)}, u32[]{:S(2)}, u32[]{:S(2)}) async-start(bf16[3,512,1024]{1,0,2:T(4,128)(2,1)} %copy.115), calls=%async_computation | async-start | bytes 8388608 | tf_op jit(solution)/shard_map/all_to_all | solution.py:305
  99.1 258.2 %all-gather.9.cloned.1.call-start = ((), (), s32[]{:S(2)}) async-start(), calls=%async_computation.9 | async-start | bytes 2359296 | tf_op jit(solution)/shard_map/all_gather | solution.py:311
  102.1 191.2 %copy-start.10 = (pred[512,2048]{1,0:T(8,128)(4,1)}, pred[512,2048]{1,0:T(8,128)(4,1)S(1)}, u32[]{:S(2)}) copy-start(pred[512,2048]{1,0:T(8,128)(4,1)S(1)} %iota_compare_fusion) | copy-start | bytes 3145732
  222.4 139.7 %collective-permute-start.1 = (bf16[512,4096]{1,0:T(8,128)(2,1)}, bf16[512,4096]{1,0:T(8,128)(2,1)}, u32[]{:S(2)}, u32[]{:S(2)}) collective-permute-start(bf16[512,4096]{1,0:T(8,128)(2,1)} %all-gather.11.cloned.1.call-done), channel_id=1, source_target_pairs={{0,8},{8,0},{16,24},{24,16},{1,9},{9,1},{17,25},{25,17},{2,10},{10... | collective-permute-start | bytes 12582920 | tf_op jit(solution)/shard_map/ppermute | solution.py:175
  251.7 7.4 copy-start.49
  253.9 47.7 %copy-start.6 = (f32[2,2,512,512]{2,3,1,0:T(8,128)}, f32[2,2,512,512]{2,3,1,0:T(8,128)S(1)}, u32[]{:S(2)}) copy-start(f32[2,2,512,512]{2,3,1,0:T(8,128)S(1)} %get-tuple-element.151) | copy-start | bytes 12582916
  256.6 8.6 copy-start.4
  261.6 18.0 %copy-start.3 = (f32[2,2,512,1536]{3,2,1,0:T(8,128)}, f32[2,2,512,1536]{3,2,1,0:T(8,128)S(1)}, u32[]{:S(2)}) copy-start(f32[2,2,512,1536]{3,2,1,0:T(8,128)S(1)} %get-tuple-element.147) | copy-start | bytes 37748740
  304.1 8.4 copy-start.86
  304.1 8.5 copy-start.87
  304.1 53.1 %copy-start.55 = (f32[1024]{0:T(1024)S(1)}, f32[1024]{0:T(1024)}, u32[]{:S(2)}) copy-start(f32[1024]{0:T(1024)} %param.21) | copy-start | bytes 12292
  308.8 48.4 %all-to-all-start.1 = ((bf16[8,512,128]{1,2,0:T(8,128)(2,1)}), bf16[8,512,128]{1,2,0:T(8,128)(2,1)S(1)}, u32[]{:S(2)}, u32[]{:S(2)}) async-start(bf16[8,512,128]{1,2,0:T(8,128)(2,1)} %copy.131), calls=%async_computation.1 | async-start | bytes 2097152 | tf_op jit(solution)/shard_map/all_to_all | solution.py:310
  312.4 48.6 %copy-start.72 = (f32[1,1024]{1,0:T(1,128)S(1)}, f32[1,1024]{1,0:T(1,128)}, u32[]{:S(2)}) copy-start(f32[1,1024]{1,0:T(1,128)} %get-tuple-element.139) | copy-start | bytes 12292
  312.4 468.9 %reduce-scatter.7.cloned.1.call-start = ((), (), s32[]{:S(2)}) async-start(), calls=%async_computation.13 | async-start | bytes 1179648 | tf_op jit(solution)/shard_map/reduce_scatter | solution.py:208
  312.7 65.0 %collective-permute-start.2 = (bf16[4096,512]{1,0:T(8,128)(2,1)}, bf16[4096,512]{1,0:T(8,128)(2,1)}, u32[]{:S(2)}, u32[]{:S(2)}) collective-permute-start(bf16[4096,512]{1,0:T(8,128)(2,1)} %all-gather.13.cloned.1.call-done), channel_id=1, source_target_pairs={{0,8},{8,0},{16,24},{24,16},{1,9},{9,1},{17,25},{25,17},{2,10},{10... | collective-permute-start | bytes 12582920 | tf_op jit(solution)/shard_map/ppermute | solution.py:175
  367.5 10.2 %copy-start.27 = (bf16[4096,512]{1,0:T(8,128)(2,1)S(1)}, bf16[4096,512]{1,0:T(8,128)(2,1)}, u32[]{:S(2)}) copy-start(bf16[4096,512]{1,0:T(8,128)(2,1)} %all-gather.13.cloned.1.call-done) | copy-start | bytes 12582916
  382.8 9.7 %copy-start.19 = (bf16[512,1024]{1,0:T(8,128)(2,1)S(1)}, bf16[512,1024]{1,0:T(8,128)(2,1)}, u32[]{:S(2)}) copy-start(bf16[512,1024]{1,0:T(8,128)(2,1)} %param.15) | copy-start | bytes 3145732
  396.9 12.7 %copy-start.28 = (bf16[512,4096]{1,0:T(8,128)(2,1)S(1)}, bf16[512,4096]{1,0:T(8,128)(2,1)}, u32[]{:S(2)}) copy-start(bf16[512,4096]{1,0:T(8,128)(2,1)} %get-tuple-element.97) | copy-start | bytes 12582916
  418.7 10.6 %copy-start.88 = (bf16[512,4096]{1,0:T(8,128)(2,1)S(1)}, bf16[512,4096]{1,0:T(8,128)(2,1)}, u32[]{:S(2)}) copy-start(bf16[512,4096]{1,0:T(8,128)(2,1)} %get-tuple-element.154) | copy-start | bytes 12582916
  443.5 17.3 %collective-permute-start.3 = (bf16[512,4096]{1,0:T(8,128)(2,1)}, bf16[512,4096]{1,0:T(8,128)(2,1)}, u32[]{:S(2)}, u32[]{:S(2)}) collective-permute-start(bf16[512,4096]{1,0:T(8,128)(2,1)} %dynamic-slice_convert_fusion.1), channel_id=1, source_target_pairs={{0,8},{8,0},{16,24},{24,16},{1,9},{9,1},{17,25},{25,17},{2,10},{10... | collective-permute-start | bytes 12582920 | tf_op jit(solution)/shard_map/ppermute | solution.py:175
  449.5 19.4 %collective-permute-start.4 = (bf16[4096,512]{1,0:T(8,128)(2,1)}, bf16[4096,512]{1,0:T(8,128)(2,1)}, u32[]{:S(2)}, u32[]{:S(2)}) collective-permute-start(bf16[4096,512]{1,0:T(8,128)(2,1)} %dynamic-slice_convert_fusion), channel_id=1, source_target_pairs={{0,8},{8,0},{16,24},{24,16},{1,9},{9,1},{17,25},{25,17},{2,10},{10... | collective-permute-start | bytes 12582920 | tf_op jit(solution)/shard_map/ppermute | solution.py:175
  456.7 2.7 collective-permute-start.6
  468.9 8.2 copy-start.47
  478.5 31.3 %all-to-all-start.2 = ((bf16[512,8,128]{0,2,1:T(8,128)(2,1)}), bf16[512,8,128]{0,2,1:T(8,128)(2,1)S(1)}, u32[]{:S(2)}, u32[]{:S(2)}) async-start(bf16[512,8,128]{0,2,1:T(8,128)(2,1)} %bitcast.25), calls=%async_computation.2 | async-start | bytes 2097152 | tf_op jit(solution)/shard_map/all_to_all | solution.py:374
  482.1 311.3 %reduce-scatter.9.cloned.1.call-start = ((), (), s32[]{:S(2)}) async-start(), calls=%async_computation.14 | async-start | bytes 4718592 | tf_op jit(solution)/shard_map/reduce_scatter | solution.py:208
  511.9 51.3 %copy-start.44 = (bf16[2,512,2,64]{1,0,3,2:T(2,128)(2,1)}, bf16[2,512,2,64]{1,0,3,2:T(2,128)(2,1)S(1)}, u32[]{:S(2)}) copy-start(bf16[2,512,2,64]{1,0,3,2:T(2,128)(2,1)S(1)} %get-tuple-element.117) | copy-start | bytes 786436
  511.9 8.1 slice-start.3
  520.0 8.4 slice-start
  520.0 8.4 slice-start.1
  563.3 14.1 %copy-start.8 = (f32[2,2,512,512]{2,3,1,0:T(8,128)S(1)}, f32[2,2,512,512]{2,3,1,0:T(8,128)}, u32[]{:S(2)}) copy-start(f32[2,2,512,512]{2,3,1,0:T(8,128)} %copy-done.6) | copy-start | bytes 12582916
  563.3 14.1 %copy-start.14 = (f32[2,2,512,512]{2,3,1,0:T(8,128)S(1)}, f32[2,2,512,512]{2,3,1,0:T(8,128)}, u32[]{:S(2)}) copy-start(f32[2,2,512,512]{2,3,1,0:T(8,128)} %get-tuple-element.166) | copy-start | bytes 12582916
  594.2 12.6 %copy-start.20 = (bf16[2,2048,2,64]{1,0,3,2:T(2,128)(2,1)S(1)}, bf16[2,2048,2,64]{1,0,3,2:T(2,128)(2,1)}, u32[]{:S(2)}) copy-start(bf16[2,2048,2,64]{1,0,3,2:T(2,128)(2,1)} %squeeze.19) | copy-start | bytes 3145732
  633.6 130.6 %all-to-all-start.3 = ((bf16[3,4096,128]{2,0,1:T(4,128)(2,1)}), bf16[3,4096,128]{2,0,1:T(4,128)(2,1)}, u32[]{:S(2)}, u32[]{:S(2)}) async-start(bf16[3,4096,128]{2,0,1:T(4,128)(2,1)} %copy.146), calls=%async_computation.3 | async-start | bytes 8388608 | tf_op jit(solution)/shard_map/all_to_all | solution.py:392
  638.2 158.8 %reduce-scatter.11.cloned.1.call-start = ((), (), s32[]{:S(2)}) async-start(), calls=%async_computation.15 | async-start | bytes 4718592 | tf_op jit(solution)/shard_map/reduce_scatter | solution.py:208
  638.9 129.6 %copy-start.16 = (bf16[512,1024]{1,0:T(8,128)(2,1)S(1)}, bf16[512,1024]{1,0:T(8,128)(2,1)}, u32[]{:S(2)}) copy-start(bf16[512,1024]{1,0:T(8,128)(2,1)} %param.14) | copy-start | bytes 3145732
  638.9 129.6 %copy-start.64 = (f32[512]{0:T(512)S(1)}, f32[512]{0:T(512)}, u32[]{:S(2)}) copy-start(f32[512]{0:T(512)} %copy-done.63) | copy-start | bytes 6148
  639.0 129.6 %copy-start.78 = (f32[1,1024]{1,0:T(1,128)S(1)}, f32[1,1024]{1,0:T(1,128)}, u32[]{:S(2)}) copy-start(f32[1,1024]{1,0:T(1,128)} %copy-done.77) | copy-start | bytes 12292
  639.0 129.6 %copy-start.80 = (f32[512]{0:T(512)S(1)}, f32[512]{0:T(512)}, u32[]{:S(2)}) copy-start(f32[512]{0:T(512)} %copy-done.79) | copy-start | bytes 6148
  639.0 129.6 %copy-start.82 = (f32[1,1024]{1,0:T(1,128)S(1)}, f32[1,1024]{1,0:T(1,128)}, u32[]{:S(2)}) copy-start(f32[1,1024]{1,0:T(1,128)} %copy-done.81) | copy-start | bytes 12292
  639.0 235.9 %reduce-scatter.5.cloned.1.call-start = ((), (), s32[]{:S(2)}) async-start(), calls=%async_computation.12 | async-start | bytes 3538944 | tf_op jit(solution)/shard_map/reduce_scatter | solution.py:208
  772.7 5.7 collective-permute-start.5
  781.3 165.8 %all-reduce.10.cloned.1.call-start = ((), (), s32[]{:S(2)}) async-start(), calls=%async_computation.16 | async-start | bytes 6291456 | tf_op jit(solution)/shard_map/psum | solution.py:424
  877.2 9.1 copy-start.67
  877.2 9.1 copy-start.71
  877.2 9.1 copy-start.84
  877.2 9.1 copy-start.66
  877.2 9.1 copy-start.70
  877.2 9.1 copy-start.83
  877.2 9.1 copy-start.65
  877.2 9.1 copy-start.73
  877.3 9.1 copy-start.76
  877.3 51.7 %copy-start.13 = (f32[512,1024]{1,0:T(8,128)S(1)}, f32[512,1024]{1,0:T(8,128)}, u32[]{:S(2)}) copy-start(f32[512,1024]{1,0:T(8,128)} %copy-done.12) | copy-start | bytes 6291460
  (54 other events, 197.5 us)
Sparse Core Ops, SparseCore 0:
  10.8 62.7 all-gather.6
  76.2 146.1 all-gather.10
  225.1 70.0 all-gather.12
  297.2 59.9 all-gather.8
  460.9 72.5 reduce-scatter.6
  537.0 87.7 reduce-scatter.8
  642.6 154.3 reduce-scatter.10
  800.6 74.1 reduce-scatter.4
  878.0 68.9 all-reduce.9

commit v9 on v8

--- a/solution.py
+++ b/solution.py
@@ -275,8 +275,9 @@
     bias_flat = jnp.concatenate([qkv_bias.reshape(-1), up_bias])
     bias_full = lax.all_gather(bias_flat, "narrow", axis=0)
     qkv_gathered = gather_mine(qkv_weight, core, 1, 2)
-    qkv_gathered, up_weight, down_weight, bias_full = lax.optimization_barrier(
-        (qkv_gathered, up_weight, down_weight, bias_full)
+    out_gathered = gather_mine(out_weight, core, 1, 0)
+    qkv_gathered, out_gathered, up_weight, down_weight, bias_full = lax.optimization_barrier(
+        (qkv_gathered, out_gathered, up_weight, down_weight, bias_full)
     )
     qkv_full = join_halves(qkv_gathered, core, 1)
     qkv_bias_full = jnp.swapaxes(bias_full[:, : 3 * inner].reshape(-1, 3, inner), 0, 1).reshape(
@@ -303,12 +304,13 @@
         .reshape(3, shard_rows, model)
     )
     qkv_heads = lax.all_to_all(qkv_tok, "narrow", 2, 1, tiled=True)
+    qkv_heads, up_weight, down_weight = lax.optimization_barrier((qkv_heads, up_weight, down_weight))
     qkv_heads = qkv_heads.reshape(3, seq_count, length, heads_here, HEAD)
     query, key_rows, values = qkv_heads[0], qkv_heads[1], qkv_heads[2]
     attn_heads, totals = attend_forward(query, key_rows, values, block_rows)
     attn_low = attn_heads.reshape(group_rows, inner).astype(jnp.bfloat16)
     attn_rows = lax.all_to_all(attn_low, "narrow", 0, 1, tiled=True)
-    out_full = lax.all_gather(out_weight, "narrow", axis=0, tiled=True)
+    out_full = join_halves(out_gathered, core, 1)
     pre_attn = jnp.dot(attn_rows, out_full, preferred_element_type=jnp.float32) + out_bias
     normed_second, inverse_second = norm_stats(pre_attn)
     residual = layer_in + normed_second * norm_gains[1] + norm_biases[1]
@@ -379,7 +381,7 @@
     out_wgrad_rows = lax.dot_general(
         attn_rows, branch_grad, (((0,), (0,)), ((), ())), preferred_element_type=jnp.float32
     )
-    out_slots = reduce_halves(out_wgrad_rows, core, 1, 0)
+    out_chip = chip_half(out_wgrad_rows, core, 1)
     qkv_grad = jnp.stack(
         [
             rotate_back(query_grad, cos_table, sine_table),
@@ -390,6 +392,8 @@
     qkv_grad = qkv_grad.reshape(3, group_rows, inner).astype(jnp.bfloat16)
     qkv_bgrad = jnp.sum(qkv_grad.astype(jnp.float32), axis=1)
     qkv_grad_rows = lax.all_to_all(qkv_grad, "narrow", 1, 2, tiled=True)
+    qkv_grad_rows, out_chip = lax.optimization_barrier((qkv_grad_rows, out_chip))
+    out_slots = scatter_slots(out_chip, core, 1, 0)
     qkv_wgrad_rows = jnp.einsum(
         "sd,tse->tde", low_first, qkv_grad_rows, preferred_element_type=jnp.float32
     )

time: 972 us -> 1070 us (1.10)
  blocking collectives: 81.9 us -> 178 us
  local copies, waits for them, and re-layouts: 94.1 us -> 137 us
  waiting for transfers between devices: 458 us -> 421 us
    all_to_all x0 -> x1, blocking collectives: none -> 97 us  [shards(): qkv_heads = lax.all_to_all(qkv_tok, 'narrow', 2, 1, tiled=True)]
    all_gather x1 -> x0, waiting for transfers between devices: 44.5 us -> none  [shards(): out_full = lax.all_gather(out_weight, 'narrow', axis=0, tiled=True)]
    reduce_scatter x4, waiting for transfers between devices: 77.6 us -> 113 us  [scatter_slots(): lax.psum_scatter(chip_sum, 'narrow', scatter_dimension=scatter_axis, tile...]
    all_gather x3 -> x4, waiting for transfers between devices: 151 us -> 126 us  [gather_mine(): return lax.all_gather(mine, 'narrow', axis=gather_axis, tiled=True)]
    all_to_all x1, waiting for transfers between devices: 27 us -> 50.4 us  [shards(): attn_grad = lax.all_to_all(attn_grad_rows, 'narrow', 1, 0, tiled=True)]
    all_to_all x1, waiting for transfers between devices: 125 us -> 103 us  [shards(): qkv_grad_rows = lax.all_to_all(qkv_grad, 'narrow', 1, 2, tiled=True)]
    squeeze x5, local copies, waits for them, and re-layouts: 11.8 us -> 26.8 us  [shards(): query, key_rows, values = (qkv_heads[0], qkv_heads[1], qkv_heads[2])]
    unnamed x207 -> x199, local copies, waits for them, and re-layouts: 17.7 us -> 29.5 us
where the time goes in v9:
time: 1070 us; the launch traced here: 1060 us
  waiting for transfers between devices  421 us (39%)
  matrix products  183 us (17%)
  blocking collectives  178 us (17%)
  local copies, waits for them, and re-layouts  137 us (13%)
  other arithmetic  113 us (11%)
  between operations  15.4 us (1%)
  starting transfers between devices  14.2 us (1%)
    all_gather x4, waiting for transfers between devices, gather_mine(): return lax.all_gather(mine, 'narrow', axis=gather_axis, tiled=True)  126 us
    reduce_scatter x4, waiting for transfers between devices, scatter_slots(): lax.psum_scatter(chip_sum, 'narrow', scatter_dimension=scatter_axis, tile...  113 us
    all_to_all x1, waiting for transfers between devices, shards(): qkv_grad_rows = lax.all_to_all(qkv_grad, 'narrow', 1, 2, tiled=True)  103 us
    all_to_all x1, blocking collectives, shards(): qkv_heads = lax.all_to_all(qkv_tok, 'narrow', 2, 1, tiled=True)  97 us
    all_to_all x1, waiting for transfers between devices, shards(): attn_grad = lax.all_to_all(attn_grad_rows, 'narrow', 1, 0, tiled=True)  50.4 us
    psum x1, blocking collectives, shards(): lax.psum((gain_local, bias_local, out_blocal, down_blocal, up_bgrad_rows)...  41.9 us
    all_gather x1, blocking collectives, shards(): bias_full = lax.all_gather(bias_flat, 'narrow', axis=0)  32.4 us
    unnamed x199, local copies, waits for them, and re-layouts  29.5 us
  transfers between devices with their start and end apart: 20, of which 12 were waited for; matrix products, arithmetic and copies ran while one was open for 31% of the time, Pallas kernels for 0%

profile of v9, /device:TPU:0, one launch (start us, length us, event | category | flops | bytes accessed | tf_op | source)
XLA Modules:
  0.0 1061.3 jit_solution(5206603935011950222)
XLA Ops:
  11.8 32.4 %all-gather.1 = f32[8,1,896]{2,1,0:T(1,128)S(1)} all-gather(f32[1,1,896]{2,1,0:T(1,128)S(1)} %reshape.386), channel_id=2, replica_groups=mesh['wide'=4,'narrow'=8] {'narrow'}, dimensions={0}, use_global_device_ids=true | all-gather | bytes 32256 | tf_op jit(solution)/shard_map/all_gather | solution.py:276
  44.3 9.5 all-gather.9.cloned.1.call-done
  53.8 61.5 %all-gather.7.cloned.1.call-done = bf16[3,512,1024]{1,2,0:T(8,128)(2,1)} async-done(((bf16[3,512,128]{1,2,0:T(8,128)(2,1)}), bf16[3,512,1024]{1,2,0:T(8,128)(2,1)}) %all-gather.7.cloned.1.call-update) | async-done | bytes 3145744 | tf_op jit(solution)/shard_map/all_gather | solution.py:181
  124.6 3.6 add_bitcast_fusion
  132.8 97.0 %all_to_all.68 = bf16[3,512,1024]{1,0,2:T(4,128)(2,1)S(1)} all-to-all(bf16[3,512,1024]{1,0,2:T(4,128)(2,1)S(1)} %copy.207), channel_id=1, replica_groups=mesh['wide'=4,'narrow'=8] {'narrow'}, dimensions={2} | all-to-all | bytes 6291456 | tf_op jit(solution)/shard_map/all_to_all | solution.py:306
  232.3 4.7 copy.209
  240.3 4.0 fusion.114
  244.3 5.0 reshape.393
  249.3 5.9 copy.215
  255.2 5.0 reshape.392
  260.2 3.5 fusion.115
  271.3 5.0 reshape.391
  276.3 5.9 copy.211
  295.8 3.5 exponential_reduce_fusion.1
  300.3 4.6 fusion
  304.9 4.5 exponential_reduce_fusion
  309.4 7.9 fusion.53
  317.3 7.6 fusion.55
  324.9 6.1 fusion.56
  331.1 3.6 fusion.54
  339.5 4.2 all-to-all-start.1
  349.8 54.9 %all-gather.13.cloned.1.call-done = bf16[4096,512]{1,0:T(8,128)(2,1)} async-done(((bf16[512,512]{1,0:T(8,128)(2,1)}), bf16[4096,512]{1,0:T(8,128)(2,1)}) %all-gather.13.cloned.1.call-update) | async-done | bytes 4194320 | tf_op jit(solution)/shard_map/all_gather | solution.py:181
  410.2 3.9 broadcast_select_fusion.3
  414.0 10.2 multiply_convert_fusion.3
  424.2 5.2 broadcast_select_fusion.1
  429.4 9.3 add_reduce_fusion
  443.5 11.2 %convert_reduce_fusion = (f32[4096]{0:T(1024)}, bf16[512,4096]{1,0:T(8,128)(2,1)S(1)}) fusion(f32[512,4096]{1,0:T(8,128)} %get-tuple-element.193, f32[4096]{0:T(1024)S(1)} %bitcast.209, bf16[512,1024]{1,0:T(8,128)(2,1)S(1)} %get-tuple-element.124, bf16[4096,512]{1,0:T(8,128)(2,1)} %get-tuple-element.131, bf16[4096,512]{1,0:T(8,128)(2,1)} %get-tuple-element.130), kind=kOutput, calls=%fused_computation.22 | convolution fusion | flops 4339003392 | bytes 22052864 | tf_op jit(solution)/shard_map/dot_general | solution.py:351
  456.7 8.7 fusion.110
  465.4 6.2 dynamic-slice_convert_fusion.1
  472.0 8.2 fusion.119
  480.2 6.1 dynamic-slice_convert_fusion
  486.3 9.1 multiply_reduce_fusion.5
  495.4 4.6 multiply_reduce_fusion.6
  504.6 8.1 add_convert_fusion.1
  512.6 8.2 add_convert_fusion
  523.4 3.6 all-to-all-start.2
  527.5 50.4 %all-to-all-done.2 = bf16[512,8,128]{0,2,1:T(8,128)(2,1)S(1)} async-done(((bf16[512,8,128]{0,2,1:T(8,128)(2,1)}), bf16[512,8,128]{0,2,1:T(8,128)(2,1)S(1)}, u32[]{:S(2)}, u32[]{:S(2)}) %all-to-all-start.2) | async-done | bytes 1048608 | tf_op jit(solution)/shard_map/all_to_all | solution.py:376
  584.6 4.3 convolution_bitcast_fusion.3
  594.6 3.4 convolution_bitcast_fusion.2
  598.0 5.5 multiply_reduce_fusion.2
  603.5 5.1 multiply_convert_fusion.2
  612.6 4.7 convolution_bitcast_fusion.1
  617.3 7.4 multiply_reduce_fusion.1
  624.7 10.5 multiply_convert_fusion.1
  640.5 11.9 %multiply_reduce_fusion = (f32[2,2,512]{2,1,0:T(2,128)}, f32[2,2,512,2048]{3,2,1,0:T(8,128)}) fusion(f32[2,2,512,2048]{3,2,1,0:T(8,128)S(1)} %bitcast.171, f32[2,2,512]{2,1,0:T(2,128)S(1)} %copy-done.57, pred[512,2048]{1,0:T(8,128)(4,1)S(1)} %copy-done.8, bf16[2,2048,2,64]{1,3,2,0:T(8,128)(2,1)} %copy.211, bf16[2,512,2,64]{1,0,3,2:T(2,128)(2,1)} %get-tuple-element.159), kind=kOutput, calls=%fused_computation.1 | convolution fusion | flops 557840384 | bytes 35930112 | tf_op jit(solution)/shard_map/bqhd,bkhd->bhqk/dot_general | solution.py:141
  652.4 8.6 multiply_convert_fusion
  670.2 3.3 copy.239
  676.4 9.8 fusion.24
  690.3 7.2 copy.242
  697.5 4.7 all-to-all-start.3
  709.0 103.2 %all-to-all-done.3 = bf16[3,4096,128]{2,0,1:T(4,128)(2,1)} async-done(((bf16[3,4096,128]{2,0,1:T(4,128)(2,1)}), bf16[3,4096,128]{2,0,1:T(4,128)(2,1)}, u32[]{:S(2)}, u32[]{:S(2)}) %all-to-all-start.3) | async-done | bytes 3145760 | tf_op jit(solution)/shard_map/all_to_all | solution.py:394
  812.2 4.3 copy.243
  816.5 4.8 copy.244
  821.4 5.5 fusion.70
  826.9 4.5 copy-done.19
  833.8 5.8 collective-permute-done.7
  839.6 6.5 fusion.11
  848.5 6.3 psum.71
  859.2 37.1 %reduce-scatter.7.cloned.1.call-done = bf16[128,512]{1,0:T(8,128)(2,1)} async-done(((bf16[1024,512]{1,0:T(8,128)(2,1)}), bf16[128,512]{1,0:T(8,128)(2,1)}) %reduce-scatter.7.cloned.1.call-update) | async-done | bytes 131088 | tf_op jit(solution)/shard_map/reduce_scatter | solution.py:208
  898.2 75.6 %reduce-scatter.5.cloned.1.call-done = bf16[3,512,128]{1,2,0:T(8,128)(2,1)} async-done(((bf16[3,512,1024]{1,2,0:T(8,128)(2,1)}), bf16[3,512,128]{1,2,0:T(8,128)(2,1)}) %reduce-scatter.5.cloned.1.call-update) | async-done | bytes 393232 | tf_op jit(solution)/shard_map/reduce_scatter | solution.py:208
  976.2 9.0 fusion.39
  985.4 41.9 %all-reduce.6 = (f32[1024]{0:T(1024)}, f32[4096]{0:T(1024)S(1)}, f32[1024]{0:T(1024)}, f32[4,1024]{1,0:T(4,128)}, f32[4,1024]{1,0:T(4,128)}) all-reduce(f32[1024]{0:T(1024)S(1)} %copy-done.70, f32[4096]{0:T(1024)S(1)} %copy-done.67, f32[1024]{0:T(1024)S(1)} %copy-done.62, ...), channel_id=1, replica_groups=mesh['wide'=4,'narrow'=8] {'wide','narrow'}, use_global_device_ids=true, to_apply=%region_37.38 | all-reduce | flops 14336 | bytes 114688 | tf_op jit(solution)/shard_map/psum | solution.py:433
  1028.0 3.3 fusion.38
  1031.3 14.7 %all-reduce.10.cloned.1.call-done = (bf16[128,1024]{0,1:T(8,128)(2,1)}, bf16[512,1024]{0,1:T(8,128)(2,1)}, bf16[3,1024,128]{2,1,0:T(8,128)(2,1)}, bf16[1024,512]{1,0:T(8,128)(2,1)}) async-done(((bf16[128,1024]{0,1:T(8,128)(2,1)}, bf16[512,1024]{0,1:T(8,128)(2,1)}, bf16[3,1024,128]{2,1,0:T(8,128)(2,1)}, bf16[1024,512]{1,0:T(8,128)(2,1)}), (bf16[128,1024]{0,1:T(8,128)(2,1)}, bf16[512,1024]{0,1:T(8,128)(2,1)}, ...) | async-done | bytes 3145744 | tf_op jit(solution)/shard_map/psum | solution.py:428
  (353 shorter events, 144.6 us)
Async XLA Ops:
  7.2 229.8 %copy-start = (bf16[1024,512]{1,0:T(8,128)(2,1)S(1)}, bf16[1024,512]{1,0:T(8,128)(2,1)}, u32[]{:S(2)}) copy-start(bf16[1024,512]{1,0:T(8,128)(2,1)} %param.22) | copy-start | bytes 3145732
  7.2 111.4 %copy-start.11 = (bf16[512,1024]{1,0:T(8,128)(2,1)S(1)}, bf16[512,1024]{1,0:T(8,128)(2,1)}, u32[]{:S(2)}) copy-start(bf16[512,1024]{1,0:T(8,128)(2,1)} %param.14) | copy-start | bytes 3145732
  7.2 111.8 %copy-start.68 = (f32[4,1024]{1,0:T(4,128)S(1)}, f32[4,1024]{1,0:T(4,128)}, u32[]{:S(2)}) copy-start(f32[4,1024]{1,0:T(4,128)} %param.26) | copy-start | bytes 49156
  7.2 111.9 %copy-start.69 = (f32[4,1024]{1,0:T(4,128)S(1)}, f32[4,1024]{1,0:T(4,128)}, u32[]{:S(2)}) copy-start(f32[4,1024]{1,0:T(4,128)} %param.27) | copy-start | bytes 49156
  7.2 46.6 %all-gather.9.cloned.1.call-start = ((), (), s32[]{:S(2)}) async-start(), calls=%async_computation.9 | async-start | bytes 1179648 | tf_op jit(solution)/shard_map/all_gather | solution.py:181
  9.0 106.3 %all-gather.7.cloned.1.call-start = ((), (), s32[]{:S(2)}) async-start(), calls=%async_computation.8 | async-start | bytes 3538944 | tf_op jit(solution)/shard_map/all_gather | solution.py:181
  11.1 319.9 %all-gather.11.cloned.1.call-start = ((), (), s32[]{:S(2)}) async-start(), calls=%async_computation.10 | async-start | bytes 4718592 | tf_op jit(solution)/shard_map/all_gather | solution.py:181
  115.3 6.0 collective-permute-start
  118.6 6.0 copy-start.60
  119.0 5.6 copy-start.73
  119.1 5.5 copy-start.71
  119.1 5.5 copy-start.75
  237.9 166.8 %all-gather.13.cloned.1.call-start = ((), (), s32[]{:S(2)}) async-start(), calls=%async_computation.11 | async-start | bytes 4718592 | tf_op jit(solution)/shard_map/all_gather | solution.py:181
  240.3 84.6 %copy-start.7 = (pred[512,2048]{1,0:T(8,128)(4,1)}, pred[512,2048]{1,0:T(8,128)(4,1)S(1)}, u32[]{:S(2)}) copy-start(pred[512,2048]{1,0:T(8,128)(4,1)S(1)} %iota_compare_fusion) | copy-start | bytes 3145732
  304.9 20.0 %copy-start.2 = (f32[2,2,512,2048]{3,2,1,0:T(8,128)}, f32[2,2,512,2048]{3,2,1,0:T(8,128)S(1)}, u32[]{:S(2)}) copy-start(f32[2,2,512,2048]{3,2,1,0:T(8,128)S(1)} %get-tuple-element.183) | copy-start | bytes 50331652
  309.4 15.5 %copy-start.56 = (f32[2,2,512]{2,1,0:T(2,128)}, f32[2,2,512]{2,1,0:T(2,128)S(1)}, u32[]{:S(2)}) copy-start(f32[2,2,512]{2,1,0:T(2,128)S(1)} %log_add_fusion) | copy-start | bytes 24580
  331.0 78.1 %collective-permute-start.2 = (bf16[512,4096]{1,0:T(8,128)(2,1)}, bf16[512,4096]{1,0:T(8,128)(2,1)}, u32[]{:S(2)}, u32[]{:S(2)}) collective-permute-start(bf16[512,4096]{1,0:T(8,128)(2,1)} %all-gather.11.cloned.1.call-done), channel_id=1, source_target_pairs={{0,8},{8,0},{16,24},{24,16},{1,9},{9,1},{17,25},{25,17},{2,10},{10... | collective-permute-start | bytes 12582920 | tf_op jit(solution)/shard_map/ppermute | solution.py:175
  334.8 9.5 copy-start.79
  334.8 9.6 copy-start.80
  338.3 66.4 %copy-start.58 = (f32[1024]{0:T(1024)S(1)}, f32[1024]{0:T(1024)}, u32[]{:S(2)}) copy-start(f32[1024]{0:T(1024)} %param.21) | copy-start | bytes 12292
  339.5 65.1 %all-to-all-start.1 = ((bf16[8,512,128]{1,2,0:T(8,128)(2,1)}), bf16[8,512,128]{1,2,0:T(8,128)(2,1)}, u32[]{:S(2)}, u32[]{:S(2)}) async-start(bf16[8,512,128]{1,2,0:T(8,128)(2,1)} %copy.227), calls=%async_computation.1 | async-start | bytes 2097152 | tf_op jit(solution)/shard_map/all_to_all | solution.py:312
  343.8 511.6 %reduce-scatter.9.cloned.1.call-start = ((), (), s32[]{:S(2)}) async-start(), calls=%async_computation.14 | async-start | bytes 4718592 | tf_op jit(solution)/shard_map/reduce_scatter | solution.py:208
  343.8 3.1 collective-permute-start.1
  349.8 57.8 %copy-start.40 = (bf16[1024,512]{1,0:T(8,128)(2,1)}, bf16[1024,512]{1,0:T(8,128)(2,1)S(1)}, u32[]{:S(2)}) copy-start(bf16[1024,512]{1,0:T(8,128)(2,1)S(1)} %get-tuple-element.150) | copy-start | bytes 3145732
  404.7 19.6 %collective-permute-start.3 = (bf16[4096,512]{1,0:T(8,128)(2,1)}, bf16[4096,512]{1,0:T(8,128)(2,1)}, u32[]{:S(2)}, u32[]{:S(2)}) collective-permute-start(bf16[4096,512]{1,0:T(8,128)(2,1)} %all-gather.13.cloned.1.call-done), channel_id=1, source_target_pairs={{0,8},{8,0},{16,24},{24,16},{1,9},{9,1},{17,25},{25,17},{2,10},{10... | collective-permute-start | bytes 12582920 | tf_op jit(solution)/shard_map/ppermute | solution.py:175
  414.0 10.2 copy-start.25
  424.2 5.2 copy-start.59
  429.4 9.7 copy-start.18
  465.4 6.7 copy-start.81
  471.5 33.0 %collective-permute-start.4 = (bf16[512,4096]{1,0:T(8,128)(2,1)}, bf16[512,4096]{1,0:T(8,128)(2,1)}, u32[]{:S(2)}, u32[]{:S(2)}) collective-permute-start(bf16[512,4096]{1,0:T(8,128)(2,1)} %dynamic-slice_convert_fusion.1), channel_id=1, source_target_pairs={{0,8},{8,0},{16,24},{24,16},{1,9},{9,1},{17,25},{25,17},{2,10},{10... | collective-permute-start | bytes 12582920 | tf_op jit(solution)/shard_map/ppermute | solution.py:175
  480.2 6.1 copy-start.26
  486.3 26.4 %collective-permute-start.5 = (bf16[4096,512]{1,0:T(8,128)(2,1)}, bf16[4096,512]{1,0:T(8,128)(2,1)}, u32[]{:S(2)}, u32[]{:S(2)}) collective-permute-start(bf16[4096,512]{1,0:T(8,128)(2,1)} %dynamic-slice_convert_fusion), channel_id=1, source_target_pairs={{0,8},{8,0},{16,24},{24,16},{1,9},{9,1},{17,25},{25,17},{2,10},{10... | collective-permute-start | bytes 12582920 | tf_op jit(solution)/shard_map/ppermute | solution.py:175
  523.4 54.6 %all-to-all-start.2 = ((bf16[512,8,128]{0,2,1:T(8,128)(2,1)}), bf16[512,8,128]{0,2,1:T(8,128)(2,1)S(1)}, u32[]{:S(2)}, u32[]{:S(2)}) async-start(bf16[512,8,128]{0,2,1:T(8,128)(2,1)} %bitcast.26), calls=%async_computation.2 | async-start | bytes 2097152 | tf_op jit(solution)/shard_map/all_to_all | solution.py:376
  526.9 328.4 %reduce-scatter.11.cloned.1.call-start = ((), (), s32[]{:S(2)}) async-start(), calls=%async_computation.15 | async-start | bytes 4718592 | tf_op jit(solution)/shard_map/reduce_scatter | solution.py:208
  527.5 57.1 %copy-start.21 = (pred[512,512]{0,1:T(8,128)(4,1)S(1)}, pred[512,512]{0,1:T(8,128)(4,1)}, u32[]{:S(2)}) copy-start(pred[512,512]{0,1:T(8,128)(4,1)} %iota_compare_fusion.3) | copy-start | bytes 786436
  581.7 7.2 copy-start.6
  581.7 7.2 copy-start.17
  588.9 5.7 slice-start.7
  598.0 14.6 %slice-start.4 = ((s8[12582912]{0:T(1024)(128)(4,1)}), s8[4194304]{0:T(1024)(128)(4,1)S(1)}, s32[]{:S(2)}) async-start(s8[12582912]{0:T(1024)(128)(4,1)} %bitcast.172), calls=%async_computation.21 | async-start | bytes 8388608
  598.0 14.6 %slice-start.5 = ((s8[12582912]{0:T(1024)(128)(4,1)}), s8[4194304]{0:T(1024)(128)(4,1)S(1)}, s32[]{:S(2)}) async-start(s8[12582912]{0:T(1024)(128)(4,1)} %bitcast.172), calls=%async_computation.22 | async-start | bytes 8388608
  603.5 9.1 slice-start.6
  624.7 15.7 %slice-start = ((s8[16777216]{0:T(1024)(128)(4,1)}), s8[4194304]{0:T(1024)(128)(4,1)S(1)}, s32[]{:S(2)}) async-start(s8[16777216]{0:T(1024)(128)(4,1)} %bitcast.170), calls=%async_computation.17 | async-start | bytes 8388608
  624.7 15.7 %slice-start.1 = ((s8[16777216]{0:T(1024)(128)(4,1)}), s8[4194304]{0:T(1024)(128)(4,1)S(1)}, s32[]{:S(2)}) async-start(s8[16777216]{0:T(1024)(128)(4,1)} %bitcast.170), calls=%async_computation.18 | async-start | bytes 8388608
  624.7 15.7 %slice-start.2 = ((s8[16777216]{0:T(1024)(128)(4,1)}), s8[4194304]{0:T(1024)(128)(4,1)S(1)}, s32[]{:S(2)}) async-start(s8[16777216]{0:T(1024)(128)(4,1)} %bitcast.170), calls=%async_computation.19 | async-start | bytes 8388608
  652.4 8.6 copy-start.15
  669.3 7.1 copy-start.38
  697.5 114.7 %all-to-all-start.3 = ((bf16[3,4096,128]{2,0,1:T(4,128)(2,1)}), bf16[3,4096,128]{2,0,1:T(4,128)(2,1)}, u32[]{:S(2)}, u32[]{:S(2)}) async-start(bf16[3,4096,128]{2,0,1:T(4,128)(2,1)} %copy.242), calls=%async_computation.3 | async-start | bytes 8388608 | tf_op jit(solution)/shard_map/all_to_all | solution.py:394
  702.2 194.1 %reduce-scatter.7.cloned.1.call-start = ((), (), s32[]{:S(2)}) async-start(), calls=%async_computation.13 | async-start | bytes 1179648 | tf_op jit(solution)/shard_map/reduce_scatter | solution.py:208
  705.0 2.7 collective-permute-start.6
  833.6 6.0 collective-permute-start.7
  833.6 140.2 %reduce-scatter.5.cloned.1.call-start = ((), (), s32[]{:S(2)}) async-start(), calls=%async_computation.12 | async-start | bytes 3538944 | tf_op jit(solution)/shard_map/reduce_scatter | solution.py:208
  846.1 199.9 %all-reduce.10.cloned.1.call-start = ((), (), s32[]{:S(2)}) async-start(), calls=%async_computation.16 | async-start | bytes 6291456 | tf_op jit(solution)/shard_map/psum | solution.py:428
  976.1 9.1 copy-start.64
  976.1 9.1 copy-start.66
  976.2 9.1 copy-start.78
  976.2 9.2 copy-start.63
  976.2 9.2 copy-start.65
  976.2 9.2 copy-start.77
  976.2 9.2 copy-start.62
  976.2 9.2 copy-start.67
  976.2 9.2 copy-start.70
  976.2 51.8 %copy-start.10 = (f32[512,1024]{1,0:T(8,128)S(1)}, f32[512,1024]{1,0:T(8,128)}, u32[]{:S(2)}) copy-start(f32[512,1024]{1,0:T(8,128)} %copy-done.9) | copy-start | bytes 6291460
  1046.0 7.0 copy-start.43
  1047.9 6.6 copy-start.1
  (48 other events, 145.6 us)
Sparse Core Ops, SparseCore 0:
  10.7 43.0 all-gather.8
  56.5 58.7 all-gather.6
  238.0 74.4 all-gather.10
  315.0 89.6 all-gather.12
  521.0 110.3 reduce-scatter.8
  634.9 115.4 reduce-scatter.10
  833.7 62.6 reduce-scatter.6
  900.0 73.7 reduce-scatter.4
  977.0 68.9 all-reduce.9

commit v10 on v6

--- a/solution.py
+++ b/solution.py
@@ -125,7 +125,7 @@
     return (jnp.concatenate(outputs, axis=1), totals)
 
 
-def attend_backward(query, key_rows, values, attn_grad, totals, block_rows):
+def attend_backward(query, key_rows, values, attn_grad, totals, block_rows, sidecar, finish):
     length = query.shape[1]
     score_scale = 1.0 / math.sqrt(HEAD)
     keys_grad = jnp.zeros(key_rows.shape, jnp.float32)
@@ -163,10 +163,17 @@
             ),
             pad_rows,
         )
+        if block_number == min(2, length // block_rows - 1):
+            keys_grad, values_grad, sidecar = lax.optimization_barrier(
+                (keys_grad, values_grad, sidecar)
+            )
+            sidecar = finish(sidecar)
+    keys_grad, values_grad, sidecar = lax.optimization_barrier((keys_grad, values_grad, sidecar))
     return (
         jnp.concatenate(query_grads, axis=1),
         keys_grad,
         values_grad,
+        sidecar,
     )
 
 
@@ -190,6 +197,36 @@
 def join_quarters(gathered, core, pair, split_axis):
     half = order_pair(pair, gathered, swap(gathered, 2), split_axis)
     return order_pair(core, half, swap(half, 1), split_axis)
+
+
+def gather_halves(shard, core, split_axis, gather_axis):
+    half = shard.shape[split_axis] // 2
+    mine = lax.dynamic_slice_in_dim(shard, core * half, half, axis=split_axis)
+    gathered = lax.all_gather(mine, "narrow", axis=gather_axis, tiled=True)
+    return gathered
+
+
+def join_halves(gathered, core, split_axis):
+    return order_pair(core, gathered, swap(gathered, 1), split_axis)
+
+
+def core_step(rows, core, split_axis):
+    half = rows.shape[split_axis] // 2
+    mine = lax.dynamic_slice_in_dim(rows, core * half, half, axis=split_axis)
+    other = lax.dynamic_slice_in_dim(rows, (1 - core) * half, half, axis=split_axis)
+    return mine + swap(other.astype(jnp.bfloat16), 1).astype(jnp.float32)
+
+
+def pair_step(chip_sum, pair, split_axis):
+    quarter = chip_sum.shape[split_axis] // 2
+    keep = lax.dynamic_slice_in_dim(chip_sum, pair * quarter, quarter, axis=split_axis)
+    give = lax.dynamic_slice_in_dim(chip_sum, (1 - pair) * quarter, quarter, axis=split_axis)
+    return (keep + swap(give.astype(jnp.bfloat16), 2).astype(jnp.float32)).astype(jnp.bfloat16)
+
+
+def finish_quarter(quarter_sum, core, pair, split_axis, scatter_axis):
+    part = lax.psum_scatter(quarter_sum, "narrow", scatter_dimension=scatter_axis, tiled=True)
+    return spread_quarters(part, core, pair, split_axis)
 
 
 def reduce_quarters(rows, core, pair, split_axis):
@@ -276,11 +313,11 @@
     bias_flat = jnp.concatenate([qkv_bias.reshape(-1), up_bias])
     bias_full = lax.all_gather(bias_flat, "narrow", axis=0)
     pair = (lax.axis_index("wide") // 2) % 2
-    qkv_gathered = gather_quarter(qkv_weight, core, pair, 1, 2)
-    qkv_gathered, up_weight, down_weight, out_weight, bias_full = lax.optimization_barrier(
-        (qkv_gathered, up_weight, down_weight, out_weight, bias_full)
-    )
-    qkv_full = join_quarters(qkv_gathered, core, pair, 1)
+    qkv_gathered = gather_halves(qkv_weight, core, 1, 2)
+    qkv_gathered, up_weight, down_weight, bias_full = lax.optimization_barrier(
+        (qkv_gathered, up_weight, down_weight, bias_full)
+    )
+    qkv_full = join_halves(qkv_gathered, core, 1)
     qkv_bias_full = jnp.swapaxes(bias_full[:, : 3 * inner].reshape(-1, 3, inner), 0, 1).reshape(
         3, model
     )
@@ -306,14 +343,14 @@
     attn_heads, totals = attend_forward(query, key_rows, values, block_rows)
     attn_low = attn_heads.reshape(group_rows, inner).astype(jnp.bfloat16)
     attn_rows = lax.all_to_all(attn_low, "narrow", 0, 1, tiled=True)
-    out_full = join_quarters(gather_quarter(out_weight, core, pair, 1, 0), core, pair, 1)
+    out_full = lax.all_gather(out_weight, "narrow", axis=0, tiled=True)
     pre_attn = jnp.dot(attn_rows, out_full, preferred_element_type=jnp.float32) + out_bias
     normed_second, inverse_second = norm_stats(pre_attn)
     residual = layer_in + normed_second * norm_gains[1] + norm_biases[1]
     normed_third, inverse_third = norm_stats(residual)
     low_third = (normed_third * norm_gains[2] + norm_biases[2]).astype(jnp.bfloat16)
-    up_full = join_quarters(gather_quarter(up_weight, core, pair, 0, 1), core, pair, 0)
-    down_full = join_quarters(gather_quarter(down_weight, core, pair, 1, 0), core, pair, 1)
+    up_full = join_halves(gather_halves(up_weight, core, 0, 1), core, 0)
+    down_full = join_halves(gather_halves(down_weight, core, 1, 0), core, 1)
     hidden = jnp.dot(low_third, up_full, preferred_element_type=jnp.float32) + up_bias_full
     act_low = gelu_value(hidden).astype(jnp.bfloat16)
     pre_mlp = jnp.dot(act_low, down_full, preferred_element_type=jnp.float32) + down_bias
@@ -355,7 +392,8 @@
     third_grad = lax.dot_general(
         hidden_grad, up_full, (((1,), (1,)), ((), ())), preferred_element_type=jnp.float32
     )
-    up_wgrad = reduce_weight(up_wgrad_rows, core, pair, 0, 1)
+    up_chip = core_step(up_wgrad_rows, core, 0)
+    down_chip = core_step(down_wgrad_rows, core, 1)
     residual_grad = upstream + norm_back(normed_third, inverse_third, norm_gains[2], third_grad)
     branch_grad = norm_back(normed_second, inverse_second, norm_gains[1], residual_grad).astype(
         jnp.bfloat16
@@ -363,15 +401,27 @@
     attn_grad_rows = lax.dot_general(
         branch_grad, out_full, (((1,), (1,)), ((), ())), preferred_element_type=jnp.float32
     ).astype(jnp.bfloat16)
+    attn_grad_rows, up_chip, down_chip = lax.optimization_barrier(
+        (attn_grad_rows, up_chip, down_chip)
+    )
+    sidecar = (pair_step(up_chip, pair, 0), pair_step(down_chip, pair, 1))
     attn_grad = lax.all_to_all(attn_grad_rows, "narrow", 1, 0, tiled=True)
     attn_grad = attn_grad.reshape(query.shape)
-    query_grad, keys_grad, values_grad = attend_backward(
-        query, key_rows, values, attn_grad, totals, block_rows
-    )
+    def scatter_pair(pieces):
+        return (
+            lax.psum_scatter(pieces[0], "narrow", scatter_dimension=1, tiled=True),
+            lax.psum_scatter(pieces[1], "narrow", scatter_dimension=0, tiled=True),
+        )
+
+    query_grad, keys_grad, values_grad, sidecar = attend_backward(
+        query, key_rows, values, attn_grad, totals, block_rows, sidecar, scatter_pair
+    )
+    up_wgrad = spread_quarters(sidecar[0], core, pair, 0)
+    down_wgrad = spread_quarters(sidecar[1], core, pair, 1)
     out_wgrad_rows = lax.dot_general(
         attn_rows, branch_grad, (((0,), (0,)), ((), ())), preferred_element_type=jnp.float32
     )
-    down_wgrad, out_wgrad = reduce_column_weights((down_wgrad_rows, out_wgrad_rows), core, pair)
+    out_wgrad = reduce_weight(out_wgrad_rows, core, pair, 1, 0)
     qkv_grad = jnp.stack(
         [
             rotate_back(query_grad, cos_table, sine_table),

time: 954 us -> 1090 us (1.14)
  waiting for transfers between devices: 270 us -> 409 us
  blocking collectives: 134 us -> 155 us
  local copies, waits for them, and re-layouts: 157 us -> 143 us
  starting transfers between devices: 36.2 us -> 23.8 us
    ppermute x24 -> x19, waiting for transfers between devices: 143 us -> 35.6 us  [swap(): lax.ppermute(block, 'wide', [(index, index ^ bit) for index in range(coun...]
    all_gather x3 -> x4, waiting for transfers between devices: 89.5 us -> 196 us  [the longest x3 139 us: gather_halves(): gathered = lax.all_gather(mine, 'narrow', axis=gather_axis, tiled=True)]
    reduce_scatter x1 -> x2, waiting for transfers between devices: 0.02 us -> 78.5 us  [the longest x1 71 us: scatter_pair(): lax.psum_scatter(pieces[1], 'narrow', scatter_dimension=0, tiled=True)]
    all_to_all x0 -> x1, blocking collectives: none -> 73.9 us  [shards(): lax.all_to_all(qkv_grad.reshape(3, group_rows, heads_here, HEAD), 'narrow...]
    reduce_scatter x2, waiting for transfers between devices: 17.6 us -> 82.5 us  [reduce_weight(): lax.psum_scatter(reduce_quarters(rows, core, pair, split_axis), 'narrow',...]
    all_gather x1 -> x0, blocking collectives: 32.2 us -> none  [gather_quarter(): return lax.all_gather(mine, 'narrow', axis=gather_axis, tiled=True)]
    add x0 -> x6, other arithmetic: none -> 23.8 us  [the longest x2 19 us: core_step(): return mine + swap(other.astype(jnp.bfloat16), 1).astype(jnp.float32)]
    psum x1, blocking collectives: 27.8 us -> 7.48 us  [shards(): lax.psum(qkv_bgrad.astype(jnp.bfloat16), 'wide').astype(jnp.float32)]
  transfers between devices with their start and end apart: 34 -> 30, of which waited for: 14 -> 15; matrix products, arithmetic and copies ran while one was open for 41% -> 30% of each run, Pallas kernels for 0% -> 0%
where the time goes in v10:
time: 1090 us; the launch traced here: 1080 us
  waiting for transfers between devices  409 us (38%)
  matrix products  179 us (16%)
  blocking collectives  155 us (14%)
  other arithmetic  152 us (14%)
  local copies, waits for them, and re-layouts  143 us (13%)
  starting transfers between devices  23.8 us (2%)
  between operations  16.1 us (1%)
    all_gather x3, waiting for transfers between devices, gather_halves(): gathered = lax.all_gather(mine, 'narrow', axis=gather_axis, tiled=True)  139 us
    reduce_scatter x2, waiting for transfers between devices, reduce_weight(): lax.psum_scatter(reduce_quarters(rows, core, pair, split_axis), 'narrow',...  82.5 us
    all_to_all x1, blocking collectives, shards(): lax.all_to_all(qkv_grad.reshape(3, group_rows, heads_here, HEAD), 'narrow...  73.9 us
    reduce_scatter x1, waiting for transfers between devices, scatter_pair(): lax.psum_scatter(pieces[1], 'narrow', scatter_dimension=0, tiled=True)  71 us
    all_gather x1, waiting for transfers between devices, shards(): out_full = lax.all_gather(out_weight, 'narrow', axis=0, tiled=True)  56.3 us
    psum x1, blocking collectives, shards(): lax.psum((gain_local, bias_local, out_blocal, down_blocal, up_bgrad_rows)...  40.9 us
    unnamed x230, local copies, waits for them, and re-layouts  36.6 us
    ppermute x19, waiting for transfers between devices, swap(): lax.ppermute(block, 'wide', [(index, index ^ bit) for index in range(coun...  35.6 us
  transfers between devices with their start and end apart: 30, of which 15 were waited for; matrix products, arithmetic and copies ran while one was open for 30% of the time, Pallas kernels for 0%

profile of v10, /device:TPU:0, one launch (start us, length us, event | category | flops | bytes accessed | tf_op | source)
XLA Modules:
  0.0 1078.4 jit_solution(6377180428892099305)
XLA Ops:
  10.2 32.8 %all-gather.1 = f32[8,1,896]{2,1,0:T(1,128)S(1)} all-gather(f32[1,1,896]{2,1,0:T(1,128)S(1)} %reshape.362), channel_id=2, replica_groups=mesh['wide'=4,'narrow'=8] {'narrow'}, dimensions={0}, use_global_device_ids=true | all-gather | bytes 32256 | tf_op jit(solution)/shard_map/all_gather | solution.py:314
  43.0 30.6 %all-gather.7.cloned.1.call-done = bf16[3,512,1024]{1,2,0:T(8,128)(2,1)} async-done(((bf16[3,512,128]{1,2,0:T(8,128)(2,1)}), bf16[3,512,1024]{1,2,0:T(8,128)(2,1)}) %all-gather.7.cloned.1.call-update) | async-done | bytes 3145744 | tf_op jit(solution)/shard_map/all_gather | solution.py:205
  80.6 3.6 broadcast_select_fusion.5
  84.3 3.7 add_bitcast_fusion
  91.4 4.5 all-to-all-start
  99.0 108.8 %all-gather.11.cloned.1.call-done = bf16[512,4096]{1,0:T(8,128)(2,1)} async-done(((bf16[512,512]{1,0:T(8,128)(2,1)}), bf16[512,4096]{1,0:T(8,128)(2,1)}) %all-gather.11.cloned.1.call-update) | async-done | bytes 4194320 | tf_op jit(solution)/shard_map/all_gather | solution.py:205
  249.9 4.3 fusion.50
  254.1 4.9 fusion
  259.1 4.7 exponential_reduce_fusion
  264.9 7.1 fusion.51
  279.1 3.8 all-to-all-start.1
  283.8 56.3 %all-gather.9.cloned.1.call-done = bf16[1024,1024]{1,0:T(8,128)(2,1)} async-done(((bf16[128,1024]{1,0:T(8,128)(2,1)}), bf16[1024,1024]{1,0:T(8,128)(2,1)}) %all-gather.9.cloned.1.call-update) | async-done | bytes 2097168 | tf_op jit(solution)/shard_map/all_gather | solution.py:346
  346.1 4.0 broadcast_select_fusion.3
  350.1 10.2 multiply_convert_fusion.3
  360.3 5.2 broadcast_select_fusion.1
  365.4 9.3 add_reduce_fusion
  379.5 11.7 %convert_reduce_fusion = (f32[4096]{0:T(1024)}, bf16[512,4096]{1,0:T(8,128)(2,1)S(1)}) fusion(f32[512,4096]{1,0:T(8,128)} %get-tuple-element.199, f32[4096]{0:T(1024)S(1)} %bitcast.197, bf16[512,1024]{1,0:T(8,128)(2,1)S(1)} %get-tuple-element.124, bf16[4096,512]{1,0:T(8,128)(2,1)} %get-tuple-element.131, bf16[4096,512]{1,0:T(8,128)(2,1)} %get-tuple-element.130), kind=kOutput, calls=%fused_computation.22 | convolution fusion | flops 4339003392 | bytes 22052864 | tf_op jit(solution)/shard_map/dot_general | solution.py:384
  393.2 8.5 fusion.116
  401.7 6.2 dynamic-slice_convert_fusion.1
  407.8 8.3 fusion.125
  416.2 6.2 dynamic-slice_convert_fusion
  422.9 9.1 multiply_reduce_fusion.5
  432.0 4.2 multiply_reduce_fusion.6
  439.9 9.8 convert_add_fusion.1
  449.7 9.3 convert_add_fusion
  464.0 3.8 dynamic-slice_convert_fusion.3
  469.2 3.8 dynamic-slice_convert_fusion.4
  473.6 16.4 %all-to-all-done.2 = bf16[512,8,128]{0,2,1:T(8,128)(2,1)S(1)} async-done(((bf16[512,8,128]{0,2,1:T(8,128)(2,1)}), bf16[512,8,128]{0,2,1:T(8,128)(2,1)S(1)}, u32[]{:S(2)}, u32[]{:S(2)}) %all-to-all-start.2) | async-done | bytes 1048608 | tf_op jit(solution)/shard_map/all_to_all | solution.py:408
  492.9 3.6 convolution_bitcast_fusion.3
  499.9 7.7 convolution_bitcast_fusion.1
  507.7 7.1 multiply_reduce_fusion.1
  514.8 5.2 multiply_reduce_fusion.2
  520.0 4.8 multiply_convert_fusion.4
  524.8 5.9 multiply_convert_fusion.2
  530.7 7.1 multiply_convert_fusion.1
  548.0 3.7 add_convert_fusion
  551.7 8.8 collective-permute-done.5
  560.5 4.7 add_convert_fusion.1
  566.6 3.6 fusion.45
  570.3 4.9 fusion.43
  575.2 13.8 %multiply_reduce_fusion = (f32[2,2,512]{2,1,0:T(2,128)S(1)}, f32[2,2,512,2048]{3,2,1,0:T(8,128)}) fusion(f32[2,2,512,2048]{3,2,1,0:T(8,128)} %copy-done.2, f32[2,2,512]{2,1,0:T(2,128)S(1)} %copy-done.73, pred[512,2048]{1,0:T(8,128)(4,1)S(1)} %copy-done.11, bf16[2,2048,2,64]{1,0,3,2:T(2,128)(2,1)S(1)} %copy-done.23, bf16[2,512,2,64]{1,0,3,2:T(2,128)(2,1)S(1)} %copy-done.55), kind=kOutput, calls=%fused_computation.1 | convolution fusion | flops 557840384 | bytes 35930112 | tf_op jit(solution)/shard_map/bqhd,bkhd->bhqk/dot_general | solution.py:141
  589.2 16.5 %multiply_convert_fusion = bf16[2,2,512,2048]{3,2,1,0:T(8,128)(2,1)} fusion(f32[2,2,512,2048]{3,2,1,0:T(8,128)} %get-tuple-element.210, f32[2,2,512,2048]{3,2,1,0:T(8,128)} %copy-done.2, f32[2,2,512]{2,1,0:T(2,128)S(1)} %get-tuple-element.209, f32[2,2,512]{2,1,0:T(2,128)S(1)} %copy-done.73, pred[512,2048]{1,0:T(8,128)(4,1)S(1)} %copy-done.11), kind=kLoop, calls=%fused_computation | loop fusion | flops 25165824 | bytes 43008000 | tf_op jit(solution)/shard_map/convert_element_type | solution.py:145
  605.7 6.6 fusion.44
  613.8 6.3 fusion.20
  620.2 4.7 convolution_bitcast_fusion
  627.8 7.6 reduce-scatter.5.cloned.1.call-done
  635.3 71.0 %reduce-scatter.7.cloned.1.call-done = bf16[512,256]{1,0:T(8,128)(2,1)} async-done(((bf16[4096,256]{1,0:T(8,128)(2,1)}), bf16[512,256]{1,0:T(8,128)(2,1)}) %reduce-scatter.7.cloned.1.call-update) | async-done | bytes 262160 | tf_op jit(solution)/shard_map/reduce_scatter | solution.py:413
  717.1 3.9 pad_maximum_fusion.10
  721.1 14.5 %copy.190 = bf16[3,4096,2,64]{3,2,0,1:T(2,128)(2,1)} copy(bf16[3,4096,2,64]{1,3,2,0:T(8,128)(2,1)} %pad_maximum_fusion.10) | data formatting | bytes 6291456 | tf_op jit(solution)/shard_map/stack | solution.py:425
  735.6 8.9 reshape.367
  744.5 73.9 %all_to_all.62 = bf16[8,2,98304]{2,1,0:T(2,128)(2,1)} all-to-all(bf16[8,2,98304]{2,1,0:T(2,128)(2,1)} %reshape.367), channel_id=1, replica_groups=mesh['wide'=4,'narrow'=8] {'narrow'}, dimensions={0} | all-to-all | bytes 6291456 | tf_op jit(solution)/shard_map/all_to_all | solution.py:434
  818.4 8.8 reshape.368
  827.2 15.4 %copy.207 = bf16[3,8,512,2,64]{2,4,3,1,0:T(8,128)(2,1)} copy(bf16[3,8,512,2,64]{4,3,0,2,1:T(2,128)(2,1)} %bitcast.168) | data formatting | bytes 6291456 | tf_op jit(solution)/shard_map/all_to_all | solution.py:434
  842.6 5.5 fusion.65
  859.8 12.5 %collective-permute-done.12 = bf16[1024,256]{1,0:T(8,128)(2,1)S(1)} collective-permute-done((bf16[1024,256]{1,0:T(8,128)(2,1)S(1)}, bf16[1024,256]{1,0:T(8,128)(2,1)S(1)}, u32[]{:S(2)}, u32[]{:S(2)}) %collective-permute-start.12) | collective-permute-done | bytes 524320 | tf_op jit(solution)/shard_map/ppermute | solution.py:182
  873.5 5.0 bitcast_add_fusion
  884.0 51.0 %reduce-scatter.11.cloned.1.call-done = bf16[128,256]{1,0:T(8,128)(2,1)} async-done(((bf16[1024,256]{1,0:T(8,128)(2,1)}), bf16[128,256]{1,0:T(8,128)(2,1)}) %reduce-scatter.11.cloned.1.call-update) | async-done | bytes 65552 | tf_op jit(solution)/shard_map/reduce_scatter | solution.py:256
  945.9 3.9 add_convert_fusion.2
  962.4 7.5 psum.42
  977.0 5.8 fusion.35
  983.4 31.5 %reduce-scatter.9.cloned.1.call-done = bf16[3,256,128]{1,2,0:T(8,128)(2,1)} async-done(((bf16[3,256,1024]{1,2,0:T(8,128)(2,1)}), bf16[3,256,128]{1,2,0:T(8,128)(2,1)}) %reduce-scatter.9.cloned.1.call-update) | async-done | bytes 196624 | tf_op jit(solution)/shard_map/reduce_scatter | solution.py:256
  1017.0 3.8 collective-permute-done.9
  1023.2 40.9 %all-reduce.6 = (f32[1024]{0:T(1024)}, f32[4096]{0:T(1024)S(1)}, f32[1024]{0:T(1024)}, f32[4,1024]{1,0:T(4,128)}, f32[4,1024]{1,0:T(4,128)}) all-reduce(f32[1024]{0:T(1024)} %get-tuple-element.125, f32[4096]{0:T(1024)} %get-tuple-element.212, f32[1024]{0:T(1024)S(1)} %copy-done.77, ...), channel_id=1, replica_groups=mesh['wide'=4,'narrow'=8] {'wide','narrow'}, use_global_device_ids=true, to_apply=%region_37.38 | all-reduce | flops 14336 | bytes 114688 | tf_op jit(solution)/shard_map/psum | solution.py:466
  1064.8 3.6 fusion.34
  (420 shorter events, 181.7 us)
Async XLA Ops:
  7.2 66.5 %copy-start = (bf16[1024,512]{1,0:T(8,128)(2,1)S(1)}, bf16[1024,512]{1,0:T(8,128)(2,1)}, u32[]{:S(2)}) copy-start(bf16[1024,512]{1,0:T(8,128)(2,1)} %param.22) | copy-start | bytes 3145732
  7.2 68.5 %copy-start.17 = (bf16[512,1024]{1,0:T(8,128)(2,1)S(1)}, bf16[512,1024]{1,0:T(8,128)(2,1)}, u32[]{:S(2)}) copy-start(bf16[512,1024]{1,0:T(8,128)(2,1)} %param.14) | copy-start | bytes 3145732
  7.2 70.0 %copy-start.83 = (f32[4,1024]{1,0:T(4,128)S(1)}, f32[4,1024]{1,0:T(4,128)}, u32[]{:S(2)}) copy-start(f32[4,1024]{1,0:T(4,128)} %param.26) | copy-start | bytes 49156
  7.2 70.1 %copy-start.84 = (f32[4,1024]{1,0:T(4,128)S(1)}, f32[4,1024]{1,0:T(4,128)}, u32[]{:S(2)}) copy-start(f32[4,1024]{1,0:T(4,128)} %param.27) | copy-start | bytes 49156
  7.2 66.4 %all-gather.7.cloned.1.call-start = ((), (), s32[]{:S(2)}) async-start(), calls=%async_computation.8 | async-start | bytes 3538944 | tf_op jit(solution)/shard_map/all_gather | solution.py:205
  9.4 67.0 %copy-start.65 = (bf16[512,1024]{1,0:T(8,128)(2,1)S(1)}, bf16[512,1024]{1,0:T(8,128)(2,1)}, u32[]{:S(2)}) copy-start(bf16[512,1024]{1,0:T(8,128)(2,1)} %param.24) | copy-start | bytes 3145732
  9.4 198.3 %all-gather.11.cloned.1.call-start = ((), (), s32[]{:S(2)}) async-start(), calls=%async_computation.10 | async-start | bytes 4718592 | tf_op jit(solution)/shard_map/all_gather | solution.py:205
  74.5 208.7 %all-gather.13.cloned.1.call-start = ((), (), s32[]{:S(2)}) async-start(), calls=%async_computation.11 | async-start | bytes 4718592 | tf_op jit(solution)/shard_map/all_gather | solution.py:205
  74.5 6.1 collective-permute-start
  91.4 116.3 %all-to-all-start = ((bf16[3,512,16,64]{1,3,0,2:T(8,128)(2,1)}), bf16[3,512,16,64]{1,3,0,2:T(8,128)(2,1)}, u32[]{:S(2)}, u32[]{:S(2)}) async-start(bf16[3,512,16,64]{1,3,0,2:T(8,128)(2,1)} %pad_maximum_fusion.9), calls=%async_computation | async-start | bytes 6291456 | tf_op jit(solution)/shard_map/all_to_all | solution.py:340
  95.9 244.2 %all-gather.9.cloned.1.call-start = ((), (), s32[]{:S(2)}) async-start(), calls=%async_computation.9 | async-start | bytes 2359296 | tf_op jit(solution)/shard_map/all_gather | solution.py:346
  98.9 164.8 %copy-start.10 = (pred[512,2048]{1,0:T(8,128)(4,1)}, pred[512,2048]{1,0:T(8,128)(4,1)S(1)}, u32[]{:S(2)}) copy-start(pred[512,2048]{1,0:T(8,128)(4,1)S(1)} %iota_compare_fusion) | copy-start | bytes 3145732
  207.7 137.4 %collective-permute-start.1 = (bf16[512,4096]{1,0:T(8,128)(2,1)}, bf16[512,4096]{1,0:T(8,128)(2,1)}, u32[]{:S(2)}, u32[]{:S(2)}) collective-permute-start(bf16[512,4096]{1,0:T(8,128)(2,1)} %all-gather.11.cloned.1.call-done), channel_id=1, source_target_pairs={{0,8},{8,0},{16,24},{24,16},{1,9},{9,1},{17,25},{25,17},{2,10},{10... | collective-permute-start | bytes 12582920 | tf_op jit(solution)/shard_map/ppermute | solution.py:182
  232.9 16.9 %copy-start.32 = (bf16[2,2048,2,64]{1,3,2,0:T(8,128)(2,1)}, bf16[2,2048,2,64]{1,3,2,0:T(8,128)(2,1)S(1)}, u32[]{:S(2)}) copy-start(bf16[2,2048,2,64]{1,3,2,0:T(8,128)(2,1)S(1)} %copy.159) | copy-start | bytes 3145732
  235.3 36.6 %copy-start.6 = (f32[2,2,512,512]{2,3,1,0:T(8,128)}, f32[2,2,512,512]{2,3,1,0:T(8,128)S(1)}, u32[]{:S(2)}) copy-start(f32[2,2,512,512]{2,3,1,0:T(8,128)S(1)} %get-tuple-element.195) | copy-start | bytes 12582916
  274.4 65.7 %copy-start.64 = (f32[1024]{0:T(1024)S(1)}, f32[1024]{0:T(1024)}, u32[]{:S(2)}) copy-start(f32[1024]{0:T(1024)} %param.21) | copy-start | bytes 12292
  279.1 61.0 %all-to-all-start.1 = ((bf16[8,512,128]{1,2,0:T(8,128)(2,1)}), bf16[8,512,128]{1,2,0:T(8,128)(2,1)S(1)}, u32[]{:S(2)}, u32[]{:S(2)}) async-start(bf16[8,512,128]{1,2,0:T(8,128)(2,1)} %copy.175), calls=%async_computation.1 | async-start | bytes 2097152 | tf_op jit(solution)/shard_map/all_to_all | solution.py:345
  282.9 61.0 %copy-start.82 = (f32[1,1024]{1,0:T(1,128)S(1)}, f32[1,1024]{1,0:T(1,128)}, u32[]{:S(2)}) copy-start(f32[1,1024]{1,0:T(1,128)} %get-tuple-element.183) | copy-start | bytes 12292
  283.2 77.1 %collective-permute-start.2 = (bf16[4096,512]{1,0:T(8,128)(2,1)}, bf16[4096,512]{1,0:T(8,128)(2,1)}, u32[]{:S(2)}, u32[]{:S(2)}) collective-permute-start(bf16[4096,512]{1,0:T(8,128)(2,1)} %all-gather.13.cloned.1.call-done), channel_id=1, source_target_pairs={{0,8},{8,0},{16,24},{24,16},{1,9},{9,1},{17,25},{25,17},{2,10},{10... | collective-permute-start | bytes 12582920 | tf_op jit(solution)/shard_map/ppermute | solution.py:182
  350.1 10.2 copy-start.35
  365.4 9.7 copy-start.21
  407.8 32.1 %collective-permute-start.3 = (bf16[512,4096]{1,0:T(8,128)(2,1)}, bf16[512,4096]{1,0:T(8,128)(2,1)}, u32[]{:S(2)}, u32[]{:S(2)}) collective-permute-start(bf16[512,4096]{1,0:T(8,128)(2,1)} %dynamic-slice_convert_fusion.1), channel_id=1, source_target_pairs={{0,8},{8,0},{16,24},{24,16},{1,9},{9,1},{17,25},{25,17},{2,10},{10... | collective-permute-start | bytes 12582920 | tf_op jit(solution)/shard_map/ppermute | solution.py:182
  422.4 27.3 %collective-permute-start.4 = (bf16[4096,512]{1,0:T(8,128)(2,1)}, bf16[4096,512]{1,0:T(8,128)(2,1)}, u32[]{:S(2)}, u32[]{:S(2)}) collective-permute-start(bf16[4096,512]{1,0:T(8,128)(2,1)} %dynamic-slice_convert_fusion), channel_id=1, source_target_pairs={{0,8},{8,0},{16,24},{24,16},{1,9},{9,1},{17,25},{25,17},{2,10},{10... | collective-permute-start | bytes 12582920 | tf_op jit(solution)/shard_map/ppermute | solution.py:182
  460.3 29.7 %all-to-all-start.2 = ((bf16[512,8,128]{0,2,1:T(8,128)(2,1)}), bf16[512,8,128]{0,2,1:T(8,128)(2,1)S(1)}, u32[]{:S(2)}, u32[]{:S(2)}) async-start(bf16[512,8,128]{0,2,1:T(8,128)(2,1)} %bitcast.29), calls=%async_computation.2 | async-start | bytes 2097152 | tf_op jit(solution)/shard_map/all_to_all | solution.py:408
  463.9 171.4 %reduce-scatter.5.cloned.1.call-start = ((), (), s32[]{:S(2)}) async-start(), calls=%async_computation.12 | async-start | bytes 2359296 | tf_op jit(solution)/shard_map/reduce_scatter | solution.py:412
  467.7 80.0 %collective-permute-start.6 = (bf16[4096,256]{1,0:T(8,128)(2,1)}, bf16[4096,256]{1,0:T(8,128)(2,1)}, u32[]{:S(2)}, u32[]{:S(2)}) collective-permute-start(bf16[4096,256]{1,0:T(8,128)(2,1)} %dynamic-slice_convert_fusion.3), channel_id=1, source_target_pairs={{0,16},{8,24},{16,0},{24,8},{1,17},{9,25},{17,1},{25,9},{2,18},{10... | collective-permute-start | bytes 6291464 | tf_op jit(solution)/shard_map/ppermute | solution.py:182
  473.0 87.5 %collective-permute-start.5 = (bf16[256,4096]{1,0:T(8,128)(2,1)}, bf16[256,4096]{1,0:T(8,128)(2,1)}, u32[]{:S(2)}, u32[]{:S(2)}) collective-permute-start(bf16[256,4096]{1,0:T(8,128)(2,1)} %dynamic-slice_convert_fusion.4), channel_id=1, source_target_pairs={{0,16},{8,24},{16,0},{24,8},{1,17},{9,25},{17,1},{25,9},{2,18},{10... | collective-permute-start | bytes 6291464 | tf_op jit(solution)/shard_map/ppermute | solution.py:182
  496.5 11.1 %slice-start.4 = ((s8[12582912]{0:T(1024)(128)(4,1)}), s8[4194304]{0:T(1024)(128)(4,1)S(1)}, s32[]{:S(2)}) async-start(s8[12582912]{0:T(1024)(128)(4,1)} %bitcast.161), calls=%async_computation.20 | async-start | bytes 8388608
  499.9 14.9 %slice-start.7 = ((s8[8388608]{0:T(1024)(128)(4,1)}), s8[4194304]{0:T(1024)(128)(4,1)S(1)}, s32[]{:S(2)}) async-start(s8[8388608]{0:T(1024)(128)(4,1)} %bitcast.163), calls=%async_computation.23 | async-start | bytes 8388608
  551.7 13.6 %copy-start.16 = (bf16[2,2,512,512]{2,3,1,0:T(8,128)(2,1)S(1)}, bf16[2,2,512,512]{2,3,1,0:T(8,128)(2,1)}, u32[]{:S(2)}) copy-start(bf16[2,2,512,512]{2,3,1,0:T(8,128)(2,1)} %multiply_convert_fusion.4) | copy-start | bytes 6291460
  551.7 13.7 %copy-start.30 = (bf16[2,2048,2,64]{1,3,2,0:T(8,128)(2,1)S(1)}, bf16[2,2048,2,64]{1,3,2,0:T(8,128)(2,1)}, u32[]{:S(2)}) copy-start(bf16[2,2048,2,64]{1,3,2,0:T(8,128)(2,1)} %copy.163) | copy-start | bytes 3145732
  565.3 141.0 %reduce-scatter.7.cloned.1.call-start = ((), (), s32[]{:S(2)}) async-start(), calls=%async_computation.13 | async-start | bytes 2359296 | tf_op jit(solution)/shard_map/reduce_scatter | solution.py:413
  589.1 346.0 %reduce-scatter.11.cloned.1.call-start = ((), (), s32[]{:S(2)}) async-start(), calls=%async_computation.15 | async-start | bytes 589824 | tf_op jit(solution)/shard_map/reduce_scatter | solution.py:256
  589.1 16.6 %copy-start.22 = (bf16[2,2048,2,64]{1,0,3,2:T(2,128)(2,1)S(1)}, bf16[2,2048,2,64]{1,0,3,2:T(2,128)(2,1)}, u32[]{:S(2)}) copy-start(bf16[2,2048,2,64]{1,0,3,2:T(2,128)(2,1)} %squeeze.19) | copy-start | bytes 3145732
  589.1 31.0 %slice-start = ((s8[16777216]{0:T(1024)(128)(4,1)}), s8[4194304]{0:T(1024)(128)(4,1)S(1)}, s32[]{:S(2)}) async-start(s8[16777216]{0:T(1024)(128)(4,1)} %bitcast.159), calls=%async_computation.16 | async-start | bytes 8388608
  589.1 31.0 %slice-start.1 = ((s8[16777216]{0:T(1024)(128)(4,1)}), s8[4194304]{0:T(1024)(128)(4,1)S(1)}, s32[]{:S(2)}) async-start(s8[16777216]{0:T(1024)(128)(4,1)} %bitcast.159), calls=%async_computation.17 | async-start | bytes 8388608
  589.1 31.0 %slice-start.2 = ((s8[16777216]{0:T(1024)(128)(4,1)}), s8[4194304]{0:T(1024)(128)(4,1)S(1)}, s32[]{:S(2)}) async-start(s8[16777216]{0:T(1024)(128)(4,1)} %bitcast.159), calls=%async_computation.18 | async-start | bytes 8388608
  605.7 14.5 %slice-start.3 = ((s8[16777216]{0:T(1024)(128)(4,1)}), s8[4194304]{0:T(1024)(128)(4,1)S(1)}, s32[]{:S(2)}) async-start(s8[16777216]{0:T(1024)(128)(4,1)} %bitcast.159), calls=%async_computation.19 | async-start | bytes 8388608
  627.5 78.8 %copy-start.52 = (f32[2048,32]{0,1:T(8,128)S(1)}, f32[2048,32]{0,1:T(8,128)}, u32[]{:S(2)}) copy-start(f32[2048,32]{0,1:T(8,128)} %copy-done.51) | copy-start | bytes 786436
  627.5 78.8 %copy-start.54 = (f32[2048,32]{0,1:T(8,128)S(1)}, f32[2048,32]{0,1:T(8,128)}, u32[]{:S(2)}) copy-start(f32[2048,32]{0,1:T(8,128)} %copy-done.53) | copy-start | bytes 786436
  712.3 8.7 copy-start.24
  827.2 15.4 %copy-start.18 = (bf16[512,1024]{1,0:T(8,128)(2,1)S(1)}, bf16[512,1024]{1,0:T(8,128)(2,1)}, u32[]{:S(2)}) copy-start(bf16[512,1024]{1,0:T(8,128)(2,1)} %param.14) | copy-start | bytes 3145732
  827.2 15.4 %copy-start.76 = (f32[512]{0:T(512)S(1)}, f32[512]{0:T(512)}, u32[]{:S(2)}) copy-start(f32[512]{0:T(512)} %copy-done.75) | copy-start | bytes 6148
  827.2 15.4 %copy-start.86 = (f32[1,1024]{1,0:T(1,128)S(1)}, f32[1,1024]{1,0:T(1,128)}, u32[]{:S(2)}) copy-start(f32[1,1024]{1,0:T(1,128)} %copy-done.85) | copy-start | bytes 12292
  827.2 15.4 %copy-start.89 = (f32[512]{0:T(512)S(1)}, f32[512]{0:T(512)}, u32[]{:S(2)}) copy-start(f32[512]{0:T(512)} %copy-done.88) | copy-start | bytes 6148
  827.2 15.4 %copy-start.92 = (f32[1,1024]{1,0:T(1,128)S(1)}, f32[1,1024]{1,0:T(1,128)}, u32[]{:S(2)}) copy-start(f32[1,1024]{1,0:T(1,128)} %copy-done.91) | copy-start | bytes 12292
  850.4 23.1 %collective-permute-start.7 = (bf16[3,512,1024]{1,2,0:T(8,128)(2,1)}, bf16[3,512,1024]{1,2,0:T(8,128)(2,1)}, u32[]{:S(2)}, u32[]{:S(2)}) collective-permute-start(bf16[3,512,1024]{1,2,0:T(8,128)(2,1)} %fusion.18), channel_id=1, source_target_pairs={{0,8},{8,0},{16,24},{24,16},{1,9},{9,1},{17,25},{25,17},{2,10},{10... | collective-permute-start | bytes 9437192 | tf_op jit(solution)/shard_map/ppermute | solution.py:182
  854.2 3.6 collective-permute-start.11
  858.2 14.0 %collective-permute-start.12 = (bf16[1024,256]{1,0:T(8,128)(2,1)S(1)}, bf16[1024,256]{1,0:T(8,128)(2,1)S(1)}, u32[]{:S(2)}, u32[]{:S(2)}) collective-permute-start(bf16[1024,256]{1,0:T(8,128)(2,1)S(1)} %dynamic-slice_convert_fusion.7), channel_id=1, source_target_pairs={{0,16},{8,24},{16,0},{24,8},{1,17},{9,25},{17,1},{25,9},{2,18},{10... | collective-permute-start | bytes 1572872 | tf_op jit(solution)/shard_map/ppermute | solution.py:182
  873.3 63.3 %copy-start.66 = (bf16[256,512]{1,0:T(8,128)(2,1)S(1)}, bf16[256,512]{1,0:T(8,128)(2,1)}, u32[]{:S(2)}) copy-start(bf16[256,512]{1,0:T(8,128)(2,1)} %reduce-scatter.5.cloned.1.call-done) | copy-start | bytes 786436
  873.3 141.6 %reduce-scatter.9.cloned.1.call-start = ((), (), s32[]{:S(2)}) async-start(), calls=%async_computation.14 | async-start | bytes 1769472 | tf_op jit(solution)/shard_map/reduce_scatter | solution.py:256
  882.6 63.4 %collective-permute-start.8 = (bf16[3,256,1024]{1,2,0:T(8,128)(2,1)}, bf16[3,256,1024]{1,2,0:T(8,128)(2,1)}, u32[]{:S(2)}, u32[]{:S(2)}) collective-permute-start(bf16[3,256,1024]{1,2,0:T(8,128)(2,1)} %dynamic-slice_convert_fusion.5), channel_id=1, source_target_pairs={{0,16},{8,24},{16,0},{24,8},{1,17},{9,25},{17,1},{25,9},{2,18},{10... | collective-permute-start | bytes 4718600 | tf_op jit(solution)/shard_map/ppermute | solution.py:182
  935.0 5.3 collective-permute-start.13
  936.5 6.6 collective-permute-start.15
  941.9 11.7 %collective-permute-start.14 = (bf16[128,512]{1,0:T(8,128)(2,1)}, bf16[128,512]{1,0:T(8,128)(2,1)}, u32[]{:S(2)}, u32[]{:S(2)}) collective-permute-start(bf16[128,512]{1,0:T(8,128)(2,1)} %pad_maximum_fusion.18), channel_id=1, source_target_pairs={{0,8},{8,0},{16,24},{24,16},{1,9},{9,1},{17,25},{25,17},{2,10},{10... | collective-permute-start | bytes 393224 | tf_op jit(solution)/shard_map/ppermute | solution.py:182
  941.9 9.0 collective-permute-start.17
  945.7 24.8 %collective-permute-start.16 = (bf16[512,512]{1,0:T(8,128)(2,1)}, bf16[512,512]{1,0:T(8,128)(2,1)}, u32[]{:S(2)}, u32[]{:S(2)}) collective-permute-start(bf16[512,512]{1,0:T(8,128)(2,1)} %pad_maximum_fusion.15), channel_id=1, source_target_pairs={{0,8},{8,0},{16,24},{24,16},{1,9},{9,1},{17,25},{25,17},{2,10},{10... | collective-permute-start | bytes 1572872 | tf_op jit(solution)/shard_map/ppermute | solution.py:182
  953.5 17.0 %collective-permute-start.18 = (bf16[512,512]{1,0:T(8,128)(2,1)}, bf16[512,512]{1,0:T(8,128)(2,1)}, u32[]{:S(2)}, u32[]{:S(2)}) collective-permute-start(bf16[512,512]{1,0:T(8,128)(2,1)} %pad_maximum_fusion.16), channel_id=1, source_target_pairs={{0,8},{8,0},{16,24},{24,16},{1,9},{9,1},{17,25},{25,17},{2,10},{10... | collective-permute-start | bytes 1572872 | tf_op jit(solution)/shard_map/ppermute | solution.py:182
  976.9 45.5 %copy-start.78 = (f32[1024]{0:T(1024)S(1)}, f32[1024]{0:T(1024)}, u32[]{:S(2)}) copy-start(f32[1024]{0:T(1024)} %get-tuple-element.114) | copy-start | bytes 12292
  977.0 45.5 %copy-start.80 = (f32[1024]{0:T(1024)S(1)}, f32[1024]{0:T(1024)}, u32[]{:S(2)}) copy-start(f32[1024]{0:T(1024)} %get-tuple-element.117) | copy-start | bytes 12292
  977.0 46.2 %copy-start.77 = (f32[1024]{0:T(1024)S(1)}, f32[1024]{0:T(1024)}, u32[]{:S(2)}) copy-start(f32[1024]{0:T(1024)} %get-tuple-element.123) | copy-start | bytes 12292
  977.0 87.8 %copy-start.14 = (f32[512,1024]{1,0:T(8,128)S(1)}, f32[512,1024]{1,0:T(8,128)}, u32[]{:S(2)}) copy-start(f32[512,1024]{1,0:T(8,128)} %copy-done.13) | copy-start | bytes 6291460
  1014.9 5.9 collective-permute-start.9
  1022.5 46.0 %collective-permute-start.10 = (bf16[3,512,128]{1,2,0:T(8,128)(2,1)}, bf16[3,512,128]{1,2,0:T(8,128)(2,1)}, u32[]{:S(2)}, u32[]{:S(2)}) collective-permute-start(bf16[3,512,128]{1,2,0:T(8,128)(2,1)} %pad_maximum_fusion.17), channel_id=1, source_target_pairs={{0,8},{8,0},{16,24},{24,16},{1,9},{9,1},{17,25},{25,17},{2,10},{10... | collective-permute-start | bytes 1179656 | tf_op jit(solution)/shard_map/ppermute | solution.py:182
  (76 other events, 364.3 us)
Sparse Core Ops, SparseCore 0:
  10.8 62.7 all-gather.6
  76.2 131.4 all-gather.10
  210.4 69.9 all-gather.12
  282.4 57.6 all-gather.8
  565.4 69.8 reduce-scatter.4
  638.7 67.5 reduce-scatter.6
  873.4 61.5 reduce-scatter.10
  949.9 64.8 reduce-scatter.8

commit v11 on v8

--- a/solution.py
+++ b/solution.py
@@ -192,20 +192,14 @@
     return jnp.concatenate([first, second], axis=split_axis)
 
 
-def chip_half(rows, core, split_axis):
+def reduce_halves(rows, core, split_axis, scatter_axis):
     half = rows.shape[split_axis] // 2
     mine = lax.dynamic_slice_in_dim(rows, core * half, half, axis=split_axis)
     other = lax.dynamic_slice_in_dim(rows, (1 - core) * half, half, axis=split_axis)
     chip_sum = mine + swap_cores(other.astype(jnp.bfloat16)).astype(jnp.float32)
-    return chip_sum.astype(jnp.bfloat16)
-
-
-def reduce_halves(rows, core, split_axis, scatter_axis):
-    return scatter_slots(chip_half(rows, core, split_axis), core, split_axis, scatter_axis)
-
-
-def scatter_slots(chip_sum, core, split_axis, scatter_axis):
-    part = lax.psum_scatter(chip_sum, "narrow", scatter_dimension=scatter_axis, tiled=True)
+    part = lax.psum_scatter(
+        chip_sum.astype(jnp.bfloat16), "narrow", scatter_dimension=scatter_axis, tiled=True
+    )
     empty = jnp.zeros_like(part)
     return jnp.stack(
         [jnp.where(core == 0, part, empty), jnp.where(core == 0, empty, part)], axis=split_axis
@@ -357,8 +351,7 @@
     third_grad = lax.dot_general(
         hidden_grad, up_full, (((1,), (1,)), ((), ())), preferred_element_type=jnp.float32
     )
-    up_chip = chip_half(up_wgrad_rows, core, 0)
-    down_chip = chip_half(down_wgrad_rows, core, 1)
+    up_slots = reduce_halves(up_wgrad_rows, core, 0, 1)
     residual_grad = upstream + norm_back(normed_third, inverse_third, norm_gains[2], third_grad)
     branch_grad = norm_back(normed_second, inverse_second, norm_gains[1], residual_grad).astype(
         jnp.bfloat16
@@ -366,11 +359,6 @@
     attn_grad_rows = lax.dot_general(
         branch_grad, out_full, (((1,), (1,)), ((), ())), preferred_element_type=jnp.float32
     ).astype(jnp.bfloat16)
-    attn_grad_rows, up_chip, down_chip = lax.optimization_barrier(
-        (attn_grad_rows, up_chip, down_chip)
-    )
-    up_slots = scatter_slots(up_chip, core, 0, 1)
-    down_slots = scatter_slots(down_chip, core, 1, 0)
     attn_grad = lax.all_to_all(attn_grad_rows, "narrow", 1, 0, tiled=True)
     attn_grad = attn_grad.reshape(query.shape)
     query_grad, keys_grad, values_grad = attend_backward(
@@ -379,7 +367,7 @@
     out_wgrad_rows = lax.dot_general(
         attn_rows, branch_grad, (((0,), (0,)), ((), ())), preferred_element_type=jnp.float32
     )
-    out_slots = reduce_halves(out_wgrad_rows, core, 1, 0)
+    down_slots, out_slots = reduce_column_halves((down_wgrad_rows, out_wgrad_rows), core)
     qkv_grad = jnp.stack(
         [
             rotate_back(query_grad, cos_table, sine_table),

time: 972 us -> 1000 us (1.029)
  blocking collectives: 81.9 us -> 236 us
  waiting for transfers between devices: 458 us -> 324 us
    all_to_all x0 -> x1, blocking collectives: none -> 154 us  [shards(): qkv_grad_rows = lax.all_to_all(qkv_grad, 'narrow', 1, 2, tiled=True)]
    all_to_all x1 -> x0, waiting for transfers between devices: 125 us -> none  [shards(): qkv_grad_rows = lax.all_to_all(qkv_grad, 'narrow', 1, 2, tiled=True)]
    all_to_all x1, waiting for transfers between devices: 27 us -> 9.27 us  [shards(): attn_grad = lax.all_to_all(attn_grad_rows, 'narrow', 1, 0, tiled=True)]
    reduce_scatter x4 -> x3, waiting for transfers between devices: 77.6 us -> 88.9 us  [the longest x2 74.2 us: reduce_halves(): lax.psum_scatter(chip_sum.astype(jnp.bfloat16), 'narrow', scatter_dimensi...]
  transfers between devices with their start and end apart: 20 -> 18, of which waited for: 12 -> 10; matrix products, arithmetic and copies ran while one was open for 31% -> 31% of each run, Pallas kernels for 0% -> 0%
where the time goes in v11:
time: 1000 us; the launch traced here: 993 us
  waiting for transfers between devices  324 us (32%)
  blocking collectives  236 us (24%)
  matrix products  196 us (20%)
  other arithmetic  113 us (11%)
  local copies, waits for them, and re-layouts  92.9 us (9%)
  between operations  16.1 us (2%)
  starting transfers between devices  14.7 us (1%)
    all_to_all x1, blocking collectives, shards(): qkv_grad_rows = lax.all_to_all(qkv_grad, 'narrow', 1, 2, tiled=True)  154 us
    all_gather x3, waiting for transfers between devices, gather_mine(): return lax.all_gather(mine, 'narrow', axis=gather_axis, tiled=True)  151 us
    reduce_scatter x2, waiting for transfers between devices, reduce_halves(): lax.psum_scatter(chip_sum.astype(jnp.bfloat16), 'narrow', scatter_dimensi...  74.2 us
    all_gather x1, waiting for transfers between devices, shards(): out_full = lax.all_gather(out_weight, 'narrow', axis=0, tiled=True)  43.5 us
    psum x1, blocking collectives, shards(): lax.psum((gain_local, bias_local, out_blocal, down_blocal, up_bgrad_rows)...  41.8 us
    dot_general x4, matrix products, attend_backward(): jnp.einsum('bqhd,bkhd->bhqk', grad_block, value_block, preferred_element_...  32.8 us
    all_gather x1, blocking collectives, shards(): bias_full = lax.all_gather(bias_flat, 'narrow', axis=0)  32.8 us
    convert_element_type x4, other arithmetic, attend_backward(): scores_grad = (probs_full * (probs_grad - row_dot)).astype(jnp.bfloat16)  26.9 us
  transfers between devices with their start and end apart: 18, of which 10 were waited for; matrix products, arithmetic and copies ran while one was open for 31% of the time, Pallas kernels for 0%

profile of v11, /device:TPU:0, one launch (start us, length us, event | category | flops | bytes accessed | tf_op | source)
XLA Modules:
  0.0 993.4 jit_solution(8454890153498322201)
XLA Ops:
  10.2 32.8 %all-gather.1 = f32[8,1,896]{2,1,0:T(1,128)S(1)} all-gather(f32[1,1,896]{2,1,0:T(1,128)S(1)} %reshape.449), channel_id=2, replica_groups=mesh['wide'=4,'narrow'=8] {'narrow'}, dimensions={0}, use_global_device_ids=true | all-gather | bytes 32256 | tf_op jit(solution)/shard_map/all_gather | solution.py:270
  43.0 30.6 %all-gather.7.cloned.1.call-done = bf16[3,512,1024]{1,2,0:T(8,128)(2,1)} async-done(((bf16[3,512,128]{1,2,0:T(8,128)(2,1)}), bf16[3,512,1024]{1,2,0:T(8,128)(2,1)}) %all-gather.7.cloned.1.call-update) | async-done | bytes 3145744 | tf_op jit(solution)/shard_map/all_gather | solution.py:181
  80.6 3.6 broadcast_select_fusion.5
  84.3 3.7 add_bitcast_fusion
  89.8 4.7 copy.113
  94.5 4.6 all-to-all-start
  102.1 120.3 %all-gather.11.cloned.1.call-done = bf16[512,4096]{1,0:T(8,128)(2,1)} async-done(((bf16[512,512]{1,0:T(8,128)(2,1)}), bf16[512,4096]{1,0:T(8,128)(2,1)}) %all-gather.11.cloned.1.call-update) | async-done | bytes 4194320 | tf_op jit(solution)/shard_map/all_gather | solution.py:181
  222.4 8.4 all-to-all-done
  230.8 4.6 copy.247
  261.7 3.5 exponential_reduce_fusion.1
  265.2 12.7 %fusion.57 = bf16[2,512,2,64]{1,3,2,0:T(8,128)(2,1)} fusion(bf16[2,2048,2,64]{1,3,2,0:T(8,128)(2,1)S(1)} %copy-done.26, f32[2,2,512,1024]{3,2,1,0:T(8,128)S(1)} %get-tuple-element.107, f32[2,2,512]{2,1,0:T(2,128)S(1)} %log_add_fusion.2, pred[512,1024]{1,0:T(8,128)(4,1)S(1)} %copy-done.18), kind=kOutput, calls=%fused_computation.153 | convolution fusion | flops 276955136 | bytes 9707520 | tf_op jit(solution)/shard_map/bhqk,bkhd->bqhd/dot_general | solution.py:117
  277.9 4.3 fusion.59
  282.2 4.9 fusion
  287.1 4.5 exponential_reduce_fusion
  292.9 7.1 fusion.60
  309.1 4.5 all-to-all-start.1
  314.0 43.5 %all-gather.9.cloned.1.call-done = bf16[1024,1024]{1,0:T(8,128)(2,1)} async-done(((bf16[128,1024]{1,0:T(8,128)(2,1)}), bf16[1024,1024]{1,0:T(8,128)(2,1)}) %all-gather.9.cloned.1.call-update) | async-done | bytes 2097168 | tf_op jit(solution)/shard_map/all_gather | solution.py:305
  357.5 3.3 add_reduce_fusion.1
  363.4 3.9 broadcast_select_fusion.3
  367.3 10.3 %multiply_convert_fusion.3 = (bf16[512,4096]{1,0:T(8,128)(2,1)}, f32[512,4096]{1,0:T(8,128)}) fusion(f32[4096]{0:T(1024)S(1)} %bitcast.224, bf16[512,4096]{1,0:T(8,128)(2,1)} %get-tuple-element.55, bf16[512,4096]{1,0:T(8,128)(2,1)S(1)} %get-tuple-element.54, f32[512,1024]{1,0:T(8,128)S(1)} %get-tuple-element.51, f32[1024]{0:T(1024)S(1)} %bitcast.234, ...), kind=kOutput, calls=%fused_computation.29 | convolution fusion | flops 4326948864 | bytes 23097344 | tf_op jit(solution)/shard_map/dot_general | solution.py:313
  377.6 5.3 broadcast_select_fusion.1
  382.9 9.3 add_reduce_fusion
  394.3 2.7 convert_reduce_fusion.2
  397.0 12.8 %convert_reduce_fusion = (f32[4096]{0:T(1024)}, bf16[512,4096]{1,0:T(8,128)(2,1)}) fusion(f32[512,4096]{1,0:T(8,128)} %get-tuple-element.113, f32[4096]{0:T(1024)S(1)} %bitcast.225, bf16[512,1024]{1,0:T(8,128)(2,1)S(1)} %get-tuple-element.46, bf16[4096,512]{1,0:T(8,128)(2,1)} %get-tuple-element.53, bf16[4096,512]{1,0:T(8,128)(2,1)} %get-tuple-element.52), kind=kOutput, calls=%fused_computation.22 | convolution fusion | flops 4339003392 | bytes 22052864 | tf_op jit(solution)/shard_map/dot_general | solution.py:343
  409.8 10.3 %multiply_reduce_fusion.5 = (f32[1024]{0:T(1024)}, f32[512]{0:T(512)S(1)}, f32[512]{0:T(512)S(1)}, f32[1024]{0:T(1024)}, f32[512,1024]{1,0:T(8,128)}) fusion(f32[512,1024]{1,0:T(8,128)S(1)} %get-tuple-element.51, f32[512]{0:T(512)S(1)} %add_rsqrt_fusion.1, f32[512]{0:T(512)S(1)} %broadcast_multiply_fusion.9, f32[1024]{0:T(1024)S(1)} %bitcast.216, ...), kind=kOutput, calls=%fused_computation.104 | convolution fusion | flops 4316460032 | bytes 16797696 | tf_op jit(solution)/shard_map/dot_general | solution.py:351
  420.1 10.6 %fusion.124 = f32[1024,4096]{1,0:T(8,128)} fusion(bf16[512,4096]{1,0:T(8,128)(2,1)} %get-tuple-element.127, f32[512,1024]{1,0:T(8,128)S(1)} %get-tuple-element.51, f32[1024]{0:T(1024)S(1)} %bitcast.235, f32[1024]{0:T(1024)S(1)} %bitcast.217, f32[512]{0:T(512)S(1)} %add_rsqrt_fusion.1, f32[512]{0:T(512)S(1)} %broadcast_multiply_fusion.9), kind=kOutput, calls=%fused_computation.285 | convolution fusion | flops 4297588736 | bytes 23080960 | tf_op jit(solution)/shard_map/dot_general | solution.py:348
  430.7 8.2 fusion.133
  438.9 3.1 multiply_reduce_fusion.6
  447.1 4.3 all-to-all-start.2
  451.4 2.8 fusion.134
  454.5 6.0 dynamic-slice_convert_fusion
  461.0 6.0 dynamic-slice_convert_fusion.1
  468.3 9.3 all-to-all-done.2
  477.6 2.8 copy.131
  482.8 2.6 fusion.129
  485.5 3.9 multiply_reduce_fusion.3
  489.5 7.6 multiply_reduce_fusion.2
  497.1 7.1 multiply_reduce_fusion.1
  504.3 7.4 multiply_convert_fusion.1
  514.4 2.8 fusion.52
  519.8 4.7 multiply_convert_fusion.2
  528.7 14.2 %multiply_reduce_fusion = (f32[2,2,512]{2,1,0:T(2,128)S(1)}, f32[2,2,512,2048]{3,2,1,0:T(8,128)}) fusion(f32[2,2,512,2048]{3,2,1,0:T(8,128)} %copy-done.2, f32[2,2,512]{2,1,0:T(2,128)S(1)} %log_add_fusion, pred[512,2048]{1,0:T(8,128)(4,1)S(1)} %iota_compare_fusion, bf16[2,2048,2,64]{1,0,3,2:T(2,128)(2,1)S(1)} %copy-done.23, ...), kind=kOutput, calls=%fused_computation.1 | convolution fusion | flops 557840384 | bytes 35930112 | tf_op jit(solution)/shard_map/bqhd,bkhd->bhqk/dot_general | solution.py:141
  542.8 12.2 %multiply_convert_fusion = bf16[2,2,512,2048]{3,2,1,0:T(8,128)(2,1)S(1)} fusion(f32[2,2,512,2048]{3,2,1,0:T(8,128)} %get-tuple-element.118, f32[2,2,512,2048]{3,2,1,0:T(8,128)} %copy-done.2, f32[2,2,512]{2,1,0:T(2,128)S(1)} %get-tuple-element.117, f32[2,2,512]{2,1,0:T(2,128)S(1)} %log_add_fusion, pred[512,2048]{1,0:T(8,128)(4,1)S(1)} %iota_compare_fusion), kind=kLoop, calls=%fused_computation | loop fusion | flops 25165824 | bytes 43008000 | tf_op jit(solution)/shard_map/convert_element_type | solution.py:145
  555.0 3.5 fusion.53
  558.6 8.0 add_convert_fusion
  582.8 4.4 convolution_bitcast_fusion.3
  588.3 6.0 convolution_bitcast_fusion.2
  594.4 7.7 convolution_bitcast_fusion.1
  602.1 7.5 fusion.29
  609.7 6.2 add_convert_fusion.1
  616.0 2.9 pad_maximum_fusion.7
  624.4 7.2 copy.144
  631.6 154.4 %all_to_all.65 = bf16[3,4096,128]{2,0,1:T(4,128)(2,1)S(1)} all-to-all(bf16[3,4096,128]{2,0,1:T(4,128)(2,1)} %copy.144), channel_id=1, replica_groups=mesh['wide'=4,'narrow'=8] {'narrow'}, dimensions={1} | all-to-all | bytes 6291456 | tf_op jit(solution)/shard_map/all_to_all | solution.py:380
  787.3 3.6 fusion.20
  791.5 5.6 collective-permute-done.3
  797.1 2.7 fusion.11
  802.3 7.3 psum.71
  812.4 14.7 %reduce-scatter.6.cloned.1.call-done = bf16[1,640,512]{2,1,0:T(8,128)(2,1)} async-done(((bf16[8,640,512]{2,1,0:T(8,128)(2,1)}), bf16[1,640,512]{2,1,0:T(8,128)(2,1)}) %reduce-scatter.6.cloned.1.call-update) | async-done | bytes 655376 | tf_op jit(solution)/shard_map/reduce_scatter | solution.py:218
  831.2 74.2 %reduce-scatter.4.cloned.1.call-done = bf16[3,512,128]{1,2,0:T(8,128)(2,1)} async-done(((bf16[3,512,1024]{1,2,0:T(8,128)(2,1)}), bf16[3,512,128]{1,2,0:T(8,128)(2,1)}) %reduce-scatter.4.cloned.1.call-update) | async-done | bytes 393232 | tf_op jit(solution)/shard_map/reduce_scatter | solution.py:200
  907.8 9.0 fusion.44
  916.9 41.8 %all-reduce.6 = (f32[1024]{0:T(1024)}, f32[4096]{0:T(1024)S(1)}, f32[1024]{0:T(1024)}, f32[4,1024]{1,0:T(4,128)}, f32[4,1024]{1,0:T(4,128)}) all-reduce(f32[1024]{0:T(1024)S(1)} %copy-done.77, f32[4096]{0:T(1024)S(1)} %copy-done.74, f32[1024]{0:T(1024)S(1)} %copy-done.66, ...), channel_id=1, replica_groups=mesh['wide'=4,'narrow'=8] {'wide','narrow'}, use_global_device_ids=true, to_apply=%region_37.38 | all-reduce | flops 14336 | bytes 114688 | tf_op jit(solution)/shard_map/psum | solution.py:417
  959.4 3.3 fusion.43
  962.7 14.7 %all-reduce.10.cloned.1.call-done = (bf16[3,1024,128]{2,1,0:T(8,128)(2,1)}, bf16[128,1024]{1,0:T(8,128)(2,1)}, bf16[1024,512]{1,0:T(8,128)(2,1)}, bf16[512,1024]{1,0:T(8,128)(2,1)}) async-done(((bf16[3,1024,128]{2,1,0:T(8,128)(2,1)}, bf16[128,1024]{1,0:T(8,128)(2,1)}, bf16[1024,512]{1,0:T(8,128)(2,1)}, bf16[512,1024]{1,0:T(8,128)(2,1)}), (bf16[3,1024,128]{2,1,0:T(8,128)(2,1)}, bf16[128,1024]{1,0:T(8,128)(2,1)}, ...) | async-done | bytes 3145744 | tf_op jit(solution)/shard_map/psum | solution.py:410
  981.8 2.8 reshape.445
  (366 shorter events, 118.0 us)
Async XLA Ops:
  7.2 66.5 %copy-start = (bf16[1024,512]{1,0:T(8,128)(2,1)S(1)}, bf16[1024,512]{1,0:T(8,128)(2,1)}, u32[]{:S(2)}) copy-start(bf16[1024,512]{1,0:T(8,128)(2,1)} %param.22) | copy-start | bytes 3145732
  7.2 67.5 %copy-start.16 = (bf16[512,1024]{1,0:T(8,128)(2,1)S(1)}, bf16[512,1024]{1,0:T(8,128)(2,1)}, u32[]{:S(2)}) copy-start(bf16[512,1024]{1,0:T(8,128)(2,1)} %param.14) | copy-start | bytes 3145732
  7.2 70.1 %copy-start.75 = (f32[4,1024]{1,0:T(4,128)S(1)}, f32[4,1024]{1,0:T(4,128)}, u32[]{:S(2)}) copy-start(f32[4,1024]{1,0:T(4,128)} %param.26) | copy-start | bytes 49156
  7.2 70.7 %copy-start.76 = (f32[4,1024]{1,0:T(4,128)S(1)}, f32[4,1024]{1,0:T(4,128)}, u32[]{:S(2)}) copy-start(f32[4,1024]{1,0:T(4,128)} %param.27) | copy-start | bytes 49156
  7.2 66.4 %all-gather.7.cloned.1.call-start = ((), (), s32[]{:S(2)}) async-start(), calls=%async_computation.7 | async-start | bytes 3538944 | tf_op jit(solution)/shard_map/all_gather | solution.py:181
  9.4 66.9 %copy-start.58 = (bf16[512,1024]{1,0:T(8,128)(2,1)S(1)}, bf16[512,1024]{1,0:T(8,128)(2,1)}, u32[]{:S(2)}) copy-start(bf16[512,1024]{1,0:T(8,128)(2,1)} %param.24) | copy-start | bytes 3145732
  9.4 213.0 %all-gather.11.cloned.1.call-start = ((), (), s32[]{:S(2)}) async-start(), calls=%async_computation.9 | async-start | bytes 4718592 | tf_op jit(solution)/shard_map/all_gather | solution.py:181
  74.5 239.4 %all-gather.13.cloned.1.call-start = ((), (), s32[]{:S(2)}) async-start(), calls=%async_computation.10 | async-start | bytes 4718592 | tf_op jit(solution)/shard_map/all_gather | solution.py:181
  74.5 6.1 collective-permute-start
  74.9 9.4 copy-start.64
  76.3 7.9 copy-start.37
  76.3 7.9 copy-start.39
  77.3 6.9 copy-start.80
  94.5 136.3 %all-to-all-start = ((bf16[3,512,1024]{1,0,2:T(4,128)(2,1)}), bf16[3,512,1024]{1,0,2:T(4,128)(2,1)}, u32[]{:S(2)}, u32[]{:S(2)}) async-start(bf16[3,512,1024]{1,0,2:T(4,128)(2,1)} %copy.113), calls=%async_computation | async-start | bytes 8388608 | tf_op jit(solution)/shard_map/all_to_all | solution.py:299
  99.1 258.4 %all-gather.9.cloned.1.call-start = ((), (), s32[]{:S(2)}) async-start(), calls=%async_computation.8 | async-start | bytes 2359296 | tf_op jit(solution)/shard_map/all_gather | solution.py:305
  101.4 402.8 %copy-start.11 = (pred[512,1536]{1,0:T(8,128)(4,1)}, pred[512,1536]{1,0:T(8,128)(4,1)S(1)}, u32[]{:S(2)}) copy-start(pred[512,1536]{1,0:T(8,128)(4,1)S(1)} %iota_compare_fusion.1) | copy-start | bytes 2359300
  222.4 140.0 %collective-permute-start.1 = (bf16[512,4096]{1,0:T(8,128)(2,1)}, bf16[512,4096]{1,0:T(8,128)(2,1)}, u32[]{:S(2)}, u32[]{:S(2)}) collective-permute-start(bf16[512,4096]{1,0:T(8,128)(2,1)} %all-gather.11.cloned.1.call-done), channel_id=1, source_target_pairs={{0,8},{8,0},{16,24},{24,16},{1,9},{9,1},{17,25},{25,17},{2,10},{10... | collective-permute-start | bytes 12582920 | tf_op jit(solution)/shard_map/ppermute | solution.py:175
  251.7 7.4 copy-start.50
  253.9 46.0 %copy-start.7 = (f32[2,2,512,512]{2,3,1,0:T(8,128)}, f32[2,2,512,512]{2,3,1,0:T(8,128)S(1)}, u32[]{:S(2)}) copy-start(f32[2,2,512,512]{2,3,1,0:T(8,128)S(1)} %get-tuple-element.109) | copy-start | bytes 12582916
  256.6 8.6 copy-start.5
  261.6 16.3 %copy-start.3 = (f32[2,2,512,1536]{3,2,1,0:T(8,128)}, f32[2,2,512,1536]{3,2,1,0:T(8,128)S(1)}, u32[]{:S(2)}) copy-start(f32[2,2,512,1536]{3,2,1,0:T(8,128)S(1)} %get-tuple-element.105) | copy-start | bytes 37748740
  292.9 250.0 %copy-start.62 = (f32[2,2,512]{2,1,0:T(2,128)}, f32[2,2,512]{2,1,0:T(2,128)S(1)}, u32[]{:S(2)}) copy-start(f32[2,2,512]{2,1,0:T(2,128)S(1)} %log_add_fusion) | copy-start | bytes 24580
  302.4 11.2 %copy-start.87 = (s32[2]{0:T(128)S(1)}, s32[2]{0:T(128)}, u32[]{:S(2)}) copy-start(s32[2]{0:T(128)} %param.16) | copy-start | bytes 28
  302.4 11.3 %copy-start.88 = (f32[8]{0:T(128)S(1)}, f32[8]{0:T(128)}, u32[]{:S(2)}) copy-start(f32[8]{0:T(128)} %param.17) | copy-start | bytes 100
  302.4 55.1 %copy-start.57 = (f32[1024]{0:T(1024)S(1)}, f32[1024]{0:T(1024)}, u32[]{:S(2)}) copy-start(f32[1024]{0:T(1024)} %param.21) | copy-start | bytes 12292
  309.1 48.4 %all-to-all-start.1 = ((bf16[8,512,128]{1,2,0:T(8,128)(2,1)}), bf16[8,512,128]{1,2,0:T(8,128)(2,1)}, u32[]{:S(2)}, u32[]{:S(2)}) async-start(bf16[8,512,128]{1,2,0:T(8,128)(2,1)} %copy.129), calls=%async_computation.1 | async-start | bytes 2097152 | tf_op jit(solution)/shard_map/all_to_all | solution.py:304
  313.6 47.6 %copy-start.73 = (f32[1,1024]{1,0:T(1,128)S(1)}, f32[1,1024]{1,0:T(1,128)}, u32[]{:S(2)}) copy-start(f32[1,1024]{1,0:T(1,128)} %get-tuple-element.97) | copy-start | bytes 12292
  313.9 63.7 %collective-permute-start.2 = (bf16[4096,512]{1,0:T(8,128)(2,1)}, bf16[4096,512]{1,0:T(8,128)(2,1)}, u32[]{:S(2)}, u32[]{:S(2)}) collective-permute-start(bf16[4096,512]{1,0:T(8,128)(2,1)} %all-gather.13.cloned.1.call-done), channel_id=1, source_target_pairs={{0,8},{8,0},{16,24},{24,16},{1,9},{9,1},{17,25},{25,17},{2,10},{10... | collective-permute-start | bytes 12582920 | tf_op jit(solution)/shard_map/ppermute | solution.py:175
  367.3 10.3 %copy-start.29 = (bf16[4096,512]{1,0:T(8,128)(2,1)S(1)}, bf16[4096,512]{1,0:T(8,128)(2,1)}, u32[]{:S(2)}) copy-start(bf16[4096,512]{1,0:T(8,128)(2,1)} %all-gather.13.cloned.1.call-done) | copy-start | bytes 12582916
  382.9 9.7 copy-start.21
  420.1 10.6 %copy-start.89 = (bf16[512,4096]{1,0:T(8,128)(2,1)S(1)}, bf16[512,4096]{1,0:T(8,128)(2,1)}, u32[]{:S(2)}) copy-start(bf16[512,4096]{1,0:T(8,128)(2,1)} %get-tuple-element.112) | copy-start | bytes 12582916
  430.7 8.2 copy-start.36
  447.1 30.5 %all-to-all-start.2 = ((bf16[512,8,128]{0,2,1:T(8,128)(2,1)}), bf16[512,8,128]{0,2,1:T(8,128)(2,1)}, u32[]{:S(2)}, u32[]{:S(2)}) async-start(bf16[512,8,128]{0,2,1:T(8,128)(2,1)} %bitcast.25), calls=%async_computation.2 | async-start | bytes 2097152 | tf_op jit(solution)/shard_map/all_to_all | solution.py:362
  451.4 358.8 %reduce-scatter.8.cloned.1.call-start = ((), (), s32[]{:S(2)}) async-start(), calls=%async_computation.13 | async-start | bytes 4718592 | tf_op jit(solution)/shard_map/reduce_scatter | solution.py:200
  454.4 12.6 %collective-permute-start.5 = (bf16[1024,512]{1,0:T(8,128)(2,1)S(1)}, bf16[1024,512]{1,0:T(8,128)(2,1)S(1)}, u32[]{:S(2)}, u32[]{:S(2)}) collective-permute-start(bf16[1024,512]{1,0:T(8,128)(2,1)S(1)} %dynamic-slice_convert_fusion.3), channel_id=1, source_target_pairs={{0,8},{8,0},{16,24},{24,16},{1,9},{9,1},{17,25},{25,17},{2,10},{10... | collective-permute-start | bytes 3145736 | tf_op jit(solution)/shard_map/ppermute | solution.py:175
  460.5 98.1 %collective-permute-start.6 = (bf16[512,4096]{1,0:T(8,128)(2,1)}, bf16[512,4096]{1,0:T(8,128)(2,1)}, u32[]{:S(2)}, u32[]{:S(2)}) collective-permute-start(bf16[512,4096]{1,0:T(8,128)(2,1)} %dynamic-slice_convert_fusion), channel_id=1, source_target_pairs={{0,8},{8,0},{16,24},{24,16},{1,9},{9,1},{17,25},{25,17},{2,10},{10... | collective-permute-start | bytes 12582920 | tf_op jit(solution)/shard_map/ppermute | solution.py:175
  466.9 142.7 %collective-permute-start.4 = (bf16[4096,512]{1,0:T(8,128)(2,1)}, bf16[4096,512]{1,0:T(8,128)(2,1)}, u32[]{:S(2)}, u32[]{:S(2)}) collective-permute-start(bf16[4096,512]{1,0:T(8,128)(2,1)} %dynamic-slice_convert_fusion.1), channel_id=1, source_target_pairs={{0,8},{8,0},{16,24},{24,16},{1,9},{9,1},{17,25},{25,17},{2,10},{10... | collective-permute-start | bytes 12582920 | tf_op jit(solution)/shard_map/ppermute | solution.py:175
  468.3 17.2 %copy-start.27 = (bf16[2,2048,2,64]{1,3,2,0:T(8,128)(2,1)S(1)}, bf16[2,2048,2,64]{1,3,2,0:T(8,128)(2,1)}, u32[]{:S(2)}) copy-start(bf16[2,2048,2,64]{1,3,2,0:T(8,128)(2,1)} %copy.115) | copy-start | bytes 3145732
  485.5 11.6 %copy-start.42 = (bf16[2,512,2,64]{1,0,3,2:T(2,128)(2,1)}, bf16[2,512,2,64]{1,0,3,2:T(2,128)(2,1)S(1)}, u32[]{:S(2)}) copy-start(bf16[2,512,2,64]{1,0,3,2:T(2,128)(2,1)S(1)} %get-tuple-element.73) | copy-start | bytes 786436
  485.5 11.6 %slice-start.4 = ((s8[12582912]{0:T(1024)(128)(4,1)}), s8[4194304]{0:T(1024)(128)(4,1)S(1)}, s32[]{:S(2)}) async-start(s8[12582912]{0:T(1024)(128)(4,1)} %bitcast.185), calls=%async_computation.19 | async-start | bytes 8388608
  485.5 11.6 %slice-start.5 = ((s8[12582912]{0:T(1024)(128)(4,1)}), s8[4194304]{0:T(1024)(128)(4,1)S(1)}, s32[]{:S(2)}) async-start(s8[12582912]{0:T(1024)(128)(4,1)} %bitcast.185), calls=%async_computation.20 | async-start | bytes 8388608
  489.5 7.6 slice-start.6
  504.3 10.1 %copy-start.25 = (bf16[2,2048,2,64]{1,3,2,0:T(8,128)(2,1)S(1)}, bf16[2,2048,2,64]{1,3,2,0:T(8,128)(2,1)}, u32[]{:S(2)}) copy-start(bf16[2,2048,2,64]{1,3,2,0:T(8,128)(2,1)} %copy.117) | copy-start | bytes 3145732
  504.3 12.9 %copy-start.8 = (f32[2,2,512,512]{2,3,1,0:T(8,128)S(1)}, f32[2,2,512,512]{2,3,1,0:T(8,128)}, u32[]{:S(2)}) copy-start(f32[2,2,512,512]{2,3,1,0:T(8,128)} %copy-done.7) | copy-start | bytes 12582916
  542.8 12.2 %copy-start.22 = (bf16[2,2048,2,64]{1,0,3,2:T(2,128)(2,1)S(1)}, bf16[2,2048,2,64]{1,0,3,2:T(2,128)(2,1)}, u32[]{:S(2)}) copy-start(bf16[2,2048,2,64]{1,0,3,2:T(2,128)(2,1)} %squeeze.20) | copy-start | bytes 3145732
  566.7 260.4 %reduce-scatter.6.cloned.1.call-start = ((), (), s32[]{:S(2)}) async-start(), calls=%async_computation.12 | async-start | bytes 5898240 | tf_op jit(solution)/shard_map/reduce_scatter | solution.py:218
  588.3 13.8 %slice-start = ((s8[16777216]{0:T(1024)(128)(4,1)}), s8[4194304]{0:T(1024)(128)(4,1)S(1)}, s32[]{:S(2)}) async-start(s8[16777216]{0:T(1024)(128)(4,1)} %bitcast.183), calls=%async_computation.15 | async-start | bytes 8388608
  588.3 13.8 %slice-start.1 = ((s8[16777216]{0:T(1024)(128)(4,1)}), s8[4194304]{0:T(1024)(128)(4,1)S(1)}, s32[]{:S(2)}) async-start(s8[16777216]{0:T(1024)(128)(4,1)} %bitcast.183), calls=%async_computation.16 | async-start | bytes 8388608
  594.4 7.8 slice-start.2
  594.4 7.8 slice-start.3
  618.9 286.5 %reduce-scatter.4.cloned.1.call-start = ((), (), s32[]{:S(2)}) async-start(), calls=%async_computation.11 | async-start | bytes 3538944 | tf_op jit(solution)/shard_map/reduce_scatter | solution.py:200
  791.4 5.7 collective-permute-start.3
  799.9 177.6 %all-reduce.10.cloned.1.call-start = ((), (), s32[]{:S(2)}) async-start(), calls=%async_computation.14 | async-start | bytes 6291456 | tf_op jit(solution)/shard_map/psum | solution.py:410
  907.7 9.1 copy-start.68
  907.7 9.1 copy-start.72
  907.7 9.1 copy-start.85
  907.7 9.1 copy-start.67
  907.7 9.1 copy-start.71
  907.7 9.1 copy-start.84
  907.7 9.1 copy-start.66
  907.7 9.1 copy-start.74
  907.8 9.1 copy-start.77
  907.8 51.6 %copy-start.14 = (f32[512,1024]{1,0:T(8,128)S(1)}, f32[512,1024]{1,0:T(8,128)}, u32[]{:S(2)}) copy-start(f32[512,1024]{1,0:T(8,128)} %copy-done.13) | copy-start | bytes 6291460
  977.4 7.2 copy-start.46
  (57 other events, 200.3 us)
Sparse Core Ops, SparseCore 0:
  10.8 62.7 all-gather.6
  76.2 146.1 all-gather.10
  225.1 70.0 all-gather.12
  297.2 60.2 all-gather.8
  566.8 107.3 reduce-scatter.7
  677.7 149.3 reduce-scatter.5
  830.7 74.5 reduce-scatter.3
  908.5 68.9 all-reduce.9

commit v12 on v5

--- a/solution.py
+++ b/solution.py
@@ -269,8 +269,9 @@
     bias_flat = jnp.concatenate([qkv_bias.reshape(-1), up_bias])
     bias_full = lax.all_gather(bias_flat, "narrow", axis=0)
     qkv_gathered = gather_mine(qkv_weight, core, 1, 2)
-    qkv_gathered, up_weight, down_weight, bias_full = lax.optimization_barrier(
-        (qkv_gathered, up_weight, down_weight, bias_full)
+    out_gathered = gather_mine(out_weight, core, 1, 0)
+    qkv_gathered, out_gathered, up_weight, down_weight, bias_full = lax.optimization_barrier(
+        (qkv_gathered, out_gathered, up_weight, down_weight, bias_full)
     )
     qkv_full = join_halves(qkv_gathered, core, 1)
     qkv_bias_full = jnp.swapaxes(bias_full[:, : 3 * inner].reshape(-1, 3, inner), 0, 1).reshape(
@@ -298,7 +299,7 @@
     attn_heads, totals = attend_forward(query, key_rows, values, block_rows)
     attn_low = attn_heads.reshape(group_rows, inner).astype(jnp.bfloat16)
     attn_rows = lax.all_to_all(attn_low, "narrow", 0, 1, tiled=True)
-    out_full = lax.all_gather(out_weight, "narrow", axis=0, tiled=True)
+    out_full = join_halves(out_gathered, core, 1)
     pre_attn = jnp.dot(attn_rows, out_full, preferred_element_type=jnp.float32) + out_bias
     normed_second, inverse_second = norm_stats(pre_attn)
     residual = layer_in + normed_second * norm_gains[1] + norm_biases[1]

time: 949 us -> 987 us (1.040)
  other arithmetic: 116 us -> 128 us
    all_gather x1 -> x0, waiting for transfers between devices: 55.1 us -> none  [shards(): out_full = lax.all_gather(out_weight, 'narrow', axis=0, tiled=True)]
    all_gather x3 -> x4, waiting for transfers between devices: 139 us -> 183 us  [gather_mine(): return lax.all_gather(mine, 'narrow', axis=gather_axis, tiled=True)]
    all_to_all x1, waiting for transfers between devices: 0.01 us -> 20 us  [shards(): attn_rows = lax.all_to_all(attn_low, 'narrow', 0, 1, tiled=True)]
    unnamed x223 -> x229, local copies, waits for them, and re-layouts: 26.4 us -> 28 us
  transfers between devices with their start and end apart: 18 -> 19, of which waited for: 8 -> 10; matrix products, arithmetic and copies ran while one was open for 36% -> 37% of each run, Pallas kernels for 0% -> 0%
where the time goes in v12:
time: 987 us; the launch traced here: 976 us
  waiting for transfers between devices  294 us (30%)
  blocking collectives  198 us (20%)
  matrix products  186 us (19%)
  local copies, waits for them, and re-layouts  138 us (14%)
  other arithmetic  128 us (13%)
  between operations  16.1 us (2%)
  starting transfers between devices  14.8 us (1%)
    all_gather x4, waiting for transfers between devices, gather_mine(): return lax.all_gather(mine, 'narrow', axis=gather_axis, tiled=True)  183 us
    all_to_all x1, blocking collectives, shards(): lax.all_to_all(qkv_grad.reshape(3, group_rows, heads_here, HEAD), 'narrow...  117 us
    reduce_scatter x2, waiting for transfers between devices, reduce_halves(): lax.psum_scatter(chip_sum.astype(jnp.bfloat16), 'narrow', scatter_dimensi...  59.3 us
    psum x1, blocking collectives, shards(): lax.psum((gain_local, bias_local, out_blocal, down_blocal, up_bgrad_rows)...  42 us
    all_gather x1, blocking collectives, shards(): bias_full = lax.all_gather(bias_flat, 'narrow', axis=0)  32.4 us
    dot_general x4, matrix products, attend_backward(): jnp.einsum('bqhd,bkhd->bhqk', grad_block, value_block, preferred_element_...  28.5 us
    unnamed x229, local copies, waits for them, and re-layouts  28 us
    dot_general x4, matrix products, attend_forward(): jnp.einsum('bhqk,bkhd->bqhd', probs_low, values[:, :key_stop], preferred_...  24.4 us
  transfers between devices with their start and end apart: 19, of which 10 were waited for; matrix products, arithmetic and copies ran while one was open for 37% of the time, Pallas kernels for 0%

profile of v12, /device:TPU:0, one launch (start us, length us, event | category | flops | bytes accessed | tf_op | source)
XLA Modules:
  0.0 975.8 jit_solution(4036950746420920267)
XLA Ops:
  11.8 32.4 %all-gather.1 = f32[8,1,896]{2,1,0:T(1,128)S(1)} all-gather(f32[1,1,896]{2,1,0:T(1,128)S(1)} %reshape.456), channel_id=2, replica_groups=mesh['wide'=4,'narrow'=8] {'narrow'}, dimensions={0}, use_global_device_ids=true | all-gather | bytes 32256 | tf_op jit(solution)/shard_map/all_gather | solution.py:270
  44.3 9.5 all-gather.9.cloned.1.call-done
  53.8 61.5 %all-gather.7.cloned.1.call-done = bf16[3,512,1024]{1,2,0:T(8,128)(2,1)} async-done(((bf16[3,512,128]{1,2,0:T(8,128)(2,1)}), bf16[3,512,1024]{1,2,0:T(8,128)(2,1)}) %all-gather.7.cloned.1.call-update) | async-done | bytes 3145744 | tf_op jit(solution)/shard_map/all_gather | solution.py:181
  121.3 3.3 broadcast_select_fusion.5
  124.6 3.6 add_bitcast_fusion
  131.8 4.5 all-to-all-start
  140.6 112.2 %all-gather.11.cloned.1.call-done = bf16[512,4096]{1,0:T(8,128)(2,1)} async-done(((bf16[512,512]{1,0:T(8,128)(2,1)}), bf16[512,4096]{1,0:T(8,128)(2,1)}) %all-gather.11.cloned.1.call-update) | async-done | bytes 4194320 | tf_op jit(solution)/shard_map/all_gather | solution.py:181
  263.4 2.8 copy.167
  268.4 2.8 fusion.129
  271.2 2.8 copy.165
  289.6 3.5 exponential_reduce_fusion.1
  294.2 4.9 fusion
  299.2 13.2 %exponential_reduce_fusion = f32[2,2,512]{2,1,0:T(2,128)S(1)} fusion(f32[2,2,512,2048]{3,2,1,0:T(8,128)S(1)} %get-tuple-element.107, f32[2,2,512]{2,1,0:T(2,128)S(1)} %get-tuple-element.106, pred[512,2048]{1,0:T(8,128)(4,1)S(1)} %iota_compare_fusion), kind=kLoop, calls=%fused_computation.3 | loop fusion | flops 16775168 | bytes 17842176 | tf_op jit(solution)/shard_map/reduce_sum | solution.py:114
  312.5 6.3 fusion.53
  318.8 8.8 fusion.55
  327.6 7.1 fusion.56
  344.0 4.2 all-to-all-start.1
  351.4 3.1 broadcast_select_fusion.7
  354.9 20.0 %all-to-all-done.1 = bf16[8,512,128]{1,2,0:T(8,128)(2,1)} async-done(((bf16[8,512,128]{1,2,0:T(8,128)(2,1)}), bf16[8,512,128]{1,2,0:T(8,128)(2,1)}, u32[]{:S(2)}, u32[]{:S(2)}) %all-to-all-start.1) | async-done | bytes 1048608 | tf_op jit(solution)/shard_map/all_to_all | solution.py:301
  374.9 3.2 add_reduce_fusion.1
  380.8 3.8 broadcast_select_fusion.3
  384.6 10.3 %multiply_convert_fusion.3 = (bf16[512,4096]{1,0:T(8,128)(2,1)}, f32[512,4096]{1,0:T(8,128)}) fusion(f32[4096]{0:T(1024)S(1)} %bitcast.233, bf16[512,4096]{1,0:T(8,128)(2,1)} %get-tuple-element.57, bf16[512,4096]{1,0:T(8,128)(2,1)S(1)} %get-tuple-element.56, f32[512,1024]{1,0:T(8,128)S(1)} %get-tuple-element.53, f32[1024]{0:T(1024)S(1)} %bitcast.243, ...), kind=kOutput, calls=%fused_computation.29 | convolution fusion | flops 4326948864 | bytes 23097344 | tf_op jit(solution)/shard_map/dot_general | solution.py:310
  394.9 5.2 broadcast_select_fusion.1
  400.1 9.3 add_reduce_fusion
  411.5 2.6 convert_reduce_fusion.2
  414.2 12.8 %convert_reduce_fusion = (f32[4096]{0:T(1024)}, bf16[512,4096]{1,0:T(8,128)(2,1)}) fusion(f32[512,4096]{1,0:T(8,128)} %get-tuple-element.117, f32[4096]{0:T(1024)S(1)} %bitcast.234, bf16[512,1024]{1,0:T(8,128)(2,1)S(1)} %get-tuple-element.48, bf16[4096,512]{1,0:T(8,128)(2,1)} %get-tuple-element.55, bf16[4096,512]{1,0:T(8,128)(2,1)} %get-tuple-element.54), kind=kOutput, calls=%fused_computation.22 | convolution fusion | flops 4339003392 | bytes 22052864 | tf_op jit(solution)/shard_map/dot_general | solution.py:340
  427.0 10.3 %multiply_reduce_fusion.5 = (f32[1024]{0:T(1024)}, f32[512]{0:T(512)S(1)}, f32[512]{0:T(512)S(1)}, f32[1024]{0:T(1024)}, f32[512,1024]{1,0:T(8,128)}) fusion(f32[512,1024]{1,0:T(8,128)S(1)} %get-tuple-element.53, f32[512]{0:T(512)S(1)} %add_rsqrt_fusion.1, f32[512]{0:T(512)S(1)} %broadcast_multiply_fusion.9, f32[1024]{0:T(1024)S(1)} %bitcast.225, ...), kind=kOutput, calls=%fused_computation.103 | convolution fusion | flops 4316460032 | bytes 16797696 | tf_op jit(solution)/shard_map/dot_general | solution.py:348
  437.3 10.7 %fusion.123 = f32[1024,4096]{1,0:T(8,128)} fusion(bf16[512,4096]{1,0:T(8,128)(2,1)} %get-tuple-element.131, f32[512,1024]{1,0:T(8,128)S(1)} %get-tuple-element.53, f32[1024]{0:T(1024)S(1)} %bitcast.244, f32[1024]{0:T(1024)S(1)} %bitcast.226, f32[512]{0:T(512)S(1)} %add_rsqrt_fusion.1, f32[512]{0:T(512)S(1)} %broadcast_multiply_fusion.9), kind=kOutput, calls=%fused_computation.286 | convolution fusion | flops 4297588736 | bytes 23080960 | tf_op jit(solution)/shard_map/dot_general | solution.py:345
  448.0 8.2 fusion.132
  456.2 3.2 multiply_reduce_fusion.6
  466.3 4.2 all-to-all-start.2
  473.4 6.1 dynamic-slice_convert_fusion
  480.0 5.9 dynamic-slice_convert_fusion.1
  487.2 9.1 all-to-all-done.2
  496.3 2.8 copy.184
  503.6 6.2 multiply_reduce_fusion.2
  520.5 7.1 multiply_reduce_fusion.1
  528.9 7.2 multiply_convert_fusion.1
  537.3 2.8 fusion.48
  540.1 13.8 %multiply_reduce_fusion = (f32[2,2,512]{2,1,0:T(2,128)S(1)}, f32[2,2,512,2048]{3,2,1,0:T(8,128)}) fusion(f32[2,2,512,2048]{3,2,1,0:T(8,128)} %copy-done.2, f32[2,2,512]{2,1,0:T(2,128)S(1)} %log_add_fusion, pred[512,2048]{1,0:T(8,128)(4,1)S(1)} %iota_compare_fusion, bf16[2,2048,2,64]{1,0,3,2:T(2,128)(2,1)S(1)} %copy-done.19, ...), kind=kOutput, calls=%fused_computation.1 | convolution fusion | flops 557840384 | bytes 35930112 | tf_op jit(solution)/shard_map/bqhd,bkhd->bhqk/dot_general | solution.py:141
  553.9 8.2 add_convert_fusion
  562.1 12.7 %multiply_convert_fusion = bf16[2,2,512,2048]{3,2,1,0:T(8,128)(2,1)S(1)} fusion(f32[2,2,512,2048]{3,2,1,0:T(8,128)} %get-tuple-element.122, f32[2,2,512,2048]{3,2,1,0:T(8,128)} %copy-done.2, f32[2,2,512]{2,1,0:T(2,128)S(1)} %get-tuple-element.121, f32[2,2,512]{2,1,0:T(2,128)S(1)} %log_add_fusion, pred[512,2048]{1,0:T(8,128)(4,1)S(1)} %iota_compare_fusion), kind=kLoop, calls=%fused_computation | loop fusion | flops 25165824 | bytes 43008000 | tf_op jit(solution)/shard_map/convert_element_type | solution.py:145
  574.9 2.7 fusion.49
  586.7 3.3 convolution_bitcast_fusion.2
  590.1 6.1 convolution_bitcast_fusion.1
  596.2 7.7 fusion.24
  603.9 6.3 add_convert_fusion.1
  610.3 2.9 pad_maximum_fusion.7
  624.7 3.8 pad_maximum_fusion.11
  628.6 14.5 %copy.197 = bf16[3,4096,2,64]{3,2,0,1:T(2,128)(2,1)} copy(bf16[3,4096,2,64]{1,3,2,0:T(8,128)(2,1)} %pad_maximum_fusion.11) | data formatting | bytes 6291456 | tf_op jit(solution)/shard_map/stack | solution.py:368
  643.1 9.0 reshape.461
  652.1 117.0 %all_to_all.62 = bf16[8,2,98304]{2,1,0:T(2,128)(2,1)} all-to-all(bf16[8,2,98304]{2,1,0:T(2,128)(2,1)} %reshape.461), channel_id=1, replica_groups=mesh['wide'=4,'narrow'=8] {'narrow'}, dimensions={0} | all-to-all | bytes 6291456 | tf_op jit(solution)/shard_map/all_to_all | solution.py:377
  769.1 8.8 reshape.462
  777.9 15.5 %copy.216 = bf16[3,8,512,2,64]{2,4,3,1,0:T(8,128)(2,1)} copy(bf16[3,8,512,2,64]{4,3,0,2,1:T(2,128)(2,1)} %bitcast.202) | data formatting | bytes 6291456 | tf_op jit(solution)/shard_map/all_to_all | solution.py:377
  793.4 5.5 fusion.70
  799.5 5.6 collective-permute-done.4
  805.2 2.7 fusion.11
  814.7 6.9 psum.71
  828.5 59.3 %reduce-scatter.4.cloned.1.call-done = bf16[3,512,128]{1,2,0:T(8,128)(2,1)} async-done(((bf16[3,512,1024]{1,2,0:T(8,128)(2,1)}), bf16[3,512,128]{1,2,0:T(8,128)(2,1)}) %reduce-scatter.4.cloned.1.call-update) | async-done | bytes 393232 | tf_op jit(solution)/shard_map/reduce_scatter | solution.py:200
  890.2 9.0 fusion.39
  899.4 42.0 %all-reduce.6 = (f32[1024]{0:T(1024)}, f32[4096]{0:T(1024)S(1)}, f32[1024]{0:T(1024)}, f32[4,1024]{1,0:T(4,128)}, f32[4,1024]{1,0:T(4,128)}) all-reduce(f32[1024]{0:T(1024)S(1)} %copy-done.83, f32[4096]{0:T(1024)S(1)} %copy-done.80, f32[1024]{0:T(1024)S(1)} %copy-done.72, ...), channel_id=1, replica_groups=mesh['wide'=4,'narrow'=8] {'wide','narrow'}, use_global_device_ids=true, to_apply=%region_37.38 | all-reduce | flops 14336 | bytes 114688 | tf_op jit(solution)/shard_map/psum | solution.py:416
  942.0 3.3 fusion.38
  945.3 14.4 %all-reduce.10.cloned.1.call-done = (bf16[3,1024,128]{2,1,0:T(8,128)(2,1)}, bf16[128,1024]{1,0:T(8,128)(2,1)}, bf16[1024,512]{1,0:T(8,128)(2,1)}, bf16[512,1024]{1,0:T(8,128)(2,1)}) async-done(((bf16[3,1024,128]{2,1,0:T(8,128)(2,1)}, bf16[128,1024]{1,0:T(8,128)(2,1)}, bf16[1024,512]{1,0:T(8,128)(2,1)}, bf16[512,1024]{1,0:T(8,128)(2,1)}), (bf16[3,1024,128]{2,1,0:T(8,128)(2,1)}, bf16[128,1024]{1,0:T(8,128)(2,1)}, ...) | async-done | bytes 3145744 | tf_op jit(solution)/shard_map/psum | solution.py:409
  964.1 2.8 reshape.452
  (389 shorter events, 138.2 us)
Async XLA Ops:
  7.2 113.1 %copy-start = (bf16[1024,512]{1,0:T(8,128)(2,1)S(1)}, bf16[1024,512]{1,0:T(8,128)(2,1)}, u32[]{:S(2)}) copy-start(bf16[1024,512]{1,0:T(8,128)(2,1)} %param.22) | copy-start | bytes 3145732
  7.2 111.4 %copy-start.11 = (bf16[512,1024]{1,0:T(8,128)(2,1)S(1)}, bf16[512,1024]{1,0:T(8,128)(2,1)}, u32[]{:S(2)}) copy-start(bf16[512,1024]{1,0:T(8,128)(2,1)} %param.14) | copy-start | bytes 3145732
  7.2 111.8 %copy-start.81 = (f32[4,1024]{1,0:T(4,128)S(1)}, f32[4,1024]{1,0:T(4,128)}, u32[]{:S(2)}) copy-start(f32[4,1024]{1,0:T(4,128)} %param.26) | copy-start | bytes 49156
  7.2 112.4 %copy-start.82 = (f32[4,1024]{1,0:T(4,128)S(1)}, f32[4,1024]{1,0:T(4,128)}, u32[]{:S(2)}) copy-start(f32[4,1024]{1,0:T(4,128)} %param.27) | copy-start | bytes 49156
  7.2 46.6 %all-gather.9.cloned.1.call-start = ((), (), s32[]{:S(2)}) async-start(), calls=%async_computation.8 | async-start | bytes 1179648 | tf_op jit(solution)/shard_map/all_gather | solution.py:181
  9.0 106.3 %all-gather.7.cloned.1.call-start = ((), (), s32[]{:S(2)}) async-start(), calls=%async_computation.7 | async-start | bytes 3538944 | tf_op jit(solution)/shard_map/all_gather | solution.py:181
  11.1 241.8 %all-gather.11.cloned.1.call-start = ((), (), s32[]{:S(2)}) async-start(), calls=%async_computation.9 | async-start | bytes 4718592 | tf_op jit(solution)/shard_map/all_gather | solution.py:181
  115.3 6.0 collective-permute-start
  131.8 121.1 %all-to-all-start = ((bf16[3,512,16,64]{1,3,0,2:T(8,128)(2,1)}), bf16[3,512,16,64]{1,3,0,2:T(8,128)(2,1)}, u32[]{:S(2)}, u32[]{:S(2)}) async-start(bf16[3,512,16,64]{1,3,0,2:T(8,128)(2,1)} %pad_maximum_fusion.10), calls=%async_computation | async-start | bytes 6291456 | tf_op jit(solution)/shard_map/all_to_all | solution.py:296
  136.2 218.3 %all-gather.13.cloned.1.call-start = ((), (), s32[]{:S(2)}) async-start(), calls=%async_computation.10 | async-start | bytes 4718592 | tf_op jit(solution)/shard_map/all_gather | solution.py:181
  138.1 390.8 %copy-start.8 = (pred[512,1536]{1,0:T(8,128)(4,1)}, pred[512,1536]{1,0:T(8,128)(4,1)S(1)}, u32[]{:S(2)}) copy-start(pred[512,1536]{1,0:T(8,128)(4,1)S(1)} %iota_compare_fusion.1) | copy-start | bytes 2359300
  252.9 126.9 %collective-permute-start.2 = (bf16[512,4096]{1,0:T(8,128)(2,1)}, bf16[512,4096]{1,0:T(8,128)(2,1)}, u32[]{:S(2)}, u32[]{:S(2)}) collective-permute-start(bf16[512,4096]{1,0:T(8,128)(2,1)} %all-gather.11.cloned.1.call-done), channel_id=1, source_target_pairs={{0,8},{8,0},{16,24},{24,16},{1,9},{9,1},{17,25},{25,17},{2,10},{10... | collective-permute-start | bytes 12582920 | tf_op jit(solution)/shard_map/ppermute | solution.py:175
  280.9 53.7 %copy-start.5 = (f32[2,2,512,512]{2,3,1,0:T(8,128)}, f32[2,2,512,512]{2,3,1,0:T(8,128)S(1)}, u32[]{:S(2)}) copy-start(f32[2,2,512,512]{2,3,1,0:T(8,128)S(1)} %get-tuple-element.113) | copy-start | bytes 12582916
  294.2 234.7 %copy-start.64 = (f32[2,2,512]{2,1,0:T(2,128)}, f32[2,2,512]{2,1,0:T(2,128)S(1)}, u32[]{:S(2)}) copy-start(f32[2,2,512]{2,1,0:T(2,128)S(1)} %log_add_fusion.1) | copy-start | bytes 24580
  299.2 28.4 %copy-start.2 = (f32[2,2,512,2048]{3,2,1,0:T(8,128)}, f32[2,2,512,2048]{3,2,1,0:T(8,128)S(1)}, u32[]{:S(2)}) copy-start(f32[2,2,512,2048]{3,2,1,0:T(8,128)S(1)} %get-tuple-element.107) | copy-start | bytes 50331652
  299.2 13.3 %copy-start.14 = (pred[512,1024]{1,0:T(8,128)(4,1)S(1)}, pred[512,1024]{1,0:T(8,128)(4,1)}, u32[]{:S(2)}) copy-start(pred[512,1024]{1,0:T(8,128)(4,1)} %iota_compare_fusion.2) | copy-start | bytes 1572868
  299.2 13.3 %copy-start.23 = (bf16[2,2048,2,64]{1,3,2,0:T(8,128)(2,1)S(1)}, bf16[2,2048,2,64]{1,3,2,0:T(8,128)(2,1)}, u32[]{:S(2)}) copy-start(bf16[2,2048,2,64]{1,3,2,0:T(8,128)(2,1)} %copy.166) | copy-start | bytes 3145732
  312.4 249.7 %copy-start.65 = (f32[2,2,512]{2,1,0:T(2,128)}, f32[2,2,512]{2,1,0:T(2,128)S(1)}, u32[]{:S(2)}) copy-start(f32[2,2,512]{2,1,0:T(2,128)S(1)} %log_add_fusion) | copy-start | bytes 24580
  337.1 11.7 %copy-start.93 = (s32[2]{0:T(128)S(1)}, s32[2]{0:T(128)}, u32[]{:S(2)}) copy-start(s32[2]{0:T(128)} %param.16) | copy-start | bytes 28
  337.1 11.8 %copy-start.94 = (f32[8]{0:T(128)S(1)}, f32[8]{0:T(128)}, u32[]{:S(2)}) copy-start(f32[8]{0:T(128)} %param.17) | copy-start | bytes 100
  341.5 33.4 %copy-start.67 = (f32[1024]{0:T(1024)S(1)}, f32[1024]{0:T(1024)}, u32[]{:S(2)}) copy-start(f32[1024]{0:T(1024)} %param.21) | copy-start | bytes 12292
  344.0 30.9 %all-to-all-start.1 = ((bf16[8,512,128]{1,2,0:T(8,128)(2,1)}), bf16[8,512,128]{1,2,0:T(8,128)(2,1)}, u32[]{:S(2)}, u32[]{:S(2)}) async-start(bf16[8,512,128]{1,2,0:T(8,128)(2,1)} %copy.182), calls=%async_computation.1 | async-start | bytes 2097152 | tf_op jit(solution)/shard_map/all_to_all | solution.py:301
  348.3 3.2 collective-permute-start.1
  354.6 40.3 %collective-permute-start.3 = (bf16[4096,512]{1,0:T(8,128)(2,1)}, bf16[4096,512]{1,0:T(8,128)(2,1)}, u32[]{:S(2)}, u32[]{:S(2)}) collective-permute-start(bf16[4096,512]{1,0:T(8,128)(2,1)} %all-gather.13.cloned.1.call-done), channel_id=1, source_target_pairs={{0,8},{8,0},{16,24},{24,16},{1,9},{9,1},{17,25},{25,17},{2,10},{10... | collective-permute-start | bytes 12582920 | tf_op jit(solution)/shard_map/ppermute | solution.py:175
  384.6 10.3 %copy-start.26 = (bf16[4096,512]{1,0:T(8,128)(2,1)S(1)}, bf16[4096,512]{1,0:T(8,128)(2,1)}, u32[]{:S(2)}) copy-start(bf16[4096,512]{1,0:T(8,128)(2,1)} %all-gather.13.cloned.1.call-done) | copy-start | bytes 12582916
  400.0 9.7 copy-start.17
  400.0 9.7 copy-start.69
  437.3 10.7 %copy-start.95 = (bf16[512,4096]{1,0:T(8,128)(2,1)S(1)}, bf16[512,4096]{1,0:T(8,128)(2,1)}, u32[]{:S(2)}) copy-start(bf16[512,4096]{1,0:T(8,128)(2,1)} %get-tuple-element.116) | copy-start | bytes 12582916
  448.0 8.2 copy-start.33
  466.3 30.0 %all-to-all-start.2 = ((bf16[512,8,128]{0,2,1:T(8,128)(2,1)}), bf16[512,8,128]{0,2,1:T(8,128)(2,1)}, u32[]{:S(2)}, u32[]{:S(2)}) async-start(bf16[512,8,128]{0,2,1:T(8,128)(2,1)} %bitcast.29), calls=%async_computation.2 | async-start | bytes 2097152 | tf_op jit(solution)/shard_map/all_to_all | solution.py:359
  470.6 351.7 %reduce-scatter.8.cloned.1.call-start = ((), (), s32[]{:S(2)}) async-start(), calls=%async_computation.13 | async-start | bytes 4718592 | tf_op jit(solution)/shard_map/reduce_scatter | solution.py:200
  473.3 12.6 %collective-permute-start.6 = (bf16[1024,512]{1,0:T(8,128)(2,1)S(1)}, bf16[1024,512]{1,0:T(8,128)(2,1)S(1)}, u32[]{:S(2)}, u32[]{:S(2)}) collective-permute-start(bf16[1024,512]{1,0:T(8,128)(2,1)S(1)} %dynamic-slice_convert_fusion.3), channel_id=1, source_target_pairs={{0,8},{8,0},{16,24},{24,16},{1,9},{9,1},{17,25},{25,17},{2,10},{10... | collective-permute-start | bytes 3145736 | tf_op jit(solution)/shard_map/ppermute | solution.py:175
  479.5 74.4 %collective-permute-start.7 = (bf16[512,4096]{1,0:T(8,128)(2,1)}, bf16[512,4096]{1,0:T(8,128)(2,1)}, u32[]{:S(2)}, u32[]{:S(2)}) collective-permute-start(bf16[512,4096]{1,0:T(8,128)(2,1)} %dynamic-slice_convert_fusion), channel_id=1, source_target_pairs={{0,8},{8,0},{16,24},{24,16},{1,9},{9,1},{17,25},{25,17},{2,10},{10... | collective-permute-start | bytes 12582920 | tf_op jit(solution)/shard_map/ppermute | solution.py:175
  485.9 118.1 %collective-permute-start.5 = (bf16[4096,512]{1,0:T(8,128)(2,1)}, bf16[4096,512]{1,0:T(8,128)(2,1)}, u32[]{:S(2)}, u32[]{:S(2)}) collective-permute-start(bf16[4096,512]{1,0:T(8,128)(2,1)} %dynamic-slice_convert_fusion.1), channel_id=1, source_target_pairs={{0,8},{8,0},{16,24},{24,16},{1,9},{9,1},{17,25},{25,17},{2,10},{10... | collective-permute-start | bytes 12582920 | tf_op jit(solution)/shard_map/ppermute | solution.py:175
  487.2 16.3 %copy-start.15 = (pred[512,1024]{1,0:T(8,128)(4,1)S(1)}, pred[512,1024]{1,0:T(8,128)(4,1)}, u32[]{:S(2)}) copy-start(pred[512,1024]{1,0:T(8,128)(4,1)} %iota_compare_fusion.2) | copy-start | bytes 1572868
  503.5 12.1 %copy-start.56 = (bf16[2,512,2,64]{1,0,3,2:T(2,128)(2,1)}, bf16[2,512,2,64]{1,0,3,2:T(2,128)(2,1)S(1)}, u32[]{:S(2)}) copy-start(bf16[2,512,2,64]{1,0,3,2:T(2,128)(2,1)S(1)} %get-tuple-element.79) | copy-start | bytes 786436
  503.5 16.9 %copy-start.44 = (bf16[2,512,2,64]{1,0,3,2:T(2,128)(2,1)}, bf16[2,512,2,64]{1,0,3,2:T(2,128)(2,1)S(1)}, u32[]{:S(2)}) copy-start(bf16[2,512,2,64]{1,0,3,2:T(2,128)(2,1)S(1)} %get-tuple-element.77) | copy-start | bytes 786436
  503.5 36.5 %copy-start.43 = (bf16[2,512,2,64]{1,0,3,2:T(2,128)(2,1)}, bf16[2,512,2,64]{1,0,3,2:T(2,128)(2,1)S(1)}, u32[]{:S(2)}) copy-start(bf16[2,512,2,64]{1,0,3,2:T(2,128)(2,1)S(1)} %get-tuple-element.76) | copy-start | bytes 786436
  528.9 7.2 copy-start.55
  562.1 262.4 %reduce-scatter.6.cloned.1.call-start = ((), (), s32[]{:S(2)}) async-start(), calls=%async_computation.12 | async-start | bytes 5898240 | tf_op jit(solution)/shard_map/reduce_scatter | solution.py:218
  562.1 12.7 %copy-start.18 = (bf16[2,2048,2,64]{1,0,3,2:T(2,128)(2,1)S(1)}, bf16[2,2048,2,64]{1,0,3,2:T(2,128)(2,1)}, u32[]{:S(2)}) copy-start(bf16[2,2048,2,64]{1,0,3,2:T(2,128)(2,1)} %squeeze.20) | copy-start | bytes 3145732
  577.6 12.4 %slice-start.7 = ((s8[12582912]{0:T(1024)(128)(4,1)}), s8[4194304]{0:T(1024)(128)(4,1)S(1)}, s32[]{:S(2)}) async-start(s8[12582912]{0:T(1024)(128)(4,1)} %bitcast.195), calls=%async_computation.22 | async-start | bytes 8388608
  579.3 10.7 %slice-start.8 = ((s8[12582912]{0:T(1024)(128)(4,1)}), s8[4194304]{0:T(1024)(128)(4,1)S(1)}, s32[]{:S(2)}) async-start(s8[12582912]{0:T(1024)(128)(4,1)} %bitcast.195), calls=%async_computation.23 | async-start | bytes 8388608
  582.6 7.5 slice-start.9
  586.7 9.5 slice-start
  586.7 9.5 slice-start.1
  613.2 274.6 %reduce-scatter.4.cloned.1.call-start = ((), (), s32[]{:S(2)}) async-start(), calls=%async_computation.11 | async-start | bytes 3538944 | tf_op jit(solution)/shard_map/reduce_scatter | solution.py:200
  777.9 15.5 %copy-start.12 = (bf16[512,1024]{1,0:T(8,128)(2,1)S(1)}, bf16[512,1024]{1,0:T(8,128)(2,1)}, u32[]{:S(2)}) copy-start(bf16[512,1024]{1,0:T(8,128)(2,1)} %param.14) | copy-start | bytes 3145732
  777.9 15.5 %copy-start.71 = (f32[512]{0:T(512)S(1)}, f32[512]{0:T(512)}, u32[]{:S(2)}) copy-start(f32[512]{0:T(512)} %copy-done.70) | copy-start | bytes 6148
  777.9 15.5 %copy-start.85 = (f32[1,1024]{1,0:T(1,128)S(1)}, f32[1,1024]{1,0:T(1,128)}, u32[]{:S(2)}) copy-start(f32[1,1024]{1,0:T(1,128)} %copy-done.84) | copy-start | bytes 12292
  777.9 15.5 %copy-start.87 = (f32[512]{0:T(512)S(1)}, f32[512]{0:T(512)}, u32[]{:S(2)}) copy-start(f32[512]{0:T(512)} %copy-done.86) | copy-start | bytes 6148
  777.9 15.5 %copy-start.89 = (f32[1,1024]{1,0:T(1,128)S(1)}, f32[1,1024]{1,0:T(1,128)}, u32[]{:S(2)}) copy-start(f32[1,1024]{1,0:T(1,128)} %copy-done.88) | copy-start | bytes 12292
  799.4 5.7 collective-permute-start.4
  807.9 151.8 %all-reduce.10.cloned.1.call-start = ((), (), s32[]{:S(2)}) async-start(), calls=%async_computation.14 | async-start | bytes 6291456 | tf_op jit(solution)/shard_map/psum | solution.py:409
  890.1 9.1 copy-start.74
  890.1 9.1 copy-start.78
  890.1 9.1 copy-start.91
  890.1 9.2 copy-start.73
  890.2 9.2 copy-start.77
  890.2 9.2 copy-start.90
  890.2 9.2 copy-start.72
  890.2 9.2 copy-start.80
  890.2 9.2 copy-start.83
  890.2 51.8 %copy-start.10 = (f32[512,1024]{1,0:T(8,128)S(1)}, f32[512,1024]{1,0:T(8,128)}, u32[]{:S(2)}) copy-start(f32[512,1024]{1,0:T(8,128)} %copy-done.9) | copy-start | bytes 6291460
  (65 other events, 241.3 us)
Sparse Core Ops, SparseCore 0:
  10.7 43.0 all-gather.8
  56.5 58.7 all-gather.6
  121.3 131.5 all-gather.10
  254.9 70.0 all-gather.12
  562.2 87.7 reduce-scatter.7
  653.4 156.2 reduce-scatter.5
  813.3 74.4 reduce-scatter.3
  890.9 68.7 all-reduce.9

commit v13 on v12

--- a/solution.py
+++ b/solution.py
@@ -269,10 +269,15 @@
     bias_flat = jnp.concatenate([qkv_bias.reshape(-1), up_bias])
     bias_full = lax.all_gather(bias_flat, "narrow", axis=0)
     qkv_gathered = gather_mine(qkv_weight, core, 1, 2)
+    qkv_gathered, out_weight, bias_full = lax.optimization_barrier(
+        (qkv_gathered, out_weight, bias_full)
+    )
     out_gathered = gather_mine(out_weight, core, 1, 0)
-    qkv_gathered, out_gathered, up_weight, down_weight, bias_full = lax.optimization_barrier(
-        (qkv_gathered, out_gathered, up_weight, down_weight, bias_full)
-    )
+    out_gathered, up_weight, down_weight = lax.optimization_barrier(
+        (out_gathered, up_weight, down_weight)
+    )
+    up_gathered = gather_mine(up_weight, core, 0, 1)
+    down_gathered = gather_mine(down_weight, core, 1, 0)
     qkv_full = join_halves(qkv_gathered, core, 1)
     qkv_bias_full = jnp.swapaxes(bias_full[:, : 3 * inner].reshape(-1, 3, inner), 0, 1).reshape(
         3, model
@@ -297,6 +302,9 @@
     qkv_heads = qkv_heads.reshape(3, seq_count, length, heads_here, HEAD)
     query, key_rows, values = qkv_heads[0], qkv_heads[1], qkv_heads[2]
     attn_heads, totals = attend_forward(query, key_rows, values, block_rows)
+    attn_heads, up_gathered, down_gathered = lax.optimization_barrier(
+        (attn_heads, up_gathered, down_gathered)
+    )
     attn_low = attn_heads.reshape(group_rows, inner).astype(jnp.bfloat16)
     attn_rows = lax.all_to_all(attn_low, "narrow", 0, 1, tiled=True)
     out_full = join_halves(out_gathered, core, 1)
@@ -305,8 +313,8 @@
     residual = layer_in + normed_second * norm_gains[1] + norm_biases[1]
     normed_third, inverse_third = norm_stats(residual)
     low_third = (normed_third * norm_gains[2] + norm_biases[2]).astype(jnp.bfloat16)
-    up_full = gather_halves(up_weight, core, 0, 1)
-    down_full = gather_halves(down_weight, core, 1, 0)
+    up_full = join_halves(up_gathered, core, 0)
+    down_full = join_halves(down_gathered, core, 1)
     hidden = jnp.dot(low_third, up_full, preferred_element_type=jnp.float32) + up_bias_full
     act_low = gelu_value(hidden).astype(jnp.bfloat16)
     pre_mlp = jnp.dot(act_low, down_full, preferred_element_type=jnp.float32) + down_bias

time: 987 us -> 970 us (0.983)
    all_gather x4, waiting for transfers between devices: 183 us -> 66.9 us  [gather_mine(): return lax.all_gather(mine, 'narrow', axis=gather_axis, tiled=True)]
    all_to_all x1, waiting for transfers between devices: 0.01 us -> 112 us  [shards(): qkv_heads = lax.all_to_all(qkv_tok, 'narrow', 2, 1, tiled=True)]
    unnamed x229 -> x243, local copies, waits for them, and re-layouts: 28 us -> 32 us
  transfers between devices with their start and end apart: 19 -> 19, of which waited for: 10 -> 9; matrix products, arithmetic and copies ran while one was open for 37% -> 36% of each run, Pallas kernels for 0% -> 0%
where the time goes in v13:
time: 970 us; the launch traced here: 959 us
  waiting for transfers between devices  290 us (30%)
  blocking collectives  199 us (21%)
  matrix products  178 us (18%)
  local copies, waits for them, and re-layouts  140 us (14%)
  other arithmetic  122 us (13%)
  between operations  16 us (2%)
  starting transfers between devices  15.1 us (2%)
    all_to_all x1, blocking collectives, shards(): lax.all_to_all(qkv_grad.reshape(3, group_rows, heads_here, HEAD), 'narrow...  117 us
    all_to_all x1, waiting for transfers between devices, shards(): qkv_heads = lax.all_to_all(qkv_tok, 'narrow', 2, 1, tiled=True)  112 us
    all_gather x4, waiting for transfers between devices, gather_mine(): return lax.all_gather(mine, 'narrow', axis=gather_axis, tiled=True)  66.9 us
    reduce_scatter x2, waiting for transfers between devices, reduce_halves(): lax.psum_scatter(chip_sum.astype(jnp.bfloat16), 'narrow', scatter_dimensi...  59.3 us
    psum x1, blocking collectives, shards(): lax.psum((gain_local, bias_local, out_blocal, down_blocal, up_bgrad_rows)...  41.9 us
    all_gather x1, blocking collectives, shards(): bias_full = lax.all_gather(bias_flat, 'narrow', axis=0)  32.8 us
    unnamed x243, local copies, waits for them, and re-layouts  32 us
    dot_general x4, matrix products, attend_backward(): jnp.einsum('bqhd,bkhd->bhqk', grad_block, value_block, preferred_element_...  28.4 us
  transfers between devices with their start and end apart: 19, of which 9 were waited for; matrix products, arithmetic and copies ran while one was open for 36% of the time, Pallas kernels for 0%

profile of v13, /device:TPU:0, one launch (start us, length us, event | category | flops | bytes accessed | tf_op | source)
XLA Modules:
  0.0 958.9 jit_solution(10513709131705622829)
XLA Ops:
  10.2 32.8 %all-gather.1 = f32[8,1,896]{2,1,0:T(1,128)S(1)} all-gather(f32[1,1,896]{2,1,0:T(1,128)S(1)} %reshape.456), channel_id=2, replica_groups=mesh['wide'=4,'narrow'=8] {'narrow'}, dimensions={0}, use_global_device_ids=true | all-gather | bytes 32256 | tf_op jit(solution)/shard_map/all_gather | solution.py:270
  43.0 30.7 %all-gather.7.cloned.1.call-done = bf16[3,512,1024]{1,2,0:T(8,128)(2,1)} async-done(((bf16[3,512,128]{1,2,0:T(8,128)(2,1)}), bf16[3,512,1024]{1,2,0:T(8,128)(2,1)}) %all-gather.7.cloned.1.call-update) | async-done | bytes 3145744 | tf_op jit(solution)/shard_map/all_gather | solution.py:181
  79.1 36.2 %all-gather.9.cloned.1.call-done = bf16[1024,512]{1,0:T(8,128)(2,1)} async-done(((bf16[128,512]{1,0:T(8,128)(2,1)}), bf16[1024,512]{1,0:T(8,128)(2,1)}) %all-gather.9.cloned.1.call-update) | async-done | bytes 1048592 | tf_op jit(solution)/shard_map/all_gather | solution.py:181
  116.2 3.3 broadcast_select_fusion.5
  119.5 3.6 add_bitcast_fusion
  126.6 4.5 all-to-all-start
  135.4 111.6 %all-to-all-done = bf16[3,512,16,64]{1,3,0,2:T(8,128)(2,1)} async-done(((bf16[3,512,16,64]{1,3,0,2:T(8,128)(2,1)}), bf16[3,512,16,64]{1,3,0,2:T(8,128)(2,1)}, u32[]{:S(2)}, u32[]{:S(2)}) %all-to-all-start) | async-done | bytes 3145760 | tf_op jit(solution)/shard_map/all_to_all | solution.py:301
  254.7 2.6 copy.170
  257.4 2.8 copy.167
  262.4 2.7 fusion.125
  274.3 6.0 fusion.1
  285.9 7.4 exponential_reduce_fusion.1
  293.3 3.8 fusion
  297.2 4.5 exponential_reduce_fusion
  303.9 2.8 slice-done.11
  309.2 7.1 convolution_bitcast_fusion.5
  316.4 5.1 convolution_bitcast_fusion.4
  322.7 3.3 copy.181
  330.6 4.4 all-to-all-start.1
  338.2 3.0 broadcast_select_fusion.7
  341.6 20.1 %all-to-all-done.1 = bf16[8,512,128]{1,2,0:T(8,128)(2,1)} async-done(((bf16[8,512,128]{1,2,0:T(8,128)(2,1)}), bf16[8,512,128]{1,2,0:T(8,128)(2,1)}, u32[]{:S(2)}, u32[]{:S(2)}) %all-to-all-start.1) | async-done | bytes 1048608 | tf_op jit(solution)/shard_map/all_to_all | solution.py:309
  361.7 3.2 add_reduce_fusion.1
  370.1 8.5 multiply_convert_fusion.3
  378.6 3.8 broadcast_select_fusion.1
  382.4 9.7 %add_reduce_fusion = (f32[512]{0:T(512)S(1)}, f32[512,1024]{1,0:T(8,128)S(1)}) fusion(f32[1024]{0:T(1024)S(1)} %copy-done.78, bf16[512,4096]{1,0:T(8,128)(2,1)} %get-tuple-element.124, bf16[4096,512]{1,0:T(8,128)(2,1)S(1)} %get-tuple-element.63, bf16[4096,512]{1,0:T(8,128)(2,1)S(1)} %get-tuple-element.62), kind=kOutput, calls=%fused_computation.132 | convolution fusion | flops 4312792576 | bytes 14686208 | tf_op jit(solution)/shard_map/dot_general | solution.py:320
  394.2 2.6 convert_reduce_fusion.2
  396.9 13.1 %convert_reduce_fusion = (f32[4096]{0:T(1024)}, bf16[512,4096]{1,0:T(8,128)(2,1)}) fusion(f32[512,4096]{1,0:T(8,128)} %get-tuple-element.125, f32[4096]{0:T(1024)S(1)} %bitcast.236, bf16[512,1024]{1,0:T(8,128)(2,1)S(1)} %get-tuple-element.56, bf16[4096,512]{1,0:T(8,128)(2,1)} %copy-done.34, bf16[4096,512]{1,0:T(8,128)(2,1)} %copy-done.33), kind=kOutput, calls=%fused_computation.22 | convolution fusion | flops 4339003392 | bytes 22052864 | tf_op jit(solution)/shard_map/dot_general | solution.py:348
  409.9 9.0 multiply_reduce_fusion.5
  419.0 10.7 %fusion.119 = f32[1024,4096]{1,0:T(8,128)} fusion(bf16[512,4096]{1,0:T(8,128)(2,1)} %get-tuple-element.139, f32[512,1024]{1,0:T(8,128)S(1)} %get-tuple-element.61, f32[1024]{0:T(1024)S(1)} %bitcast.246, f32[1024]{0:T(1024)S(1)} %bitcast.228, f32[512]{0:T(512)S(1)} %add_rsqrt_fusion.1, f32[512]{0:T(512)S(1)} %broadcast_multiply_fusion.9), kind=kOutput, calls=%fused_computation.282 | convolution fusion | flops 4297588736 | bytes 23080960 | tf_op jit(solution)/shard_map/dot_general | solution.py:353
  429.7 8.2 fusion.128
  437.9 3.4 multiply_reduce_fusion.6
  448.3 4.2 all-to-all-start.2
  455.3 6.1 dynamic-slice_convert_fusion
  462.0 5.9 dynamic-slice_convert_fusion.1
  469.3 9.1 all-to-all-done.2
  478.4 2.8 copy.184
  485.6 6.0 multiply_reduce_fusion.2
  503.2 7.0 multiply_reduce_fusion.1
  511.5 7.0 multiply_convert_fusion.1
  522.9 13.7 %multiply_reduce_fusion = (f32[2,2,512]{2,1,0:T(2,128)S(1)}, f32[2,2,512,2048]{3,2,1,0:T(8,128)}) fusion(f32[2,2,512,2048]{3,2,1,0:T(8,128)} %copy-done.2, f32[2,2,512]{2,1,0:T(2,128)S(1)} %log_add_fusion, pred[512,2048]{1,0:T(8,128)(4,1)S(1)} %iota_compare_fusion, bf16[2,2048,2,64]{1,0,3,2:T(2,128)(2,1)S(1)} %copy-done.19, ...), kind=kOutput, calls=%fused_computation.1 | convolution fusion | flops 557840384 | bytes 35930112 | tf_op jit(solution)/shard_map/bqhd,bkhd->bhqk/dot_general | solution.py:141
  536.7 8.2 add_convert_fusion
  544.9 12.9 %multiply_convert_fusion = bf16[2,2,512,2048]{3,2,1,0:T(8,128)(2,1)S(1)} fusion(f32[2,2,512,2048]{3,2,1,0:T(8,128)} %get-tuple-element.130, f32[2,2,512,2048]{3,2,1,0:T(8,128)} %copy-done.2, f32[2,2,512]{2,1,0:T(2,128)S(1)} %get-tuple-element.129, f32[2,2,512]{2,1,0:T(2,128)S(1)} %log_add_fusion, pred[512,2048]{1,0:T(8,128)(4,1)S(1)} %iota_compare_fusion), kind=kLoop, calls=%fused_computation | loop fusion | flops 25165824 | bytes 43008000 | tf_op jit(solution)/shard_map/convert_element_type | solution.py:145
  557.9 2.7 fusion.49
  569.8 3.3 convolution_bitcast_fusion.2
  573.1 6.1 convolution_bitcast_fusion.1
  579.3 7.7 fusion.24
  587.0 6.3 add_convert_fusion.1
  593.3 2.8 pad_maximum_fusion.7
  607.8 3.8 pad_maximum_fusion.11
  611.6 14.6 %copy.197 = bf16[3,4096,2,64]{3,2,0,1:T(2,128)(2,1)} copy(bf16[3,4096,2,64]{1,3,2,0:T(8,128)(2,1)} %pad_maximum_fusion.11) | data formatting | bytes 6291456 | tf_op jit(solution)/shard_map/stack | solution.py:376
  626.2 9.0 reshape.461
  635.2 116.9 %all_to_all.62 = bf16[8,2,98304]{2,1,0:T(2,128)(2,1)} all-to-all(bf16[8,2,98304]{2,1,0:T(2,128)(2,1)} %reshape.461), channel_id=1, replica_groups=mesh['wide'=4,'narrow'=8] {'narrow'}, dimensions={0} | all-to-all | bytes 6291456 | tf_op jit(solution)/shard_map/all_to_all | solution.py:385
  752.1 8.8 reshape.462
  760.9 15.5 %copy.216 = bf16[3,8,512,2,64]{2,4,3,1,0:T(8,128)(2,1)} copy(bf16[3,8,512,2,64]{4,3,0,2,1:T(2,128)(2,1)} %bitcast.204) | data formatting | bytes 6291456 | tf_op jit(solution)/shard_map/all_to_all | solution.py:385
  776.5 5.5 fusion.66
  782.5 5.6 collective-permute-done.4
  788.2 2.7 fusion.11
  797.8 7.0 psum.71
  811.6 59.3 %reduce-scatter.4.cloned.1.call-done = bf16[3,512,128]{1,2,0:T(8,128)(2,1)} async-done(((bf16[3,512,1024]{1,2,0:T(8,128)(2,1)}), bf16[3,512,128]{1,2,0:T(8,128)(2,1)}) %reduce-scatter.4.cloned.1.call-update) | async-done | bytes 393232 | tf_op jit(solution)/shard_map/reduce_scatter | solution.py:200
  873.4 9.0 fusion.39
  882.5 41.9 %all-reduce.6 = (f32[1024]{0:T(1024)}, f32[4096]{0:T(1024)S(1)}, f32[1024]{0:T(1024)}, f32[4,1024]{1,0:T(4,128)}, f32[4,1024]{1,0:T(4,128)}) all-reduce(f32[1024]{0:T(1024)S(1)} %copy-done.89, f32[4096]{0:T(1024)S(1)} %copy-done.86, f32[1024]{0:T(1024)S(1)} %copy-done.81, ...), channel_id=1, replica_groups=mesh['wide'=4,'narrow'=8] {'wide','narrow'}, use_global_device_ids=true, to_apply=%region_37.38 | all-reduce | flops 14336 | bytes 114688 | tf_op jit(solution)/shard_map/psum | solution.py:424
  925.1 3.3 fusion.38
  928.4 14.7 %all-reduce.10.cloned.1.call-done = (bf16[3,1024,128]{2,1,0:T(8,128)(2,1)}, bf16[128,1024]{1,0:T(8,128)(2,1)}, bf16[1024,512]{1,0:T(8,128)(2,1)}, bf16[512,1024]{1,0:T(8,128)(2,1)}) async-done(((bf16[3,1024,128]{2,1,0:T(8,128)(2,1)}, bf16[128,1024]{1,0:T(8,128)(2,1)}, bf16[1024,512]{1,0:T(8,128)(2,1)}, bf16[512,1024]{1,0:T(8,128)(2,1)}), (bf16[3,1024,128]{2,1,0:T(8,128)(2,1)}, bf16[128,1024]{1,0:T(8,128)(2,1)}, ...) | async-done | bytes 3145744 | tf_op jit(solution)/shard_map/psum | solution.py:417
  947.4 2.8 reshape.452
  (404 shorter events, 139.8 us)
Async XLA Ops:
  7.2 108.1 %copy-start = (bf16[1024,512]{1,0:T(8,128)(2,1)S(1)}, bf16[1024,512]{1,0:T(8,128)(2,1)}, u32[]{:S(2)}) copy-start(bf16[1024,512]{1,0:T(8,128)(2,1)} %param.22) | copy-start | bytes 3145732
  7.2 71.4 %copy-start.11 = (bf16[512,1024]{1,0:T(8,128)(2,1)S(1)}, bf16[512,1024]{1,0:T(8,128)(2,1)}, u32[]{:S(2)}) copy-start(bf16[512,1024]{1,0:T(8,128)(2,1)} %param.14) | copy-start | bytes 3145732
  7.2 71.8 %copy-start.87 = (f32[4,1024]{1,0:T(4,128)S(1)}, f32[4,1024]{1,0:T(4,128)}, u32[]{:S(2)}) copy-start(f32[4,1024]{1,0:T(4,128)} %param.26) | copy-start | bytes 49156
  7.2 71.8 %copy-start.88 = (f32[4,1024]{1,0:T(4,128)S(1)}, f32[4,1024]{1,0:T(4,128)}, u32[]{:S(2)}) copy-start(f32[4,1024]{1,0:T(4,128)} %param.27) | copy-start | bytes 49156
  7.2 66.4 %all-gather.7.cloned.1.call-start = ((), (), s32[]{:S(2)}) async-start(), calls=%async_computation.7 | async-start | bytes 3538944 | tf_op jit(solution)/shard_map/all_gather | solution.py:181
  9.4 105.9 %all-gather.9.cloned.1.call-start = ((), (), s32[]{:S(2)}) async-start(), calls=%async_computation.8 | async-start | bytes 1179648 | tf_op jit(solution)/shard_map/all_gather | solution.py:181
  73.6 42.5 %collective-permute-start = (bf16[3,512,1024]{1,2,0:T(8,128)(2,1)}, bf16[3,512,1024]{1,2,0:T(8,128)(2,1)}, u32[]{:S(2)}, u32[]{:S(2)}) collective-permute-start(bf16[3,512,1024]{1,2,0:T(8,128)(2,1)} %all-gather.7.cloned.1.call-done), channel_id=1, source_target_pairs={{0,8},{8,0},{16,24},{24,16},{1,9},{9,1},{17,25},{25,17},{2,10},{10... | collective-permute-start | bytes 9437192 | tf_op jit(solution)/shard_map/ppermute | solution.py:175
  75.2 247.3 %all-gather.11.cloned.1.call-start = ((), (), s32[]{:S(2)}) async-start(), calls=%async_computation.9 | async-start | bytes 4718592 | tf_op jit(solution)/shard_map/all_gather | solution.py:181
  78.6 40.9 %copy-start.79 = (f32[512]{0:T(512)}, f32[512]{0:T(512)S(1)}, u32[]{:S(2)}) copy-start(f32[512]{0:T(512)S(1)} %broadcast_multiply_fusion.11) | copy-start | bytes 6148
  79.0 40.4 %copy-start.92 = (f32[512]{0:T(512)}, f32[512]{0:T(512)S(1)}, u32[]{:S(2)}) copy-start(f32[512]{0:T(512)S(1)} %add_rsqrt_fusion.3) | copy-start | bytes 6148
  79.1 40.4 %copy-start.90 = (f32[1,1024]{1,0:T(1,128)}, f32[1,1024]{1,0:T(1,128)S(1)}, u32[]{:S(2)}) copy-start(f32[1,1024]{1,0:T(1,128)S(1)} %get-tuple-element.106) | copy-start | bytes 12292
  79.1 40.4 %copy-start.94 = (f32[1,1024]{1,0:T(1,128)}, f32[1,1024]{1,0:T(1,128)S(1)}, u32[]{:S(2)}) copy-start(f32[1,1024]{1,0:T(1,128)S(1)} %get-tuple-element.110) | copy-start | bytes 12292
  126.6 120.4 %all-to-all-start = ((bf16[3,512,16,64]{1,3,0,2:T(8,128)(2,1)}), bf16[3,512,16,64]{1,3,0,2:T(8,128)(2,1)}, u32[]{:S(2)}, u32[]{:S(2)}) async-start(bf16[3,512,16,64]{1,3,0,2:T(8,128)(2,1)} %pad_maximum_fusion.10), calls=%async_computation | async-start | bytes 6291456 | tf_op jit(solution)/shard_map/all_to_all | solution.py:301
  131.0 191.6 %all-gather.13.cloned.1.call-start = ((), (), s32[]{:S(2)}) async-start(), calls=%async_computation.10 | async-start | bytes 4718592 | tf_op jit(solution)/shard_map/all_gather | solution.py:181
  132.3 359.3 %copy-start.13 = (pred[512,1024]{1,0:T(8,128)(4,1)}, pred[512,1024]{1,0:T(8,128)(4,1)S(1)}, u32[]{:S(2)}) copy-start(pred[512,1024]{1,0:T(8,128)(4,1)S(1)} %iota_compare_fusion.2) | copy-start | bytes 1572868
  132.8 378.7 %copy-start.8 = (pred[512,1536]{1,0:T(8,128)(4,1)}, pred[512,1536]{1,0:T(8,128)(4,1)S(1)}, u32[]{:S(2)}) copy-start(pred[512,1536]{1,0:T(8,128)(4,1)S(1)} %iota_compare_fusion.1) | copy-start | bytes 2359300
  265.1 9.3 copy-start.66
  285.8 23.4 %copy-start.23 = (bf16[2,2048,2,64]{1,3,2,0:T(8,128)(2,1)}, bf16[2,2048,2,64]{1,3,2,0:T(8,128)(2,1)S(1)}, u32[]{:S(2)}) copy-start(bf16[2,2048,2,64]{1,3,2,0:T(8,128)(2,1)S(1)} %copy.166) | copy-start | bytes 3145732
  293.3 218.2 %copy-start.74 = (f32[2,2,512]{2,1,0:T(2,128)}, f32[2,2,512]{2,1,0:T(2,128)S(1)}, u32[]{:S(2)}) copy-start(f32[2,2,512]{2,1,0:T(2,128)S(1)} %log_add_fusion.1) | copy-start | bytes 24580
  293.3 10.6 %slice-start.10 = ((s8[8388608]{0:T(1024)(128)(4,1)}), s8[4194304]{0:T(1024)(128)(4,1)S(1)}, s32[]{:S(2)}) async-start(s8[8388608]{0:T(1024)(128)(4,1)} %bitcast.197), calls=%async_computation.25 | async-start | bytes 8388608
  297.2 19.2 %copy-start.2 = (f32[2,2,512,2048]{3,2,1,0:T(8,128)}, f32[2,2,512,2048]{3,2,1,0:T(8,128)S(1)}, u32[]{:S(2)}) copy-start(f32[2,2,512,2048]{3,2,1,0:T(8,128)S(1)} %get-tuple-element.115) | copy-start | bytes 50331652
  297.2 9.6 slice-start.11
  302.7 242.2 %copy-start.75 = (f32[2,2,512]{2,1,0:T(2,128)}, f32[2,2,512]{2,1,0:T(2,128)S(1)}, u32[]{:S(2)}) copy-start(f32[2,2,512]{2,1,0:T(2,128)S(1)} %log_add_fusion) | copy-start | bytes 24580
  322.6 13.0 %copy-start.98 = (s32[2]{0:T(128)S(1)}, s32[2]{0:T(128)}, u32[]{:S(2)}) copy-start(s32[2]{0:T(128)} %param.16) | copy-start | bytes 28
  322.6 13.1 %copy-start.99 = (f32[8]{0:T(128)S(1)}, f32[8]{0:T(128)}, u32[]{:S(2)}) copy-start(f32[8]{0:T(128)} %param.17) | copy-start | bytes 100
  322.6 43.9 %collective-permute-start.2 = (bf16[512,4096]{1,0:T(8,128)(2,1)}, bf16[512,4096]{1,0:T(8,128)(2,1)}, u32[]{:S(2)}, u32[]{:S(2)}) collective-permute-start(bf16[512,4096]{1,0:T(8,128)(2,1)} %all-gather.11.cloned.1.call-done), channel_id=1, source_target_pairs={{0,8},{8,0},{16,24},{24,16},{1,9},{9,1},{17,25},{25,17},{2,10},{10... | collective-permute-start | bytes 12582920 | tf_op jit(solution)/shard_map/ppermute | solution.py:175
  328.1 33.6 %copy-start.77 = (f32[1024]{0:T(1024)S(1)}, f32[1024]{0:T(1024)}, u32[]{:S(2)}) copy-start(f32[1024]{0:T(1024)} %param.21) | copy-start | bytes 12292
  330.6 31.1 %all-to-all-start.1 = ((bf16[8,512,128]{1,2,0:T(8,128)(2,1)}), bf16[8,512,128]{1,2,0:T(8,128)(2,1)}, u32[]{:S(2)}, u32[]{:S(2)}) async-start(bf16[8,512,128]{1,2,0:T(8,128)(2,1)} %copy.182), calls=%async_computation.1 | async-start | bytes 2097152 | tf_op jit(solution)/shard_map/all_to_all | solution.py:309
  335.0 3.2 collective-permute-start.1
  341.2 37.3 %collective-permute-start.3 = (bf16[4096,512]{1,0:T(8,128)(2,1)}, bf16[4096,512]{1,0:T(8,128)(2,1)}, u32[]{:S(2)}, u32[]{:S(2)}) collective-permute-start(bf16[4096,512]{1,0:T(8,128)(2,1)} %all-gather.13.cloned.1.call-done), channel_id=1, source_target_pairs={{0,8},{8,0},{16,24},{24,16},{1,9},{9,1},{17,25},{25,17},{2,10},{10... | collective-permute-start | bytes 12582920 | tf_op jit(solution)/shard_map/ppermute | solution.py:175
  382.3 9.7 %copy-start.33 = (bf16[4096,512]{1,0:T(8,128)(2,1)}, bf16[4096,512]{1,0:T(8,128)(2,1)S(1)}, u32[]{:S(2)}) copy-start(bf16[4096,512]{1,0:T(8,128)(2,1)S(1)} %get-tuple-element.62) | copy-start | bytes 12582916
  382.3 9.7 %copy-start.34 = (bf16[4096,512]{1,0:T(8,128)(2,1)}, bf16[4096,512]{1,0:T(8,128)(2,1)S(1)}, u32[]{:S(2)}) copy-start(bf16[4096,512]{1,0:T(8,128)(2,1)S(1)} %get-tuple-element.63) | copy-start | bytes 12582916
  382.4 10.1 %copy-start.15 = (bf16[512,1024]{1,0:T(8,128)(2,1)S(1)}, bf16[512,1024]{1,0:T(8,128)(2,1)}, u32[]{:S(2)}) copy-start(bf16[512,1024]{1,0:T(8,128)(2,1)} %param.15) | copy-start | bytes 3145732
  396.9 13.1 %copy-start.59 = (bf16[512,1024]{1,0:T(8,128)(2,1)}, bf16[512,1024]{1,0:T(8,128)(2,1)S(1)}, u32[]{:S(2)}) copy-start(bf16[512,1024]{1,0:T(8,128)(2,1)S(1)} %get-tuple-element.56) | copy-start | bytes 3145732
  396.9 13.1 %copy-start.32 = (bf16[512,4096]{1,0:T(8,128)(2,1)S(1)}, bf16[512,4096]{1,0:T(8,128)(2,1)}, u32[]{:S(2)}) copy-start(bf16[512,4096]{1,0:T(8,128)(2,1)} %copy-done.31) | copy-start | bytes 12582916
  419.0 10.7 %copy-start.60 = (bf16[512,1024]{1,0:T(8,128)(2,1)S(1)}, bf16[512,1024]{1,0:T(8,128)(2,1)}, u32[]{:S(2)}) copy-start(bf16[512,1024]{1,0:T(8,128)(2,1)} %copy-done.59) | copy-start | bytes 3145732
  419.0 10.7 %copy-start.100 = (bf16[512,4096]{1,0:T(8,128)(2,1)S(1)}, bf16[512,4096]{1,0:T(8,128)(2,1)}, u32[]{:S(2)}) copy-start(bf16[512,4096]{1,0:T(8,128)(2,1)} %get-tuple-element.124) | copy-start | bytes 12582916
  448.3 30.1 %all-to-all-start.2 = ((bf16[512,8,128]{0,2,1:T(8,128)(2,1)}), bf16[512,8,128]{0,2,1:T(8,128)(2,1)}, u32[]{:S(2)}, u32[]{:S(2)}) async-start(bf16[512,8,128]{0,2,1:T(8,128)(2,1)} %bitcast.29), calls=%async_computation.2 | async-start | bytes 2097152 | tf_op jit(solution)/shard_map/all_to_all | solution.py:367
  452.5 352.8 %reduce-scatter.8.cloned.1.call-start = ((), (), s32[]{:S(2)}) async-start(), calls=%async_computation.13 | async-start | bytes 4718592 | tf_op jit(solution)/shard_map/reduce_scatter | solution.py:200
  455.3 12.6 %collective-permute-start.6 = (bf16[1024,512]{1,0:T(8,128)(2,1)S(1)}, bf16[1024,512]{1,0:T(8,128)(2,1)S(1)}, u32[]{:S(2)}, u32[]{:S(2)}) collective-permute-start(bf16[1024,512]{1,0:T(8,128)(2,1)S(1)} %dynamic-slice_convert_fusion.3), channel_id=1, source_target_pairs={{0,8},{8,0},{16,24},{24,16},{1,9},{9,1},{17,25},{25,17},{2,10},{10... | collective-permute-start | bytes 3145736 | tf_op jit(solution)/shard_map/ppermute | solution.py:175
  461.5 75.2 %collective-permute-start.7 = (bf16[512,4096]{1,0:T(8,128)(2,1)}, bf16[512,4096]{1,0:T(8,128)(2,1)}, u32[]{:S(2)}, u32[]{:S(2)}) collective-permute-start(bf16[512,4096]{1,0:T(8,128)(2,1)} %dynamic-slice_convert_fusion), channel_id=1, source_target_pairs={{0,8},{8,0},{16,24},{24,16},{1,9},{9,1},{17,25},{25,17},{2,10},{10... | collective-permute-start | bytes 12582920 | tf_op jit(solution)/shard_map/ppermute | solution.py:175
  467.9 119.1 %collective-permute-start.5 = (bf16[4096,512]{1,0:T(8,128)(2,1)}, bf16[4096,512]{1,0:T(8,128)(2,1)}, u32[]{:S(2)}, u32[]{:S(2)}) collective-permute-start(bf16[4096,512]{1,0:T(8,128)(2,1)} %dynamic-slice_convert_fusion.1), channel_id=1, source_target_pairs={{0,8},{8,0},{16,24},{24,16},{1,9},{9,1},{17,25},{25,17},{2,10},{10... | collective-permute-start | bytes 12582920 | tf_op jit(solution)/shard_map/ppermute | solution.py:175
  469.3 16.3 %copy-start.24 = (bf16[2,2048,2,64]{1,3,2,0:T(8,128)(2,1)S(1)}, bf16[2,2048,2,64]{1,3,2,0:T(8,128)(2,1)}, u32[]{:S(2)}) copy-start(bf16[2,2048,2,64]{1,3,2,0:T(8,128)(2,1)} %copy-done.23) | copy-start | bytes 3145732
  485.5 12.7 %copy-start.68 = (bf16[2,512,2,64]{1,0,3,2:T(2,128)(2,1)}, bf16[2,512,2,64]{1,0,3,2:T(2,128)(2,1)S(1)}, u32[]{:S(2)}) copy-start(bf16[2,512,2,64]{1,0,3,2:T(2,128)(2,1)S(1)} %get-tuple-element.87) | copy-start | bytes 786436
  485.5 17.5 %copy-start.53 = (bf16[2,512,2,64]{1,0,3,2:T(2,128)(2,1)}, bf16[2,512,2,64]{1,0,3,2:T(2,128)(2,1)S(1)}, u32[]{:S(2)}) copy-start(bf16[2,512,2,64]{1,0,3,2:T(2,128)(2,1)S(1)} %get-tuple-element.85) | copy-start | bytes 786436
  485.5 37.4 %copy-start.52 = (bf16[2,512,2,64]{1,0,3,2:T(2,128)(2,1)}, bf16[2,512,2,64]{1,0,3,2:T(2,128)(2,1)S(1)}, u32[]{:S(2)}) copy-start(bf16[2,512,2,64]{1,0,3,2:T(2,128)(2,1)S(1)} %get-tuple-element.84) | copy-start | bytes 786436
  544.9 262.7 %reduce-scatter.6.cloned.1.call-start = ((), (), s32[]{:S(2)}) async-start(), calls=%async_computation.12 | async-start | bytes 5898240 | tf_op jit(solution)/shard_map/reduce_scatter | solution.py:218
  544.9 13.0 %copy-start.17 = (bf16[2,2048,2,64]{1,0,3,2:T(2,128)(2,1)S(1)}, bf16[2,2048,2,64]{1,0,3,2:T(2,128)(2,1)}, u32[]{:S(2)}) copy-start(bf16[2,2048,2,64]{1,0,3,2:T(2,128)(2,1)} %squeeze.20) | copy-start | bytes 3145732
  560.7 12.4 %slice-start.7 = ((s8[12582912]{0:T(1024)(128)(4,1)}), s8[4194304]{0:T(1024)(128)(4,1)S(1)}, s32[]{:S(2)}) async-start(s8[12582912]{0:T(1024)(128)(4,1)} %bitcast.195), calls=%async_computation.22 | async-start | bytes 8388608
  562.3 10.8 %slice-start.8 = ((s8[12582912]{0:T(1024)(128)(4,1)}), s8[4194304]{0:T(1024)(128)(4,1)S(1)}, s32[]{:S(2)}) async-start(s8[12582912]{0:T(1024)(128)(4,1)} %bitcast.195), calls=%async_computation.23 | async-start | bytes 8388608
  569.8 9.5 slice-start
  569.8 9.5 slice-start.1
  596.2 274.7 %reduce-scatter.4.cloned.1.call-start = ((), (), s32[]{:S(2)}) async-start(), calls=%async_computation.11 | async-start | bytes 3538944 | tf_op jit(solution)/shard_map/reduce_scatter | solution.py:200
  760.9 15.5 %copy-start.12 = (bf16[512,1024]{1,0:T(8,128)(2,1)S(1)}, bf16[512,1024]{1,0:T(8,128)(2,1)}, u32[]{:S(2)}) copy-start(bf16[512,1024]{1,0:T(8,128)(2,1)} %param.14) | copy-start | bytes 3145732
  760.9 15.5 %copy-start.80 = (f32[512]{0:T(512)S(1)}, f32[512]{0:T(512)}, u32[]{:S(2)}) copy-start(f32[512]{0:T(512)} %copy-done.79) | copy-start | bytes 6148
  760.9 15.5 %copy-start.91 = (f32[1,1024]{1,0:T(1,128)S(1)}, f32[1,1024]{1,0:T(1,128)}, u32[]{:S(2)}) copy-start(f32[1,1024]{1,0:T(1,128)} %copy-done.90) | copy-start | bytes 12292
  760.9 15.5 %copy-start.93 = (f32[512]{0:T(512)S(1)}, f32[512]{0:T(512)}, u32[]{:S(2)}) copy-start(f32[512]{0:T(512)} %copy-done.92) | copy-start | bytes 6148
  760.9 15.5 %copy-start.95 = (f32[1,1024]{1,0:T(1,128)S(1)}, f32[1,1024]{1,0:T(1,128)}, u32[]{:S(2)}) copy-start(f32[1,1024]{1,0:T(1,128)} %copy-done.94) | copy-start | bytes 12292
  782.5 5.7 collective-permute-start.4
  791.0 152.1 %all-reduce.10.cloned.1.call-start = ((), (), s32[]{:S(2)}) async-start(), calls=%async_computation.14 | async-start | bytes 6291456 | tf_op jit(solution)/shard_map/psum | solution.py:417
  873.3 9.2 copy-start.81
  873.3 9.2 copy-start.86
  873.4 9.2 copy-start.89
  873.4 51.7 %copy-start.10 = (f32[512,1024]{1,0:T(8,128)S(1)}, f32[512,1024]{1,0:T(8,128)}, u32[]{:S(2)}) copy-start(f32[512,1024]{1,0:T(8,128)} %copy-done.9) | copy-start | bytes 6291460
  (72 other events, 331.3 us)
Sparse Core Ops, SparseCore 0:
  10.8 62.7 all-gather.6
  76.3 38.9 all-gather.8
  117.9 128.9 all-gather.10
  249.5 71.5 all-gather.12
  545.0 87.8 reduce-scatter.7
  636.3 156.4 reduce-scatter.5
  796.4 74.4 reduce-scatter.3
  874.1 68.8 all-reduce.9

commit v14 on v5

--- a/solution.py
+++ b/solution.py
@@ -268,33 +268,14 @@
     heads_here = inner // HEAD
     bias_flat = jnp.concatenate([qkv_bias.reshape(-1), up_bias])
     bias_full = lax.all_gather(bias_flat, "narrow", axis=0)
-    qkv_gathered = gather_mine(qkv_weight, core, 1, 2)
-    qkv_gathered, up_weight, down_weight, bias_full = lax.optimization_barrier(
-        (qkv_gathered, up_weight, down_weight, bias_full)
-    )
-    qkv_full = join_halves(qkv_gathered, core, 1)
-    qkv_bias_full = jnp.swapaxes(bias_full[:, : 3 * inner].reshape(-1, 3, inner), 0, 1).reshape(
-        3, model
+    gathered_first = lax.all_gather(low_first, "narrow", axis=0, tiled=True)
+    gathered_first, up_weight, down_weight, bias_full = lax.optimization_barrier(
+        (gathered_first, up_weight, down_weight, bias_full)
     )
     up_bias_full = bias_full[:, 3 * inner :].reshape(-1)
-    position_start = first_row % length
-    cos_rows = lax.dynamic_slice_in_dim(cos_table, position_start, shard_rows, 0)
-    sine_rows = lax.dynamic_slice_in_dim(sine_table, position_start, shard_rows, 0)
-    qkv_rows = (
-        jnp.einsum("sd,tde->tse", low_first, qkv_full, preferred_element_type=jnp.float32)
-        + qkv_bias_full[:, None, :]
-    )
-    shaped = qkv_rows.reshape(3, shard_rows, model // HEAD, HEAD)
-    qkv_tok = jnp.stack(
-        [
-            rotate(shaped[0], cos_rows, sine_rows),
-            rotate(shaped[1], cos_rows, sine_rows),
-            shaped[2],
-        ]
-    ).astype(jnp.bfloat16)
-    qkv_heads = lax.all_to_all(qkv_tok, "narrow", 2, 1, tiled=True)
-    qkv_heads = qkv_heads.reshape(3, seq_count, length, heads_here, HEAD)
-    query, key_rows, values = qkv_heads[0], qkv_heads[1], qkv_heads[2]
+    query, key_rows, values = project_qkv(
+        gathered_first, qkv_weight, qkv_bias, cos_table, sine_table, seq_count, length
+    )
     attn_heads, totals = attend_forward(query, key_rows, values, block_rows)
     attn_low = attn_heads.reshape(group_rows, inner).astype(jnp.bfloat16)
     attn_rows = lax.all_to_all(attn_low, "narrow", 0, 1, tiled=True)
@@ -308,6 +289,8 @@
     down_full = gather_halves(down_weight, core, 1, 0)
     hidden = jnp.dot(low_third, up_full, preferred_element_type=jnp.float32) + up_bias_full
     act_low = gelu_value(hidden).astype(jnp.bfloat16)
+    act_low, qkv_late = lax.optimization_barrier((act_low, qkv_weight))
+    qkv_full = join_halves(gather_mine(qkv_late, core, 1, 2), core, 1)
     pre_mlp = jnp.dot(act_low, down_full, preferred_element_type=jnp.float32) + down_bias
     normed_fourth, inverse_fourth = norm_stats(pre_mlp)
     final_sum = residual + normed_fourth * norm_gains[3] + norm_biases[3]
@@ -376,13 +359,12 @@
     qkv_grad_rows = lax.all_to_all(
         qkv_grad.reshape(3, group_rows, heads_here, HEAD), "narrow", 1, 2, tiled=True
     ).reshape(3, shard_rows, model)
-    qkv_wgrad_rows = jnp.einsum(
-        "sd,tse->tde", low_first, qkv_grad_rows, preferred_element_type=jnp.float32
+    qkv_wgrad = jnp.einsum(
+        "sd,tse->tde", gathered_first, qkv_grad, preferred_element_type=jnp.float32
     )
     first_grad = jnp.einsum(
         "tse,tde->sd", qkv_grad_rows, qkv_full, preferred_element_type=jnp.float32
     )
-    qkv_slots = reduce_halves(qkv_wgrad_rows, core, 1, 2)
     input_grad = (
         residual_grad + norm_back(normed_first, inverse_first, norm_gains[0], first_grad)
     ).astype(jnp.bfloat16)
@@ -405,7 +387,7 @@
     out_blocal = jnp.sum(branch_grad.astype(jnp.float32), axis=0)
     down_blocal = jnp.sum(mlp_grad.astype(jnp.float32), axis=0)
     weight_sums = (
-        lax.psum(qkv_slots, "wide").astype(jnp.float32),
+        lax.psum(qkv_wgrad.astype(jnp.bfloat16), "wide").astype(jnp.float32),
         lax.psum(qkv_bgrad.astype(jnp.bfloat16), "wide").astype(jnp.float32),
         lax.psum(out_slots, "wide").astype(jnp.float32),
         lax.psum(up_slots, "wide").astype(jnp.float32),
@@ -420,7 +402,7 @@
     up_wgrad = merge_slots(weight_sums[3], 0)
     down_wgrad = merge_slots(weight_sums[5], 1)
     out_wgrad = merge_slots(weight_sums[2], 1)
-    qkv_wgrad = merge_slots(weight_sums[0], 1)
+    qkv_wgrad = weight_sums[0]
     return (
         layer_out,
         input_grad,

time: 949 us -> 876 us (0.923)
  blocking collectives: 198 us -> 83.9 us
  local copies, waits for them, and re-layouts: 132 us -> 184 us
  waiting for transfers between devices: 285 us -> 247 us
  matrix products: 177 us -> 196 us
  other arithmetic: 116 us -> 130 us
    all_gather x3, waiting for transfers between devices: 139 us -> 1.78 us  [gather_mine(): return lax.all_gather(mine, 'narrow', axis=gather_axis, tiled=True)]
    all_to_all x1 -> x0, blocking collectives: 116 us -> none  [shards(): lax.all_to_all(qkv_grad.reshape(3, group_rows, heads_here, HEAD), 'narrow...]
    all_gather x0 -> x1, waiting for transfers between devices: none -> 93.9 us  [shards(): gathered_first = lax.all_gather(low_first, 'narrow', axis=0, tiled=True)]
    reduce_scatter x2 -> x1, waiting for transfers between devices: 59.3 us -> 0.01 us  [reduce_halves(): lax.psum_scatter(chip_sum.astype(jnp.bfloat16), 'narrow', scatter_dimensi...]
    all_to_all x1, waiting for transfers between devices: 0.01 us -> 58.6 us  [shards(): lax.all_to_all(qkv_grad.reshape(3, group_rows, heads_here, HEAD), 'narrow...]
    unnamed x223 -> x227, local copies, waits for them, and re-layouts: 26.4 us -> 63.9 us
    convert_element_type x4, other arithmetic: 23.5 us -> 36.5 us  [attend_backward(): scores_grad = (probs_full * (probs_grad - row_dot)).astype(jnp.bfloat16)]
    slice x7 -> x4, local copies, waits for them, and re-layouts: 12.1 us -> 23.5 us  [the longest x2 20.1 us: rotate(): front_half = vectors[..., :half_size]]
  transfers between devices with their start and end apart: 18 -> 17, of which waited for: 8 -> 7; matrix products, arithmetic and copies ran while one was open for 36% -> 47% of each run, Pallas kernels for 0% -> 0%
where the time goes in v14:
time: 876 us; the launch traced here: 869 us
  waiting for transfers between devices  247 us (28%)
  matrix products  196 us (22%)
  local copies, waits for them, and re-layouts  184 us (21%)
  other arithmetic  130 us (15%)
  blocking collectives  83.9 us (10%)
  between operations  15.9 us (2%)
  starting transfers between devices  13.7 us (2%)
    all_gather x1, waiting for transfers between devices, shards(): gathered_first = lax.all_gather(low_first, 'narrow', axis=0, tiled=True)  93.9 us
    unnamed x227, local copies, waits for them, and re-layouts  63.9 us
    all_gather x1, waiting for transfers between devices, shards(): out_full = lax.all_gather(out_weight, 'narrow', axis=0, tiled=True)  59.1 us
    all_to_all x1, waiting for transfers between devices, shards(): lax.all_to_all(qkv_grad.reshape(3, group_rows, heads_here, HEAD), 'narrow...  58.6 us
    psum x1, blocking collectives, shards(): lax.psum((gain_local, bias_local, out_blocal, down_blocal, up_bgrad_rows)...  42.5 us
    convert_element_type x4, other arithmetic, attend_backward(): scores_grad = (probs_full * (probs_grad - row_dot)).astype(jnp.bfloat16)  36.5 us
    all_gather x1, blocking collectives, shards(): bias_full = lax.all_gather(bias_flat, 'narrow', axis=0)  33.4 us
    dot_general x4, matrix products, attend_backward(): jnp.einsum('bqhd,bkhd->bhqk', grad_block, value_block, preferred_element_...  30.9 us
  transfers between devices with their start and end apart: 17, of which 7 were waited for; matrix products, arithmetic and copies ran while one was open for 47% of the time, Pallas kernels for 0%

profile of v14, /device:TPU:0, one launch (start us, length us, event | category | flops | bytes accessed | tf_op | source)
XLA Modules:
  0.0 869.3 jit_solution(15121293974901205220)
XLA Ops:
  15.0 33.4 %all-gather.1 = f32[8,1,896]{2,1,0:T(1,128)S(1)} all-gather(f32[1,1,896]{2,1,0:T(1,128)S(1)} %reshape.435), channel_id=2, replica_groups=mesh['wide'=4,'narrow'=8] {'narrow'}, dimensions={0}, use_global_device_ids=true | all-gather | bytes 32256 | tf_op jit(solution)/shard_map/all_gather | solution.py:270
  48.4 93.9 %all-gather.8.cloned.1.call-done = bf16[4096,1024]{1,0:T(8,128)(2,1)} async-done(((bf16[512,1024]{1,0:T(8,128)(2,1)}), bf16[4096,1024]{1,0:T(8,128)(2,1)}) %all-gather.8.cloned.1.call-update) | async-done | bytes 8388624 | tf_op jit(solution)/shard_map/all_gather | solution.py:271
  147.5 7.3 add_bitcast_fusion
  158.2 5.0 reshape.440
  163.1 5.9 copy.114
  169.0 5.6 reshape.442
  174.6 10.1 %fusion.130 = (f32[2,2048,2,32]{3,2,1,0:T(2,128)}, f32[2,2048,2,32]{3,2,1,0:T(2,128)}) fusion(f32[2,2048,2,64]{3,2,1,0:T(2,128)} %reshape.442), kind=kLoop, calls=%fused_computation.276 | loop fusion | bytes 4194304 | tf_op jit(solution)/shard_map/slice | solution.py:41
  184.7 6.4 copy.168
  191.1 6.4 copy.167
  197.6 5.6 reshape.441
  203.2 10.0 %fusion.131 = (f32[2,2048,2,32]{3,2,1,0:T(2,128)}, f32[2,2048,2,32]{3,2,1,0:T(2,128)}) fusion(f32[2,2048,2,64]{3,2,1,0:T(2,128)} %reshape.441), kind=kLoop, calls=%fused_computation.277 | loop fusion | bytes 4194304 | tf_op jit(solution)/shard_map/slice | solution.py:41
  213.1 6.4 copy.166
  219.5 6.6 copy.165
  229.3 3.3 fusion
  232.6 4.5 exponential_reduce_fusion
  237.1 6.0 fusion.1
  243.1 6.7 exponential_reduce_fusion.1
  254.9 7.0 fusion.66
  262.0 5.6 fusion.64
  271.5 4.4 fusion.67
  276.0 3.6 fusion.65
  284.6 4.4 all-to-all-start
  291.0 59.1 %all-gather.10.cloned.1.call-done = bf16[1024,1024]{1,0:T(8,128)(2,1)} async-done(((bf16[128,1024]{1,0:T(8,128)(2,1)}), bf16[1024,1024]{1,0:T(8,128)(2,1)}) %all-gather.10.cloned.1.call-update) | async-done | bytes 2097168 | tf_op jit(solution)/shard_map/all_gather | solution.py:282
  355.9 3.9 broadcast_select_fusion.3
  359.8 10.2 %multiply_convert_fusion.3 = (bf16[512,4096]{1,0:T(8,128)(2,1)}, f32[512,4096]{1,0:T(8,128)}) fusion(f32[4096]{0:T(1024)S(1)} %bitcast.206, bf16[512,4096]{1,0:T(8,128)(2,1)} %get-tuple-element.107, bf16[512,4096]{1,0:T(8,128)(2,1)S(1)} %get-tuple-element.106, f32[512,1024]{1,0:T(8,128)S(1)} %get-tuple-element.103, f32[1024]{0:T(1024)S(1)} %bitcast.210, ...), kind=kOutput, calls=%fused_computation.33 | convolution fusion | flops 4326948864 | bytes 23097344 | tf_op jit(solution)/shard_map/dot_general | solution.py:290
  369.9 5.1 broadcast_select_fusion.1
  375.1 9.3 %add_reduce_fusion = (f32[512]{0:T(512)S(1)}, f32[512,1024]{1,0:T(8,128)S(1)}) fusion(f32[1024]{0:T(1024)S(1)} %copy-done.67, bf16[512,4096]{1,0:T(8,128)(2,1)} %get-tuple-element.21, bf16[4096,512]{1,0:T(8,128)(2,1)} %get-tuple-element.105, bf16[4096,512]{1,0:T(8,128)(2,1)} %get-tuple-element.104), kind=kOutput, calls=%fused_computation.129 | convolution fusion | flops 4312792576 | bytes 14686208 | tf_op jit(solution)/shard_map/dot_general | solution.py:294
  389.2 8.4 fusion.135
  397.6 12.3 %convert_reduce_fusion = (f32[4096]{0:T(1024)}, bf16[512,4096]{1,0:T(8,128)(2,1)}) fusion(f32[512,4096]{1,0:T(8,128)} %get-tuple-element.160, f32[4096]{0:T(1024)S(1)} %bitcast.207, bf16[512,1024]{1,0:T(8,128)(2,1)S(1)} %get-tuple-element.98, bf16[4096,512]{1,0:T(8,128)(2,1)} %get-tuple-element.105, bf16[4096,512]{1,0:T(8,128)(2,1)} %get-tuple-element.104), kind=kOutput, calls=%fused_computation.26 | convolution fusion | flops 4339003392 | bytes 22052864 | tf_op jit(solution)/shard_map/dot_general | solution.py:322
  409.9 9.1 %multiply_reduce_fusion.5 = (f32[1024]{0:T(1024)}, f32[512]{0:T(512)S(1)}, f32[512]{0:T(512)S(1)}, f32[1024]{0:T(1024)}, f32[512,1024]{1,0:T(8,128)S(1)}) fusion(f32[512,1024]{1,0:T(8,128)S(1)} %get-tuple-element.103, f32[512]{0:T(512)S(1)} %add_rsqrt_fusion.1, f32[512]{0:T(512)S(1)} %broadcast_multiply_fusion.9, f32[1024]{0:T(1024)S(1)} %bitcast.196, ...), kind=kOutput, calls=%fused_computation.101 | convolution fusion | flops 4316460032 | bytes 16797696 | tf_op jit(solution)/shard_map/dot_general | solution.py:330
  419.0 10.5 %fusion.126 = f32[1024,4096]{1,0:T(8,128)} fusion(bf16[512,4096]{1,0:T(8,128)(2,1)} %get-tuple-element.174, f32[512,1024]{1,0:T(8,128)S(1)} %get-tuple-element.103, f32[1024]{0:T(1024)S(1)} %bitcast.211, f32[1024]{0:T(1024)S(1)} %bitcast.197, f32[512]{0:T(512)S(1)} %add_rsqrt_fusion.1, f32[512]{0:T(512)S(1)} %broadcast_multiply_fusion.9), kind=kOutput, calls=%fused_computation.273 | convolution fusion | flops 4297588736 | bytes 23080960 | tf_op jit(solution)/shard_map/dot_general | solution.py:327
  429.6 3.4 multiply_reduce_fusion.6
  438.0 3.6 all-to-all-start.1
  446.5 5.9 dynamic-slice_convert_fusion.1
  452.9 6.2 dynamic-slice_convert_fusion
  460.5 18.5 %all-to-all-done.1 = bf16[512,8,128]{0,2,1:T(8,128)(2,1)S(1)} async-done(((bf16[512,8,128]{0,2,1:T(8,128)(2,1)}), bf16[512,8,128]{0,2,1:T(8,128)(2,1)S(1)}, u32[]{:S(2)}, u32[]{:S(2)}) %all-to-all-start.1) | async-done | bytes 1048608 | tf_op jit(solution)/shard_map/all_to_all | solution.py:341
  483.7 6.2 convolution_bitcast_fusion.2
  494.1 11.8 %multiply_reduce_fusion.1 = (f32[2,2,512]{2,1,0:T(2,128)}, f32[2,2,512,1536]{3,2,1,0:T(8,128)}) fusion(f32[2,2,512,1536]{3,2,1,0:T(8,128)} %get-tuple-element.152, f32[2,2,512]{2,1,0:T(2,128)S(1)} %log_add_fusion.1, pred[512,1536]{1,0:T(8,128)(4,1)S(1)} %copy-done.12, bf16[2,2048,2,64]{1,3,2,0:T(8,128)(2,1)S(1)} %copy-done.28, ...), kind=kOutput, calls=%fused_computation.7 | convolution fusion | flops 418379776 | bytes 27017216 | tf_op jit(solution)/shard_map/bqhd,bkhd->bhqk/dot_general | solution.py:141
  505.9 11.5 %multiply_reduce_fusion = (f32[2,2,512]{2,1,0:T(2,128)}, f32[2,2,512,2048]{3,2,1,0:T(8,128)}) fusion(f32[2,2,512,2048]{3,2,1,0:T(8,128)S(1)} %bitcast.165, f32[2,2,512]{2,1,0:T(2,128)} %copy-done.64, pred[512,2048]{1,0:T(8,128)(4,1)S(1)} %iota_compare_fusion, bf16[2,2048,2,64]{1,3,2,0:T(8,128)(2,1)} %copy.114, bf16[2,512,2,64]{1,0,3,2:T(2,128)(2,1)} %get-tuple-element.125), kind=kOutput, calls=%fused_computation.1 | convolution fusion | flops 557840384 | bytes 35930112 | tf_op jit(solution)/shard_map/bqhd,bkhd->bhqk/dot_general | solution.py:141
  517.3 12.0 %multiply_convert_fusion.1 = bf16[2,2,512,1536]{3,2,1,0:T(8,128)(2,1)} fusion(f32[2,2,512,1536]{3,2,1,0:T(8,128)} %get-tuple-element.167, f32[2,2,512,1536]{3,2,1,0:T(8,128)} %get-tuple-element.152, f32[2,2,512]{2,1,0:T(2,128)} %get-tuple-element.166, f32[2,2,512]{2,1,0:T(2,128)S(1)} %log_add_fusion.1, pred[512,1536]{1,0:T(8,128)(4,1)} %copy-done.11), kind=kLoop, calls=%fused_computation.6 | loop fusion | flops 18874368 | bytes 32260096 | tf_op jit(solution)/shard_map/convert_element_type | solution.py:145
  529.3 8.1 add_convert_fusion
  538.6 5.7 fusion.59
  544.3 12.4 %multiply_convert_fusion = bf16[2,2,512,2048]{3,2,1,0:T(8,128)(2,1)S(1)} fusion(f32[2,2,512,2048]{3,2,1,0:T(8,128)} %get-tuple-element.165, f32[2,2,512,2048]{3,2,1,0:T(8,128)} %copy-done.2, f32[2,2,512]{2,1,0:T(2,128)S(1)} %copy-done.73, f32[2,2,512]{2,1,0:T(2,128)S(1)} %copy-done.65, pred[512,2048]{1,0:T(8,128)(4,1)S(1)} %iota_compare_fusion), kind=kLoop, calls=%fused_computation | loop fusion | flops 25165824 | bytes 43008000 | tf_op jit(solution)/shard_map/convert_element_type | solution.py:145
  560.0 3.5 fusion.60
  565.7 6.1 multiply_reduce_fusion.2
  571.9 4.7 convolution_bitcast_fusion.1
  576.6 9.5 %multiply_convert_fusion.2 = bf16[2,2,512,1024]{3,2,1,0:T(8,128)(2,1)} fusion(f32[2,2,512,1024]{3,2,1,0:T(8,128)} %get-tuple-element.169, f32[2,2,512,1024]{3,2,1,0:T(8,128)} %copy-done.4, f32[2,2,512]{2,1,0:T(2,128)S(1)} %copy-done.70, f32[2,2,512]{2,1,0:T(2,128)S(1)} %copy-done.61, pred[512,1024]{1,0:T(8,128)(4,1)} %copy-done.25), kind=kLoop, calls=%fused_computation.31 | loop fusion | flops 12582912 | bytes 21512192 | tf_op jit(solution)/shard_map/convert_element_type | solution.py:145
  586.6 7.9 fusion.30
  594.6 6.3 add_convert_fusion.1
  611.6 3.9 fusion.61
  628.6 3.5 pad_maximum_fusion.7
  632.1 14.6 %copy.140 = bf16[3,4096,2,64]{3,2,0,1:T(2,128)(2,1)} copy(bf16[3,4096,2,64]{1,3,2,0:T(8,128)(2,1)} %pad_maximum_fusion.7) | data formatting | bytes 6291456 | tf_op jit(solution)/shard_map/stack | solution.py:350
  646.7 8.9 %reshape.443 = bf16[8,2,98304]{2,1,0:T(2,128)(2,1)} reshape(bf16[4096,3,2,64]{3,2,1,0:T(2,128)(2,1)} %bitcast.176) | data formatting | bytes 6291456
  655.6 4.6 all-to-all-start.2
  671.2 7.9 psum.71
  679.7 8.7 %fusion.56 = bf16[3,1024,128]{1,2,0:T(8,128)(2,1)} fusion(bf16[3,4096,128]{1,2,0:T(8,128)(2,1)} %constant_dynamic-update-slice_fusion, bf16[4096,1024]{1,0:T(8,128)(2,1)} %all-gather.8.cloned.1.call-done), kind=kOutput, calls=%fused_computation.147 | convolution fusion | flops 3221618688 | bytes 12320768 | tf_op jit(solution)/shard_map/sd,tse->tde/dot_general | solution.py:362
  688.4 58.6 %all-to-all-done.2 = bf16[8,2,98304]{2,1,0:T(2,128)(2,1)} async-done(((bf16[8,2,98304]{2,1,0:T(2,128)(2,1)}), bf16[8,2,98304]{2,1,0:T(2,128)(2,1)}, u32[]{:S(2)}, u32[]{:S(2)}) %all-to-all-start.2) | async-done | bytes 3145760 | tf_op jit(solution)/shard_map/all_to_all | solution.py:359
  747.1 8.8 %reshape.444 = bf16[4096,3,2,64]{3,2,1,0:T(2,128)(2,1)} reshape(bf16[8,2,98304]{2,1,0:T(2,128)(2,1)} %all-to-all-done.2) | data formatting | bytes 6291456
  755.8 15.3 %copy.157 = bf16[3,8,512,2,64]{2,4,3,1,0:T(8,128)(2,1)} copy(bf16[3,8,512,2,64]{4,3,0,2,1:T(2,128)(2,1)} %bitcast.177) | data formatting | bytes 6291456 | tf_op jit(solution)/shard_map/all_to_all | solution.py:359
  771.1 6.0 broadcast_select_fusion.5
  783.9 9.2 %fusion.45 = (f32[1024]{0:T(1024)S(1)}, f32[512]{0:T(512)S(1)}, f32[512]{0:T(512)S(1)}, f32[1024]{0:T(1024)S(1)}, f32[512,1024,1]{1,0,2:T(8,128)}) fusion(bf16[512,1024]{1,0:T(8,128)(2,1)S(1)} %copy-done.10, f32[512]{0:T(512)S(1)} %copy-done.75, f32[512]{0:T(512)S(1)} %copy-done.72, f32[1024]{0:T(1024)S(1)} %bitcast.193, ...), kind=kOutput, calls=%fused_computation.91 | convolution fusion | flops 3239048192 | bytes 12603392 | tf_op jit(solution)/shard_map/tse,tde->sd/dot_general | solution.py:365
  793.2 42.5 %all-reduce.6 = (f32[1024]{0:T(1024)}, f32[4096]{0:T(1024)S(1)}, f32[1024]{0:T(1024)}, f32[4,1024]{1,0:T(4,128)}, f32[4,1024]{1,0:T(4,128)}) all-reduce(f32[1024]{0:T(1024)S(1)} %copy-done.82, f32[4096]{0:T(1024)S(1)} %copy-done.81, f32[1024]{0:T(1024)S(1)} %copy-done.76, ...), channel_id=1, replica_groups=mesh['wide'=4,'narrow'=8] {'wide','narrow'}, use_global_device_ids=true, to_apply=%region_36.37 | all-reduce | flops 14336 | bytes 114688 | tf_op jit(solution)/shard_map/psum | solution.py:397
  836.4 3.3 fusion.44
  839.7 13.7 %all-reduce.10.cloned.1.call-done = (bf16[3,1024,128]{1,2,0:T(8,128)(2,1)}, bf16[128,1024]{1,0:T(8,128)(2,1)}, bf16[1024,512]{1,0:T(8,128)(2,1)}, bf16[512,1024]{1,0:T(8,128)(2,1)}) async-done(((bf16[3,1024,128]{1,2,0:T(8,128)(2,1)}, bf16[128,1024]{1,0:T(8,128)(2,1)}, bf16[1024,512]{1,0:T(8,128)(2,1)}, bf16[512,1024]{1,0:T(8,128)(2,1)}), (bf16[3,1024,128]{1,2,0:T(8,128)(2,1)}, bf16[128,1024]{1,0:T(8,128)(2,1)}, ...) | async-done | bytes 3145744 | tf_op jit(solution)/shard_map/psum | solution.py:390
  (369 shorter events, 124.5 us)
Async XLA Ops:
  7.2 135.2 %copy-start = (bf16[1024,512]{1,0:T(8,128)(2,1)S(1)}, bf16[1024,512]{1,0:T(8,128)(2,1)}, u32[]{:S(2)}) copy-start(bf16[1024,512]{1,0:T(8,128)(2,1)} %param.22) | copy-start | bytes 3145732
  7.2 136.0 %copy-start.58 = (bf16[512,1024]{1,0:T(8,128)(2,1)S(1)}, bf16[512,1024]{1,0:T(8,128)(2,1)}, u32[]{:S(2)}) copy-start(bf16[512,1024]{1,0:T(8,128)(2,1)} %param.24) | copy-start | bytes 3145732
  7.2 135.1 %all-gather.8.cloned.1.call-start = ((), (), s32[]{:S(2)}) async-start(), calls=%async_computation.5 | async-start | bytes 9437184 | tf_op jit(solution)/shard_map/all_gather | solution.py:271
  9.1 135.1 %copy-start.68 = (f32[1,1024]{1,0:T(1,128)}, f32[1,1024]{1,0:T(1,128)S(1)}, u32[]{:S(2)}) copy-start(f32[1,1024]{1,0:T(1,128)S(1)} %get-tuple-element.141) | copy-start | bytes 12292
  10.5 135.0 %copy-start.71 = (f32[512]{0:T(512)}, f32[512]{0:T(512)S(1)}, u32[]{:S(2)}) copy-start(f32[512]{0:T(512)S(1)} %broadcast_multiply_fusion.11) | copy-start | bytes 6148
  12.2 134.4 %copy-start.74 = (f32[512]{0:T(512)}, f32[512]{0:T(512)S(1)}, u32[]{:S(2)}) copy-start(f32[512]{0:T(512)S(1)} %add_rsqrt_fusion.3) | copy-start | bytes 6148
  14.9 261.1 %all-gather.12.cloned.1.call-start = ((), (), s32[]{:S(2)}) async-start(), calls=%async_computation.7 | async-start | bytes 4718592 | tf_op jit(solution)/shard_map/all_gather | solution.py:181
  143.2 147.8 %all-gather.14.cloned.1.call-start = ((), (), s32[]{:S(2)}) async-start(), calls=%async_computation.8 | async-start | bytes 4718592 | tf_op jit(solution)/shard_map/all_gather | solution.py:181
  144.1 205.9 %all-gather.10.cloned.1.call-start = ((), (), s32[]{:S(2)}) async-start(), calls=%async_computation.6 | async-start | bytes 2359296 | tf_op jit(solution)/shard_map/all_gather | solution.py:282
  144.9 346.6 %copy-start.30 = (pred[512,512]{0,1:T(8,128)(4,1)}, pred[512,512]{0,1:T(8,128)(4,1)S(1)}, u32[]{:S(2)}) copy-start(pred[512,512]{0,1:T(8,128)(4,1)S(1)} %iota_compare_fusion.3) | copy-start | bytes 786436
  146.6 79.6 %copy-start.41 = (f32[2048,32]{0,1:T(8,128)}, f32[2048,32]{0,1:T(8,128)S(1)}, u32[]{:S(2)}) copy-start(f32[2048,32]{0,1:T(8,128)S(1)} %get-tuple-element.147) | copy-start | bytes 786436
  146.6 79.6 %copy-start.43 = (f32[2048,32]{0,1:T(8,128)}, f32[2048,32]{0,1:T(8,128)S(1)}, u32[]{:S(2)}) copy-start(f32[2048,32]{0,1:T(8,128)S(1)} %get-tuple-element.148) | copy-start | bytes 786436
  147.1 107.8 %copy-start.11 = (pred[512,1536]{1,0:T(8,128)(4,1)}, pred[512,1536]{1,0:T(8,128)(4,1)S(1)}, u32[]{:S(2)}) copy-start(pred[512,1536]{1,0:T(8,128)(4,1)S(1)} %iota_compare_fusion.1) | copy-start | bytes 2359300
  147.5 336.2 %copy-start.25 = (pred[512,1024]{1,0:T(8,128)(4,1)}, pred[512,1024]{1,0:T(8,128)(4,1)S(1)}, u32[]{:S(2)}) copy-start(pred[512,1024]{1,0:T(8,128)(4,1)S(1)} %iota_compare_fusion.2) | copy-start | bytes 1572868
  229.2 20.7 %copy-start.21 = (bf16[2,2048,2,32]{1,3,2,0:T(8,128)(2,1)}, bf16[2,2048,2,32]{1,3,2,0:T(8,128)(2,1)S(1)}, u32[]{:S(2)}) copy-start(bf16[2,2048,2,32]{1,3,2,0:T(8,128)(2,1)S(1)} %get-tuple-element.120) | copy-start | bytes 1572868
  229.2 20.7 %copy-start.23 = (bf16[2,2048,2,32]{1,3,2,0:T(8,128)(2,1)}, bf16[2,2048,2,32]{1,3,2,0:T(8,128)(2,1)S(1)}, u32[]{:S(2)}) copy-start(bf16[2,2048,2,32]{1,3,2,0:T(8,128)(2,1)S(1)} %get-tuple-element.121) | copy-start | bytes 1572868
  229.2 38.4 %copy-start.16 = (bf16[2,2048,2,32]{1,3,2,0:T(8,128)(2,1)}, bf16[2,2048,2,32]{1,3,2,0:T(8,128)(2,1)S(1)}, u32[]{:S(2)}) copy-start(bf16[2,2048,2,32]{1,3,2,0:T(8,128)(2,1)S(1)} %get-tuple-element.137) | copy-start | bytes 1572868
  229.2 38.4 %copy-start.18 = (bf16[2,2048,2,32]{1,3,2,0:T(8,128)(2,1)}, bf16[2,2048,2,32]{1,3,2,0:T(8,128)(2,1)S(1)}, u32[]{:S(2)}) copy-start(bf16[2,2048,2,32]{1,3,2,0:T(8,128)(2,1)S(1)} %get-tuple-element.138) | copy-start | bytes 1572868
  229.3 38.4 %copy-start.39 = (bf16[2,512,2,64]{1,3,2,0:T(8,128)(2,1)}, bf16[2,512,2,64]{1,3,2,0:T(8,128)(2,1)S(1)}, u32[]{:S(2)}) copy-start(bf16[2,512,2,64]{1,3,2,0:T(8,128)(2,1)S(1)} %get-tuple-element.176) | copy-start | bytes 786436
  232.6 38.9 %copy-start.2 = (f32[2,2,512,2048]{3,2,1,0:T(8,128)}, f32[2,2,512,2048]{3,2,1,0:T(8,128)S(1)}, u32[]{:S(2)}) copy-start(f32[2,2,512,2048]{3,2,1,0:T(8,128)S(1)} %get-tuple-element.150) | copy-start | bytes 50331652
  237.1 34.4 %copy-start.64 = (f32[2,2,512]{2,1,0:T(2,128)}, f32[2,2,512]{2,1,0:T(2,128)S(1)}, u32[]{:S(2)}) copy-start(f32[2,2,512]{2,1,0:T(2,128)S(1)} %log_add_fusion) | copy-start | bytes 24580
  254.9 228.7 %copy-start.59 = (f32[2,2,512]{2,1,0:T(2,128)}, f32[2,2,512]{2,1,0:T(2,128)S(1)}, u32[]{:S(2)}) copy-start(f32[2,2,512]{2,1,0:T(2,128)S(1)} %log_add_fusion.2) | copy-start | bytes 24580
  271.5 220.0 %copy-start.62 = (f32[2,2,512]{2,1,0:T(2,128)}, f32[2,2,512]{2,1,0:T(2,128)S(1)}, u32[]{:S(2)}) copy-start(f32[2,2,512]{2,1,0:T(2,128)S(1)} %log_add_fusion.3) | copy-start | bytes 24580
  276.0 78.9 %collective-permute-start = (bf16[512,4096]{1,0:T(8,128)(2,1)}, bf16[512,4096]{1,0:T(8,128)(2,1)}, u32[]{:S(2)}, u32[]{:S(2)}) collective-permute-start(bf16[512,4096]{1,0:T(8,128)(2,1)} %all-gather.12.cloned.1.call-done), channel_id=1, source_target_pairs={{0,8},{8,0},{16,24},{24,16},{1,9},{9,1},{17,25},{25,17},{2,10},{10... | collective-permute-start | bytes 12582920 | tf_op jit(solution)/shard_map/ppermute | solution.py:175
  279.8 9.2 %copy-start.87 = (s32[2]{0:T(128)S(1)}, s32[2]{0:T(128)}, u32[]{:S(2)}) copy-start(s32[2]{0:T(128)} %param.16) | copy-start | bytes 28
  279.8 9.3 %copy-start.88 = (f32[8]{0:T(128)S(1)}, f32[8]{0:T(128)}, u32[]{:S(2)}) copy-start(f32[8]{0:T(128)} %param.17) | copy-start | bytes 100
  279.8 70.2 %copy-start.57 = (f32[1024]{0:T(1024)S(1)}, f32[1024]{0:T(1024)}, u32[]{:S(2)}) copy-start(f32[1024]{0:T(1024)} %param.21) | copy-start | bytes 12292
  284.6 65.5 %all-to-all-start = ((bf16[8,512,128]{1,2,0:T(8,128)(2,1)}), bf16[8,512,128]{1,2,0:T(8,128)(2,1)}, u32[]{:S(2)}, u32[]{:S(2)}) async-start(bf16[8,512,128]{1,2,0:T(8,128)(2,1)} %copy.126), calls=%async_computation | async-start | bytes 2097152 | tf_op jit(solution)/shard_map/all_to_all | solution.py:281
  289.0 64.7 %copy-start.9 = (bf16[512,1024]{1,0:T(8,128)(2,1)S(1)}, bf16[512,1024]{1,0:T(8,128)(2,1)}, u32[]{:S(2)}) copy-start(bf16[512,1024]{1,0:T(8,128)(2,1)} %param.14) | copy-start | bytes 3145732
  291.0 79.0 %collective-permute-start.1 = (bf16[4096,512]{1,0:T(8,128)(2,1)}, bf16[4096,512]{1,0:T(8,128)(2,1)}, u32[]{:S(2)}, u32[]{:S(2)}) collective-permute-start(bf16[4096,512]{1,0:T(8,128)(2,1)} %all-gather.14.cloned.1.call-done), channel_id=1, source_target_pairs={{0,8},{8,0},{16,24},{24,16},{1,9},{9,1},{17,25},{25,17},{2,10},{10... | collective-permute-start | bytes 12582920 | tf_op jit(solution)/shard_map/ppermute | solution.py:175
  359.8 10.2 %copy-start.35 = (bf16[4096,512]{1,0:T(8,128)(2,1)S(1)}, bf16[4096,512]{1,0:T(8,128)(2,1)}, u32[]{:S(2)}) copy-start(bf16[4096,512]{1,0:T(8,128)(2,1)} %all-gather.14.cloned.1.call-done) | copy-start | bytes 12582916
  375.1 9.7 %copy-start.32 = (bf16[512,1024]{1,0:T(8,128)(2,1)S(1)}, bf16[512,1024]{1,0:T(8,128)(2,1)}, u32[]{:S(2)}) copy-start(bf16[512,1024]{1,0:T(8,128)(2,1)} %param.15) | copy-start | bytes 3145732
  438.0 41.0 %all-to-all-start.1 = ((bf16[512,8,128]{0,2,1:T(8,128)(2,1)}), bf16[512,8,128]{0,2,1:T(8,128)(2,1)S(1)}, u32[]{:S(2)}, u32[]{:S(2)}) async-start(bf16[512,8,128]{0,2,1:T(8,128)(2,1)} %bitcast.183), calls=%async_computation.1 | async-start | bytes 2097152 | tf_op jit(solution)/shard_map/all_to_all | solution.py:341
  441.6 218.8 %all-gather.16.cloned.1.call-start = ((), (), s32[]{:S(2)}) async-start(), calls=%async_computation.9 | async-start | bytes 3538944 | tf_op jit(solution)/shard_map/all_gather | solution.py:181
  443.4 333.7 %reduce-scatter.5.cloned.1.call-start = ((), (), s32[]{:S(2)}) async-start(), calls=%async_computation.11 | async-start | bytes 4718592 | tf_op jit(solution)/shard_map/reduce_scatter | solution.py:200
  446.4 12.7 %collective-permute-start.4 = (bf16[1024,512]{1,0:T(8,128)(2,1)S(1)}, bf16[1024,512]{1,0:T(8,128)(2,1)S(1)}, u32[]{:S(2)}, u32[]{:S(2)}) collective-permute-start(bf16[1024,512]{1,0:T(8,128)(2,1)S(1)} %dynamic-slice_convert_fusion.2), channel_id=1, source_target_pairs={{0,8},{8,0},{16,24},{24,16},{1,9},{9,1},{17,25},{25,17},{2,10},{10... | collective-permute-start | bytes 3145736 | tf_op jit(solution)/shard_map/ppermute | solution.py:175
  452.4 142.2 %collective-permute-start.3 = (bf16[4096,512]{1,0:T(8,128)(2,1)}, bf16[4096,512]{1,0:T(8,128)(2,1)}, u32[]{:S(2)}, u32[]{:S(2)}) collective-permute-start(bf16[4096,512]{1,0:T(8,128)(2,1)} %dynamic-slice_convert_fusion.1), channel_id=1, source_target_pairs={{0,8},{8,0},{16,24},{24,16},{1,9},{9,1},{17,25},{25,17},{2,10},{10... | collective-permute-start | bytes 12582920 | tf_op jit(solution)/shard_map/ppermute | solution.py:175
  459.1 70.2 %collective-permute-start.5 = (bf16[512,4096]{1,0:T(8,128)(2,1)}, bf16[512,4096]{1,0:T(8,128)(2,1)}, u32[]{:S(2)}, u32[]{:S(2)}) collective-permute-start(bf16[512,4096]{1,0:T(8,128)(2,1)} %dynamic-slice_convert_fusion), channel_id=1, source_target_pairs={{0,8},{8,0},{16,24},{24,16},{1,9},{9,1},{17,25},{25,17},{2,10},{10... | collective-permute-start | bytes 12582920 | tf_op jit(solution)/shard_map/ppermute | solution.py:175
  483.6 10.4 %copy-start.47 = (bf16[2,512,2,64]{1,0,3,2:T(2,128)(2,1)}, bf16[2,512,2,64]{1,0,3,2:T(2,128)(2,1)S(1)}, u32[]{:S(2)}) copy-start(bf16[2,512,2,64]{1,0,3,2:T(2,128)(2,1)S(1)} %get-tuple-element.126) | copy-start | bytes 786436
  491.5 14.4 %slice-start = ((s8[16777216]{0:T(1024)(128)(4,1)}), s8[4194304]{0:T(1024)(128)(4,1)S(1)}, s32[]{:S(2)}) async-start(s8[16777216]{0:T(1024)(128)(4,1)} %bitcast.164), calls=%async_computation.13 | async-start | bytes 8388608
  491.5 14.4 %slice-start.1 = ((s8[16777216]{0:T(1024)(128)(4,1)}), s8[4194304]{0:T(1024)(128)(4,1)S(1)}, s32[]{:S(2)}) async-start(s8[16777216]{0:T(1024)(128)(4,1)} %bitcast.164), calls=%async_computation.14 | async-start | bytes 8388608
  494.1 11.8 %slice-start.2 = ((s8[16777216]{0:T(1024)(128)(4,1)}), s8[4194304]{0:T(1024)(128)(4,1)S(1)}, s32[]{:S(2)}) async-start(s8[16777216]{0:T(1024)(128)(4,1)} %bitcast.164), calls=%async_computation.15 | async-start | bytes 8388608
  494.1 11.8 %slice-start.3 = ((s8[16777216]{0:T(1024)(128)(4,1)}), s8[4194304]{0:T(1024)(128)(4,1)S(1)}, s32[]{:S(2)}) async-start(s8[16777216]{0:T(1024)(128)(4,1)} %bitcast.164), calls=%async_computation.16 | async-start | bytes 8388608
  537.4 242.1 %reduce-scatter.3.cloned.1.call-start = ((), (), s32[]{:S(2)}) async-start(), calls=%async_computation.10 | async-start | bytes 5898240 | tf_op jit(solution)/shard_map/reduce_scatter | solution.py:218
  538.6 27.0 %slice-start.13 = ((s8[8388608]{0:T(1024)(128)(4,1)}), s8[4194304]{0:T(1024)(128)(4,1)S(1)}, s32[]{:S(2)}) async-start(s8[8388608]{0:T(1024)(128)(4,1)} %bitcast.172), calls=%async_computation.26 | async-start | bytes 8388608
  544.3 21.3 %slice-start.14 = ((s8[8388608]{0:T(1024)(128)(4,1)}), s8[4194304]{0:T(1024)(128)(4,1)S(1)}, s32[]{:S(2)}) async-start(s8[8388608]{0:T(1024)(128)(4,1)} %bitcast.172), calls=%async_computation.27 | async-start | bytes 8388608
  571.9 14.3 %slice-start.4 = ((s8[16777216]{0:T(1024)(128)(4,1)}), s8[4194304]{0:T(1024)(128)(4,1)S(1)}, s32[]{:S(2)}) async-start(s8[16777216]{0:T(1024)(128)(4,1)} %bitcast.166), calls=%async_computation.17 | async-start | bytes 8388608
  571.9 14.3 %slice-start.5 = ((s8[16777216]{0:T(1024)(128)(4,1)}), s8[4194304]{0:T(1024)(128)(4,1)S(1)}, s32[]{:S(2)}) async-start(s8[16777216]{0:T(1024)(128)(4,1)} %bitcast.166), calls=%async_computation.18 | async-start | bytes 8388608
  576.6 9.6 %slice-start.6 = ((s8[16777216]{0:T(1024)(128)(4,1)}), s8[4194304]{0:T(1024)(128)(4,1)S(1)}, s32[]{:S(2)}) async-start(s8[16777216]{0:T(1024)(128)(4,1)} %bitcast.166), calls=%async_computation.19 | async-start | bytes 8388608
  576.6 10.0 %slice-start.7 = ((s8[16777216]{0:T(1024)(128)(4,1)}), s8[4194304]{0:T(1024)(128)(4,1)S(1)}, s32[]{:S(2)}) async-start(s8[16777216]{0:T(1024)(128)(4,1)} %bitcast.166), calls=%async_computation.20 | async-start | bytes 8388608
  576.6 10.0 %copy-start.66 = (f32[2,2,512]{2,1,0:T(2,128)S(1)}, f32[2,2,512]{2,1,0:T(2,128)}, u32[]{:S(2)}) copy-start(f32[2,2,512]{2,1,0:T(2,128)} %copy-done.64) | copy-start | bytes 24580
  655.6 91.4 %all-to-all-start.2 = ((bf16[8,2,98304]{2,1,0:T(2,128)(2,1)}), bf16[8,2,98304]{2,1,0:T(2,128)(2,1)}, u32[]{:S(2)}, u32[]{:S(2)}) async-start(bf16[8,2,98304]{2,1,0:T(2,128)(2,1)} %reshape.443), calls=%async_computation.2 | async-start | bytes 6291456 | tf_op jit(solution)/shard_map/all_to_all | solution.py:359
  660.3 193.1 %all-reduce.10.cloned.1.call-start = ((), (), s32[]{:S(2)}) async-start(), calls=%async_computation.12 | async-start | bytes 6291456 | tf_op jit(solution)/shard_map/psum | solution.py:390
  660.3 110.8 %collective-permute-start.2 = (bf16[3,512,1024]{2,1,0:T(8,128)(2,1)}, bf16[3,512,1024]{2,1,0:T(8,128)(2,1)}, u32[]{:S(2)}, u32[]{:S(2)}) collective-permute-start(bf16[3,512,1024]{2,1,0:T(8,128)(2,1)} %all-gather.16.cloned.1.call-done), channel_id=1, source_target_pairs={{0,8},{8,0},{16,24},{24,16},{1,9},{9,1},{17,25},{25,17},{2,10},{10... | collective-permute-start | bytes 9437192 | tf_op jit(solution)/shard_map/ppermute | solution.py:175
  783.8 9.3 %copy-start.78 = (f32[1024]{0:T(1024)S(1)}, f32[1024]{0:T(1024)}, u32[]{:S(2)}) copy-start(f32[1024]{0:T(1024)} %get-tuple-element.72) | copy-start | bytes 12292
  783.8 9.3 %copy-start.80 = (f32[1024]{0:T(1024)S(1)}, f32[1024]{0:T(1024)}, u32[]{:S(2)}) copy-start(f32[1024]{0:T(1024)} %get-tuple-element.76) | copy-start | bytes 12292
  783.8 9.3 %copy-start.84 = (f32[1024]{0:T(1024)S(1)}, f32[1024]{0:T(1024)}, u32[]{:S(2)}) copy-start(f32[1024]{0:T(1024)} %get-tuple-element.74) | copy-start | bytes 12292
  783.8 9.3 %copy-start.77 = (f32[1024]{0:T(1024)S(1)}, f32[1024]{0:T(1024)}, u32[]{:S(2)}) copy-start(f32[1024]{0:T(1024)} %get-tuple-element.84) | copy-start | bytes 12292
  783.8 9.3 %copy-start.79 = (f32[1024]{0:T(1024)S(1)}, f32[1024]{0:T(1024)}, u32[]{:S(2)}) copy-start(f32[1024]{0:T(1024)} %get-tuple-element.87) | copy-start | bytes 12292
  783.8 9.3 %copy-start.83 = (f32[1024]{0:T(1024)S(1)}, f32[1024]{0:T(1024)}, u32[]{:S(2)}) copy-start(f32[1024]{0:T(1024)} %get-tuple-element.85) | copy-start | bytes 12292
  783.8 9.3 %copy-start.76 = (f32[1024]{0:T(1024)S(1)}, f32[1024]{0:T(1024)}, u32[]{:S(2)}) copy-start(f32[1024]{0:T(1024)} %get-tuple-element.97) | copy-start | bytes 12292
  783.8 9.3 %copy-start.81 = (f32[4096]{0:T(1024)S(1)}, f32[4096]{0:T(1024)}, u32[]{:S(2)}) copy-start(f32[4096]{0:T(1024)} %get-tuple-element.173) | copy-start | bytes 49156
  783.9 9.3 %copy-start.82 = (f32[1024]{0:T(1024)S(1)}, f32[1024]{0:T(1024)}, u32[]{:S(2)}) copy-start(f32[1024]{0:T(1024)} %get-tuple-element.99) | copy-start | bytes 12292
  783.9 52.5 %copy-start.15 = (f32[512,1024]{1,0:T(8,128)S(1)}, f32[512,1024]{1,0:T(8,128)}, u32[]{:S(2)}) copy-start(f32[512,1024]{1,0:T(8,128)} %copy-done.14) | copy-start | bytes 6291460
  (60 other events, 238.0 us)
Sparse Core Ops, SparseCore 0:
  15.0 127.3 all-gather.7
  145.0 72.8 all-gather.11
  220.0 70.9 all-gather.13
  292.9 57.0 all-gather.9
  444.1 71.1 all-gather.15
  537.5 86.4 reduce-scatter.4
  627.6 151.8 reduce-scatter.2
  783.8 69.4 all-reduce.9

commit v15 on v14

--- a/solution.py
+++ b/solution.py
@@ -356,9 +356,7 @@
     )
     qkv_grad = qkv_grad.reshape(3, group_rows, inner).astype(jnp.bfloat16)
     qkv_bgrad = jnp.sum(qkv_grad.astype(jnp.float32), axis=1)
-    qkv_grad_rows = lax.all_to_all(
-        qkv_grad.reshape(3, group_rows, heads_here, HEAD), "narrow", 1, 2, tiled=True
-    ).reshape(3, shard_rows, model)
+    qkv_grad_rows = lax.all_to_all(qkv_grad, "narrow", 1, 2, tiled=True)
     qkv_wgrad = jnp.einsum(
         "sd,tse->tde", gathered_first, qkv_grad, preferred_element_type=jnp.float32
     )

time: 876 us -> 906 us (1.034)
  waiting for transfers between devices: 247 us -> 312 us
  local copies, waits for them, and re-layouts: 184 us -> 154 us
  other arithmetic: 130 us -> 114 us
    all_to_all x1, waiting for transfers between devices: 58.6 us -> 106 us  [shards(): qkv_grad_rows = lax.all_to_all(qkv_grad, 'narrow', 1, 2, tiled=True)]
    unnamed x227 -> x211, local copies, waits for them, and re-layouts: 63.9 us -> 44.8 us
    convert_element_type x4, other arithmetic: 36.5 us -> 21.8 us  [attend_backward(): scores_grad = (probs_full * (probs_grad - row_dot)).astype(jnp.bfloat16)]
    reduce_scatter x1, waiting for transfers between devices: 0.3 us -> 12.1 us  [reduce_column_halves(): lax.psum_scatter(jnp.concatenate(pieces, axis=1), 'narrow', scatter_dimen...]
    another operation x8 -> x5, local copies, waits for them, and re-layouts: 23.8 us -> 13.4 us  [shards(): jnp.stack([rotate_back(query_grad, cos_table, sine_table), rotate_back(ke...]
  transfers between devices with their start and end apart: 17 -> 17, of which waited for: 7 -> 7; matrix products, arithmetic and copies ran while one was open for 47% -> 40% of each run, Pallas kernels for 0% -> 0%
where the time goes in v15:
time: 906 us; the launch traced here: 894 us
  waiting for transfers between devices  312 us (34%)
  matrix products  201 us (22%)
  local copies, waits for them, and re-layouts  154 us (17%)
  other arithmetic  114 us (13%)
  blocking collectives  83.8 us (9%)
  between operations  15.8 us (2%)
  starting transfers between devices  14.4 us (2%)
    all_to_all x1, waiting for transfers between devices, shards(): qkv_grad_rows = lax.all_to_all(qkv_grad, 'narrow', 1, 2, tiled=True)  106 us
    all_gather x1, waiting for transfers between devices, shards(): gathered_first = lax.all_gather(low_first, 'narrow', axis=0, tiled=True)  93.8 us
    all_gather x1, waiting for transfers between devices, shards(): out_full = lax.all_gather(out_weight, 'narrow', axis=0, tiled=True)  56.4 us
    unnamed x211, local copies, waits for them, and re-layouts  44.8 us
    psum x1, blocking collectives, shards(): lax.psum((gain_local, bias_local, out_blocal, down_blocal, up_bgrad_rows)...  42.5 us
    dot_general x4, matrix products, attend_backward(): jnp.einsum('bqhd,bkhd->bhqk', grad_block, value_block, preferred_element_...  34.7 us
    all_gather x1, blocking collectives, shards(): bias_full = lax.all_gather(bias_flat, 'narrow', axis=0)  33.5 us
    dot_general x4, matrix products, attend_backward(): jnp.einsum('bhqk,bqhd->bkhd', probs_low, grad_block, preferred_element_ty...  25.1 us
  transfers between devices with their start and end apart: 17, of which 7 were waited for; matrix products, arithmetic and copies ran while one was open for 40% of the time, Pallas kernels for 0%

profile of v15, /device:TPU:0, one launch (start us, length us, event | category | flops | bytes accessed | tf_op | source)
XLA Modules:
  0.0 894.5 jit_solution(2962395490089792207)
XLA Ops:
  15.0 33.5 %all-gather.1 = f32[8,1,896]{2,1,0:T(1,128)S(1)} all-gather(f32[1,1,896]{2,1,0:T(1,128)S(1)} %reshape.420), channel_id=2, replica_groups=mesh['wide'=4,'narrow'=8] {'narrow'}, dimensions={0}, use_global_device_ids=true | all-gather | bytes 32256 | tf_op jit(solution)/shard_map/all_gather | solution.py:270
  48.5 93.8 %all-gather.8.cloned.1.call-done = bf16[4096,1024]{1,0:T(8,128)(2,1)} async-done(((bf16[512,1024]{1,0:T(8,128)(2,1)}), bf16[4096,1024]{1,0:T(8,128)(2,1)}) %all-gather.8.cloned.1.call-update) | async-done | bytes 8388624 | tf_op jit(solution)/shard_map/all_gather | solution.py:271
  149.0 7.6 add_bitcast_fusion
  159.9 5.6 reshape.426
  165.5 9.9 %fusion.131 = (f32[2,2048,2,32]{3,2,1,0:T(2,128)}, f32[2,2048,2,32]{3,2,1,0:T(2,128)}) fusion(f32[2,2048,2,64]{3,2,1,0:T(2,128)} %reshape.426), kind=kLoop, calls=%fused_computation.277 | loop fusion | bytes 4194304 | tf_op jit(solution)/shard_map/slice | solution.py:41
  175.4 6.5 copy.149
  181.9 6.4 copy.150
  188.3 5.6 reshape.427
  193.9 9.8 %fusion.130 = (f32[2,2048,2,32]{3,2,1,0:T(2,128)}, f32[2,2048,2,32]{3,2,1,0:T(2,128)}) fusion(f32[2,2048,2,64]{3,2,1,0:T(2,128)} %reshape.427), kind=kLoop, calls=%fused_computation.276 | loop fusion | bytes 4194304 | tf_op jit(solution)/shard_map/slice | solution.py:41
  203.8 6.4 copy.151
  210.2 6.7 copy.152
  225.6 5.0 reshape.425
  230.6 5.9 copy.106
  244.3 3.5 exponential_reduce_fusion.1
  247.9 3.2 fusion.64
  251.1 4.3 fusion.66
  255.4 3.2 fusion
  258.6 4.3 exponential_reduce_fusion
  264.4 5.5 fusion.67
  269.9 3.4 fusion.65
  278.2 4.5 all-to-all-start
  282.9 10.8 %all-gather.14.cloned.1.call-done = bf16[4096,512]{1,0:T(8,128)(2,1)} async-done(((bf16[512,512]{1,0:T(8,128)(2,1)}), bf16[4096,512]{1,0:T(8,128)(2,1)}) %all-gather.14.cloned.1.call-update) | async-done | bytes 4194320 | tf_op jit(solution)/shard_map/all_gather | solution.py:181
  293.7 56.4 %all-gather.10.cloned.1.call-done = bf16[1024,1024]{1,0:T(8,128)(2,1)} async-done(((bf16[128,1024]{1,0:T(8,128)(2,1)}), bf16[1024,1024]{1,0:T(8,128)(2,1)}) %all-gather.10.cloned.1.call-update) | async-done | bytes 2097168 | tf_op jit(solution)/shard_map/all_gather | solution.py:282
  350.1 3.3 add_reduce_fusion.1
  356.0 3.9 broadcast_select_fusion.3
  359.9 10.2 %multiply_convert_fusion.3 = (bf16[512,4096]{1,0:T(8,128)(2,1)}, f32[512,4096]{1,0:T(8,128)}) fusion(f32[4096]{0:T(1024)S(1)} %bitcast.191, bf16[512,4096]{1,0:T(8,128)(2,1)} %get-tuple-element.107, bf16[512,4096]{1,0:T(8,128)(2,1)S(1)} %get-tuple-element.106, f32[512,1024]{1,0:T(8,128)S(1)} %get-tuple-element.103, f32[1024]{0:T(1024)S(1)} %bitcast.195, ...), kind=kOutput, calls=%fused_computation.33 | convolution fusion | flops 4326948864 | bytes 23097344 | tf_op jit(solution)/shard_map/dot_general | solution.py:290
  370.2 5.1 broadcast_select_fusion.1
  375.3 9.3 %add_reduce_fusion = (f32[512]{0:T(512)S(1)}, f32[512,1024]{1,0:T(8,128)S(1)}) fusion(f32[1024]{0:T(1024)S(1)} %copy-done.68, bf16[512,4096]{1,0:T(8,128)(2,1)} %get-tuple-element.21, bf16[4096,512]{1,0:T(8,128)(2,1)} %get-tuple-element.105, bf16[4096,512]{1,0:T(8,128)(2,1)} %get-tuple-element.104), kind=kOutput, calls=%fused_computation.127 | convolution fusion | flops 4312792576 | bytes 14686208 | tf_op jit(solution)/shard_map/dot_general | solution.py:294
  389.4 8.6 fusion.135
  398.0 12.6 %convert_reduce_fusion = (f32[4096]{0:T(1024)}, bf16[512,4096]{1,0:T(8,128)(2,1)}) fusion(f32[512,4096]{1,0:T(8,128)} %get-tuple-element.160, f32[4096]{0:T(1024)S(1)} %bitcast.192, bf16[512,1024]{1,0:T(8,128)(2,1)S(1)} %get-tuple-element.98, bf16[4096,512]{1,0:T(8,128)(2,1)} %get-tuple-element.105, bf16[4096,512]{1,0:T(8,128)(2,1)} %get-tuple-element.104), kind=kOutput, calls=%fused_computation.26 | convolution fusion | flops 4339003392 | bytes 22052864 | tf_op jit(solution)/shard_map/dot_general | solution.py:322
  410.6 9.1 %multiply_reduce_fusion.5 = (f32[1024]{0:T(1024)}, f32[512]{0:T(512)S(1)}, f32[512]{0:T(512)S(1)}, f32[1024]{0:T(1024)}, f32[512,1024]{1,0:T(8,128)}) fusion(f32[512,1024]{1,0:T(8,128)S(1)} %get-tuple-element.103, f32[512]{0:T(512)S(1)} %add_rsqrt_fusion.1, f32[512]{0:T(512)S(1)} %broadcast_multiply_fusion.9, f32[1024]{0:T(1024)S(1)} %bitcast.181, ...), kind=kOutput, calls=%fused_computation.99 | convolution fusion | flops 4316460032 | bytes 16797696 | tf_op jit(solution)/shard_map/dot_general | solution.py:330
  419.6 10.6 %fusion.126 = f32[1024,4096]{1,0:T(8,128)} fusion(bf16[512,4096]{1,0:T(8,128)(2,1)} %get-tuple-element.174, f32[512,1024]{1,0:T(8,128)S(1)} %get-tuple-element.103, f32[1024]{0:T(1024)S(1)} %bitcast.196, f32[1024]{0:T(1024)S(1)} %bitcast.182, f32[512]{0:T(512)S(1)} %add_rsqrt_fusion.1, f32[512]{0:T(512)S(1)} %broadcast_multiply_fusion.9), kind=kOutput, calls=%fused_computation.273 | convolution fusion | flops 4297588736 | bytes 23080960 | tf_op jit(solution)/shard_map/dot_general | solution.py:327
  438.5 4.3 all-to-all-start.1
  447.7 6.0 dynamic-slice_convert_fusion.1
  454.1 6.1 dynamic-slice_convert_fusion
  461.8 18.2 %all-to-all-done.1 = bf16[512,8,128]{0,2,1:T(8,128)(2,1)} async-done(((bf16[512,8,128]{0,2,1:T(8,128)(2,1)}), bf16[512,8,128]{0,2,1:T(8,128)(2,1)}, u32[]{:S(2)}, u32[]{:S(2)}) %all-to-all-start.1) | async-done | bytes 1048608 | tf_op jit(solution)/shard_map/all_to_all | solution.py:341
  487.9 3.9 multiply_reduce_fusion.3
  491.9 7.8 multiply_reduce_fusion.2
  500.2 4.8 multiply_convert_fusion.2
  513.0 7.1 multiply_reduce_fusion.1
  520.1 7.3 multiply_convert_fusion.1
  533.0 8.0 add_convert_fusion
  542.0 4.2 convolution_bitcast_fusion.3
  546.2 5.7 convolution_bitcast_fusion.2
  552.0 15.8 %multiply_reduce_fusion = (f32[2,2,512]{2,1,0:T(2,128)}, f32[2,2,512,2048]{3,2,1,0:T(8,128)}) fusion(f32[2,2,512,2048]{3,2,1,0:T(8,128)} %copy-done.2, f32[2,2,512]{2,1,0:T(2,128)} %copy-done.67, pred[512,2048]{1,0:T(8,128)(4,1)S(1)} %copy-done.11, bf16[2,2048,2,64]{1,3,2,0:T(8,128)(2,1)} %copy.106, bf16[2,512,2,64]{1,0,3,2:T(2,128)(2,1)} %get-tuple-element.128), kind=kOutput, calls=%fused_computation.1 | convolution fusion | flops 557840384 | bytes 35930112 | tf_op jit(solution)/shard_map/bqhd,bkhd->bhqk/dot_general | solution.py:141
  569.2 8.4 multiply_convert_fusion
  577.6 5.6 fusion.60
  583.2 7.5 convolution_bitcast_fusion.1
  590.7 7.7 fusion.30
  598.5 6.2 add_convert_fusion.1
  617.4 4.2 fusion.26
  635.4 7.3 copy.132
  642.7 4.6 all-to-all-start.2
  649.8 7.8 psum.71
  658.1 8.7 fusion.56
  666.9 106.1 %all-to-all-done.2 = bf16[3,4096,128]{2,0,1:T(4,128)(2,1)} async-done(((bf16[3,4096,128]{2,0,1:T(4,128)(2,1)}), bf16[3,4096,128]{2,0,1:T(4,128)(2,1)}, u32[]{:S(2)}, u32[]{:S(2)}) %all-to-all-start.2) | async-done | bytes 3145760 | tf_op jit(solution)/shard_map/all_to_all | solution.py:359
  773.0 6.4 copy.186
  779.4 5.9 all_to_all.46
  785.2 5.9 broadcast_select_fusion.5
  793.3 12.1 %reduce-scatter.3.cloned.1.call-done = bf16[1,640,512]{2,1,0:T(8,128)(2,1)} async-done(((bf16[8,640,512]{2,1,0:T(8,128)(2,1)}), bf16[1,640,512]{2,1,0:T(8,128)(2,1)}) %reduce-scatter.3.cloned.1.call-update) | async-done | bytes 655376 | tf_op jit(solution)/shard_map/reduce_scatter | solution.py:218
  809.7 9.0 %fusion.45 = (f32[1024]{0:T(1024)S(1)}, f32[512]{0:T(512)S(1)}, f32[512]{0:T(512)S(1)}, f32[1024]{0:T(1024)S(1)}, f32[512,1024,1]{1,0,2:T(8,128)}) fusion(bf16[512,1024]{1,0:T(8,128)(2,1)S(1)} %copy-done.13, f32[512]{0:T(512)S(1)} %copy-done.74, f32[512]{0:T(512)S(1)} %copy-done.72, f32[1024]{0:T(1024)S(1)} %bitcast.178, ...), kind=kOutput, calls=%fused_computation.91 | convolution fusion | flops 3239048192 | bytes 12603392 | tf_op jit(solution)/shard_map/tse,tde->sd/dot_general | solution.py:363
  818.9 42.5 %all-reduce.6 = (f32[1024]{0:T(1024)}, f32[4096]{0:T(1024)S(1)}, f32[1024]{0:T(1024)}, f32[4,1024]{1,0:T(4,128)}, f32[4,1024]{1,0:T(4,128)}) all-reduce(f32[1024]{0:T(1024)S(1)} %copy-done.81, f32[4096]{0:T(1024)S(1)} %copy-done.80, f32[1024]{0:T(1024)S(1)} %copy-done.75, ...), channel_id=1, replica_groups=mesh['wide'=4,'narrow'=8] {'wide','narrow'}, use_global_device_ids=true, to_apply=%region_36.37 | all-reduce | flops 14336 | bytes 114688 | tf_op jit(solution)/shard_map/psum | solution.py:395
  862.1 3.3 fusion.44
  865.4 13.8 %all-reduce.10.cloned.1.call-done = (bf16[3,1024,128]{1,2,0:T(8,128)(2,1)}, bf16[128,1024]{1,0:T(8,128)(2,1)}, bf16[1024,512]{1,0:T(8,128)(2,1)}, bf16[512,1024]{1,0:T(8,128)(2,1)}) async-done(((bf16[3,1024,128]{1,2,0:T(8,128)(2,1)}, bf16[128,1024]{1,0:T(8,128)(2,1)}, bf16[1024,512]{1,0:T(8,128)(2,1)}, bf16[512,1024]{1,0:T(8,128)(2,1)}), (bf16[3,1024,128]{1,2,0:T(8,128)(2,1)}, bf16[128,1024]{1,0:T(8,128)(2,1)}, ...) | async-done | bytes 3145744 | tf_op jit(solution)/shard_map/psum | solution.py:388
  (348 shorter events, 131.6 us)
Async XLA Ops:
  7.2 135.2 %copy-start = (bf16[1024,512]{1,0:T(8,128)(2,1)S(1)}, bf16[1024,512]{1,0:T(8,128)(2,1)}, u32[]{:S(2)}) copy-start(bf16[1024,512]{1,0:T(8,128)(2,1)} %param.22) | copy-start | bytes 3145732
  7.2 7.7 copy-start.85
  7.2 7.7 copy-start.84
  7.2 136.0 %copy-start.62 = (bf16[512,1024]{1,0:T(8,128)(2,1)S(1)}, bf16[512,1024]{1,0:T(8,128)(2,1)}, u32[]{:S(2)}) copy-start(bf16[512,1024]{1,0:T(8,128)(2,1)} %param.24) | copy-start | bytes 3145732
  7.2 135.1 %all-gather.8.cloned.1.call-start = ((), (), s32[]{:S(2)}) async-start(), calls=%async_computation.5 | async-start | bytes 9437184 | tf_op jit(solution)/shard_map/all_gather | solution.py:271
  8.2 135.9 %copy-start.69 = (f32[1,1024]{1,0:T(1,128)}, f32[1,1024]{1,0:T(1,128)S(1)}, u32[]{:S(2)}) copy-start(f32[1,1024]{1,0:T(1,128)S(1)} %get-tuple-element.141) | copy-start | bytes 12292
  9.6 137.7 %copy-start.71 = (f32[512]{0:T(512)}, f32[512]{0:T(512)S(1)}, u32[]{:S(2)}) copy-start(f32[512]{0:T(512)S(1)} %broadcast_multiply_fusion.11) | copy-start | bytes 6148
  11.3 137.0 %copy-start.73 = (f32[512]{0:T(512)}, f32[512]{0:T(512)S(1)}, u32[]{:S(2)}) copy-start(f32[512]{0:T(512)S(1)} %add_rsqrt_fusion.3) | copy-start | bytes 6148
  14.9 134.1 %copy-start.66 = (bf16[3,1024,128]{2,1,0:T(8,128)(2,1)S(1)}, bf16[3,1024,128]{2,1,0:T(8,128)(2,1)}, u32[]{:S(2)}) copy-start(bf16[3,1024,128]{2,1,0:T(8,128)(2,1)} %param.18) | copy-start | bytes 2359300
  14.9 254.9 %all-gather.12.cloned.1.call-start = ((), (), s32[]{:S(2)}) async-start(), calls=%async_computation.7 | async-start | bytes 4718592 | tf_op jit(solution)/shard_map/all_gather | solution.py:181
  143.2 150.5 %all-gather.14.cloned.1.call-start = ((), (), s32[]{:S(2)}) async-start(), calls=%async_computation.8 | async-start | bytes 4718592 | tf_op jit(solution)/shard_map/all_gather | solution.py:181
  144.1 206.0 %all-gather.10.cloned.1.call-start = ((), (), s32[]{:S(2)}) async-start(), calls=%async_computation.6 | async-start | bytes 2359296 | tf_op jit(solution)/shard_map/all_gather | solution.py:282
  148.3 371.9 %copy-start.14 = (pred[512,1536]{1,0:T(8,128)(4,1)}, pred[512,1536]{1,0:T(8,128)(4,1)S(1)}, u32[]{:S(2)}) copy-start(pred[512,1536]{1,0:T(8,128)(4,1)S(1)} %iota_compare_fusion.1) | copy-start | bytes 2359300
  148.9 114.0 %copy-start.10 = (pred[512,2048]{1,0:T(8,128)(4,1)}, pred[512,2048]{1,0:T(8,128)(4,1)S(1)}, u32[]{:S(2)}) copy-start(pred[512,2048]{1,0:T(8,128)(4,1)S(1)} %iota_compare_fusion) | copy-start | bytes 3145732
  220.0 21.7 %copy-start.18 = (bf16[2,2048,2,32]{1,3,2,0:T(8,128)(2,1)}, bf16[2,2048,2,32]{1,3,2,0:T(8,128)(2,1)S(1)}, u32[]{:S(2)}) copy-start(bf16[2,2048,2,32]{1,3,2,0:T(8,128)(2,1)S(1)} %get-tuple-element.137) | copy-start | bytes 1572868
  220.0 21.7 %copy-start.21 = (bf16[2,2048,2,32]{1,3,2,0:T(8,128)(2,1)}, bf16[2,2048,2,32]{1,3,2,0:T(8,128)(2,1)S(1)}, u32[]{:S(2)}) copy-start(bf16[2,2048,2,32]{1,3,2,0:T(8,128)(2,1)S(1)} %get-tuple-element.138) | copy-start | bytes 1572868
  239.2 8.7 copy-start.5
  244.3 6.8 copy-start.3
  269.8 85.2 %collective-permute-start = (bf16[512,4096]{1,0:T(8,128)(2,1)}, bf16[512,4096]{1,0:T(8,128)(2,1)}, u32[]{:S(2)}, u32[]{:S(2)}) collective-permute-start(bf16[512,4096]{1,0:T(8,128)(2,1)} %all-gather.12.cloned.1.call-done), channel_id=1, source_target_pairs={{0,8},{8,0},{16,24},{24,16},{1,9},{9,1},{17,25},{25,17},{2,10},{10... | collective-permute-start | bytes 12582920 | tf_op jit(solution)/shard_map/ppermute | solution.py:175
  273.5 9.2 %copy-start.86 = (s32[2]{0:T(128)S(1)}, s32[2]{0:T(128)}, u32[]{:S(2)}) copy-start(s32[2]{0:T(128)} %param.16) | copy-start | bytes 28
  273.5 9.3 %copy-start.87 = (f32[8]{0:T(128)S(1)}, f32[8]{0:T(128)}, u32[]{:S(2)}) copy-start(f32[8]{0:T(128)} %param.17) | copy-start | bytes 100
  273.5 76.6 %copy-start.60 = (f32[1024]{0:T(1024)S(1)}, f32[1024]{0:T(1024)}, u32[]{:S(2)}) copy-start(f32[1024]{0:T(1024)} %param.21) | copy-start | bytes 12292
  278.2 71.9 %all-to-all-start = ((bf16[8,512,128]{1,2,0:T(8,128)(2,1)}), bf16[8,512,128]{1,2,0:T(8,128)(2,1)}, u32[]{:S(2)}, u32[]{:S(2)}) async-start(bf16[8,512,128]{1,2,0:T(8,128)(2,1)} %copy.118), calls=%async_computation | async-start | bytes 2097152 | tf_op jit(solution)/shard_map/all_to_all | solution.py:281
  282.7 71.2 %copy-start.12 = (bf16[512,1024]{1,0:T(8,128)(2,1)S(1)}, bf16[512,1024]{1,0:T(8,128)(2,1)}, u32[]{:S(2)}) copy-start(bf16[512,1024]{1,0:T(8,128)(2,1)} %param.14) | copy-start | bytes 3145732
  293.7 76.5 %collective-permute-start.1 = (bf16[4096,512]{1,0:T(8,128)(2,1)}, bf16[4096,512]{1,0:T(8,128)(2,1)}, u32[]{:S(2)}, u32[]{:S(2)}) collective-permute-start(bf16[4096,512]{1,0:T(8,128)(2,1)} %all-gather.14.cloned.1.call-done), channel_id=1, source_target_pairs={{0,8},{8,0},{16,24},{24,16},{1,9},{9,1},{17,25},{25,17},{2,10},{10... | collective-permute-start | bytes 12582920 | tf_op jit(solution)/shard_map/ppermute | solution.py:175
  359.9 10.2 %copy-start.37 = (bf16[4096,512]{1,0:T(8,128)(2,1)S(1)}, bf16[4096,512]{1,0:T(8,128)(2,1)}, u32[]{:S(2)}) copy-start(bf16[4096,512]{1,0:T(8,128)(2,1)} %all-gather.14.cloned.1.call-done) | copy-start | bytes 12582916
  375.3 9.7 %copy-start.36 = (bf16[512,1024]{1,0:T(8,128)(2,1)S(1)}, bf16[512,1024]{1,0:T(8,128)(2,1)}, u32[]{:S(2)}) copy-start(bf16[512,1024]{1,0:T(8,128)(2,1)} %param.15) | copy-start | bytes 3145732
  398.0 12.6 %copy-start.39 = (bf16[512,4096]{1,0:T(8,128)(2,1)S(1)}, bf16[512,4096]{1,0:T(8,128)(2,1)}, u32[]{:S(2)}) copy-start(bf16[512,4096]{1,0:T(8,128)(2,1)} %get-tuple-element.107) | copy-start | bytes 12582916
  419.6 10.6 %copy-start.47 = (f32[512,1024]{1,0:T(8,128)S(1)}, f32[512,1024]{1,0:T(8,128)}, u32[]{:S(2)}) copy-start(f32[512,1024]{1,0:T(8,128)} %get-tuple-element.163) | copy-start | bytes 6291460
  438.5 41.6 %all-to-all-start.1 = ((bf16[512,8,128]{0,2,1:T(8,128)(2,1)}), bf16[512,8,128]{0,2,1:T(8,128)(2,1)}, u32[]{:S(2)}, u32[]{:S(2)}) async-start(bf16[512,8,128]{0,2,1:T(8,128)(2,1)} %bitcast.17), calls=%async_computation.1 | async-start | bytes 2097152 | tf_op jit(solution)/shard_map/all_to_all | solution.py:341
  442.7 204.6 %all-gather.16.cloned.1.call-start = ((), (), s32[]{:S(2)}) async-start(), calls=%async_computation.9 | async-start | bytes 3538944 | tf_op jit(solution)/shard_map/all_gather | solution.py:181
  444.6 346.6 %reduce-scatter.5.cloned.1.call-start = ((), (), s32[]{:S(2)}) async-start(), calls=%async_computation.11 | async-start | bytes 4718592 | tf_op jit(solution)/shard_map/reduce_scatter | solution.py:200
  447.6 12.8 %collective-permute-start.4 = (bf16[1024,512]{1,0:T(8,128)(2,1)S(1)}, bf16[1024,512]{1,0:T(8,128)(2,1)S(1)}, u32[]{:S(2)}, u32[]{:S(2)}) collective-permute-start(bf16[1024,512]{1,0:T(8,128)(2,1)S(1)} %dynamic-slice_convert_fusion.2), channel_id=1, source_target_pairs={{0,8},{8,0},{16,24},{24,16},{1,9},{9,1},{17,25},{25,17},{2,10},{10... | collective-permute-start | bytes 3145736 | tf_op jit(solution)/shard_map/ppermute | solution.py:175
  453.7 144.8 %collective-permute-start.3 = (bf16[4096,512]{1,0:T(8,128)(2,1)}, bf16[4096,512]{1,0:T(8,128)(2,1)}, u32[]{:S(2)}, u32[]{:S(2)}) collective-permute-start(bf16[4096,512]{1,0:T(8,128)(2,1)} %dynamic-slice_convert_fusion.1), channel_id=1, source_target_pairs={{0,8},{8,0},{16,24},{24,16},{1,9},{9,1},{17,25},{25,17},{2,10},{10... | collective-permute-start | bytes 12582920 | tf_op jit(solution)/shard_map/ppermute | solution.py:175
  460.3 72.7 %collective-permute-start.5 = (bf16[512,4096]{1,0:T(8,128)(2,1)}, bf16[512,4096]{1,0:T(8,128)(2,1)}, u32[]{:S(2)}, u32[]{:S(2)}) collective-permute-start(bf16[512,4096]{1,0:T(8,128)(2,1)} %dynamic-slice_convert_fusion), channel_id=1, source_target_pairs={{0,8},{8,0},{16,24},{24,16},{1,9},{9,1},{17,25},{25,17},{2,10},{10... | collective-permute-start | bytes 12582920 | tf_op jit(solution)/shard_map/ppermute | solution.py:175
  461.8 26.1 %copy-start.33 = (pred[512,512]{0,1:T(8,128)(4,1)S(1)}, pred[512,512]{0,1:T(8,128)(4,1)}, u32[]{:S(2)}) copy-start(pred[512,512]{0,1:T(8,128)(4,1)} %iota_compare_fusion.3) | copy-start | bytes 786436
  487.9 24.2 %copy-start.49 = (bf16[2,512,2,64]{1,0,3,2:T(2,128)(2,1)}, bf16[2,512,2,64]{1,0,3,2:T(2,128)(2,1)S(1)}, u32[]{:S(2)}) copy-start(bf16[2,512,2,64]{1,0,3,2:T(2,128)(2,1)S(1)} %get-tuple-element.126) | copy-start | bytes 786436
  491.9 7.9 slice-start.9
  491.9 8.3 slice-start.10
  505.1 7.0 slice-start.4
  505.1 7.0 slice-start.5
  541.0 264.4 %reduce-scatter.3.cloned.1.call-start = ((), (), s32[]{:S(2)}) async-start(), calls=%async_computation.10 | async-start | bytes 5898240 | tf_op jit(solution)/shard_map/reduce_scatter | solution.py:218
  552.0 15.8 %slice-start = ((s8[16777216]{0:T(1024)(128)(4,1)}), s8[4194304]{0:T(1024)(128)(4,1)S(1)}, s32[]{:S(2)}) async-start(s8[16777216]{0:T(1024)(128)(4,1)} %bitcast.157), calls=%async_computation.13 | async-start | bytes 8388608
  552.0 15.8 %slice-start.1 = ((s8[16777216]{0:T(1024)(128)(4,1)}), s8[4194304]{0:T(1024)(128)(4,1)S(1)}, s32[]{:S(2)}) async-start(s8[16777216]{0:T(1024)(128)(4,1)} %bitcast.157), calls=%async_computation.14 | async-start | bytes 8388608
  552.0 15.8 %slice-start.2 = ((s8[16777216]{0:T(1024)(128)(4,1)}), s8[4194304]{0:T(1024)(128)(4,1)S(1)}, s32[]{:S(2)}) async-start(s8[16777216]{0:T(1024)(128)(4,1)} %bitcast.157), calls=%async_computation.15 | async-start | bytes 8388608
  552.0 17.2 %slice-start.3 = ((s8[16777216]{0:T(1024)(128)(4,1)}), s8[4194304]{0:T(1024)(128)(4,1)S(1)}, s32[]{:S(2)}) async-start(s8[16777216]{0:T(1024)(128)(4,1)} %bitcast.157), calls=%async_computation.16 | async-start | bytes 8388608
  607.6 6.5 copy-start.20
  607.7 6.5 copy-start.23
  614.2 7.5 slice-start.7
  642.7 130.3 %all-to-all-start.2 = ((bf16[3,4096,128]{2,0,1:T(4,128)(2,1)}), bf16[3,4096,128]{2,0,1:T(4,128)(2,1)}, u32[]{:S(2)}, u32[]{:S(2)}) async-start(bf16[3,4096,128]{2,0,1:T(4,128)(2,1)} %copy.132), calls=%async_computation.2 | async-start | bytes 8388608 | tf_op jit(solution)/shard_map/all_to_all | solution.py:359
  647.2 232.0 %all-reduce.10.cloned.1.call-start = ((), (), s32[]{:S(2)}) async-start(), calls=%async_computation.12 | async-start | bytes 6291456 | tf_op jit(solution)/shard_map/psum | solution.py:388
  647.3 138.0 %collective-permute-start.2 = (bf16[3,512,1024]{2,1,0:T(8,128)(2,1)}, bf16[3,512,1024]{2,1,0:T(8,128)(2,1)}, u32[]{:S(2)}, u32[]{:S(2)}) collective-permute-start(bf16[3,512,1024]{2,1,0:T(8,128)(2,1)} %all-gather.16.cloned.1.call-done), channel_id=1, source_target_pairs={{0,8},{8,0},{16,24},{24,16},{1,9},{9,1},{17,25},{25,17},{2,10},{10... | collective-permute-start | bytes 9437192 | tf_op jit(solution)/shard_map/ppermute | solution.py:175
  809.6 9.1 %copy-start.77 = (f32[1024]{0:T(1024)S(1)}, f32[1024]{0:T(1024)}, u32[]{:S(2)}) copy-start(f32[1024]{0:T(1024)} %get-tuple-element.84) | copy-start | bytes 12292
  809.6 9.1 %copy-start.79 = (f32[1024]{0:T(1024)S(1)}, f32[1024]{0:T(1024)}, u32[]{:S(2)}) copy-start(f32[1024]{0:T(1024)} %get-tuple-element.87) | copy-start | bytes 12292
  809.6 9.1 %copy-start.83 = (f32[1024]{0:T(1024)S(1)}, f32[1024]{0:T(1024)}, u32[]{:S(2)}) copy-start(f32[1024]{0:T(1024)} %get-tuple-element.85) | copy-start | bytes 12292
  809.7 9.2 %copy-start.76 = (f32[1024]{0:T(1024)S(1)}, f32[1024]{0:T(1024)}, u32[]{:S(2)}) copy-start(f32[1024]{0:T(1024)} %get-tuple-element.72) | copy-start | bytes 12292
  809.7 9.2 %copy-start.78 = (f32[1024]{0:T(1024)S(1)}, f32[1024]{0:T(1024)}, u32[]{:S(2)}) copy-start(f32[1024]{0:T(1024)} %get-tuple-element.76) | copy-start | bytes 12292
  809.7 9.2 %copy-start.82 = (f32[1024]{0:T(1024)S(1)}, f32[1024]{0:T(1024)}, u32[]{:S(2)}) copy-start(f32[1024]{0:T(1024)} %get-tuple-element.74) | copy-start | bytes 12292
  809.7 9.2 %copy-start.75 = (f32[1024]{0:T(1024)S(1)}, f32[1024]{0:T(1024)}, u32[]{:S(2)}) copy-start(f32[1024]{0:T(1024)} %get-tuple-element.97) | copy-start | bytes 12292
  809.7 9.2 %copy-start.80 = (f32[4096]{0:T(1024)S(1)}, f32[4096]{0:T(1024)}, u32[]{:S(2)}) copy-start(f32[4096]{0:T(1024)} %get-tuple-element.173) | copy-start | bytes 49156
  809.7 9.2 %copy-start.81 = (f32[1024]{0:T(1024)S(1)}, f32[1024]{0:T(1024)}, u32[]{:S(2)}) copy-start(f32[1024]{0:T(1024)} %get-tuple-element.99) | copy-start | bytes 12292
  809.7 52.4 %copy-start.17 = (f32[512,1024]{1,0:T(8,128)S(1)}, f32[512,1024]{1,0:T(8,128)}, u32[]{:S(2)}) copy-start(f32[512,1024]{1,0:T(8,128)} %copy-done.16) | copy-start | bytes 6291460
  879.2 8.0 copy-start.1
  879.2 7.2 copy-start.61
  (53 other events, 182.7 us)
Sparse Core Ops, SparseCore 0:
  15.0 127.3 all-gather.7
  145.0 72.8 all-gather.11
  220.0 73.6 all-gather.13
  295.7 54.3 all-gather.9
  445.3 70.2 all-gather.15
  541.2 86.3 reduce-scatter.4
  631.1 174.2 reduce-scatter.2
  809.7 69.4 all-reduce.9

commit v16 on v14

--- a/solution.py
+++ b/solution.py
@@ -269,8 +269,8 @@
     bias_flat = jnp.concatenate([qkv_bias.reshape(-1), up_bias])
     bias_full = lax.all_gather(bias_flat, "narrow", axis=0)
     gathered_first = lax.all_gather(low_first, "narrow", axis=0, tiled=True)
-    gathered_first, up_weight, down_weight, bias_full = lax.optimization_barrier(
-        (gathered_first, up_weight, down_weight, bias_full)
+    gathered_first, up_weight, down_weight, out_weight, bias_full = lax.optimization_barrier(
+        (gathered_first, up_weight, down_weight, out_weight, bias_full)
     )
     up_bias_full = bias_full[:, 3 * inner :].reshape(-1)
     query, key_rows, values = project_qkv(
@@ -279,7 +279,7 @@
     attn_heads, totals = attend_forward(query, key_rows, values, block_rows)
     attn_low = attn_heads.reshape(group_rows, inner).astype(jnp.bfloat16)
     attn_rows = lax.all_to_all(attn_low, "narrow", 0, 1, tiled=True)
-    out_full = lax.all_gather(out_weight, "narrow", axis=0, tiled=True)
+    out_full = join_halves(gather_mine(out_weight, core, 1, 0), core, 1)
     pre_attn = jnp.dot(attn_rows, out_full, preferred_element_type=jnp.float32) + out_bias
     normed_second, inverse_second = norm_stats(pre_attn)
     residual = layer_in + normed_second * norm_gains[1] + norm_biases[1]

time: 876 us -> 905 us (1.033)
  waiting for transfers between devices: 247 us -> 262 us
  local copies, waits for them, and re-layouts: 184 us -> 194 us
    all_gather x3 -> x4, waiting for transfers between devices: 1.78 us -> 75.8 us  [gather_mine(): return lax.all_gather(mine, 'narrow', axis=gather_axis, tiled=True)]
    all_gather x1 -> x0, waiting for transfers between devices: 59.1 us -> none  [shards(): out_full = lax.all_gather(out_weight, 'narrow', axis=0, tiled=True)]
    unnamed x227 -> x255, local copies, waits for them, and re-layouts: 63.9 us -> 77.3 us
  transfers between devices with their start and end apart: 17 -> 18, of which waited for: 7 -> 7; matrix products, arithmetic and copies ran while one was open for 47% -> 45% of each run, Pallas kernels for 0% -> 0%
where the time goes in v16:
time: 905 us; the launch traced here: 899 us
  waiting for transfers between devices  262 us (29%)
  matrix products  196 us (22%)
  local copies, waits for them, and re-layouts  194 us (21%)
  other arithmetic  133 us (15%)
  blocking collectives  83.7 us (9%)
  between operations  16 us (2%)
  starting transfers between devices  15 us (2%)
    all_gather x1, waiting for transfers between devices, shards(): gathered_first = lax.all_gather(low_first, 'narrow', axis=0, tiled=True)  90.9 us
    unnamed x255, local copies, waits for them, and re-layouts  77.3 us
    all_gather x4, waiting for transfers between devices, gather_mine(): return lax.all_gather(mine, 'narrow', axis=gather_axis, tiled=True)  75.8 us
    all_to_all x1, waiting for transfers between devices, shards(): lax.all_to_all(qkv_grad.reshape(3, group_rows, heads_here, HEAD), 'narrow...  60.1 us
    psum x1, blocking collectives, shards(): lax.psum((gain_local, bias_local, out_blocal, down_blocal, up_bgrad_rows)...  42.5 us
    convert_element_type x4, other arithmetic, attend_backward(): scores_grad = (probs_full * (probs_grad - row_dot)).astype(jnp.bfloat16)  36.7 us
    all_gather x1, blocking collectives, shards(): bias_full = lax.all_gather(bias_flat, 'narrow', axis=0)  33.4 us
    dot_general x4, matrix products, attend_backward(): jnp.einsum('bqhd,bkhd->bhqk', grad_block, value_block, preferred_element_...  31.1 us
  transfers between devices with their start and end apart: 18, of which 7 were waited for; matrix products, arithmetic and copies ran while one was open for 45% of the time, Pallas kernels for 0%

profile of v16, /device:TPU:0, one launch (start us, length us, event | category | flops | bytes accessed | tf_op | source)
XLA Modules:
  0.0 898.6 jit_solution(10861646503214705904)
XLA Ops:
  15.5 33.4 %all-gather.1 = f32[8,1,896]{2,1,0:T(1,128)S(1)} all-gather(f32[1,1,896]{2,1,0:T(1,128)S(1)} %reshape.435), channel_id=2, replica_groups=mesh['wide'=4,'narrow'=8] {'narrow'}, dimensions={0}, use_global_device_ids=true | all-gather | bytes 32256 | tf_op jit(solution)/shard_map/all_gather | solution.py:270
  52.0 90.9 %all-gather.8.cloned.1.call-done = bf16[4096,1024]{1,0:T(8,128)(2,1)} async-done(((bf16[512,1024]{1,0:T(8,128)(2,1)}), bf16[4096,1024]{1,0:T(8,128)(2,1)}) %all-gather.8.cloned.1.call-update) | async-done | bytes 8388624 | tf_op jit(solution)/shard_map/all_gather | solution.py:271
  145.3 7.1 add_bitcast_fusion
  157.1 5.9 copy.114
  162.9 4.5 fusion.132
  167.4 5.6 reshape.442
  173.1 9.9 %fusion.133 = (f32[2,2048,2,32]{3,2,1,0:T(2,128)}, f32[2,2048,2,32]{3,2,1,0:T(2,128)}) fusion(f32[2,2048,2,64]{3,2,1,0:T(2,128)} %reshape.442), kind=kLoop, calls=%fused_computation.283 | loop fusion | bytes 4194304 | tf_op jit(solution)/shard_map/slice | solution.py:41
  182.9 6.4 copy.168
  189.4 6.4 copy.167
  195.8 5.6 reshape.441
  201.4 9.9 %fusion.134 = (f32[2,2048,2,32]{3,2,1,0:T(2,128)}, f32[2,2048,2,32]{3,2,1,0:T(2,128)}) fusion(f32[2,2048,2,64]{3,2,1,0:T(2,128)} %reshape.441), kind=kLoop, calls=%fused_computation.284 | loop fusion | bytes 4194304 | tf_op jit(solution)/shard_map/slice | solution.py:41
  211.3 6.5 copy.166
  217.8 6.9 copy.165
  229.2 4.9 fusion.14
  237.5 5.8 copy-done.2
  243.3 4.4 exponential_reduce_fusion
  249.7 3.6 fusion.1
  253.3 4.6 copy-done.3
  257.9 3.7 exponential_reduce_fusion.1
  261.7 4.8 exponential_reduce_fusion.2
  273.6 7.5 fusion.67
  281.1 5.7 fusion.68
  287.0 3.5 fusion.66
  293.3 4.5 all-to-all-start
  303.2 75.8 %all-gather.14.cloned.1.call-done = bf16[4096,512]{1,0:T(8,128)(2,1)} async-done(((bf16[512,512]{1,0:T(8,128)(2,1)}), bf16[4096,512]{1,0:T(8,128)(2,1)}) %all-gather.14.cloned.1.call-update) | async-done | bytes 4194320 | tf_op jit(solution)/shard_map/all_gather | solution.py:181
  384.6 3.9 broadcast_select_fusion.3
  388.5 10.3 %multiply_convert_fusion.3 = (bf16[512,4096]{1,0:T(8,128)(2,1)}, f32[512,4096]{1,0:T(8,128)}) fusion(f32[4096]{0:T(1024)S(1)} %bitcast.207, bf16[512,4096]{1,0:T(8,128)(2,1)} %get-tuple-element.109, bf16[512,4096]{1,0:T(8,128)(2,1)S(1)} %get-tuple-element.108, f32[512,1024]{1,0:T(8,128)S(1)} %get-tuple-element.105, f32[1024]{0:T(1024)S(1)} %bitcast.210, ...), kind=kOutput, calls=%fused_computation.33 | convolution fusion | flops 4326948864 | bytes 23097344 | tf_op jit(solution)/shard_map/dot_general | solution.py:290
  398.8 3.9 broadcast_select_fusion.1
  402.7 8.9 add_reduce_fusion
  416.4 8.6 fusion.138
  424.9 12.6 %convert_reduce_fusion = (f32[4096]{0:T(1024)}, bf16[512,4096]{1,0:T(8,128)(2,1)}) fusion(f32[512,4096]{1,0:T(8,128)} %get-tuple-element.164, f32[4096]{0:T(1024)S(1)} %bitcast.208, bf16[512,1024]{1,0:T(8,128)(2,1)S(1)} %get-tuple-element.100, bf16[4096,512]{1,0:T(8,128)(2,1)} %get-tuple-element.107, bf16[4096,512]{1,0:T(8,128)(2,1)} %copy-done.42), kind=kOutput, calls=%fused_computation.26 | convolution fusion | flops 4339003392 | bytes 22052864 | tf_op jit(solution)/shard_map/dot_general | solution.py:322
  437.5 9.1 %multiply_reduce_fusion.5 = (f32[1024]{0:T(1024)}, f32[512]{0:T(512)S(1)}, f32[512]{0:T(512)S(1)}, f32[1024]{0:T(1024)}, f32[512,1024]{1,0:T(8,128)}) fusion(f32[512,1024]{1,0:T(8,128)S(1)} %get-tuple-element.105, f32[512]{0:T(512)S(1)} %add_rsqrt_fusion.1, f32[512]{0:T(512)S(1)} %broadcast_multiply_fusion.9, f32[1024]{0:T(1024)S(1)} %bitcast.197, ...), kind=kOutput, calls=%fused_computation.102 | convolution fusion | flops 4316460032 | bytes 16797696 | tf_op jit(solution)/shard_map/dot_general | solution.py:330
  446.6 10.7 %fusion.129 = f32[1024,4096]{1,0:T(8,128)} fusion(bf16[512,4096]{1,0:T(8,128)(2,1)} %get-tuple-element.178, f32[512,1024]{1,0:T(8,128)S(1)} %get-tuple-element.105, f32[1024]{0:T(1024)S(1)} %bitcast.211, f32[1024]{0:T(1024)S(1)} %bitcast.198, f32[512]{0:T(512)S(1)} %add_rsqrt_fusion.1, f32[512]{0:T(512)S(1)} %broadcast_multiply_fusion.9), kind=kOutput, calls=%fused_computation.280 | convolution fusion | flops 4297588736 | bytes 23080960 | tf_op jit(solution)/shard_map/dot_general | solution.py:327
  467.5 3.6 all-to-all-start.1
  476.2 5.9 dynamic-slice_convert_fusion.1
  482.1 6.2 dynamic-slice_convert_fusion
  490.1 18.6 %all-to-all-done.1 = bf16[512,8,128]{0,2,1:T(8,128)(2,1)S(1)} async-done(((bf16[512,8,128]{0,2,1:T(8,128)(2,1)}), bf16[512,8,128]{0,2,1:T(8,128)(2,1)S(1)}, u32[]{:S(2)}, u32[]{:S(2)}) %all-to-all-start.1) | async-done | bytes 1048608 | tf_op jit(solution)/shard_map/all_to_all | solution.py:341
  511.4 6.0 convolution_bitcast_fusion.2
  521.6 12.0 %multiply_reduce_fusion.1 = (f32[2,2,512]{2,1,0:T(2,128)}, f32[2,2,512,1536]{3,2,1,0:T(8,128)}) fusion(f32[2,2,512,1536]{3,2,1,0:T(8,128)} %copy-done.3, f32[2,2,512]{2,1,0:T(2,128)S(1)} %copy-done.67, pred[512,1536]{1,0:T(8,128)(4,1)S(1)} %copy-done.14, bf16[2,2048,2,64]{1,3,2,0:T(8,128)(2,1)S(1)} %copy-done.30, ...), kind=kOutput, calls=%fused_computation.7 | convolution fusion | flops 418379776 | bytes 27017216 | tf_op jit(solution)/shard_map/bqhd,bkhd->bhqk/dot_general | solution.py:141
  533.7 11.4 %multiply_reduce_fusion = (f32[2,2,512]{2,1,0:T(2,128)}, f32[2,2,512,2048]{3,2,1,0:T(8,128)}) fusion(f32[2,2,512,2048]{3,2,1,0:T(8,128)S(1)} %bitcast.165, f32[2,2,512]{2,1,0:T(2,128)} %copy-done.71, pred[512,2048]{1,0:T(8,128)(4,1)S(1)} %copy-done.10, bf16[2,2048,2,64]{1,3,2,0:T(8,128)(2,1)} %copy.114, bf16[2,512,2,64]{1,0,3,2:T(2,128)(2,1)} %get-tuple-element.129), kind=kOutput, calls=%fused_computation.1 | convolution fusion | flops 557840384 | bytes 35930112 | tf_op jit(solution)/shard_map/bqhd,bkhd->bhqk/dot_general | solution.py:141
  545.1 12.2 %multiply_convert_fusion.1 = bf16[2,2,512,1536]{3,2,1,0:T(8,128)(2,1)} fusion(f32[2,2,512,1536]{3,2,1,0:T(8,128)} %get-tuple-element.171, f32[2,2,512,1536]{3,2,1,0:T(8,128)} %copy-done.3, f32[2,2,512]{2,1,0:T(2,128)} %get-tuple-element.170, f32[2,2,512]{2,1,0:T(2,128)} %copy-done.66, pred[512,1536]{1,0:T(8,128)(4,1)} %copy-done.13), kind=kLoop, calls=%fused_computation.6 | loop fusion | flops 18874368 | bytes 32260096 | tf_op jit(solution)/shard_map/convert_element_type | solution.py:145
  557.3 8.1 add_convert_fusion
  566.6 5.8 fusion.60
  572.4 12.3 %multiply_convert_fusion = bf16[2,2,512,2048]{3,2,1,0:T(8,128)(2,1)S(1)} fusion(f32[2,2,512,2048]{3,2,1,0:T(8,128)} %get-tuple-element.169, f32[2,2,512,2048]{3,2,1,0:T(8,128)} %copy-done.2, f32[2,2,512]{2,1,0:T(2,128)S(1)} %copy-done.81, f32[2,2,512]{2,1,0:T(2,128)S(1)} %copy-done.72, pred[512,2048]{1,0:T(8,128)(4,1)S(1)} %copy-done.10), kind=kLoop, calls=%fused_computation | loop fusion | flops 25165824 | bytes 43008000 | tf_op jit(solution)/shard_map/convert_element_type | solution.py:145
  588.0 3.5 fusion.61
  593.7 6.2 multiply_reduce_fusion.2
  600.0 4.7 convolution_bitcast_fusion.1
  604.7 9.6 %multiply_convert_fusion.2 = bf16[2,2,512,1024]{3,2,1,0:T(8,128)(2,1)} fusion(f32[2,2,512,1024]{3,2,1,0:T(8,128)} %get-tuple-element.173, f32[2,2,512,1024]{3,2,1,0:T(8,128)} %get-tuple-element.158, f32[2,2,512]{2,1,0:T(2,128)S(1)} %copy-done.78, f32[2,2,512]{2,1,0:T(2,128)S(1)} %log_add_fusion.2, pred[512,1024]{1,0:T(8,128)(4,1)} %copy-done.23), kind=kLoop, calls=%fused_computation.31 | loop fusion | flops 12582912 | bytes 21512192 | tf_op jit(solution)/shard_map/convert_element_type | solution.py:145
  614.7 7.7 fusion.30
  622.4 6.3 add_convert_fusion.1
  639.7 3.9 fusion.62
  656.6 3.5 pad_maximum_fusion.7
  660.2 14.6 %copy.140 = bf16[3,4096,2,64]{3,2,0,1:T(2,128)(2,1)} copy(bf16[3,4096,2,64]{1,3,2,0:T(8,128)(2,1)} %pad_maximum_fusion.7) | data formatting | bytes 6291456 | tf_op jit(solution)/shard_map/stack | solution.py:350
  674.8 8.9 reshape.443
  683.7 4.6 all-to-all-start.2
  699.2 7.7 psum.71
  707.5 8.7 fusion.57
  716.3 60.1 %all-to-all-done.2 = bf16[8,2,98304]{2,1,0:T(2,128)(2,1)} async-done(((bf16[8,2,98304]{2,1,0:T(2,128)(2,1)}), bf16[8,2,98304]{2,1,0:T(2,128)(2,1)}, u32[]{:S(2)}, u32[]{:S(2)}) %all-to-all-start.2) | async-done | bytes 3145760 | tf_op jit(solution)/shard_map/all_to_all | solution.py:359
  776.3 8.8 reshape.444
  785.1 15.3 %copy.157 = bf16[3,8,512,2,64]{2,4,3,1,0:T(8,128)(2,1)} copy(bf16[3,8,512,2,64]{4,3,0,2,1:T(2,128)(2,1)} %bitcast.179) | data formatting | bytes 6291456 | tf_op jit(solution)/shard_map/all_to_all | solution.py:359
  800.4 5.9 broadcast_select_fusion.5
  813.1 9.2 %fusion.45 = (f32[1024]{0:T(1024)S(1)}, f32[512]{0:T(512)S(1)}, f32[512]{0:T(512)S(1)}, f32[1024]{0:T(1024)S(1)}, f32[512,1024,1]{1,0,2:T(8,128)}) fusion(bf16[512,1024]{1,0:T(8,128)(2,1)S(1)} %copy-done.12, f32[512]{0:T(512)S(1)} %copy-done.83, f32[512]{0:T(512)S(1)} %copy-done.80, f32[1024]{0:T(1024)S(1)} %bitcast.194, ...), kind=kOutput, calls=%fused_computation.91 | convolution fusion | flops 3239048192 | bytes 12603392 | tf_op jit(solution)/shard_map/tse,tde->sd/dot_general | solution.py:365
  822.5 42.5 %all-reduce.6 = (f32[1024]{0:T(1024)}, f32[4096]{0:T(1024)S(1)}, f32[1024]{0:T(1024)}, f32[4,1024]{1,0:T(4,128)}, f32[4,1024]{1,0:T(4,128)}) all-reduce(f32[1024]{0:T(1024)S(1)} %copy-done.90, f32[4096]{0:T(1024)S(1)} %copy-done.89, f32[1024]{0:T(1024)S(1)} %copy-done.84, ...), channel_id=1, replica_groups=mesh['wide'=4,'narrow'=8] {'wide','narrow'}, use_global_device_ids=true, to_apply=%region_36.37 | all-reduce | flops 14336 | bytes 114688 | tf_op jit(solution)/shard_map/psum | solution.py:397
  868.9 13.7 %all-reduce.10.cloned.1.call-done = (bf16[3,1024,128]{1,2,0:T(8,128)(2,1)}, bf16[128,1024]{1,0:T(8,128)(2,1)}, bf16[1024,512]{1,0:T(8,128)(2,1)}, bf16[512,1024]{1,0:T(8,128)(2,1)}) async-done(((bf16[3,1024,128]{1,2,0:T(8,128)(2,1)}, bf16[128,1024]{1,0:T(8,128)(2,1)}, bf16[1024,512]{1,0:T(8,128)(2,1)}, bf16[512,1024]{1,0:T(8,128)(2,1)}), (bf16[3,1024,128]{1,2,0:T(8,128)(2,1)}, bf16[128,1024]{1,0:T(8,128)(2,1)}, ...) | async-done | bytes 3145744 | tf_op jit(solution)/shard_map/psum | solution.py:390
  (403 shorter events, 139.4 us)
Async XLA Ops:
  7.2 135.7 %copy-start = (bf16[1024,512]{1,0:T(8,128)(2,1)S(1)}, bf16[1024,512]{1,0:T(8,128)(2,1)}, u32[]{:S(2)}) copy-start(bf16[1024,512]{1,0:T(8,128)(2,1)} %param.22) | copy-start | bytes 3145732
  7.2 8.3 copy-start.93
  7.2 8.3 copy-start.94
  7.2 135.7 %all-gather.8.cloned.1.call-start = ((), (), s32[]{:S(2)}) async-start(), calls=%async_computation.5 | async-start | bytes 9437184 | tf_op jit(solution)/shard_map/all_gather | solution.py:271
  15.4 271.5 %all-gather.12.cloned.1.call-start = ((), (), s32[]{:S(2)}) async-start(), calls=%async_computation.7 | async-start | bytes 4718592 | tf_op jit(solution)/shard_map/all_gather | solution.py:181
  51.5 229.6 %copy-start.9 = (pred[512,2048]{1,0:T(8,128)(4,1)}, pred[512,2048]{1,0:T(8,128)(4,1)S(1)}, u32[]{:S(2)}) copy-start(pred[512,2048]{1,0:T(8,128)(4,1)S(1)} %iota_compare_fusion) | copy-start | bytes 3145732
  52.0 221.6 %copy-start.13 = (pred[512,1536]{1,0:T(8,128)(4,1)}, pred[512,1536]{1,0:T(8,128)(4,1)S(1)}, u32[]{:S(2)}) copy-start(pred[512,1536]{1,0:T(8,128)(4,1)S(1)} %iota_compare_fusion.1) | copy-start | bytes 2359300
  143.7 154.1 %all-gather.10.cloned.1.call-start = ((), (), s32[]{:S(2)}) async-start(), calls=%async_computation.6 | async-start | bytes 1179648 | tf_op jit(solution)/shard_map/all_gather | solution.py:181
  144.4 366.9 %copy-start.23 = (pred[512,1024]{1,0:T(8,128)(4,1)}, pred[512,1024]{1,0:T(8,128)(4,1)S(1)}, u32[]{:S(2)}) copy-start(pred[512,1024]{1,0:T(8,128)(4,1)S(1)} %iota_compare_fusion.2) | copy-start | bytes 1572868
  211.3 13.4 %copy-start.74 = (bf16[128,1024]{1,0:T(8,128)(2,1)S(1)}, bf16[128,1024]{1,0:T(8,128)(2,1)}, u32[]{:S(2)}) copy-start(bf16[128,1024]{1,0:T(8,128)(2,1)} %param.20) | copy-start | bytes 786436
  228.4 38.1 %copy-start.18 = (bf16[2,2048,2,32]{1,3,2,0:T(8,128)(2,1)}, bf16[2,2048,2,32]{1,3,2,0:T(8,128)(2,1)S(1)}, u32[]{:S(2)}) copy-start(bf16[2,2048,2,32]{1,3,2,0:T(8,128)(2,1)S(1)} %get-tuple-element.141) | copy-start | bytes 1572868
  228.4 38.1 %copy-start.20 = (bf16[2,2048,2,32]{1,3,2,0:T(8,128)(2,1)}, bf16[2,2048,2,32]{1,3,2,0:T(8,128)(2,1)S(1)}, u32[]{:S(2)}) copy-start(bf16[2,2048,2,32]{1,3,2,0:T(8,128)(2,1)S(1)} %get-tuple-element.142) | copy-start | bytes 1572868
  247.7 131.3 %all-gather.14.cloned.1.call-start = ((), (), s32[]{:S(2)}) async-start(), calls=%async_computation.8 | async-start | bytes 4718592 | tf_op jit(solution)/shard_map/all_gather | solution.py:181
  249.6 31.4 %copy-start.71 = (f32[2,2,512]{2,1,0:T(2,128)}, f32[2,2,512]{2,1,0:T(2,128)S(1)}, u32[]{:S(2)}) copy-start(f32[2,2,512]{2,1,0:T(2,128)S(1)} %log_add_fusion) | copy-start | bytes 24580
  261.7 12.0 %copy-start.66 = (f32[2,2,512]{2,1,0:T(2,128)}, f32[2,2,512]{2,1,0:T(2,128)S(1)}, u32[]{:S(2)}) copy-start(f32[2,2,512]{2,1,0:T(2,128)S(1)} %log_add_fusion.1) | copy-start | bytes 24580
  261.7 8.0 slice-start.17
  270.6 248.4 %copy-start.69 = (f32[2,2,512]{2,1,0:T(2,128)}, f32[2,2,512]{2,1,0:T(2,128)S(1)}, u32[]{:S(2)}) copy-start(f32[2,2,512]{2,1,0:T(2,128)S(1)} %log_add_fusion.3) | copy-start | bytes 24580
  270.6 10.5 %slice-start = ((s8[16777216]{0:T(1024)(128)(4,1)}), s8[4194304]{0:T(1024)(128)(4,1)S(1)}, s32[]{:S(2)}) async-start(s8[16777216]{0:T(1024)(128)(4,1)} %bitcast.162), calls=%async_computation.13 | async-start | bytes 8388608
  270.6 10.5 %slice-start.1 = ((s8[16777216]{0:T(1024)(128)(4,1)}), s8[4194304]{0:T(1024)(128)(4,1)S(1)}, s32[]{:S(2)}) async-start(s8[16777216]{0:T(1024)(128)(4,1)} %bitcast.162), calls=%async_computation.14 | async-start | bytes 8388608
  286.9 96.7 %collective-permute-start.1 = (bf16[512,4096]{1,0:T(8,128)(2,1)}, bf16[512,4096]{1,0:T(8,128)(2,1)}, u32[]{:S(2)}, u32[]{:S(2)}) collective-permute-start(bf16[512,4096]{1,0:T(8,128)(2,1)} %all-gather.12.cloned.1.call-done), channel_id=1, source_target_pairs={{0,8},{8,0},{16,24},{24,16},{1,9},{9,1},{17,25},{25,17},{2,10},{10... | collective-permute-start | bytes 12582920 | tf_op jit(solution)/shard_map/ppermute | solution.py:175
  292.0 86.9 %copy-start.73 = (f32[1024]{0:T(1024)S(1)}, f32[1024]{0:T(1024)}, u32[]{:S(2)}) copy-start(f32[1024]{0:T(1024)} %param.21) | copy-start | bytes 12292
  293.3 85.6 %all-to-all-start = ((bf16[8,512,128]{1,2,0:T(8,128)(2,1)}), bf16[8,512,128]{1,2,0:T(8,128)(2,1)}, u32[]{:S(2)}, u32[]{:S(2)}) async-start(bf16[8,512,128]{1,2,0:T(8,128)(2,1)} %copy.126), calls=%async_computation | async-start | bytes 2097152 | tf_op jit(solution)/shard_map/all_to_all | solution.py:281
  297.8 3.0 collective-permute-start
  379.0 19.8 %collective-permute-start.2 = (bf16[4096,512]{1,0:T(8,128)(2,1)}, bf16[4096,512]{1,0:T(8,128)(2,1)}, u32[]{:S(2)}, u32[]{:S(2)}) collective-permute-start(bf16[4096,512]{1,0:T(8,128)(2,1)} %all-gather.14.cloned.1.call-done), channel_id=1, source_target_pairs={{0,8},{8,0},{16,24},{24,16},{1,9},{9,1},{17,25},{25,17},{2,10},{10... | collective-permute-start | bytes 12582920 | tf_op jit(solution)/shard_map/ppermute | solution.py:175
  388.5 10.3 %copy-start.40 = (bf16[4096,512]{1,0:T(8,128)(2,1)S(1)}, bf16[4096,512]{1,0:T(8,128)(2,1)}, u32[]{:S(2)}) copy-start(bf16[4096,512]{1,0:T(8,128)(2,1)} %all-gather.14.cloned.1.call-done) | copy-start | bytes 12582916
  402.7 8.9 copy-start.42
  402.7 9.3 %copy-start.35 = (bf16[512,1024]{1,0:T(8,128)(2,1)S(1)}, bf16[512,1024]{1,0:T(8,128)(2,1)}, u32[]{:S(2)}) copy-start(bf16[512,1024]{1,0:T(8,128)(2,1)} %param.15) | copy-start | bytes 3145732
  424.9 12.6 %copy-start.41 = (bf16[512,4096]{1,0:T(8,128)(2,1)S(1)}, bf16[512,4096]{1,0:T(8,128)(2,1)}, u32[]{:S(2)}) copy-start(bf16[512,4096]{1,0:T(8,128)(2,1)} %get-tuple-element.109) | copy-start | bytes 12582916
  446.6 10.7 %copy-start.49 = (f32[512,1024]{1,0:T(8,128)S(1)}, f32[512,1024]{1,0:T(8,128)}, u32[]{:S(2)}) copy-start(f32[512,1024]{1,0:T(8,128)} %get-tuple-element.167) | copy-start | bytes 6291460
  467.5 41.3 %all-to-all-start.1 = ((bf16[512,8,128]{0,2,1:T(8,128)(2,1)}), bf16[512,8,128]{0,2,1:T(8,128)(2,1)S(1)}, u32[]{:S(2)}, u32[]{:S(2)}) async-start(bf16[512,8,128]{0,2,1:T(8,128)(2,1)} %bitcast.17), calls=%async_computation.1 | async-start | bytes 2097152 | tf_op jit(solution)/shard_map/all_to_all | solution.py:341
  471.0 217.3 %all-gather.16.cloned.1.call-start = ((), (), s32[]{:S(2)}) async-start(), calls=%async_computation.9 | async-start | bytes 3538944 | tf_op jit(solution)/shard_map/all_gather | solution.py:181
  472.9 333.5 %reduce-scatter.5.cloned.1.call-start = ((), (), s32[]{:S(2)}) async-start(), calls=%async_computation.11 | async-start | bytes 4718592 | tf_op jit(solution)/shard_map/reduce_scatter | solution.py:200
  475.6 13.1 %collective-permute-start.5 = (bf16[1024,512]{1,0:T(8,128)(2,1)S(1)}, bf16[1024,512]{1,0:T(8,128)(2,1)S(1)}, u32[]{:S(2)}, u32[]{:S(2)}) collective-permute-start(bf16[1024,512]{1,0:T(8,128)(2,1)S(1)} %dynamic-slice_convert_fusion.2), channel_id=1, source_target_pairs={{0,8},{8,0},{16,24},{24,16},{1,9},{9,1},{17,25},{25,17},{2,10},{10... | collective-permute-start | bytes 3145736 | tf_op jit(solution)/shard_map/ppermute | solution.py:175
  482.0 140.4 %collective-permute-start.4 = (bf16[4096,512]{1,0:T(8,128)(2,1)}, bf16[4096,512]{1,0:T(8,128)(2,1)}, u32[]{:S(2)}, u32[]{:S(2)}) collective-permute-start(bf16[4096,512]{1,0:T(8,128)(2,1)} %dynamic-slice_convert_fusion.1), channel_id=1, source_target_pairs={{0,8},{8,0},{16,24},{24,16},{1,9},{9,1},{17,25},{25,17},{2,10},{10... | collective-permute-start | bytes 12582920 | tf_op jit(solution)/shard_map/ppermute | solution.py:175
  488.2 69.0 %collective-permute-start.6 = (bf16[512,4096]{1,0:T(8,128)(2,1)}, bf16[512,4096]{1,0:T(8,128)(2,1)}, u32[]{:S(2)}, u32[]{:S(2)}) collective-permute-start(bf16[512,4096]{1,0:T(8,128)(2,1)} %dynamic-slice_convert_fusion), channel_id=1, source_target_pairs={{0,8},{8,0},{16,24},{24,16},{1,9},{9,1},{17,25},{25,17},{2,10},{10... | collective-permute-start | bytes 12582920 | tf_op jit(solution)/shard_map/ppermute | solution.py:175
  511.4 10.2 %copy-start.51 = (bf16[2,512,2,64]{1,0,3,2:T(2,128)(2,1)}, bf16[2,512,2,64]{1,0,3,2:T(2,128)(2,1)S(1)}, u32[]{:S(2)}) copy-start(bf16[2,512,2,64]{1,0,3,2:T(2,128)(2,1)S(1)} %get-tuple-element.130) | copy-start | bytes 786436
  519.0 14.7 %slice-start.4 = ((s8[16777216]{0:T(1024)(128)(4,1)}), s8[4194304]{0:T(1024)(128)(4,1)S(1)}, s32[]{:S(2)}) async-start(s8[16777216]{0:T(1024)(128)(4,1)} %bitcast.164), calls=%async_computation.17 | async-start | bytes 8388608
  519.0 14.7 %slice-start.5 = ((s8[16777216]{0:T(1024)(128)(4,1)}), s8[4194304]{0:T(1024)(128)(4,1)S(1)}, s32[]{:S(2)}) async-start(s8[16777216]{0:T(1024)(128)(4,1)} %bitcast.164), calls=%async_computation.18 | async-start | bytes 8388608
  521.6 12.1 %slice-start.6 = ((s8[16777216]{0:T(1024)(128)(4,1)}), s8[4194304]{0:T(1024)(128)(4,1)S(1)}, s32[]{:S(2)}) async-start(s8[16777216]{0:T(1024)(128)(4,1)} %bitcast.164), calls=%async_computation.19 | async-start | bytes 8388608
  521.6 12.1 %slice-start.7 = ((s8[16777216]{0:T(1024)(128)(4,1)}), s8[4194304]{0:T(1024)(128)(4,1)S(1)}, s32[]{:S(2)}) async-start(s8[16777216]{0:T(1024)(128)(4,1)} %bitcast.164), calls=%async_computation.20 | async-start | bytes 8388608
  521.6 12.1 %copy-start.10 = (pred[512,2048]{1,0:T(8,128)(4,1)S(1)}, pred[512,2048]{1,0:T(8,128)(4,1)}, u32[]{:S(2)}) copy-start(pred[512,2048]{1,0:T(8,128)(4,1)} %copy-done.9) | copy-start | bytes 3145732
  565.5 243.4 %reduce-scatter.3.cloned.1.call-start = ((), (), s32[]{:S(2)}) async-start(), calls=%async_computation.10 | async-start | bytes 5898240 | tf_op jit(solution)/shard_map/reduce_scatter | solution.py:218
  566.6 27.0 %slice-start.19 = ((s8[8388608]{0:T(1024)(128)(4,1)}), s8[4194304]{0:T(1024)(128)(4,1)S(1)}, s32[]{:S(2)}) async-start(s8[8388608]{0:T(1024)(128)(4,1)} %bitcast.174), calls=%async_computation.32 | async-start | bytes 8388608
  572.4 21.3 %slice-start.20 = ((s8[8388608]{0:T(1024)(128)(4,1)}), s8[4194304]{0:T(1024)(128)(4,1)S(1)}, s32[]{:S(2)}) async-start(s8[8388608]{0:T(1024)(128)(4,1)} %bitcast.174), calls=%async_computation.33 | async-start | bytes 8388608
  591.6 8.3 slice-start.12
  600.0 14.3 %slice-start.8 = ((s8[16777216]{0:T(1024)(128)(4,1)}), s8[4194304]{0:T(1024)(128)(4,1)S(1)}, s32[]{:S(2)}) async-start(s8[16777216]{0:T(1024)(128)(4,1)} %bitcast.166), calls=%async_computation.21 | async-start | bytes 8388608
  600.0 14.3 %slice-start.9 = ((s8[16777216]{0:T(1024)(128)(4,1)}), s8[4194304]{0:T(1024)(128)(4,1)S(1)}, s32[]{:S(2)}) async-start(s8[16777216]{0:T(1024)(128)(4,1)} %bitcast.166), calls=%async_computation.22 | async-start | bytes 8388608
  604.7 9.6 %slice-start.10 = ((s8[16777216]{0:T(1024)(128)(4,1)}), s8[4194304]{0:T(1024)(128)(4,1)S(1)}, s32[]{:S(2)}) async-start(s8[16777216]{0:T(1024)(128)(4,1)} %bitcast.166), calls=%async_computation.23 | async-start | bytes 8388608
  604.7 10.0 %slice-start.11 = ((s8[16777216]{0:T(1024)(128)(4,1)}), s8[4194304]{0:T(1024)(128)(4,1)S(1)}, s32[]{:S(2)}) async-start(s8[16777216]{0:T(1024)(128)(4,1)} %bitcast.166), calls=%async_computation.24 | async-start | bytes 8388608
  683.7 8.0 copy-start.37
  683.7 92.7 %all-to-all-start.2 = ((bf16[8,2,98304]{2,1,0:T(2,128)(2,1)}), bf16[8,2,98304]{2,1,0:T(2,128)(2,1)}, u32[]{:S(2)}, u32[]{:S(2)}) async-start(bf16[8,2,98304]{2,1,0:T(2,128)(2,1)} %reshape.443), calls=%async_computation.2 | async-start | bytes 6291456 | tf_op jit(solution)/shard_map/all_to_all | solution.py:359
  688.3 194.3 %all-reduce.10.cloned.1.call-start = ((), (), s32[]{:S(2)}) async-start(), calls=%async_computation.12 | async-start | bytes 6291456 | tf_op jit(solution)/shard_map/psum | solution.py:390
  688.4 112.1 %collective-permute-start.3 = (bf16[3,512,1024]{2,1,0:T(8,128)(2,1)}, bf16[3,512,1024]{2,1,0:T(8,128)(2,1)}, u32[]{:S(2)}, u32[]{:S(2)}) collective-permute-start(bf16[3,512,1024]{2,1,0:T(8,128)(2,1)} %all-gather.16.cloned.1.call-done), channel_id=1, source_target_pairs={{0,8},{8,0},{16,24},{24,16},{1,9},{9,1},{17,25},{25,17},{2,10},{10... | collective-permute-start | bytes 9437192 | tf_op jit(solution)/shard_map/ppermute | solution.py:175
  813.0 9.3 %copy-start.86 = (f32[1024]{0:T(1024)S(1)}, f32[1024]{0:T(1024)}, u32[]{:S(2)}) copy-start(f32[1024]{0:T(1024)} %get-tuple-element.74) | copy-start | bytes 12292
  813.0 9.3 %copy-start.88 = (f32[1024]{0:T(1024)S(1)}, f32[1024]{0:T(1024)}, u32[]{:S(2)}) copy-start(f32[1024]{0:T(1024)} %get-tuple-element.78) | copy-start | bytes 12292
  813.1 9.3 %copy-start.92 = (f32[1024]{0:T(1024)S(1)}, f32[1024]{0:T(1024)}, u32[]{:S(2)}) copy-start(f32[1024]{0:T(1024)} %get-tuple-element.76) | copy-start | bytes 12292
  813.1 9.3 %copy-start.85 = (f32[1024]{0:T(1024)S(1)}, f32[1024]{0:T(1024)}, u32[]{:S(2)}) copy-start(f32[1024]{0:T(1024)} %get-tuple-element.86) | copy-start | bytes 12292
  813.1 9.3 %copy-start.87 = (f32[1024]{0:T(1024)S(1)}, f32[1024]{0:T(1024)}, u32[]{:S(2)}) copy-start(f32[1024]{0:T(1024)} %get-tuple-element.89) | copy-start | bytes 12292
  813.1 9.3 %copy-start.91 = (f32[1024]{0:T(1024)S(1)}, f32[1024]{0:T(1024)}, u32[]{:S(2)}) copy-start(f32[1024]{0:T(1024)} %get-tuple-element.87) | copy-start | bytes 12292
  813.1 9.3 %copy-start.84 = (f32[1024]{0:T(1024)S(1)}, f32[1024]{0:T(1024)}, u32[]{:S(2)}) copy-start(f32[1024]{0:T(1024)} %get-tuple-element.99) | copy-start | bytes 12292
  813.1 9.3 %copy-start.89 = (f32[4096]{0:T(1024)S(1)}, f32[4096]{0:T(1024)}, u32[]{:S(2)}) copy-start(f32[4096]{0:T(1024)} %get-tuple-element.177) | copy-start | bytes 49156
  813.1 9.3 %copy-start.90 = (f32[1024]{0:T(1024)S(1)}, f32[1024]{0:T(1024)}, u32[]{:S(2)}) copy-start(f32[1024]{0:T(1024)} %get-tuple-element.101) | copy-start | bytes 12292
  813.1 52.5 %copy-start.17 = (f32[512,1024]{1,0:T(8,128)S(1)}, f32[512,1024]{1,0:T(8,128)}, u32[]{:S(2)}) copy-start(f32[512,1024]{1,0:T(8,128)} %copy-done.16) | copy-start | bytes 6291460
  882.6 8.9 copy-start.1
  (75 other events, 298.5 us)
Sparse Core Ops, SparseCore 0:
  15.5 127.3 all-gather.7
  145.5 72.8 all-gather.11
  247.8 38.4 all-gather.9
  288.9 90.0 all-gather.13
  473.6 73.0 all-gather.15
  565.6 87.6 reduce-scatter.4
  656.9 151.9 reduce-scatter.2
  813.1 69.4 all-reduce.9

commit v17 on v14

--- a/solution.py
+++ b/solution.py
@@ -331,6 +331,7 @@
         hidden_grad, up_full, (((1,), (1,)), ((), ())), preferred_element_type=jnp.float32
     )
     up_slots = reduce_halves(up_wgrad_rows, core, 0, 1)
+    down_slots = reduce_halves(down_wgrad_rows, core, 1, 0)
     residual_grad = upstream + norm_back(normed_third, inverse_third, norm_gains[2], third_grad)
     branch_grad = norm_back(normed_second, inverse_second, norm_gains[1], residual_grad).astype(
         jnp.bfloat16
@@ -346,7 +347,7 @@
     out_wgrad_rows = lax.dot_general(
         attn_rows, branch_grad, (((0,), (0,)), ((), ())), preferred_element_type=jnp.float32
     )
-    down_slots, out_slots = reduce_column_halves((down_wgrad_rows, out_wgrad_rows), core)
+    out_slots = reduce_halves(out_wgrad_rows, core, 1, 0)
     qkv_grad = jnp.stack(
         [
             rotate_back(query_grad, cos_table, sine_table),

time: 876 us -> 898 us (1.025)
  matrix products: 196 us -> 213 us
  waiting for transfers between devices: 247 us -> 262 us
  other arithmetic: 130 us -> 121 us
    all_to_all x1, waiting for transfers between devices: 58.6 us -> 78.2 us  [shards(): lax.all_to_all(qkv_grad.reshape(3, group_rows, heads_here, HEAD), 'narrow...]
    all_to_all x1, waiting for transfers between devices: 18.5 us -> 5.66 us  [shards(): attn_grad = lax.all_to_all(attn_grad_rows, 'narrow', 1, 0, tiled=True)]
    reduce_scatter x1 -> x3, waiting for transfers between devices: 0.01 us -> 11.8 us  [reduce_halves(): lax.psum_scatter(chip_sum.astype(jnp.bfloat16), 'narrow', scatter_dimensi...]
    convert_element_type x4, other arithmetic: 36.5 us -> 25.9 us  [attend_backward(): scores_grad = (probs_full * (probs_grad - row_dot)).astype(jnp.bfloat16)]
    convert_element_type x1 -> x3, other arithmetic: 8.06 us -> 18.1 us  [reduce_halves(): chip_sum.astype(jnp.bfloat16)]
    dot_general x4, matrix products: 20.7 us -> 30.4 us  [attend_forward(): jnp.einsum('bhqk,bkhd->bqhd', probs_low, values[:, :key_stop], preferred_...]
    dot_general x4, matrix products: 4.36 us -> 13.4 us  [attend_backward(): jnp.einsum('bhqk,bqhd->bkhd', scores_grad, query_block, preferred_element...]
    unnamed x227 -> x217, local copies, waits for them, and re-layouts: 63.9 us -> 63.9 us
  transfers between devices with their start and end apart: 17 -> 18, of which waited for: 7 -> 6; matrix products, arithmetic and copies ran while one was open for 47% -> 49% of each run, Pallas kernels for 0% -> 0%
where the time goes in v17:
time: 898 us; the launch traced here: 885 us
  waiting for transfers between devices  262 us (29%)
  matrix products  213 us (24%)
  local copies, waits for them, and re-layouts  176 us (20%)
  other arithmetic  121 us (13%)
  blocking collectives  83.5 us (9%)
  between operations  15.7 us (2%)
  starting transfers between devices  13.8 us (2%)
    all_gather x1, waiting for transfers between devices, shards(): gathered_first = lax.all_gather(low_first, 'narrow', axis=0, tiled=True)  93.8 us
    all_to_all x1, waiting for transfers between devices, shards(): lax.all_to_all(qkv_grad.reshape(3, group_rows, heads_here, HEAD), 'narrow...  78.2 us
    unnamed x217, local copies, waits for them, and re-layouts  63.9 us
    all_gather x1, waiting for transfers between devices, shards(): out_full = lax.all_gather(out_weight, 'narrow', axis=0, tiled=True)  57 us
    psum x1, blocking collectives, shards(): lax.psum((gain_local, bias_local, out_blocal, down_blocal, up_bgrad_rows)...  42.6 us
    dot_general x4, matrix products, attend_backward(): jnp.einsum('bqhd,bkhd->bhqk', grad_block, value_block, preferred_element_...  35.1 us
    all_gather x1, blocking collectives, shards(): bias_full = lax.all_gather(bias_flat, 'narrow', axis=0)  33.5 us
    dot_general x4, matrix products, attend_forward(): jnp.einsum('bhqk,bkhd->bqhd', probs_low, values[:, :key_stop], preferred_...  30.4 us
  transfers between devices with their start and end apart: 18, of which 6 were waited for; matrix products, arithmetic and copies ran while one was open for 49% of the time, Pallas kernels for 0%

profile of v17, /device:TPU:0, one launch (start us, length us, event | category | flops | bytes accessed | tf_op | source)
XLA Modules:
  0.0 885.4 jit_solution(14103019572010198671)
XLA Ops:
  15.0 33.5 %all-gather.1 = f32[8,1,896]{2,1,0:T(1,128)S(1)} all-gather(f32[1,1,896]{2,1,0:T(1,128)S(1)} %reshape.373), channel_id=2, replica_groups=mesh['wide'=4,'narrow'=8] {'narrow'}, dimensions={0}, use_global_device_ids=true | all-gather | bytes 32256 | tf_op jit(solution)/shard_map/all_gather | solution.py:270
  48.5 93.8 %all-gather.8.cloned.1.call-done = bf16[4096,1024]{1,0:T(8,128)(2,1)} async-done(((bf16[512,1024]{1,0:T(8,128)(2,1)}), bf16[4096,1024]{1,0:T(8,128)(2,1)}) %all-gather.8.cloned.1.call-update) | async-done | bytes 8388624 | tf_op jit(solution)/shard_map/all_gather | solution.py:271
  149.0 7.4 add_bitcast_fusion
  160.6 4.6 copy.116
  165.3 6.0 reshape.380
  171.3 9.9 %fusion.130 = (f32[2,2048,2,32]{3,2,1,0:T(2,128)}, f32[2,2048,2,32]{3,2,1,0:T(2,128)}) fusion(f32[2,2048,2,64]{3,2,1,0:T(2,128)} %reshape.380), kind=kLoop, calls=%fused_computation.275 | loop fusion | bytes 4194304 | tf_op jit(solution)/shard_map/slice | solution.py:41
  181.2 6.4 copy.172
  187.7 6.4 copy.171
  194.1 5.6 reshape.379
  199.7 10.0 %fusion.131 = (f32[2,2048,2,32]{3,2,1,0:T(2,128)}, f32[2,2048,2,32]{3,2,1,0:T(2,128)}) fusion(f32[2,2048,2,64]{3,2,1,0:T(2,128)} %reshape.379), kind=kLoop, calls=%fused_computation.276 | loop fusion | bytes 4194304 | tf_op jit(solution)/shard_map/slice | solution.py:41
  209.7 6.4 copy.170
  216.1 6.7 copy.169
  225.9 3.3 fusion
  229.2 4.5 exponential_reduce_fusion
  233.7 6.1 fusion.1
  239.7 6.7 exponential_reduce_fusion.1
  251.6 17.0 %fusion.66 = bf16[2,512,2,64]{1,3,2,0:T(8,128)(2,1)} fusion(bf16[2,2048,2,64]{1,3,2,0:T(8,128)(2,1)S(1)} %copy.116, f32[2,2,512,1536]{3,2,1,0:T(8,128)} %get-tuple-element.152, f32[2,2,512]{2,1,0:T(2,128)S(1)} %log_add_fusion.1, pred[512,1536]{1,0:T(8,128)(4,1)S(1)} %iota_compare_fusion.1), kind=kOutput, calls=%fused_computation.164 | convolution fusion | flops 415367168 | bytes 14426112 | tf_op jit(solution)/shard_map/bhqk,bkhd->bqhd/dot_general | solution.py:117
  268.6 5.7 fusion.64
  278.2 4.4 fusion.67
  282.8 3.3 fusion.65
  288.9 3.6 all-to-all-start
  293.4 57.0 %all-gather.10.cloned.1.call-done = bf16[1024,1024]{1,0:T(8,128)(2,1)} async-done(((bf16[128,1024]{1,0:T(8,128)(2,1)}), bf16[1024,1024]{1,0:T(8,128)(2,1)}) %all-gather.10.cloned.1.call-update) | async-done | bytes 2097168 | tf_op jit(solution)/shard_map/all_gather | solution.py:282
  351.4 3.3 add_reduce_fusion.1
  358.0 4.1 broadcast_select_fusion.3
  362.0 10.3 %multiply_convert_fusion.3 = (bf16[512,4096]{1,0:T(8,128)(2,1)}, f32[512,4096]{1,0:T(8,128)}) fusion(f32[4096]{0:T(1024)S(1)} %bitcast.194, bf16[512,4096]{1,0:T(8,128)(2,1)} %get-tuple-element.107, bf16[512,4096]{1,0:T(8,128)(2,1)S(1)} %get-tuple-element.106, f32[512,1024]{1,0:T(8,128)S(1)} %get-tuple-element.103, f32[1024]{0:T(1024)S(1)} %bitcast.196, ...), kind=kOutput, calls=%fused_computation.33 | convolution fusion | flops 4326948864 | bytes 23097344 | tf_op jit(solution)/shard_map/dot_general | solution.py:290
  372.3 5.2 broadcast_select_fusion.1
  377.5 9.3 %add_reduce_fusion = (f32[512]{0:T(512)S(1)}, f32[512,1024]{1,0:T(8,128)S(1)}) fusion(f32[1024]{0:T(1024)S(1)} %copy-done.68, bf16[512,4096]{1,0:T(8,128)(2,1)} %get-tuple-element.21, bf16[4096,512]{1,0:T(8,128)(2,1)} %get-tuple-element.105, bf16[4096,512]{1,0:T(8,128)(2,1)} %get-tuple-element.104), kind=kOutput, calls=%fused_computation.128 | convolution fusion | flops 4312792576 | bytes 14686208 | tf_op jit(solution)/shard_map/dot_general | solution.py:294
  391.6 13.3 %convert_reduce_fusion = (f32[4096]{0:T(1024)}, bf16[512,4096]{1,0:T(8,128)(2,1)}) fusion(f32[512,4096]{1,0:T(8,128)} %get-tuple-element.160, f32[4096]{0:T(1024)S(1)} %bitcast.195, bf16[512,1024]{1,0:T(8,128)(2,1)S(1)} %get-tuple-element.98, bf16[4096,512]{1,0:T(8,128)(2,1)} %get-tuple-element.105, bf16[4096,512]{1,0:T(8,128)(2,1)} %get-tuple-element.104), kind=kOutput, calls=%fused_computation.28 | convolution fusion | flops 4339003392 | bytes 22052864 | tf_op jit(solution)/shard_map/dot_general | solution.py:322
  404.9 7.9 multiply_reduce_fusion.5
  412.8 3.8 multiply_reduce_fusion.6
  417.4 3.0 convert_reduce_fusion.3
  424.1 4.3 all-to-all-start.1
  428.4 7.1 fusion.126
  435.6 8.8 fusion.136
  447.2 6.1 dynamic-slice_convert_fusion
  457.9 5.7 all-to-all-done.1
  469.5 10.2 %multiply_reduce_fusion.1 = (f32[2,2,512]{2,1,0:T(2,128)S(1)}, f32[2,2,512,1536]{3,2,1,0:T(8,128)}) fusion(f32[2,2,512,1536]{3,2,1,0:T(8,128)} %get-tuple-element.152, f32[2,2,512]{2,1,0:T(2,128)S(1)} %log_add_fusion.1, pred[512,1536]{1,0:T(8,128)(4,1)S(1)} %copy-done.13, bf16[2,2048,2,64]{1,3,2,0:T(8,128)(2,1)S(1)} %copy-done.32, ...), kind=kOutput, calls=%fused_computation.7 | convolution fusion | flops 418379776 | bytes 27017216 | tf_op jit(solution)/shard_map/bqhd,bkhd->bhqk/dot_general | solution.py:141
  479.7 7.8 multiply_reduce_fusion.2
  487.9 4.8 multiply_convert_fusion.2
  499.5 7.3 multiply_convert_fusion.1
  516.1 8.2 add_convert_fusion
  525.5 15.6 %multiply_reduce_fusion = (f32[2,2,512]{2,1,0:T(2,128)}, f32[2,2,512,2048]{3,2,1,0:T(8,128)}) fusion(f32[2,2,512,2048]{3,2,1,0:T(8,128)} %copy-done.2, f32[2,2,512]{2,1,0:T(2,128)} %copy-done.67, pred[512,2048]{1,0:T(8,128)(4,1)S(1)} %copy-done.9, bf16[2,2048,2,64]{1,3,2,0:T(8,128)(2,1)} %copy-done.31, bf16[2,512,2,64]{1,0,3,2:T(2,128)(2,1)} %get-tuple-element.125), kind=kOutput, calls=%fused_computation.1 | convolution fusion | flops 557840384 | bytes 35930112 | tf_op jit(solution)/shard_map/bqhd,bkhd->bhqk/dot_general | solution.py:141
  541.2 11.1 %multiply_convert_fusion = bf16[2,2,512,2048]{3,2,1,0:T(8,128)(2,1)} fusion(f32[2,2,512,2048]{3,2,1,0:T(8,128)} %get-tuple-element.165, f32[2,2,512,2048]{3,2,1,0:T(8,128)S(1)} %bitcast.159, f32[2,2,512]{2,1,0:T(2,128)} %get-tuple-element.164, f32[2,2,512]{2,1,0:T(2,128)} %copy-done.67, pred[512,2048]{1,0:T(8,128)(4,1)S(1)} %copy-done.9), kind=kLoop, calls=%fused_computation | loop fusion | flops 25165824 | bytes 43008000 | tf_op jit(solution)/shard_map/convert_element_type | solution.py:145
  554.0 5.9 convolution_bitcast_fusion.2
  559.9 7.2 fusion.60
  567.1 7.7 fusion.29
  574.8 5.9 convolution_bitcast_fusion.1
  580.7 7.5 fusion.30
  588.2 8.5 add_convert_fusion.1
  612.9 3.9 pad_maximum_fusion.6
  616.8 14.5 %copy.142 = bf16[3,4096,2,64]{3,2,0,1:T(2,128)(2,1)} copy(bf16[3,4096,2,64]{1,3,2,0:T(8,128)(2,1)} %pad_maximum_fusion.6) | data formatting | bytes 6291456 | tf_op jit(solution)/shard_map/stack | solution.py:351
  631.3 9.0 %reshape.381 = bf16[8,2,98304]{2,1,0:T(2,128)(2,1)} reshape(bf16[4096,3,2,64]{3,2,1,0:T(2,128)(2,1)} %bitcast.166) | data formatting | bytes 6291456
  640.3 4.4 all-to-all-start.2
  655.7 7.4 psum.71
  663.7 8.7 fusion.56
  674.2 78.2 %all-to-all-done.2 = bf16[8,2,98304]{2,1,0:T(2,128)(2,1)} async-done(((bf16[8,2,98304]{2,1,0:T(2,128)(2,1)}), bf16[8,2,98304]{2,1,0:T(2,128)(2,1)}, u32[]{:S(2)}, u32[]{:S(2)}) %all-to-all-start.2) | async-done | bytes 3145760 | tf_op jit(solution)/shard_map/all_to_all | solution.py:360
  752.4 8.7 reshape.382
  761.1 15.3 %copy.161 = bf16[3,8,512,2,64]{2,4,3,1,0:T(8,128)(2,1)} copy(bf16[3,8,512,2,64]{4,3,0,2,1:T(2,128)(2,1)} %bitcast.167) | data formatting | bytes 6291456 | tf_op jit(solution)/shard_map/all_to_all | solution.py:360
  776.4 5.9 broadcast_select_fusion.5
  785.0 11.8 %reduce-scatter.6.cloned.1.call-done = bf16[512,512]{1,0:T(8,128)(2,1)} async-done(((bf16[512,4096]{1,0:T(8,128)(2,1)}), bf16[512,512]{1,0:T(8,128)(2,1)}) %reduce-scatter.6.cloned.1.call-update) | async-done | bytes 524304 | tf_op jit(solution)/shard_map/reduce_scatter | solution.py:200
  799.1 9.2 %fusion.45 = (f32[1024]{0:T(1024)S(1)}, f32[512]{0:T(512)S(1)}, f32[512]{0:T(512)S(1)}, f32[1024]{0:T(1024)S(1)}, f32[512,1024,1]{1,0,2:T(8,128)}) fusion(bf16[512,1024]{1,0:T(8,128)(2,1)S(1)} %copy-done.11, f32[512]{0:T(512)S(1)} %copy-done.74, f32[512]{0:T(512)S(1)} %copy-done.72, f32[1024]{0:T(1024)S(1)} %bitcast.181, ...), kind=kOutput, calls=%fused_computation.90 | convolution fusion | flops 3239048192 | bytes 12603392 | tf_op jit(solution)/shard_map/tse,tde->sd/dot_general | solution.py:366
  808.4 42.6 %all-reduce.6 = (f32[1024]{0:T(1024)}, f32[4096]{0:T(1024)S(1)}, f32[1024]{0:T(1024)}, f32[4,1024]{1,0:T(4,128)}, f32[4,1024]{1,0:T(4,128)}) all-reduce(f32[1024]{0:T(1024)S(1)} %copy-done.81, f32[4096]{0:T(1024)S(1)} %copy-done.80, f32[1024]{0:T(1024)S(1)} %copy-done.75, ...), channel_id=1, replica_groups=mesh['wide'=4,'narrow'=8] {'wide','narrow'}, use_global_device_ids=true, to_apply=%region_36.37 | all-reduce | flops 14336 | bytes 114688 | tf_op jit(solution)/shard_map/psum | solution.py:398
  851.6 3.3 fusion.44
  854.9 14.5 %all-reduce.10.cloned.1.call-done = (bf16[3,1024,128]{1,2,0:T(8,128)(2,1)}, bf16[128,1024]{0,1:T(8,128)(2,1)}, bf16[512,1024]{0,1:T(8,128)(2,1)}, bf16[1024,512]{1,0:T(8,128)(2,1)}) async-done(((bf16[3,1024,128]{1,2,0:T(8,128)(2,1)}, bf16[128,1024]{0,1:T(8,128)(2,1)}, bf16[512,1024]{0,1:T(8,128)(2,1)}, bf16[1024,512]{1,0:T(8,128)(2,1)}), (bf16[3,1024,128]{1,2,0:T(8,128)(2,1)}, bf16[128,1024]{0,1:T(8,128)(2,1)}, ...) | async-done | bytes 3145744 | tf_op jit(solution)/shard_map/psum | solution.py:391
  (357 shorter events, 124.1 us)
Async XLA Ops:
  7.2 135.2 %copy-start = (bf16[1024,512]{1,0:T(8,128)(2,1)S(1)}, bf16[1024,512]{1,0:T(8,128)(2,1)}, u32[]{:S(2)}) copy-start(bf16[1024,512]{1,0:T(8,128)(2,1)} %param.22) | copy-start | bytes 3145732
  7.2 136.0 %copy-start.61 = (bf16[512,1024]{1,0:T(8,128)(2,1)S(1)}, bf16[512,1024]{1,0:T(8,128)(2,1)}, u32[]{:S(2)}) copy-start(bf16[512,1024]{1,0:T(8,128)(2,1)} %param.24) | copy-start | bytes 3145732
  7.2 135.1 %all-gather.8.cloned.1.call-start = ((), (), s32[]{:S(2)}) async-start(), calls=%async_computation.6 | async-start | bytes 9437184 | tf_op jit(solution)/shard_map/all_gather | solution.py:271
  9.1 135.0 %copy-start.69 = (f32[1,1024]{1,0:T(1,128)}, f32[1,1024]{1,0:T(1,128)S(1)}, u32[]{:S(2)}) copy-start(f32[1,1024]{1,0:T(1,128)S(1)} %get-tuple-element.141) | copy-start | bytes 12292
  10.5 135.7 %copy-start.71 = (f32[512]{0:T(512)}, f32[512]{0:T(512)S(1)}, u32[]{:S(2)}) copy-start(f32[512]{0:T(512)S(1)} %broadcast_multiply_fusion.11) | copy-start | bytes 6148
  12.2 135.9 %copy-start.73 = (f32[512]{0:T(512)}, f32[512]{0:T(512)S(1)}, u32[]{:S(2)}) copy-start(f32[512]{0:T(512)S(1)} %add_rsqrt_fusion.3) | copy-start | bytes 6148
  14.8 134.1 %copy-start.63 = (bf16[3,1024,128]{2,1,0:T(8,128)(2,1)S(1)}, bf16[3,1024,128]{2,1,0:T(8,128)(2,1)}, u32[]{:S(2)}) copy-start(bf16[3,1024,128]{2,1,0:T(8,128)(2,1)} %param.18) | copy-start | bytes 2359300
  14.9 267.8 %all-gather.12.cloned.1.call-start = ((), (), s32[]{:S(2)}) async-start(), calls=%async_computation.8 | async-start | bytes 4718592 | tf_op jit(solution)/shard_map/all_gather | solution.py:181
  143.2 149.6 %all-gather.14.cloned.1.call-start = ((), (), s32[]{:S(2)}) async-start(), calls=%async_computation.9 | async-start | bytes 4718592 | tf_op jit(solution)/shard_map/all_gather | solution.py:181
  144.1 206.2 %all-gather.10.cloned.1.call-start = ((), (), s32[]{:S(2)}) async-start(), calls=%async_computation.7 | async-start | bytes 2359296 | tf_op jit(solution)/shard_map/all_gather | solution.py:282
  146.2 131.9 %copy-start.8 = (pred[512,2048]{1,0:T(8,128)(4,1)}, pred[512,2048]{1,0:T(8,128)(4,1)S(1)}, u32[]{:S(2)}) copy-start(pred[512,2048]{1,0:T(8,128)(4,1)S(1)} %iota_compare_fusion) | copy-start | bytes 3145732
  148.6 103.0 %copy-start.12 = (pred[512,1536]{1,0:T(8,128)(4,1)}, pred[512,1536]{1,0:T(8,128)(4,1)S(1)}, u32[]{:S(2)}) copy-start(pred[512,1536]{1,0:T(8,128)(4,1)S(1)} %iota_compare_fusion.1) | copy-start | bytes 2359300
  149.0 119.6 %copy-start.23 = (pred[512,1024]{1,0:T(8,128)(4,1)}, pred[512,1024]{1,0:T(8,128)(4,1)S(1)}, u32[]{:S(2)}) copy-start(pred[512,1024]{1,0:T(8,128)(4,1)S(1)} %iota_compare_fusion.2) | copy-start | bytes 1572868
  165.3 117.5 %copy-start.31 = (bf16[2,2048,2,64]{1,3,2,0:T(8,128)(2,1)}, bf16[2,2048,2,64]{1,3,2,0:T(8,128)(2,1)S(1)}, u32[]{:S(2)}) copy-start(bf16[2,2048,2,64]{1,3,2,0:T(8,128)(2,1)S(1)} %copy.116) | copy-start | bytes 3145732
  225.8 20.8 %copy-start.26 = (bf16[2,2048,2,32]{1,3,2,0:T(8,128)(2,1)}, bf16[2,2048,2,32]{1,3,2,0:T(8,128)(2,1)S(1)}, u32[]{:S(2)}) copy-start(bf16[2,2048,2,32]{1,3,2,0:T(8,128)(2,1)S(1)} %get-tuple-element.120) | copy-start | bytes 1572868
  225.8 20.8 %copy-start.29 = (bf16[2,2048,2,32]{1,3,2,0:T(8,128)(2,1)}, bf16[2,2048,2,32]{1,3,2,0:T(8,128)(2,1)S(1)}, u32[]{:S(2)}) copy-start(bf16[2,2048,2,32]{1,3,2,0:T(8,128)(2,1)S(1)} %get-tuple-element.121) | copy-start | bytes 1572868
  225.8 48.5 %copy-start.15 = (bf16[2,2048,2,32]{1,3,2,0:T(8,128)(2,1)}, bf16[2,2048,2,32]{1,3,2,0:T(8,128)(2,1)S(1)}, u32[]{:S(2)}) copy-start(bf16[2,2048,2,32]{1,3,2,0:T(8,128)(2,1)S(1)} %get-tuple-element.135) | copy-start | bytes 1572868
  225.8 48.5 %copy-start.18 = (bf16[2,2048,2,32]{1,3,2,0:T(8,128)(2,1)}, bf16[2,2048,2,32]{1,3,2,0:T(8,128)(2,1)S(1)}, u32[]{:S(2)}) copy-start(bf16[2,2048,2,32]{1,3,2,0:T(8,128)(2,1)S(1)} %get-tuple-element.136) | copy-start | bytes 1572868
  225.9 48.4 %copy-start.44 = (bf16[2,512,2,64]{1,3,2,0:T(8,128)(2,1)}, bf16[2,512,2,64]{1,3,2,0:T(8,128)(2,1)S(1)}, u32[]{:S(2)}) copy-start(bf16[2,512,2,64]{1,3,2,0:T(8,128)(2,1)S(1)} %get-tuple-element.176) | copy-start | bytes 786436
  229.2 49.0 %copy-start.2 = (f32[2,2,512,2048]{3,2,1,0:T(8,128)}, f32[2,2,512,2048]{3,2,1,0:T(8,128)S(1)}, u32[]{:S(2)}) copy-start(f32[2,2,512,2048]{3,2,1,0:T(8,128)S(1)} %get-tuple-element.150) | copy-start | bytes 50331652
  233.7 44.5 %copy-start.67 = (f32[2,2,512]{2,1,0:T(2,128)}, f32[2,2,512]{2,1,0:T(2,128)S(1)}, u32[]{:S(2)}) copy-start(f32[2,2,512]{2,1,0:T(2,128)S(1)} %log_add_fusion) | copy-start | bytes 24580
  251.6 235.9 %copy-start.65 = (f32[2,2,512]{2,1,0:T(2,128)}, f32[2,2,512]{2,1,0:T(2,128)S(1)}, u32[]{:S(2)}) copy-start(f32[2,2,512]{2,1,0:T(2,128)S(1)} %log_add_fusion.2) | copy-start | bytes 24580
  282.7 73.5 %collective-permute-start = (bf16[512,4096]{1,0:T(8,128)(2,1)}, bf16[512,4096]{1,0:T(8,128)(2,1)}, u32[]{:S(2)}, u32[]{:S(2)}) collective-permute-start(bf16[512,4096]{1,0:T(8,128)(2,1)} %all-gather.12.cloned.1.call-done), channel_id=1, source_target_pairs={{0,8},{8,0},{16,24},{24,16},{1,9},{9,1},{17,25},{25,17},{2,10},{10... | collective-permute-start | bytes 12582920 | tf_op jit(solution)/shard_map/ppermute | solution.py:175
  286.3 65.1 %copy-start.60 = (f32[1024]{0:T(1024)S(1)}, f32[1024]{0:T(1024)}, u32[]{:S(2)}) copy-start(f32[1024]{0:T(1024)} %param.21) | copy-start | bytes 12292
  288.9 61.4 %all-to-all-start = ((bf16[8,512,128]{1,2,0:T(8,128)(2,1)}), bf16[8,512,128]{1,2,0:T(8,128)(2,1)S(1)}, u32[]{:S(2)}, u32[]{:S(2)}) async-start(bf16[8,512,128]{1,2,0:T(8,128)(2,1)} %copy.128), calls=%async_computation | async-start | bytes 2097152 | tf_op jit(solution)/shard_map/all_to_all | solution.py:281
  292.5 62.5 %copy-start.10 = (bf16[512,1024]{1,0:T(8,128)(2,1)S(1)}, bf16[512,1024]{1,0:T(8,128)(2,1)}, u32[]{:S(2)}) copy-start(bf16[512,1024]{1,0:T(8,128)(2,1)} %param.14) | copy-start | bytes 3145732
  292.5 352.3 %all-gather.16.cloned.1.call-start = ((), (), s32[]{:S(2)}) async-start(), calls=%async_computation.10 | async-start | bytes 3538944 | tf_op jit(solution)/shard_map/all_gather | solution.py:181
  292.8 79.5 %collective-permute-start.1 = (bf16[4096,512]{1,0:T(8,128)(2,1)}, bf16[4096,512]{1,0:T(8,128)(2,1)}, u32[]{:S(2)}, u32[]{:S(2)}) collective-permute-start(bf16[4096,512]{1,0:T(8,128)(2,1)} %all-gather.14.cloned.1.call-done), channel_id=1, source_target_pairs={{0,8},{8,0},{16,24},{24,16},{1,9},{9,1},{17,25},{25,17},{2,10},{10... | collective-permute-start | bytes 12582920 | tf_op jit(solution)/shard_map/ppermute | solution.py:175
  355.8 57.0 %copy-start.6 = (f32[512,1024]{1,0:T(8,128)}, f32[512,1024]{1,0:T(8,128)S(1)}, u32[]{:S(2)}) copy-start(f32[512,1024]{1,0:T(8,128)S(1)} %get-tuple-element.103) | copy-start | bytes 6291460
  362.0 10.3 %copy-start.38 = (bf16[4096,512]{1,0:T(8,128)(2,1)S(1)}, bf16[4096,512]{1,0:T(8,128)(2,1)}, u32[]{:S(2)}) copy-start(bf16[4096,512]{1,0:T(8,128)(2,1)} %all-gather.14.cloned.1.call-done) | copy-start | bytes 12582916
  391.6 13.3 %copy-start.54 = (bf16[512,1024]{1,0:T(8,128)(2,1)}, bf16[512,1024]{1,0:T(8,128)(2,1)S(1)}, u32[]{:S(2)}) copy-start(bf16[512,1024]{1,0:T(8,128)(2,1)S(1)} %get-tuple-element.98) | copy-start | bytes 3145732
  391.6 13.3 %copy-start.40 = (bf16[512,4096]{1,0:T(8,128)(2,1)S(1)}, bf16[512,4096]{1,0:T(8,128)(2,1)}, u32[]{:S(2)}) copy-start(bf16[512,4096]{1,0:T(8,128)(2,1)} %get-tuple-element.107) | copy-start | bytes 12582916
  424.1 39.4 %all-to-all-start.1 = ((bf16[512,8,128]{0,2,1:T(8,128)(2,1)}), bf16[512,8,128]{0,2,1:T(8,128)(2,1)}, u32[]{:S(2)}, u32[]{:S(2)}) async-start(bf16[512,8,128]{0,2,1:T(8,128)(2,1)} %bitcast.17), calls=%async_computation.1 | async-start | bytes 2097152 | tf_op jit(solution)/shard_map/all_to_all | solution.py:342
  428.4 244.0 %reduce-scatter.4.cloned.1.call-start = ((), (), s32[]{:S(2)}) async-start(), calls=%async_computation.11 | async-start | bytes 1179648 | tf_op jit(solution)/shard_map/reduce_scatter | solution.py:200
  435.6 17.9 %copy-start.35 = (f32[1024,4096]{1,0:T(8,128)}, f32[1024,4096]{1,0:T(8,128)S(1)}, u32[]{:S(2)}) copy-start(f32[1024,4096]{1,0:T(8,128)S(1)} %fusion.126) | copy-start | bytes 50331652
  447.1 9.2 %collective-permute-start.3 = (bf16[1024,512]{1,0:T(8,128)(2,1)}, bf16[1024,512]{1,0:T(8,128)(2,1)S(1)}, u32[]{:S(2)}, u32[]{:S(2)}) collective-permute-start(bf16[1024,512]{1,0:T(8,128)(2,1)} %dynamic-slice_convert_fusion.2), channel_id=1, source_target_pairs={{0,8},{8,0},{16,24},{24,16},{1,9},{9,1},{17,25},{25,17},{2,10},{10... | collective-permute-start | bytes 3145736 | tf_op jit(solution)/shard_map/ppermute | solution.py:175
  453.3 62.8 %collective-permute-start.5 = (bf16[4096,512]{1,0:T(8,128)(2,1)}, bf16[4096,512]{1,0:T(8,128)(2,1)}, u32[]{:S(2)}, u32[]{:S(2)}) collective-permute-start(bf16[4096,512]{1,0:T(8,128)(2,1)} %dynamic-slice_convert_fusion), channel_id=1, source_target_pairs={{0,8},{8,0},{16,24},{24,16},{1,9},{9,1},{17,25},{25,17},{2,10},{10... | collective-permute-start | bytes 12582920 | tf_op jit(solution)/shard_map/ppermute | solution.py:175
  456.1 132.1 %collective-permute-start.4 = (bf16[512,4096]{1,0:T(8,128)(2,1)}, bf16[512,4096]{1,0:T(8,128)(2,1)}, u32[]{:S(2)}, u32[]{:S(2)}) collective-permute-start(bf16[512,4096]{1,0:T(8,128)(2,1)} %dynamic-slice_convert_fusion.1), channel_id=1, source_target_pairs={{0,8},{8,0},{16,24},{24,16},{1,9},{9,1},{17,25},{25,17},{2,10},{10... | collective-permute-start | bytes 12582920 | tf_op jit(solution)/shard_map/ppermute | solution.py:175
  457.8 11.7 %copy-start.13 = (pred[512,1536]{1,0:T(8,128)(4,1)S(1)}, pred[512,1536]{1,0:T(8,128)(4,1)}, u32[]{:S(2)}) copy-start(pred[512,1536]{1,0:T(8,128)(4,1)} %copy-done.12) | copy-start | bytes 2359300
  457.8 11.7 %copy-start.32 = (bf16[2,2048,2,64]{1,3,2,0:T(8,128)(2,1)S(1)}, bf16[2,2048,2,64]{1,3,2,0:T(8,128)(2,1)}, u32[]{:S(2)}) copy-start(bf16[2,2048,2,64]{1,3,2,0:T(8,128)(2,1)} %copy-done.31) | copy-start | bytes 3145732
  457.8 324.5 %reduce-scatter.8.cloned.1.call-start = ((), (), s32[]{:S(2)}) async-start(), calls=%async_computation.13 | async-start | bytes 4718592 | tf_op jit(solution)/shard_map/reduce_scatter | solution.py:200
  487.9 11.5 %slice-start.4 = ((s8[12582912]{0:T(1024)(128)(4,1)}), s8[4194304]{0:T(1024)(128)(4,1)S(1)}, s32[]{:S(2)}) async-start(s8[12582912]{0:T(1024)(128)(4,1)} %bitcast.160), calls=%async_computation.19 | async-start | bytes 8388608
  487.9 11.5 %slice-start.5 = ((s8[12582912]{0:T(1024)(128)(4,1)}), s8[4194304]{0:T(1024)(128)(4,1)S(1)}, s32[]{:S(2)}) async-start(s8[12582912]{0:T(1024)(128)(4,1)} %bitcast.160), calls=%async_computation.20 | async-start | bytes 8388608
  524.3 272.4 %reduce-scatter.6.cloned.1.call-start = ((), (), s32[]{:S(2)}) async-start(), calls=%async_computation.12 | async-start | bytes 4718592 | tf_op jit(solution)/shard_map/reduce_scatter | solution.py:200
  524.4 16.7 %slice-start = ((s8[16777216]{0:T(1024)(128)(4,1)}), s8[4194304]{0:T(1024)(128)(4,1)S(1)}, s32[]{:S(2)}) async-start(s8[16777216]{0:T(1024)(128)(4,1)} %bitcast.158), calls=%async_computation.15 | async-start | bytes 8388608
  525.5 15.6 %slice-start.1 = ((s8[16777216]{0:T(1024)(128)(4,1)}), s8[4194304]{0:T(1024)(128)(4,1)S(1)}, s32[]{:S(2)}) async-start(s8[16777216]{0:T(1024)(128)(4,1)} %bitcast.158), calls=%async_computation.16 | async-start | bytes 8388608
  525.5 15.6 %slice-start.2 = ((s8[16777216]{0:T(1024)(128)(4,1)}), s8[4194304]{0:T(1024)(128)(4,1)S(1)}, s32[]{:S(2)}) async-start(s8[16777216]{0:T(1024)(128)(4,1)} %bitcast.158), calls=%async_computation.17 | async-start | bytes 8388608
  525.5 15.7 %slice-start.3 = ((s8[16777216]{0:T(1024)(128)(4,1)}), s8[4194304]{0:T(1024)(128)(4,1)S(1)}, s32[]{:S(2)}) async-start(s8[16777216]{0:T(1024)(128)(4,1)} %bitcast.158), calls=%async_computation.18 | async-start | bytes 8388608
  541.2 11.2 %copy-start.17 = (bf16[2,2048,2,32]{1,3,2,0:T(8,128)(2,1)S(1)}, bf16[2,2048,2,32]{1,3,2,0:T(8,128)(2,1)}, u32[]{:S(2)}) copy-start(bf16[2,2048,2,32]{1,3,2,0:T(8,128)(2,1)} %copy-done.15) | copy-start | bytes 1572868
  541.2 11.2 %copy-start.20 = (bf16[2,2048,2,32]{1,3,2,0:T(8,128)(2,1)S(1)}, bf16[2,2048,2,32]{1,3,2,0:T(8,128)(2,1)}, u32[]{:S(2)}) copy-start(bf16[2,2048,2,32]{1,3,2,0:T(8,128)(2,1)} %copy-done.18) | copy-start | bytes 1572868
  541.2 11.2 %copy-start.21 = (bf16[2,2,512,512]{2,3,1,0:T(8,128)(2,1)S(1)}, bf16[2,2,512,512]{2,3,1,0:T(8,128)(2,1)}, u32[]{:S(2)}) copy-start(bf16[2,2,512,512]{2,3,1,0:T(8,128)(2,1)} %multiply_convert_fusion.4) | copy-start | bytes 6291460
  541.2 12.8 %copy-start.25 = (pred[512,1024]{1,0:T(8,128)(4,1)S(1)}, pred[512,1024]{1,0:T(8,128)(4,1)}, u32[]{:S(2)}) copy-start(pred[512,1024]{1,0:T(8,128)(4,1)} %copy-done.23) | copy-start | bytes 1572868
  541.2 12.7 %copy-start.53 = (bf16[2,512,2,64]{1,0,3,2:T(2,128)(2,1)S(1)}, bf16[2,512,2,64]{1,0,3,2:T(2,128)(2,1)}, u32[]{:S(2)}) copy-start(bf16[2,512,2,64]{1,0,3,2:T(2,128)(2,1)} %copy-done.52) | copy-start | bytes 786436
  541.2 12.7 %copy-start.66 = (f32[2,2,512]{2,1,0:T(2,128)S(1)}, f32[2,2,512]{2,1,0:T(2,128)}, u32[]{:S(2)}) copy-start(f32[2,2,512]{2,1,0:T(2,128)} %copy-done.65) | copy-start | bytes 24580
  559.9 14.9 %slice-start.7 = ((s8[12582912]{0:T(1024)(128)(4,1)}), s8[4194304]{0:T(1024)(128)(4,1)S(1)}, s32[]{:S(2)}) async-start(s8[12582912]{0:T(1024)(128)(4,1)} %bitcast.162), calls=%async_computation.22 | async-start | bytes 8388608
  559.9 14.9 %slice-start.8 = ((s8[12582912]{0:T(1024)(128)(4,1)}), s8[4194304]{0:T(1024)(128)(4,1)S(1)}, s32[]{:S(2)}) async-start(s8[12582912]{0:T(1024)(128)(4,1)} %bitcast.162), calls=%async_computation.23 | async-start | bytes 8388608
  640.3 112.1 %all-to-all-start.2 = ((bf16[8,2,98304]{2,1,0:T(2,128)(2,1)}), bf16[8,2,98304]{2,1,0:T(2,128)(2,1)}, u32[]{:S(2)}, u32[]{:S(2)}) async-start(bf16[8,2,98304]{2,1,0:T(2,128)(2,1)} %reshape.381), calls=%async_computation.2 | async-start | bytes 6291456 | tf_op jit(solution)/shard_map/all_to_all | solution.py:360
  644.7 224.7 %all-reduce.10.cloned.1.call-start = ((), (), s32[]{:S(2)}) async-start(), calls=%async_computation.14 | async-start | bytes 6291456 | tf_op jit(solution)/shard_map/psum | solution.py:391
  644.8 131.6 %collective-permute-start.2 = (bf16[3,512,1024]{2,1,0:T(8,128)(2,1)}, bf16[3,512,1024]{2,1,0:T(8,128)(2,1)}, u32[]{:S(2)}, u32[]{:S(2)}) collective-permute-start(bf16[3,512,1024]{2,1,0:T(8,128)(2,1)} %all-gather.16.cloned.1.call-done), channel_id=1, source_target_pairs={{0,8},{8,0},{16,24},{24,16},{1,9},{9,1},{17,25},{25,17},{2,10},{10... | collective-permute-start | bytes 9437192 | tf_op jit(solution)/shard_map/ppermute | solution.py:175
  783.6 15.3 %copy-start.11 = (bf16[512,1024]{1,0:T(8,128)(2,1)S(1)}, bf16[512,1024]{1,0:T(8,128)(2,1)}, u32[]{:S(2)}) copy-start(bf16[512,1024]{1,0:T(8,128)(2,1)} %param.14) | copy-start | bytes 3145732
  783.6 15.3 %copy-start.70 = (f32[1,1024]{1,0:T(1,128)S(1)}, f32[1,1024]{1,0:T(1,128)}, u32[]{:S(2)}) copy-start(f32[1,1024]{1,0:T(1,128)} %copy-done.69) | copy-start | bytes 12292
  783.6 15.3 %copy-start.72 = (f32[512]{0:T(512)S(1)}, f32[512]{0:T(512)}, u32[]{:S(2)}) copy-start(f32[512]{0:T(512)} %copy-done.71) | copy-start | bytes 6148
  783.6 15.3 %copy-start.74 = (f32[512]{0:T(512)S(1)}, f32[512]{0:T(512)}, u32[]{:S(2)}) copy-start(f32[512]{0:T(512)} %copy-done.73) | copy-start | bytes 6148
  799.1 52.6 %copy-start.14 = (f32[512,1024]{1,0:T(8,128)S(1)}, f32[512,1024]{1,0:T(8,128)}, u32[]{:S(2)}) copy-start(f32[512,1024]{1,0:T(8,128)} %get-tuple-element.101) | copy-start | bytes 6291460
  (55 other events, 324.0 us)
Sparse Core Ops, SparseCore 0:
  15.0 127.3 all-gather.7
  145.0 72.8 all-gather.11
  220.0 70.9 all-gather.13
  293.0 57.3 all-gather.9
  417.5 77.5 all-gather.15
  498.4 62.5 reduce-scatter.3
  564.6 89.1 reduce-scatter.7
  657.4 139.2 reduce-scatter.5
  799.9 69.4 all-reduce.9

commit v18 on v14

--- a/solution.py
+++ b/solution.py
@@ -228,6 +228,30 @@
             jnp.stack([jnp.where(core == 0, part, empty), jnp.where(core == 0, empty, part)], axis=1)
         )
     return results
+
+
+def swap_pairs(block):
+    count = lax.axis_size("wide")
+    return lax.ppermute(block, "wide", [(index, index ^ 2) for index in range(count)])
+
+
+def sum_slots(slots, core, split_axis):
+    if lax.axis_size("wide") != 4:
+        return merge_slots(lax.psum(slots, "wide"), split_axis).astype(jnp.float32)
+    part = lax.dynamic_index_in_dim(slots, core, axis=split_axis, keepdims=False)
+    pair_sum = part.astype(jnp.float32) + swap_pairs(part).astype(jnp.float32)
+    other = swap_cores(pair_sum)
+    first = jnp.where(core == 0, pair_sum, other)
+    second = jnp.where(core == 0, other, pair_sum)
+    return jnp.concatenate([first, second], axis=split_axis)
+
+
+def sum_wide(block):
+    low_block = block.astype(jnp.bfloat16)
+    if lax.axis_size("wide") != 4:
+        return lax.psum(low_block, "wide").astype(jnp.float32)
+    pair_sum = low_block.astype(jnp.float32) + swap_pairs(low_block).astype(jnp.float32)
+    return pair_sum + swap_cores(pair_sum)
 
 
 def merge_slots(slots, split_axis):
@@ -387,21 +411,21 @@
     out_blocal = jnp.sum(branch_grad.astype(jnp.float32), axis=0)
     down_blocal = jnp.sum(mlp_grad.astype(jnp.float32), axis=0)
     weight_sums = (
-        lax.psum(qkv_wgrad.astype(jnp.bfloat16), "wide").astype(jnp.float32),
-        lax.psum(qkv_bgrad.astype(jnp.bfloat16), "wide").astype(jnp.float32),
-        lax.psum(out_slots, "wide").astype(jnp.float32),
-        lax.psum(up_slots, "wide").astype(jnp.float32),
+        sum_wide(qkv_wgrad),
+        sum_wide(qkv_bgrad),
+        sum_slots(out_slots, core, 1),
+        sum_slots(up_slots, core, 0),
         None,
-        lax.psum(down_slots, "wide").astype(jnp.float32),
+        sum_slots(down_slots, core, 1),
     )
     small_sums = lax.psum(
         (gain_local, bias_local, out_blocal, down_blocal, up_bgrad_rows), ("wide", "narrow")
     )
     units = up_bias.shape[0]
     up_bgrad = lax.dynamic_slice_in_dim(small_sums[4], lax.axis_index("narrow") * units, units)
-    up_wgrad = merge_slots(weight_sums[3], 0)
-    down_wgrad = merge_slots(weight_sums[5], 1)
-    out_wgrad = merge_slots(weight_sums[2], 1)
+    up_wgrad = weight_sums[3]
+    down_wgrad = weight_sums[5]
+    out_wgrad = weight_sums[2]
     qkv_wgrad = weight_sums[0]
     return (
         layer_out,

time: 876 us -> 892 us (1.018)
  waiting for transfers between devices: 247 us -> 260 us
  local copies, waits for them, and re-layouts: 184 us -> 173 us
    ppermute x0 -> x5, waiting for transfers between devices: none -> 31.3 us  [swap_pairs(): lax.ppermute(block, 'wide', [(index, index ^ 2) for index in range(count)])]
    psum x1 -> x0, waiting for transfers between devices: 13.7 us -> none  [shards(): lax.psum(qkv_wgrad.astype(jnp.bfloat16), 'wide').astype(jnp.float32)]
    unnamed x227 -> x221, local copies, waits for them, and re-layouts: 63.9 us -> 59.4 us
  transfers between devices with their start and end apart: 17 -> 26, of which waited for: 7 -> 10; matrix products, arithmetic and copies ran while one was open for 47% -> 47% of each run, Pallas kernels for 0% -> 0%
where the time goes in v18:
time: 892 us; the launch traced here: 880 us
  waiting for transfers between devices  260 us (29%)
  matrix products  201 us (23%)
  local copies, waits for them, and re-layouts  173 us (19%)
  other arithmetic  128 us (14%)
  blocking collectives  80 us (9%)
  starting transfers between devices  22.1 us (2%)
  between operations  16 us (2%)
    all_gather x1, waiting for transfers between devices, shards(): gathered_first = lax.all_gather(low_first, 'narrow', axis=0, tiled=True)  93.8 us
    unnamed x221, local copies, waits for them, and re-layouts  59.4 us
    all_gather x1, waiting for transfers between devices, shards(): out_full = lax.all_gather(out_weight, 'narrow', axis=0, tiled=True)  57.9 us
    all_to_all x1, waiting for transfers between devices, shards(): lax.all_to_all(qkv_grad.reshape(3, group_rows, heads_here, HEAD), 'narrow...  52.9 us
    psum x1, blocking collectives, shards(): lax.psum((gain_local, bias_local, out_blocal, down_blocal, up_bgrad_rows)...  46.5 us
    all_gather x1, blocking collectives, shards(): bias_full = lax.all_gather(bias_flat, 'narrow', axis=0)  33.5 us
    convert_element_type x4, other arithmetic, attend_backward(): scores_grad = (probs_full * (probs_grad - row_dot)).astype(jnp.bfloat16)  31.6 us
    dot_general x4, matrix products, attend_backward(): jnp.einsum('bqhd,bkhd->bhqk', grad_block, value_block, preferred_element_...  31.4 us
  transfers between devices with their start and end apart: 26, of which 10 were waited for; matrix products, arithmetic and copies ran while one was open for 47% of the time, Pallas kernels for 0%

profile of v18, /device:TPU:0, one launch (start us, length us, event | category | flops | bytes accessed | tf_op | source)
XLA Modules:
  0.0 879.7 jit_solution(7858878488365304629)
XLA Ops:
  15.0 33.5 %all-gather.1 = f32[8,1,896]{2,1,0:T(1,128)S(1)} all-gather(f32[1,1,896]{2,1,0:T(1,128)S(1)} %reshape.411), channel_id=2, replica_groups=mesh['wide'=4,'narrow'=8] {'narrow'}, dimensions={0}, use_global_device_ids=true | all-gather | bytes 32256 | tf_op jit(solution)/shard_map/all_gather | solution.py:294
  48.5 93.8 %all-gather.8.cloned.1.call-done = bf16[4096,1024]{1,0:T(8,128)(2,1)} async-done(((bf16[512,1024]{1,0:T(8,128)(2,1)}), bf16[4096,1024]{1,0:T(8,128)(2,1)}) %all-gather.8.cloned.1.call-update) | async-done | bytes 8388624 | tf_op jit(solution)/shard_map/all_gather | solution.py:295
  149.1 7.2 add_bitcast_fusion
  160.5 5.9 copy.108
  166.4 5.7 reshape.418
  172.0 9.8 %fusion.138 = (f32[2,2048,2,32]{3,2,1,0:T(2,128)}, f32[2,2048,2,32]{3,2,1,0:T(2,128)}) fusion(f32[2,2048,2,64]{3,2,1,0:T(2,128)} %reshape.418), kind=kLoop, calls=%fused_computation.301 | loop fusion | bytes 4194304 | tf_op jit(solution)/shard_map/slice | solution.py:41
  181.8 6.4 copy.160
  188.3 6.4 copy.159
  194.7 5.7 reshape.417
  200.4 9.8 %fusion.139 = (f32[2,2048,2,32]{3,2,1,0:T(2,128)}, f32[2,2048,2,32]{3,2,1,0:T(2,128)}) fusion(f32[2,2048,2,64]{3,2,1,0:T(2,128)} %reshape.417), kind=kLoop, calls=%fused_computation.302 | loop fusion | bytes 4194304 | tf_op jit(solution)/shard_map/slice | solution.py:41
  210.2 6.5 copy.158
  216.6 6.6 copy.157
  229.7 4.5 exponential_reduce_fusion
  234.2 6.0 fusion.1
  240.2 6.8 exponential_reduce_fusion.1
  252.5 7.7 fusion.66
  260.2 5.7 fusion.64
  269.8 4.4 fusion.67
  274.3 3.5 fusion.65
  282.7 4.4 all-to-all-start
  287.4 3.6 all-gather.14.cloned.1.call-done
  291.0 57.9 %all-gather.10.cloned.1.call-done = bf16[1024,1024]{1,0:T(8,128)(2,1)} async-done(((bf16[128,1024]{1,0:T(8,128)(2,1)}), bf16[1024,1024]{1,0:T(8,128)(2,1)}) %all-gather.10.cloned.1.call-update) | async-done | bytes 2097168 | tf_op jit(solution)/shard_map/all_gather | solution.py:306
  354.8 3.9 broadcast_select_fusion.3
  358.7 10.3 %multiply_convert_fusion.3 = (bf16[512,4096]{1,0:T(8,128)(2,1)}, f32[512,4096]{1,0:T(8,128)}) fusion(f32[4096]{0:T(1024)S(1)} %bitcast.198, bf16[512,4096]{1,0:T(8,128)(2,1)} %get-tuple-element.103, bf16[512,4096]{1,0:T(8,128)(2,1)S(1)} %get-tuple-element.102, f32[512,1024]{1,0:T(8,128)S(1)} %get-tuple-element.99, f32[1024]{0:T(1024)S(1)} %bitcast.202, ...), kind=kOutput, calls=%fused_computation.33 | convolution fusion | flops 4326948864 | bytes 23097344 | tf_op jit(solution)/shard_map/dot_general | solution.py:314
  369.0 5.1 broadcast_select_fusion.1
  374.1 9.3 %add_reduce_fusion = (f32[512]{0:T(512)S(1)}, f32[512,1024]{1,0:T(8,128)S(1)}) fusion(f32[1024]{0:T(1024)S(1)} %copy-done.70, bf16[512,4096]{1,0:T(8,128)(2,1)} %get-tuple-element.21, bf16[4096,512]{1,0:T(8,128)(2,1)} %get-tuple-element.101, bf16[4096,512]{1,0:T(8,128)(2,1)} %get-tuple-element.100), kind=kOutput, calls=%fused_computation.131 | convolution fusion | flops 4312792576 | bytes 14686208 | tf_op jit(solution)/shard_map/dot_general | solution.py:318
  388.2 8.4 fusion.143
  396.6 12.4 %convert_reduce_fusion = (f32[4096]{0:T(1024)}, bf16[512,4096]{1,0:T(8,128)(2,1)}) fusion(f32[512,4096]{1,0:T(8,128)} %get-tuple-element.162, f32[4096]{0:T(1024)S(1)} %bitcast.199, bf16[512,1024]{1,0:T(8,128)(2,1)S(1)} %get-tuple-element.94, bf16[4096,512]{1,0:T(8,128)(2,1)} %get-tuple-element.101, bf16[4096,512]{1,0:T(8,128)(2,1)} %get-tuple-element.100), kind=kOutput, calls=%fused_computation.26 | convolution fusion | flops 4339003392 | bytes 22052864 | tf_op jit(solution)/shard_map/dot_general | solution.py:346
  409.0 9.2 %multiply_reduce_fusion.5 = (f32[1024]{0:T(1024)}, f32[512]{0:T(512)S(1)}, f32[512]{0:T(512)S(1)}, f32[1024]{0:T(1024)}, f32[512,1024]{1,0:T(8,128)S(1)}) fusion(f32[512,1024]{1,0:T(8,128)S(1)} %get-tuple-element.99, f32[512]{0:T(512)S(1)} %add_rsqrt_fusion.1, f32[512]{0:T(512)S(1)} %broadcast_multiply_fusion.9, f32[1024]{0:T(1024)S(1)} %bitcast.190, ...), kind=kOutput, calls=%fused_computation.103 | convolution fusion | flops 4316460032 | bytes 16797696 | tf_op jit(solution)/shard_map/dot_general | solution.py:354
  418.3 10.5 %fusion.134 = f32[1024,4096]{1,0:T(8,128)} fusion(bf16[512,4096]{1,0:T(8,128)(2,1)} %get-tuple-element.176, f32[512,1024]{1,0:T(8,128)S(1)} %get-tuple-element.99, f32[1024]{0:T(1024)S(1)} %bitcast.203, f32[1024]{0:T(1024)S(1)} %bitcast.191, f32[512]{0:T(512)S(1)} %add_rsqrt_fusion.1, f32[512]{0:T(512)S(1)} %broadcast_multiply_fusion.9), kind=kOutput, calls=%fused_computation.298 | convolution fusion | flops 4297588736 | bytes 23080960 | tf_op jit(solution)/shard_map/dot_general | solution.py:351
  428.8 3.4 multiply_reduce_fusion.6
  437.2 3.6 all-to-all-start.1
  445.8 5.9 dynamic-slice_convert_fusion.1
  452.1 6.2 dynamic-slice_convert_fusion
  459.8 18.5 %all-to-all-done.1 = bf16[512,8,128]{0,2,1:T(8,128)(2,1)S(1)} async-done(((bf16[512,8,128]{0,2,1:T(8,128)(2,1)}), bf16[512,8,128]{0,2,1:T(8,128)(2,1)S(1)}, u32[]{:S(2)}, u32[]{:S(2)}) %all-to-all-start.1) | async-done | bytes 1048608 | tf_op jit(solution)/shard_map/all_to_all | solution.py:365
  483.0 4.7 convolution_bitcast_fusion.3
  487.7 3.5 multiply_reduce_fusion.3
  491.2 5.4 multiply_reduce_fusion.2
  496.6 4.8 multiply_convert_fusion.2
  510.2 10.9 %multiply_reduce_fusion.1 = (f32[2,2,512]{2,1,0:T(2,128)}, f32[2,2,512,1536]{3,2,1,0:T(8,128)}) fusion(f32[2,2,512,1536]{3,2,1,0:T(8,128)} %get-tuple-element.154, f32[2,2,512]{2,1,0:T(2,128)S(1)} %log_add_fusion.1, pred[512,1536]{1,0:T(8,128)(4,1)S(1)} %copy-done.9, bf16[2,2048,2,64]{1,3,2,0:T(8,128)(2,1)S(1)} %copy-done.31, ...), kind=kOutput, calls=%fused_computation.7 | convolution fusion | flops 418379776 | bytes 27017216 | tf_op jit(solution)/shard_map/bqhd,bkhd->bhqk/dot_general | solution.py:141
  521.1 11.6 %multiply_reduce_fusion = (f32[2,2,512]{2,1,0:T(2,128)}, f32[2,2,512,2048]{3,2,1,0:T(8,128)}) fusion(f32[2,2,512,2048]{3,2,1,0:T(8,128)S(1)} %bitcast.164, f32[2,2,512]{2,1,0:T(2,128)} %copy-done.68, pred[512,2048]{1,0:T(8,128)(4,1)S(1)} %iota_compare_fusion, bf16[2,2048,2,64]{1,3,2,0:T(8,128)(2,1)} %copy.108, bf16[2,512,2,64]{1,0,3,2:T(2,128)(2,1)} %get-tuple-element.125), kind=kOutput, calls=%fused_computation.1 | convolution fusion | flops 557840384 | bytes 35930112 | tf_op jit(solution)/shard_map/bqhd,bkhd->bhqk/dot_general | solution.py:141
  532.7 11.8 %multiply_convert_fusion.1 = bf16[2,2,512,1536]{3,2,1,0:T(8,128)(2,1)} fusion(f32[2,2,512,1536]{3,2,1,0:T(8,128)} %get-tuple-element.169, f32[2,2,512,1536]{3,2,1,0:T(8,128)} %get-tuple-element.154, f32[2,2,512]{2,1,0:T(2,128)} %get-tuple-element.168, f32[2,2,512]{2,1,0:T(2,128)S(1)} %log_add_fusion.1, pred[512,1536]{1,0:T(8,128)(4,1)} %copy-done.8), kind=kLoop, calls=%fused_computation.6 | loop fusion | flops 18874368 | bytes 32260096 | tf_op jit(solution)/shard_map/convert_element_type | solution.py:145
  544.5 8.0 add_convert_fusion
  553.7 5.1 fusion.26
  558.9 5.8 fusion.59
  564.7 13.7 %multiply_convert_fusion = bf16[2,2,512,2048]{3,2,1,0:T(8,128)(2,1)S(1)} fusion(f32[2,2,512,2048]{3,2,1,0:T(8,128)} %get-tuple-element.167, f32[2,2,512,2048]{3,2,1,0:T(8,128)} %copy-done.2, f32[2,2,512]{2,1,0:T(2,128)S(1)} %copy-done.75, f32[2,2,512]{2,1,0:T(2,128)S(1)} %copy-done.69, pred[512,2048]{1,0:T(8,128)(4,1)S(1)} %iota_compare_fusion), kind=kLoop, calls=%fused_computation | loop fusion | flops 25165824 | bytes 43008000 | tf_op jit(solution)/shard_map/convert_element_type | solution.py:145
  580.0 3.3 convolution_bitcast_fusion.2
  583.4 3.5 fusion.60
  589.9 8.3 convolution_bitcast_fusion.1
  598.2 7.7 fusion.30
  606.0 6.2 add_convert_fusion.1
  629.3 3.9 pad_maximum_fusion.7
  633.2 14.5 %copy.134 = bf16[3,4096,2,64]{3,2,0,1:T(2,128)(2,1)} copy(bf16[3,4096,2,64]{1,3,2,0:T(8,128)(2,1)} %pad_maximum_fusion.7) | data formatting | bytes 6291456 | tf_op jit(solution)/shard_map/stack | solution.py:374
  647.7 8.9 %reshape.419 = bf16[8,2,98304]{2,1,0:T(2,128)(2,1)} reshape(bf16[4096,3,2,64]{3,2,1,0:T(2,128)(2,1)} %bitcast.171) | data formatting | bytes 6291456
  656.7 4.7 all-to-all-start.2
  669.8 7.9 fusion.56
  679.1 18.6 %collective-permute-done.3 = bf16[3,1024,128]{1,2,0:T(8,128)(2,1)S(1)} collective-permute-done((bf16[3,1024,128]{1,2,0:T(8,128)(2,1)S(1)}, bf16[3,1024,128]{1,2,0:T(8,128)(2,1)S(1)}, u32[]{:S(2)}, u32[]{:S(2)}) %collective-permute-start.3) | collective-permute-done | bytes 786464 | tf_op jit(solution)/shard_map/ppermute | solution.py:235
  709.2 52.9 %all-to-all-done.2 = bf16[8,2,98304]{2,1,0:T(2,128)(2,1)} async-done(((bf16[8,2,98304]{2,1,0:T(2,128)(2,1)}), bf16[8,2,98304]{2,1,0:T(2,128)(2,1)}, u32[]{:S(2)}, u32[]{:S(2)}) %all-to-all-start.2) | async-done | bytes 3145760 | tf_op jit(solution)/shard_map/all_to_all | solution.py:383
  762.1 8.8 reshape.420
  770.9 15.5 %copy.149 = bf16[3,8,512,2,64]{2,4,3,1,0:T(8,128)(2,1)} copy(bf16[3,8,512,2,64]{4,3,0,2,1:T(2,128)(2,1)} %bitcast.172) | data formatting | bytes 6291456 | tf_op jit(solution)/shard_map/all_to_all | solution.py:383
  786.5 3.4 broadcast_select_fusion.5
  790.6 5.3 fusion.45
  802.3 7.8 collective-permute-done.12
  814.3 46.5 %all-reduce.6 = (f32[1024]{0:T(1024)}, f32[4096]{0:T(1024)S(1)}, f32[1024]{0:T(1024)}, f32[4,1024]{1,0:T(4,128)}, f32[4,1024]{1,0:T(4,128)}) all-reduce(f32[1024]{0:T(1024)S(1)} %copy-done.84, f32[4096]{0:T(1024)S(1)} %copy-done.83, f32[1024]{0:T(1024)S(1)} %copy-done.78, ...), channel_id=1, replica_groups=mesh['wide'=4,'narrow'=8] {'wide','narrow'}, use_global_device_ids=true, to_apply=%region_33.34 | all-reduce | flops 14336 | bytes 114688 | tf_op jit(solution)/shard_map/psum | solution.py:421
  (384 shorter events, 142.0 us)
Async XLA Ops:
  7.2 135.2 %copy-start = (bf16[1024,512]{1,0:T(8,128)(2,1)S(1)}, bf16[1024,512]{1,0:T(8,128)(2,1)}, u32[]{:S(2)}) copy-start(bf16[1024,512]{1,0:T(8,128)(2,1)} %param.22) | copy-start | bytes 3145732
  7.2 136.0 %copy-start.63 = (bf16[512,1024]{1,0:T(8,128)(2,1)S(1)}, bf16[512,1024]{1,0:T(8,128)(2,1)}, u32[]{:S(2)}) copy-start(bf16[512,1024]{1,0:T(8,128)(2,1)} %param.24) | copy-start | bytes 3145732
  7.2 135.1 %all-gather.8.cloned.1.call-start = ((), (), s32[]{:S(2)}) async-start(), calls=%async_computation.5 | async-start | bytes 9437184 | tf_op jit(solution)/shard_map/all_gather | solution.py:295
  9.1 135.1 %copy-start.71 = (f32[1,1024]{1,0:T(1,128)}, f32[1,1024]{1,0:T(1,128)S(1)}, u32[]{:S(2)}) copy-start(f32[1,1024]{1,0:T(1,128)S(1)} %get-tuple-element.143) | copy-start | bytes 12292
  10.5 135.0 %copy-start.73 = (f32[512]{0:T(512)}, f32[512]{0:T(512)S(1)}, u32[]{:S(2)}) copy-start(f32[512]{0:T(512)S(1)} %broadcast_multiply_fusion.11) | copy-start | bytes 6148
  12.2 135.2 %copy-start.76 = (f32[512]{0:T(512)}, f32[512]{0:T(512)S(1)}, u32[]{:S(2)}) copy-start(f32[512]{0:T(512)S(1)} %add_rsqrt_fusion.3) | copy-start | bytes 6148
  14.9 134.2 %copy-start.65 = (bf16[3,1024,128]{2,1,0:T(8,128)(2,1)S(1)}, bf16[3,1024,128]{2,1,0:T(8,128)(2,1)}, u32[]{:S(2)}) copy-start(bf16[3,1024,128]{2,1,0:T(8,128)(2,1)} %param.18) | copy-start | bytes 2359300
  14.9 259.4 %all-gather.12.cloned.1.call-start = ((), (), s32[]{:S(2)}) async-start(), calls=%async_computation.7 | async-start | bytes 4718592 | tf_op jit(solution)/shard_map/all_gather | solution.py:181
  143.2 147.8 %all-gather.14.cloned.1.call-start = ((), (), s32[]{:S(2)}) async-start(), calls=%async_computation.8 | async-start | bytes 4718592 | tf_op jit(solution)/shard_map/all_gather | solution.py:181
  144.2 204.7 %all-gather.10.cloned.1.call-start = ((), (), s32[]{:S(2)}) async-start(), calls=%async_computation.6 | async-start | bytes 2359296 | tf_op jit(solution)/shard_map/all_gather | solution.py:306
  147.9 104.6 %copy-start.8 = (pred[512,1536]{1,0:T(8,128)(4,1)}, pred[512,1536]{1,0:T(8,128)(4,1)S(1)}, u32[]{:S(2)}) copy-start(pred[512,1536]{1,0:T(8,128)(4,1)S(1)} %iota_compare_fusion.1) | copy-start | bytes 2359300
  210.2 13.1 %copy-start.44 = (f32[2048,32]{0,1:T(8,128)S(1)}, f32[2048,32]{0,1:T(8,128)}, u32[]{:S(2)}) copy-start(f32[2048,32]{0,1:T(8,128)} %get-tuple-element.149) | copy-start | bytes 786436
  226.2 20.8 %copy-start.23 = (bf16[2,2048,2,32]{1,3,2,0:T(8,128)(2,1)}, bf16[2,2048,2,32]{1,3,2,0:T(8,128)(2,1)S(1)}, u32[]{:S(2)}) copy-start(bf16[2,2048,2,32]{1,3,2,0:T(8,128)(2,1)S(1)} %get-tuple-element.116) | copy-start | bytes 1572868
  226.2 20.8 %copy-start.26 = (bf16[2,2048,2,32]{1,3,2,0:T(8,128)(2,1)}, bf16[2,2048,2,32]{1,3,2,0:T(8,128)(2,1)S(1)}, u32[]{:S(2)}) copy-start(bf16[2,2048,2,32]{1,3,2,0:T(8,128)(2,1)S(1)} %get-tuple-element.117) | copy-start | bytes 1572868
  226.3 277.4 %copy-start.13 = (bf16[2,2048,2,32]{1,3,2,0:T(8,128)(2,1)}, bf16[2,2048,2,32]{1,3,2,0:T(8,128)(2,1)S(1)}, u32[]{:S(2)}) copy-start(bf16[2,2048,2,32]{1,3,2,0:T(8,128)(2,1)S(1)} %get-tuple-element.139) | copy-start | bytes 1572868
  226.3 277.4 %copy-start.15 = (bf16[2,2048,2,32]{1,3,2,0:T(8,128)(2,1)}, bf16[2,2048,2,32]{1,3,2,0:T(8,128)(2,1)S(1)}, u32[]{:S(2)}) copy-start(bf16[2,2048,2,32]{1,3,2,0:T(8,128)(2,1)S(1)} %get-tuple-element.140) | copy-start | bytes 1572868
  226.3 39.6 %copy-start.42 = (bf16[2,512,2,64]{1,3,2,0:T(8,128)(2,1)}, bf16[2,512,2,64]{1,3,2,0:T(8,128)(2,1)S(1)}, u32[]{:S(2)}) copy-start(bf16[2,512,2,64]{1,3,2,0:T(8,128)(2,1)S(1)} %get-tuple-element.178) | copy-start | bytes 786436
  229.6 40.1 %copy-start.2 = (f32[2,2,512,2048]{3,2,1,0:T(8,128)}, f32[2,2,512,2048]{3,2,1,0:T(8,128)S(1)}, u32[]{:S(2)}) copy-start(f32[2,2,512,2048]{3,2,1,0:T(8,128)S(1)} %get-tuple-element.152) | copy-start | bytes 50331652
  234.1 35.6 %copy-start.68 = (f32[2,2,512]{2,1,0:T(2,128)}, f32[2,2,512]{2,1,0:T(2,128)S(1)}, u32[]{:S(2)}) copy-start(f32[2,2,512]{2,1,0:T(2,128)S(1)} %log_add_fusion) | copy-start | bytes 24580
  252.5 244.1 %copy-start.66 = (f32[2,2,512]{2,1,0:T(2,128)}, f32[2,2,512]{2,1,0:T(2,128)S(1)}, u32[]{:S(2)}) copy-start(f32[2,2,512]{2,1,0:T(2,128)S(1)} %log_add_fusion.2) | copy-start | bytes 24580
  274.3 79.5 %collective-permute-start = (bf16[512,4096]{1,0:T(8,128)(2,1)}, bf16[512,4096]{1,0:T(8,128)(2,1)}, u32[]{:S(2)}, u32[]{:S(2)}) collective-permute-start(bf16[512,4096]{1,0:T(8,128)(2,1)} %all-gather.12.cloned.1.call-done), channel_id=1, source_target_pairs={{0,8},{8,0},{16,24},{24,16},{1,9},{9,1},{17,25},{25,17},{2,10},{10... | collective-permute-start | bytes 12582920 | tf_op jit(solution)/shard_map/ppermute | solution.py:175
  278.0 70.9 %copy-start.62 = (f32[1024]{0:T(1024)S(1)}, f32[1024]{0:T(1024)}, u32[]{:S(2)}) copy-start(f32[1024]{0:T(1024)} %param.21) | copy-start | bytes 12292
  282.7 66.2 %all-to-all-start = ((bf16[8,512,128]{1,2,0:T(8,128)(2,1)}), bf16[8,512,128]{1,2,0:T(8,128)(2,1)}, u32[]{:S(2)}, u32[]{:S(2)}) async-start(bf16[8,512,128]{1,2,0:T(8,128)(2,1)} %copy.120), calls=%async_computation | async-start | bytes 2097152 | tf_op jit(solution)/shard_map/all_to_all | solution.py:305
  287.1 65.5 %copy-start.6 = (bf16[512,1024]{1,0:T(8,128)(2,1)S(1)}, bf16[512,1024]{1,0:T(8,128)(2,1)}, u32[]{:S(2)}) copy-start(bf16[512,1024]{1,0:T(8,128)(2,1)} %param.14) | copy-start | bytes 3145732
  291.0 78.0 %collective-permute-start.1 = (bf16[4096,512]{1,0:T(8,128)(2,1)}, bf16[4096,512]{1,0:T(8,128)(2,1)}, u32[]{:S(2)}, u32[]{:S(2)}) collective-permute-start(bf16[4096,512]{1,0:T(8,128)(2,1)} %all-gather.14.cloned.1.call-done), channel_id=1, source_target_pairs={{0,8},{8,0},{16,24},{24,16},{1,9},{9,1},{17,25},{25,17},{2,10},{10... | collective-permute-start | bytes 12582920 | tf_op jit(solution)/shard_map/ppermute | solution.py:175
  437.2 41.0 %all-to-all-start.1 = ((bf16[512,8,128]{0,2,1:T(8,128)(2,1)}), bf16[512,8,128]{0,2,1:T(8,128)(2,1)S(1)}, u32[]{:S(2)}, u32[]{:S(2)}) async-start(bf16[512,8,128]{0,2,1:T(8,128)(2,1)} %bitcast.176), calls=%async_computation.1 | async-start | bytes 2097152 | tf_op jit(solution)/shard_map/all_to_all | solution.py:365
  440.8 229.0 %all-gather.16.cloned.1.call-start = ((), (), s32[]{:S(2)}) async-start(), calls=%async_computation.9 | async-start | bytes 3538944 | tf_op jit(solution)/shard_map/all_gather | solution.py:181
  442.7 353.2 %reduce-scatter.5.cloned.1.call-start = ((), (), s32[]{:S(2)}) async-start(), calls=%async_computation.11 | async-start | bytes 4718592 | tf_op jit(solution)/shard_map/reduce_scatter | solution.py:200
  445.7 12.7 %collective-permute-start.8 = (bf16[1024,512]{1,0:T(8,128)(2,1)S(1)}, bf16[1024,512]{1,0:T(8,128)(2,1)S(1)}, u32[]{:S(2)}, u32[]{:S(2)}) collective-permute-start(bf16[1024,512]{1,0:T(8,128)(2,1)S(1)} %dynamic-slice_convert_fusion.2), channel_id=1, source_target_pairs={{0,8},{8,0},{16,24},{24,16},{1,9},{9,1},{17,25},{25,17},{2,10},{10... | collective-permute-start | bytes 3145736 | tf_op jit(solution)/shard_map/ppermute | solution.py:175
  451.6 154.3 %collective-permute-start.7 = (bf16[4096,512]{1,0:T(8,128)(2,1)}, bf16[4096,512]{1,0:T(8,128)(2,1)}, u32[]{:S(2)}, u32[]{:S(2)}) collective-permute-start(bf16[4096,512]{1,0:T(8,128)(2,1)} %dynamic-slice_convert_fusion.1), channel_id=1, source_target_pairs={{0,8},{8,0},{16,24},{24,16},{1,9},{9,1},{17,25},{25,17},{2,10},{10... | collective-permute-start | bytes 12582920 | tf_op jit(solution)/shard_map/ppermute | solution.py:175
  458.3 86.2 %collective-permute-start.11 = (bf16[512,4096]{1,0:T(8,128)(2,1)}, bf16[512,4096]{1,0:T(8,128)(2,1)}, u32[]{:S(2)}, u32[]{:S(2)}) collective-permute-start(bf16[512,4096]{1,0:T(8,128)(2,1)} %dynamic-slice_convert_fusion), channel_id=1, source_target_pairs={{0,8},{8,0},{16,24},{24,16},{1,9},{9,1},{17,25},{25,17},{2,10},{10... | collective-permute-start | bytes 12582920 | tf_op jit(solution)/shard_map/ppermute | solution.py:175
  506.3 14.8 %slice-start = ((s8[16777216]{0:T(1024)(128)(4,1)}), s8[4194304]{0:T(1024)(128)(4,1)S(1)}, s32[]{:S(2)}) async-start(s8[16777216]{0:T(1024)(128)(4,1)} %bitcast.163), calls=%async_computation.12 | async-start | bytes 8388608
  506.3 14.8 %slice-start.1 = ((s8[16777216]{0:T(1024)(128)(4,1)}), s8[4194304]{0:T(1024)(128)(4,1)S(1)}, s32[]{:S(2)}) async-start(s8[16777216]{0:T(1024)(128)(4,1)} %bitcast.163), calls=%async_computation.13 | async-start | bytes 8388608
  552.6 258.7 %reduce-scatter.3.cloned.1.call-start = ((), (), s32[]{:S(2)}) async-start(), calls=%async_computation.10 | async-start | bytes 5898240 | tf_op jit(solution)/shard_map/reduce_scatter | solution.py:218
  558.9 21.1 %slice-start.10 = ((s8[8388608]{0:T(1024)(128)(4,1)}), s8[4194304]{0:T(1024)(128)(4,1)S(1)}, s32[]{:S(2)}) async-start(s8[8388608]{0:T(1024)(128)(4,1)} %bitcast.169), calls=%async_computation.22 | async-start | bytes 8388608
  564.6 13.8 %copy-start.18 = (bf16[2,2,512,512]{2,3,1,0:T(8,128)(2,1)S(1)}, bf16[2,2,512,512]{2,3,1,0:T(8,128)(2,1)}, u32[]{:S(2)}) copy-start(bf16[2,2,512,512]{2,3,1,0:T(8,128)(2,1)} %copy-done.17) | copy-start | bytes 6291460
  564.6 15.3 %slice-start.11 = ((s8[8388608]{0:T(1024)(128)(4,1)}), s8[4194304]{0:T(1024)(128)(4,1)S(1)}, s32[]{:S(2)}) async-start(s8[8388608]{0:T(1024)(128)(4,1)} %bitcast.169), calls=%async_computation.23 | async-start | bytes 8388608
  564.7 15.3 %copy-start.22 = (pred[512,1024]{1,0:T(8,128)(4,1)S(1)}, pred[512,1024]{1,0:T(8,128)(4,1)}, u32[]{:S(2)}) copy-start(pred[512,1024]{1,0:T(8,128)(4,1)} %iota_compare_fusion.2) | copy-start | bytes 1572868
  564.7 15.3 %copy-start.57 = (bf16[2,512,2,64]{1,0,3,2:T(2,128)(2,1)S(1)}, bf16[2,512,2,64]{1,0,3,2:T(2,128)(2,1)}, u32[]{:S(2)}) copy-start(bf16[2,512,2,64]{1,0,3,2:T(2,128)(2,1)} %copy-done.56) | copy-start | bytes 786436
  564.7 15.3 %copy-start.67 = (f32[2,2,512]{2,1,0:T(2,128)S(1)}, f32[2,2,512]{2,1,0:T(2,128)}, u32[]{:S(2)}) copy-start(f32[2,2,512]{2,1,0:T(2,128)} %copy-done.66) | copy-start | bytes 24580
  656.7 105.4 %all-to-all-start.2 = ((bf16[8,2,98304]{2,1,0:T(2,128)(2,1)}), bf16[8,2,98304]{2,1,0:T(2,128)(2,1)}, u32[]{:S(2)}, u32[]{:S(2)}) async-start(bf16[8,2,98304]{2,1,0:T(2,128)(2,1)} %reshape.419), calls=%async_computation.2 | async-start | bytes 6291456 | tf_op jit(solution)/shard_map/all_to_all | solution.py:383
  669.8 116.7 %collective-permute-start.2 = (bf16[3,512,1024]{2,1,0:T(8,128)(2,1)}, bf16[3,512,1024]{2,1,0:T(8,128)(2,1)}, u32[]{:S(2)}, u32[]{:S(2)}) collective-permute-start(bf16[3,512,1024]{2,1,0:T(8,128)(2,1)} %all-gather.16.cloned.1.call-done), channel_id=1, source_target_pairs={{0,8},{8,0},{16,24},{24,16},{1,9},{9,1},{17,25},{25,17},{2,10},{10... | collective-permute-start | bytes 9437192 | tf_op jit(solution)/shard_map/ppermute | solution.py:175
  677.7 20.0 %collective-permute-start.3 = (bf16[3,1024,128]{1,2,0:T(8,128)(2,1)S(1)}, bf16[3,1024,128]{1,2,0:T(8,128)(2,1)S(1)}, u32[]{:S(2)}, u32[]{:S(2)}) collective-permute-start(bf16[3,1024,128]{1,2,0:T(8,128)(2,1)S(1)} %fusion.56), channel_id=1, source_target_pairs={{0,16},{8,24},{16,0},{24,8},{1,17},{9,25},{17,1},{25,9},{2,18},{10... | collective-permute-start | bytes 2359304 | tf_op jit(solution)/shard_map/ppermute | solution.py:235
  698.0 7.9 collective-permute-start.4
  700.5 3.6 collective-permute-start.5
  704.1 1.2 collective-permute-start.6
  797.4 13.9 %copy-start.34 = (bf16[512,512]{1,0:T(8,128)(2,1)}, bf16[512,512]{1,0:T(8,128)(2,1)S(1)}, u32[]{:S(2)}) copy-start(bf16[512,512]{1,0:T(8,128)(2,1)S(1)} %fusion.76) | copy-start | bytes 1572868
  797.4 12.7 %collective-permute-start.12 = (bf16[512,512]{1,0:T(8,128)(2,1)S(1)}, bf16[512,512]{1,0:T(8,128)(2,1)S(1)}, u32[]{:S(2)}, u32[]{:S(2)}) collective-permute-start(bf16[512,512]{1,0:T(8,128)(2,1)S(1)} %fusion.76), channel_id=1, source_target_pairs={{0,16},{8,24},{16,0},{24,8},{1,17},{9,25},{17,1},{25,9},{2,18},{10... | collective-permute-start | bytes 1572872 | tf_op jit(solution)/shard_map/ppermute | solution.py:235
  802.2 12.0 %copy-start.80 = (f32[1024]{0:T(1024)S(1)}, f32[1024]{0:T(1024)}, u32[]{:S(2)}) copy-start(f32[1024]{0:T(1024)} %get-tuple-element.72) | copy-start | bytes 12292
  802.2 12.0 %copy-start.82 = (f32[1024]{0:T(1024)S(1)}, f32[1024]{0:T(1024)}, u32[]{:S(2)}) copy-start(f32[1024]{0:T(1024)} %get-tuple-element.76) | copy-start | bytes 12292
  802.2 12.0 %copy-start.86 = (f32[1024]{0:T(1024)S(1)}, f32[1024]{0:T(1024)}, u32[]{:S(2)}) copy-start(f32[1024]{0:T(1024)} %get-tuple-element.74) | copy-start | bytes 12292
  802.2 12.0 %copy-start.79 = (f32[1024]{0:T(1024)S(1)}, f32[1024]{0:T(1024)}, u32[]{:S(2)}) copy-start(f32[1024]{0:T(1024)} %get-tuple-element.84) | copy-start | bytes 12292
  802.2 12.0 %copy-start.81 = (f32[1024]{0:T(1024)S(1)}, f32[1024]{0:T(1024)}, u32[]{:S(2)}) copy-start(f32[1024]{0:T(1024)} %get-tuple-element.87) | copy-start | bytes 12292
  802.2 12.0 %copy-start.85 = (f32[1024]{0:T(1024)S(1)}, f32[1024]{0:T(1024)}, u32[]{:S(2)}) copy-start(f32[1024]{0:T(1024)} %get-tuple-element.85) | copy-start | bytes 12292
  802.2 12.1 %copy-start.78 = (f32[1024]{0:T(1024)S(1)}, f32[1024]{0:T(1024)}, u32[]{:S(2)}) copy-start(f32[1024]{0:T(1024)} %get-tuple-element.93) | copy-start | bytes 12292
  802.2 12.1 %copy-start.83 = (f32[4096]{0:T(1024)S(1)}, f32[4096]{0:T(1024)}, u32[]{:S(2)}) copy-start(f32[4096]{0:T(1024)} %get-tuple-element.175) | copy-start | bytes 49156
  802.3 12.1 %copy-start.84 = (f32[1024]{0:T(1024)S(1)}, f32[1024]{0:T(1024)}, u32[]{:S(2)}) copy-start(f32[1024]{0:T(1024)} %get-tuple-element.95) | copy-start | bytes 12292
  811.3 56.6 %collective-permute-start.13 = (f32[512,512]{1,0:T(8,128)}, f32[512,512]{1,0:T(8,128)S(1)}, u32[]{:S(2)}, u32[]{:S(2)}) collective-permute-start(f32[512,512]{1,0:T(8,128)} %convert_add_fusion.3), channel_id=1, source_target_pairs={{0,8},{8,0},{16,24},{24,16},{1,9},{9,1},{17,25},{25,17},{2,10},{10... | collective-permute-start | bytes 3145736 | tf_op jit(solution)/shard_map/ppermute | solution.py:175
  811.3 56.6 %copy-start.35 = (bf16[512,512]{1,0:T(8,128)(2,1)S(1)}, bf16[512,512]{1,0:T(8,128)(2,1)}, u32[]{:S(2)}) copy-start(bf16[512,512]{1,0:T(8,128)(2,1)} %copy-done.34) | copy-start | bytes 1572868
  811.3 56.6 %copy-start.48 = (bf16[512,512]{1,0:T(8,128)(2,1)S(1)}, bf16[512,512]{1,0:T(8,128)(2,1)}, u32[]{:S(2)}) copy-start(bf16[512,512]{1,0:T(8,128)(2,1)} %copy-done.47) | copy-start | bytes 1572868
  812.7 52.1 %collective-permute-start.14 = (bf16[512,512]{1,0:T(8,128)(2,1)S(1)}, bf16[512,512]{1,0:T(8,128)(2,1)S(1)}, u32[]{:S(2)}, u32[]{:S(2)}) collective-permute-start(bf16[512,512]{1,0:T(8,128)(2,1)S(1)} %fusion.74), channel_id=1, source_target_pairs={{0,16},{8,24},{16,0},{24,8},{1,17},{9,25},{17,1},{25,9},{2,18},{10... | collective-permute-start | bytes 1572872 | tf_op jit(solution)/shard_map/ppermute | solution.py:235
  862.5 5.2 collective-permute-start.9
  864.9 5.6 collective-permute-start.15
  867.8 1.9 collective-permute-start.10
  (66 other events, 312.3 us)
Sparse Core Ops, SparseCore 0:
  15.0 127.3 all-gather.7
  145.0 72.8 all-gather.11
  220.0 70.9 all-gather.13
  292.9 55.8 all-gather.9
  443.3 71.1 all-gather.15
  552.7 86.3 reduce-scatter.4
  642.7 151.9 reduce-scatter.2

commit v19 on v16

--- a/solution.py
+++ b/solution.py
@@ -269,8 +269,12 @@
     bias_flat = jnp.concatenate([qkv_bias.reshape(-1), up_bias])
     bias_full = lax.all_gather(bias_flat, "narrow", axis=0)
     gathered_first = lax.all_gather(low_first, "narrow", axis=0, tiled=True)
-    gathered_first, up_weight, down_weight, out_weight, bias_full = lax.optimization_barrier(
-        (gathered_first, up_weight, down_weight, out_weight, bias_full)
+    gathered_first, out_weight, bias_full = lax.optimization_barrier(
+        (gathered_first, out_weight, bias_full)
+    )
+    out_gathered = gather_mine(out_weight, core, 1, 0)
+    out_gathered, up_weight, down_weight = lax.optimization_barrier(
+        (out_gathered, up_weight, down_weight)
     )
     up_bias_full = bias_full[:, 3 * inner :].reshape(-1)
     query, key_rows, values = project_qkv(
@@ -279,7 +283,7 @@
     attn_heads, totals = attend_forward(query, key_rows, values, block_rows)
     attn_low = attn_heads.reshape(group_rows, inner).astype(jnp.bfloat16)
     attn_rows = lax.all_to_all(attn_low, "narrow", 0, 1, tiled=True)
-    out_full = join_halves(gather_mine(out_weight, core, 1, 0), core, 1)
+    out_full = join_halves(out_gathered, core, 1)
     pre_attn = jnp.dot(attn_rows, out_full, preferred_element_type=jnp.float32) + out_bias
     normed_second, inverse_second = norm_stats(pre_attn)
     residual = layer_in + normed_second * norm_gains[1] + norm_biases[1]

time: 905 us -> 891 us (0.985)
    unnamed x255 -> x259, local copies, waits for them, and re-layouts: 77.3 us -> 68.1 us
  transfers between devices with their start and end apart: 18 -> 18, of which waited for: 7 -> 8; matrix products, arithmetic and copies ran while one was open for 45% -> 46% of each run, Pallas kernels for 0% -> 0%
where the time goes in v19:
time: 891 us; the launch traced here: 881 us
  waiting for transfers between devices  254 us (29%)
  matrix products  195 us (22%)
  local copies, waits for them, and re-layouts  186 us (21%)
  other arithmetic  132 us (15%)
  blocking collectives  83.6 us (9%)
  between operations  15.9 us (2%)
  starting transfers between devices  14.6 us (2%)
    all_gather x1, waiting for transfers between devices, shards(): gathered_first = lax.all_gather(low_first, 'narrow', axis=0, tiled=True)  90.6 us
    all_gather x4, waiting for transfers between devices, gather_mine(): return lax.all_gather(mine, 'narrow', axis=gather_axis, tiled=True)  69.1 us
    unnamed x259, local copies, waits for them, and re-layouts  68.1 us
    all_to_all x1, waiting for transfers between devices, shards(): lax.all_to_all(qkv_grad.reshape(3, group_rows, heads_here, HEAD), 'narrow...  60.1 us
    psum x1, blocking collectives, shards(): lax.psum((gain_local, bias_local, out_blocal, down_blocal, up_bgrad_rows)...  42.6 us
    convert_element_type x4, other arithmetic, attend_backward(): scores_grad = (probs_full * (probs_grad - row_dot)).astype(jnp.bfloat16)  36.5 us
    all_gather x1, blocking collectives, shards(): bias_full = lax.all_gather(bias_flat, 'narrow', axis=0)  33.4 us
    dot_general x4, matrix products, attend_backward(): jnp.einsum('bqhd,bkhd->bhqk', grad_block, value_block, preferred_element_...  31.2 us
  transfers between devices with their start and end apart: 18, of which 8 were waited for; matrix products, arithmetic and copies ran while one was open for 46% of the time, Pallas kernels for 0%

profile of v19, /device:TPU:0, one launch (start us, length us, event | category | flops | bytes accessed | tf_op | source)
XLA Modules:
  0.0 881.5 jit_solution(4558639679370342774)
XLA Ops:
  14.9 33.4 %all-gather.1 = f32[8,1,896]{2,1,0:T(1,128)S(1)} all-gather(f32[1,1,896]{2,1,0:T(1,128)S(1)} %reshape.435), channel_id=2, replica_groups=mesh['wide'=4,'narrow'=8] {'narrow'}, dimensions={0}, use_global_device_ids=true | all-gather | bytes 32256 | tf_op jit(solution)/shard_map/all_gather | solution.py:270
  51.7 90.6 %all-gather.8.cloned.1.call-done = bf16[4096,1024]{1,0:T(8,128)(2,1)} async-done(((bf16[512,1024]{1,0:T(8,128)(2,1)}), bf16[4096,1024]{1,0:T(8,128)(2,1)}) %all-gather.8.cloned.1.call-update) | async-done | bytes 8388624 | tf_op jit(solution)/shard_map/all_gather | solution.py:271
  144.0 7.4 add_bitcast_fusion
  155.1 5.0 reshape.440
  160.1 5.9 copy.114
  166.0 17.5 %all-gather.10.cloned.1.call-done = bf16[1024,512]{1,0:T(8,128)(2,1)} async-done(((bf16[128,512]{1,0:T(8,128)(2,1)}), bf16[1024,512]{1,0:T(8,128)(2,1)}) %all-gather.10.cloned.1.call-update) | async-done | bytes 1048592 | tf_op jit(solution)/shard_map/all_gather | solution.py:181
  184.6 4.5 fusion.132
  189.1 5.6 reshape.442
  194.7 9.9 %fusion.133 = (f32[2,2048,2,32]{3,2,1,0:T(2,128)}, f32[2,2048,2,32]{3,2,1,0:T(2,128)}) fusion(f32[2,2048,2,64]{3,2,1,0:T(2,128)} %reshape.442), kind=kLoop, calls=%fused_computation.283 | loop fusion | bytes 4194304 | tf_op jit(solution)/shard_map/slice | solution.py:41
  204.6 6.4 copy.168
  211.0 6.4 copy.167
  217.4 5.6 reshape.441
  223.0 9.9 %fusion.134 = (f32[2,2048,2,32]{3,2,1,0:T(2,128)}, f32[2,2048,2,32]{3,2,1,0:T(2,128)}) fusion(f32[2,2048,2,64]{3,2,1,0:T(2,128)} %reshape.441), kind=kLoop, calls=%fused_computation.284 | loop fusion | bytes 4194304 | tf_op jit(solution)/shard_map/slice | solution.py:41
  232.9 6.4 copy.166
  239.3 6.4 copy.165
  253.0 4.8 exponential_reduce_fusion
  258.8 4.9 fusion.14
  266.3 3.5 exponential_reduce_fusion.1
  271.8 4.8 exponential_reduce_fusion.2
  284.0 7.5 fusion.67
  291.5 5.9 fusion.68
  297.5 3.5 fusion.66
  303.9 4.2 all-to-all-start
  312.4 51.5 %all-gather.14.cloned.1.call-done = bf16[4096,512]{1,0:T(8,128)(2,1)} async-done(((bf16[512,512]{1,0:T(8,128)(2,1)}), bf16[4096,512]{1,0:T(8,128)(2,1)}) %all-gather.14.cloned.1.call-update) | async-done | bytes 4194320 | tf_op jit(solution)/shard_map/all_gather | solution.py:181
  369.8 3.9 broadcast_select_fusion.3
  373.7 10.1 %multiply_convert_fusion.3 = (bf16[512,4096]{1,0:T(8,128)(2,1)}, f32[512,4096]{1,0:T(8,128)}) fusion(f32[4096]{0:T(1024)S(1)} %bitcast.207, bf16[512,4096]{1,0:T(8,128)(2,1)} %get-tuple-element.111, bf16[512,4096]{1,0:T(8,128)(2,1)S(1)} %get-tuple-element.110, f32[512,1024]{1,0:T(8,128)S(1)} %get-tuple-element.107, f32[1024]{0:T(1024)S(1)} %bitcast.210, ...), kind=kOutput, calls=%fused_computation.33 | convolution fusion | flops 4326948864 | bytes 23097344 | tf_op jit(solution)/shard_map/dot_general | solution.py:294
  383.9 3.9 broadcast_select_fusion.1
  387.8 8.9 %add_reduce_fusion = (f32[512]{0:T(512)S(1)}, f32[512,1024]{1,0:T(8,128)S(1)}) fusion(f32[1024]{0:T(1024)S(1)} %copy-done.77, bf16[512,4096]{1,0:T(8,128)(2,1)} %get-tuple-element.25, bf16[4096,512]{1,0:T(8,128)(2,1)} %get-tuple-element.109, bf16[4096,512]{1,0:T(8,128)(2,1)S(1)} %get-tuple-element.108), kind=kOutput, calls=%fused_computation.130 | convolution fusion | flops 4312792576 | bytes 14686208 | tf_op jit(solution)/shard_map/dot_general | solution.py:298
  401.5 8.4 fusion.138
  409.8 12.4 %convert_reduce_fusion = (f32[4096]{0:T(1024)}, bf16[512,4096]{1,0:T(8,128)(2,1)}) fusion(f32[512,4096]{1,0:T(8,128)} %get-tuple-element.166, f32[4096]{0:T(1024)S(1)} %bitcast.208, bf16[512,1024]{1,0:T(8,128)(2,1)S(1)} %get-tuple-element.102, bf16[4096,512]{1,0:T(8,128)(2,1)} %get-tuple-element.109, bf16[4096,512]{1,0:T(8,128)(2,1)} %copy-done.42), kind=kOutput, calls=%fused_computation.26 | convolution fusion | flops 4339003392 | bytes 22052864 | tf_op jit(solution)/shard_map/dot_general | solution.py:326
  422.3 9.1 %multiply_reduce_fusion.5 = (f32[1024]{0:T(1024)}, f32[512]{0:T(512)S(1)}, f32[512]{0:T(512)S(1)}, f32[1024]{0:T(1024)}, f32[512,1024]{1,0:T(8,128)}) fusion(f32[512,1024]{1,0:T(8,128)S(1)} %get-tuple-element.107, f32[512]{0:T(512)S(1)} %add_rsqrt_fusion.1, f32[512]{0:T(512)S(1)} %broadcast_multiply_fusion.9, f32[1024]{0:T(1024)S(1)} %bitcast.197, ...), kind=kOutput, calls=%fused_computation.102 | convolution fusion | flops 4316460032 | bytes 16797696 | tf_op jit(solution)/shard_map/dot_general | solution.py:334
  431.3 10.7 %fusion.129 = f32[1024,4096]{1,0:T(8,128)} fusion(bf16[512,4096]{1,0:T(8,128)(2,1)} %get-tuple-element.180, f32[512,1024]{1,0:T(8,128)S(1)} %get-tuple-element.107, f32[1024]{0:T(1024)S(1)} %bitcast.211, f32[1024]{0:T(1024)S(1)} %bitcast.198, f32[512]{0:T(512)S(1)} %add_rsqrt_fusion.1, f32[512]{0:T(512)S(1)} %broadcast_multiply_fusion.9), kind=kOutput, calls=%fused_computation.280 | convolution fusion | flops 4297588736 | bytes 23080960 | tf_op jit(solution)/shard_map/dot_general | solution.py:331
  442.1 3.4 multiply_reduce_fusion.6
  450.5 3.6 all-to-all-start.1
  459.4 5.9 dynamic-slice_convert_fusion.1
  465.4 6.2 dynamic-slice_convert_fusion
  473.4 18.2 %all-to-all-done.1 = bf16[512,8,128]{0,2,1:T(8,128)(2,1)S(1)} async-done(((bf16[512,8,128]{0,2,1:T(8,128)(2,1)}), bf16[512,8,128]{0,2,1:T(8,128)(2,1)S(1)}, u32[]{:S(2)}, u32[]{:S(2)}) %all-to-all-start.1) | async-done | bytes 1048608 | tf_op jit(solution)/shard_map/all_to_all | solution.py:345
  494.3 6.0 convolution_bitcast_fusion.2
  504.5 12.0 %multiply_reduce_fusion.1 = (f32[2,2,512]{2,1,0:T(2,128)}, f32[2,2,512,1536]{3,2,1,0:T(8,128)}) fusion(f32[2,2,512,1536]{3,2,1,0:T(8,128)} %copy-done.3, f32[2,2,512]{2,1,0:T(2,128)S(1)} %copy-done.69, pred[512,1536]{1,0:T(8,128)(4,1)S(1)} %copy-done.14, bf16[2,2048,2,64]{1,3,2,0:T(8,128)(2,1)S(1)} %copy-done.30, ...), kind=kOutput, calls=%fused_computation.7 | convolution fusion | flops 418379776 | bytes 27017216 | tf_op jit(solution)/shard_map/bqhd,bkhd->bhqk/dot_general | solution.py:141
  516.6 11.4 %multiply_reduce_fusion = (f32[2,2,512]{2,1,0:T(2,128)}, f32[2,2,512,2048]{3,2,1,0:T(8,128)}) fusion(f32[2,2,512,2048]{3,2,1,0:T(8,128)S(1)} %bitcast.165, f32[2,2,512]{2,1,0:T(2,128)} %copy-done.73, pred[512,2048]{1,0:T(8,128)(4,1)S(1)} %copy-done.10, bf16[2,2048,2,64]{1,3,2,0:T(8,128)(2,1)} %copy.114, bf16[2,512,2,64]{1,0,3,2:T(2,128)(2,1)} %get-tuple-element.131), kind=kOutput, calls=%fused_computation.1 | convolution fusion | flops 557840384 | bytes 35930112 | tf_op jit(solution)/shard_map/bqhd,bkhd->bhqk/dot_general | solution.py:141
  528.0 12.0 %multiply_convert_fusion.1 = bf16[2,2,512,1536]{3,2,1,0:T(8,128)(2,1)} fusion(f32[2,2,512,1536]{3,2,1,0:T(8,128)} %get-tuple-element.173, f32[2,2,512,1536]{3,2,1,0:T(8,128)} %copy-done.3, f32[2,2,512]{2,1,0:T(2,128)} %get-tuple-element.172, f32[2,2,512]{2,1,0:T(2,128)} %copy-done.68, pred[512,1536]{1,0:T(8,128)(4,1)} %copy-done.13), kind=kLoop, calls=%fused_computation.6 | loop fusion | flops 18874368 | bytes 32260096 | tf_op jit(solution)/shard_map/convert_element_type | solution.py:145
  540.0 8.1 add_convert_fusion
  549.4 5.8 fusion.60
  555.1 12.3 %multiply_convert_fusion = bf16[2,2,512,2048]{3,2,1,0:T(8,128)(2,1)S(1)} fusion(f32[2,2,512,2048]{3,2,1,0:T(8,128)} %get-tuple-element.171, f32[2,2,512,2048]{3,2,1,0:T(8,128)} %copy-done.2, f32[2,2,512]{2,1,0:T(2,128)S(1)} %copy-done.83, f32[2,2,512]{2,1,0:T(2,128)S(1)} %copy-done.74, pred[512,2048]{1,0:T(8,128)(4,1)S(1)} %copy-done.10), kind=kLoop, calls=%fused_computation | loop fusion | flops 25165824 | bytes 43008000 | tf_op jit(solution)/shard_map/convert_element_type | solution.py:145
  570.8 3.5 fusion.61
  576.5 6.2 multiply_reduce_fusion.2
  582.7 4.7 convolution_bitcast_fusion.1
  587.4 9.6 %multiply_convert_fusion.2 = bf16[2,2,512,1024]{3,2,1,0:T(8,128)(2,1)} fusion(f32[2,2,512,1024]{3,2,1,0:T(8,128)} %get-tuple-element.175, f32[2,2,512,1024]{3,2,1,0:T(8,128)} %get-tuple-element.160, f32[2,2,512]{2,1,0:T(2,128)S(1)} %copy-done.80, f32[2,2,512]{2,1,0:T(2,128)S(1)} %log_add_fusion.2, pred[512,1024]{1,0:T(8,128)(4,1)} %copy-done.23), kind=kLoop, calls=%fused_computation.31 | loop fusion | flops 12582912 | bytes 21512192 | tf_op jit(solution)/shard_map/convert_element_type | solution.py:145
  597.4 7.9 fusion.30
  605.4 6.3 add_convert_fusion.1
  622.6 3.9 fusion.62
  639.6 3.5 pad_maximum_fusion.7
  643.1 14.6 %copy.140 = bf16[3,4096,2,64]{3,2,0,1:T(2,128)(2,1)} copy(bf16[3,4096,2,64]{1,3,2,0:T(8,128)(2,1)} %pad_maximum_fusion.7) | data formatting | bytes 6291456 | tf_op jit(solution)/shard_map/stack | solution.py:354
  657.7 8.9 %reshape.443 = bf16[8,2,98304]{2,1,0:T(2,128)(2,1)} reshape(bf16[4096,3,2,64]{3,2,1,0:T(2,128)(2,1)} %bitcast.178) | data formatting | bytes 6291456
  666.7 4.6 all-to-all-start.2
  682.2 7.6 psum.71
  690.4 8.7 fusion.57
  699.1 60.1 %all-to-all-done.2 = bf16[8,2,98304]{2,1,0:T(2,128)(2,1)} async-done(((bf16[8,2,98304]{2,1,0:T(2,128)(2,1)}), bf16[8,2,98304]{2,1,0:T(2,128)(2,1)}, u32[]{:S(2)}, u32[]{:S(2)}) %all-to-all-start.2) | async-done | bytes 3145760 | tf_op jit(solution)/shard_map/all_to_all | solution.py:363
  759.2 8.8 reshape.444
  768.0 15.3 %copy.157 = bf16[3,8,512,2,64]{2,4,3,1,0:T(8,128)(2,1)} copy(bf16[3,8,512,2,64]{4,3,0,2,1:T(2,128)(2,1)} %bitcast.179) | data formatting | bytes 6291456 | tf_op jit(solution)/shard_map/all_to_all | solution.py:363
  783.3 5.9 broadcast_select_fusion.5
  796.0 9.2 %fusion.45 = (f32[1024]{0:T(1024)S(1)}, f32[512]{0:T(512)S(1)}, f32[512]{0:T(512)S(1)}, f32[1024]{0:T(1024)S(1)}, f32[512,1024,1]{1,0,2:T(8,128)}) fusion(bf16[512,1024]{1,0:T(8,128)(2,1)S(1)} %copy-done.12, f32[512]{0:T(512)S(1)} %copy-done.85, f32[512]{0:T(512)S(1)} %copy-done.82, f32[1024]{0:T(1024)S(1)} %bitcast.194, ...), kind=kOutput, calls=%fused_computation.91 | convolution fusion | flops 3239048192 | bytes 12603392 | tf_op jit(solution)/shard_map/tse,tde->sd/dot_general | solution.py:369
  805.3 42.6 %all-reduce.6 = (f32[1024]{0:T(1024)}, f32[4096]{0:T(1024)S(1)}, f32[1024]{0:T(1024)}, f32[4,1024]{1,0:T(4,128)}, f32[4,1024]{1,0:T(4,128)}) all-reduce(f32[1024]{0:T(1024)S(1)} %copy-done.92, f32[4096]{0:T(1024)S(1)} %copy-done.91, f32[1024]{0:T(1024)S(1)} %copy-done.86, ...), channel_id=1, replica_groups=mesh['wide'=4,'narrow'=8] {'wide','narrow'}, use_global_device_ids=true, to_apply=%region_36.37 | all-reduce | flops 14336 | bytes 114688 | tf_op jit(solution)/shard_map/psum | solution.py:401
  851.9 13.6 %all-reduce.10.cloned.1.call-done = (bf16[3,1024,128]{1,2,0:T(8,128)(2,1)}, bf16[128,1024]{1,0:T(8,128)(2,1)}, bf16[1024,512]{1,0:T(8,128)(2,1)}, bf16[512,1024]{1,0:T(8,128)(2,1)}) async-done(((bf16[3,1024,128]{1,2,0:T(8,128)(2,1)}, bf16[128,1024]{1,0:T(8,128)(2,1)}, bf16[1024,512]{1,0:T(8,128)(2,1)}, bf16[512,1024]{1,0:T(8,128)(2,1)}), (bf16[3,1024,128]{1,2,0:T(8,128)(2,1)}, bf16[128,1024]{1,0:T(8,128)(2,1)}, ...) | async-done | bytes 3145744 | tf_op jit(solution)/shard_map/psum | solution.py:394
  (407 shorter events, 135.9 us)
Async XLA Ops:
  7.2 176.3 %copy-start = (bf16[1024,512]{1,0:T(8,128)(2,1)S(1)}, bf16[1024,512]{1,0:T(8,128)(2,1)}, u32[]{:S(2)}) copy-start(bf16[1024,512]{1,0:T(8,128)(2,1)} %param.22) | copy-start | bytes 3145732
  7.2 135.1 %copy-start.76 = (bf16[128,1024]{1,0:T(8,128)(2,1)S(1)}, bf16[128,1024]{1,0:T(8,128)(2,1)}, u32[]{:S(2)}) copy-start(bf16[128,1024]{1,0:T(8,128)(2,1)} %param.20) | copy-start | bytes 786436
  7.2 135.1 %all-gather.8.cloned.1.call-start = ((), (), s32[]{:S(2)}) async-start(), calls=%async_computation.5 | async-start | bytes 9437184 | tf_op jit(solution)/shard_map/all_gather | solution.py:271
  9.0 134.0 %copy-start.78 = (f32[1,1024]{1,0:T(1,128)}, f32[1,1024]{1,0:T(1,128)S(1)}, u32[]{:S(2)}) copy-start(f32[1,1024]{1,0:T(1,128)S(1)} %get-tuple-element.147) | copy-start | bytes 12292
  10.5 132.6 %copy-start.81 = (f32[512]{0:T(512)}, f32[512]{0:T(512)S(1)}, u32[]{:S(2)}) copy-start(f32[512]{0:T(512)S(1)} %broadcast_multiply_fusion.11) | copy-start | bytes 6148
  12.2 130.9 %copy-start.84 = (f32[512]{0:T(512)}, f32[512]{0:T(512)S(1)}, u32[]{:S(2)}) copy-start(f32[512]{0:T(512)S(1)} %add_rsqrt_fusion.3) | copy-start | bytes 6148
  14.8 168.7 %all-gather.10.cloned.1.call-start = ((), (), s32[]{:S(2)}) async-start(), calls=%async_computation.6 | async-start | bytes 1179648 | tf_op jit(solution)/shard_map/all_gather | solution.py:181
  51.7 239.7 %copy-start.9 = (pred[512,2048]{1,0:T(8,128)(4,1)}, pred[512,2048]{1,0:T(8,128)(4,1)S(1)}, u32[]{:S(2)}) copy-start(pred[512,2048]{1,0:T(8,128)(4,1)S(1)} %iota_compare_fusion) | copy-start | bytes 3145732
  143.0 154.4 %all-gather.12.cloned.1.call-start = ((), (), s32[]{:S(2)}) async-start(), calls=%async_computation.7 | async-start | bytes 4718592 | tf_op jit(solution)/shard_map/all_gather | solution.py:181
  143.5 350.8 %copy-start.23 = (pred[512,1024]{1,0:T(8,128)(4,1)}, pred[512,1024]{1,0:T(8,128)(4,1)S(1)}, u32[]{:S(2)}) copy-start(pred[512,1024]{1,0:T(8,128)(4,1)S(1)} %iota_compare_fusion.2) | copy-start | bytes 1572868
  144.0 140.0 %copy-start.13 = (pred[512,1536]{1,0:T(8,128)(4,1)}, pred[512,1536]{1,0:T(8,128)(4,1)S(1)}, u32[]{:S(2)}) copy-start(pred[512,1536]{1,0:T(8,128)(4,1)S(1)} %iota_compare_fusion.1) | copy-start | bytes 2359300
  184.4 179.6 %all-gather.14.cloned.1.call-start = ((), (), s32[]{:S(2)}) async-start(), calls=%async_computation.8 | async-start | bytes 4718592 | tf_op jit(solution)/shard_map/all_gather | solution.py:181
  248.8 15.0 %copy-start.25 = (bf16[2,2048,2,32]{1,3,2,0:T(8,128)(2,1)}, bf16[2,2048,2,32]{1,3,2,0:T(8,128)(2,1)S(1)}, u32[]{:S(2)}) copy-start(bf16[2,2048,2,32]{1,3,2,0:T(8,128)(2,1)S(1)} %get-tuple-element.124) | copy-start | bytes 1572868
  248.8 14.9 %copy-start.27 = (bf16[2,2048,2,32]{1,3,2,0:T(8,128)(2,1)}, bf16[2,2048,2,32]{1,3,2,0:T(8,128)(2,1)S(1)}, u32[]{:S(2)}) copy-start(bf16[2,2048,2,32]{1,3,2,0:T(8,128)(2,1)S(1)} %get-tuple-element.125) | copy-start | bytes 1572868
  248.8 27.9 %copy-start.18 = (bf16[2,2048,2,32]{1,3,2,0:T(8,128)(2,1)}, bf16[2,2048,2,32]{1,3,2,0:T(8,128)(2,1)S(1)}, u32[]{:S(2)}) copy-start(bf16[2,2048,2,32]{1,3,2,0:T(8,128)(2,1)S(1)} %get-tuple-element.143) | copy-start | bytes 1572868
  248.8 27.9 %copy-start.20 = (bf16[2,2048,2,32]{1,3,2,0:T(8,128)(2,1)}, bf16[2,2048,2,32]{1,3,2,0:T(8,128)(2,1)S(1)}, u32[]{:S(2)}) copy-start(bf16[2,2048,2,32]{1,3,2,0:T(8,128)(2,1)S(1)} %get-tuple-element.144) | copy-start | bytes 1572868
  258.8 32.7 %copy-start.73 = (f32[2,2,512]{2,1,0:T(2,128)}, f32[2,2,512]{2,1,0:T(2,128)S(1)}, u32[]{:S(2)}) copy-start(f32[2,2,512]{2,1,0:T(2,128)S(1)} %log_add_fusion) | copy-start | bytes 24580
  271.8 12.2 %copy-start.68 = (f32[2,2,512]{2,1,0:T(2,128)}, f32[2,2,512]{2,1,0:T(2,128)S(1)}, u32[]{:S(2)}) copy-start(f32[2,2,512]{2,1,0:T(2,128)S(1)} %log_add_fusion.1) | copy-start | bytes 24580
  280.9 220.9 %copy-start.71 = (f32[2,2,512]{2,1,0:T(2,128)}, f32[2,2,512]{2,1,0:T(2,128)S(1)}, u32[]{:S(2)}) copy-start(f32[2,2,512]{2,1,0:T(2,128)S(1)} %log_add_fusion.3) | copy-start | bytes 24580
  280.9 10.5 %slice-start = ((s8[16777216]{0:T(1024)(128)(4,1)}), s8[4194304]{0:T(1024)(128)(4,1)S(1)}, s32[]{:S(2)}) async-start(s8[16777216]{0:T(1024)(128)(4,1)} %bitcast.162), calls=%async_computation.13 | async-start | bytes 8388608
  280.9 10.5 %slice-start.1 = ((s8[16777216]{0:T(1024)(128)(4,1)}), s8[4194304]{0:T(1024)(128)(4,1)S(1)}, s32[]{:S(2)}) async-start(s8[16777216]{0:T(1024)(128)(4,1)} %bitcast.162), calls=%async_computation.14 | async-start | bytes 8388608
  297.4 71.5 %collective-permute-start.1 = (bf16[512,4096]{1,0:T(8,128)(2,1)}, bf16[512,4096]{1,0:T(8,128)(2,1)}, u32[]{:S(2)}, u32[]{:S(2)}) collective-permute-start(bf16[512,4096]{1,0:T(8,128)(2,1)} %all-gather.12.cloned.1.call-done), channel_id=1, source_target_pairs={{0,8},{8,0},{16,24},{24,16},{1,9},{9,1},{17,25},{25,17},{2,10},{10... | collective-permute-start | bytes 12582920 | tf_op jit(solution)/shard_map/ppermute | solution.py:175
  302.6 61.4 %copy-start.75 = (f32[1024]{0:T(1024)S(1)}, f32[1024]{0:T(1024)}, u32[]{:S(2)}) copy-start(f32[1024]{0:T(1024)} %param.21) | copy-start | bytes 12292
  303.9 60.1 %all-to-all-start = ((bf16[8,512,128]{1,2,0:T(8,128)(2,1)}), bf16[8,512,128]{1,2,0:T(8,128)(2,1)}, u32[]{:S(2)}, u32[]{:S(2)}) async-start(bf16[8,512,128]{1,2,0:T(8,128)(2,1)} %copy.126), calls=%async_computation | async-start | bytes 2097152 | tf_op jit(solution)/shard_map/all_to_all | solution.py:285
  308.1 2.8 collective-permute-start
  363.9 20.0 %collective-permute-start.2 = (bf16[4096,512]{1,0:T(8,128)(2,1)}, bf16[4096,512]{1,0:T(8,128)(2,1)}, u32[]{:S(2)}, u32[]{:S(2)}) collective-permute-start(bf16[4096,512]{1,0:T(8,128)(2,1)} %all-gather.14.cloned.1.call-done), channel_id=1, source_target_pairs={{0,8},{8,0},{16,24},{24,16},{1,9},{9,1},{17,25},{25,17},{2,10},{10... | collective-permute-start | bytes 12582920 | tf_op jit(solution)/shard_map/ppermute | solution.py:175
  373.7 10.2 %copy-start.40 = (bf16[4096,512]{1,0:T(8,128)(2,1)S(1)}, bf16[4096,512]{1,0:T(8,128)(2,1)}, u32[]{:S(2)}) copy-start(bf16[4096,512]{1,0:T(8,128)(2,1)} %all-gather.14.cloned.1.call-done) | copy-start | bytes 12582916
  387.8 8.9 %copy-start.42 = (bf16[4096,512]{1,0:T(8,128)(2,1)}, bf16[4096,512]{1,0:T(8,128)(2,1)S(1)}, u32[]{:S(2)}) copy-start(bf16[4096,512]{1,0:T(8,128)(2,1)S(1)} %get-tuple-element.108) | copy-start | bytes 12582916
  387.8 9.3 %copy-start.35 = (bf16[512,1024]{1,0:T(8,128)(2,1)S(1)}, bf16[512,1024]{1,0:T(8,128)(2,1)}, u32[]{:S(2)}) copy-start(bf16[512,1024]{1,0:T(8,128)(2,1)} %param.15) | copy-start | bytes 3145732
  409.8 12.5 %copy-start.41 = (bf16[512,4096]{1,0:T(8,128)(2,1)S(1)}, bf16[512,4096]{1,0:T(8,128)(2,1)}, u32[]{:S(2)}) copy-start(bf16[512,4096]{1,0:T(8,128)(2,1)} %get-tuple-element.111) | copy-start | bytes 12582916
  431.3 10.7 %copy-start.49 = (f32[512,1024]{1,0:T(8,128)S(1)}, f32[512,1024]{1,0:T(8,128)}, u32[]{:S(2)}) copy-start(f32[512,1024]{1,0:T(8,128)} %get-tuple-element.169) | copy-start | bytes 6291460
  450.5 41.1 %all-to-all-start.1 = ((bf16[512,8,128]{0,2,1:T(8,128)(2,1)}), bf16[512,8,128]{0,2,1:T(8,128)(2,1)S(1)}, u32[]{:S(2)}, u32[]{:S(2)}) async-start(bf16[512,8,128]{0,2,1:T(8,128)(2,1)} %bitcast.17), calls=%async_computation.1 | async-start | bytes 2097152 | tf_op jit(solution)/shard_map/all_to_all | solution.py:345
  454.0 217.3 %all-gather.16.cloned.1.call-start = ((), (), s32[]{:S(2)}) async-start(), calls=%async_computation.9 | async-start | bytes 3538944 | tf_op jit(solution)/shard_map/all_gather | solution.py:181
  455.9 333.4 %reduce-scatter.5.cloned.1.call-start = ((), (), s32[]{:S(2)}) async-start(), calls=%async_computation.11 | async-start | bytes 4718592 | tf_op jit(solution)/shard_map/reduce_scatter | solution.py:200
  458.9 13.1 %collective-permute-start.5 = (bf16[1024,512]{1,0:T(8,128)(2,1)S(1)}, bf16[1024,512]{1,0:T(8,128)(2,1)S(1)}, u32[]{:S(2)}, u32[]{:S(2)}) collective-permute-start(bf16[1024,512]{1,0:T(8,128)(2,1)S(1)} %dynamic-slice_convert_fusion.2), channel_id=1, source_target_pairs={{0,8},{8,0},{16,24},{24,16},{1,9},{9,1},{17,25},{25,17},{2,10},{10... | collective-permute-start | bytes 3145736 | tf_op jit(solution)/shard_map/ppermute | solution.py:175
  465.3 140.0 %collective-permute-start.4 = (bf16[4096,512]{1,0:T(8,128)(2,1)}, bf16[4096,512]{1,0:T(8,128)(2,1)}, u32[]{:S(2)}, u32[]{:S(2)}) collective-permute-start(bf16[4096,512]{1,0:T(8,128)(2,1)} %dynamic-slice_convert_fusion.1), channel_id=1, source_target_pairs={{0,8},{8,0},{16,24},{24,16},{1,9},{9,1},{17,25},{25,17},{2,10},{10... | collective-permute-start | bytes 12582920 | tf_op jit(solution)/shard_map/ppermute | solution.py:175
  471.5 68.5 %collective-permute-start.6 = (bf16[512,4096]{1,0:T(8,128)(2,1)}, bf16[512,4096]{1,0:T(8,128)(2,1)}, u32[]{:S(2)}, u32[]{:S(2)}) collective-permute-start(bf16[512,4096]{1,0:T(8,128)(2,1)} %dynamic-slice_convert_fusion), channel_id=1, source_target_pairs={{0,8},{8,0},{16,24},{24,16},{1,9},{9,1},{17,25},{25,17},{2,10},{10... | collective-permute-start | bytes 12582920 | tf_op jit(solution)/shard_map/ppermute | solution.py:175
  494.2 10.2 %copy-start.51 = (bf16[2,512,2,64]{1,0,3,2:T(2,128)(2,1)}, bf16[2,512,2,64]{1,0,3,2:T(2,128)(2,1)S(1)}, u32[]{:S(2)}) copy-start(bf16[2,512,2,64]{1,0,3,2:T(2,128)(2,1)S(1)} %get-tuple-element.132) | copy-start | bytes 786436
  501.9 14.7 %slice-start.4 = ((s8[16777216]{0:T(1024)(128)(4,1)}), s8[4194304]{0:T(1024)(128)(4,1)S(1)}, s32[]{:S(2)}) async-start(s8[16777216]{0:T(1024)(128)(4,1)} %bitcast.164), calls=%async_computation.17 | async-start | bytes 8388608
  501.9 14.7 %slice-start.5 = ((s8[16777216]{0:T(1024)(128)(4,1)}), s8[4194304]{0:T(1024)(128)(4,1)S(1)}, s32[]{:S(2)}) async-start(s8[16777216]{0:T(1024)(128)(4,1)} %bitcast.164), calls=%async_computation.18 | async-start | bytes 8388608
  504.5 12.1 %slice-start.6 = ((s8[16777216]{0:T(1024)(128)(4,1)}), s8[4194304]{0:T(1024)(128)(4,1)S(1)}, s32[]{:S(2)}) async-start(s8[16777216]{0:T(1024)(128)(4,1)} %bitcast.164), calls=%async_computation.19 | async-start | bytes 8388608
  504.5 12.1 %slice-start.7 = ((s8[16777216]{0:T(1024)(128)(4,1)}), s8[4194304]{0:T(1024)(128)(4,1)S(1)}, s32[]{:S(2)}) async-start(s8[16777216]{0:T(1024)(128)(4,1)} %bitcast.164), calls=%async_computation.20 | async-start | bytes 8388608
  504.5 12.1 %copy-start.10 = (pred[512,2048]{1,0:T(8,128)(4,1)S(1)}, pred[512,2048]{1,0:T(8,128)(4,1)}, u32[]{:S(2)}) copy-start(pred[512,2048]{1,0:T(8,128)(4,1)} %copy-done.9) | copy-start | bytes 3145732
  548.2 243.5 %reduce-scatter.3.cloned.1.call-start = ((), (), s32[]{:S(2)}) async-start(), calls=%async_computation.10 | async-start | bytes 5898240 | tf_op jit(solution)/shard_map/reduce_scatter | solution.py:218
  549.4 27.0 %slice-start.19 = ((s8[8388608]{0:T(1024)(128)(4,1)}), s8[4194304]{0:T(1024)(128)(4,1)S(1)}, s32[]{:S(2)}) async-start(s8[8388608]{0:T(1024)(128)(4,1)} %bitcast.174), calls=%async_computation.32 | async-start | bytes 8388608
  555.1 21.3 %slice-start.20 = ((s8[8388608]{0:T(1024)(128)(4,1)}), s8[4194304]{0:T(1024)(128)(4,1)S(1)}, s32[]{:S(2)}) async-start(s8[8388608]{0:T(1024)(128)(4,1)} %bitcast.174), calls=%async_computation.33 | async-start | bytes 8388608
  582.7 14.3 %slice-start.8 = ((s8[16777216]{0:T(1024)(128)(4,1)}), s8[4194304]{0:T(1024)(128)(4,1)S(1)}, s32[]{:S(2)}) async-start(s8[16777216]{0:T(1024)(128)(4,1)} %bitcast.166), calls=%async_computation.21 | async-start | bytes 8388608
  582.7 14.3 %slice-start.9 = ((s8[16777216]{0:T(1024)(128)(4,1)}), s8[4194304]{0:T(1024)(128)(4,1)S(1)}, s32[]{:S(2)}) async-start(s8[16777216]{0:T(1024)(128)(4,1)} %bitcast.166), calls=%async_computation.22 | async-start | bytes 8388608
  587.4 9.6 %slice-start.10 = ((s8[16777216]{0:T(1024)(128)(4,1)}), s8[4194304]{0:T(1024)(128)(4,1)S(1)}, s32[]{:S(2)}) async-start(s8[16777216]{0:T(1024)(128)(4,1)} %bitcast.166), calls=%async_computation.23 | async-start | bytes 8388608
  587.4 10.0 %slice-start.11 = ((s8[16777216]{0:T(1024)(128)(4,1)}), s8[4194304]{0:T(1024)(128)(4,1)S(1)}, s32[]{:S(2)}) async-start(s8[16777216]{0:T(1024)(128)(4,1)} %bitcast.166), calls=%async_computation.24 | async-start | bytes 8388608
  666.7 92.6 %all-to-all-start.2 = ((bf16[8,2,98304]{2,1,0:T(2,128)(2,1)}), bf16[8,2,98304]{2,1,0:T(2,128)(2,1)}, u32[]{:S(2)}, u32[]{:S(2)}) async-start(bf16[8,2,98304]{2,1,0:T(2,128)(2,1)} %reshape.443), calls=%async_computation.2 | async-start | bytes 6291456 | tf_op jit(solution)/shard_map/all_to_all | solution.py:363
  671.3 194.2 %all-reduce.10.cloned.1.call-start = ((), (), s32[]{:S(2)}) async-start(), calls=%async_computation.12 | async-start | bytes 6291456 | tf_op jit(solution)/shard_map/psum | solution.py:394
  671.3 112.0 %collective-permute-start.3 = (bf16[3,512,1024]{2,1,0:T(8,128)(2,1)}, bf16[3,512,1024]{2,1,0:T(8,128)(2,1)}, u32[]{:S(2)}, u32[]{:S(2)}) collective-permute-start(bf16[3,512,1024]{2,1,0:T(8,128)(2,1)} %all-gather.16.cloned.1.call-done), channel_id=1, source_target_pairs={{0,8},{8,0},{16,24},{24,16},{1,9},{9,1},{17,25},{25,17},{2,10},{10... | collective-permute-start | bytes 9437192 | tf_op jit(solution)/shard_map/ppermute | solution.py:175
  795.9 9.3 %copy-start.88 = (f32[1024]{0:T(1024)S(1)}, f32[1024]{0:T(1024)}, u32[]{:S(2)}) copy-start(f32[1024]{0:T(1024)} %get-tuple-element.76) | copy-start | bytes 12292
  795.9 9.3 %copy-start.90 = (f32[1024]{0:T(1024)S(1)}, f32[1024]{0:T(1024)}, u32[]{:S(2)}) copy-start(f32[1024]{0:T(1024)} %get-tuple-element.80) | copy-start | bytes 12292
  796.0 9.3 %copy-start.94 = (f32[1024]{0:T(1024)S(1)}, f32[1024]{0:T(1024)}, u32[]{:S(2)}) copy-start(f32[1024]{0:T(1024)} %get-tuple-element.78) | copy-start | bytes 12292
  796.0 9.3 %copy-start.87 = (f32[1024]{0:T(1024)S(1)}, f32[1024]{0:T(1024)}, u32[]{:S(2)}) copy-start(f32[1024]{0:T(1024)} %get-tuple-element.88) | copy-start | bytes 12292
  796.0 9.3 %copy-start.89 = (f32[1024]{0:T(1024)S(1)}, f32[1024]{0:T(1024)}, u32[]{:S(2)}) copy-start(f32[1024]{0:T(1024)} %get-tuple-element.91) | copy-start | bytes 12292
  796.0 9.3 %copy-start.93 = (f32[1024]{0:T(1024)S(1)}, f32[1024]{0:T(1024)}, u32[]{:S(2)}) copy-start(f32[1024]{0:T(1024)} %get-tuple-element.89) | copy-start | bytes 12292
  796.0 9.3 %copy-start.86 = (f32[1024]{0:T(1024)S(1)}, f32[1024]{0:T(1024)}, u32[]{:S(2)}) copy-start(f32[1024]{0:T(1024)} %get-tuple-element.101) | copy-start | bytes 12292
  796.0 9.3 %copy-start.91 = (f32[4096]{0:T(1024)S(1)}, f32[4096]{0:T(1024)}, u32[]{:S(2)}) copy-start(f32[4096]{0:T(1024)} %get-tuple-element.179) | copy-start | bytes 49156
  796.0 9.3 %copy-start.92 = (f32[1024]{0:T(1024)S(1)}, f32[1024]{0:T(1024)}, u32[]{:S(2)}) copy-start(f32[1024]{0:T(1024)} %get-tuple-element.103) | copy-start | bytes 12292
  796.0 52.5 %copy-start.17 = (f32[512,1024]{1,0:T(8,128)S(1)}, f32[512,1024]{1,0:T(8,128)}, u32[]{:S(2)}) copy-start(f32[512,1024]{1,0:T(8,128)} %copy-done.16) | copy-start | bytes 6291460
  865.5 8.9 %copy-start.1 = (bf16[1024,512]{1,0:T(8,128)(2,1)S(1)}, bf16[1024,512]{1,0:T(8,128)(2,1)}, u32[]{:S(2)}) copy-start(bf16[1024,512]{1,0:T(8,128)(2,1)} %param.22) | copy-start | bytes 3145732
  (77 other events, 325.0 us)
Sparse Core Ops, SparseCore 0:
  15.0 127.3 all-gather.7
  145.0 38.4 all-gather.9
  186.1 73.3 all-gather.11
  271.9 91.9 all-gather.13
  456.6 73.0 all-gather.15
  548.3 87.8 reduce-scatter.4
  639.8 151.8 reduce-scatter.2
  796.0 69.4 all-reduce.9

commit v20 on v14

--- a/solution.py
+++ b/solution.py
@@ -277,6 +277,8 @@
         gathered_first, qkv_weight, qkv_bias, cos_table, sine_table, seq_count, length
     )
     attn_heads, totals = attend_forward(query, key_rows, values, block_rows)
+    attn_heads, qkv_late = lax.optimization_barrier((attn_heads, qkv_weight))
+    qkv_full = join_halves(gather_mine(qkv_late, core, 1, 2), core, 1)
     attn_low = attn_heads.reshape(group_rows, inner).astype(jnp.bfloat16)
     attn_rows = lax.all_to_all(attn_low, "narrow", 0, 1, tiled=True)
     out_full = lax.all_gather(out_weight, "narrow", axis=0, tiled=True)
@@ -289,8 +291,6 @@
     down_full = gather_halves(down_weight, core, 1, 0)
     hidden = jnp.dot(low_third, up_full, preferred_element_type=jnp.float32) + up_bias_full
     act_low = gelu_value(hidden).astype(jnp.bfloat16)
-    act_low, qkv_late = lax.optimization_barrier((act_low, qkv_weight))
-    qkv_full = join_halves(gather_mine(qkv_late, core, 1, 2), core, 1)
     pre_mlp = jnp.dot(act_low, down_full, preferred_element_type=jnp.float32) + down_bias
     normed_fourth, inverse_fourth = norm_stats(pre_mlp)
     final_sum = residual + normed_fourth * norm_gains[3] + norm_biases[3]

time: 876 us -> 926 us (1.057)
  waiting for transfers between devices: 247 us -> 294 us
    all_gather x3, waiting for transfers between devices: 1.78 us -> 67.7 us  [gather_mine(): return lax.all_gather(mine, 'narrow', axis=gather_axis, tiled=True)]
    all_to_all x1, waiting for transfers between devices: 58.6 us -> 46.9 us  [shards(): lax.all_to_all(qkv_grad.reshape(3, group_rows, heads_here, HEAD), 'narrow...]
    unnamed x227 -> x243, local copies, waits for them, and re-layouts: 63.9 us -> 68.6 us
  transfers between devices with their start and end apart: 17 -> 17, of which waited for: 7 -> 8; matrix products, arithmetic and copies ran while one was open for 47% -> 51% of each run, Pallas kernels for 0% -> 0%
where the time goes in v20:
time: 926 us; the launch traced here: 913 us
  waiting for transfers between devices  294 us (32%)
  matrix products  193 us (21%)
  local copies, waits for them, and re-layouts  186 us (20%)
  other arithmetic  127 us (14%)
  blocking collectives  82.7 us (9%)
  between operations  16.1 us (2%)
  starting transfers between devices  14.1 us (2%)
    all_gather x1, waiting for transfers between devices, shards(): gathered_first = lax.all_gather(low_first, 'narrow', axis=0, tiled=True)  93.9 us
    unnamed x243, local copies, waits for them, and re-layouts  68.6 us
    all_gather x3, waiting for transfers between devices, gather_mine(): return lax.all_gather(mine, 'narrow', axis=gather_axis, tiled=True)  67.7 us
    all_gather x1, waiting for transfers between devices, shards(): out_full = lax.all_gather(out_weight, 'narrow', axis=0, tiled=True)  55.3 us
    all_to_all x1, waiting for transfers between devices, shards(): lax.all_to_all(qkv_grad.reshape(3, group_rows, heads_here, HEAD), 'narrow...  46.9 us
    psum x1, blocking collectives, shards(): lax.psum((gain_local, bias_local, out_blocal, down_blocal, up_bgrad_rows)...  42.5 us
    dot_general x4, matrix products, attend_backward(): jnp.einsum('bqhd,bkhd->bhqk', grad_block, value_block, preferred_element_...  34.8 us
    all_gather x1, blocking collectives, shards(): bias_full = lax.all_gather(bias_flat, 'narrow', axis=0)  33.4 us
  transfers between devices with their start and end apart: 17, of which 8 were waited for; matrix products, arithmetic and copies ran while one was open for 51% of the time, Pallas kernels for 0%

profile of v20, /device:TPU:0, one launch (start us, length us, event | category | flops | bytes accessed | tf_op | source)
XLA Modules:
  0.0 913.3 jit_solution(14545556819054237916)
XLA Ops:
  15.0 33.4 %all-gather.1 = f32[8,1,896]{2,1,0:T(1,128)S(1)} all-gather(f32[1,1,896]{2,1,0:T(1,128)S(1)} %reshape.435), channel_id=2, replica_groups=mesh['wide'=4,'narrow'=8] {'narrow'}, dimensions={0}, use_global_device_ids=true | all-gather | bytes 32256 | tf_op jit(solution)/shard_map/all_gather | solution.py:270
  48.4 93.9 %all-gather.8.cloned.1.call-done = bf16[4096,1024]{1,0:T(8,128)(2,1)} async-done(((bf16[512,1024]{1,0:T(8,128)(2,1)}), bf16[4096,1024]{1,0:T(8,128)(2,1)}) %all-gather.8.cloned.1.call-update) | async-done | bytes 8388624 | tf_op jit(solution)/shard_map/all_gather | solution.py:271
  147.5 7.3 add_bitcast_fusion
  159.7 5.6 reshape.442
  165.4 9.9 %fusion.126 = (f32[2,2048,2,32]{3,2,1,0:T(2,128)}, f32[2,2048,2,32]{3,2,1,0:T(2,128)}) fusion(f32[2,2048,2,64]{3,2,1,0:T(2,128)} %reshape.442), kind=kLoop, calls=%fused_computation.272 | loop fusion | bytes 4194304 | tf_op jit(solution)/shard_map/slice | solution.py:41
  175.3 6.5 copy.168
  181.8 6.4 copy.167
  188.2 5.6 reshape.441
  193.8 9.9 %fusion.127 = (f32[2,2048,2,32]{3,2,1,0:T(2,128)}, f32[2,2048,2,32]{3,2,1,0:T(2,128)}) fusion(f32[2,2048,2,64]{3,2,1,0:T(2,128)} %reshape.441), kind=kLoop, calls=%fused_computation.273 | loop fusion | bytes 4194304 | tf_op jit(solution)/shard_map/slice | solution.py:41
  203.7 6.4 copy.166
  210.2 6.7 copy.165
  219.9 3.3 fusion
  223.2 4.4 exponential_reduce_fusion
  231.8 3.5 exponential_reduce_fusion.1
  248.9 4.7 copy.114
  253.6 3.7 convolution_bitcast_fusion.6
  257.4 5.8 convolution_bitcast_fusion.7
  263.2 6.7 convolution_bitcast_fusion.5
  270.2 4.4 convolution_bitcast_fusion.4
  278.4 3.8 all-to-all-start
  282.4 12.4 %all-gather.14.cloned.1.call-done = bf16[4096,512]{1,0:T(8,128)(2,1)} async-done(((bf16[512,512]{1,0:T(8,128)(2,1)}), bf16[4096,512]{1,0:T(8,128)(2,1)}) %all-gather.14.cloned.1.call-update) | async-done | bytes 4194320 | tf_op jit(solution)/shard_map/all_gather | solution.py:181
  294.8 55.3 %all-gather.10.cloned.1.call-done = bf16[1024,1024]{1,0:T(8,128)(2,1)} async-done(((bf16[128,1024]{1,0:T(8,128)(2,1)}), bf16[1024,1024]{1,0:T(8,128)(2,1)}) %all-gather.10.cloned.1.call-update) | async-done | bytes 2097168 | tf_op jit(solution)/shard_map/all_gather | solution.py:284
  358.4 55.3 %all-gather.16.cloned.1.call-done = bf16[3,512,1024]{2,1,0:T(8,128)(2,1)} async-done(((bf16[3,512,128]{2,1,0:T(8,128)(2,1)}), bf16[3,512,1024]{2,1,0:T(8,128)(2,1)}) %all-gather.16.cloned.1.call-update) | async-done | bytes 3145744 | tf_op jit(solution)/shard_map/all_gather | solution.py:181
  413.8 5.2 broadcast_select_fusion.3
  419.0 10.2 %multiply_convert_fusion.3 = (bf16[512,4096]{1,0:T(8,128)(2,1)}, f32[512,4096]{1,0:T(8,128)}) fusion(f32[4096]{0:T(1024)S(1)} %bitcast.210, bf16[512,4096]{1,0:T(8,128)(2,1)} %get-tuple-element.107, bf16[512,4096]{1,0:T(8,128)(2,1)S(1)} %get-tuple-element.106, f32[512,1024]{1,0:T(8,128)S(1)} %copy-done.11, f32[1024]{0:T(1024)S(1)} %bitcast.212, ...), kind=kOutput, calls=%fused_computation.33 | convolution fusion | flops 4326948864 | bytes 23097344 | tf_op jit(solution)/shard_map/dot_general | solution.py:292
  429.2 5.2 broadcast_select_fusion.1
  434.5 9.3 %add_reduce_fusion = (f32[512]{0:T(512)S(1)}, f32[512,1024]{1,0:T(8,128)S(1)}) fusion(f32[1024]{0:T(1024)S(1)} %copy-done.71, bf16[512,4096]{1,0:T(8,128)(2,1)} %get-tuple-element.159, bf16[4096,512]{1,0:T(8,128)(2,1)} %get-tuple-element.105, bf16[4096,512]{1,0:T(8,128)(2,1)} %get-tuple-element.104), kind=kOutput, calls=%fused_computation.130 | convolution fusion | flops 4312792576 | bytes 14686208 | tf_op jit(solution)/shard_map/dot_general | solution.py:294
  448.6 8.6 fusion.131
  457.2 12.4 %convert_reduce_fusion = (f32[4096]{0:T(1024)}, bf16[512,4096]{1,0:T(8,128)(2,1)}) fusion(f32[512,4096]{1,0:T(8,128)} %get-tuple-element.160, f32[4096]{0:T(1024)S(1)} %bitcast.211, bf16[512,1024]{1,0:T(8,128)(2,1)S(1)} %get-tuple-element.98, bf16[4096,512]{1,0:T(8,128)(2,1)} %get-tuple-element.105, bf16[4096,512]{1,0:T(8,128)(2,1)} %get-tuple-element.104), kind=kOutput, calls=%fused_computation.26 | convolution fusion | flops 4339003392 | bytes 22052864 | tf_op jit(solution)/shard_map/dot_general | solution.py:322
  469.5 9.1 multiply_reduce_fusion.5
  478.7 10.5 %fusion.122 = f32[1024,4096]{1,0:T(8,128)} fusion(bf16[512,4096]{1,0:T(8,128)(2,1)} %get-tuple-element.174, f32[512,1024]{1,0:T(8,128)S(1)} %copy-done.11, f32[1024]{0:T(1024)S(1)} %bitcast.213, f32[1024]{0:T(1024)S(1)} %bitcast.201, f32[512]{0:T(512)S(1)} %add_rsqrt_fusion.1, f32[512]{0:T(512)S(1)} %broadcast_multiply_fusion.9), kind=kOutput, calls=%fused_computation.269 | convolution fusion | flops 4297588736 | bytes 23080960 | tf_op jit(solution)/shard_map/dot_general | solution.py:327
  497.4 4.2 all-to-all-start.1
  504.8 5.9 dynamic-slice_convert_fusion.1
  510.8 6.0 dynamic-slice_convert_fusion
  518.5 9.7 %all-to-all-done.1 = bf16[512,8,128]{0,2,1:T(8,128)(2,1)} async-done(((bf16[512,8,128]{0,2,1:T(8,128)(2,1)}), bf16[512,8,128]{0,2,1:T(8,128)(2,1)}, u32[]{:S(2)}, u32[]{:S(2)}) %all-to-all-start.1) | async-done | bytes 1048608 | tf_op jit(solution)/shard_map/all_to_all | solution.py:341
  536.1 8.2 multiply_reduce_fusion.2
  544.4 3.6 multiply_reduce_fusion.3
  548.0 6.1 multiply_convert_fusion.2
  555.9 7.2 multiply_reduce_fusion.1
  563.0 8.8 multiply_convert_fusion.1
  571.8 8.1 add_convert_fusion
  580.3 4.9 multiply_convert_fusion.4
  591.5 15.8 %multiply_reduce_fusion = (f32[2,2,512]{2,1,0:T(2,128)}, f32[2,2,512,2048]{3,2,1,0:T(8,128)}) fusion(f32[2,2,512,2048]{3,2,1,0:T(8,128)} %copy-done.2, f32[2,2,512]{2,1,0:T(2,128)} %copy-done.70, pred[512,2048]{1,0:T(8,128)(4,1)S(1)} %iota_compare_fusion, bf16[2,2048,2,64]{1,3,2,0:T(8,128)(2,1)} %copy-done.31, bf16[2,512,2,64]{1,0,3,2:T(2,128)(2,1)} %get-tuple-element.125), kind=kOutput, calls=%fused_computation.1 | convolution fusion | flops 557840384 | bytes 35930112 | tf_op jit(solution)/shard_map/bqhd,bkhd->bhqk/dot_general | solution.py:141
  608.8 8.9 multiply_convert_fusion
  617.7 4.0 fusion.60
  630.3 6.4 add_convert_fusion.1
  640.5 3.4 multiply_add_fusion.2
  650.5 7.9 convolution_bitcast_fusion.1
  658.4 7.5 fusion.30
  678.9 3.9 pad_maximum_fusion.7
  682.8 14.5 %copy.140 = bf16[3,4096,2,64]{3,2,0,1:T(2,128)(2,1)} copy(bf16[3,4096,2,64]{1,3,2,0:T(8,128)(2,1)} %pad_maximum_fusion.7) | data formatting | bytes 6291456 | tf_op jit(solution)/shard_map/stack | solution.py:350
  697.3 9.0 reshape.443
  706.3 4.4 all-to-all-start.2
  710.9 6.0 broadcast_select_fusion.5
  728.0 6.8 psum.71
  735.3 8.6 fusion.56
  743.9 46.9 %all-to-all-done.2 = bf16[8,2,98304]{2,1,0:T(2,128)(2,1)} async-done(((bf16[8,2,98304]{2,1,0:T(2,128)(2,1)}), bf16[8,2,98304]{2,1,0:T(2,128)(2,1)}, u32[]{:S(2)}, u32[]{:S(2)}) %all-to-all-start.2) | async-done | bytes 3145760 | tf_op jit(solution)/shard_map/all_to_all | solution.py:359
  790.8 8.8 reshape.444
  799.6 15.3 %copy.157 = bf16[3,8,512,2,64]{2,4,3,1,0:T(8,128)(2,1)} copy(bf16[3,8,512,2,64]{4,3,0,2,1:T(2,128)(2,1)} %bitcast.181) | data formatting | bytes 6291456 | tf_op jit(solution)/shard_map/all_to_all | solution.py:359
  817.1 6.3 reduce-scatter.3.cloned.1.call-done
  827.7 9.2 %fusion.45 = (f32[1024]{0:T(1024)S(1)}, f32[512]{0:T(512)S(1)}, f32[512]{0:T(512)S(1)}, f32[1024]{0:T(1024)S(1)}, f32[512,1024,1]{1,0,2:T(8,128)}) fusion(bf16[512,1024]{1,0:T(8,128)(2,1)S(1)} %copy-done.12, f32[512]{0:T(512)S(1)} %copy-done.77, f32[512]{0:T(512)S(1)} %copy-done.75, f32[1024]{0:T(1024)S(1)} %bitcast.197, ...), kind=kOutput, calls=%fused_computation.91 | convolution fusion | flops 3239048192 | bytes 12603392 | tf_op jit(solution)/shard_map/tse,tde->sd/dot_general | solution.py:365
  837.0 42.5 %all-reduce.6 = (f32[1024]{0:T(1024)}, f32[4096]{0:T(1024)S(1)}, f32[1024]{0:T(1024)}, f32[4,1024]{1,0:T(4,128)}, f32[4,1024]{1,0:T(4,128)}) all-reduce(f32[1024]{0:T(1024)S(1)} %copy-done.84, f32[4096]{0:T(1024)S(1)} %copy-done.83, f32[1024]{0:T(1024)S(1)} %copy-done.78, ...), channel_id=1, replica_groups=mesh['wide'=4,'narrow'=8] {'wide','narrow'}, use_global_device_ids=true, to_apply=%region_36.37 | all-reduce | flops 14336 | bytes 114688 | tf_op jit(solution)/shard_map/psum | solution.py:397
  880.2 3.3 fusion.44
  883.5 13.6 %all-reduce.10.cloned.1.call-done = (bf16[3,1024,128]{1,2,0:T(8,128)(2,1)}, bf16[128,1024]{1,0:T(8,128)(2,1)}, bf16[1024,512]{1,0:T(8,128)(2,1)}, bf16[512,1024]{1,0:T(8,128)(2,1)}) async-done(((bf16[3,1024,128]{1,2,0:T(8,128)(2,1)}, bf16[128,1024]{1,0:T(8,128)(2,1)}, bf16[1024,512]{1,0:T(8,128)(2,1)}, bf16[512,1024]{1,0:T(8,128)(2,1)}), (bf16[3,1024,128]{1,2,0:T(8,128)(2,1)}, bf16[128,1024]{1,0:T(8,128)(2,1)}, ...) | async-done | bytes 3145744 | tf_op jit(solution)/shard_map/psum | solution.py:390
  (387 shorter events, 145.6 us)
Async XLA Ops:
  7.2 135.2 %copy-start = (bf16[1024,512]{1,0:T(8,128)(2,1)S(1)}, bf16[1024,512]{1,0:T(8,128)(2,1)}, u32[]{:S(2)}) copy-start(bf16[1024,512]{1,0:T(8,128)(2,1)} %param.22) | copy-start | bytes 3145732
  7.2 136.0 %copy-start.64 = (bf16[512,1024]{1,0:T(8,128)(2,1)S(1)}, bf16[512,1024]{1,0:T(8,128)(2,1)}, u32[]{:S(2)}) copy-start(bf16[512,1024]{1,0:T(8,128)(2,1)} %param.24) | copy-start | bytes 3145732
  7.2 135.1 %all-gather.8.cloned.1.call-start = ((), (), s32[]{:S(2)}) async-start(), calls=%async_computation.5 | async-start | bytes 9437184 | tf_op jit(solution)/shard_map/all_gather | solution.py:271
  9.1 135.1 %copy-start.72 = (f32[1,1024]{1,0:T(1,128)}, f32[1,1024]{1,0:T(1,128)S(1)}, u32[]{:S(2)}) copy-start(f32[1,1024]{1,0:T(1,128)S(1)} %get-tuple-element.141) | copy-start | bytes 12292
  10.5 135.0 %copy-start.74 = (f32[512]{0:T(512)}, f32[512]{0:T(512)S(1)}, u32[]{:S(2)}) copy-start(f32[512]{0:T(512)S(1)} %broadcast_multiply_fusion.11) | copy-start | bytes 6148
  12.2 134.4 %copy-start.76 = (f32[512]{0:T(512)}, f32[512]{0:T(512)S(1)}, u32[]{:S(2)}) copy-start(f32[512]{0:T(512)S(1)} %add_rsqrt_fusion.3) | copy-start | bytes 6148
  14.9 260.8 %all-gather.12.cloned.1.call-start = ((), (), s32[]{:S(2)}) async-start(), calls=%async_computation.7 | async-start | bytes 4718592 | tf_op jit(solution)/shard_map/all_gather | solution.py:181
  143.2 151.6 %all-gather.14.cloned.1.call-start = ((), (), s32[]{:S(2)}) async-start(), calls=%async_computation.8 | async-start | bytes 4718592 | tf_op jit(solution)/shard_map/all_gather | solution.py:181
  144.1 206.0 %all-gather.10.cloned.1.call-start = ((), (), s32[]{:S(2)}) async-start(), calls=%async_computation.6 | async-start | bytes 2359296 | tf_op jit(solution)/shard_map/all_gather | solution.py:284
  144.7 269.1 %all-gather.16.cloned.1.call-start = ((), (), s32[]{:S(2)}) async-start(), calls=%async_computation.9 | async-start | bytes 3538944 | tf_op jit(solution)/shard_map/all_gather | solution.py:181
  144.9 97.5 %copy-start.33 = (pred[512,512]{0,1:T(8,128)(4,1)}, pred[512,512]{0,1:T(8,128)(4,1)S(1)}, u32[]{:S(2)}) copy-start(pred[512,512]{0,1:T(8,128)(4,1)S(1)} %iota_compare_fusion.3) | copy-start | bytes 786436
  146.6 70.3 %copy-start.46 = (f32[2048,32]{0,1:T(8,128)}, f32[2048,32]{0,1:T(8,128)S(1)}, u32[]{:S(2)}) copy-start(f32[2048,32]{0,1:T(8,128)S(1)} %get-tuple-element.147) | copy-start | bytes 786436
  146.6 70.3 %copy-start.48 = (f32[2048,32]{0,1:T(8,128)}, f32[2048,32]{0,1:T(8,128)S(1)}, u32[]{:S(2)}) copy-start(f32[2048,32]{0,1:T(8,128)S(1)} %get-tuple-element.148) | copy-start | bytes 786436
  147.1 116.0 %copy-start.13 = (pred[512,1536]{1,0:T(8,128)(4,1)}, pred[512,1536]{1,0:T(8,128)(4,1)S(1)}, u32[]{:S(2)}) copy-start(pred[512,1536]{1,0:T(8,128)(4,1)S(1)} %iota_compare_fusion.1) | copy-start | bytes 2359300
  147.5 109.8 %copy-start.24 = (pred[512,1024]{1,0:T(8,128)(4,1)}, pred[512,1024]{1,0:T(8,128)(4,1)S(1)}, u32[]{:S(2)}) copy-start(pred[512,1024]{1,0:T(8,128)(4,1)S(1)} %iota_compare_fusion.2) | copy-start | bytes 1572868
  219.7 16.7 %copy-start.27 = (bf16[2,2048,2,32]{1,3,2,0:T(8,128)(2,1)}, bf16[2,2048,2,32]{1,3,2,0:T(8,128)(2,1)S(1)}, u32[]{:S(2)}) copy-start(bf16[2,2048,2,32]{1,3,2,0:T(8,128)(2,1)S(1)} %get-tuple-element.120) | copy-start | bytes 1572868
  219.7 16.7 %copy-start.29 = (bf16[2,2048,2,32]{1,3,2,0:T(8,128)(2,1)}, bf16[2,2048,2,32]{1,3,2,0:T(8,128)(2,1)S(1)}, u32[]{:S(2)}) copy-start(bf16[2,2048,2,32]{1,3,2,0:T(8,128)(2,1)S(1)} %get-tuple-element.121) | copy-start | bytes 1572868
  219.8 21.7 %copy-start.18 = (bf16[2,2048,2,32]{1,3,2,0:T(8,128)(2,1)}, bf16[2,2048,2,32]{1,3,2,0:T(8,128)(2,1)S(1)}, u32[]{:S(2)}) copy-start(bf16[2,2048,2,32]{1,3,2,0:T(8,128)(2,1)S(1)} %get-tuple-element.137) | copy-start | bytes 1572868
  219.8 21.7 %copy-start.20 = (bf16[2,2048,2,32]{1,3,2,0:T(8,128)(2,1)}, bf16[2,2048,2,32]{1,3,2,0:T(8,128)(2,1)S(1)}, u32[]{:S(2)}) copy-start(bf16[2,2048,2,32]{1,3,2,0:T(8,128)(2,1)S(1)} %get-tuple-element.138) | copy-start | bytes 1572868
  219.8 21.7 %copy-start.44 = (bf16[2,512,2,64]{1,3,2,0:T(8,128)(2,1)}, bf16[2,512,2,64]{1,3,2,0:T(8,128)(2,1)S(1)}, u32[]{:S(2)}) copy-start(bf16[2,512,2,64]{1,3,2,0:T(8,128)(2,1)S(1)} %get-tuple-element.176) | copy-start | bytes 786436
  229.3 40.7 %copy-start.70 = (f32[2,2,512]{2,1,0:T(2,128)}, f32[2,2,512]{2,1,0:T(2,128)S(1)}, u32[]{:S(2)}) copy-start(f32[2,2,512]{2,1,0:T(2,128)S(1)} %log_add_fusion) | copy-start | bytes 24580
  241.5 306.5 %copy-start.66 = (f32[2,2,512]{2,1,0:T(2,128)}, f32[2,2,512]{2,1,0:T(2,128)S(1)}, u32[]{:S(2)}) copy-start(f32[2,2,512]{2,1,0:T(2,128)S(1)} %log_add_fusion.2) | copy-start | bytes 24580
  245.3 334.9 %copy-start.68 = (f32[2,2,512]{2,1,0:T(2,128)}, f32[2,2,512]{2,1,0:T(2,128)S(1)}, u32[]{:S(2)}) copy-start(f32[2,2,512]{2,1,0:T(2,128)S(1)} %log_add_fusion.3) | copy-start | bytes 24580
  253.6 16.4 %copy-start.31 = (bf16[2,2048,2,64]{1,3,2,0:T(8,128)(2,1)}, bf16[2,2048,2,64]{1,3,2,0:T(8,128)(2,1)S(1)}, u32[]{:S(2)}) copy-start(bf16[2,2048,2,64]{1,3,2,0:T(8,128)(2,1)S(1)} %copy.114) | copy-start | bytes 3145732
  257.3 12.6 %slice-start = ((s8[16777216]{0:T(1024)(128)(4,1)}), s8[4194304]{0:T(1024)(128)(4,1)S(1)}, s32[]{:S(2)}) async-start(s8[16777216]{0:T(1024)(128)(4,1)} %bitcast.164), calls=%async_computation.13 | async-start | bytes 8388608
  257.3 12.6 %slice-start.1 = ((s8[16777216]{0:T(1024)(128)(4,1)}), s8[4194304]{0:T(1024)(128)(4,1)S(1)}, s32[]{:S(2)}) async-start(s8[16777216]{0:T(1024)(128)(4,1)} %bitcast.164), calls=%async_computation.14 | async-start | bytes 8388608
  275.6 75.5 %copy-start.63 = (f32[1024]{0:T(1024)S(1)}, f32[1024]{0:T(1024)}, u32[]{:S(2)}) copy-start(f32[1024]{0:T(1024)} %param.21) | copy-start | bytes 12292
  275.7 138.1 %collective-permute-start = (bf16[512,4096]{1,0:T(8,128)(2,1)}, bf16[512,4096]{1,0:T(8,128)(2,1)}, u32[]{:S(2)}, u32[]{:S(2)}) collective-permute-start(bf16[512,4096]{1,0:T(8,128)(2,1)} %all-gather.12.cloned.1.call-done), channel_id=1, source_target_pairs={{0,8},{8,0},{16,24},{24,16},{1,9},{9,1},{17,25},{25,17},{2,10},{10... | collective-permute-start | bytes 12582920 | tf_op jit(solution)/shard_map/ppermute | solution.py:175
  278.4 71.7 %all-to-all-start = ((bf16[8,512,128]{1,2,0:T(8,128)(2,1)}), bf16[8,512,128]{1,2,0:T(8,128)(2,1)S(1)}, u32[]{:S(2)}, u32[]{:S(2)}) async-start(bf16[8,512,128]{1,2,0:T(8,128)(2,1)} %copy.126), calls=%async_computation | async-start | bytes 2097152 | tf_op jit(solution)/shard_map/all_to_all | solution.py:283
  294.8 134.4 %collective-permute-start.1 = (bf16[4096,512]{1,0:T(8,128)(2,1)}, bf16[4096,512]{1,0:T(8,128)(2,1)}, u32[]{:S(2)}, u32[]{:S(2)}) collective-permute-start(bf16[4096,512]{1,0:T(8,128)(2,1)} %all-gather.14.cloned.1.call-done), channel_id=1, source_target_pairs={{0,8},{8,0},{16,24},{24,16},{1,9},{9,1},{17,25},{25,17},{2,10},{10... | collective-permute-start | bytes 12582920 | tf_op jit(solution)/shard_map/ppermute | solution.py:175
  413.8 297.1 %collective-permute-start.2 = (bf16[3,512,1024]{2,1,0:T(8,128)(2,1)}, bf16[3,512,1024]{2,1,0:T(8,128)(2,1)}, u32[]{:S(2)}, u32[]{:S(2)}) collective-permute-start(bf16[3,512,1024]{2,1,0:T(8,128)(2,1)} %all-gather.16.cloned.1.call-done), channel_id=1, source_target_pairs={{0,8},{8,0},{16,24},{24,16},{1,9},{9,1},{17,25},{25,17},{2,10},{10... | collective-permute-start | bytes 9437192 | tf_op jit(solution)/shard_map/ppermute | solution.py:175
  419.0 10.2 %copy-start.38 = (bf16[4096,512]{1,0:T(8,128)(2,1)S(1)}, bf16[4096,512]{1,0:T(8,128)(2,1)}, u32[]{:S(2)}) copy-start(bf16[4096,512]{1,0:T(8,128)(2,1)} %all-gather.14.cloned.1.call-done) | copy-start | bytes 12582916
  434.5 9.7 %copy-start.36 = (bf16[512,1024]{1,0:T(8,128)(2,1)S(1)}, bf16[512,1024]{1,0:T(8,128)(2,1)}, u32[]{:S(2)}) copy-start(bf16[512,1024]{1,0:T(8,128)(2,1)} %param.15) | copy-start | bytes 3145732
  497.4 30.8 %all-to-all-start.1 = ((bf16[512,8,128]{0,2,1:T(8,128)(2,1)}), bf16[512,8,128]{0,2,1:T(8,128)(2,1)}, u32[]{:S(2)}, u32[]{:S(2)}) async-start(bf16[512,8,128]{0,2,1:T(8,128)(2,1)} %bitcast.17), calls=%async_computation.1 | async-start | bytes 2097152 | tf_op jit(solution)/shard_map/all_to_all | solution.py:341
  501.6 313.3 %reduce-scatter.5.cloned.1.call-start = ((), (), s32[]{:S(2)}) async-start(), calls=%async_computation.11 | async-start | bytes 4718592 | tf_op jit(solution)/shard_map/reduce_scatter | solution.py:200
  504.3 12.8 %collective-permute-start.4 = (bf16[1024,512]{1,0:T(8,128)(2,1)S(1)}, bf16[1024,512]{1,0:T(8,128)(2,1)S(1)}, u32[]{:S(2)}, u32[]{:S(2)}) collective-permute-start(bf16[1024,512]{1,0:T(8,128)(2,1)S(1)} %dynamic-slice_convert_fusion.2), channel_id=1, source_target_pairs={{0,8},{8,0},{16,24},{24,16},{1,9},{9,1},{17,25},{25,17},{2,10},{10... | collective-permute-start | bytes 3145736 | tf_op jit(solution)/shard_map/ppermute | solution.py:175
  510.7 119.7 %collective-permute-start.3 = (bf16[4096,512]{1,0:T(8,128)(2,1)}, bf16[4096,512]{1,0:T(8,128)(2,1)}, u32[]{:S(2)}, u32[]{:S(2)}) collective-permute-start(bf16[4096,512]{1,0:T(8,128)(2,1)} %dynamic-slice_convert_fusion.1), channel_id=1, source_target_pairs={{0,8},{8,0},{16,24},{24,16},{1,9},{9,1},{17,25},{25,17},{2,10},{10... | collective-permute-start | bytes 12582920 | tf_op jit(solution)/shard_map/ppermute | solution.py:175
  516.7 55.1 %collective-permute-start.5 = (bf16[512,4096]{1,0:T(8,128)(2,1)}, bf16[512,4096]{1,0:T(8,128)(2,1)}, u32[]{:S(2)}, u32[]{:S(2)}) collective-permute-start(bf16[512,4096]{1,0:T(8,128)(2,1)} %dynamic-slice_convert_fusion), channel_id=1, source_target_pairs={{0,8},{8,0},{16,24},{24,16},{1,9},{9,1},{17,25},{25,17},{2,10},{10... | collective-permute-start | bytes 12582920 | tf_op jit(solution)/shard_map/ppermute | solution.py:175
  518.5 17.6 %copy-start.25 = (pred[512,1024]{1,0:T(8,128)(4,1)S(1)}, pred[512,1024]{1,0:T(8,128)(4,1)}, u32[]{:S(2)}) copy-start(pred[512,1024]{1,0:T(8,128)(4,1)} %copy-done.24) | copy-start | bytes 1572868
  518.5 17.6 %copy-start.32 = (bf16[2,2048,2,64]{1,3,2,0:T(8,128)(2,1)S(1)}, bf16[2,2048,2,64]{1,3,2,0:T(8,128)(2,1)}, u32[]{:S(2)}) copy-start(bf16[2,2048,2,64]{1,3,2,0:T(8,128)(2,1)} %copy-done.31) | copy-start | bytes 3145732
  536.0 18.1 %copy-start.53 = (bf16[2,512,2,64]{1,0,3,2:T(2,128)(2,1)}, bf16[2,512,2,64]{1,0,3,2:T(2,128)(2,1)S(1)}, u32[]{:S(2)}) copy-start(bf16[2,512,2,64]{1,0,3,2:T(2,128)(2,1)S(1)} %get-tuple-element.126) | copy-start | bytes 786436
  536.0 11.9 %slice-start.15 = ((s8[8388608]{0:T(1024)(128)(4,1)}), s8[4194304]{0:T(1024)(128)(4,1)S(1)}, s32[]{:S(2)}) async-start(s8[8388608]{0:T(1024)(128)(4,1)} %bitcast.172), calls=%async_computation.28 | async-start | bytes 8388608
  536.1 11.9 %slice-start.16 = ((s8[8388608]{0:T(1024)(128)(4,1)}), s8[4194304]{0:T(1024)(128)(4,1)S(1)}, s32[]{:S(2)}) async-start(s8[8388608]{0:T(1024)(128)(4,1)} %bitcast.172), calls=%async_computation.29 | async-start | bytes 8388608
  544.4 9.8 %slice-start.12 = ((s8[12582912]{0:T(1024)(128)(4,1)}), s8[4194304]{0:T(1024)(128)(4,1)S(1)}, s32[]{:S(2)}) async-start(s8[12582912]{0:T(1024)(128)(4,1)} %bitcast.170), calls=%async_computation.25 | async-start | bytes 8388608
  580.0 243.4 %reduce-scatter.3.cloned.1.call-start = ((), (), s32[]{:S(2)}) async-start(), calls=%async_computation.10 | async-start | bytes 5898240 | tf_op jit(solution)/shard_map/reduce_scatter | solution.py:218
  591.5 15.8 %slice-start.4 = ((s8[16777216]{0:T(1024)(128)(4,1)}), s8[4194304]{0:T(1024)(128)(4,1)S(1)}, s32[]{:S(2)}) async-start(s8[16777216]{0:T(1024)(128)(4,1)} %bitcast.166), calls=%async_computation.17 | async-start | bytes 8388608
  591.5 15.8 %slice-start.5 = ((s8[16777216]{0:T(1024)(128)(4,1)}), s8[4194304]{0:T(1024)(128)(4,1)S(1)}, s32[]{:S(2)}) async-start(s8[16777216]{0:T(1024)(128)(4,1)} %bitcast.166), calls=%async_computation.18 | async-start | bytes 8388608
  591.5 15.8 %slice-start.6 = ((s8[16777216]{0:T(1024)(128)(4,1)}), s8[4194304]{0:T(1024)(128)(4,1)S(1)}, s32[]{:S(2)}) async-start(s8[16777216]{0:T(1024)(128)(4,1)} %bitcast.166), calls=%async_computation.19 | async-start | bytes 8388608
  591.5 17.3 %slice-start.7 = ((s8[16777216]{0:T(1024)(128)(4,1)}), s8[4194304]{0:T(1024)(128)(4,1)S(1)}, s32[]{:S(2)}) async-start(s8[16777216]{0:T(1024)(128)(4,1)} %bitcast.166), calls=%async_computation.20 | async-start | bytes 8388608
  647.3 11.1 %slice-start.8 = ((s8[16777216]{0:T(1024)(128)(4,1)}), s8[4194304]{0:T(1024)(128)(4,1)S(1)}, s32[]{:S(2)}) async-start(s8[16777216]{0:T(1024)(128)(4,1)} %bitcast.168), calls=%async_computation.21 | async-start | bytes 8388608
  647.3 11.1 %slice-start.9 = ((s8[16777216]{0:T(1024)(128)(4,1)}), s8[4194304]{0:T(1024)(128)(4,1)S(1)}, s32[]{:S(2)}) async-start(s8[16777216]{0:T(1024)(128)(4,1)} %bitcast.168), calls=%async_computation.22 | async-start | bytes 8388608
  706.3 84.5 %all-to-all-start.2 = ((bf16[8,2,98304]{2,1,0:T(2,128)(2,1)}), bf16[8,2,98304]{2,1,0:T(2,128)(2,1)}, u32[]{:S(2)}, u32[]{:S(2)}) async-start(bf16[8,2,98304]{2,1,0:T(2,128)(2,1)} %reshape.443), calls=%async_computation.2 | async-start | bytes 6291456 | tf_op jit(solution)/shard_map/all_to_all | solution.py:359
  710.8 186.4 %all-reduce.10.cloned.1.call-start = ((), (), s32[]{:S(2)}) async-start(), calls=%async_computation.12 | async-start | bytes 6291456 | tf_op jit(solution)/shard_map/psum | solution.py:390
  827.6 9.3 %copy-start.80 = (f32[1024]{0:T(1024)S(1)}, f32[1024]{0:T(1024)}, u32[]{:S(2)}) copy-start(f32[1024]{0:T(1024)} %get-tuple-element.72) | copy-start | bytes 12292
  827.6 9.3 %copy-start.82 = (f32[1024]{0:T(1024)S(1)}, f32[1024]{0:T(1024)}, u32[]{:S(2)}) copy-start(f32[1024]{0:T(1024)} %get-tuple-element.76) | copy-start | bytes 12292
  827.6 9.3 %copy-start.86 = (f32[1024]{0:T(1024)S(1)}, f32[1024]{0:T(1024)}, u32[]{:S(2)}) copy-start(f32[1024]{0:T(1024)} %get-tuple-element.74) | copy-start | bytes 12292
  827.6 9.3 %copy-start.79 = (f32[1024]{0:T(1024)S(1)}, f32[1024]{0:T(1024)}, u32[]{:S(2)}) copy-start(f32[1024]{0:T(1024)} %get-tuple-element.84) | copy-start | bytes 12292
  827.6 9.3 %copy-start.81 = (f32[1024]{0:T(1024)S(1)}, f32[1024]{0:T(1024)}, u32[]{:S(2)}) copy-start(f32[1024]{0:T(1024)} %get-tuple-element.87) | copy-start | bytes 12292
  827.6 9.3 %copy-start.85 = (f32[1024]{0:T(1024)S(1)}, f32[1024]{0:T(1024)}, u32[]{:S(2)}) copy-start(f32[1024]{0:T(1024)} %get-tuple-element.85) | copy-start | bytes 12292
  827.6 9.3 %copy-start.78 = (f32[1024]{0:T(1024)S(1)}, f32[1024]{0:T(1024)}, u32[]{:S(2)}) copy-start(f32[1024]{0:T(1024)} %get-tuple-element.97) | copy-start | bytes 12292
  827.7 9.3 %copy-start.83 = (f32[4096]{0:T(1024)S(1)}, f32[4096]{0:T(1024)}, u32[]{:S(2)}) copy-start(f32[4096]{0:T(1024)} %get-tuple-element.173) | copy-start | bytes 49156
  827.7 9.3 %copy-start.84 = (f32[1024]{0:T(1024)S(1)}, f32[1024]{0:T(1024)}, u32[]{:S(2)}) copy-start(f32[1024]{0:T(1024)} %get-tuple-element.99) | copy-start | bytes 12292
  827.7 52.5 %copy-start.17 = (f32[512,1024]{1,0:T(8,128)S(1)}, f32[512,1024]{1,0:T(8,128)}, u32[]{:S(2)}) copy-start(f32[512,1024]{1,0:T(8,128)} %copy-done.16) | copy-start | bytes 6291460
  897.2 8.9 copy-start.1
  (68 other events, 323.7 us)
Sparse Core Ops, SparseCore 0:
  15.0 127.3 all-gather.7
  145.0 72.8 all-gather.11
  220.0 74.7 all-gather.13
  296.8 53.2 all-gather.9
  352.6 61.1 all-gather.15
  580.1 87.7 reduce-scatter.4
  671.4 151.8 reduce-scatter.2
  827.7 69.4 all-reduce.9
